TPU v7x, 32 devices: a whole 2x2x4 slice. The times are simulated.
32 devices in a mesh: row: 8 (over y, x, core), col: 4 (over z).
Axes of the slice: x: 2, y: 2, z: 4, core: 2. Of those that a mesh axis runs over, the one named last changes fastest.
Arguments:
- tokens: bfloat16 [192, 8192], P('col', 'row'), may hold values from -6 to 6
- grad_out: bfloat16 [192, 8192], P('col', 'row'), may hold values from -6 to 6
- gate_weight: bfloat16 [8192, 14336], P('row', 'col'), may hold values from -0.0625 to 0.0625
- up_weight: bfloat16 [8192, 14336], P('row', 'col'), may hold values from -0.0625 to 0.0625
- down_weight: bfloat16 [14336, 8192], P('col', 'row'), may hold values from -0.046875 to 0.046875
Outputs:
- grad_tokens: bfloat16 [192, 8192], P('col', 'row')
- grad_gate_weight: bfloat16 [8192, 14336], P('row', 'col')
- grad_up_weight: bfloat16 [8192, 14336], P('row', 'col')
- grad_down_weight: bfloat16 [14336, 8192], P('col', 'row')
All inputs are finite; a program needn't handle non-finite values.
Results may differ from a plain program's by a relative error of at most 0.024.
Values may be sent and summed in bfloat16 or wider, within the bound.
No kernel may reach another device: no remote copies, remote signals or barrier semaphores. Data moves between devices by JAX's collectives and lax.ppermute only.
A program may use at most 128 MiB of HBM per device.

v0:
```python
import jax
import jax.numpy as jnp
from jax import lax
from jax.sharding import PartitionSpec as P


def contract_first(left, right):
    return lax.dot_general(
        left, right, (((0,), (0,)), ((), ())), preferred_element_type=jnp.float32
    )


def contract_last(left, right):
    return lax.dot_general(
        left, right, (((1,), (1,)), ((), ())), preferred_element_type=jnp.float32
    )


def gated_grads(gate_sum, up_sum, grad_hidden):
    sigmoid_gate = jax.nn.sigmoid(gate_sum)
    hidden = (gate_sum * sigmoid_gate * up_sum).astype(jnp.bfloat16)
    grad_up = (grad_hidden * gate_sum * sigmoid_gate).astype(jnp.bfloat16)
    grad_gate = (
        grad_hidden * up_sum * sigmoid_gate * (1.0 + gate_sum * (1.0 - sigmoid_gate))
    ).astype(jnp.bfloat16)
    return (hidden, grad_gate, grad_up)


def body(tokens, grad_out, gate_weight, up_weight, down_weight):
    tok_all, grad_all = (
        lax.all_gather(tokens, "col", axis=0, tiled=True),
        lax.all_gather(grad_out, "col", axis=0, tiled=True),
    )
    gate_sum, up_sum, grad_hidden = (
        lax.psum(
            jnp.dot(tok_all, gate_weight, preferred_element_type=jnp.float32).astype(jnp.bfloat16),
            "row",
        ).astype(jnp.float32),
        lax.psum(
            jnp.dot(tok_all, up_weight, preferred_element_type=jnp.float32).astype(jnp.bfloat16),
            "row",
        ).astype(jnp.float32),
        lax.psum(contract_last(grad_all, down_weight).astype(jnp.bfloat16), "row").astype(
            jnp.float32
        ),
    )
    hidden, grad_gate, grad_up = gated_grads(gate_sum, up_sum, grad_hidden)
    acc_gate = contract_first(tok_all, grad_gate)
    acc_up = contract_first(tok_all, grad_up)
    acc_down = contract_first(hidden, grad_all)
    partial_grad = contract_last(grad_gate, gate_weight) + contract_last(grad_up, up_weight)
    grad_tokens = lax.psum_scatter(
        partial_grad.astype(jnp.bfloat16), "col", scatter_dimension=0, tiled=True
    )
    return (
        grad_tokens,
        acc_gate.astype(jnp.bfloat16),
        acc_up.astype(jnp.bfloat16),
        acc_down.astype(jnp.bfloat16),
    )


def solution(mesh):
    return jax.shard_map(
        body,
        mesh=mesh,
        in_specs=(
            P("col", "row"),
            P("col", "row"),
            P("row", "col"),
            P("row", "col"),
            P("col", "row"),
        ),
        out_specs=(P("col", "row"), P("row", "col"), P("row", "col"), P("col", "row")),
        check_vma=False,
    )
```

profile of v0, /device:TPU:0, one launch (start us, length us, event | category | flops | bytes accessed | tf_op | source)
XLA Modules:
  0.0 188.0 jit_solution(11670191383653160460)
XLA Ops:
  7.2 0.0 all-reduce.3.cloned.1.call-start
  7.2 16.5 %all_gather.7 = bf16[192,1024]{1,0:T(8,128)(2,1)S(1)} all-gather(bf16[48,1024]{1,0:T(8,128)(2,1)} %param.5), channel_id=1, replica_groups=mesh['row'=8,'col'=4] {'col'}, dimensions={0}, use_global_device_ids=true | all-gather | bytes 491520 | tf_op jit(solution)/shard_map/all_gather | solution.py:31
  23.7 15.8 %all_gather.6 = bf16[192,1024]{1,0:T(8,128)(2,1)S(1)} all-gather(bf16[48,1024]{1,0:T(8,128)(2,1)} %param.6), channel_id=1, replica_groups=mesh['row'=8,'col'=4] {'col'}, dimensions={0}, use_global_device_ids=true | all-gather | bytes 491520 | tf_op jit(solution)/shard_map/all_gather | solution.py:32
  39.4 0.0 copy-start.4
  39.4 0.0 slice-start
  39.4 5.9 %convolution_convert_fusion.4 = bf16[192,3584]{1,0:T(8,128)(2,1)} fusion(bf16[192,1024]{1,0:T(8,128)(2,1)S(1)} %all_gather.7, bf16[1024,3584]{1,0:T(8,128)(2,1)} %param.8), kind=kOutput, calls=%fused_computation.6 | convolution fusion | flops 1409974272 | bytes 9109504 | tf_op jit(solution)/shard_map/dot_general | solution.py:40
  45.4 0.0 copy-done.4
  45.4 0.0 slice-start.1
  45.4 2.7 %convolution_convert_fusion.3 = bf16[192,3584]{1,0:T(8,128)(2,1)} fusion(bf16[192,1024]{1,0:T(8,128)(2,1)S(1)} %all_gather.7, bf16[1024,3584]{1,0:T(8,128)(2,1)S(1)} %copy-done.4), kind=kOutput, calls=%fused_computation.5 | convolution fusion | flops 1409974272 | bytes 9109504 | tf_op jit(solution)/shard_map/dot_general | solution.py:36
  48.1 0.0 slice-done
  48.1 0.0 slice-done.1
  48.1 3.6 %convolution_convert_fusion.5 = bf16[192,3584]{1,0:T(8,128)(2,1)} fusion(bf16[192,1024]{1,0:T(8,128)(2,1)S(1)} %all_gather.6, bf16[3584,1024]{1,0:T(8,128)(2,1)S(1)} %bitcast.18), kind=kOutput, calls=%fused_computation.7 | convolution fusion | flops 1409974272 | bytes 9109504 | tf_op jit(solution)/shard_map/dot_general | solution.py:14
  51.7 0.0 all-reduce.3.cloned.1.call-update
  51.7 0.2 reduce-scatter.2.cloned.1.call-start
  51.9 81.2 %all-reduce.3.cloned.1.call-done = (bf16[192,3584]{1,0:T(8,128)(2,1)}, bf16[192,3584]{1,0:T(8,128)(2,1)}, bf16[192,3584]{1,0:T(8,128)(2,1)}) async-done(((bf16[192,3584]{1,0:T(8,128)(2,1)}, bf16[192,3584]{1,0:T(8,128)(2,1)}, bf16[192,3584]{1,0:T(8,128)(2,1)}), (bf16[192,3584]{1,0:T(8,128)(2,1)}, bf16[192,3584]{1,0:T(8,128)(2,1)}, bf16[192,3584]{1,0:T(8,128)(2,1)})) %all-reduce.3.cloned.1.call-update) | async-done | bytes 4128784 | tf_op jit(solution)/shard_map/psum | solution.py:39
  133.2 0.0 copy-start
  133.2 0.0 copy-start.1
  133.2 0.0 copy-start.3
  133.2 7.0 %fusion.1 = bf16[1024,3584]{0,1:T(8,128)(2,1)} fusion(bf16[192,1024]{1,0:T(8,128)(2,1)S(1)} %all_gather.7, bf16[192,3584]{1,0:T(8,128)(2,1)} %get-tuple-element.10, bf16[192,3584]{1,0:T(8,128)(2,1)} %get-tuple-element.9), kind=kOutput, calls=%fused_computation.4 | convolution fusion | flops 1418461184 | bytes 10485760 | tf_op jit(solution)/shard_map/dot_general | solution.py:8
  140.2 0.0 copy-done
  140.2 0.0 copy-done.1
  140.2 0.0 copy-done.3
  140.2 0.0 slice-start.2
  140.3 1.2 fusion.4
  141.5 0.0 slice-start.3
  141.5 5.7 %fusion.18 = f32[192,1024]{1,0:T(8,128)S(1)} fusion(bf16[192,3584]{1,0:T(8,128)(2,1)S(1)} %fusion.4, bf16[1024,3584]{1,0:T(8,128)(2,1)} %param.7), kind=kOutput, calls=%fused_computation.28 | convolution fusion | flops 1409286144 | bytes 9502720 | tf_op jit(solution)/shard_map/dot_general | solution.py:14
  147.2 0.0 slice-done.2
  147.3 0.0 slice-done.3
  147.3 3.4 %fusion.14 = bf16[192,1024]{1,0:T(8,128)(2,1)} fusion(f32[192,1024]{1,0:T(8,128)S(1)} %fusion.18, bf16[1024,3584]{1,0:T(8,128)(2,1)S(1)} %bitcast.20, bf16[192,3584]{1,0:T(8,128)(2,1)S(1)} %copy-done.1, bf16[192,3584]{1,0:T(8,128)(2,1)S(1)} %copy-done.3), kind=kOutput, calls=%fused_computation.26 | convolution fusion | flops 1415184384 | bytes 11272192 | tf_op jit(solution)/shard_map/dot_general | solution.py:14
  150.6 0.0 reduce-scatter.2.cloned.1.call-update
  150.7 5.2 %fusion = bf16[1024,3584]{0,1:T(8,128)(2,1)} fusion(bf16[192,3584]{1,0:T(8,128)(2,1)S(1)} %fusion.4, bf16[192,1024]{1,0:T(8,128)(2,1)S(1)} %all_gather.7), kind=kOutput, calls=%fused_computation.3 | convolution fusion | flops 1412956160 | bytes 9109504 | tf_op jit(solution)/shard_map/dot_general | solution.py:8
  155.8 10.0 %copy.9 = bf16[1024,3584]{1,0:T(8,128)(2,1)} copy(bf16[1024,3584]{0,1:T(8,128)(2,1)} %fusion) | data formatting | bytes 14680064
  165.8 0.0 copy-start.2
  165.8 10.0 %copy.10 = bf16[1024,3584]{1,0:T(8,128)(2,1)} copy(bf16[1024,3584]{0,1:T(8,128)(2,1)} %fusion.1) | data formatting | bytes 14680064
  175.8 0.0 copy-done.2
  175.8 5.3 %convolution_convert_fusion = bf16[3584,1024]{1,0:T(8,128)(2,1)} fusion(bf16[192,1024]{1,0:T(8,128)(2,1)S(1)} %all_gather.6, bf16[192,3584]{1,0:T(8,128)(2,1)S(1)} %copy-done, bf16[192,3584]{1,0:T(8,128)(2,1)S(1)} %copy-done.2), kind=kOutput, calls=%fused_computation | convolution fusion | flops 1418461184 | bytes 10485760 | tf_op jit(solution)/shard_map/dot_general | solution.py:8
  181.1 0.0 reduce-scatter.2.cloned.1.call-done
  (2 shorter events, 0.0 us)
Async XLA Ops:
  7.2 126.0 %all-reduce.3.cloned.1.call-start = ((), (), s32[]{:S(2)}) async-start(), calls=%async_computation.2 | async-start | bytes 8257536 | tf_op jit(solution)/shard_map/psum | solution.py:39
  39.4 5.9 %copy-start.4 = (bf16[1024,3584]{1,0:T(8,128)(2,1)S(1)}, bf16[1024,3584]{1,0:T(8,128)(2,1)}, u32[]{:S(2)}) copy-start(bf16[1024,3584]{1,0:T(8,128)(2,1)} %param.7) | copy-start | bytes 22020100
  39.4 8.6 %slice-start = ((s8[7340032]{0:T(1024)(128)(4,1)}), s8[4194304]{0:T(1024)(128)(4,1)S(1)}, s32[]{:S(2)}) async-start(s8[7340032]{0:T(1024)(128)(4,1)} %bitcast.17), calls=%async_computation.3 | async-start | bytes 8388608
  45.4 2.7 %slice-start.1 = ((s8[7340032]{0:T(1024)(128)(4,1)}), s8[3145728]{0:T(1024)(128)(4,1)S(1)}, s32[]{:S(2)}) async-start(s8[7340032]{0:T(1024)(128)(4,1)} %bitcast.17), calls=%async_computation.4 | async-start | bytes 6291456
  51.7 129.4 %reduce-scatter.2.cloned.1.call-start = ((), (), s32[]{:S(2)}) async-start(), calls=%async_computation.1 | async-start | bytes 491520 | tf_op jit(solution)/shard_map/reduce_scatter | solution.py:52
  133.2 7.1 %copy-start = (bf16[192,3584]{1,0:T(8,128)(2,1)S(1)}, bf16[192,3584]{1,0:T(8,128)(2,1)}, u32[]{:S(2)}) copy-start(bf16[192,3584]{1,0:T(8,128)(2,1)} %get-tuple-element.8) | copy-start | bytes 4128772
  133.2 7.1 %copy-start.1 = (bf16[192,3584]{1,0:T(8,128)(2,1)S(1)}, bf16[192,3584]{1,0:T(8,128)(2,1)}, u32[]{:S(2)}) copy-start(bf16[192,3584]{1,0:T(8,128)(2,1)} %get-tuple-element.10) | copy-start | bytes 4128772
  133.2 7.1 %copy-start.3 = (bf16[192,3584]{1,0:T(8,128)(2,1)S(1)}, bf16[192,3584]{1,0:T(8,128)(2,1)}, u32[]{:S(2)}) copy-start(bf16[192,3584]{1,0:T(8,128)(2,1)} %get-tuple-element.9) | copy-start | bytes 4128772
  140.2 7.0 %slice-start.2 = ((s8[7340032]{0:T(1024)(128)(4,1)}), s8[4194304]{0:T(1024)(128)(4,1)S(1)}, s32[]{:S(2)}) async-start(s8[7340032]{0:T(1024)(128)(4,1)} %bitcast.19), calls=%async_computation.5 | async-start | bytes 8388608
  141.5 5.8 %slice-start.3 = ((s8[7340032]{0:T(1024)(128)(4,1)}), s8[3145728]{0:T(1024)(128)(4,1)S(1)}, s32[]{:S(2)}) async-start(s8[7340032]{0:T(1024)(128)(4,1)} %bitcast.19), calls=%async_computation.6 | async-start | bytes 6291456
  165.8 10.0 %copy-start.2 = (bf16[192,3584]{1,0:T(8,128)(2,1)S(1)}, bf16[192,3584]{1,0:T(8,128)(2,1)}, u32[]{:S(2)}) copy-start(bf16[192,3584]{1,0:T(8,128)(2,1)} %get-tuple-element.10) | copy-start | bytes 4128772
Sparse Core Ops, SparseCore 0:
  51.8 81.3 all-reduce.2
  150.8 20.8 reduce-scatter.1
where the time goes:
time: 189 us; the launch traced here: 188 us
  waiting for transfers between devices  81.3 us (43%)
  matrix products  38.8 us (21%)
  blocking collectives  32.2 us (17%)
  local copies, waits for them, and re-layouts  20.1 us (11%)
  between operations  14.1 us (7%)
    psum x1, waiting for transfers between devices, body(): lax.psum(jnp.dot(tok_all, up_weight, preferred_element_type=jnp.float32)....  81.2 us
    unnamed x20, local copies, waits for them, and re-layouts  20.1 us
    dot_general x3, matrix products, contract_first(): lax.dot_general(left, right, (((0,), (0,)), ((), ())), preferred_element_...  17.5 us
    all_gather x1, blocking collectives, body(): lax.all_gather(tokens, 'col', axis=0, tiled=True)  16.5 us
    all_gather x1, blocking collectives, body(): lax.all_gather(grad_out, 'col', axis=0, tiled=True)  15.8 us
    dot_general x3, matrix products, contract_last(): lax.dot_general(left, right, (((1,), (1,)), ((), ())), preferred_element_...  12.7 us
    dot_general x1, matrix products, body(): jnp.dot(tok_all, up_weight, preferred_element_type=jnp.float32)  5.91 us
  transfers between devices with their start and end apart: 2, of which 1 were waited for; matrix products, arithmetic and copies ran while one was open for 16% of the time, Pallas kernels for 0%

commit v1 on v0

v1 whole, which is shorter than its diff:
```python
import jax
import jax.numpy as jnp
from jax import lax
from jax.sharding import PartitionSpec as P


def contract_first(left, right):
    return lax.dot_general(
        left, right, (((0,), (0,)), ((), ())), preferred_element_type=jnp.float32
    )


def contract_last(left, right):
    return lax.dot_general(
        left, right, (((1,), (1,)), ((), ())), preferred_element_type=jnp.float32
    )


def gated_grads(gate_sum, up_sum, grad_hidden):
    sigmoid_gate = jax.nn.sigmoid(gate_sum)
    hidden = (gate_sum * sigmoid_gate * up_sum).astype(jnp.bfloat16)
    grad_up = (grad_hidden * gate_sum * sigmoid_gate).astype(jnp.bfloat16)
    grad_gate = (
        grad_hidden * up_sum * sigmoid_gate * (1.0 + gate_sum * (1.0 - sigmoid_gate))
    ).astype(jnp.bfloat16)
    return (hidden, grad_gate, grad_up)


def pick_chunks(units, wanted):
    for n in range(wanted, 0, -1):
        if units % n == 0 and (units // n) % 128 == 0:
            return n
    return 1


N_CHUNKS = 2


def body(tokens, grad_out, gate_weight, up_weight, down_weight):
    feat = tokens.shape[1]
    both = jnp.concatenate([tokens, grad_out], axis=1)
    both_all = lax.all_gather(both, "col", axis=0, tiled=True)
    tok_all = both_all[:, :feat]
    grad_all = both_all[:, feat:]
    tok_t = tok_all.T
    units = gate_weight.shape[1]
    n_chunks = pick_chunks(units, N_CHUNKS)
    span = units // n_chunks
    acc_gate, acc_up, acc_down = [], [], []
    partial_grad = None
    prev = None
    for k in range(n_chunks):
        lo = k * span
        gw = gate_weight[:, lo:lo + span]
        uw = up_weight[:, lo:lo + span]
        dw = down_weight[lo:lo + span, :]
        parts = (
            jnp.dot(tok_all, gw, preferred_element_type=jnp.float32).astype(jnp.bfloat16),
            jnp.dot(tok_all, uw, preferred_element_type=jnp.float32).astype(jnp.bfloat16),
            contract_last(grad_all, dw).astype(jnp.bfloat16),
        )
        if prev is not None:
            parts, _ = lax.optimization_barrier((parts, prev))
        sums = lax.psum(parts, "row")
        prev = sums
        gate_sum, up_sum, grad_hidden = (s.astype(jnp.float32) for s in sums)
        hidden, grad_gate, grad_up = gated_grads(gate_sum, up_sum, grad_hidden)
        acc_gate.append(jnp.dot(tok_t, grad_gate, preferred_element_type=jnp.float32).astype(jnp.bfloat16))
        acc_up.append(jnp.dot(tok_t, grad_up, preferred_element_type=jnp.float32).astype(jnp.bfloat16))
        acc_down.append(contract_first(hidden, grad_all).astype(jnp.bfloat16))
        part = contract_last(grad_gate, gw) + contract_last(grad_up, uw)
        partial_grad = part if partial_grad is None else partial_grad + part
    grad_tokens = lax.psum_scatter(
        partial_grad.astype(jnp.bfloat16), "col", scatter_dimension=0, tiled=True
    )
    return (
        grad_tokens,
        jnp.concatenate(acc_gate, axis=1),
        jnp.concatenate(acc_up, axis=1),
        jnp.concatenate(acc_down, axis=0),
    )


def solution(mesh):
    return jax.shard_map(
        body,
        mesh=mesh,
        in_specs=(
            P("col", "row"),
            P("col", "row"),
            P("row", "col"),
            P("row", "col"),
            P("col", "row"),
        ),
        out_specs=(P("col", "row"), P("row", "col"), P("row", "col"), P("col", "row")),
        check_vma=False,
    )
```

time: 189 us -> 215 us (1.14)
  waiting for transfers between devices: 81.3 us -> 106 us
  local copies, waits for them, and re-layouts: 20.1 us -> 0.36 us
  other arithmetic: 1.21 us -> 17.6 us
  matrix products: 38.8 us -> 54.4 us
  blocking collectives: 32.2 us -> 21.4 us
    psum x1 -> x2, waiting for transfers between devices: 81.2 us -> 103 us  [body(): sums = lax.psum(parts, 'row')]
    unnamed x20 -> x28, local copies, waits for them, and re-layouts: 20.1 us -> 0.36 us
    dot_general x2 -> x8, matrix products: 8.61 us -> 28.2 us  [the longest x2 7.96 us: body(): jnp.dot(tok_all, uw, preferred_element_type=jnp.float32)]
    concatenate x0 -> x3, other arithmetic: none -> 17.6 us  [the longest x1 9.45 us: body(): jnp.concatenate(acc_gate, axis=1)]
    all_gather x2 -> x1, blocking collectives: 32.2 us -> 21.4 us  [body(): both_all = lax.all_gather(both, 'col', axis=0, tiled=True)]
    dot_general x3 -> x2, matrix products: 17.5 us -> 7.56 us  [contract_first(): lax.dot_general(left, right, (((0,), (0,)), ((), ())), preferred_element_...]
    dot_general x3 -> x6, matrix products: 12.7 us -> 18.6 us  [contract_last(): lax.dot_general(left, right, (((1,), (1,)), ((), ())), preferred_element_...]
    reduce_scatter x1, waiting for transfers between devices: 0.01 us -> 3.58 us  [body(): lax.psum_scatter(partial_grad.astype(jnp.bfloat16), 'col', scatter_dimens...]
  transfers between devices with their start and end apart: 2 -> 3, of which waited for: 1 -> 3; matrix products, arithmetic and copies ran while one was open for 16% -> 17% of each run, Pallas kernels for 0% -> 0%
where the time goes in v1:
time: 215 us; the launch traced here: 214 us
  waiting for transfers between devices  106 us (49%)
  matrix products  54.4 us (25%)
  blocking collectives  21.4 us (10%)
  other arithmetic  17.6 us (8%)
  between operations  13.8 us (6%)
    psum x2, waiting for transfers between devices, body(): sums = lax.psum(parts, 'row')  103 us
    all_gather x1, blocking collectives, body(): both_all = lax.all_gather(both, 'col', axis=0, tiled=True)  21.4 us
    dot_general x6, matrix products, contract_last(): lax.dot_general(left, right, (((1,), (1,)), ((), ())), preferred_element_...  18.6 us
    concatenate x1, other arithmetic, body(): jnp.concatenate(acc_gate, axis=1)  9.45 us
    dot_general x2, matrix products, body(): jnp.dot(tok_all, uw, preferred_element_type=jnp.float32)  7.96 us
    dot_general x2, matrix products, body(): jnp.dot(tok_all, gw, preferred_element_type=jnp.float32)  7.7 us
    dot_general x2, matrix products, contract_first(): lax.dot_general(left, right, (((0,), (0,)), ((), ())), preferred_element_...  7.56 us
    concatenate x1, other arithmetic, body(): jnp.concatenate(acc_down, axis=0)  7.2 us
  transfers between devices with their start and end apart: 3, of which 3 were waited for; matrix products, arithmetic and copies ran while one was open for 17% of the time, Pallas kernels for 0%

profile of v1, /device:TPU:0, one launch (start us, length us, event | category | flops | bytes accessed | tf_op | source)
XLA Modules:
  0.0 214.4 jit_solution(11317851768424443296)
XLA Ops:
  7.2 0.0 all-reduce.7.cloned.1.call-start
  7.2 1.0 pad_maximum_fusion.3
  8.2 0.0 slice-start
  8.2 21.4 %all_gather.3 = bf16[192,2048]{1,0:T(8,128)(2,1)S(1)} all-gather(bf16[48,2048]{1,0:T(8,128)(2,1)S(1)} %pad_maximum_fusion.3), channel_id=1, replica_groups=mesh['row'=8,'col'=4] {'col'}, dimensions={0}, use_global_device_ids=true | all-gather | bytes 983040 | tf_op jit(solution)/shard_map/all_gather | solution.py:42
  29.6 0.0 slice-start.1
  29.6 3.9 %fusion.23 = bf16[192,1792]{1,0:T(8,128)(2,1)} fusion(bf16[1024,3584]{1,0:T(8,128)(2,1)} %param.7, bf16[192,2048]{1,0:T(8,128)(2,1)S(1)} %all_gather.3), kind=kOutput, calls=%fused_computation.30 | convolution fusion | flops 704987136 | bytes 4751360 | tf_op jit(solution)/shard_map/dot_general | solution.py:58
  33.5 3.8 %fusion.20 = bf16[192,1792]{1,0:T(8,128)(2,1)} fusion(bf16[1024,3584]{1,0:T(8,128)(2,1)} %param.8, bf16[192,2048]{1,0:T(8,128)(2,1)S(1)} %all_gather.3), kind=kOutput, calls=%fused_computation.29 | convolution fusion | flops 704987136 | bytes 4751360 | tf_op jit(solution)/shard_map/dot_general | solution.py:59
  37.3 0.0 slice-done
  37.3 0.0 slice-done.1
  37.3 2.2 %fusion.32 = bf16[192,1792]{1,0:T(8,128)(2,1)} fusion(bf16[3584,1024]{1,0:T(8,128)(2,1)S(1)} %bitcast.1, bf16[192,2048]{1,0:T(8,128)(2,1)S(1)} %all_gather.3), kind=kOutput, calls=%fused_computation.33 | convolution fusion | flops 704987136 | bytes 4751360 | tf_op jit(solution)/shard_map/dot_general | solution.py:14
  39.6 0.0 all-reduce.7.cloned.1.call-update
  39.6 0.0 all-reduce.5.cloned.1.call-start
  39.6 3.8 %fusion.26 = bf16[192,1792]{1,0:T(8,128)(2,1)} fusion(bf16[1024,3584]{1,0:T(8,128)(2,1)} %param.7, bf16[192,2048]{1,0:T(8,128)(2,1)S(1)} %all_gather.3), kind=kOutput, calls=%fused_computation.31 | convolution fusion | flops 704987136 | bytes 4751360 | tf_op jit(solution)/shard_map/dot_general | solution.py:58
  43.4 4.2 %fusion.29 = bf16[192,1792]{1,0:T(8,128)(2,1)} fusion(bf16[1024,3584]{1,0:T(8,128)(2,1)} %param.8, bf16[192,2048]{1,0:T(8,128)(2,1)S(1)} %all_gather.3), kind=kOutput, calls=%fused_computation.32 | convolution fusion | flops 704987136 | bytes 4751360 | tf_op jit(solution)/shard_map/dot_general | solution.py:59
  47.6 4.3 %fusion.35 = bf16[192,1792]{1,0:T(8,128)(2,1)} fusion(bf16[3584,1024]{1,0:T(8,128)(2,1)} %param.9, bf16[192,2048]{1,0:T(8,128)(2,1)S(1)} %all_gather.3), kind=kOutput, calls=%fused_computation.34 | convolution fusion | flops 704987136 | bytes 4751360 | tf_op jit(solution)/shard_map/dot_general | solution.py:14
  51.9 49.2 %all-reduce.7.cloned.1.call-done = (bf16[192,1792]{1,0:T(8,128)(2,1)}, bf16[192,1792]{1,0:T(8,128)(2,1)}, bf16[192,1792]{1,0:T(8,128)(2,1)}) async-done(((bf16[192,1792]{1,0:T(8,128)(2,1)}, bf16[192,1792]{1,0:T(8,128)(2,1)}, bf16[192,1792]{1,0:T(8,128)(2,1)}), (bf16[192,1792]{1,0:T(8,128)(2,1)}, bf16[192,1792]{1,0:T(8,128)(2,1)}, bf16[192,1792]{1,0:T(8,128)(2,1)})) %all-reduce.7.cloned.1.call-update) | async-done | bytes 2064400 | tf_op jit(solution)/shard_map/psum | solution.py:64
  101.1 0.0 copy-start.1
  101.1 0.0 copy-start.2
  101.1 0.0 copy-start.3
  101.1 4.5 %convolution_convert_fusion.1 = bf16[1792,1024]{1,0:T(8,128)(2,1)} fusion(bf16[192,1792]{1,0:T(8,128)(2,1)} %get-tuple-element.14, bf16[192,1792]{1,0:T(8,128)(2,1)} %get-tuple-element.13, bf16[192,2048]{1,0:T(8,128)(2,1)S(1)} %all_gather.3), kind=kOutput, calls=%fused_computation.4 | convolution fusion | flops 709230592 | bytes 5439488 | tf_op jit(solution)/shard_map/dot_general | solution.py:8
  105.6 0.0 copy-done.1
  105.6 0.0 copy-done.2
  105.6 0.0 copy-done.3
  105.6 3.2 %convolution_convert_fusion.5 = bf16[1024,1792]{1,0:T(8,128)(2,1)} fusion(bf16[192,2048]{1,0:T(8,128)(2,1)S(1)} %all_gather.3, bf16[192,1792]{1,0:T(8,128)(2,1)S(1)} %copy-done.3, bf16[192,1792]{1,0:T(8,128)(2,1)S(1)} %copy-done.2, bf16[192,1792]{1,0:T(8,128)(2,1)S(1)} %copy-done.1), kind=kOutput, calls=%fused_computation.8 | convolution fusion | flops 710950912 | bytes 6127616 | tf_op jit(solution)/shard_map/dot_general | solution.py:68
  108.7 0.0 all-reduce.5.cloned.1.call-update
  108.8 0.2 reduce-scatter.2.cloned.1.call-start
  109.0 3.0 %convolution_convert_fusion.3 = bf16[1024,1792]{1,0:T(8,128)(2,1)} fusion(bf16[192,2048]{1,0:T(8,128)(2,1)S(1)} %all_gather.3, bf16[192,1792]{1,0:T(8,128)(2,1)S(1)} %copy-done.1, bf16[192,1792]{1,0:T(8,128)(2,1)S(1)} %copy-done.2), kind=kOutput, calls=%fused_computation.6 | convolution fusion | flops 709230592 | bytes 5439488 | tf_op jit(solution)/shard_map/dot_general | solution.py:69
  112.0 4.6 %fusion.12 = f32[192,1024]{1,0:T(8,128)} fusion(bf16[1024,3584]{1,0:T(8,128)(2,1)} %param.7, bf16[192,1792]{1,0:T(8,128)(2,1)S(1)} %copy-done.3, bf16[192,1792]{1,0:T(8,128)(2,1)S(1)} %copy-done.2, bf16[192,1792]{1,0:T(8,128)(2,1)S(1)} %copy-done.1), kind=kOutput, calls=%fused_computation.21 | convolution fusion | flops 709115904 | bytes 6520832 | tf_op jit(solution)/shard_map/dot_general | solution.py:14
  116.6 53.7 %all-reduce.5.cloned.1.call-done = (bf16[192,1792]{1,0:T(8,128)(2,1)}, bf16[192,1792]{1,0:T(8,128)(2,1)}, bf16[192,1792]{1,0:T(8,128)(2,1)}) async-done(((bf16[192,1792]{1,0:T(8,128)(2,1)}, bf16[192,1792]{1,0:T(8,128)(2,1)}, bf16[192,1792]{1,0:T(8,128)(2,1)}), (bf16[192,1792]{1,0:T(8,128)(2,1)}, bf16[192,1792]{1,0:T(8,128)(2,1)}, bf16[192,1792]{1,0:T(8,128)(2,1)})) %all-reduce.5.cloned.1.call-update) | async-done | bytes 2064400 | tf_op jit(solution)/shard_map/psum | solution.py:64
  170.3 0.0 copy-start.4
  170.3 0.0 copy-start.5
  170.3 3.9 %fusion.4 = f32[192,1024]{1,0:T(8,128)S(1)} fusion(bf16[1024,3584]{1,0:T(8,128)(2,1)} %param.8, bf16[192,1792]{1,0:T(8,128)(2,1)} %get-tuple-element.10, bf16[192,1792]{1,0:T(8,128)(2,1)} %get-tuple-element.11), kind=kOutput, calls=%fused_computation.13 | convolution fusion | flops 707395584 | bytes 5832704 | tf_op jit(solution)/shard_map/dot_general | solution.py:14
  174.2 0.0 copy-done.4
  174.2 0.0 copy-done.5
  174.2 0.0 copy-start.6
  174.2 3.1 %convolution_convert_fusion.2 = bf16[1024,1792]{1,0:T(8,128)(2,1)} fusion(bf16[192,2048]{1,0:T(8,128)(2,1)S(1)} %all_gather.3, bf16[192,1792]{1,0:T(8,128)(2,1)S(1)} %copy-done.4, bf16[192,1792]{1,0:T(8,128)(2,1)S(1)} %copy-done.5), kind=kOutput, calls=%fused_computation.5 | convolution fusion | flops 709230592 | bytes 5439488 | tf_op jit(solution)/shard_map/dot_general | solution.py:69
  177.4 0.0 copy-done.6
  177.4 0.0 slice-start.2
  177.4 0.0 slice-start.4
  177.4 3.2 %convolution_convert_fusion.4 = bf16[1024,1792]{1,0:T(8,128)(2,1)} fusion(bf16[192,2048]{1,0:T(8,128)(2,1)S(1)} %all_gather.3, bf16[192,1792]{1,0:T(8,128)(2,1)S(1)} %copy-done.6, bf16[192,1792]{1,0:T(8,128)(2,1)S(1)} %copy-done.5, bf16[192,1792]{1,0:T(8,128)(2,1)S(1)} %copy-done.4), kind=kOutput, calls=%fused_computation.7 | convolution fusion | flops 710950912 | bytes 6127616 | tf_op jit(solution)/shard_map/dot_general | solution.py:68
  180.6 0.0 slice-start.3
  180.6 0.0 slice-start.5
  180.6 3.1 %convolution_convert_fusion = bf16[1792,1024]{1,0:T(8,128)(2,1)} fusion(bf16[192,1792]{1,0:T(8,128)(2,1)S(1)} %copy-done.6, bf16[192,1792]{1,0:T(8,128)(2,1)S(1)} %copy-done.4, bf16[192,2048]{1,0:T(8,128)(2,1)S(1)} %all_gather.3), kind=kOutput, calls=%fused_computation.3 | convolution fusion | flops 709230592 | bytes 5439488 | tf_op jit(solution)/shard_map/dot_general | solution.py:8
  183.7 0.0 slice-done.2
  183.7 0.0 slice-done.3
  183.7 0.0 copy-start.7
  183.7 1.4 fusion.64
  185.1 0.0 slice-done.4
  185.1 0.3 slice-done.5
  185.4 0.0 copy-done.7
  185.4 2.2 %fusion.67 = bf16[192,1024]{1,0:T(8,128)(2,1)} fusion(f32[192,1024]{1,0:T(8,128)S(1)} %fusion.64, f32[192,1024]{1,0:T(8,128)S(1)} %copy-done.7, bf16[1024,3584]{1,0:T(8,128)(2,1)S(1)} %bitcast.5, bf16[192,1792]{1,0:T(8,128)(2,1)S(1)} %copy-done.1, bf16[192,1792]{1,0:T(8,128)(2,1)S(1)} %copy-done.2), kind=kOutput, calls=%fused_computation.70 | convolution fusion | flops 707985408 | bytes 7012352 | tf_op jit(solution)/shard_map/dot_general | solution.py:14
  187.6 0.0 reduce-scatter.2.cloned.1.call-update
  187.6 0.0 copy-start
  187.6 7.2 %pad_maximum_fusion.2 = bf16[3584,1024]{1,0:T(8,128)(2,1)} fusion(bf16[1792,1024]{1,0:T(8,128)(2,1)} %convolution_convert_fusion, bf16[1792,1024]{1,0:T(8,128)(2,1)} %convolution_convert_fusion.1), kind=kLoop, calls=%fused_computation.2 | loop fusion | flops 14680064 | bytes 14680064 | tf_op jit(solution)/shard_map/concatenate | solution.py:80
  194.8 0.0 copy-done
  194.8 9.4 %pad_maximum_fusion = (bf16[1024,3584]{1,0:T(8,128)(2,1)}, bf16[1024,3584]{1,0:T(8,128)(2,1)}) fusion(bf16[1024,1792]{1,0:T(8,128)(2,1)} %convolution_convert_fusion.4, bf16[1024,1792]{1,0:T(8,128)(2,1)S(1)} %copy-done, bf16[1024,1792]{1,0:T(8,128)(2,1)} %convolution_convert_fusion.2, bf16[1024,1792]{1,0:T(8,128)(2,1)} %convolution_convert_fusion.3), kind=kLoop, calls=%fused_computation | loop fusion | flops 29360128 | bytes 29360128 | tf_op jit(solution)/shard_map/concatenate | solution.py:78
  204.3 3.6 %reduce-scatter.2.cloned.1.call-done = bf16[48,1024]{1,0:T(8,128)(2,1)} async-done(((bf16[192,1024]{1,0:T(8,128)(2,1)}), bf16[48,1024]{1,0:T(8,128)(2,1)}) %reduce-scatter.2.cloned.1.call-update) | async-done | bytes 98320 | tf_op jit(solution)/shard_map/reduce_scatter | solution.py:73
  (3 shorter events, 0.0 us)
Async XLA Ops:
  7.2 94.0 %all-reduce.7.cloned.1.call-start = ((), (), s32[]{:S(2)}) async-start(), calls=%async_computation.3 | async-start | bytes 4128768 | tf_op jit(solution)/shard_map/psum | solution.py:64
  8.2 29.2 %slice-start = ((s8[7340032]{0:T(1024)(128)(4,1)}), s8[4194304]{0:T(1024)(128)(4,1)S(1)}, s32[]{:S(2)}) async-start(s8[7340032]{0:T(1024)(128)(4,1)} %bitcast), calls=%async_computation.4 | async-start | bytes 8388608
  29.6 7.7 %slice-start.1 = ((s8[7340032]{0:T(1024)(128)(4,1)}), s8[3145728]{0:T(1024)(128)(4,1)S(1)}, s32[]{:S(2)}) async-start(s8[7340032]{0:T(1024)(128)(4,1)} %bitcast), calls=%async_computation.5 | async-start | bytes 6291456
  39.6 130.7 %all-reduce.5.cloned.1.call-start = ((), (), s32[]{:S(2)}) async-start(), calls=%async_computation.2 | async-start | bytes 4128768 | tf_op jit(solution)/shard_map/psum | solution.py:64
  101.1 4.5 %copy-start.1 = (bf16[192,1792]{1,0:T(8,128)(2,1)S(1)}, bf16[192,1792]{1,0:T(8,128)(2,1)}, u32[]{:S(2)}) copy-start(bf16[192,1792]{1,0:T(8,128)(2,1)} %get-tuple-element.13) | copy-start | bytes 2064388
  101.1 4.5 %copy-start.2 = (bf16[192,1792]{1,0:T(8,128)(2,1)S(1)}, bf16[192,1792]{1,0:T(8,128)(2,1)}, u32[]{:S(2)}) copy-start(bf16[192,1792]{1,0:T(8,128)(2,1)} %get-tuple-element.15) | copy-start | bytes 2064388
  101.1 4.5 %copy-start.3 = (bf16[192,1792]{1,0:T(8,128)(2,1)S(1)}, bf16[192,1792]{1,0:T(8,128)(2,1)}, u32[]{:S(2)}) copy-start(bf16[192,1792]{1,0:T(8,128)(2,1)} %get-tuple-element.14) | copy-start | bytes 2064388
  108.8 99.1 %reduce-scatter.2.cloned.1.call-start = ((), (), s32[]{:S(2)}) async-start(), calls=%async_computation.1 | async-start | bytes 491520 | tf_op jit(solution)/shard_map/reduce_scatter | solution.py:73
  170.3 3.9 %copy-start.4 = (bf16[192,1792]{1,0:T(8,128)(2,1)S(1)}, bf16[192,1792]{1,0:T(8,128)(2,1)}, u32[]{:S(2)}) copy-start(bf16[192,1792]{1,0:T(8,128)(2,1)} %get-tuple-element.10) | copy-start | bytes 2064388
  170.3 3.9 %copy-start.5 = (bf16[192,1792]{1,0:T(8,128)(2,1)S(1)}, bf16[192,1792]{1,0:T(8,128)(2,1)}, u32[]{:S(2)}) copy-start(bf16[192,1792]{1,0:T(8,128)(2,1)} %get-tuple-element.11) | copy-start | bytes 2064388
  174.2 3.1 %copy-start.6 = (bf16[192,1792]{1,0:T(8,128)(2,1)S(1)}, bf16[192,1792]{1,0:T(8,128)(2,1)}, u32[]{:S(2)}) copy-start(bf16[192,1792]{1,0:T(8,128)(2,1)} %get-tuple-element.12) | copy-start | bytes 2064388
  177.4 6.4 %slice-start.2 = ((s8[7340032]{0:T(1024)(128)(4,1)}), s8[4194304]{0:T(1024)(128)(4,1)S(1)}, s32[]{:S(2)}) async-start(s8[7340032]{0:T(1024)(128)(4,1)} %bitcast.2), calls=%async_computation.6 | async-start | bytes 8388608
  177.4 7.7 %slice-start.4 = ((s8[7340032]{0:T(1024)(128)(4,1)}), s8[4194304]{0:T(1024)(128)(4,1)S(1)}, s32[]{:S(2)}) async-start(s8[7340032]{0:T(1024)(128)(4,1)} %bitcast.4), calls=%async_computation.8 | async-start | bytes 8388608
  180.6 3.1 %slice-start.3 = ((s8[7340032]{0:T(1024)(128)(4,1)}), s8[3145728]{0:T(1024)(128)(4,1)S(1)}, s32[]{:S(2)}) async-start(s8[7340032]{0:T(1024)(128)(4,1)} %bitcast.2), calls=%async_computation.7 | async-start | bytes 6291456
  180.6 4.8 %slice-start.5 = ((s8[7340032]{0:T(1024)(128)(4,1)}), s8[3145728]{0:T(1024)(128)(4,1)S(1)}, s32[]{:S(2)}) async-start(s8[7340032]{0:T(1024)(128)(4,1)} %bitcast.4), calls=%async_computation.9 | async-start | bytes 6291456
  183.7 1.7 copy-start.7
  187.6 7.2 %copy-start = (bf16[1024,1792]{1,0:T(8,128)(2,1)S(1)}, bf16[1024,1792]{1,0:T(8,128)(2,1)}, u32[]{:S(2)}) copy-start(bf16[1024,1792]{1,0:T(8,128)(2,1)} %convolution_convert_fusion.5) | copy-start | bytes 11010052
Sparse Core Ops, SparseCore 0:
  39.7 61.3 all-reduce.6
  108.9 61.3 all-reduce.4
  187.7 20.0 reduce-scatter.1

commit v2 on v0

--- a/solution.py
+++ b/solution.py
@@ -26,27 +26,81 @@
     return (hidden, grad_gate, grad_up)
 
 
+def halving_reduce(parts, order, n_dev):
+    r = lax.axis_index("row")
+    cur = parts
+    for step, bit in enumerate(order):
+        n = cur[0].shape[0] // 2
+        hi = (r // bit) % 2
+        keep = tuple(lax.dynamic_slice_in_dim(c, hi * n, n, 0) for c in cur)
+        send = tuple(lax.dynamic_slice_in_dim(c, (1 - hi) * n, n, 0) for c in cur)
+        got = lax.ppermute(send, "row", [(j, j ^ bit) for j in range(n_dev)])
+        summed = tuple(k.astype(jnp.float32) + g.astype(jnp.float32) for k, g in zip(keep, got))
+        if step + 1 < len(order):
+            summed = tuple(s.astype(jnp.bfloat16) for s in summed)
+        cur = summed
+    return cur
+
+
+def doubling_gather(parts, order, n_dev):
+    r = lax.axis_index("row")
+    cur = parts
+    for bit in reversed(order):
+        n = cur[0].shape[0]
+        hi = (r // bit) % 2
+        got = lax.ppermute(cur, "row", [(j, j ^ bit) for j in range(n_dev)])
+        nxt = []
+        for c, g in zip(cur, got):
+            out = jnp.zeros((2 * n,) + c.shape[1:], c.dtype)
+            out = lax.dynamic_update_slice_in_dim(out, c, hi * n, 0)
+            out = lax.dynamic_update_slice_in_dim(out, g, (1 - hi) * n, 0)
+            nxt.append(out)
+        cur = tuple(nxt)
+    return cur
+
+
+def row_bits(n_dev, tokens, units):
+    if n_dev < 2 or n_dev & (n_dev - 1) or tokens % n_dev or units % 2:
+        return None
+    bits, b = [], 1
+    while b < n_dev:
+        bits.append(b)
+        b *= 2
+    return bits
+
+
+def row_gated(gate_p, up_p, gh_p, n_dev):
+    tokens, units = gate_p.shape
+    bits = row_bits(n_dev, tokens, units)
+    if bits is None:
+        sums = lax.psum((gate_p, up_p, gh_p), "row")
+        return gated_grads(*(s.astype(jnp.float32) for s in sums))
+    orders = (bits, bits[:1] + bits[:0:-1])
+    half = units // 2
+    reduced = []
+    for h, order in enumerate(orders):
+        cols = tuple(a[:, h * half:(h + 1) * half] for a in (gate_p, up_p, gh_p))
+        reduced.append(halving_reduce(cols, order, n_dev))
+    outs = []
+    for h, order in enumerate(orders):
+        outs.append(doubling_gather(gated_grads(*reduced[h]), order, n_dev))
+    return tuple(jnp.concatenate([outs[0][i], outs[1][i]], axis=1) for i in range(3))
+
+
 def body(tokens, grad_out, gate_weight, up_weight, down_weight):
-    tok_all, grad_all = (
-        lax.all_gather(tokens, "col", axis=0, tiled=True),
-        lax.all_gather(grad_out, "col", axis=0, tiled=True),
-    )
-    gate_sum, up_sum, grad_hidden = (
-        lax.psum(
-            jnp.dot(tok_all, gate_weight, preferred_element_type=jnp.float32).astype(jnp.bfloat16),
-            "row",
-        ).astype(jnp.float32),
-        lax.psum(
-            jnp.dot(tok_all, up_weight, preferred_element_type=jnp.float32).astype(jnp.bfloat16),
-            "row",
-        ).astype(jnp.float32),
-        lax.psum(contract_last(grad_all, down_weight).astype(jnp.bfloat16), "row").astype(
-            jnp.float32
-        ),
-    )
-    hidden, grad_gate, grad_up = gated_grads(gate_sum, up_sum, grad_hidden)
-    acc_gate = contract_first(tok_all, grad_gate)
-    acc_up = contract_first(tok_all, grad_up)
+    n_row = lax.psum(1, "row")
+    feat = tokens.shape[1]
+    both = jnp.concatenate([tokens, grad_out], axis=1)
+    both_all = lax.all_gather(both, "col", axis=0, tiled=True)
+    tok_all = both_all[:, :feat]
+    grad_all = both_all[:, feat:]
+    tok_t = tok_all.T
+    gate_p = jnp.dot(tok_all, gate_weight, preferred_element_type=jnp.float32).astype(jnp.bfloat16)
+    up_p = jnp.dot(tok_all, up_weight, preferred_element_type=jnp.float32).astype(jnp.bfloat16)
+    gh_p = contract_last(grad_all, down_weight).astype(jnp.bfloat16)
+    hidden, grad_gate, grad_up = row_gated(gate_p, up_p, gh_p, n_row)
+    acc_gate = jnp.dot(tok_t, grad_gate, preferred_element_type=jnp.float32)
+    acc_up = jnp.dot(tok_t, grad_up, preferred_element_type=jnp.float32)
     acc_down = contract_first(hidden, grad_all)
     partial_grad = contract_last(grad_gate, gate_weight) + contract_last(grad_up, up_weight)
     grad_tokens = lax.psum_scatter(

time: 189 us -> 128 us (0.68)
  waiting for transfers between devices: 81.3 us -> 4.42 us
  starting transfers between devices: 0.26 us -> 30.5 us
  blocking collectives: 32.2 us -> 21.3 us
  other arithmetic: 1.21 us -> 7.34 us
  local copies, waits for them, and re-layouts: 20.1 us -> 15 us
  matrix products: 38.8 us -> 34.1 us
    psum x1 -> x0, waiting for transfers between devices: 81.2 us -> none  [body(): lax.psum(jnp.dot(tok_all, up_weight, preferred_element_type=jnp.float32)....]
    ppermute x0 -> x36, starting transfers between devices: none -> 30.5 us  [the longest x18 15.8 us: halving_reduce(): got = lax.ppermute(send, 'row', [(j, j ^ bit) for j in range(n_dev)])]
    unnamed x20 -> x26, local copies, waits for them, and re-layouts: 20.1 us -> 0.43 us
    dot_general x3 -> x1, matrix products: 17.5 us -> 5.17 us  [contract_first(): lax.dot_general(left, right, (((0,), (0,)), ((), ())), preferred_element_...]
    all_gather x2 -> x1, blocking collectives: 32.2 us -> 21.3 us  [body(): both_all = lax.all_gather(both, 'col', axis=0, tiled=True)]
    dot_general x0 -> x2, matrix products: none -> 10.3 us  [the longest x1 5.17 us: body(): acc_gate = jnp.dot(tok_t, grad_gate, preferred_element_type=jnp.float32)]
    dynamic_update_slice x0 -> x30, local copies, waits for them, and re-layouts: none -> 8.09 us  [the longest x18 4.5 us: doubling_gather(): out = lax.dynamic_update_slice_in_dim(out, g, (1 - hi) * n, 0)]
    convert_element_type x1 -> x12, other arithmetic: 1.21 us -> 5.76 us  [halving_reduce(): summed = tuple((s.astype(jnp.bfloat16) for s in summed))]
  transfers between devices with their start and end apart: 2 -> 37, of which waited for: 1 -> 6; matrix products, arithmetic and copies ran while one was open for 16% -> 39% of each run, Pallas kernels for 0% -> 0%
where the time goes in v2:
time: 128 us; the launch traced here: 127 us
  matrix products  34.1 us (27%)
  starting transfers between devices  30.5 us (24%)
  blocking collectives  21.3 us (17%)
  local copies, waits for them, and re-layouts  15 us (12%)
  between operations  14.8 us (12%)
  other arithmetic  7.34 us (6%)
  waiting for transfers between devices  4.42 us (3%)
    all_gather x1, blocking collectives, body(): both_all = lax.all_gather(both, 'col', axis=0, tiled=True)  21.3 us
    ppermute x18, starting transfers between devices, halving_reduce(): got = lax.ppermute(send, 'row', [(j, j ^ bit) for j in range(n_dev)])  15.8 us
    ppermute x18, starting transfers between devices, doubling_gather(): got = lax.ppermute(cur, 'row', [(j, j ^ bit) for j in range(n_dev)])  14.6 us
    dot_general x3, matrix products, contract_last(): lax.dot_general(left, right, (((1,), (1,)), ((), ())), preferred_element_...  8.51 us
    convert_element_type x12, other arithmetic, halving_reduce(): summed = tuple((s.astype(jnp.bfloat16) for s in summed))  5.76 us
    dot_general x1, matrix products, body(): jnp.dot(tok_all, up_weight, preferred_element_type=jnp.float32)  5.4 us
    dot_general x1, matrix products, contract_first(): lax.dot_general(left, right, (((0,), (0,)), ((), ())), preferred_element_...  5.17 us
    dot_general x1, matrix products, body(): acc_gate = jnp.dot(tok_t, grad_gate, preferred_element_type=jnp.float32)  5.17 us
  transfers between devices with their start and end apart: 37, of which 6 were waited for; matrix products, arithmetic and copies ran while one was open for 39% of the time, Pallas kernels for 0%

profile of v2, /device:TPU:0, one launch (start us, length us, event | category | flops | bytes accessed | tf_op | source)
XLA Modules:
  0.0 127.5 jit_solution(8418239300360467956)
XLA Ops:
  7.2 1.0 pad_maximum_fusion.6
  8.2 21.3 %all_gather.3 = bf16[192,2048]{1,0:T(8,128)(2,1)S(1)} all-gather(bf16[48,2048]{1,0:T(8,128)(2,1)S(1)} %pad_maximum_fusion.6), channel_id=1, replica_groups=mesh['row'=8,'col'=4] {'col'}, dimensions={0}, use_global_device_ids=true | all-gather | bytes 983040 | tf_op jit(solution)/shard_map/all_gather | solution.py:94
  29.5 4.7 %convolution_convert_fusion.3 = bf16[192,3584]{1,0:T(8,128)(2,1)S(1)} fusion(bf16[1024,3584]{1,0:T(8,128)(2,1)} %param.7, bf16[192,2048]{1,0:T(8,128)(2,1)S(1)} %all_gather.3), kind=kOutput, calls=%fused_computation.3 | convolution fusion | flops 1409974272 | bytes 9109504 | tf_op jit(solution)/shard_map/dot_general | solution.py:98
  34.3 0.8 constant_dynamic-slice_fusion.2
  35.1 0.8 constant_dynamic-slice_fusion.11
  35.9 0.5 collective-permute-start.6
  36.4 5.4 %convolution_convert_fusion.4 = bf16[192,3584]{1,0:T(8,128)(2,1)S(1)} fusion(bf16[1024,3584]{1,0:T(8,128)(2,1)} %param.8, bf16[192,2048]{1,0:T(8,128)(2,1)S(1)} %all_gather.3), kind=kOutput, calls=%fused_computation.4 | convolution fusion | flops 1409974272 | bytes 9109504 | tf_op jit(solution)/shard_map/dot_general | solution.py:99
  41.9 0.8 constant_dynamic-slice_fusion.5
  42.8 0.8 constant_dynamic-slice_fusion.14
  43.5 0.5 collective-permute-start.3
  44.0 2.6 %convolution_convert_fusion.5 = bf16[192,3584]{1,0:T(8,128)(2,1)S(1)} fusion(bf16[3584,1024]{1,0:T(8,128)(2,1)S(1)} %bitcast.6, bf16[192,2048]{1,0:T(8,128)(2,1)S(1)} %all_gather.3), kind=kOutput, calls=%fused_computation.5 | convolution fusion | flops 1409974272 | bytes 9109504 | tf_op jit(solution)/shard_map/dot_general | solution.py:14
  46.7 0.8 constant_dynamic-slice_fusion.8
  47.5 0.6 collective-permute-start
  48.1 1.2 add_convert_fusion
  49.3 1.6 %collective-permute-start.19 = (bf16[48,1792]{1,0:T(8,128)(2,1)S(1)}, bf16[48,1792]{1,0:T(8,128)(2,1)S(1)}, u32[]{:S(2)}, u32[]{:S(2)}) collective-permute-start(bf16[48,1792]{1,0:T(8,128)(2,1)S(1)} %constant_dynamic-slice_fusion.1), channel_id=1, source_target_pairs={{0,16},{4,20},{8,24},{12,28},{16,0},{20,4},{24,8},{28,12},{1,17},{... | collective-permute-start | bytes 516104 | tf_op jit(solution)/shard_map/ppermute | solution.py:37
  50.9 1.1 add_convert_fusion.3
  52.0 1.6 %collective-permute-start.7 = (bf16[48,1792]{1,0:T(8,128)(2,1)S(1)}, bf16[48,1792]{1,0:T(8,128)(2,1)S(1)}, u32[]{:S(2)}, u32[]{:S(2)}) collective-permute-start(bf16[48,1792]{1,0:T(8,128)(2,1)S(1)} %constant_dynamic-slice_fusion.10), channel_id=1, source_target_pairs={{0,8},{4,12},{8,0},{12,4},{16,24},{20,28},{24,16},{28,20},{1,9},{5... | collective-permute-start | bytes 516104 | tf_op jit(solution)/shard_map/ppermute | solution.py:37
  53.5 1.1 add_convert_fusion.1
  54.7 0.6 collective-permute-start.16
  55.2 1.1 add_convert_fusion.4
  56.3 0.6 collective-permute-start.4
  56.9 1.1 add_convert_fusion.2
  58.0 1.6 %collective-permute-start.13 = (bf16[48,1792]{1,0:T(8,128)(2,1)S(1)}, bf16[48,1792]{1,0:T(8,128)(2,1)S(1)}, u32[]{:S(2)}, u32[]{:S(2)}) collective-permute-start(bf16[48,1792]{1,0:T(8,128)(2,1)S(1)} %constant_dynamic-slice_fusion.7), channel_id=1, source_target_pairs={{0,16},{4,20},{8,24},{12,28},{16,0},{20,4},{24,8},{28,12},{1,17},{... | collective-permute-start | bytes 516104 | tf_op jit(solution)/shard_map/ppermute | solution.py:37
  59.7 1.6 %collective-permute-start.1 = (bf16[48,1792]{1,0:T(8,128)(2,1)S(1)}, bf16[48,1792]{1,0:T(8,128)(2,1)S(1)}, u32[]{:S(2)}, u32[]{:S(2)}) collective-permute-start(bf16[48,1792]{1,0:T(8,128)(2,1)S(1)} %constant_dynamic-slice_fusion.16), channel_id=1, source_target_pairs={{0,8},{4,12},{8,0},{12,4},{16,24},{20,28},{24,16},{28,20},{1,9},{5... | collective-permute-start | bytes 516104 | tf_op jit(solution)/shard_map/ppermute | solution.py:37
  61.4 0.6 collective-permute-start.20
  62.1 0.6 collective-permute-start.8
  62.7 1.5 %collective-permute-start.17 = (bf16[24,1792]{1,0:T(8,128)(2,1)S(1)}, bf16[24,1792]{1,0:T(8,128)(2,1)S(1)}, u32[]{:S(2)}, u32[]{:S(2)}) collective-permute-start(bf16[24,1792]{1,0:T(8,128)(2,1)S(1)} %constant_dynamic-slice_fusion.3), channel_id=1, source_target_pairs={{0,8},{4,12},{8,0},{12,4},{16,24},{20,28},{24,16},{28,20},{1,9},{5... | collective-permute-start | bytes 258056 | tf_op jit(solution)/shard_map/ppermute | solution.py:37
  64.4 0.8 collective-permute-done.13
  65.1 0.8 collective-permute-start.5
  66.0 1.0 collective-permute-done.1
  67.1 1.5 %collective-permute-start.14 = (bf16[24,1792]{1,0:T(8,128)(2,1)S(1)}, bf16[24,1792]{1,0:T(8,128)(2,1)S(1)}, u32[]{:S(2)}, u32[]{:S(2)}) collective-permute-start(bf16[24,1792]{1,0:T(8,128)(2,1)S(1)} %constant_dynamic-slice_fusion.6), channel_id=1, source_target_pairs={{0,8},{4,12},{8,0},{12,4},{16,24},{20,28},{24,16},{28,20},{1,9},{5... | collective-permute-start | bytes 258056 | tf_op jit(solution)/shard_map/ppermute | solution.py:37
  68.9 1.8 %collective-permute-start.2 = (bf16[24,1792]{1,0:T(8,128)(2,1)S(1)}, bf16[24,1792]{1,0:T(8,128)(2,1)S(1)}, u32[]{:S(2)}, u32[]{:S(2)}) collective-permute-start(bf16[24,1792]{1,0:T(8,128)(2,1)S(1)} %constant_dynamic-slice_fusion.15), channel_id=1, source_target_pairs={{0,16},{4,20},{8,24},{12,28},{16,0},{20,4},{24,8},{28,12},{1,17},{... | collective-permute-start | bytes 258056 | tf_op jit(solution)/shard_map/ppermute | solution.py:37
  70.8 1.0 collective-permute-start.33
  71.9 0.9 collective-permute-start.30
  72.9 1.4 %collective-permute-start.21 = (bf16[24,1792]{1,0:T(8,128)(2,1)S(1)}, bf16[24,1792]{1,0:T(8,128)(2,1)S(1)}, u32[]{:S(2)}, u32[]{:S(2)}) collective-permute-start(bf16[24,1792]{1,0:T(8,128)(2,1)S(1)} %get-tuple-element.11), channel_id=1, source_target_pairs={{0,8},{4,12},{8,0},{12,4},{16,24},{20,28},{24,16},{28,20},{1,9},{5... | collective-permute-start | bytes 258056 | tf_op jit(solution)/shard_map/ppermute | solution.py:51
  74.5 0.8 collective-permute-start.27
  75.4 1.3 collective-permute-start.9
  76.8 0.9 collective-permute-start.24
  77.7 0.8 broadcast.19.clone.4
  78.4 0.7 constant_dynamic-update-slice_fusion.3
  79.1 1.2 collective-permute-start.34
  80.3 0.8 broadcast.19.clone.5
  81.1 0.7 constant_dynamic-update-slice_fusion.9
  81.8 1.1 collective-permute-start.31
  83.0 1.1 collective-permute-start.28
  84.2 1.1 collective-permute-start.22
  85.3 1.0 collective-permute-start.25
  86.4 1.3 %collective-permute-start.10 = (bf16[48,1792]{1,0:T(8,128)(2,1)S(1)}, bf16[48,1792]{1,0:T(8,128)(2,1)S(1)}, u32[]{:S(2)}, u32[]{:S(2)}) collective-permute-start(bf16[48,1792]{1,0:T(8,128)(2,1)S(1)} %constant_dynamic-update-slice_fusion.34), channel_id=1, source_target_pairs={{0,8},{4,12},{8,0},{12,4},{16,24},{20,28},{24,16},{28,20},{1,9},{5... | collective-permute-start | bytes 516104 | tf_op jit(solution)/shard_map/ppermute | solution.py:51
  87.7 0.7 constant_dynamic-update-slice_fusion.2
  88.4 1.0 constant_dynamic-update-slice_fusion.1
  89.5 0.8 constant_dynamic-update-slice_fusion.8
  90.4 1.0 constant_dynamic-update-slice_fusion.7
  91.5 0.4 collective-permute-start.32
  92.4 0.4 collective-permute-start.29
  93.3 1.1 collective-permute-done.29
  94.9 2.5 %fusion.4 = f32[192,1024]{1,0:T(8,128)S(1)} fusion(bf16[1024,3584]{1,0:T(8,128)(2,1)S(1)} %bitcast.8, bf16[192,1792]{1,0:T(8,128)(2,1)S(1)} %constant_dynamic-update-slice_fusion.12, bf16[192,1792]{1,0:T(8,128)(2,1)S(1)} %constant_dynamic-update-slice_fusion.18), kind=kOutput, calls=%fused_computation.13 | convolution fusion | flops 1412038656 | bytes 9502720 | tf_op jit(solution)/shard_map/dot_general | solution.py:14
  97.6 0.4 slice-done.5
  97.9 3.5 %fusion.3 = bf16[192,1024]{1,0:T(8,128)(2,1)} fusion(f32[192,1024]{1,0:T(8,128)S(1)} %fusion.4, bf16[1024,3584]{1,0:T(8,128)(2,1)S(1)} %bitcast.10, bf16[192,1792]{1,0:T(8,128)(2,1)S(1)} %constant_dynamic-update-slice_fusion.24, bf16[192,1792]{1,0:T(8,128)(2,1)S(1)} %constant_dynamic-update-slice_fusion.30), kind=kOutput, calls=%fused_computation.12 | convolution fusion | flops 1412431872 | bytes 9895936 | tf_op jit(solution)/shard_map/dot_general | solution.py:14
  101.4 1.7 %constant_dynamic-update-slice_fusion = bf16[192,1792]{1,0:T(8,128)(2,1)} fusion(bf16[192,1792]{1,0:T(8,128)(2,1)} %copy-done.3, bf16[96,1792]{1,0:T(8,128)(2,1)} %collective-permute-done.35, s32[]{:T(128)S(6)} %select_n.72), kind=kLoop, calls=%fused_computation.47 | loop fusion | bytes 688132 | tf_op jit(solution)/shard_map/dynamic_update_slice | solution.py:56
  103.2 5.2 %convolution_convert_fusion.2 = bf16[1024,3584]{1,0:T(8,128)(2,1)} fusion(bf16[192,1792]{1,0:T(8,128)(2,1)S(1)} %constant_dynamic-update-slice_fusion.24, bf16[192,1792]{1,0:T(8,128)(2,1)S(1)} %constant_dynamic-update-slice_fusion.30, bf16[192,2048]{1,0:T(8,128)(2,1)S(1)} %all_gather.3), kind=kOutput, calls=%fused_computation.2 | convolution fusion | flops 1415708672 | bytes 9109504 | tf_op jit(solution)/shard_map/dot_general | solution.py:102
  108.3 1.0 constant_dynamic-update-slice_fusion.6
  109.3 5.2 %convolution_convert_fusion.1 = bf16[1024,3584]{1,0:T(8,128)(2,1)} fusion(bf16[192,1792]{1,0:T(8,128)(2,1)S(1)} %constant_dynamic-update-slice_fusion.12, bf16[192,1792]{1,0:T(8,128)(2,1)S(1)} %constant_dynamic-update-slice_fusion.18, bf16[192,2048]{1,0:T(8,128)(2,1)S(1)} %all_gather.3), kind=kOutput, calls=%fused_computation.1 | convolution fusion | flops 1415708672 | bytes 9109504 | tf_op jit(solution)/shard_map/dot_general | solution.py:103
  114.5 5.2 %convolution_convert_fusion = bf16[3584,1024]{1,0:T(8,128)(2,1)} fusion(bf16[192,1792]{1,0:T(8,128)(2,1)S(1)} %copy-done.4, bf16[192,1792]{1,0:T(8,128)(2,1)S(1)} %constant_dynamic-update-slice_fusion.6, bf16[192,2048]{1,0:T(8,128)(2,1)S(1)} %all_gather.3), kind=kOutput, calls=%fused_computation | convolution fusion | flops 1415708672 | bytes 9109504 | tf_op jit(solution)/shard_map/dot_general | solution.py:8
  119.7 0.9 reduce-scatter.2.cloned.1.call-done
  (137 shorter events, 4.0 us)
Async XLA Ops:
  7.2 113.4 %reduce-scatter.2.cloned.1.call-start = ((), (), s32[]{:S(2)}) async-start(), calls=%async_computation.1 | async-start | bytes 491520 | tf_op jit(solution)/shard_map/reduce_scatter | solution.py:106
  34.3 2.1 %copy-start.2 = (bf16[192,1792]{1,0:T(8,128)(2,1)}, bf16[192,1792]{1,0:T(8,128)(2,1)S(1)}, u32[]{:S(2)}) copy-start(bf16[192,1792]{1,0:T(8,128)(2,1)S(1)} %get-tuple-element.21) | copy-start | bytes 2064388
  35.1 12.4 %collective-permute-start.18 = (bf16[96,1792]{1,0:T(8,128)(2,1)}, bf16[96,1792]{1,0:T(8,128)(2,1)}, u32[]{:S(2)}, u32[]{:S(2)}) collective-permute-start(bf16[96,1792]{1,0:T(8,128)(2,1)} %constant_dynamic-slice_fusion.2), channel_id=1, source_target_pairs={{0,4},{4,0},{8,12},{12,8},{16,20},{20,16},{24,28},{28,24},{1,5},{5... | collective-permute-start | bytes 1032200 | tf_op jit(solution)/shard_map/ppermute | solution.py:37
  35.1 8.9 %slice-start = ((s8[7340032]{0:T(1024)(128)(4,1)}), s8[4194304]{0:T(1024)(128)(4,1)S(1)}, s32[]{:S(2)}) async-start(s8[7340032]{0:T(1024)(128)(4,1)} %bitcast.5), calls=%async_computation.2 | async-start | bytes 8388608
  35.9 8.1 %slice-start.1 = ((s8[7340032]{0:T(1024)(128)(4,1)}), s8[3145728]{0:T(1024)(128)(4,1)S(1)}, s32[]{:S(2)}) async-start(s8[7340032]{0:T(1024)(128)(4,1)} %bitcast.5), calls=%async_computation.3 | async-start | bytes 6291456
  35.9 13.4 %collective-permute-start.6 = (bf16[96,1792]{1,0:T(8,128)(2,1)}, bf16[96,1792]{1,0:T(8,128)(2,1)}, u32[]{:S(2)}, u32[]{:S(2)}) collective-permute-start(bf16[96,1792]{1,0:T(8,128)(2,1)} %constant_dynamic-slice_fusion.11), channel_id=1, source_target_pairs={{0,4},{4,0},{8,12},{12,8},{16,20},{20,16},{24,28},{28,24},{1,5},{5... | collective-permute-start | bytes 1032200 | tf_op jit(solution)/shard_map/ppermute | solution.py:37
  41.9 2.1 %copy-start = (bf16[192,1792]{1,0:T(8,128)(2,1)}, bf16[192,1792]{1,0:T(8,128)(2,1)S(1)}, u32[]{:S(2)}) copy-start(bf16[192,1792]{1,0:T(8,128)(2,1)S(1)} %get-tuple-element.17) | copy-start | bytes 2064388
  42.8 9.2 %collective-permute-start.15 = (bf16[96,1792]{1,0:T(8,128)(2,1)}, bf16[96,1792]{1,0:T(8,128)(2,1)}, u32[]{:S(2)}, u32[]{:S(2)}) collective-permute-start(bf16[96,1792]{1,0:T(8,128)(2,1)} %constant_dynamic-slice_fusion.5), channel_id=1, source_target_pairs={{0,4},{4,0},{8,12},{12,8},{16,20},{20,16},{24,28},{28,24},{1,5},{5... | collective-permute-start | bytes 1032200 | tf_op jit(solution)/shard_map/ppermute | solution.py:37
  43.5 11.1 %collective-permute-start.3 = (bf16[96,1792]{1,0:T(8,128)(2,1)}, bf16[96,1792]{1,0:T(8,128)(2,1)}, u32[]{:S(2)}, u32[]{:S(2)}) collective-permute-start(bf16[96,1792]{1,0:T(8,128)(2,1)} %constant_dynamic-slice_fusion.14), channel_id=1, source_target_pairs={{0,4},{4,0},{8,12},{12,8},{16,20},{20,16},{24,28},{28,24},{1,5},{5... | collective-permute-start | bytes 1032200 | tf_op jit(solution)/shard_map/ppermute | solution.py:37
  47.5 8.9 %collective-permute-start.12 = (bf16[96,1792]{1,0:T(8,128)(2,1)}, bf16[96,1792]{1,0:T(8,128)(2,1)}, u32[]{:S(2)}, u32[]{:S(2)}) collective-permute-start(bf16[96,1792]{1,0:T(8,128)(2,1)} %constant_dynamic-slice_fusion.8), channel_id=1, source_target_pairs={{0,4},{4,0},{8,12},{12,8},{16,20},{20,16},{24,28},{28,24},{1,5},{5... | collective-permute-start | bytes 1032200 | tf_op jit(solution)/shard_map/ppermute | solution.py:37
  47.5 6.1 %copy-start.1 = (bf16[192,1792]{1,0:T(8,128)(2,1)S(1)}, bf16[192,1792]{1,0:T(8,128)(2,1)}, u32[]{:S(2)}) copy-start(bf16[192,1792]{1,0:T(8,128)(2,1)} %copy-done) | copy-start | bytes 2064388
  47.5 10.5 %collective-permute-start = (bf16[96,1792]{1,0:T(8,128)(2,1)S(1)}, bf16[96,1792]{1,0:T(8,128)(2,1)S(1)}, u32[]{:S(2)}, u32[]{:S(2)}) collective-permute-start(bf16[96,1792]{1,0:T(8,128)(2,1)S(1)} %constant_dynamic-slice_fusion.17), channel_id=1, source_target_pairs={{0,4},{4,0},{8,12},{12,8},{16,20},{20,16},{24,28},{28,24},{1,5},{5... | collective-permute-start | bytes 1032200 | tf_op jit(solution)/shard_map/ppermute | solution.py:37
  49.3 10.4 %collective-permute-start.19 = (bf16[48,1792]{1,0:T(8,128)(2,1)S(1)}, bf16[48,1792]{1,0:T(8,128)(2,1)S(1)}, u32[]{:S(2)}, u32[]{:S(2)}) collective-permute-start(bf16[48,1792]{1,0:T(8,128)(2,1)S(1)} %constant_dynamic-slice_fusion.1), channel_id=1, source_target_pairs={{0,16},{4,20},{8,24},{12,28},{16,0},{20,4},{24,8},{28,12},{1,17},{... | collective-permute-start | bytes 516104 | tf_op jit(solution)/shard_map/ppermute | solution.py:37
  52.0 9.4 %collective-permute-start.7 = (bf16[48,1792]{1,0:T(8,128)(2,1)S(1)}, bf16[48,1792]{1,0:T(8,128)(2,1)S(1)}, u32[]{:S(2)}, u32[]{:S(2)}) collective-permute-start(bf16[48,1792]{1,0:T(8,128)(2,1)S(1)} %constant_dynamic-slice_fusion.10), channel_id=1, source_target_pairs={{0,8},{4,12},{8,0},{12,4},{16,24},{20,28},{24,16},{28,20},{1,9},{5... | collective-permute-start | bytes 516104 | tf_op jit(solution)/shard_map/ppermute | solution.py:37
  54.7 7.4 %collective-permute-start.16 = (bf16[48,1792]{1,0:T(8,128)(2,1)S(1)}, bf16[48,1792]{1,0:T(8,128)(2,1)S(1)}, u32[]{:S(2)}, u32[]{:S(2)}) collective-permute-start(bf16[48,1792]{1,0:T(8,128)(2,1)S(1)} %constant_dynamic-slice_fusion.4), channel_id=1, source_target_pairs={{0,16},{4,20},{8,24},{12,28},{16,0},{20,4},{24,8},{28,12},{1,17},{... | collective-permute-start | bytes 516104 | tf_op jit(solution)/shard_map/ppermute | solution.py:37
  56.3 6.4 %collective-permute-start.4 = (bf16[48,1792]{1,0:T(8,128)(2,1)S(1)}, bf16[48,1792]{1,0:T(8,128)(2,1)S(1)}, u32[]{:S(2)}, u32[]{:S(2)}) collective-permute-start(bf16[48,1792]{1,0:T(8,128)(2,1)S(1)} %constant_dynamic-slice_fusion.13), channel_id=1, source_target_pairs={{0,8},{4,12},{8,0},{12,4},{16,24},{20,28},{24,16},{28,20},{1,9},{5... | collective-permute-start | bytes 516104 | tf_op jit(solution)/shard_map/ppermute | solution.py:37
  58.0 7.1 %collective-permute-start.13 = (bf16[48,1792]{1,0:T(8,128)(2,1)S(1)}, bf16[48,1792]{1,0:T(8,128)(2,1)S(1)}, u32[]{:S(2)}, u32[]{:S(2)}) collective-permute-start(bf16[48,1792]{1,0:T(8,128)(2,1)S(1)} %constant_dynamic-slice_fusion.7), channel_id=1, source_target_pairs={{0,16},{4,20},{8,24},{12,28},{16,0},{20,4},{24,8},{28,12},{1,17},{... | collective-permute-start | bytes 516104 | tf_op jit(solution)/shard_map/ppermute | solution.py:37
  59.7 7.3 %collective-permute-start.1 = (bf16[48,1792]{1,0:T(8,128)(2,1)S(1)}, bf16[48,1792]{1,0:T(8,128)(2,1)S(1)}, u32[]{:S(2)}, u32[]{:S(2)}) collective-permute-start(bf16[48,1792]{1,0:T(8,128)(2,1)S(1)} %constant_dynamic-slice_fusion.16), channel_id=1, source_target_pairs={{0,8},{4,12},{8,0},{12,4},{16,24},{20,28},{24,16},{28,20},{1,9},{5... | collective-permute-start | bytes 516104 | tf_op jit(solution)/shard_map/ppermute | solution.py:37
  61.4 7.5 %collective-permute-start.20 = (bf16[24,1792]{1,0:T(8,128)(2,1)S(1)}, bf16[24,1792]{1,0:T(8,128)(2,1)S(1)}, u32[]{:S(2)}, u32[]{:S(2)}) collective-permute-start(bf16[24,1792]{1,0:T(8,128)(2,1)S(1)} %constant_dynamic-slice_fusion), channel_id=1, source_target_pairs={{0,8},{4,12},{8,0},{12,4},{16,24},{20,28},{24,16},{28,20},{1,9},{5... | collective-permute-start | bytes 258056 | tf_op jit(solution)/shard_map/ppermute | solution.py:37
  62.1 9.7 %collective-permute-start.8 = (bf16[24,1792]{1,0:T(8,128)(2,1)S(1)}, bf16[24,1792]{1,0:T(8,128)(2,1)S(1)}, u32[]{:S(2)}, u32[]{:S(2)}) collective-permute-start(bf16[24,1792]{1,0:T(8,128)(2,1)S(1)} %constant_dynamic-slice_fusion.9), channel_id=1, source_target_pairs={{0,16},{4,20},{8,24},{12,28},{16,0},{20,4},{24,8},{28,12},{1,17},{... | collective-permute-start | bytes 258056 | tf_op jit(solution)/shard_map/ppermute | solution.py:37
  62.7 7.9 %collective-permute-start.17 = (bf16[24,1792]{1,0:T(8,128)(2,1)S(1)}, bf16[24,1792]{1,0:T(8,128)(2,1)S(1)}, u32[]{:S(2)}, u32[]{:S(2)}) collective-permute-start(bf16[24,1792]{1,0:T(8,128)(2,1)S(1)} %constant_dynamic-slice_fusion.3), channel_id=1, source_target_pairs={{0,8},{4,12},{8,0},{12,4},{16,24},{20,28},{24,16},{28,20},{1,9},{5... | collective-permute-start | bytes 258056 | tf_op jit(solution)/shard_map/ppermute | solution.py:37
  65.1 6.7 %collective-permute-start.5 = (bf16[24,1792]{1,0:T(8,128)(2,1)S(1)}, bf16[24,1792]{1,0:T(8,128)(2,1)S(1)}, u32[]{:S(2)}, u32[]{:S(2)}) collective-permute-start(bf16[24,1792]{1,0:T(8,128)(2,1)S(1)} %constant_dynamic-slice_fusion.12), channel_id=1, source_target_pairs={{0,16},{4,20},{8,24},{12,28},{16,0},{20,4},{24,8},{28,12},{1,17},{... | collective-permute-start | bytes 258056 | tf_op jit(solution)/shard_map/ppermute | solution.py:37
  67.1 5.7 %collective-permute-start.14 = (bf16[24,1792]{1,0:T(8,128)(2,1)S(1)}, bf16[24,1792]{1,0:T(8,128)(2,1)S(1)}, u32[]{:S(2)}, u32[]{:S(2)}) collective-permute-start(bf16[24,1792]{1,0:T(8,128)(2,1)S(1)} %constant_dynamic-slice_fusion.6), channel_id=1, source_target_pairs={{0,8},{4,12},{8,0},{12,4},{16,24},{20,28},{24,16},{28,20},{1,9},{5... | collective-permute-start | bytes 258056 | tf_op jit(solution)/shard_map/ppermute | solution.py:37
  68.9 6.3 %collective-permute-start.2 = (bf16[24,1792]{1,0:T(8,128)(2,1)S(1)}, bf16[24,1792]{1,0:T(8,128)(2,1)S(1)}, u32[]{:S(2)}, u32[]{:S(2)}) collective-permute-start(bf16[24,1792]{1,0:T(8,128)(2,1)S(1)} %constant_dynamic-slice_fusion.15), channel_id=1, source_target_pairs={{0,16},{4,20},{8,24},{12,28},{16,0},{20,4},{24,8},{28,12},{1,17},{... | collective-permute-start | bytes 258056 | tf_op jit(solution)/shard_map/ppermute | solution.py:37
  70.8 6.0 %collective-permute-start.33 = (bf16[24,1792]{1,0:T(8,128)(2,1)S(1)}, bf16[24,1792]{1,0:T(8,128)(2,1)S(1)}, u32[]{:S(2)}, u32[]{:S(2)}) collective-permute-start(bf16[24,1792]{1,0:T(8,128)(2,1)S(1)} %get-tuple-element.7), channel_id=1, source_target_pairs={{0,8},{4,12},{8,0},{12,4},{16,24},{20,28},{24,16},{28,20},{1,9},{5... | collective-permute-start | bytes 258056 | tf_op jit(solution)/shard_map/ppermute | solution.py:51
  71.9 7.2 %collective-permute-start.30 = (bf16[24,1792]{1,0:T(8,128)(2,1)S(1)}, bf16[24,1792]{1,0:T(8,128)(2,1)S(1)}, u32[]{:S(2)}, u32[]{:S(2)}) collective-permute-start(bf16[24,1792]{1,0:T(8,128)(2,1)S(1)} %get-tuple-element.5), channel_id=1, source_target_pairs={{0,16},{4,20},{8,24},{12,28},{16,0},{20,4},{24,8},{28,12},{1,17},{... | collective-permute-start | bytes 258056 | tf_op jit(solution)/shard_map/ppermute | solution.py:51
  72.9 10.0 %collective-permute-start.21 = (bf16[24,1792]{1,0:T(8,128)(2,1)S(1)}, bf16[24,1792]{1,0:T(8,128)(2,1)S(1)}, u32[]{:S(2)}, u32[]{:S(2)}) collective-permute-start(bf16[24,1792]{1,0:T(8,128)(2,1)S(1)} %get-tuple-element.11), channel_id=1, source_target_pairs={{0,8},{4,12},{8,0},{12,4},{16,24},{20,28},{24,16},{28,20},{1,9},{5... | collective-permute-start | bytes 258056 | tf_op jit(solution)/shard_map/ppermute | solution.py:51
  74.5 7.3 %collective-permute-start.27 = (bf16[24,1792]{1,0:T(8,128)(2,1)S(1)}, bf16[24,1792]{1,0:T(8,128)(2,1)S(1)}, u32[]{:S(2)}, u32[]{:S(2)}) collective-permute-start(bf16[24,1792]{1,0:T(8,128)(2,1)S(1)} %get-tuple-element.15), channel_id=1, source_target_pairs={{0,8},{4,12},{8,0},{12,4},{16,24},{20,28},{24,16},{28,20},{1,9},{5... | collective-permute-start | bytes 258056 | tf_op jit(solution)/shard_map/ppermute | solution.py:51
  75.4 9.9 %collective-permute-start.9 = (bf16[24,1792]{1,0:T(8,128)(2,1)S(1)}, bf16[24,1792]{1,0:T(8,128)(2,1)S(1)}, u32[]{:S(2)}, u32[]{:S(2)}) collective-permute-start(bf16[24,1792]{1,0:T(8,128)(2,1)S(1)} %get-tuple-element.9), channel_id=1, source_target_pairs={{0,16},{4,20},{8,24},{12,28},{16,0},{20,4},{24,8},{28,12},{1,17},{... | collective-permute-start | bytes 258056 | tf_op jit(solution)/shard_map/ppermute | solution.py:51
  76.8 7.4 %collective-permute-start.24 = (bf16[24,1792]{1,0:T(8,128)(2,1)S(1)}, bf16[24,1792]{1,0:T(8,128)(2,1)S(1)}, u32[]{:S(2)}, u32[]{:S(2)}) collective-permute-start(bf16[24,1792]{1,0:T(8,128)(2,1)S(1)} %get-tuple-element.13), channel_id=1, source_target_pairs={{0,16},{4,20},{8,24},{12,28},{16,0},{20,4},{24,8},{28,12},{1,17},{... | collective-permute-start | bytes 258056 | tf_op jit(solution)/shard_map/ppermute | solution.py:51
  79.1 7.3 %collective-permute-start.34 = (bf16[48,1792]{1,0:T(8,128)(2,1)S(1)}, bf16[48,1792]{1,0:T(8,128)(2,1)S(1)}, u32[]{:S(2)}, u32[]{:S(2)}) collective-permute-start(bf16[48,1792]{1,0:T(8,128)(2,1)S(1)} %constant_dynamic-update-slice_fusion.4), channel_id=1, source_target_pairs={{0,16},{4,20},{8,24},{12,28},{16,0},{20,4},{24,8},{28,12},{1,17},{... | collective-permute-start | bytes 516104 | tf_op jit(solution)/shard_map/ppermute | solution.py:51
  81.8 7.7 %collective-permute-start.31 = (bf16[48,1792]{1,0:T(8,128)(2,1)S(1)}, bf16[48,1792]{1,0:T(8,128)(2,1)S(1)}, u32[]{:S(2)}, u32[]{:S(2)}) collective-permute-start(bf16[48,1792]{1,0:T(8,128)(2,1)S(1)} %constant_dynamic-update-slice_fusion.10), channel_id=1, source_target_pairs={{0,8},{4,12},{8,0},{12,4},{16,24},{20,28},{24,16},{28,20},{1,9},{5... | collective-permute-start | bytes 516104 | tf_op jit(solution)/shard_map/ppermute | solution.py:51
  82.9 12.0 %slice-start.2 = ((s8[7340032]{0:T(1024)(128)(4,1)}), s8[4194304]{0:T(1024)(128)(4,1)S(1)}, s32[]{:S(2)}) async-start(s8[7340032]{0:T(1024)(128)(4,1)} %bitcast.7), calls=%async_computation.4 | async-start | bytes 8388608
  83.0 9.0 %collective-permute-start.28 = (bf16[48,1792]{1,0:T(8,128)(2,1)S(1)}, bf16[48,1792]{1,0:T(8,128)(2,1)S(1)}, u32[]{:S(2)}, u32[]{:S(2)}) collective-permute-start(bf16[48,1792]{1,0:T(8,128)(2,1)S(1)} %constant_dynamic-update-slice_fusion.16), channel_id=1, source_target_pairs={{0,16},{4,20},{8,24},{12,28},{16,0},{20,4},{24,8},{28,12},{1,17},{... | collective-permute-start | bytes 516104 | tf_op jit(solution)/shard_map/ppermute | solution.py:51
  84.2 7.3 %collective-permute-start.22 = (bf16[48,1792]{1,0:T(8,128)(2,1)S(1)}, bf16[48,1792]{1,0:T(8,128)(2,1)S(1)}, u32[]{:S(2)}, u32[]{:S(2)}) collective-permute-start(bf16[48,1792]{1,0:T(8,128)(2,1)S(1)} %constant_dynamic-update-slice_fusion.28), channel_id=1, source_target_pairs={{0,16},{4,20},{8,24},{12,28},{16,0},{20,4},{24,8},{28,12},{1,17},{... | collective-permute-start | bytes 516104 | tf_op jit(solution)/shard_map/ppermute | solution.py:51
  85.3 7.1 %collective-permute-start.25 = (bf16[48,1792]{1,0:T(8,128)(2,1)S(1)}, bf16[48,1792]{1,0:T(8,128)(2,1)S(1)}, u32[]{:S(2)}, u32[]{:S(2)}) collective-permute-start(bf16[48,1792]{1,0:T(8,128)(2,1)S(1)} %constant_dynamic-update-slice_fusion.22), channel_id=1, source_target_pairs={{0,8},{4,12},{8,0},{12,4},{16,24},{20,28},{24,16},{28,20},{1,9},{5... | collective-permute-start | bytes 516104 | tf_op jit(solution)/shard_map/ppermute | solution.py:51
  86.4 6.5 %collective-permute-start.10 = (bf16[48,1792]{1,0:T(8,128)(2,1)S(1)}, bf16[48,1792]{1,0:T(8,128)(2,1)S(1)}, u32[]{:S(2)}, u32[]{:S(2)}) collective-permute-start(bf16[48,1792]{1,0:T(8,128)(2,1)S(1)} %constant_dynamic-update-slice_fusion.34), channel_id=1, source_target_pairs={{0,8},{4,12},{8,0},{12,4},{16,24},{20,28},{24,16},{28,20},{1,9},{5... | collective-permute-start | bytes 516104 | tf_op jit(solution)/shard_map/ppermute | solution.py:51
  89.4 3.3 %copy-start.3 = (bf16[192,1792]{1,0:T(8,128)(2,1)}, bf16[192,1792]{1,0:T(8,128)(2,1)S(1)}, u32[]{:S(2)}) copy-start(bf16[192,1792]{1,0:T(8,128)(2,1)S(1)} %constant_dynamic-update-slice_fusion.1) | copy-start | bytes 2064388
  89.5 11.9 %collective-permute-start.35 = (bf16[96,1792]{1,0:T(8,128)(2,1)}, bf16[96,1792]{1,0:T(8,128)(2,1)}, u32[]{:S(2)}, u32[]{:S(2)}) collective-permute-start(bf16[96,1792]{1,0:T(8,128)(2,1)} %constant_dynamic-update-slice_fusion.2), channel_id=1, source_target_pairs={{0,4},{4,0},{8,12},{12,8},{16,20},{20,16},{24,28},{28,24},{1,5},{5... | collective-permute-start | bytes 1032200 | tf_op jit(solution)/shard_map/ppermute | solution.py:51
  91.4 1.7 %copy-start.5 = (bf16[192,1792]{1,0:T(8,128)(2,1)}, bf16[192,1792]{1,0:T(8,128)(2,1)S(1)}, u32[]{:S(2)}) copy-start(bf16[192,1792]{1,0:T(8,128)(2,1)S(1)} %constant_dynamic-update-slice_fusion.7) | copy-start | bytes 2064388
  91.5 16.9 %collective-permute-start.32 = (bf16[96,1792]{1,0:T(8,128)(2,1)}, bf16[96,1792]{1,0:T(8,128)(2,1)}, u32[]{:S(2)}, u32[]{:S(2)}) collective-permute-start(bf16[96,1792]{1,0:T(8,128)(2,1)} %constant_dynamic-update-slice_fusion.8), channel_id=1, source_target_pairs={{0,4},{4,0},{8,12},{12,8},{16,20},{20,16},{24,28},{28,24},{1,5},{5... | collective-permute-start | bytes 1032200 | tf_op jit(solution)/shard_map/ppermute | solution.py:51
  91.9 3.0 %slice-start.3 = ((s8[7340032]{0:T(1024)(128)(4,1)}), s8[3145728]{0:T(1024)(128)(4,1)S(1)}, s32[]{:S(2)}) async-start(s8[7340032]{0:T(1024)(128)(4,1)} %bitcast.7), calls=%async_computation.5 | async-start | bytes 6291456
  92.0 5.5 %collective-permute-start.23 = (bf16[96,1792]{1,0:T(8,128)(2,1)S(1)}, bf16[96,1792]{1,0:T(8,128)(2,1)S(1)}, u32[]{:S(2)}, u32[]{:S(2)}) collective-permute-start(bf16[96,1792]{1,0:T(8,128)(2,1)S(1)} %constant_dynamic-update-slice_fusion.26), channel_id=1, source_target_pairs={{0,4},{4,0},{8,12},{12,8},{16,20},{20,16},{24,28},{28,24},{1,5},{5... | collective-permute-start | bytes 1032200 | tf_op jit(solution)/shard_map/ppermute | solution.py:51
  92.4 2.0 %collective-permute-start.29 = (bf16[96,1792]{1,0:T(8,128)(2,1)S(1)}, bf16[96,1792]{1,0:T(8,128)(2,1)S(1)}, u32[]{:S(2)}, u32[]{:S(2)}) collective-permute-start(bf16[96,1792]{1,0:T(8,128)(2,1)S(1)} %constant_dynamic-update-slice_fusion.14), channel_id=1, source_target_pairs={{0,4},{4,0},{8,12},{12,8},{16,20},{20,16},{24,28},{28,24},{1,5},{5... | collective-permute-start | bytes 1032200 | tf_op jit(solution)/shard_map/ppermute | solution.py:51
  92.9 2.0 %collective-permute-start.26 = (bf16[96,1792]{1,0:T(8,128)(2,1)S(1)}, bf16[96,1792]{1,0:T(8,128)(2,1)S(1)}, u32[]{:S(2)}, u32[]{:S(2)}) collective-permute-start(bf16[96,1792]{1,0:T(8,128)(2,1)S(1)} %constant_dynamic-update-slice_fusion.20), channel_id=1, source_target_pairs={{0,4},{4,0},{8,12},{12,8},{16,20},{20,16},{24,28},{28,24},{1,5},{5... | collective-permute-start | bytes 1032200 | tf_op jit(solution)/shard_map/ppermute | solution.py:51
  94.4 3.1 %collective-permute-start.11 = (bf16[96,1792]{1,0:T(8,128)(2,1)S(1)}, bf16[96,1792]{1,0:T(8,128)(2,1)S(1)}, u32[]{:S(2)}, u32[]{:S(2)}) collective-permute-start(bf16[96,1792]{1,0:T(8,128)(2,1)S(1)} %constant_dynamic-update-slice_fusion.32), channel_id=1, source_target_pairs={{0,4},{4,0},{8,12},{12,8},{16,20},{20,16},{24,28},{28,24},{1,5},{5... | collective-permute-start | bytes 1032200 | tf_op jit(solution)/shard_map/ppermute | solution.py:51
  94.7 2.9 %slice-start.4 = ((s8[7340032]{0:T(1024)(128)(4,1)}), s8[4194304]{0:T(1024)(128)(4,1)S(1)}, s32[]{:S(2)}) async-start(s8[7340032]{0:T(1024)(128)(4,1)} %bitcast.9), calls=%async_computation.6 | async-start | bytes 8388608
  94.9 3.0 %slice-start.5 = ((s8[7340032]{0:T(1024)(128)(4,1)}), s8[3145728]{0:T(1024)(128)(4,1)S(1)}, s32[]{:S(2)}) async-start(s8[7340032]{0:T(1024)(128)(4,1)} %bitcast.9), calls=%async_computation.7 | async-start | bytes 6291456
  103.2 5.2 %copy-start.6 = (bf16[192,1792]{1,0:T(8,128)(2,1)S(1)}, bf16[192,1792]{1,0:T(8,128)(2,1)}, u32[]{:S(2)}) copy-start(bf16[192,1792]{1,0:T(8,128)(2,1)} %copy-done.5) | copy-start | bytes 2064388
  109.3 5.2 %copy-start.4 = (bf16[192,1792]{1,0:T(8,128)(2,1)S(1)}, bf16[192,1792]{1,0:T(8,128)(2,1)}, u32[]{:S(2)}) copy-start(bf16[192,1792]{1,0:T(8,128)(2,1)} %constant_dynamic-update-slice_fusion) | copy-start | bytes 2064388
Sparse Core Ops, SparseCore 0:
  101.5 19.0 reduce-scatter.1

commit v3 on v2

v3 whole, which is shorter than its diff:
```python
import jax
import jax.numpy as jnp
from jax import lax
from jax.sharding import PartitionSpec as P


def contract_first(left, right):
    return lax.dot_general(
        left, right, (((0,), (0,)), ((), ())), preferred_element_type=jnp.float32
    )


def contract_last(left, right):
    return lax.dot_general(
        left, right, (((1,), (1,)), ((), ())), preferred_element_type=jnp.float32
    )


def gated_grads(gate_sum, up_sum, grad_hidden):
    sigmoid_gate = jax.nn.sigmoid(gate_sum)
    hidden = (gate_sum * sigmoid_gate * up_sum).astype(jnp.bfloat16)
    grad_up = (grad_hidden * gate_sum * sigmoid_gate).astype(jnp.bfloat16)
    grad_gate = (
        grad_hidden * up_sum * sigmoid_gate * (1.0 + gate_sum * (1.0 - sigmoid_gate))
    ).astype(jnp.bfloat16)
    return (hidden, grad_gate, grad_up)


def halving_reduce(parts, order, n_dev):
    cur = parts
    for step, bit in enumerate(order):
        n = cur[0].shape[0] // 2
        got = lax.ppermute(tuple(c[n:] for c in cur), "row", [(j, j ^ bit) for j in range(n_dev)])
        summed = tuple(c[:n].astype(jnp.float32) + g.astype(jnp.float32) for c, g in zip(cur, got))
        if step + 1 < len(order):
            summed = tuple(s.astype(jnp.bfloat16) for s in summed)
        cur = summed
    return cur


def doubling_gather(parts, order, n_dev):
    cur = parts
    for bit in reversed(order):
        got = lax.ppermute(cur, "row", [(j, j ^ bit) for j in range(n_dev)])
        cur = tuple(jnp.concatenate([c, g], axis=0) for c, g in zip(cur, got))
    return cur


def row_bits(n_dev, tokens, units):
    if n_dev < 2 or n_dev & (n_dev - 1) or tokens % n_dev or units % 2:
        return None
    bits, b = [], 1
    while b < n_dev:
        bits.append(b)
        b *= 2
    return bits


def block_mask(order):
    r = lax.axis_index("row")
    levels = len(order)
    mask = 0
    for k, bit in enumerate(order):
        mask = mask + ((r // bit) % 2) * (1 << (levels - 1 - k))
    return mask


def permute_blocks(x, n_dev, mask):
    idx = jnp.arange(n_dev, dtype=jnp.int32) ^ mask
    blocks = x.reshape((n_dev, x.shape[0] // n_dev) + x.shape[1:])
    return jnp.take(blocks, idx, axis=0).reshape(x.shape)


def body(tokens, grad_out, gate_weight, up_weight, down_weight):
    n_row = lax.psum(1, "row")
    feat = tokens.shape[1]
    both = jnp.concatenate([tokens, grad_out], axis=1)
    both_all = lax.all_gather(both, "col", axis=0, tiled=True)
    n_tok = both_all.shape[0]
    units = gate_weight.shape[1]
    bits = row_bits(n_row, n_tok, units)
    if bits is None:
        tok_all = both_all[:, :feat]
        grad_all = both_all[:, feat:]
        sums = lax.psum(
            (
                jnp.dot(tok_all, gate_weight, preferred_element_type=jnp.float32).astype(jnp.bfloat16),
                jnp.dot(tok_all, up_weight, preferred_element_type=jnp.float32).astype(jnp.bfloat16),
                contract_last(grad_all, down_weight).astype(jnp.bfloat16),
            ),
            "row",
        )
        hidden, grad_gate, grad_up = gated_grads(*(s.astype(jnp.float32) for s in sums))
        mask_a = None
    else:
        orders = (bits, bits[:1] + bits[:0:-1])
        masks = [block_mask(o) for o in orders]
        mask_a = masks[0]
        half = units // 2
        outs = []
        for h, order in enumerate(orders):
            both_h = permute_blocks(both_all, n_row, masks[h])
            tok_h = both_h[:, :feat]
            grad_h = both_h[:, feat:]
            cols = slice(h * half, (h + 1) * half)
            parts = (
                jnp.dot(tok_h, gate_weight[:, cols], preferred_element_type=jnp.float32).astype(jnp.bfloat16),
                jnp.dot(tok_h, up_weight[:, cols], preferred_element_type=jnp.float32).astype(jnp.bfloat16),
                contract_last(grad_h, down_weight[cols, :]).astype(jnp.bfloat16),
            )
            reduced = halving_reduce(parts, order, n_row)
            outs.append(doubling_gather(gated_grads(*reduced), order, n_row))
            if h == 0:
                tok_all, grad_all = tok_h, grad_h
        hidden, grad_gate, grad_up = (
            jnp.concatenate([outs[0][i], permute_blocks(outs[1][i], n_row, masks[0] ^ masks[1])], axis=1)
            for i in range(3)
        )
    tok_t = tok_all.T
    acc_gate = jnp.dot(tok_t, grad_gate, preferred_element_type=jnp.float32)
    acc_up = jnp.dot(tok_t, grad_up, preferred_element_type=jnp.float32)
    acc_down = contract_first(hidden, grad_all)
    partial_grad = contract_last(grad_gate, gate_weight) + contract_last(grad_up, up_weight)
    partial_grad = partial_grad.astype(jnp.bfloat16)
    if mask_a is not None:
        partial_grad = permute_blocks(partial_grad, n_row, mask_a)
    grad_tokens = lax.psum_scatter(partial_grad, "col", scatter_dimension=0, tiled=True)
    return (
        grad_tokens,
        acc_gate.astype(jnp.bfloat16),
        acc_up.astype(jnp.bfloat16),
        acc_down.astype(jnp.bfloat16),
    )


def solution(mesh):
    return jax.shard_map(
        body,
        mesh=mesh,
        in_specs=(
            P("col", "row"),
            P("col", "row"),
            P("row", "col"),
            P("row", "col"),
            P("col", "row"),
        ),
        out_specs=(P("col", "row"), P("row", "col"), P("row", "col"), P("col", "row")),
        check_vma=False,
    )
```

time: 128 us -> 150 us (1.17)
  waiting for transfers between devices: 4.42 us -> 16.6 us
  matrix products: 34.1 us -> 45.9 us
  other arithmetic: 7.34 us -> 14.5 us
  local copies, waits for them, and re-layouts: 15 us -> 9.27 us
  starting transfers between devices: 30.5 us -> 26.5 us
    dynamic_update_slice x30 -> x0, local copies, waits for them, and re-layouts: 8.09 us -> none  [the longest x18 4.5 us: doubling_gather(): out = lax.dynamic_update_slice_in_dim(out, g, (1 - hi) * n, 0)]
    ppermute x18, waiting for transfers between devices: 1.29 us -> 8.57 us  [doubling_gather(): got = lax.ppermute(cur, 'row', [(j, j ^ bit) for j in range(n_dev)])]
    dot_general x3 -> x4, matrix products: 8.51 us -> 15.2 us  [contract_last(): lax.dot_general(left, right, (((1,), (1,)), ((), ())), preferred_element_...]
    concatenate x0 -> x15, other arithmetic: none -> 6 us  [doubling_gather(): cur = tuple((jnp.concatenate([c, g], axis=0) for c, g in zip(cur, got)))]
    ppermute x18, waiting for transfers between devices: 2.18 us -> 7.82 us  [halving_reduce(): lax.ppermute(tuple((c[n:] for c in cur)), 'row', [(j, j ^ bit) for j in r...]
    dynamic_slice x18 -> x0, local copies, waits for them, and re-layouts: 4.22 us -> none  [halving_reduce(): send = tuple((lax.dynamic_slice_in_dim(c, (1 - hi) * n, n, 0) for c in cur))]
    slice x3 -> x18, local copies, waits for them, and re-layouts: 0.27 us -> 4.12 us  [halving_reduce(): c[n:]]
    gather x0 -> x6, local copies, waits for them, and re-layouts: none -> 3.54 us  [permute_blocks(): return jnp.take(blocks, idx, axis=0).reshape(x.shape)]
  transfers between devices with their start and end apart: 37 -> 37, of which waited for: 6 -> 13; matrix products, arithmetic and copies ran while one was open for 39% -> 42% of each run, Pallas kernels for 0% -> 0%
where the time goes in v3:
time: 150 us; the launch traced here: 149 us
  matrix products  45.9 us (31%)
  starting transfers between devices  26.5 us (18%)
  blocking collectives  21.3 us (14%)
  waiting for transfers between devices  16.6 us (11%)
  between operations  15 us (10%)
  other arithmetic  14.5 us (10%)
  local copies, waits for them, and re-layouts  9.27 us (6%)
    all_gather x1, blocking collectives, body(): both_all = lax.all_gather(both, 'col', axis=0, tiled=True)  21.3 us
    dot_general x4, matrix products, contract_last(): lax.dot_general(left, right, (((1,), (1,)), ((), ())), preferred_element_...  15.2 us
    ppermute x18, starting transfers between devices, halving_reduce(): lax.ppermute(tuple((c[n:] for c in cur)), 'row', [(j, j ^ bit) for j in r...  14.4 us
    ppermute x18, starting transfers between devices, doubling_gather(): got = lax.ppermute(cur, 'row', [(j, j ^ bit) for j in range(n_dev)])  12.1 us
    ppermute x18, waiting for transfers between devices, doubling_gather(): got = lax.ppermute(cur, 'row', [(j, j ^ bit) for j in range(n_dev)])  8.57 us
    ppermute x18, waiting for transfers between devices, halving_reduce(): lax.ppermute(tuple((c[n:] for c in cur)), 'row', [(j, j ^ bit) for j in r...  7.82 us
    dot_general x1, matrix products, body(): acc_gate = jnp.dot(tok_t, grad_gate, preferred_element_type=jnp.float32)  6.43 us
    dot_general x1, matrix products, body(): acc_up = jnp.dot(tok_t, grad_up, preferred_element_type=jnp.float32)  6.22 us
  transfers between devices with their start and end apart: 37, of which 13 were waited for; matrix products, arithmetic and copies ran while one was open for 42% of the time, Pallas kernels for 0%

profile of v3, /device:TPU:0, one launch (start us, length us, event | category | flops | bytes accessed | tf_op | source)
XLA Modules:
  0.0 149.0 jit_solution(2268570305578768991)
XLA Ops:
  7.3 1.0 pad_maximum_fusion.11
  8.3 21.3 %all_gather.3 = bf16[192,2048]{1,0:T(8,128)(2,1)S(1)} all-gather(bf16[48,2048]{1,0:T(8,128)(2,1)S(1)} %pad_maximum_fusion.11), channel_id=1, replica_groups=mesh['row'=8,'col'=4] {'col'}, dimensions={0}, use_global_device_ids=true | all-gather | bytes 983040 | tf_op jit(solution)/shard_map/all_gather | solution.py:78
  29.6 0.6 gather_fusion.2
  30.4 3.1 %fusion.27 = bf16[192,1792]{1,0:T(8,128)(2,1)S(1)} fusion(bf16[1024,3584]{1,0:T(8,128)(2,1)} %param.11, bf16[192,2048]{1,0:T(8,128)(2,1)S(1)} %bitcast.27), kind=kOutput, calls=%fused_computation.26 | convolution fusion | flops 704987136 | bytes 4751360 | tf_op jit(solution)/shard_map/dot_general | solution.py:107
  33.5 0.8 slice.231
  34.4 2.9 %fusion.24 = bf16[192,1792]{1,0:T(8,128)(2,1)S(1)} fusion(bf16[1024,3584]{1,0:T(8,128)(2,1)} %param.12, bf16[192,2048]{1,0:T(8,128)(2,1)S(1)} %bitcast.28), kind=kOutput, calls=%fused_computation.25 | convolution fusion | flops 704987136 | bytes 4751360 | tf_op jit(solution)/shard_map/dot_general | solution.py:108
  37.4 0.8 slice.225
  38.8 1.4 fusion.21
  40.2 0.8 slice.218
  41.0 0.6 gather_fusion.1
  41.8 2.9 %fusion.18 = bf16[192,1792]{1,0:T(8,128)(2,1)S(1)} fusion(bf16[1024,3584]{1,0:T(8,128)(2,1)} %param.11, bf16[192,2048]{1,0:T(8,128)(2,1)S(1)} %bitcast.21), kind=kOutput, calls=%fused_computation.23 | convolution fusion | flops 704987136 | bytes 4751360 | tf_op jit(solution)/shard_map/dot_general | solution.py:107
  44.7 0.8 slice.211
  46.2 2.9 %fusion.15 = bf16[192,1792]{1,0:T(8,128)(2,1)S(1)} fusion(bf16[1024,3584]{1,0:T(8,128)(2,1)} %param.12, bf16[192,2048]{1,0:T(8,128)(2,1)S(1)} %bitcast.22), kind=kOutput, calls=%fused_computation.22 | convolution fusion | flops 704987136 | bytes 4751360 | tf_op jit(solution)/shard_map/dot_general | solution.py:108
  49.2 0.8 copy-done.8
  50.0 0.7 slice.205
  50.8 3.5 %fusion.12 = bf16[192,1792]{1,0:T(8,128)(2,1)S(1)} fusion(bf16[3584,1024]{1,0:T(8,128)(2,1)} %param.13, bf16[192,2048]{1,0:T(8,128)(2,1)S(1)} %bitcast.23), kind=kOutput, calls=%fused_computation.21 | convolution fusion | flops 704987136 | bytes 4751360 | tf_op jit(solution)/shard_map/dot_general | solution.py:14
  55.1 1.2 add_convert_fusion
  56.3 1.6 %collective-permute-start.19 = (bf16[48,1792]{1,0:T(8,128)(2,1)S(1)}, bf16[48,1792]{1,0:T(8,128)(2,1)S(1)}, u32[]{:S(2)}, u32[]{:S(2)}) collective-permute-start(bf16[48,1792]{1,0:T(8,128)(2,1)S(1)} %slice.233), channel_id=1, source_target_pairs={{0,16},{4,20},{8,24},{12,28},{16,0},{20,4},{24,8},{28,12},{1,17},{... | collective-permute-start | bytes 516104 | tf_op jit(solution)/shard_map/ppermute | solution.py:33
  57.9 1.1 add_convert_fusion.1
  59.0 0.6 collective-permute-start.16
  59.6 1.6 %collective-permute-start.13 = (bf16[48,1792]{1,0:T(8,128)(2,1)S(1)}, bf16[48,1792]{1,0:T(8,128)(2,1)S(1)}, u32[]{:S(2)}, u32[]{:S(2)}) collective-permute-start(bf16[48,1792]{1,0:T(8,128)(2,1)S(1)} %slice.220), channel_id=1, source_target_pairs={{0,16},{4,20},{8,24},{12,28},{16,0},{20,4},{24,8},{28,12},{1,17},{... | collective-permute-start | bytes 516104 | tf_op jit(solution)/shard_map/ppermute | solution.py:33
  61.2 1.2 add_convert_fusion.3
  62.4 1.6 %collective-permute-start.7 = (bf16[48,1792]{1,0:T(8,128)(2,1)S(1)}, bf16[48,1792]{1,0:T(8,128)(2,1)S(1)}, u32[]{:S(2)}, u32[]{:S(2)}) collective-permute-start(bf16[48,1792]{1,0:T(8,128)(2,1)S(1)} %slice.213), channel_id=1, source_target_pairs={{0,8},{4,12},{8,0},{12,4},{16,24},{20,28},{24,16},{28,20},{1,9},{5... | collective-permute-start | bytes 516104 | tf_op jit(solution)/shard_map/ppermute | solution.py:33
  64.0 1.1 add_convert_fusion.4
  65.1 0.6 collective-permute-start.4
  65.8 1.6 %collective-permute-start.1 = (bf16[48,1792]{1,0:T(8,128)(2,1)S(1)}, bf16[48,1792]{1,0:T(8,128)(2,1)S(1)}, u32[]{:S(2)}, u32[]{:S(2)}) collective-permute-start(bf16[48,1792]{1,0:T(8,128)(2,1)S(1)} %slice.200), channel_id=1, source_target_pairs={{0,8},{4,12},{8,0},{12,4},{16,24},{20,28},{24,16},{28,20},{1,9},{5... | collective-permute-start | bytes 516104 | tf_op jit(solution)/shard_map/ppermute | solution.py:33
  67.4 1.3 collective-permute-start.20
  68.8 1.2 collective-permute-done.13
  70.1 1.5 collective-permute-start.17
  71.6 0.6 collective-permute-start.14
  72.3 0.7 collective-permute-done.4
  73.0 0.9 collective-permute-start.8
  73.9 2.7 %collective-permute-done.1 = bf16[48,1792]{1,0:T(8,128)(2,1)S(1)} collective-permute-done((bf16[48,1792]{1,0:T(8,128)(2,1)S(1)}, bf16[48,1792]{1,0:T(8,128)(2,1)S(1)}, u32[]{:S(2)}, u32[]{:S(2)}) %collective-permute-start.1) | collective-permute-done | bytes 172064 | tf_op jit(solution)/shard_map/ppermute | solution.py:33
  77.2 1.3 collective-permute-done.20
  79.0 1.0 collective-permute-done.17
  80.0 0.9 collective-permute-done.14
  81.0 1.6 %collective-permute-start.33 = (bf16[24,1792]{1,0:T(8,128)(2,1)S(1)}, bf16[24,1792]{1,0:T(8,128)(2,1)S(1)}, u32[]{:S(2)}, u32[]{:S(2)}) collective-permute-start(bf16[24,1792]{1,0:T(8,128)(2,1)S(1)} %get-tuple-element.9), channel_id=1, source_target_pairs={{0,8},{4,12},{8,0},{12,4},{16,24},{20,28},{24,16},{28,20},{1,9},{5... | collective-permute-start | bytes 258056 | tf_op jit(solution)/shard_map/ppermute | solution.py:44
  83.1 1.5 collective-permute-start.27
  85.4 1.5 %collective-permute-start.9 = (bf16[24,1792]{1,0:T(8,128)(2,1)S(1)}, bf16[24,1792]{1,0:T(8,128)(2,1)S(1)}, u32[]{:S(2)}, u32[]{:S(2)}) collective-permute-start(bf16[24,1792]{1,0:T(8,128)(2,1)S(1)} %get-tuple-element.7), channel_id=1, source_target_pairs={{0,16},{4,20},{8,24},{12,28},{16,0},{20,4},{24,8},{28,12},{1,17},{... | collective-permute-start | bytes 258056 | tf_op jit(solution)/shard_map/ppermute | solution.py:44
  87.5 1.6 %collective-permute-start.34 = (bf16[48,1792]{1,0:T(8,128)(2,1)S(1)}, bf16[48,1792]{1,0:T(8,128)(2,1)S(1)}, u32[]{:S(2)}, u32[]{:S(2)}) collective-permute-start(bf16[48,1792]{1,0:T(8,128)(2,1)S(1)} %pad_maximum_fusion.17), channel_id=1, source_target_pairs={{0,16},{4,20},{8,24},{12,28},{16,0},{20,4},{24,8},{28,12},{1,17},{... | collective-permute-start | bytes 516104 | tf_op jit(solution)/shard_map/ppermute | solution.py:44
  89.7 0.6 collective-permute-done.30
  90.3 1.0 collective-permute-start.28
  91.3 0.9 collective-permute-done.9
  92.7 1.3 collective-permute-done.24
  94.5 3.1 %collective-permute-done.34 = bf16[48,1792]{1,0:T(8,128)(2,1)S(1)} collective-permute-done((bf16[48,1792]{1,0:T(8,128)(2,1)S(1)}, bf16[48,1792]{1,0:T(8,128)(2,1)S(1)}, u32[]{:S(2)}, u32[]{:S(2)}) %collective-permute-start.34) | collective-permute-done | bytes 172064 | tf_op jit(solution)/shard_map/ppermute | solution.py:44
  98.2 1.5 %collective-permute-done.22 = bf16[48,1792]{1,0:T(8,128)(2,1)S(1)} collective-permute-done((bf16[48,1792]{1,0:T(8,128)(2,1)S(1)}, bf16[48,1792]{1,0:T(8,128)(2,1)S(1)}, u32[]{:S(2)}, u32[]{:S(2)}) %collective-permute-start.22) | collective-permute-done | bytes 172064 | tf_op jit(solution)/shard_map/ppermute | solution.py:44
  99.8 0.8 pad_maximum_fusion.6
  100.5 1.1 collective-permute-done.28
  101.6 0.8 pad_maximum_fusion.8
  102.9 0.8 pad_maximum_fusion.9
  103.7 0.8 pad_maximum_fusion.5
  105.0 0.8 pad_maximum_fusion.7
  106.0 0.6 gather_fusion.5
  106.6 1.0 pad_maximum_fusion.2
  107.6 0.6 gather_fusion.3
  108.2 1.0 pad_maximum_fusion.3
  109.3 0.6 gather_fusion.4
  109.9 1.1 broadcast_select_fusion.2
  111.1 6.7 %fusion.51 = f32[192,1024]{1,0:T(8,128)S(1)} fusion(bf16[1024,3584]{1,0:T(8,128)(2,1)} %param.12, bf16[192,1792]{1,0:T(8,128)(2,1)S(1)} %bitcast.31, bf16[96,1792]{1,0:T(8,128)(2,1)} %collective-permute-done.26, bf16[48,1792]{1,0:T(8,128)(2,1)S(1)} %copy-done.28, bf16[24,1792]{1,0:T(8,128)(2,1)S(1)} %copy-done.21, bf16[24,1792]{1,0:T(8,128)(2,1)S(1)} %copy-done.3), kind=kOutput, calls=%fused_computation.110 | convolution fusion | flops 1416167424 | bytes 9502720 | tf_op jit(solution)/shard_map/dot_general | solution.py:14
  117.9 3.7 %fusion.39 = bf16[192,1024]{1,0:T(8,128)(2,1)S(1)} fusion(f32[192,1024]{1,0:T(8,128)S(1)} %fusion.51, bf16[1024,3584]{1,0:T(8,128)(2,1)S(1)} %bitcast.39, bf16[192,1792]{1,0:T(8,128)(2,1)S(1)} %bitcast.33, bf16[96,1792]{1,0:T(8,128)(2,1)} %collective-permute-done.11, bf16[48,1792]{1,0:T(8,128)(2,1)S(1)} %copy-done.26, bf16[24,1792]{1,0:T(8,128)(2,1)S(1)} %copy-done.19, ...), kind=kOutput, calls=%fused_computation.39 | convolution fusion | flops 1416560640 | bytes 9895936 | tf_op jit(solution)/shard_map/dot_general | solution.py:14
  122.2 0.9 bitcast_select_fusion
  123.1 6.4 %convolution_convert_fusion.2 = bf16[1024,3584]{1,0:T(8,128)(2,1)} fusion(bf16[192,2048]{1,0:T(8,128)(2,1)S(1)} %bitcast.24, bf16[192,1792]{1,0:T(8,128)(2,1)} %bitcast.34, bf16[96,1792]{1,0:T(8,128)(2,1)} %collective-permute-done.11, bf16[48,1792]{1,0:T(8,128)(2,1)S(1)} %copy-done.26, bf16[24,1792]{1,0:T(8,128)(2,1)S(1)} %copy-done.19, ...), kind=kOutput, calls=%fused_computation.8 | convolution fusion | flops 1419837440 | bytes 9109504 | tf_op jit(solution)/shard_map/dot_general | solution.py:120
  129.6 6.2 %convolution_convert_fusion.1 = bf16[1024,3584]{1,0:T(8,128)(2,1)} fusion(bf16[192,2048]{1,0:T(8,128)(2,1)S(1)} %bitcast.25, bf16[192,1792]{1,0:T(8,128)(2,1)S(1)} %bitcast.32, bf16[96,1792]{1,0:T(8,128)(2,1)} %collective-permute-done.26, bf16[48,1792]{1,0:T(8,128)(2,1)S(1)} %copy-done.29, bf16[24,1792]{1,0:T(8,128)(2,1)S(1)} %copy-done.22, ...), kind=kOutput, calls=%fused_computation.7 | convolution fusion | flops 1419837440 | bytes 9109504 | tf_op jit(solution)/shard_map/dot_general | solution.py:121
  135.8 6.2 %convolution_convert_fusion = bf16[3584,1024]{1,0:T(8,128)(2,1)} fusion(bf16[192,1792]{1,0:T(8,128)(2,1)S(1)} %bitcast.30, bf16[96,1792]{1,0:T(8,128)(2,1)} %collective-permute-done.32, bf16[48,1792]{1,0:T(8,128)(2,1)S(1)} %copy-done.24, bf16[24,1792]{1,0:T(8,128)(2,1)S(1)} %copy-done.17, bf16[24,1792]{1,0:T(8,128)(2,1)S(1)} %copy-done.1, ...), kind=kOutput, calls=%fused_computation.6 | convolution fusion | flops 1419837440 | bytes 9109504 | tf_op jit(solution)/shard_map/dot_general | solution.py:8
  (164 shorter events, 10.6 us)
Async XLA Ops:
  7.2 135.0 %reduce-scatter.2.cloned.1.call-start = ((), (), s32[]{:S(2)}) async-start(), calls=%async_computation.1 | async-start | bytes 491520 | tf_op jit(solution)/shard_map/reduce_scatter | solution.py:127
  30.2 8.7 %slice-start = ((s8[7340032]{0:T(1024)(128)(4,1)}), s8[4194304]{0:T(1024)(128)(4,1)S(1)}, s32[]{:S(2)}) async-start(s8[7340032]{0:T(1024)(128)(4,1)} %bitcast.36), calls=%async_computation.2 | async-start | bytes 8388608
  30.3 8.5 %slice-start.1 = ((s8[7340032]{0:T(1024)(128)(4,1)}), s8[3145728]{0:T(1024)(128)(4,1)S(1)}, s32[]{:S(2)}) async-start(s8[7340032]{0:T(1024)(128)(4,1)} %bitcast.36), calls=%async_computation.3 | async-start | bytes 6291456
  34.4 20.1 %collective-permute-start.18 = (bf16[96,1792]{1,0:T(8,128)(2,1)}, bf16[96,1792]{1,0:T(8,128)(2,1)}, u32[]{:S(2)}, u32[]{:S(2)}) collective-permute-start(bf16[96,1792]{1,0:T(8,128)(2,1)} %slice.231), channel_id=1, source_target_pairs={{0,4},{4,0},{8,12},{12,8},{16,20},{20,16},{24,28},{28,24},{1,5},{5... | collective-permute-start | bytes 1032200 | tf_op jit(solution)/shard_map/ppermute | solution.py:33
  38.3 17.9 %collective-permute-start.15 = (bf16[96,1792]{1,0:T(8,128)(2,1)}, bf16[96,1792]{1,0:T(8,128)(2,1)}, u32[]{:S(2)}, u32[]{:S(2)}) collective-permute-start(bf16[96,1792]{1,0:T(8,128)(2,1)} %slice.225), channel_id=1, source_target_pairs={{0,4},{4,0},{8,12},{12,8},{16,20},{20,16},{24,28},{28,24},{1,5},{5... | collective-permute-start | bytes 1032200 | tf_op jit(solution)/shard_map/ppermute | solution.py:33
  41.0 18.0 %collective-permute-start.12 = (bf16[96,1792]{1,0:T(8,128)(2,1)}, bf16[96,1792]{1,0:T(8,128)(2,1)S(1)}, u32[]{:S(2)}, u32[]{:S(2)}) collective-permute-start(bf16[96,1792]{1,0:T(8,128)(2,1)} %slice.218), channel_id=1, source_target_pairs={{0,4},{4,0},{8,12},{12,8},{16,20},{20,16},{24,28},{28,24},{1,5},{5... | collective-permute-start | bytes 1032200 | tf_op jit(solution)/shard_map/ppermute | solution.py:33
  45.7 13.9 %collective-permute-start.6 = (bf16[96,1792]{1,0:T(8,128)(2,1)}, bf16[96,1792]{1,0:T(8,128)(2,1)}, u32[]{:S(2)}, u32[]{:S(2)}) collective-permute-start(bf16[96,1792]{1,0:T(8,128)(2,1)} %slice.211), channel_id=1, source_target_pairs={{0,4},{4,0},{8,12},{12,8},{16,20},{20,16},{24,28},{28,24},{1,5},{5... | collective-permute-start | bytes 1032200 | tf_op jit(solution)/shard_map/ppermute | solution.py:33
  50.7 11.7 %collective-permute-start.3 = (bf16[96,1792]{1,0:T(8,128)(2,1)}, bf16[96,1792]{1,0:T(8,128)(2,1)}, u32[]{:S(2)}, u32[]{:S(2)}) collective-permute-start(bf16[96,1792]{1,0:T(8,128)(2,1)} %slice.205), channel_id=1, source_target_pairs={{0,4},{4,0},{8,12},{12,8},{16,20},{20,16},{24,28},{28,24},{1,5},{5... | collective-permute-start | bytes 1032200 | tf_op jit(solution)/shard_map/ppermute | solution.py:33
  50.8 7.1 %copy-start.7 = (bf16[192,1792]{1,0:T(8,128)(2,1)S(1)}, bf16[192,1792]{1,0:T(8,128)(2,1)}, u32[]{:S(2)}) copy-start(bf16[192,1792]{1,0:T(8,128)(2,1)} %copy-done.6) | copy-start | bytes 2064388
  54.5 9.5 %copy-start.9 = (bf16[192,1792]{1,0:T(8,128)(2,1)S(1)}, bf16[192,1792]{1,0:T(8,128)(2,1)}, u32[]{:S(2)}) copy-start(bf16[192,1792]{1,0:T(8,128)(2,1)} %copy-done.8) | copy-start | bytes 2064388
  54.5 10.6 %collective-permute-start = (bf16[96,1792]{1,0:T(8,128)(2,1)S(1)}, bf16[96,1792]{1,0:T(8,128)(2,1)S(1)}, u32[]{:S(2)}, u32[]{:S(2)}) collective-permute-start(bf16[96,1792]{1,0:T(8,128)(2,1)S(1)} %slice.198), channel_id=1, source_target_pairs={{0,4},{4,0},{8,12},{12,8},{16,20},{20,16},{24,28},{28,24},{1,5},{5... | collective-permute-start | bytes 1032200 | tf_op jit(solution)/shard_map/ppermute | solution.py:33
  56.3 9.5 %collective-permute-start.19 = (bf16[48,1792]{1,0:T(8,128)(2,1)S(1)}, bf16[48,1792]{1,0:T(8,128)(2,1)S(1)}, u32[]{:S(2)}, u32[]{:S(2)}) collective-permute-start(bf16[48,1792]{1,0:T(8,128)(2,1)S(1)} %slice.233), channel_id=1, source_target_pairs={{0,16},{4,20},{8,24},{12,28},{16,0},{20,4},{24,8},{28,12},{1,17},{... | collective-permute-start | bytes 516104 | tf_op jit(solution)/shard_map/ppermute | solution.py:33
  59.0 8.5 %collective-permute-start.16 = (bf16[48,1792]{1,0:T(8,128)(2,1)S(1)}, bf16[48,1792]{1,0:T(8,128)(2,1)S(1)}, u32[]{:S(2)}, u32[]{:S(2)}) collective-permute-start(bf16[48,1792]{1,0:T(8,128)(2,1)S(1)} %slice.227), channel_id=1, source_target_pairs={{0,16},{4,20},{8,24},{12,28},{16,0},{20,4},{24,8},{28,12},{1,17},{... | collective-permute-start | bytes 516104 | tf_op jit(solution)/shard_map/ppermute | solution.py:33
  59.6 10.4 %collective-permute-start.13 = (bf16[48,1792]{1,0:T(8,128)(2,1)S(1)}, bf16[48,1792]{1,0:T(8,128)(2,1)S(1)}, u32[]{:S(2)}, u32[]{:S(2)}) collective-permute-start(bf16[48,1792]{1,0:T(8,128)(2,1)S(1)} %slice.220), channel_id=1, source_target_pairs={{0,16},{4,20},{8,24},{12,28},{16,0},{20,4},{24,8},{28,12},{1,17},{... | collective-permute-start | bytes 516104 | tf_op jit(solution)/shard_map/ppermute | solution.py:33
  62.4 9.2 %collective-permute-start.7 = (bf16[48,1792]{1,0:T(8,128)(2,1)S(1)}, bf16[48,1792]{1,0:T(8,128)(2,1)S(1)}, u32[]{:S(2)}, u32[]{:S(2)}) collective-permute-start(bf16[48,1792]{1,0:T(8,128)(2,1)S(1)} %slice.213), channel_id=1, source_target_pairs={{0,8},{4,12},{8,0},{12,4},{16,24},{20,28},{24,16},{28,20},{1,9},{5... | collective-permute-start | bytes 516104 | tf_op jit(solution)/shard_map/ppermute | solution.py:33
  65.1 7.9 %collective-permute-start.4 = (bf16[48,1792]{1,0:T(8,128)(2,1)S(1)}, bf16[48,1792]{1,0:T(8,128)(2,1)S(1)}, u32[]{:S(2)}, u32[]{:S(2)}) collective-permute-start(bf16[48,1792]{1,0:T(8,128)(2,1)S(1)} %slice.207), channel_id=1, source_target_pairs={{0,8},{4,12},{8,0},{12,4},{16,24},{20,28},{24,16},{28,20},{1,9},{5... | collective-permute-start | bytes 516104 | tf_op jit(solution)/shard_map/ppermute | solution.py:33
  65.8 10.9 %collective-permute-start.1 = (bf16[48,1792]{1,0:T(8,128)(2,1)S(1)}, bf16[48,1792]{1,0:T(8,128)(2,1)S(1)}, u32[]{:S(2)}, u32[]{:S(2)}) collective-permute-start(bf16[48,1792]{1,0:T(8,128)(2,1)S(1)} %slice.200), channel_id=1, source_target_pairs={{0,8},{4,12},{8,0},{12,4},{16,24},{20,28},{24,16},{28,20},{1,9},{5... | collective-permute-start | bytes 516104 | tf_op jit(solution)/shard_map/ppermute | solution.py:33
  67.4 11.1 %collective-permute-start.20 = (bf16[24,1792]{1,0:T(8,128)(2,1)S(1)}, bf16[24,1792]{1,0:T(8,128)(2,1)S(1)}, u32[]{:S(2)}, u32[]{:S(2)}) collective-permute-start(bf16[24,1792]{1,0:T(8,128)(2,1)S(1)} %slice.235), channel_id=1, source_target_pairs={{0,8},{4,12},{8,0},{12,4},{16,24},{20,28},{24,16},{28,20},{1,9},{5... | collective-permute-start | bytes 258056 | tf_op jit(solution)/shard_map/ppermute | solution.py:33
  70.1 9.9 %collective-permute-start.17 = (bf16[24,1792]{1,0:T(8,128)(2,1)S(1)}, bf16[24,1792]{1,0:T(8,128)(2,1)S(1)}, u32[]{:S(2)}, u32[]{:S(2)}) collective-permute-start(bf16[24,1792]{1,0:T(8,128)(2,1)S(1)} %slice.229), channel_id=1, source_target_pairs={{0,8},{4,12},{8,0},{12,4},{16,24},{20,28},{24,16},{28,20},{1,9},{5... | collective-permute-start | bytes 258056 | tf_op jit(solution)/shard_map/ppermute | solution.py:33
  71.6 9.3 %collective-permute-start.14 = (bf16[24,1792]{1,0:T(8,128)(2,1)S(1)}, bf16[24,1792]{1,0:T(8,128)(2,1)S(1)}, u32[]{:S(2)}, u32[]{:S(2)}) collective-permute-start(bf16[24,1792]{1,0:T(8,128)(2,1)S(1)} %slice.222), channel_id=1, source_target_pairs={{0,8},{4,12},{8,0},{12,4},{16,24},{20,28},{24,16},{28,20},{1,9},{5... | collective-permute-start | bytes 258056 | tf_op jit(solution)/shard_map/ppermute | solution.py:33
  73.0 10.2 %collective-permute-start.8 = (bf16[24,1792]{1,0:T(8,128)(2,1)S(1)}, bf16[24,1792]{1,0:T(8,128)(2,1)S(1)}, u32[]{:S(2)}, u32[]{:S(2)}) collective-permute-start(bf16[24,1792]{1,0:T(8,128)(2,1)S(1)} %slice.215), channel_id=1, source_target_pairs={{0,16},{4,20},{8,24},{12,28},{16,0},{20,4},{24,8},{28,12},{1,17},{... | collective-permute-start | bytes 258056 | tf_op jit(solution)/shard_map/ppermute | solution.py:33
  76.7 8.0 %collective-permute-start.5 = (bf16[24,1792]{1,0:T(8,128)(2,1)S(1)}, bf16[24,1792]{1,0:T(8,128)(2,1)S(1)}, u32[]{:S(2)}, u32[]{:S(2)}) collective-permute-start(bf16[24,1792]{1,0:T(8,128)(2,1)S(1)} %slice.209), channel_id=1, source_target_pairs={{0,16},{4,20},{8,24},{12,28},{16,0},{20,4},{24,8},{28,12},{1,17},{... | collective-permute-start | bytes 258056 | tf_op jit(solution)/shard_map/ppermute | solution.py:33
  78.5 6.1 %collective-permute-start.2 = (bf16[24,1792]{1,0:T(8,128)(2,1)S(1)}, bf16[24,1792]{1,0:T(8,128)(2,1)S(1)}, u32[]{:S(2)}, u32[]{:S(2)}) collective-permute-start(bf16[24,1792]{1,0:T(8,128)(2,1)S(1)} %slice.202), channel_id=1, source_target_pairs={{0,16},{4,20},{8,24},{12,28},{16,0},{20,4},{24,8},{28,12},{1,17},{... | collective-permute-start | bytes 258056 | tf_op jit(solution)/shard_map/ppermute | solution.py:33
  81.0 5.9 %collective-permute-start.33 = (bf16[24,1792]{1,0:T(8,128)(2,1)S(1)}, bf16[24,1792]{1,0:T(8,128)(2,1)S(1)}, u32[]{:S(2)}, u32[]{:S(2)}) collective-permute-start(bf16[24,1792]{1,0:T(8,128)(2,1)S(1)} %get-tuple-element.9), channel_id=1, source_target_pairs={{0,8},{4,12},{8,0},{12,4},{16,24},{20,28},{24,16},{28,20},{1,9},{5... | collective-permute-start | bytes 258056 | tf_op jit(solution)/shard_map/ppermute | solution.py:44
  82.6 4.8 %collective-permute-start.21 = (bf16[24,1792]{1,0:T(8,128)(2,1)S(1)}, bf16[24,1792]{1,0:T(8,128)(2,1)S(1)}, u32[]{:S(2)}, u32[]{:S(2)}) collective-permute-start(bf16[24,1792]{1,0:T(8,128)(2,1)S(1)} %get-tuple-element.10), channel_id=1, source_target_pairs={{0,8},{4,12},{8,0},{12,4},{16,24},{20,28},{24,16},{28,20},{1,9},{5... | collective-permute-start | bytes 258056 | tf_op jit(solution)/shard_map/ppermute | solution.py:44
  83.1 5.9 %collective-permute-start.27 = (bf16[24,1792]{1,0:T(8,128)(2,1)S(1)}, bf16[24,1792]{1,0:T(8,128)(2,1)S(1)}, u32[]{:S(2)}, u32[]{:S(2)}) collective-permute-start(bf16[24,1792]{1,0:T(8,128)(2,1)S(1)} %get-tuple-element.11), channel_id=1, source_target_pairs={{0,8},{4,12},{8,0},{12,4},{16,24},{20,28},{24,16},{28,20},{1,9},{5... | collective-permute-start | bytes 258056 | tf_op jit(solution)/shard_map/ppermute | solution.py:44
  84.8 19.7 %copy-start = (bf16[24,1792]{1,0:T(8,128)(2,1)}, bf16[24,1792]{1,0:T(8,128)(2,1)S(1)}, u32[]{:S(2)}) copy-start(bf16[24,1792]{1,0:T(8,128)(2,1)S(1)} %get-tuple-element.6) | copy-start | bytes 258052
  84.8 19.7 %copy-start.4 = (bf16[24,1792]{1,0:T(8,128)(2,1)}, bf16[24,1792]{1,0:T(8,128)(2,1)S(1)}, u32[]{:S(2)}) copy-start(bf16[24,1792]{1,0:T(8,128)(2,1)S(1)} %get-tuple-element.7) | copy-start | bytes 258052
  84.8 20.2 %copy-start.2 = (bf16[24,1792]{1,0:T(8,128)(2,1)}, bf16[24,1792]{1,0:T(8,128)(2,1)S(1)}, u32[]{:S(2)}) copy-start(bf16[24,1792]{1,0:T(8,128)(2,1)S(1)} %get-tuple-element.8) | copy-start | bytes 258052
  84.8 5.5 %collective-permute-start.30 = (bf16[24,1792]{1,0:T(8,128)(2,1)S(1)}, bf16[24,1792]{1,0:T(8,128)(2,1)S(1)}, u32[]{:S(2)}, u32[]{:S(2)}) collective-permute-start(bf16[24,1792]{1,0:T(8,128)(2,1)S(1)} %get-tuple-element.6), channel_id=1, source_target_pairs={{0,16},{4,20},{8,24},{12,28},{16,0},{20,4},{24,8},{28,12},{1,17},{... | collective-permute-start | bytes 258056 | tf_op jit(solution)/shard_map/ppermute | solution.py:44
  85.4 6.7 %collective-permute-start.9 = (bf16[24,1792]{1,0:T(8,128)(2,1)S(1)}, bf16[24,1792]{1,0:T(8,128)(2,1)S(1)}, u32[]{:S(2)}, u32[]{:S(2)}) collective-permute-start(bf16[24,1792]{1,0:T(8,128)(2,1)S(1)} %get-tuple-element.7), channel_id=1, source_target_pairs={{0,16},{4,20},{8,24},{12,28},{16,0},{20,4},{24,8},{28,12},{1,17},{... | collective-permute-start | bytes 258056 | tf_op jit(solution)/shard_map/ppermute | solution.py:44
  86.9 7.1 %collective-permute-start.24 = (bf16[24,1792]{1,0:T(8,128)(2,1)S(1)}, bf16[24,1792]{1,0:T(8,128)(2,1)S(1)}, u32[]{:S(2)}, u32[]{:S(2)}) collective-permute-start(bf16[24,1792]{1,0:T(8,128)(2,1)S(1)} %get-tuple-element.8), channel_id=1, source_target_pairs={{0,16},{4,20},{8,24},{12,28},{16,0},{20,4},{24,8},{28,12},{1,17},{... | collective-permute-start | bytes 258056 | tf_op jit(solution)/shard_map/ppermute | solution.py:44
  87.5 10.2 %collective-permute-start.34 = (bf16[48,1792]{1,0:T(8,128)(2,1)S(1)}, bf16[48,1792]{1,0:T(8,128)(2,1)S(1)}, u32[]{:S(2)}, u32[]{:S(2)}) collective-permute-start(bf16[48,1792]{1,0:T(8,128)(2,1)S(1)} %pad_maximum_fusion.17), channel_id=1, source_target_pairs={{0,16},{4,20},{8,24},{12,28},{16,0},{20,4},{24,8},{28,12},{1,17},{... | collective-permute-start | bytes 516104 | tf_op jit(solution)/shard_map/ppermute | solution.py:44
  89.1 10.7 %collective-permute-start.22 = (bf16[48,1792]{1,0:T(8,128)(2,1)S(1)}, bf16[48,1792]{1,0:T(8,128)(2,1)S(1)}, u32[]{:S(2)}, u32[]{:S(2)}) collective-permute-start(bf16[48,1792]{1,0:T(8,128)(2,1)S(1)} %pad_maximum_fusion.13), channel_id=1, source_target_pairs={{0,16},{4,20},{8,24},{12,28},{16,0},{20,4},{24,8},{28,12},{1,17},{... | collective-permute-start | bytes 516104 | tf_op jit(solution)/shard_map/ppermute | solution.py:44
  90.3 15.7 %copy-start.16 = (bf16[24,1792]{1,0:T(8,128)(2,1)}, bf16[24,1792]{1,0:T(8,128)(2,1)S(1)}, u32[]{:S(2)}) copy-start(bf16[24,1792]{1,0:T(8,128)(2,1)S(1)} %collective-permute-done.30) | copy-start | bytes 258052
  90.3 11.3 %collective-permute-start.28 = (bf16[48,1792]{1,0:T(8,128)(2,1)S(1)}, bf16[48,1792]{1,0:T(8,128)(2,1)S(1)}, u32[]{:S(2)}, u32[]{:S(2)}) collective-permute-start(bf16[48,1792]{1,0:T(8,128)(2,1)S(1)} %pad_maximum_fusion.15), channel_id=1, source_target_pairs={{0,16},{4,20},{8,24},{12,28},{16,0},{20,4},{24,8},{28,12},{1,17},{... | collective-permute-start | bytes 516104 | tf_op jit(solution)/shard_map/ppermute | solution.py:44
  92.1 13.6 %copy-start.18 = (bf16[24,1792]{1,0:T(8,128)(2,1)}, bf16[24,1792]{1,0:T(8,128)(2,1)S(1)}, u32[]{:S(2)}) copy-start(bf16[24,1792]{1,0:T(8,128)(2,1)S(1)} %collective-permute-done.9) | copy-start | bytes 258052
  92.1 10.2 %collective-permute-start.31 = (bf16[48,1792]{1,0:T(8,128)(2,1)S(1)}, bf16[48,1792]{1,0:T(8,128)(2,1)S(1)}, u32[]{:S(2)}, u32[]{:S(2)}) collective-permute-start(bf16[48,1792]{1,0:T(8,128)(2,1)S(1)} %pad_maximum_fusion.16), channel_id=1, source_target_pairs={{0,8},{4,12},{8,0},{12,4},{16,24},{20,28},{24,16},{28,20},{1,9},{5... | collective-permute-start | bytes 516104 | tf_op jit(solution)/shard_map/ppermute | solution.py:44
  94.0 11.8 %copy-start.20 = (bf16[24,1792]{1,0:T(8,128)(2,1)}, bf16[24,1792]{1,0:T(8,128)(2,1)S(1)}, u32[]{:S(2)}) copy-start(bf16[24,1792]{1,0:T(8,128)(2,1)S(1)} %collective-permute-done.24) | copy-start | bytes 258052
  94.0 9.7 %collective-permute-start.10 = (bf16[48,1792]{1,0:T(8,128)(2,1)S(1)}, bf16[48,1792]{1,0:T(8,128)(2,1)S(1)}, u32[]{:S(2)}, u32[]{:S(2)}) collective-permute-start(bf16[48,1792]{1,0:T(8,128)(2,1)S(1)} %pad_maximum_fusion.12), channel_id=1, source_target_pairs={{0,8},{4,12},{8,0},{12,4},{16,24},{20,28},{24,16},{28,20},{1,9},{5... | collective-permute-start | bytes 516104 | tf_op jit(solution)/shard_map/ppermute | solution.py:44
  97.7 6.8 %collective-permute-start.25 = (bf16[48,1792]{1,0:T(8,128)(2,1)S(1)}, bf16[48,1792]{1,0:T(8,128)(2,1)S(1)}, u32[]{:S(2)}, u32[]{:S(2)}) collective-permute-start(bf16[48,1792]{1,0:T(8,128)(2,1)S(1)} %pad_maximum_fusion.14), channel_id=1, source_target_pairs={{0,8},{4,12},{8,0},{12,4},{16,24},{20,28},{24,16},{28,20},{1,9},{5... | collective-permute-start | bytes 516104 | tf_op jit(solution)/shard_map/ppermute | solution.py:44
  99.8 6.0 %collective-permute-start.35 = (bf16[96,1792]{1,0:T(8,128)(2,1)S(1)}, bf16[96,1792]{1,0:T(8,128)(2,1)S(1)}, u32[]{:S(2)}, u32[]{:S(2)}) collective-permute-start(bf16[96,1792]{1,0:T(8,128)(2,1)S(1)} %pad_maximum_fusion.10), channel_id=1, source_target_pairs={{0,4},{4,0},{8,12},{12,8},{16,20},{20,16},{24,28},{28,24},{1,5},{5... | collective-permute-start | bytes 1032200 | tf_op jit(solution)/shard_map/ppermute | solution.py:44
  101.6 5.0 %collective-permute-start.23 = (bf16[96,1792]{1,0:T(8,128)(2,1)}, bf16[96,1792]{1,0:T(8,128)(2,1)}, u32[]{:S(2)}, u32[]{:S(2)}) collective-permute-start(bf16[96,1792]{1,0:T(8,128)(2,1)} %pad_maximum_fusion.6), channel_id=1, source_target_pairs={{0,4},{4,0},{8,12},{12,8},{16,20},{20,16},{24,28},{28,24},{1,5},{5... | collective-permute-start | bytes 1032200 | tf_op jit(solution)/shard_map/ppermute | solution.py:44
  102.4 3.4 %copy-start.23 = (bf16[48,1792]{1,0:T(8,128)(2,1)}, bf16[48,1792]{1,0:T(8,128)(2,1)S(1)}, u32[]{:S(2)}) copy-start(bf16[48,1792]{1,0:T(8,128)(2,1)S(1)} %collective-permute-done.31) | copy-start | bytes 516100
  102.4 5.9 %collective-permute-start.29 = (bf16[96,1792]{1,0:T(8,128)(2,1)}, bf16[96,1792]{1,0:T(8,128)(2,1)}, u32[]{:S(2)}, u32[]{:S(2)}) collective-permute-start(bf16[96,1792]{1,0:T(8,128)(2,1)} %pad_maximum_fusion.8), channel_id=1, source_target_pairs={{0,4},{4,0},{8,12},{12,8},{16,20},{20,16},{24,28},{28,24},{1,5},{5... | collective-permute-start | bytes 1032200 | tf_op jit(solution)/shard_map/ppermute | solution.py:44
  103.6 2.2 %copy-start.25 = (bf16[48,1792]{1,0:T(8,128)(2,1)}, bf16[48,1792]{1,0:T(8,128)(2,1)S(1)}, u32[]{:S(2)}) copy-start(bf16[48,1792]{1,0:T(8,128)(2,1)S(1)} %collective-permute-done.10) | copy-start | bytes 516100
  103.6 32.1 %collective-permute-start.32 = (bf16[96,1792]{1,0:T(8,128)(2,1)}, bf16[96,1792]{1,0:T(8,128)(2,1)}, u32[]{:S(2)}, u32[]{:S(2)}) collective-permute-start(bf16[96,1792]{1,0:T(8,128)(2,1)} %pad_maximum_fusion.9), channel_id=1, source_target_pairs={{0,4},{4,0},{8,12},{12,8},{16,20},{20,16},{24,28},{28,24},{1,5},{5... | collective-permute-start | bytes 1032200 | tf_op jit(solution)/shard_map/ppermute | solution.py:44
  104.5 1.3 copy-start.27
  104.5 13.3 %collective-permute-start.11 = (bf16[96,1792]{1,0:T(8,128)(2,1)}, bf16[96,1792]{1,0:T(8,128)(2,1)}, u32[]{:S(2)}, u32[]{:S(2)}) collective-permute-start(bf16[96,1792]{1,0:T(8,128)(2,1)} %pad_maximum_fusion.5), channel_id=1, source_target_pairs={{0,4},{4,0},{8,12},{12,8},{16,20},{20,16},{24,28},{28,24},{1,5},{5... | collective-permute-start | bytes 1032200 | tf_op jit(solution)/shard_map/ppermute | solution.py:44
  105.8 5.2 %collective-permute-start.26 = (bf16[96,1792]{1,0:T(8,128)(2,1)}, bf16[96,1792]{1,0:T(8,128)(2,1)}, u32[]{:S(2)}, u32[]{:S(2)}) collective-permute-start(bf16[96,1792]{1,0:T(8,128)(2,1)} %pad_maximum_fusion.7), channel_id=1, source_target_pairs={{0,4},{4,0},{8,12},{12,8},{16,20},{20,16},{24,28},{28,24},{1,5},{5... | collective-permute-start | bytes 1032200 | tf_op jit(solution)/shard_map/ppermute | solution.py:44
  109.9 7.9 %slice-start.2 = ((s8[7340032]{0:T(1024)(128)(4,1)}), s8[4194304]{0:T(1024)(128)(4,1)S(1)}, s32[]{:S(2)}) async-start(s8[7340032]{0:T(1024)(128)(4,1)} %bitcast.38), calls=%async_computation.4 | async-start | bytes 8388608
  111.0 6.8 %copy-start.13 = (bf16[8,24,1792]{2,1,0:T(8,128)(2,1)}, bf16[8,24,1792]{2,1,0:T(8,128)(2,1)S(1)}, u32[]{:S(2)}) copy-start(bf16[8,24,1792]{2,1,0:T(8,128)(2,1)S(1)} %get-tuple-element.13) | copy-start | bytes 2064388
  111.0 10.6 %copy-start.15 = (bf16[8,24,1792]{2,1,0:T(8,128)(2,1)}, bf16[8,24,1792]{2,1,0:T(8,128)(2,1)S(1)}, u32[]{:S(2)}) copy-start(bf16[8,24,1792]{2,1,0:T(8,128)(2,1)S(1)} %get-tuple-element.14) | copy-start | bytes 2064388
  111.0 6.8 %copy-start.5 = (bf16[24,1792]{1,0:T(8,128)(2,1)S(1)}, bf16[24,1792]{1,0:T(8,128)(2,1)}, u32[]{:S(2)}) copy-start(bf16[24,1792]{1,0:T(8,128)(2,1)} %copy-done.4) | copy-start | bytes 258052
  111.0 6.8 %copy-start.19 = (bf16[24,1792]{1,0:T(8,128)(2,1)S(1)}, bf16[24,1792]{1,0:T(8,128)(2,1)}, u32[]{:S(2)}) copy-start(bf16[24,1792]{1,0:T(8,128)(2,1)} %copy-done.18) | copy-start | bytes 258052
  111.1 6.8 %copy-start.26 = (bf16[48,1792]{1,0:T(8,128)(2,1)S(1)}, bf16[48,1792]{1,0:T(8,128)(2,1)}, u32[]{:S(2)}) copy-start(bf16[48,1792]{1,0:T(8,128)(2,1)} %copy-done.25) | copy-start | bytes 516100
  111.1 6.8 %slice-start.3 = ((s8[7340032]{0:T(1024)(128)(4,1)}), s8[3145728]{0:T(1024)(128)(4,1)S(1)}, s32[]{:S(2)}) async-start(s8[7340032]{0:T(1024)(128)(4,1)} %bitcast.38), calls=%async_computation.5 | async-start | bytes 6291456
  123.1 6.5 %copy-start.14 = (bf16[8,24,1792]{2,1,0:T(8,128)(2,1)S(1)}, bf16[8,24,1792]{2,1,0:T(8,128)(2,1)}, u32[]{:S(2)}) copy-start(bf16[8,24,1792]{2,1,0:T(8,128)(2,1)} %copy-done.13) | copy-start | bytes 2064388
  123.1 6.5 %copy-start.22 = (bf16[24,1792]{1,0:T(8,128)(2,1)S(1)}, bf16[24,1792]{1,0:T(8,128)(2,1)}, u32[]{:S(2)}) copy-start(bf16[24,1792]{1,0:T(8,128)(2,1)} %copy-done.20) | copy-start | bytes 258052
  123.1 6.4 %copy-start.29 = (bf16[48,1792]{1,0:T(8,128)(2,1)S(1)}, bf16[48,1792]{1,0:T(8,128)(2,1)}, u32[]{:S(2)}) copy-start(bf16[48,1792]{1,0:T(8,128)(2,1)} %copy-done.27) | copy-start | bytes 516100
  129.5 6.3 %copy-start.1 = (bf16[24,1792]{1,0:T(8,128)(2,1)S(1)}, bf16[24,1792]{1,0:T(8,128)(2,1)}, u32[]{:S(2)}) copy-start(bf16[24,1792]{1,0:T(8,128)(2,1)} %copy-done) | copy-start | bytes 258052
  129.5 6.3 %copy-start.12 = (bf16[8,24,1792]{2,1,0:T(8,128)(2,1)S(1)}, bf16[8,24,1792]{2,1,0:T(8,128)(2,1)}, u32[]{:S(2)}) copy-start(bf16[8,24,1792]{2,1,0:T(8,128)(2,1)} %get-tuple-element.12) | copy-start | bytes 2064388
  129.5 6.3 %copy-start.17 = (bf16[24,1792]{1,0:T(8,128)(2,1)S(1)}, bf16[24,1792]{1,0:T(8,128)(2,1)}, u32[]{:S(2)}) copy-start(bf16[24,1792]{1,0:T(8,128)(2,1)} %copy-done.16) | copy-start | bytes 258052
  129.6 6.3 %copy-start.24 = (bf16[48,1792]{1,0:T(8,128)(2,1)S(1)}, bf16[48,1792]{1,0:T(8,128)(2,1)}, u32[]{:S(2)}) copy-start(bf16[48,1792]{1,0:T(8,128)(2,1)} %copy-done.23) | copy-start | bytes 516100
  (7 other events, 7.2 us)
Sparse Core Ops, SparseCore 0:
  123.2 18.9 reduce-scatter.1

commit v4 on v2

v4 whole, which is shorter than its diff:
```python
import jax
import jax.numpy as jnp
from jax import lax
from jax.sharding import PartitionSpec as P


def contract_first(left, right):
    return lax.dot_general(
        left, right, (((0,), (0,)), ((), ())), preferred_element_type=jnp.float32
    )


def contract_last(left, right):
    return lax.dot_general(
        left, right, (((1,), (1,)), ((), ())), preferred_element_type=jnp.float32
    )


def gated_grads(gate_sum, up_sum, grad_hidden):
    sigmoid_gate = jax.nn.sigmoid(gate_sum)
    hidden = (gate_sum * sigmoid_gate * up_sum).astype(jnp.bfloat16)
    grad_up = (grad_hidden * gate_sum * sigmoid_gate).astype(jnp.bfloat16)
    grad_gate = (
        grad_hidden * up_sum * sigmoid_gate * (1.0 + gate_sum * (1.0 - sigmoid_gate))
    ).astype(jnp.bfloat16)
    return (hidden, grad_gate, grad_up)


def halving_reduce(x, order, n_dev):
    r = lax.axis_index("row")
    cur = x
    for step, bit in enumerate(order):
        n = cur.shape[1] // 2
        hi = (r // bit) % 2
        keep = lax.dynamic_slice_in_dim(cur, hi * n, n, 1)
        send = lax.dynamic_slice_in_dim(cur, (1 - hi) * n, n, 1)
        got = lax.ppermute(send, "row", [(j, j ^ bit) for j in range(n_dev)])
        cur = keep.astype(jnp.float32) + got.astype(jnp.float32)
        if step + 1 < len(order):
            cur = cur.astype(jnp.bfloat16)
    return cur


def doubling_gather(x, order, n_dev):
    r = lax.axis_index("row")
    cur = x
    for bit in reversed(order):
        hi = (r // bit) % 2
        got = lax.ppermute(cur, "row", [(j, j ^ bit) for j in range(n_dev)])
        cur = jnp.where(hi == 1, jnp.concatenate([got, cur], axis=1), jnp.concatenate([cur, got], axis=1))
    return cur


def row_bits(n_dev, tokens, units):
    if n_dev < 2 or n_dev & (n_dev - 1) or tokens % n_dev or units % 2:
        return None
    bits, b = [], 1
    while b < n_dev:
        bits.append(b)
        b *= 2
    return bits


def row_gated(stacked, n_dev):
    _, tokens, units = stacked.shape
    bits = row_bits(n_dev, tokens, units)
    if bits is None:
        sums = lax.psum(stacked, "row").astype(jnp.float32)
        return jnp.stack(gated_grads(sums[0], sums[1], sums[2]))
    orders = (bits, bits[:1] + bits[:0:-1])
    half = units // 2
    reduced = [halving_reduce(stacked[:, :, h * half:(h + 1) * half], o, n_dev) for h, o in enumerate(orders)]
    outs = [doubling_gather(jnp.stack(gated_grads(red[0], red[1], red[2])), o, n_dev) for red, o in zip(reduced, orders)]
    return jnp.concatenate(outs, axis=2)


def col_gather(x, n_col):
    parts = [x]
    for s in range(1, n_col):
        parts.append(lax.ppermute(x, "col", [(j, (j + s) % n_col) for j in range(n_col)]))
    return jnp.concatenate(parts, axis=0)


def col_reduce_scatter(x, n_col):
    span = x.shape[0] // n_col
    total = x[:span].astype(jnp.float32)
    for s in range(1, n_col):
        got = lax.ppermute(x[s * span:(s + 1) * span], "col", [(j, (j - s) % n_col) for j in range(n_col)])
        total = total + got.astype(jnp.float32)
    return total.astype(jnp.bfloat16)


def body(tokens, grad_out, gate_weight, up_weight, down_weight):
    n_row = lax.psum(1, "row")
    n_col = lax.psum(1, "col")
    tok_all = col_gather(tokens, n_col)
    grad_all = col_gather(grad_out, n_col)
    tok_t = tok_all.T
    stacked = jnp.stack(
        [
            jnp.dot(tok_all, gate_weight, preferred_element_type=jnp.float32).astype(jnp.bfloat16),
            jnp.dot(tok_all, up_weight, preferred_element_type=jnp.float32).astype(jnp.bfloat16),
            contract_last(grad_all, down_weight).astype(jnp.bfloat16),
        ]
    )
    gated = row_gated(stacked, n_row)
    hidden, grad_gate, grad_up = gated[0], gated[1], gated[2]
    partial_grad = contract_last(grad_gate, gate_weight) + contract_last(grad_up, up_weight)
    partial_grad, grad_gate, grad_up, hidden = lax.optimization_barrier(
        (partial_grad.astype(jnp.bfloat16), grad_gate, grad_up, hidden)
    )
    grad_tokens = col_reduce_scatter(partial_grad, n_col)
    acc_gate = jnp.dot(tok_t, grad_gate, preferred_element_type=jnp.float32)
    acc_up = jnp.dot(tok_t, grad_up, preferred_element_type=jnp.float32)
    acc_down = contract_first(hidden, grad_all)
    return (
        grad_tokens,
        acc_gate.astype(jnp.bfloat16),
        acc_up.astype(jnp.bfloat16),
        acc_down.astype(jnp.bfloat16),
    )


def solution(mesh):
    return jax.shard_map(
        body,
        mesh=mesh,
        in_specs=(
            P("col", "row"),
            P("col", "row"),
            P("row", "col"),
            P("row", "col"),
            P("col", "row"),
        ),
        out_specs=(P("col", "row"), P("row", "col"), P("row", "col"), P("col", "row")),
        check_vma=False,
    )
```

time: 128 us -> 112 us (0.88)
  waiting for transfers between devices: 4.42 us -> 34.7 us
  blocking collectives: 21.3 us -> 0 us
  between operations: 14.8 us -> 1.02 us
  local copies, waits for them, and re-layouts: 15 us -> 6.29 us
  matrix products: 34.1 us -> 29.6 us
    all_gather x1 -> x0, blocking collectives: 21.3 us -> none  [body(): both_all = lax.all_gather(both, 'col', axis=0, tiled=True)]
    ppermute x0 -> x9, starting transfers between devices: none -> 19.2 us  [the longest x6 10.4 us: col_gather(): lax.ppermute(x, 'col', [(j, (j + s) % n_col) for j in range(n_col)])]
    ppermute x18 -> x6, waiting for transfers between devices: 1.29 us -> 16.2 us  [doubling_gather(): got = lax.ppermute(cur, 'row', [(j, j ^ bit) for j in range(n_dev)])]
    ppermute x18 -> x6, waiting for transfers between devices: 2.18 us -> 16.1 us  [halving_reduce(): got = lax.ppermute(send, 'row', [(j, j ^ bit) for j in range(n_dev)])]
    ppermute x18 -> x6, starting transfers between devices: 15.8 us -> 6.67 us  [halving_reduce(): got = lax.ppermute(send, 'row', [(j, j ^ bit) for j in range(n_dev)])]
    ppermute x18 -> x6, starting transfers between devices: 14.6 us -> 5.81 us  [doubling_gather(): got = lax.ppermute(cur, 'row', [(j, j ^ bit) for j in range(n_dev)])]
    dynamic_update_slice x30 -> x0, local copies, waits for them, and re-layouts: 8.09 us -> none  [the longest x18 4.5 us: doubling_gather(): out = lax.dynamic_update_slice_in_dim(out, g, (1 - hi) * n, 0)]
    select_n x0 -> x6, other arithmetic: none -> 3.52 us  [doubling_gather(): jnp.where(hi == 1, jnp.concatenate([got, cur], axis=1), jnp.concatenate([...]
  transfers between devices with their start and end apart: 37 -> 21, of which waited for: 6 -> 10; matrix products, arithmetic and copies ran while one was open for 39% -> 26% of each run, Pallas kernels for 0% -> 0%
where the time goes in v4:
time: 112 us; the launch traced here: 111 us
  waiting for transfers between devices  34.7 us (31%)
  starting transfers between devices  31.7 us (28%)
  matrix products  29.6 us (26%)
  other arithmetic  7.76 us (7%)
  local copies, waits for them, and re-layouts  6.29 us (6%)
    ppermute x6, waiting for transfers between devices, doubling_gather(): got = lax.ppermute(cur, 'row', [(j, j ^ bit) for j in range(n_dev)])  16.2 us
    ppermute x6, waiting for transfers between devices, halving_reduce(): got = lax.ppermute(send, 'row', [(j, j ^ bit) for j in range(n_dev)])  16.1 us
    ppermute x6, starting transfers between devices, col_gather(): lax.ppermute(x, 'col', [(j, (j + s) % n_col) for j in range(n_col)])  10.4 us
    ppermute x3, starting transfers between devices, col_reduce_scatter(): lax.ppermute(x[s * span:(s + 1) * span], 'col', [(j, (j - s) % n_col) for...  8.81 us
    dot_general x3, matrix products, contract_last(): lax.dot_general(left, right, (((1,), (1,)), ((), ())), preferred_element_...  7.59 us
    ppermute x6, starting transfers between devices, halving_reduce(): got = lax.ppermute(send, 'row', [(j, j ^ bit) for j in range(n_dev)])  6.67 us
    ppermute x6, starting transfers between devices, doubling_gather(): got = lax.ppermute(cur, 'row', [(j, j ^ bit) for j in range(n_dev)])  5.81 us
    dot_general x1, matrix products, contract_first(): lax.dot_general(left, right, (((0,), (0,)), ((), ())), preferred_element_...  5.19 us
  transfers between devices with their start and end apart: 21, of which 10 were waited for; matrix products, arithmetic and copies ran while one was open for 26% of the time, Pallas kernels for 0%

profile of v4, /device:TPU:0, one launch (start us, length us, event | category | flops | bytes accessed | tf_op | source)
XLA Modules:
  0.0 111.1 jit_solution(6860958871822673469)
XLA Ops:
  0.6 4.1 %collective-permute-start.1 = (bf16[48,1024]{1,0:T(8,128)(2,1)}, bf16[48,1024]{1,0:T(8,128)(2,1)S(1)}, u32[]{:S(2)}, u32[]{:S(2)}) collective-permute-start(bf16[48,1024]{1,0:T(8,128)(2,1)} %param.5), channel_id=1, source_target_pairs={{0,2},{1,3},{2,0},{3,1},{4,6},{5,7},{6,4},{7,5},{8,10},{9,11},{10,... | collective-permute-start | bytes 294920 | tf_op jit(solution)/shard_map/ppermute | solution.py:80
  4.8 1.6 %collective-permute-start = (bf16[48,1024]{1,0:T(8,128)(2,1)}, bf16[48,1024]{1,0:T(8,128)(2,1)S(1)}, u32[]{:S(2)}, u32[]{:S(2)}) collective-permute-start(bf16[48,1024]{1,0:T(8,128)(2,1)} %param.5), channel_id=1, source_target_pairs={{0,1},{1,2},{2,3},{3,0},{4,5},{5,6},{6,7},{7,4},{8,9},{9,10},{10,1... | collective-permute-start | bytes 294920 | tf_op jit(solution)/shard_map/ppermute | solution.py:80
  6.3 2.2 %collective-permute-start.2 = (bf16[48,1024]{1,0:T(8,128)(2,1)}, bf16[48,1024]{1,0:T(8,128)(2,1)S(1)}, u32[]{:S(2)}, u32[]{:S(2)}) collective-permute-start(bf16[48,1024]{1,0:T(8,128)(2,1)} %param.5), channel_id=1, source_target_pairs={{0,3},{1,0},{2,1},{3,2},{4,7},{5,4},{6,5},{7,6},{8,11},{9,8},{10,9... | collective-permute-start | bytes 294920 | tf_op jit(solution)/shard_map/ppermute | solution.py:80
  8.6 0.6 collective-permute-start.3
  9.2 0.9 constant_dynamic-update-slice_fusion.3
  10.1 0.9 constant_dynamic-update-slice_fusion.7
  11.0 1.5 %collective-permute-done = bf16[48,1024]{1,0:T(8,128)(2,1)S(1)} collective-permute-done((bf16[48,1024]{1,0:T(8,128)(2,1)}, bf16[48,1024]{1,0:T(8,128)(2,1)S(1)}, u32[]{:S(2)}, u32[]{:S(2)}) %collective-permute-start) | collective-permute-done | bytes 98336 | tf_op jit(solution)/shard_map/ppermute | solution.py:80
  12.4 1.8 %collective-permute-start.5 = (bf16[48,1024]{1,0:T(8,128)(2,1)}, bf16[48,1024]{1,0:T(8,128)(2,1)S(1)}, u32[]{:S(2)}, u32[]{:S(2)}) collective-permute-start(bf16[48,1024]{1,0:T(8,128)(2,1)} %param.6), channel_id=1, source_target_pairs={{0,3},{1,0},{2,1},{3,2},{4,7},{5,4},{6,5},{7,6},{8,11},{9,8},{10,9... | collective-permute-start | bytes 294920 | tf_op jit(solution)/shard_map/ppermute | solution.py:80
  14.3 0.0 copy-start.3
  14.3 0.0 slice-start
  14.4 4.8 %fusion.1 = bf16[1,192,3584]{2,1,0:T(8,128)(2,1)S(1)} fusion(bf16[192,1024]{1,0:T(8,128)(2,1)S(1)} %constant_dynamic-update-slice_fusion, bf16[1024,3584]{1,0:T(8,128)(2,1)} %param.8), kind=kOutput, calls=%fused_computation.7 | convolution fusion | flops 1409974272 | bytes 9109504 | tf_op jit(solution)/shard_map/dot_general | solution.py:102
  19.2 0.3 copy-done.3
  19.5 1.7 %fusion = bf16[1,192,3584]{2,1,0:T(8,128)(2,1)S(1)} fusion(bf16[192,1024]{1,0:T(8,128)(2,1)S(1)} %constant_dynamic-update-slice_fusion, bf16[1024,3584]{1,0:T(8,128)(2,1)S(1)} %copy-done.3), kind=kOutput, calls=%fused_computation.6 | convolution fusion | flops 1409974272 | bytes 9109504 | tf_op jit(solution)/shard_map/dot_general | solution.py:101
  21.2 0.9 collective-permute-done.5
  22.2 2.6 %fusion.2 = bf16[1,192,3584]{2,1,0:T(8,128)(2,1)S(1)} fusion(bf16[192,1024]{1,0:T(8,128)(2,1)S(1)} %constant_dynamic-update-slice_fusion.4, bf16[3584,1024]{1,0:T(8,128)(2,1)S(1)} %bitcast.29), kind=kOutput, calls=%fused_computation.8 | convolution fusion | flops 1409974272 | bytes 9109504 | tf_op jit(solution)/shard_map/dot_general | solution.py:14
  24.7 0.5 pad_maximum_fusion
  25.2 0.3 fusion.9
  25.5 1.1 %constant_dynamic-slice_fusion.5 = bf16[3,96,1792]{2,1,0:T(8,128)(2,1)} fusion(bf16[3,192,1792]{2,1,0:T(8,128)(2,1)S(1)} %get-tuple-element.16, s32[]{:T(128)S(6)} %select_n.131), kind=kLoop, calls=%fused_computation.58 | loop fusion | bytes 2064388 | tf_op jit(solution)/shard_map/dynamic_slice | solution.py:36
  26.7 1.0 constant_dynamic-slice_fusion.2
  27.7 0.5 collective-permute-start.12
  28.2 1.4 %collective-permute-done.6 = bf16[3,96,1792]{2,1,0:T(8,128)(2,1)} collective-permute-done((bf16[3,96,1792]{2,1,0:T(8,128)(2,1)}, bf16[3,96,1792]{2,1,0:T(8,128)(2,1)}, u32[]{:S(2)}, u32[]{:S(2)}) %collective-permute-start.6) | collective-permute-done | bytes 1032224 | tf_op jit(solution)/shard_map/ppermute | solution.py:37
  29.6 1.8 %add_convert_fusion.1 = bf16[3,96,1792]{2,1,0:T(8,128)(2,1)S(1)} fusion(bf16[3,96,1792]{2,1,0:T(8,128)(2,1)} %collective-permute-done.6, bf16[3,192,1792]{2,1,0:T(8,128)(2,1)} %copy-done, s32[]{:T(128)S(6)} %select_n.130), kind=kLoop, calls=%fused_computation.17 | loop fusion | flops 2064384 | bytes 3096580 | tf_op jit(solution)/shard_map/convert_element_type | solution.py:40
  31.5 1.5 %collective-permute-start.7 = (bf16[3,48,1792]{2,1,0:T(8,128)(2,1)S(1)}, bf16[3,48,1792]{2,1,0:T(8,128)(2,1)S(1)}, u32[]{:S(2)}, u32[]{:S(2)}) collective-permute-start(bf16[3,48,1792]{2,1,0:T(8,128)(2,1)S(1)} %constant_dynamic-slice_fusion.4), channel_id=1, source_target_pairs={{0,8},{4,12},{8,0},{12,4},{16,24},{20,28},{24,16},{28,20},{1,9},{5... | collective-permute-start | bytes 1548296 | tf_op jit(solution)/shard_map/ppermute | solution.py:37
  33.0 0.3 add_convert_fusion
  33.3 1.6 %collective-permute-start.13 = (bf16[3,48,1792]{2,1,0:T(8,128)(2,1)S(1)}, bf16[3,48,1792]{2,1,0:T(8,128)(2,1)S(1)}, u32[]{:S(2)}, u32[]{:S(2)}) collective-permute-start(bf16[3,48,1792]{2,1,0:T(8,128)(2,1)S(1)} %constant_dynamic-slice_fusion.1), channel_id=1, source_target_pairs={{0,16},{4,20},{8,24},{12,28},{16,0},{20,4},{24,8},{28,12},{1,17},{... | collective-permute-start | bytes 1548296 | tf_op jit(solution)/shard_map/ppermute | solution.py:37
  34.9 10.5 %collective-permute-done.7 = bf16[3,48,1792]{2,1,0:T(8,128)(2,1)S(1)} collective-permute-done((bf16[3,48,1792]{2,1,0:T(8,128)(2,1)S(1)}, bf16[3,48,1792]{2,1,0:T(8,128)(2,1)S(1)}, u32[]{:S(2)}, u32[]{:S(2)}) %collective-permute-start.7) | collective-permute-done | bytes 516128 | tf_op jit(solution)/shard_map/ppermute | solution.py:37
  45.3 0.1 add_convert_fusion.3
  45.5 1.5 %collective-permute-start.8 = (bf16[3,24,1792]{2,1,0:T(8,128)(2,1)S(1)}, bf16[3,24,1792]{2,1,0:T(8,128)(2,1)S(1)}, u32[]{:S(2)}, u32[]{:S(2)}) collective-permute-start(bf16[3,24,1792]{2,1,0:T(8,128)(2,1)S(1)} %constant_dynamic-slice_fusion.3), channel_id=1, source_target_pairs={{0,16},{4,20},{8,24},{12,28},{16,0},{20,4},{24,8},{28,12},{1,17},{... | collective-permute-start | bytes 774152 | tf_op jit(solution)/shard_map/ppermute | solution.py:37
  47.0 0.1 add_convert_fusion.2
  47.2 1.5 %collective-permute-start.14 = (bf16[3,24,1792]{2,1,0:T(8,128)(2,1)S(1)}, bf16[3,24,1792]{2,1,0:T(8,128)(2,1)S(1)}, u32[]{:S(2)}, u32[]{:S(2)}) collective-permute-start(bf16[3,24,1792]{2,1,0:T(8,128)(2,1)S(1)} %constant_dynamic-slice_fusion), channel_id=1, source_target_pairs={{0,8},{4,12},{8,0},{12,4},{16,24},{20,28},{24,16},{28,20},{1,9},{5... | collective-permute-start | bytes 774152 | tf_op jit(solution)/shard_map/ppermute | solution.py:37
  48.7 4.2 %collective-permute-done.8 = bf16[3,24,1792]{2,1,0:T(8,128)(2,1)S(1)} collective-permute-done((bf16[3,24,1792]{2,1,0:T(8,128)(2,1)S(1)}, bf16[3,24,1792]{2,1,0:T(8,128)(2,1)S(1)}, u32[]{:S(2)}, u32[]{:S(2)}) %collective-permute-start.8) | collective-permute-done | bytes 258080 | tf_op jit(solution)/shard_map/ppermute | solution.py:37
  53.0 0.1 convert_add_fusion.1
  53.0 0.1 multiply_convert_fusion.5
  53.2 1.5 %collective-permute-start.9 = (bf16[3,24,1792]{2,1,0:T(8,128)(2,1)S(1)}, bf16[3,24,1792]{2,1,0:T(8,128)(2,1)S(1)}, u32[]{:S(2)}, u32[]{:S(2)}) collective-permute-start(bf16[3,24,1792]{2,1,0:T(8,128)(2,1)S(1)} %pad_maximum_fusion.2), channel_id=1, source_target_pairs={{0,16},{4,20},{8,24},{12,28},{16,0},{20,4},{24,8},{28,12},{1,17},{... | collective-permute-start | bytes 774152 | tf_op jit(solution)/shard_map/ppermute | solution.py:49
  54.7 0.1 convert_add_fusion
  54.8 0.1 multiply_convert_fusion.2
  54.9 1.5 %collective-permute-start.15 = (bf16[3,24,1792]{2,1,0:T(8,128)(2,1)S(1)}, bf16[3,24,1792]{2,1,0:T(8,128)(2,1)S(1)}, u32[]{:S(2)}, u32[]{:S(2)}) collective-permute-start(bf16[3,24,1792]{2,1,0:T(8,128)(2,1)S(1)} %pad_maximum_fusion.3), channel_id=1, source_target_pairs={{0,8},{4,12},{8,0},{12,4},{16,24},{20,28},{24,16},{28,20},{1,9},{5... | collective-permute-start | bytes 774152 | tf_op jit(solution)/shard_map/ppermute | solution.py:49
  56.5 3.3 %collective-permute-done.9 = bf16[3,24,1792]{2,1,0:T(8,128)(2,1)S(1)} collective-permute-done((bf16[3,24,1792]{2,1,0:T(8,128)(2,1)S(1)}, bf16[3,24,1792]{2,1,0:T(8,128)(2,1)S(1)}, u32[]{:S(2)}, u32[]{:S(2)}) %collective-permute-start.9) | collective-permute-done | bytes 258080 | tf_op jit(solution)/shard_map/ppermute | solution.py:49
  59.8 0.1 maximum_select_fusion.4
  59.9 1.5 %collective-permute-start.10 = (bf16[3,48,1792]{2,1,0:T(8,128)(2,1)S(1)}, bf16[3,48,1792]{2,1,0:T(8,128)(2,1)S(1)}, u32[]{:S(2)}, u32[]{:S(2)}) collective-permute-start(bf16[3,48,1792]{2,1,0:T(8,128)(2,1)S(1)} %maximum_select_fusion.4), channel_id=1, source_target_pairs={{0,8},{4,12},{8,0},{12,4},{16,24},{20,28},{24,16},{28,20},{1,9},{5... | collective-permute-start | bytes 1548296 | tf_op jit(solution)/shard_map/ppermute | solution.py:49
  61.4 1.1 %collective-permute-done.15 = bf16[3,24,1792]{2,1,0:T(8,128)(2,1)S(1)} collective-permute-done((bf16[3,24,1792]{2,1,0:T(8,128)(2,1)S(1)}, bf16[3,24,1792]{2,1,0:T(8,128)(2,1)S(1)}, u32[]{:S(2)}, u32[]{:S(2)}) %collective-permute-start.15) | collective-permute-done | bytes 258080 | tf_op jit(solution)/shard_map/ppermute | solution.py:49
  62.5 0.1 maximum_select_fusion.5
  62.6 0.6 collective-permute-start.16
  63.2 9.1 %collective-permute-done.10 = bf16[3,48,1792]{2,1,0:T(8,128)(2,1)S(1)} collective-permute-done((bf16[3,48,1792]{2,1,0:T(8,128)(2,1)S(1)}, bf16[3,48,1792]{2,1,0:T(8,128)(2,1)S(1)}, u32[]{:S(2)}, u32[]{:S(2)}) %collective-permute-start.10) | collective-permute-done | bytes 516128 | tf_op jit(solution)/shard_map/ppermute | solution.py:49
  72.4 0.3 maximum_select_fusion.2
  72.6 0.1 collective-permute-start.11
  72.7 0.3 maximum_select_fusion.3
  73.0 0.6 collective-permute-start.17
  73.5 1.8 %collective-permute-done.11 = bf16[3,96,1792]{2,1,0:T(8,128)(2,1)S(1)} collective-permute-done((bf16[3,96,1792]{2,1,0:T(8,128)(2,1)S(1)}, bf16[3,96,1792]{2,1,0:T(8,128)(2,1)S(1)}, u32[]{:S(2)}, u32[]{:S(2)}) %collective-permute-start.11) | collective-permute-done | bytes 1032224 | tf_op jit(solution)/shard_map/ppermute | solution.py:49
  75.3 0.8 maximum_select_fusion
  76.1 0.8 collective-permute-done.17
  77.0 2.0 %maximum_select_fusion.1 = bf16[3,192,1792]{2,1,0:T(8,128)(2,1)S(1)} fusion(bf16[3,96,1792]{2,1,0:T(8,128)(2,1)S(1)} %maximum_select_fusion.3, bf16[3,96,1792]{2,1,0:T(8,128)(2,1)} %collective-permute-done.17, pred[]{:T(512)S(6)} %eq.25), kind=kLoop, calls=%fused_computation.15 | loop fusion | flops 9289728 | bytes 4128769 | tf_op jit(solution)/shard_map/jit(_where)/select_n | solution.py:50
  79.0 0.0 slice-start.3
  79.0 0.0 slice-start.4
  79.0 0.4 fusion.7
  79.4 1.5 %slice-done.3 = s8[3145728]{0:T(1024)(128)(4,1)S(1)} async-done(((s8[7340032]{0:T(1024)(128)(4,1)}), s8[3145728]{0:T(1024)(128)(4,1)S(1)}, s32[]{:S(2)}) %slice-start.3) | async-done | bytes 3145752
  80.9 2.5 %fusion.11 = f32[192,1024]{1,0:T(8,128)S(1)} fusion(bf16[192,3584]{1,0:T(8,128)(2,1)S(1)} %get-tuple-element.10, bf16[1024,3584]{1,0:T(8,128)(2,1)S(1)} %bitcast.31), kind=kOutput, calls=%fused_computation.61 | convolution fusion | flops 1409286144 | bytes 9502720 | tf_op jit(solution)/shard_map/dot_general | solution.py:14
  83.4 2.5 %fusion.8 = bf16[192,1024]{1,0:T(8,128)(2,1)S(1)} fusion(f32[192,1024]{1,0:T(8,128)S(1)} %fusion.11, bf16[192,3584]{1,0:T(8,128)(2,1)S(1)} %get-tuple-element.9, bf16[1024,3584]{1,0:T(8,128)(2,1)S(1)} %bitcast.33), kind=kOutput, calls=%fused_computation.25 | convolution fusion | flops 1409679360 | bytes 9895936 | tf_op jit(solution)/shard_map/dot_general | solution.py:14
  86.0 8.0 %collective-permute-start.18 = (bf16[48,1024]{1,0:T(8,128)(2,1)S(1)}, bf16[48,1024]{1,0:T(8,128)(2,1)S(1)}, u32[]{:S(2)}, u32[]{:S(2)}) collective-permute-start(bf16[48,1024]{1,0:T(8,128)(2,1)S(1)} %get-tuple-element.23), channel_id=1, source_target_pairs={{0,3},{1,0},{2,1},{3,2},{4,7},{5,4},{6,5},{7,6},{8,11},{9,8},{10,9... | collective-permute-start | bytes 294920 | tf_op jit(solution)/shard_map/ppermute | solution.py:88
  94.0 0.8 collective-permute-start.19
  94.8 5.2 %convolution_convert_fusion.2 = bf16[1024,3584]{1,0:T(8,128)(2,1)} fusion(bf16[192,1024]{1,0:T(8,128)(2,1)S(1)} %constant_dynamic-update-slice_fusion, bf16[192,3584]{1,0:T(8,128)(2,1)S(1)} %get-tuple-element.9), kind=kOutput, calls=%fused_computation.2 | convolution fusion | flops 1412956160 | bytes 9109504 | tf_op jit(solution)/shard_map/dot_general | solution.py:113
  100.0 5.2 %convolution_convert_fusion.1 = bf16[1024,3584]{1,0:T(8,128)(2,1)} fusion(bf16[192,1024]{1,0:T(8,128)(2,1)S(1)} %constant_dynamic-update-slice_fusion, bf16[192,3584]{1,0:T(8,128)(2,1)S(1)} %get-tuple-element.10), kind=kOutput, calls=%fused_computation.1 | convolution fusion | flops 1412956160 | bytes 9109504 | tf_op jit(solution)/shard_map/dot_general | solution.py:114
  105.2 5.2 %convolution_convert_fusion = bf16[3584,1024]{1,0:T(8,128)(2,1)} fusion(bf16[192,3584]{1,0:T(8,128)(2,1)S(1)} %get-tuple-element.11, bf16[192,1024]{1,0:T(8,128)(2,1)S(1)} %copy-done.2), kind=kOutput, calls=%fused_computation | convolution fusion | flops 1412956160 | bytes 9109504 | tf_op jit(solution)/shard_map/dot_general | solution.py:8
  110.4 0.7 add_convert_fusion.4
  (44 shorter events, 0.3 us)
Async XLA Ops:
  0.6 13.7 %collective-permute-start.1 = (bf16[48,1024]{1,0:T(8,128)(2,1)}, bf16[48,1024]{1,0:T(8,128)(2,1)S(1)}, u32[]{:S(2)}, u32[]{:S(2)}) collective-permute-start(bf16[48,1024]{1,0:T(8,128)(2,1)} %param.5), channel_id=1, source_target_pairs={{0,2},{1,3},{2,0},{3,1},{4,6},{5,7},{6,4},{7,5},{8,10},{9,11},{10,... | collective-permute-start | bytes 294920 | tf_op jit(solution)/shard_map/ppermute | solution.py:80
  4.8 7.7 %collective-permute-start = (bf16[48,1024]{1,0:T(8,128)(2,1)}, bf16[48,1024]{1,0:T(8,128)(2,1)S(1)}, u32[]{:S(2)}, u32[]{:S(2)}) collective-permute-start(bf16[48,1024]{1,0:T(8,128)(2,1)} %param.5), channel_id=1, source_target_pairs={{0,1},{1,2},{2,3},{3,0},{4,5},{5,6},{6,7},{7,4},{8,9},{9,10},{10,1... | collective-permute-start | bytes 294920 | tf_op jit(solution)/shard_map/ppermute | solution.py:80
  6.3 8.0 %collective-permute-start.2 = (bf16[48,1024]{1,0:T(8,128)(2,1)}, bf16[48,1024]{1,0:T(8,128)(2,1)S(1)}, u32[]{:S(2)}, u32[]{:S(2)}) collective-permute-start(bf16[48,1024]{1,0:T(8,128)(2,1)} %param.5), channel_id=1, source_target_pairs={{0,3},{1,0},{2,1},{3,2},{4,7},{5,4},{6,5},{7,6},{8,11},{9,8},{10,9... | collective-permute-start | bytes 294920 | tf_op jit(solution)/shard_map/ppermute | solution.py:80
  8.6 12.6 %collective-permute-start.4 = (bf16[48,1024]{1,0:T(8,128)(2,1)}, bf16[48,1024]{1,0:T(8,128)(2,1)S(1)}, u32[]{:S(2)}, u32[]{:S(2)}) collective-permute-start(bf16[48,1024]{1,0:T(8,128)(2,1)} %param.6), channel_id=1, source_target_pairs={{0,2},{1,3},{2,0},{3,1},{4,6},{5,7},{6,4},{7,5},{8,10},{9,11},{10,... | collective-permute-start | bytes 294920 | tf_op jit(solution)/shard_map/ppermute | solution.py:80
  8.6 12.6 %collective-permute-start.3 = (bf16[48,1024]{1,0:T(8,128)(2,1)}, bf16[48,1024]{1,0:T(8,128)(2,1)S(1)}, u32[]{:S(2)}, u32[]{:S(2)}) collective-permute-start(bf16[48,1024]{1,0:T(8,128)(2,1)} %param.6), channel_id=1, source_target_pairs={{0,1},{1,2},{2,3},{3,0},{4,5},{5,6},{6,7},{7,4},{8,9},{9,10},{10,1... | collective-permute-start | bytes 294920 | tf_op jit(solution)/shard_map/ppermute | solution.py:80
  12.4 9.7 %collective-permute-start.5 = (bf16[48,1024]{1,0:T(8,128)(2,1)}, bf16[48,1024]{1,0:T(8,128)(2,1)S(1)}, u32[]{:S(2)}, u32[]{:S(2)}) collective-permute-start(bf16[48,1024]{1,0:T(8,128)(2,1)} %param.6), channel_id=1, source_target_pairs={{0,3},{1,0},{2,1},{3,2},{4,7},{5,4},{6,5},{7,6},{8,11},{9,8},{10,9... | collective-permute-start | bytes 294920 | tf_op jit(solution)/shard_map/ppermute | solution.py:80
  14.3 5.2 %copy-start.3 = (bf16[1024,3584]{1,0:T(8,128)(2,1)S(1)}, bf16[1024,3584]{1,0:T(8,128)(2,1)}, u32[]{:S(2)}) copy-start(bf16[1024,3584]{1,0:T(8,128)(2,1)} %param.7) | copy-start | bytes 22020100
  14.3 7.8 %slice-start = ((s8[7340032]{0:T(1024)(128)(4,1)}), s8[4194304]{0:T(1024)(128)(4,1)S(1)}, s32[]{:S(2)}) async-start(s8[7340032]{0:T(1024)(128)(4,1)} %bitcast.28), calls=%async_computation | async-start | bytes 8388608
  19.5 2.6 %slice-start.1 = ((s8[7340032]{0:T(1024)(128)(4,1)}), s8[3145728]{0:T(1024)(128)(4,1)S(1)}, s32[]{:S(2)}) async-start(s8[7340032]{0:T(1024)(128)(4,1)} %bitcast.28), calls=%async_computation.1 | async-start | bytes 6291456
  22.2 2.6 %copy-start.1 = (bf16[192,1024]{1,0:T(8,128)(2,1)}, bf16[192,1024]{1,0:T(8,128)(2,1)S(1)}, u32[]{:S(2)}) copy-start(bf16[192,1024]{1,0:T(8,128)(2,1)S(1)} %constant_dynamic-update-slice_fusion.4) | copy-start | bytes 1179652
  25.5 2.2 %copy-start = (bf16[3,192,1792]{2,1,0:T(8,128)(2,1)}, bf16[3,192,1792]{2,1,0:T(8,128)(2,1)S(1)}, u32[]{:S(2)}) copy-start(bf16[3,192,1792]{2,1,0:T(8,128)(2,1)S(1)} %get-tuple-element.16) | copy-start | bytes 6193156
  26.7 3.0 %collective-permute-start.6 = (bf16[3,96,1792]{2,1,0:T(8,128)(2,1)}, bf16[3,96,1792]{2,1,0:T(8,128)(2,1)}, u32[]{:S(2)}, u32[]{:S(2)}) collective-permute-start(bf16[3,96,1792]{2,1,0:T(8,128)(2,1)} %constant_dynamic-slice_fusion.5), channel_id=1, source_target_pairs={{0,4},{4,0},{8,12},{12,8},{16,20},{20,16},{24,28},{28,24},{1,5},{5... | collective-permute-start | bytes 3096584 | tf_op jit(solution)/shard_map/ppermute | solution.py:37
  27.7 5.3 %collective-permute-start.12 = (bf16[3,96,1792]{2,1,0:T(8,128)(2,1)}, bf16[3,96,1792]{2,1,0:T(8,128)(2,1)S(1)}, u32[]{:S(2)}, u32[]{:S(2)}) collective-permute-start(bf16[3,96,1792]{2,1,0:T(8,128)(2,1)} %constant_dynamic-slice_fusion.2), channel_id=1, source_target_pairs={{0,4},{4,0},{8,12},{12,8},{16,20},{20,16},{24,28},{28,24},{1,5},{5... | collective-permute-start | bytes 3096584 | tf_op jit(solution)/shard_map/ppermute | solution.py:37
  31.5 13.9 %collective-permute-start.7 = (bf16[3,48,1792]{2,1,0:T(8,128)(2,1)S(1)}, bf16[3,48,1792]{2,1,0:T(8,128)(2,1)S(1)}, u32[]{:S(2)}, u32[]{:S(2)}) collective-permute-start(bf16[3,48,1792]{2,1,0:T(8,128)(2,1)S(1)} %constant_dynamic-slice_fusion.4), channel_id=1, source_target_pairs={{0,8},{4,12},{8,0},{12,4},{16,24},{20,28},{24,16},{28,20},{1,9},{5... | collective-permute-start | bytes 1548296 | tf_op jit(solution)/shard_map/ppermute | solution.py:37
  33.3 13.7 %collective-permute-start.13 = (bf16[3,48,1792]{2,1,0:T(8,128)(2,1)S(1)}, bf16[3,48,1792]{2,1,0:T(8,128)(2,1)S(1)}, u32[]{:S(2)}, u32[]{:S(2)}) collective-permute-start(bf16[3,48,1792]{2,1,0:T(8,128)(2,1)S(1)} %constant_dynamic-slice_fusion.1), channel_id=1, source_target_pairs={{0,16},{4,20},{8,24},{12,28},{16,0},{20,4},{24,8},{28,12},{1,17},{... | collective-permute-start | bytes 1548296 | tf_op jit(solution)/shard_map/ppermute | solution.py:37
  45.5 7.5 %collective-permute-start.8 = (bf16[3,24,1792]{2,1,0:T(8,128)(2,1)S(1)}, bf16[3,24,1792]{2,1,0:T(8,128)(2,1)S(1)}, u32[]{:S(2)}, u32[]{:S(2)}) collective-permute-start(bf16[3,24,1792]{2,1,0:T(8,128)(2,1)S(1)} %constant_dynamic-slice_fusion.3), channel_id=1, source_target_pairs={{0,16},{4,20},{8,24},{12,28},{16,0},{20,4},{24,8},{28,12},{1,17},{... | collective-permute-start | bytes 774152 | tf_op jit(solution)/shard_map/ppermute | solution.py:37
  47.2 7.5 %collective-permute-start.14 = (bf16[3,24,1792]{2,1,0:T(8,128)(2,1)S(1)}, bf16[3,24,1792]{2,1,0:T(8,128)(2,1)S(1)}, u32[]{:S(2)}, u32[]{:S(2)}) collective-permute-start(bf16[3,24,1792]{2,1,0:T(8,128)(2,1)S(1)} %constant_dynamic-slice_fusion), channel_id=1, source_target_pairs={{0,8},{4,12},{8,0},{12,4},{16,24},{20,28},{24,16},{28,20},{1,9},{5... | collective-permute-start | bytes 774152 | tf_op jit(solution)/shard_map/ppermute | solution.py:37
  53.2 6.6 %collective-permute-start.9 = (bf16[3,24,1792]{2,1,0:T(8,128)(2,1)S(1)}, bf16[3,24,1792]{2,1,0:T(8,128)(2,1)S(1)}, u32[]{:S(2)}, u32[]{:S(2)}) collective-permute-start(bf16[3,24,1792]{2,1,0:T(8,128)(2,1)S(1)} %pad_maximum_fusion.2), channel_id=1, source_target_pairs={{0,16},{4,20},{8,24},{12,28},{16,0},{20,4},{24,8},{28,12},{1,17},{... | collective-permute-start | bytes 774152 | tf_op jit(solution)/shard_map/ppermute | solution.py:49
  54.9 7.6 %collective-permute-start.15 = (bf16[3,24,1792]{2,1,0:T(8,128)(2,1)S(1)}, bf16[3,24,1792]{2,1,0:T(8,128)(2,1)S(1)}, u32[]{:S(2)}, u32[]{:S(2)}) collective-permute-start(bf16[3,24,1792]{2,1,0:T(8,128)(2,1)S(1)} %pad_maximum_fusion.3), channel_id=1, source_target_pairs={{0,8},{4,12},{8,0},{12,4},{16,24},{20,28},{24,16},{28,20},{1,9},{5... | collective-permute-start | bytes 774152 | tf_op jit(solution)/shard_map/ppermute | solution.py:49
  59.9 12.5 %collective-permute-start.10 = (bf16[3,48,1792]{2,1,0:T(8,128)(2,1)S(1)}, bf16[3,48,1792]{2,1,0:T(8,128)(2,1)S(1)}, u32[]{:S(2)}, u32[]{:S(2)}) collective-permute-start(bf16[3,48,1792]{2,1,0:T(8,128)(2,1)S(1)} %maximum_select_fusion.4), channel_id=1, source_target_pairs={{0,8},{4,12},{8,0},{12,4},{16,24},{20,28},{24,16},{28,20},{1,9},{5... | collective-permute-start | bytes 1548296 | tf_op jit(solution)/shard_map/ppermute | solution.py:49
  62.6 10.1 %collective-permute-start.16 = (bf16[3,48,1792]{2,1,0:T(8,128)(2,1)S(1)}, bf16[3,48,1792]{2,1,0:T(8,128)(2,1)S(1)}, u32[]{:S(2)}, u32[]{:S(2)}) collective-permute-start(bf16[3,48,1792]{2,1,0:T(8,128)(2,1)S(1)} %maximum_select_fusion.5), channel_id=1, source_target_pairs={{0,16},{4,20},{8,24},{12,28},{16,0},{20,4},{24,8},{28,12},{1,17},{... | collective-permute-start | bytes 1548296 | tf_op jit(solution)/shard_map/ppermute | solution.py:49
  72.6 2.7 %collective-permute-start.11 = (bf16[3,96,1792]{2,1,0:T(8,128)(2,1)S(1)}, bf16[3,96,1792]{2,1,0:T(8,128)(2,1)S(1)}, u32[]{:S(2)}, u32[]{:S(2)}) collective-permute-start(bf16[3,96,1792]{2,1,0:T(8,128)(2,1)S(1)} %maximum_select_fusion.2), channel_id=1, source_target_pairs={{0,4},{4,0},{8,12},{12,8},{16,20},{20,16},{24,28},{28,24},{1,5},{5... | collective-permute-start | bytes 3096584 | tf_op jit(solution)/shard_map/ppermute | solution.py:49
  73.0 4.0 %collective-permute-start.17 = (bf16[3,96,1792]{2,1,0:T(8,128)(2,1)S(1)}, bf16[3,96,1792]{2,1,0:T(8,128)(2,1)}, u32[]{:S(2)}, u32[]{:S(2)}) collective-permute-start(bf16[3,96,1792]{2,1,0:T(8,128)(2,1)S(1)} %maximum_select_fusion.3), channel_id=1, source_target_pairs={{0,4},{4,0},{8,12},{12,8},{16,20},{20,16},{24,28},{28,24},{1,5},{5... | collective-permute-start | bytes 3096584 | tf_op jit(solution)/shard_map/ppermute | solution.py:49
  75.3 4.1 %slice-start.2 = ((s8[7340032]{0:T(1024)(128)(4,1)}), s8[4194304]{0:T(1024)(128)(4,1)S(1)}, s32[]{:S(2)}) async-start(s8[7340032]{0:T(1024)(128)(4,1)} %bitcast.30), calls=%async_computation.2 | async-start | bytes 8388608
  79.0 1.9 %slice-start.3 = ((s8[7340032]{0:T(1024)(128)(4,1)}), s8[3145728]{0:T(1024)(128)(4,1)S(1)}, s32[]{:S(2)}) async-start(s8[7340032]{0:T(1024)(128)(4,1)} %bitcast.30), calls=%async_computation.3 | async-start | bytes 6291456
  79.0 4.4 %slice-start.4 = ((s8[7340032]{0:T(1024)(128)(4,1)}), s8[4194304]{0:T(1024)(128)(4,1)S(1)}, s32[]{:S(2)}) async-start(s8[7340032]{0:T(1024)(128)(4,1)} %bitcast.32), calls=%async_computation.4 | async-start | bytes 8388608
  80.9 2.5 %slice-start.5 = ((s8[7340032]{0:T(1024)(128)(4,1)}), s8[3145728]{0:T(1024)(128)(4,1)S(1)}, s32[]{:S(2)}) async-start(s8[7340032]{0:T(1024)(128)(4,1)} %bitcast.32), calls=%async_computation.5 | async-start | bytes 6291456
  86.0 24.4 %collective-permute-start.18 = (bf16[48,1024]{1,0:T(8,128)(2,1)S(1)}, bf16[48,1024]{1,0:T(8,128)(2,1)S(1)}, u32[]{:S(2)}, u32[]{:S(2)}) collective-permute-start(bf16[48,1024]{1,0:T(8,128)(2,1)S(1)} %get-tuple-element.23), channel_id=1, source_target_pairs={{0,3},{1,0},{2,1},{3,2},{4,7},{5,4},{6,5},{7,6},{8,11},{9,8},{10,9... | collective-permute-start | bytes 294920 | tf_op jit(solution)/shard_map/ppermute | solution.py:88
  94.0 16.4 %collective-permute-start.20 = (bf16[48,1024]{1,0:T(8,128)(2,1)S(1)}, bf16[48,1024]{1,0:T(8,128)(2,1)S(1)}, u32[]{:S(2)}, u32[]{:S(2)}) collective-permute-start(bf16[48,1024]{1,0:T(8,128)(2,1)S(1)} %get-tuple-element.24), channel_id=1, source_target_pairs={{0,1},{1,2},{2,3},{3,0},{4,5},{5,6},{6,7},{7,4},{8,9},{9,10},{10,1... | collective-permute-start | bytes 294920 | tf_op jit(solution)/shard_map/ppermute | solution.py:88
  94.0 16.4 %collective-permute-start.19 = (bf16[48,1024]{1,0:T(8,128)(2,1)S(1)}, bf16[48,1024]{1,0:T(8,128)(2,1)S(1)}, u32[]{:S(2)}, u32[]{:S(2)}) collective-permute-start(bf16[48,1024]{1,0:T(8,128)(2,1)S(1)} %get-tuple-element.25), channel_id=1, source_target_pairs={{0,2},{1,3},{2,0},{3,1},{4,6},{5,7},{6,4},{7,5},{8,10},{9,11},{10,... | collective-permute-start | bytes 294920 | tf_op jit(solution)/shard_map/ppermute | solution.py:88
  100.0 5.2 %copy-start.2 = (bf16[192,1024]{1,0:T(8,128)(2,1)S(1)}, bf16[192,1024]{1,0:T(8,128)(2,1)}, u32[]{:S(2)}) copy-start(bf16[192,1024]{1,0:T(8,128)(2,1)} %copy-done.1) | copy-start | bytes 1179652

commit v5 on v4

--- a/solution.py
+++ b/solution.py
@@ -61,15 +61,22 @@
     return bits
 
 
-def row_gated(stacked, n_dev):
+def row_reduce(stacked, n_dev):
     _, tokens, units = stacked.shape
     bits = row_bits(n_dev, tokens, units)
     if bits is None:
-        sums = lax.psum(stacked, "row").astype(jnp.float32)
-        return jnp.stack(gated_grads(sums[0], sums[1], sums[2]))
+        return (lax.psum(stacked, "row").astype(jnp.float32),)
     orders = (bits, bits[:1] + bits[:0:-1])
     half = units // 2
-    reduced = [halving_reduce(stacked[:, :, h * half:(h + 1) * half], o, n_dev) for h, o in enumerate(orders)]
+    return tuple(halving_reduce(stacked[:, :, h * half:(h + 1) * half], o, n_dev) for h, o in enumerate(orders))
+
+
+def row_gather_gated(reduced, n_dev):
+    if len(reduced) == 1:
+        sums = reduced[0]
+        return jnp.stack(gated_grads(sums[0], sums[1], sums[2]))
+    bits = row_bits(n_dev, n_dev, 2)
+    orders = (bits, bits[:1] + bits[:0:-1])
     outs = [doubling_gather(jnp.stack(gated_grads(red[0], red[1], red[2])), o, n_dev) for red, o in zip(reduced, orders)]
     return jnp.concatenate(outs, axis=2)
 
@@ -90,34 +97,67 @@
     return total.astype(jnp.bfloat16)
 
 
+def pick_groups(units, wanted):
+    for n in range(wanted, 0, -1):
+        if units % (2 * n) == 0 and (units // (2 * n)) % 128 == 0:
+            return n
+    return 1
+
+
+N_GROUPS = 2
+
+
 def body(tokens, grad_out, gate_weight, up_weight, down_weight):
     n_row = lax.psum(1, "row")
     n_col = lax.psum(1, "col")
     tok_all = col_gather(tokens, n_col)
     grad_all = col_gather(grad_out, n_col)
     tok_t = tok_all.T
-    stacked = jnp.stack(
-        [
-            jnp.dot(tok_all, gate_weight, preferred_element_type=jnp.float32).astype(jnp.bfloat16),
-            jnp.dot(tok_all, up_weight, preferred_element_type=jnp.float32).astype(jnp.bfloat16),
-            contract_last(grad_all, down_weight).astype(jnp.bfloat16),
-        ]
+    units = gate_weight.shape[1]
+    n_groups = pick_groups(units, N_GROUPS)
+    span = units // n_groups
+    hidden_g, grad_gate_g, grad_up_g = [], [], []
+    for g in range(n_groups):
+        cols = slice(g * span, (g + 1) * span)
+        stacked = jnp.stack(
+            [
+                jnp.dot(tok_all, gate_weight[:, cols], preferred_element_type=jnp.float32).astype(jnp.bfloat16),
+                jnp.dot(tok_all, up_weight[:, cols], preferred_element_type=jnp.float32).astype(jnp.bfloat16),
+                contract_last(grad_all, down_weight[cols, :]).astype(jnp.bfloat16),
+            ]
+        )
+        if g > 0:
+            stacked, reduced = lax.optimization_barrier((stacked, reduced))
+            gated = row_gather_gated(reduced, n_row)
+            hidden_g.append(gated[0])
+            grad_gate_g.append(gated[1])
+            grad_up_g.append(gated[2])
+        reduced = row_reduce(stacked, n_row)
+    gated = row_gather_gated(reduced, n_row)
+    hidden_g.append(gated[0])
+    grad_gate_g.append(gated[1])
+    grad_up_g.append(gated[2])
+    partial_grad = None
+    for g in range(n_groups):
+        cols = slice(g * span, (g + 1) * span)
+        part = contract_last(grad_gate_g[g], gate_weight[:, cols]) + contract_last(grad_up_g[g], up_weight[:, cols])
+        partial_grad = part if partial_grad is None else partial_grad + part
+    acc_down = jnp.concatenate(
+        [contract_first(h, grad_all).astype(jnp.bfloat16) for h in hidden_g], axis=0
     )
-    gated = row_gated(stacked, n_row)
-    hidden, grad_gate, grad_up = gated[0], gated[1], gated[2]
-    partial_grad = contract_last(grad_gate, gate_weight) + contract_last(grad_up, up_weight)
-    partial_grad, grad_gate, grad_up, hidden = lax.optimization_barrier(
-        (partial_grad.astype(jnp.bfloat16), grad_gate, grad_up, hidden)
+    grad_gate = jnp.concatenate(grad_gate_g, axis=1)
+    grad_up = jnp.concatenate(grad_up_g, axis=1)
+    partial_grad, grad_gate, grad_up = lax.optimization_barrier(
+        (partial_grad.astype(jnp.bfloat16), grad_gate, grad_up)
     )
     grad_tokens = col_reduce_scatter(partial_grad, n_col)
     acc_gate = jnp.dot(tok_t, grad_gate, preferred_element_type=jnp.float32)
     acc_up = jnp.dot(tok_t, grad_up, preferred_element_type=jnp.float32)
-    acc_down = contract_first(hidden, grad_all)
     return (
         grad_tokens,
         acc_gate.astype(jnp.bfloat16),
         acc_up.astype(jnp.bfloat16),
-        acc_down.astype(jnp.bfloat16),
+        acc_down,
     )
 
 

time: 112 us -> 135 us (1.21)
  waiting for transfers between devices: 34.7 us -> 44.3 us
  other arithmetic: 7.76 us -> 16.9 us
  starting transfers between devices: 31.7 us -> 35.7 us
  matrix products: 29.6 us -> 31.7 us
  local copies, waits for them, and re-layouts: 6.29 us -> 4.62 us
    ppermute x6, waiting for transfers between devices: 2.39 us -> 15.1 us  [col_gather(): lax.ppermute(x, 'col', [(j, (j + s) % n_col) for j in range(n_col)])]
    concatenate x0 -> x3, other arithmetic: none -> 6.11 us  [the longest x1 5.93 us: body(): jnp.concatenate([contract_first(h, grad_all).astype(jnp.bfloat16) for h i...]
    ppermute x6 -> x12, starting transfers between devices: 6.67 us -> 12.2 us  [halving_reduce(): got = lax.ppermute(send, 'row', [(j, j ^ bit) for j in range(n_dev)])]
    dot_general x3 -> x6, matrix products: 7.59 us -> 12.5 us  [contract_last(): lax.dot_general(left, right, (((1,), (1,)), ((), ())), preferred_element_...]
    ppermute x6 -> x12, waiting for transfers between devices: 16.2 us -> 12.2 us  [doubling_gather(): got = lax.ppermute(cur, 'row', [(j, j ^ bit) for j in range(n_dev)])]
    ppermute x6 -> x12, starting transfers between devices: 5.81 us -> 9.14 us  [doubling_gather(): got = lax.ppermute(cur, 'row', [(j, j ^ bit) for j in range(n_dev)])]
    ppermute x3, starting transfers between devices: 8.81 us -> 5.56 us  [col_reduce_scatter(): lax.ppermute(x[s * span:(s + 1) * span], 'col', [(j, (j - s) % n_col) for...]
    dot_general x2 -> x4, matrix products: 6.48 us -> 3.55 us  [the longest x2 1.77 us: body(): jnp.dot(tok_all, gate_weight[:, cols], preferred_element_type=jnp.float32)]
  transfers between devices with their start and end apart: 21 -> 33, of which waited for: 10 -> 17; matrix products, arithmetic and copies ran while one was open for 26% -> 30% of each run, Pallas kernels for 0% -> 0%
where the time goes in v5:
time: 135 us
  waiting for transfers between devices  44.3 us (33%)
  starting transfers between devices  35.7 us (26%)
  matrix products  31.7 us (23%)
  other arithmetic  16.9 us (13%)
  local copies, waits for them, and re-layouts  4.62 us (3%)
  between operations  1.38 us (1%)
    ppermute x12, waiting for transfers between devices, halving_reduce(): got = lax.ppermute(send, 'row', [(j, j ^ bit) for j in range(n_dev)])  16.9 us
    ppermute x6, waiting for transfers between devices, col_gather(): lax.ppermute(x, 'col', [(j, (j + s) % n_col) for j in range(n_col)])  15.1 us
    dot_general x6, matrix products, contract_last(): lax.dot_general(left, right, (((1,), (1,)), ((), ())), preferred_element_...  12.5 us
    ppermute x12, waiting for transfers between devices, doubling_gather(): got = lax.ppermute(cur, 'row', [(j, j ^ bit) for j in range(n_dev)])  12.2 us
    ppermute x12, starting transfers between devices, halving_reduce(): got = lax.ppermute(send, 'row', [(j, j ^ bit) for j in range(n_dev)])  12.2 us
    ppermute x12, starting transfers between devices, doubling_gather(): got = lax.ppermute(cur, 'row', [(j, j ^ bit) for j in range(n_dev)])  9.14 us
    ppermute x6, starting transfers between devices, col_gather(): lax.ppermute(x, 'col', [(j, (j + s) % n_col) for j in range(n_col)])  8.8 us
    dot_general x1, matrix products, body(): acc_up = jnp.dot(tok_t, grad_up, preferred_element_type=jnp.float32)  6.17 us
  transfers between devices with their start and end apart: 33, of which 17 were waited for; matrix products, arithmetic and copies ran while one was open for 30% of the time, Pallas kernels for 0%

profile of v5, /device:TPU:0, one launch (start us, length us, event | category | flops | bytes accessed | tf_op | source)
XLA Modules:
  0.0 134.5 jit_solution(12770280302684267676)
XLA Ops:
  0.6 4.1 %collective-permute-start.1 = (bf16[48,1024]{1,0:T(8,128)(2,1)}, bf16[48,1024]{1,0:T(8,128)(2,1)S(1)}, u32[]{:S(2)}, u32[]{:S(2)}) collective-permute-start(bf16[48,1024]{1,0:T(8,128)(2,1)} %param.5), channel_id=1, source_target_pairs={{0,2},{1,3},{2,0},{3,1},{4,6},{5,7},{6,4},{7,5},{8,10},{9,11},{10,... | collective-permute-start | bytes 294920 | tf_op jit(solution)/shard_map/ppermute | solution.py:87
  4.8 1.6 %collective-permute-start = (bf16[48,1024]{1,0:T(8,128)(2,1)}, bf16[48,1024]{1,0:T(8,128)(2,1)S(1)}, u32[]{:S(2)}, u32[]{:S(2)}) collective-permute-start(bf16[48,1024]{1,0:T(8,128)(2,1)} %param.5), channel_id=1, source_target_pairs={{0,1},{1,2},{2,3},{3,0},{4,5},{5,6},{6,7},{7,4},{8,9},{9,10},{10,1... | collective-permute-start | bytes 294920 | tf_op jit(solution)/shard_map/ppermute | solution.py:87
  6.3 2.2 %collective-permute-start.2 = (bf16[48,1024]{1,0:T(8,128)(2,1)}, bf16[48,1024]{1,0:T(8,128)(2,1)S(1)}, u32[]{:S(2)}, u32[]{:S(2)}) collective-permute-start(bf16[48,1024]{1,0:T(8,128)(2,1)} %param.5), channel_id=1, source_target_pairs={{0,3},{1,0},{2,1},{3,2},{4,7},{5,4},{6,5},{7,6},{8,11},{9,8},{10,9... | collective-permute-start | bytes 294920 | tf_op jit(solution)/shard_map/ppermute | solution.py:87
  8.6 0.6 collective-permute-start.3
  9.2 0.9 constant_dynamic-update-slice_fusion.3
  10.1 1.1 constant_dynamic-update-slice_fusion.7
  11.1 6.2 %collective-permute-done.3 = bf16[48,1024]{1,0:T(8,128)(2,1)S(1)} collective-permute-done((bf16[48,1024]{1,0:T(8,128)(2,1)}, bf16[48,1024]{1,0:T(8,128)(2,1)S(1)}, u32[]{:S(2)}, u32[]{:S(2)}) %collective-permute-start.3) | collective-permute-done | bytes 98336 | tf_op jit(solution)/shard_map/ppermute | solution.py:87
  17.6 2.8 %collective-permute-done.4 = bf16[48,1024]{1,0:T(8,128)(2,1)S(1)} collective-permute-done((bf16[48,1024]{1,0:T(8,128)(2,1)}, bf16[48,1024]{1,0:T(8,128)(2,1)S(1)}, u32[]{:S(2)}, u32[]{:S(2)}) %collective-permute-start.4) | collective-permute-done | bytes 98336 | tf_op jit(solution)/shard_map/ppermute | solution.py:87
  20.5 6.1 %collective-permute-done.5 = bf16[48,1024]{1,0:T(8,128)(2,1)S(1)} collective-permute-done((bf16[48,1024]{1,0:T(8,128)(2,1)}, bf16[48,1024]{1,0:T(8,128)(2,1)S(1)}, u32[]{:S(2)}, u32[]{:S(2)}) %collective-permute-start.5) | collective-permute-done | bytes 98336 | tf_op jit(solution)/shard_map/ppermute | solution.py:87
  26.6 3.6 %fusion.38 = bf16[1,192,1792]{2,1,0:T(8,128)(2,1)S(1)} fusion(bf16[192,1024]{1,0:T(8,128)(2,1)S(1)} %constant_dynamic-update-slice_fusion.4, bf16[3584,1024]{1,0:T(8,128)(2,1)} %param.9), kind=kOutput, calls=%fused_computation.31 | convolution fusion | flops 704987136 | bytes 4751360 | tf_op jit(solution)/shard_map/dot_general | solution.py:14
  30.2 3.6 %fusion.41 = bf16[1,192,1792]{2,1,0:T(8,128)(2,1)S(1)} fusion(bf16[192,1024]{1,0:T(8,128)(2,1)S(1)} %constant_dynamic-update-slice_fusion.4, bf16[3584,1024]{1,0:T(8,128)(2,1)} %param.9), kind=kOutput, calls=%fused_computation.32 | convolution fusion | flops 704987136 | bytes 4751360 | tf_op jit(solution)/shard_map/dot_general | solution.py:14
  33.9 0.9 fusion.44
  34.8 0.9 fusion.50
  35.9 0.9 fusion.47
  37.5 0.5 collective-permute-start.9
  38.0 0.9 fusion.53
  39.5 1.6 %collective-permute-start.7 = (bf16[3,48,896]{2,1,0:T(8,128)(2,1)S(1)}, bf16[3,48,896]{2,1,0:T(8,128)(2,1)S(1)}, u32[]{:S(2)}, u32[]{:S(2)}) collective-permute-start(bf16[3,48,896]{2,1,0:T(8,128)(2,1)S(1)} %constant_dynamic-slice_fusion.10), channel_id=1, source_target_pairs={{0,8},{4,12},{8,0},{12,4},{16,24},{20,28},{24,16},{28,20},{1,9},{5... | collective-permute-start | bytes 774152 | tf_op jit(solution)/shard_map/ppermute | solution.py:37
  41.3 1.6 %collective-permute-start.10 = (bf16[3,48,896]{2,1,0:T(8,128)(2,1)S(1)}, bf16[3,48,896]{2,1,0:T(8,128)(2,1)S(1)}, u32[]{:S(2)}, u32[]{:S(2)}) collective-permute-start(bf16[3,48,896]{2,1,0:T(8,128)(2,1)S(1)} %constant_dynamic-slice_fusion.7), channel_id=1, source_target_pairs={{0,16},{4,20},{8,24},{12,28},{16,0},{20,4},{24,8},{28,12},{1,17},{... | collective-permute-start | bytes 774152 | tf_op jit(solution)/shard_map/ppermute | solution.py:37
  42.9 5.0 %collective-permute-done.7 = bf16[3,48,896]{2,1,0:T(8,128)(2,1)S(1)} collective-permute-done((bf16[3,48,896]{2,1,0:T(8,128)(2,1)S(1)}, bf16[3,48,896]{2,1,0:T(8,128)(2,1)S(1)}, u32[]{:S(2)}, u32[]{:S(2)}) %collective-permute-start.7) | collective-permute-done | bytes 258080 | tf_op jit(solution)/shard_map/ppermute | solution.py:37
  47.9 1.6 %collective-permute-start.8 = (bf16[3,24,896]{2,1,0:T(8,128)(2,1)S(1)}, bf16[3,24,896]{2,1,0:T(8,128)(2,1)S(1)}, u32[]{:S(2)}, u32[]{:S(2)}) collective-permute-start(bf16[3,24,896]{2,1,0:T(8,128)(2,1)S(1)} %constant_dynamic-slice_fusion.9), channel_id=1, source_target_pairs={{0,16},{4,20},{8,24},{12,28},{16,0},{20,4},{24,8},{28,12},{1,17},{... | collective-permute-start | bytes 387080 | tf_op jit(solution)/shard_map/ppermute | solution.py:37
  49.6 1.6 %collective-permute-start.11 = (bf16[3,24,896]{2,1,0:T(8,128)(2,1)S(1)}, bf16[3,24,896]{2,1,0:T(8,128)(2,1)S(1)}, u32[]{:S(2)}, u32[]{:S(2)}) collective-permute-start(bf16[3,24,896]{2,1,0:T(8,128)(2,1)S(1)} %constant_dynamic-slice_fusion.6), channel_id=1, source_target_pairs={{0,8},{4,12},{8,0},{12,4},{16,24},{20,28},{24,16},{28,20},{1,9},{5... | collective-permute-start | bytes 387080 | tf_op jit(solution)/shard_map/ppermute | solution.py:37
  51.2 1.8 %collective-permute-done.8 = bf16[3,24,896]{2,1,0:T(8,128)(2,1)S(1)} collective-permute-done((bf16[3,24,896]{2,1,0:T(8,128)(2,1)S(1)}, bf16[3,24,896]{2,1,0:T(8,128)(2,1)S(1)}, u32[]{:S(2)}, u32[]{:S(2)}) %collective-permute-start.8) | collective-permute-done | bytes 129056 | tf_op jit(solution)/shard_map/ppermute | solution.py:37
  53.0 1.7 %collective-permute-done.11 = bf16[3,24,896]{2,1,0:T(8,128)(2,1)S(1)} collective-permute-done((bf16[3,24,896]{2,1,0:T(8,128)(2,1)S(1)}, bf16[3,24,896]{2,1,0:T(8,128)(2,1)S(1)}, u32[]{:S(2)}, u32[]{:S(2)}) %collective-permute-start.11) | collective-permute-done | bytes 129056 | tf_op jit(solution)/shard_map/ppermute | solution.py:37
  54.8 1.4 %collective-permute-start.12 = (bf16[3,24,896]{2,1,0:T(8,128)(2,1)S(1)}, bf16[3,24,896]{2,1,0:T(8,128)(2,1)S(1)}, u32[]{:S(2)}, u32[]{:S(2)}) collective-permute-start(bf16[3,24,896]{2,1,0:T(8,128)(2,1)S(1)} %pad_maximum_fusion.7), channel_id=1, source_target_pairs={{0,16},{4,20},{8,24},{12,28},{16,0},{20,4},{24,8},{28,12},{1,17},{... | collective-permute-start | bytes 387080 | tf_op jit(solution)/shard_map/ppermute | solution.py:49
  56.2 0.7 pad_maximum_fusion.8
  56.9 0.8 collective-permute-start.15
  58.0 1.8 %collective-permute-done.12 = bf16[3,24,896]{2,1,0:T(8,128)(2,1)S(1)} collective-permute-done((bf16[3,24,896]{2,1,0:T(8,128)(2,1)S(1)}, bf16[3,24,896]{2,1,0:T(8,128)(2,1)S(1)}, u32[]{:S(2)}, u32[]{:S(2)}) %collective-permute-start.12) | collective-permute-done | bytes 129056 | tf_op jit(solution)/shard_map/ppermute | solution.py:49
  59.9 1.6 %collective-permute-start.13 = (bf16[3,48,896]{2,1,0:T(8,128)(2,1)S(1)}, bf16[3,48,896]{2,1,0:T(8,128)(2,1)}, u32[]{:S(2)}, u32[]{:S(2)}) collective-permute-start(bf16[3,48,896]{2,1,0:T(8,128)(2,1)S(1)} %maximum_select_fusion.8), channel_id=1, source_target_pairs={{0,8},{4,12},{8,0},{12,4},{16,24},{20,28},{24,16},{28,20},{1,9},{5... | collective-permute-start | bytes 774152 | tf_op jit(solution)/shard_map/ppermute | solution.py:49
  61.5 1.5 %collective-permute-done.15 = bf16[3,24,896]{2,1,0:T(8,128)(2,1)} collective-permute-done((bf16[3,24,896]{2,1,0:T(8,128)(2,1)}, bf16[3,24,896]{2,1,0:T(8,128)(2,1)}, u32[]{:S(2)}, u32[]{:S(2)}) %collective-permute-start.15) | collective-permute-done | bytes 129056 | tf_op jit(solution)/shard_map/ppermute | solution.py:49
  62.9 1.1 maximum_select_fusion.9
  64.3 3.4 %collective-permute-done.13 = bf16[3,48,896]{2,1,0:T(8,128)(2,1)} collective-permute-done((bf16[3,48,896]{2,1,0:T(8,128)(2,1)S(1)}, bf16[3,48,896]{2,1,0:T(8,128)(2,1)}, u32[]{:S(2)}, u32[]{:S(2)}) %collective-permute-start.13) | collective-permute-done | bytes 258080 | tf_op jit(solution)/shard_map/ppermute | solution.py:49
  67.7 1.2 maximum_select_fusion.4
  69.0 1.6 %collective-permute-done.16 = bf16[3,48,896]{2,1,0:T(8,128)(2,1)} collective-permute-done((bf16[3,48,896]{2,1,0:T(8,128)(2,1)S(1)}, bf16[3,48,896]{2,1,0:T(8,128)(2,1)}, u32[]{:S(2)}, u32[]{:S(2)}) %collective-permute-start.16) | collective-permute-done | bytes 258080 | tf_op jit(solution)/shard_map/ppermute | solution.py:49
  70.6 1.2 maximum_select_fusion.5
  71.9 1.2 add_convert_fusion.1
  73.1 0.5 collective-permute-start.19
  73.8 2.1 %collective-permute-start.25 = (bf16[3,48,896]{2,1,0:T(8,128)(2,1)S(1)}, bf16[3,48,896]{2,1,0:T(8,128)(2,1)S(1)}, u32[]{:S(2)}, u32[]{:S(2)}) collective-permute-start(bf16[3,48,896]{2,1,0:T(8,128)(2,1)S(1)} %constant_dynamic-slice_fusion.1), channel_id=1, source_target_pairs={{0,16},{4,20},{8,24},{12,28},{16,0},{20,4},{24,8},{28,12},{1,17},{... | collective-permute-start | bytes 774152 | tf_op jit(solution)/shard_map/ppermute | solution.py:37
  75.9 5.9 %collective-permute-done.19 = bf16[3,48,896]{2,1,0:T(8,128)(2,1)S(1)} collective-permute-done((bf16[3,48,896]{2,1,0:T(8,128)(2,1)S(1)}, bf16[3,48,896]{2,1,0:T(8,128)(2,1)S(1)}, u32[]{:S(2)}, u32[]{:S(2)}) %collective-permute-start.19) | collective-permute-done | bytes 258080 | tf_op jit(solution)/shard_map/ppermute | solution.py:37
  81.9 0.8 collective-permute-start.20
  82.7 1.8 %collective-permute-start.26 = (bf16[3,24,896]{2,1,0:T(8,128)(2,1)S(1)}, bf16[3,24,896]{2,1,0:T(8,128)(2,1)S(1)}, u32[]{:S(2)}, u32[]{:S(2)}) collective-permute-start(bf16[3,24,896]{2,1,0:T(8,128)(2,1)S(1)} %constant_dynamic-slice_fusion), channel_id=1, source_target_pairs={{0,8},{4,12},{8,0},{12,4},{16,24},{20,28},{24,16},{28,20},{1,9},{5... | collective-permute-start | bytes 387080 | tf_op jit(solution)/shard_map/ppermute | solution.py:37
  84.6 2.4 %collective-permute-done.20 = bf16[3,24,896]{2,1,0:T(8,128)(2,1)S(1)} collective-permute-done((bf16[3,24,896]{2,1,0:T(8,128)(2,1)S(1)}, bf16[3,24,896]{2,1,0:T(8,128)(2,1)S(1)}, u32[]{:S(2)}, u32[]{:S(2)}) %collective-permute-start.20) | collective-permute-done | bytes 129056 | tf_op jit(solution)/shard_map/ppermute | solution.py:37
  87.0 1.1 collective-permute-start.21
  88.3 1.5 %collective-permute-start.27 = (bf16[3,24,896]{2,1,0:T(8,128)(2,1)S(1)}, bf16[3,24,896]{2,1,0:T(8,128)(2,1)S(1)}, u32[]{:S(2)}, u32[]{:S(2)}) collective-permute-start(bf16[3,24,896]{2,1,0:T(8,128)(2,1)S(1)} %pad_maximum_fusion.10), channel_id=1, source_target_pairs={{0,8},{4,12},{8,0},{12,4},{16,24},{20,28},{24,16},{28,20},{1,9},{5... | collective-permute-start | bytes 387080 | tf_op jit(solution)/shard_map/ppermute | solution.py:49
  90.7 1.3 fusion.4
  92.1 0.9 collective-permute-start.22
  93.1 0.5 collective-permute-done.27
  93.6 1.5 %collective-permute-start.28 = (bf16[3,48,896]{2,1,0:T(8,128)(2,1)S(1)}, bf16[3,48,896]{2,1,0:T(8,128)(2,1)S(1)}, u32[]{:S(2)}, u32[]{:S(2)}) collective-permute-start(bf16[3,48,896]{2,1,0:T(8,128)(2,1)S(1)} %maximum_select_fusion.11), channel_id=1, source_target_pairs={{0,16},{4,20},{8,24},{12,28},{16,0},{20,4},{24,8},{28,12},{1,17},{... | collective-permute-start | bytes 774152 | tf_op jit(solution)/shard_map/ppermute | solution.py:49
  95.2 1.3 convolution_convert_fusion.3
  96.5 2.3 %collective-permute-done.22 = bf16[3,48,896]{2,1,0:T(8,128)(2,1)S(1)} collective-permute-done((bf16[3,48,896]{2,1,0:T(8,128)(2,1)S(1)}, bf16[3,48,896]{2,1,0:T(8,128)(2,1)S(1)}, u32[]{:S(2)}, u32[]{:S(2)}) %collective-permute-start.22) | collective-permute-done | bytes 258080 | tf_op jit(solution)/shard_map/ppermute | solution.py:49
  99.0 1.0 collective-permute-done.28
  100.2 1.3 fusion.62
  101.6 0.4 maximum_select_fusion.2
  102.1 0.4 maximum_select_fusion.3
  102.7 1.3 fusion.12
  104.1 3.0 %convolution_convert_fusion.2 = bf16[1792,1024]{1,0:T(8,128)(2,1)} fusion(bf16[192,1024]{1,0:T(8,128)(2,1)S(1)} %copy-done.3, bf16[3,192,896]{2,1,0:T(8,128)(2,1)S(1)} %maximum_select_fusion.3, bf16[3,192,896]{2,1,0:T(8,128)(2,1)S(1)} %maximum_select_fusion.2), kind=kOutput, calls=%fused_computation.3 | convolution fusion | flops 707854336 | bytes 6127616 | tf_op jit(solution)/shard_map/dot_general | solution.py:8
  107.2 1.3 %fusion.65 = bf16[192,1024]{1,0:T(8,128)(2,1)S(1)} fusion(f32[192,1024]{1,0:T(8,128)S(1)} %fusion.62, f32[192,1024]{1,0:T(8,128)S(1)} %fusion.12, bf16[192,1792]{1,0:T(8,128)(2,1)S(1)} %get-tuple-element.16, bf16[1024,3584]{1,0:T(8,128)(2,1)S(1)} %bitcast.49), kind=kOutput, calls=%fused_computation.52 | convolution fusion | flops 705232896 | bytes 6324224 | tf_op jit(solution)/shard_map/dot_general | solution.py:14
  108.5 0.7 copy-done.4
  109.3 0.7 fusion.86
  110.0 2.6 %collective-permute-start.30 = (bf16[48,1024]{1,0:T(8,128)(2,1)}, bf16[48,1024]{1,0:T(8,128)(2,1)}, u32[]{:S(2)}, u32[]{:S(2)}) collective-permute-start(bf16[48,1024]{1,0:T(8,128)(2,1)} %get-tuple-element.24), channel_id=1, source_target_pairs={{0,3},{1,0},{2,1},{3,2},{4,7},{5,4},{6,5},{7,6},{8,11},{9,8},{10,9... | collective-permute-start | bytes 294920 | tf_op jit(solution)/shard_map/ppermute | solution.py:95
  112.6 2.9 %collective-permute-start.31 = (bf16[48,1024]{1,0:T(8,128)(2,1)}, bf16[48,1024]{1,0:T(8,128)(2,1)}, u32[]{:S(2)}, u32[]{:S(2)}) collective-permute-start(bf16[48,1024]{1,0:T(8,128)(2,1)} %get-tuple-element.26), channel_id=1, source_target_pairs={{0,2},{1,3},{2,0},{3,1},{4,6},{5,7},{6,4},{7,5},{8,10},{9,11},{10,... | collective-permute-start | bytes 294920 | tf_op jit(solution)/shard_map/ppermute | solution.py:95
  115.5 5.2 %convolution_convert_fusion.1 = bf16[1024,3584]{1,0:T(8,128)(2,1)} fusion(bf16[192,1024]{1,0:T(8,128)(2,1)S(1)} %copy-done.1, bf16[192,3584]{1,0:T(8,128)(2,1)S(1)} %pad_maximum_fusion.3), kind=kOutput, calls=%fused_computation.1 | convolution fusion | flops 1412956160 | bytes 9109504 | tf_op jit(solution)/shard_map/dot_general | solution.py:154
  120.7 5.9 %pad_maximum_fusion = bf16[3584,1024]{1,0:T(8,128)(2,1)} fusion(bf16[1792,1024]{1,0:T(8,128)(2,1)} %convolution_convert_fusion.2, bf16[1792,1024]{1,0:T(8,128)(2,1)S(1)} %convolution_convert_fusion.3), kind=kLoop, calls=%fused_computation.2 | loop fusion | flops 14680064 | bytes 14680064 | tf_op jit(solution)/shard_map/concatenate | solution.py:145
  126.6 6.2 %convolution_convert_fusion = bf16[1024,3584]{1,0:T(8,128)(2,1)} fusion(bf16[192,1024]{1,0:T(8,128)(2,1)} %copy-done, bf16[192,3584]{1,0:T(8,128)(2,1)S(1)} %pad_maximum_fusion.4), kind=kOutput, calls=%fused_computation | convolution fusion | flops 1412956160 | bytes 9109504 | tf_op jit(solution)/shard_map/dot_general | solution.py:155
  132.8 1.7 %add_convert_fusion.8 = bf16[48,1024]{1,0:T(8,128)(2,1)} fusion(bf16[48,1024]{1,0:T(8,128)(2,1)} %collective-permute-done.32, bf16[48,1024]{1,0:T(8,128)(2,1)} %collective-permute-done.31, bf16[48,1024]{1,0:T(8,128)(2,1)} %collective-permute-done.30, bf16[192,1024]{1,0:T(8,128)(2,1)} %copy-done.4), kind=kLoop, calls=%fused_computation.91 | loop fusion | flops 393216 | bytes 491520 | tf_op jit(solution)/shard_map/convert_element_type | solution.py:97
  (112 shorter events, 5.6 us)
Async XLA Ops:
  0.6 33.1 %collective-permute-start.1 = (bf16[48,1024]{1,0:T(8,128)(2,1)}, bf16[48,1024]{1,0:T(8,128)(2,1)S(1)}, u32[]{:S(2)}, u32[]{:S(2)}) collective-permute-start(bf16[48,1024]{1,0:T(8,128)(2,1)} %param.5), channel_id=1, source_target_pairs={{0,2},{1,3},{2,0},{3,1},{4,6},{5,7},{6,4},{7,5},{8,10},{9,11},{10,... | collective-permute-start | bytes 294920 | tf_op jit(solution)/shard_map/ppermute | solution.py:87
  4.8 29.0 %collective-permute-start = (bf16[48,1024]{1,0:T(8,128)(2,1)}, bf16[48,1024]{1,0:T(8,128)(2,1)S(1)}, u32[]{:S(2)}, u32[]{:S(2)}) collective-permute-start(bf16[48,1024]{1,0:T(8,128)(2,1)} %param.5), channel_id=1, source_target_pairs={{0,1},{1,2},{2,3},{3,0},{4,5},{5,6},{6,7},{7,4},{8,9},{9,10},{10,1... | collective-permute-start | bytes 294920 | tf_op jit(solution)/shard_map/ppermute | solution.py:87
  6.3 27.4 %collective-permute-start.2 = (bf16[48,1024]{1,0:T(8,128)(2,1)}, bf16[48,1024]{1,0:T(8,128)(2,1)S(1)}, u32[]{:S(2)}, u32[]{:S(2)}) collective-permute-start(bf16[48,1024]{1,0:T(8,128)(2,1)} %param.5), channel_id=1, source_target_pairs={{0,3},{1,0},{2,1},{3,2},{4,7},{5,4},{6,5},{7,6},{8,11},{9,8},{10,9... | collective-permute-start | bytes 294920 | tf_op jit(solution)/shard_map/ppermute | solution.py:87
  8.6 11.9 %collective-permute-start.4 = (bf16[48,1024]{1,0:T(8,128)(2,1)}, bf16[48,1024]{1,0:T(8,128)(2,1)S(1)}, u32[]{:S(2)}, u32[]{:S(2)}) collective-permute-start(bf16[48,1024]{1,0:T(8,128)(2,1)} %param.6), channel_id=1, source_target_pairs={{0,2},{1,3},{2,0},{3,1},{4,6},{5,7},{6,4},{7,5},{8,10},{9,11},{10,... | collective-permute-start | bytes 294920 | tf_op jit(solution)/shard_map/ppermute | solution.py:87
  8.6 8.8 %collective-permute-start.3 = (bf16[48,1024]{1,0:T(8,128)(2,1)}, bf16[48,1024]{1,0:T(8,128)(2,1)S(1)}, u32[]{:S(2)}, u32[]{:S(2)}) collective-permute-start(bf16[48,1024]{1,0:T(8,128)(2,1)} %param.6), channel_id=1, source_target_pairs={{0,1},{1,2},{2,3},{3,0},{4,5},{5,6},{6,7},{7,4},{8,9},{9,10},{10,1... | collective-permute-start | bytes 294920 | tf_op jit(solution)/shard_map/ppermute | solution.py:87
  10.1 23.8 %slice-start = ((s8[7340032]{0:T(1024)(128)(4,1)}), s8[4194304]{0:T(1024)(128)(4,1)S(1)}, s32[]{:S(2)}) async-start(s8[7340032]{0:T(1024)(128)(4,1)} %bitcast.42), calls=%async_computation | async-start | bytes 8388608
  17.3 9.2 %collective-permute-start.5 = (bf16[48,1024]{1,0:T(8,128)(2,1)}, bf16[48,1024]{1,0:T(8,128)(2,1)S(1)}, u32[]{:S(2)}, u32[]{:S(2)}) collective-permute-start(bf16[48,1024]{1,0:T(8,128)(2,1)} %param.6), channel_id=1, source_target_pairs={{0,3},{1,0},{2,1},{3,2},{4,7},{5,4},{6,5},{7,6},{8,11},{9,8},{10,9... | collective-permute-start | bytes 294920 | tf_op jit(solution)/shard_map/ppermute | solution.py:87
  26.5 68.6 %copy-start.2 = (bf16[192,1024]{1,0:T(8,128)(2,1)}, bf16[192,1024]{1,0:T(8,128)(2,1)S(1)}, u32[]{:S(2)}) copy-start(bf16[192,1024]{1,0:T(8,128)(2,1)S(1)} %constant_dynamic-update-slice_fusion.4) | copy-start | bytes 1179652
  26.5 7.3 %slice-start.1 = ((s8[7340032]{0:T(1024)(128)(4,1)}), s8[3145728]{0:T(1024)(128)(4,1)S(1)}, s32[]{:S(2)}) async-start(s8[7340032]{0:T(1024)(128)(4,1)} %bitcast.42), calls=%async_computation.1 | async-start | bytes 6291456
  30.2 5.5 %slice-start.4 = ((s8[7340032]{0:T(1024)(128)(4,1)}), s8[4194304]{0:T(1024)(128)(4,1)S(1)}, s32[]{:S(2)}) async-start(s8[7340032]{0:T(1024)(128)(4,1)} %bitcast.46), calls=%async_computation.4 | async-start | bytes 8388608
  33.8 4.1 %copy-start = (bf16[192,1024]{1,0:T(8,128)(2,1)}, bf16[192,1024]{1,0:T(8,128)(2,1)S(1)}, u32[]{:S(2)}) copy-start(bf16[192,1024]{1,0:T(8,128)(2,1)S(1)} %constant_dynamic-update-slice_fusion) | copy-start | bytes 1179652
  33.9 2.0 %slice-start.5 = ((s8[7340032]{0:T(1024)(128)(4,1)}), s8[3145728]{0:T(1024)(128)(4,1)S(1)}, s32[]{:S(2)}) async-start(s8[7340032]{0:T(1024)(128)(4,1)} %bitcast.46), calls=%async_computation.5 | async-start | bytes 6291456
  37.4 2.0 %collective-permute-start.6 = (bf16[3,96,896]{2,1,0:T(8,128)(2,1)S(1)}, bf16[3,96,896]{2,1,0:T(8,128)(2,1)S(1)}, u32[]{:S(2)}, u32[]{:S(2)}) collective-permute-start(bf16[3,96,896]{2,1,0:T(8,128)(2,1)S(1)} %constant_dynamic-slice_fusion.11), channel_id=1, source_target_pairs={{0,4},{4,0},{8,12},{12,8},{16,20},{20,16},{24,28},{28,24},{1,5},{5... | collective-permute-start | bytes 1548296 | tf_op jit(solution)/shard_map/ppermute | solution.py:37
  37.5 3.6 %collective-permute-start.9 = (bf16[3,96,896]{2,1,0:T(8,128)(2,1)S(1)}, bf16[3,96,896]{2,1,0:T(8,128)(2,1)S(1)}, u32[]{:S(2)}, u32[]{:S(2)}) collective-permute-start(bf16[3,96,896]{2,1,0:T(8,128)(2,1)S(1)} %constant_dynamic-slice_fusion.8), channel_id=1, source_target_pairs={{0,4},{4,0},{8,12},{12,8},{16,20},{20,16},{24,28},{28,24},{1,5},{5... | collective-permute-start | bytes 1548296 | tf_op jit(solution)/shard_map/ppermute | solution.py:37
  39.5 8.3 %collective-permute-start.7 = (bf16[3,48,896]{2,1,0:T(8,128)(2,1)S(1)}, bf16[3,48,896]{2,1,0:T(8,128)(2,1)S(1)}, u32[]{:S(2)}, u32[]{:S(2)}) collective-permute-start(bf16[3,48,896]{2,1,0:T(8,128)(2,1)S(1)} %constant_dynamic-slice_fusion.10), channel_id=1, source_target_pairs={{0,8},{4,12},{8,0},{12,4},{16,24},{20,28},{24,16},{28,20},{1,9},{5... | collective-permute-start | bytes 774152 | tf_op jit(solution)/shard_map/ppermute | solution.py:37
  41.3 8.3 %collective-permute-start.10 = (bf16[3,48,896]{2,1,0:T(8,128)(2,1)S(1)}, bf16[3,48,896]{2,1,0:T(8,128)(2,1)S(1)}, u32[]{:S(2)}, u32[]{:S(2)}) collective-permute-start(bf16[3,48,896]{2,1,0:T(8,128)(2,1)S(1)} %constant_dynamic-slice_fusion.7), channel_id=1, source_target_pairs={{0,16},{4,20},{8,24},{12,28},{16,0},{20,4},{24,8},{28,12},{1,17},{... | collective-permute-start | bytes 774152 | tf_op jit(solution)/shard_map/ppermute | solution.py:37
  47.9 5.0 %collective-permute-start.8 = (bf16[3,24,896]{2,1,0:T(8,128)(2,1)S(1)}, bf16[3,24,896]{2,1,0:T(8,128)(2,1)S(1)}, u32[]{:S(2)}, u32[]{:S(2)}) collective-permute-start(bf16[3,24,896]{2,1,0:T(8,128)(2,1)S(1)} %constant_dynamic-slice_fusion.9), channel_id=1, source_target_pairs={{0,16},{4,20},{8,24},{12,28},{16,0},{20,4},{24,8},{28,12},{1,17},{... | collective-permute-start | bytes 387080 | tf_op jit(solution)/shard_map/ppermute | solution.py:37
  49.6 5.0 %collective-permute-start.11 = (bf16[3,24,896]{2,1,0:T(8,128)(2,1)S(1)}, bf16[3,24,896]{2,1,0:T(8,128)(2,1)S(1)}, u32[]{:S(2)}, u32[]{:S(2)}) collective-permute-start(bf16[3,24,896]{2,1,0:T(8,128)(2,1)S(1)} %constant_dynamic-slice_fusion.6), channel_id=1, source_target_pairs={{0,8},{4,12},{8,0},{12,4},{16,24},{20,28},{24,16},{28,20},{1,9},{5... | collective-permute-start | bytes 387080 | tf_op jit(solution)/shard_map/ppermute | solution.py:37
  54.8 3.2 %copy-start.5 = (bf16[1,24,896]{2,1,0:T(8,128)(2,1)}, bf16[1,24,896]{2,1,0:T(8,128)(2,1)S(1)}, u32[]{:S(2)}) copy-start(bf16[1,24,896]{2,1,0:T(8,128)(2,1)S(1)} %get-tuple-element.34) | copy-start | bytes 129028
  54.8 3.2 %copy-start.6 = (bf16[1,24,896]{2,1,0:T(8,128)(2,1)}, bf16[1,24,896]{2,1,0:T(8,128)(2,1)S(1)}, u32[]{:S(2)}) copy-start(bf16[1,24,896]{2,1,0:T(8,128)(2,1)S(1)} %get-tuple-element.35) | copy-start | bytes 129028
  54.8 5.0 %collective-permute-start.12 = (bf16[3,24,896]{2,1,0:T(8,128)(2,1)S(1)}, bf16[3,24,896]{2,1,0:T(8,128)(2,1)S(1)}, u32[]{:S(2)}, u32[]{:S(2)}) collective-permute-start(bf16[3,24,896]{2,1,0:T(8,128)(2,1)S(1)} %pad_maximum_fusion.7), channel_id=1, source_target_pairs={{0,16},{4,20},{8,24},{12,28},{16,0},{20,4},{24,8},{28,12},{1,17},{... | collective-permute-start | bytes 387080 | tf_op jit(solution)/shard_map/ppermute | solution.py:49
  56.9 6.1 %collective-permute-start.15 = (bf16[3,24,896]{2,1,0:T(8,128)(2,1)}, bf16[3,24,896]{2,1,0:T(8,128)(2,1)}, u32[]{:S(2)}, u32[]{:S(2)}) collective-permute-start(bf16[3,24,896]{2,1,0:T(8,128)(2,1)} %pad_maximum_fusion.8), channel_id=1, source_target_pairs={{0,8},{4,12},{8,0},{12,4},{16,24},{20,28},{24,16},{28,20},{1,9},{5... | collective-permute-start | bytes 387080 | tf_op jit(solution)/shard_map/ppermute | solution.py:49
  57.9 13.9 %collective-permute-start.18 = (bf16[3,96,896]{2,1,0:T(8,128)(2,1)S(1)}, bf16[3,96,896]{2,1,0:T(8,128)(2,1)}, u32[]{:S(2)}, u32[]{:S(2)}) collective-permute-start(bf16[3,96,896]{2,1,0:T(8,128)(2,1)S(1)} %constant_dynamic-slice_fusion.5), channel_id=1, source_target_pairs={{0,4},{4,0},{8,12},{12,8},{16,20},{20,16},{24,28},{28,24},{1,5},{5... | collective-permute-start | bytes 1548296 | tf_op jit(solution)/shard_map/ppermute | solution.py:37
  59.9 7.8 %collective-permute-start.13 = (bf16[3,48,896]{2,1,0:T(8,128)(2,1)S(1)}, bf16[3,48,896]{2,1,0:T(8,128)(2,1)}, u32[]{:S(2)}, u32[]{:S(2)}) collective-permute-start(bf16[3,48,896]{2,1,0:T(8,128)(2,1)S(1)} %maximum_select_fusion.8), channel_id=1, source_target_pairs={{0,8},{4,12},{8,0},{12,4},{16,24},{20,28},{24,16},{28,20},{1,9},{5... | collective-permute-start | bytes 774152 | tf_op jit(solution)/shard_map/ppermute | solution.py:49
  64.1 6.5 %collective-permute-start.16 = (bf16[3,48,896]{2,1,0:T(8,128)(2,1)S(1)}, bf16[3,48,896]{2,1,0:T(8,128)(2,1)}, u32[]{:S(2)}, u32[]{:S(2)}) collective-permute-start(bf16[3,48,896]{2,1,0:T(8,128)(2,1)S(1)} %maximum_select_fusion.9), channel_id=1, source_target_pairs={{0,16},{4,20},{8,24},{12,28},{16,0},{20,4},{24,8},{28,12},{1,17},{... | collective-permute-start | bytes 774152 | tf_op jit(solution)/shard_map/ppermute | solution.py:49
  64.2 9.4 %collective-permute-start.24 = (bf16[3,96,896]{2,1,0:T(8,128)(2,1)S(1)}, bf16[3,96,896]{2,1,0:T(8,128)(2,1)S(1)}, u32[]{:S(2)}, u32[]{:S(2)}) collective-permute-start(bf16[3,96,896]{2,1,0:T(8,128)(2,1)S(1)} %constant_dynamic-slice_fusion.2), channel_id=1, source_target_pairs={{0,4},{4,0},{8,12},{12,8},{16,20},{20,16},{24,28},{28,24},{1,5},{5... | collective-permute-start | bytes 1548296 | tf_op jit(solution)/shard_map/ppermute | solution.py:37
  68.9 20.9 %collective-permute-start.14 = (bf16[3,96,896]{2,1,0:T(8,128)(2,1)S(1)}, bf16[3,96,896]{2,1,0:T(8,128)(2,1)S(1)}, u32[]{:S(2)}, u32[]{:S(2)}) collective-permute-start(bf16[3,96,896]{2,1,0:T(8,128)(2,1)S(1)} %maximum_select_fusion.4), channel_id=1, source_target_pairs={{0,4},{4,0},{8,12},{12,8},{16,20},{20,16},{24,28},{28,24},{1,5},{5... | collective-permute-start | bytes 1548296 | tf_op jit(solution)/shard_map/ppermute | solution.py:49
  71.8 18.4 %collective-permute-start.17 = (bf16[3,96,896]{2,1,0:T(8,128)(2,1)S(1)}, bf16[3,96,896]{2,1,0:T(8,128)(2,1)S(1)}, u32[]{:S(2)}, u32[]{:S(2)}) collective-permute-start(bf16[3,96,896]{2,1,0:T(8,128)(2,1)S(1)} %maximum_select_fusion.5), channel_id=1, source_target_pairs={{0,4},{4,0},{8,12},{12,8},{16,20},{20,16},{24,28},{28,24},{1,5},{5... | collective-permute-start | bytes 1548296 | tf_op jit(solution)/shard_map/ppermute | solution.py:49
  73.1 8.7 %collective-permute-start.19 = (bf16[3,48,896]{2,1,0:T(8,128)(2,1)S(1)}, bf16[3,48,896]{2,1,0:T(8,128)(2,1)S(1)}, u32[]{:S(2)}, u32[]{:S(2)}) collective-permute-start(bf16[3,48,896]{2,1,0:T(8,128)(2,1)S(1)} %constant_dynamic-slice_fusion.4), channel_id=1, source_target_pairs={{0,8},{4,12},{8,0},{12,4},{16,24},{20,28},{24,16},{28,20},{1,9},{5... | collective-permute-start | bytes 774152 | tf_op jit(solution)/shard_map/ppermute | solution.py:37
  73.6 17.1 %slice-start.2 = ((s8[7340032]{0:T(1024)(128)(4,1)}), s8[4194304]{0:T(1024)(128)(4,1)S(1)}, s32[]{:S(2)}) async-start(s8[7340032]{0:T(1024)(128)(4,1)} %bitcast.44), calls=%async_computation.2 | async-start | bytes 8388608
  73.8 8.9 %collective-permute-start.25 = (bf16[3,48,896]{2,1,0:T(8,128)(2,1)S(1)}, bf16[3,48,896]{2,1,0:T(8,128)(2,1)S(1)}, u32[]{:S(2)}, u32[]{:S(2)}) collective-permute-start(bf16[3,48,896]{2,1,0:T(8,128)(2,1)S(1)} %constant_dynamic-slice_fusion.1), channel_id=1, source_target_pairs={{0,16},{4,20},{8,24},{12,28},{16,0},{20,4},{24,8},{28,12},{1,17},{... | collective-permute-start | bytes 774152 | tf_op jit(solution)/shard_map/ppermute | solution.py:37
  81.9 5.1 %collective-permute-start.20 = (bf16[3,24,896]{2,1,0:T(8,128)(2,1)S(1)}, bf16[3,24,896]{2,1,0:T(8,128)(2,1)S(1)}, u32[]{:S(2)}, u32[]{:S(2)}) collective-permute-start(bf16[3,24,896]{2,1,0:T(8,128)(2,1)S(1)} %constant_dynamic-slice_fusion.3), channel_id=1, source_target_pairs={{0,16},{4,20},{8,24},{12,28},{16,0},{20,4},{24,8},{28,12},{1,17},{... | collective-permute-start | bytes 387080 | tf_op jit(solution)/shard_map/ppermute | solution.py:37
  82.7 5.4 %collective-permute-start.26 = (bf16[3,24,896]{2,1,0:T(8,128)(2,1)S(1)}, bf16[3,24,896]{2,1,0:T(8,128)(2,1)S(1)}, u32[]{:S(2)}, u32[]{:S(2)}) collective-permute-start(bf16[3,24,896]{2,1,0:T(8,128)(2,1)S(1)} %constant_dynamic-slice_fusion), channel_id=1, source_target_pairs={{0,8},{4,12},{8,0},{12,4},{16,24},{20,28},{24,16},{28,20},{1,9},{5... | collective-permute-start | bytes 387080 | tf_op jit(solution)/shard_map/ppermute | solution.py:37
  87.0 5.0 %collective-permute-start.21 = (bf16[3,24,896]{2,1,0:T(8,128)(2,1)S(1)}, bf16[3,24,896]{2,1,0:T(8,128)(2,1)S(1)}, u32[]{:S(2)}, u32[]{:S(2)}) collective-permute-start(bf16[3,24,896]{2,1,0:T(8,128)(2,1)S(1)} %pad_maximum_fusion.9), channel_id=1, source_target_pairs={{0,16},{4,20},{8,24},{12,28},{16,0},{20,4},{24,8},{28,12},{1,17},{... | collective-permute-start | bytes 387080 | tf_op jit(solution)/shard_map/ppermute | solution.py:49
  88.2 2.4 %slice-start.3 = ((s8[7340032]{0:T(1024)(128)(4,1)}), s8[3145728]{0:T(1024)(128)(4,1)S(1)}, s32[]{:S(2)}) async-start(s8[7340032]{0:T(1024)(128)(4,1)} %bitcast.44), calls=%async_computation.3 | async-start | bytes 6291456
  88.3 5.3 %collective-permute-start.27 = (bf16[3,24,896]{2,1,0:T(8,128)(2,1)S(1)}, bf16[3,24,896]{2,1,0:T(8,128)(2,1)S(1)}, u32[]{:S(2)}, u32[]{:S(2)}) collective-permute-start(bf16[3,24,896]{2,1,0:T(8,128)(2,1)S(1)} %pad_maximum_fusion.10), channel_id=1, source_target_pairs={{0,8},{4,12},{8,0},{12,4},{16,24},{20,28},{24,16},{28,20},{1,9},{5... | collective-permute-start | bytes 387080 | tf_op jit(solution)/shard_map/ppermute | solution.py:49
  90.7 9.5 %slice-start.6 = ((s8[7340032]{0:T(1024)(128)(4,1)}), s8[4194304]{0:T(1024)(128)(4,1)S(1)}, s32[]{:S(2)}) async-start(s8[7340032]{0:T(1024)(128)(4,1)} %bitcast.48), calls=%async_computation.6 | async-start | bytes 8388608
  92.1 6.7 %collective-permute-start.22 = (bf16[3,48,896]{2,1,0:T(8,128)(2,1)S(1)}, bf16[3,48,896]{2,1,0:T(8,128)(2,1)S(1)}, u32[]{:S(2)}, u32[]{:S(2)}) collective-permute-start(bf16[3,48,896]{2,1,0:T(8,128)(2,1)S(1)} %maximum_select_fusion.10), channel_id=1, source_target_pairs={{0,8},{4,12},{8,0},{12,4},{16,24},{20,28},{24,16},{28,20},{1,9},{5... | collective-permute-start | bytes 774152 | tf_op jit(solution)/shard_map/ppermute | solution.py:49
  93.6 6.6 %slice-start.7 = ((s8[7340032]{0:T(1024)(128)(4,1)}), s8[3145728]{0:T(1024)(128)(4,1)S(1)}, s32[]{:S(2)}) async-start(s8[7340032]{0:T(1024)(128)(4,1)} %bitcast.48), calls=%async_computation.7 | async-start | bytes 6291456
  93.6 6.4 %collective-permute-start.28 = (bf16[3,48,896]{2,1,0:T(8,128)(2,1)S(1)}, bf16[3,48,896]{2,1,0:T(8,128)(2,1)S(1)}, u32[]{:S(2)}, u32[]{:S(2)}) collective-permute-start(bf16[3,48,896]{2,1,0:T(8,128)(2,1)S(1)} %maximum_select_fusion.11), channel_id=1, source_target_pairs={{0,16},{4,20},{8,24},{12,28},{16,0},{20,4},{24,8},{28,12},{1,17},{... | collective-permute-start | bytes 774152 | tf_op jit(solution)/shard_map/ppermute | solution.py:49
  98.9 2.7 %collective-permute-start.23 = (bf16[3,96,896]{2,1,0:T(8,128)(2,1)S(1)}, bf16[3,96,896]{2,1,0:T(8,128)(2,1)S(1)}, u32[]{:S(2)}, u32[]{:S(2)}) collective-permute-start(bf16[3,96,896]{2,1,0:T(8,128)(2,1)S(1)} %maximum_select_fusion.6), channel_id=1, source_target_pairs={{0,4},{4,0},{8,12},{12,8},{16,20},{20,16},{24,28},{28,24},{1,5},{5... | collective-permute-start | bytes 1548296 | tf_op jit(solution)/shard_map/ppermute | solution.py:49
  100.1 2.0 %collective-permute-start.29 = (bf16[3,96,896]{2,1,0:T(8,128)(2,1)S(1)}, bf16[3,96,896]{2,1,0:T(8,128)(2,1)S(1)}, u32[]{:S(2)}, u32[]{:S(2)}) collective-permute-start(bf16[3,96,896]{2,1,0:T(8,128)(2,1)S(1)} %maximum_select_fusion.7), channel_id=1, source_target_pairs={{0,4},{4,0},{8,12},{12,8},{16,20},{20,16},{24,28},{28,24},{1,5},{5... | collective-permute-start | bytes 1548296 | tf_op jit(solution)/shard_map/ppermute | solution.py:49
  102.7 1.4 %copy-start.3 = (bf16[192,1024]{1,0:T(8,128)(2,1)S(1)}, bf16[192,1024]{1,0:T(8,128)(2,1)}, u32[]{:S(2)}) copy-start(bf16[192,1024]{1,0:T(8,128)(2,1)} %copy-done.2) | copy-start | bytes 1179652
  107.1 8.4 %copy-start.1 = (bf16[192,1024]{1,0:T(8,128)(2,1)S(1)}, bf16[192,1024]{1,0:T(8,128)(2,1)}, u32[]{:S(2)}) copy-start(bf16[192,1024]{1,0:T(8,128)(2,1)} %copy-done) | copy-start | bytes 1179652
  108.5 0.7 copy-start.4
  110.0 22.8 %collective-permute-start.30 = (bf16[48,1024]{1,0:T(8,128)(2,1)}, bf16[48,1024]{1,0:T(8,128)(2,1)}, u32[]{:S(2)}, u32[]{:S(2)}) collective-permute-start(bf16[48,1024]{1,0:T(8,128)(2,1)} %get-tuple-element.24), channel_id=1, source_target_pairs={{0,3},{1,0},{2,1},{3,2},{4,7},{5,4},{6,5},{7,6},{8,11},{9,8},{10,9... | collective-permute-start | bytes 294920 | tf_op jit(solution)/shard_map/ppermute | solution.py:95
  112.6 20.2 %collective-permute-start.32 = (bf16[48,1024]{1,0:T(8,128)(2,1)}, bf16[48,1024]{1,0:T(8,128)(2,1)}, u32[]{:S(2)}, u32[]{:S(2)}) collective-permute-start(bf16[48,1024]{1,0:T(8,128)(2,1)} %get-tuple-element.25), channel_id=1, source_target_pairs={{0,1},{1,2},{2,3},{3,0},{4,5},{5,6},{6,7},{7,4},{8,9},{9,10},{10,1... | collective-permute-start | bytes 294920 | tf_op jit(solution)/shard_map/ppermute | solution.py:95
  112.6 20.2 %collective-permute-start.31 = (bf16[48,1024]{1,0:T(8,128)(2,1)}, bf16[48,1024]{1,0:T(8,128)(2,1)}, u32[]{:S(2)}, u32[]{:S(2)}) collective-permute-start(bf16[48,1024]{1,0:T(8,128)(2,1)} %get-tuple-element.26), channel_id=1, source_target_pairs={{0,2},{1,3},{2,0},{3,1},{4,6},{5,7},{6,4},{7,5},{8,10},{9,11},{10,... | collective-permute-start | bytes 294920 | tf_op jit(solution)/shard_map/ppermute | solution.py:95

commit v6 on v4

--- a/solution.py
+++ b/solution.py
@@ -109,13 +109,14 @@
     partial_grad, grad_gate, grad_up, hidden = lax.optimization_barrier(
         (partial_grad.astype(jnp.bfloat16), grad_gate, grad_up, hidden)
     )
+    acc_gate = jnp.dot(tok_t, grad_gate, preferred_element_type=jnp.float32).astype(jnp.bfloat16)
+    partial_grad, acc_gate, grad_up, hidden = lax.optimization_barrier((partial_grad, acc_gate, grad_up, hidden))
     grad_tokens = col_reduce_scatter(partial_grad, n_col)
-    acc_gate = jnp.dot(tok_t, grad_gate, preferred_element_type=jnp.float32)
     acc_up = jnp.dot(tok_t, grad_up, preferred_element_type=jnp.float32)
     acc_down = contract_first(hidden, grad_all)
     return (
         grad_tokens,
-        acc_gate.astype(jnp.bfloat16),
+        acc_gate,
         acc_up.astype(jnp.bfloat16),
         acc_down.astype(jnp.bfloat16),
     )

time: 112 us -> 112 us (level)
  transfers between devices with their start and end apart: 21 -> 21, of which waited for: 10 -> 10; matrix products, arithmetic and copies ran while one was open for 26% -> 22% of each run, Pallas kernels for 0% -> 0%
where the time goes in v6:
time: 112 us; the launch traced here: 111 us
  waiting for transfers between devices  34.7 us (31%)
  starting transfers between devices  31.7 us (28%)
  matrix products  29.6 us (26%)
  other arithmetic  7.94 us (7%)
  local copies, waits for them, and re-layouts  6.29 us (6%)
    ppermute x6, waiting for transfers between devices, doubling_gather(): got = lax.ppermute(cur, 'row', [(j, j ^ bit) for j in range(n_dev)])  16.2 us
    ppermute x6, waiting for transfers between devices, halving_reduce(): got = lax.ppermute(send, 'row', [(j, j ^ bit) for j in range(n_dev)])  16.1 us
    ppermute x6, starting transfers between devices, col_gather(): lax.ppermute(x, 'col', [(j, (j + s) % n_col) for j in range(n_col)])  10.4 us
    ppermute x3, starting transfers between devices, col_reduce_scatter(): lax.ppermute(x[s * span:(s + 1) * span], 'col', [(j, (j - s) % n_col) for...  8.85 us
    dot_general x3, matrix products, contract_last(): lax.dot_general(left, right, (((1,), (1,)), ((), ())), preferred_element_...  7.58 us
    ppermute x6, starting transfers between devices, halving_reduce(): got = lax.ppermute(send, 'row', [(j, j ^ bit) for j in range(n_dev)])  6.67 us
    ppermute x6, starting transfers between devices, doubling_gather(): got = lax.ppermute(cur, 'row', [(j, j ^ bit) for j in range(n_dev)])  5.81 us
    dot_general x1, matrix products, body(): jnp.dot(tok_t, grad_gate, preferred_element_type=jnp.float32)  5.18 us
  transfers between devices with their start and end apart: 21, of which 10 were waited for; matrix products, arithmetic and copies ran while one was open for 22% of the time, Pallas kernels for 0%

profile of v6, /device:TPU:0, one launch (start us, length us, event | category | flops | bytes accessed | tf_op | source)
XLA Modules:
  0.0 111.3 jit_solution(12730645468141361854)
XLA Ops:
  0.6 4.1 %collective-permute-start.1 = (bf16[48,1024]{1,0:T(8,128)(2,1)}, bf16[48,1024]{1,0:T(8,128)(2,1)S(1)}, u32[]{:S(2)}, u32[]{:S(2)}) collective-permute-start(bf16[48,1024]{1,0:T(8,128)(2,1)} %param.5), channel_id=1, source_target_pairs={{0,2},{1,3},{2,0},{3,1},{4,6},{5,7},{6,4},{7,5},{8,10},{9,11},{10,... | collective-permute-start | bytes 294920 | tf_op jit(solution)/shard_map/ppermute | solution.py:80
  4.8 1.6 %collective-permute-start = (bf16[48,1024]{1,0:T(8,128)(2,1)}, bf16[48,1024]{1,0:T(8,128)(2,1)S(1)}, u32[]{:S(2)}, u32[]{:S(2)}) collective-permute-start(bf16[48,1024]{1,0:T(8,128)(2,1)} %param.5), channel_id=1, source_target_pairs={{0,1},{1,2},{2,3},{3,0},{4,5},{5,6},{6,7},{7,4},{8,9},{9,10},{10,1... | collective-permute-start | bytes 294920 | tf_op jit(solution)/shard_map/ppermute | solution.py:80
  6.3 2.2 %collective-permute-start.2 = (bf16[48,1024]{1,0:T(8,128)(2,1)}, bf16[48,1024]{1,0:T(8,128)(2,1)S(1)}, u32[]{:S(2)}, u32[]{:S(2)}) collective-permute-start(bf16[48,1024]{1,0:T(8,128)(2,1)} %param.5), channel_id=1, source_target_pairs={{0,3},{1,0},{2,1},{3,2},{4,7},{5,4},{6,5},{7,6},{8,11},{9,8},{10,9... | collective-permute-start | bytes 294920 | tf_op jit(solution)/shard_map/ppermute | solution.py:80
  8.6 0.6 collective-permute-start.3
  9.2 0.9 constant_dynamic-update-slice_fusion.3
  10.1 0.9 constant_dynamic-update-slice_fusion.7
  11.0 1.5 %collective-permute-done = bf16[48,1024]{1,0:T(8,128)(2,1)S(1)} collective-permute-done((bf16[48,1024]{1,0:T(8,128)(2,1)}, bf16[48,1024]{1,0:T(8,128)(2,1)S(1)}, u32[]{:S(2)}, u32[]{:S(2)}) %collective-permute-start) | collective-permute-done | bytes 98336 | tf_op jit(solution)/shard_map/ppermute | solution.py:80
  12.4 1.8 %collective-permute-start.5 = (bf16[48,1024]{1,0:T(8,128)(2,1)}, bf16[48,1024]{1,0:T(8,128)(2,1)S(1)}, u32[]{:S(2)}, u32[]{:S(2)}) collective-permute-start(bf16[48,1024]{1,0:T(8,128)(2,1)} %param.6), channel_id=1, source_target_pairs={{0,3},{1,0},{2,1},{3,2},{4,7},{5,4},{6,5},{7,6},{8,11},{9,8},{10,9... | collective-permute-start | bytes 294920 | tf_op jit(solution)/shard_map/ppermute | solution.py:80
  14.3 0.0 copy-start.3
  14.3 0.0 slice-start
  14.4 4.8 %fusion.1 = bf16[1,192,3584]{2,1,0:T(8,128)(2,1)S(1)} fusion(bf16[192,1024]{1,0:T(8,128)(2,1)S(1)} %constant_dynamic-update-slice_fusion, bf16[1024,3584]{1,0:T(8,128)(2,1)} %param.8), kind=kOutput, calls=%fused_computation.7 | convolution fusion | flops 1409974272 | bytes 9109504 | tf_op jit(solution)/shard_map/dot_general | solution.py:102
  19.2 0.3 copy-done.3
  19.5 1.7 %fusion = bf16[1,192,3584]{2,1,0:T(8,128)(2,1)S(1)} fusion(bf16[192,1024]{1,0:T(8,128)(2,1)S(1)} %constant_dynamic-update-slice_fusion, bf16[1024,3584]{1,0:T(8,128)(2,1)S(1)} %copy-done.3), kind=kOutput, calls=%fused_computation.6 | convolution fusion | flops 1409974272 | bytes 9109504 | tf_op jit(solution)/shard_map/dot_general | solution.py:101
  21.2 0.9 collective-permute-done.5
  22.2 2.6 %fusion.2 = bf16[1,192,3584]{2,1,0:T(8,128)(2,1)S(1)} fusion(bf16[192,1024]{1,0:T(8,128)(2,1)S(1)} %constant_dynamic-update-slice_fusion.4, bf16[3584,1024]{1,0:T(8,128)(2,1)S(1)} %bitcast.29), kind=kOutput, calls=%fused_computation.8 | convolution fusion | flops 1409974272 | bytes 9109504 | tf_op jit(solution)/shard_map/dot_general | solution.py:14
  24.7 0.7 pad_maximum_fusion
  25.4 0.3 fusion.9
  25.7 1.1 %constant_dynamic-slice_fusion.5 = bf16[3,96,1792]{2,1,0:T(8,128)(2,1)} fusion(bf16[3,192,1792]{2,1,0:T(8,128)(2,1)S(1)} %get-tuple-element.24, s32[]{:T(128)S(6)} %select_n.131), kind=kLoop, calls=%fused_computation.58 | loop fusion | bytes 2064388 | tf_op jit(solution)/shard_map/dynamic_slice | solution.py:36
  26.8 1.0 constant_dynamic-slice_fusion.2
  27.9 0.5 collective-permute-start.12
  28.4 1.4 %collective-permute-done.6 = bf16[3,96,1792]{2,1,0:T(8,128)(2,1)} collective-permute-done((bf16[3,96,1792]{2,1,0:T(8,128)(2,1)}, bf16[3,96,1792]{2,1,0:T(8,128)(2,1)}, u32[]{:S(2)}, u32[]{:S(2)}) %collective-permute-start.6) | collective-permute-done | bytes 1032224 | tf_op jit(solution)/shard_map/ppermute | solution.py:37
  29.8 1.8 %add_convert_fusion.1 = bf16[3,96,1792]{2,1,0:T(8,128)(2,1)S(1)} fusion(bf16[3,96,1792]{2,1,0:T(8,128)(2,1)} %collective-permute-done.6, bf16[3,192,1792]{2,1,0:T(8,128)(2,1)} %copy-done, s32[]{:T(128)S(6)} %select_n.130), kind=kLoop, calls=%fused_computation.17 | loop fusion | flops 2064384 | bytes 3096580 | tf_op jit(solution)/shard_map/convert_element_type | solution.py:40
  31.6 1.5 %collective-permute-start.7 = (bf16[3,48,1792]{2,1,0:T(8,128)(2,1)S(1)}, bf16[3,48,1792]{2,1,0:T(8,128)(2,1)S(1)}, u32[]{:S(2)}, u32[]{:S(2)}) collective-permute-start(bf16[3,48,1792]{2,1,0:T(8,128)(2,1)S(1)} %constant_dynamic-slice_fusion.4), channel_id=1, source_target_pairs={{0,8},{4,12},{8,0},{12,4},{16,24},{20,28},{24,16},{28,20},{1,9},{5... | collective-permute-start | bytes 1548296 | tf_op jit(solution)/shard_map/ppermute | solution.py:37
  33.2 0.3 add_convert_fusion
  33.5 1.6 %collective-permute-start.13 = (bf16[3,48,1792]{2,1,0:T(8,128)(2,1)S(1)}, bf16[3,48,1792]{2,1,0:T(8,128)(2,1)S(1)}, u32[]{:S(2)}, u32[]{:S(2)}) collective-permute-start(bf16[3,48,1792]{2,1,0:T(8,128)(2,1)S(1)} %constant_dynamic-slice_fusion.1), channel_id=1, source_target_pairs={{0,16},{4,20},{8,24},{12,28},{16,0},{20,4},{24,8},{28,12},{1,17},{... | collective-permute-start | bytes 1548296 | tf_op jit(solution)/shard_map/ppermute | solution.py:37
  35.0 10.5 %collective-permute-done.7 = bf16[3,48,1792]{2,1,0:T(8,128)(2,1)S(1)} collective-permute-done((bf16[3,48,1792]{2,1,0:T(8,128)(2,1)S(1)}, bf16[3,48,1792]{2,1,0:T(8,128)(2,1)S(1)}, u32[]{:S(2)}, u32[]{:S(2)}) %collective-permute-start.7) | collective-permute-done | bytes 516128 | tf_op jit(solution)/shard_map/ppermute | solution.py:37
  45.5 0.1 add_convert_fusion.3
  45.7 1.5 %collective-permute-start.8 = (bf16[3,24,1792]{2,1,0:T(8,128)(2,1)S(1)}, bf16[3,24,1792]{2,1,0:T(8,128)(2,1)S(1)}, u32[]{:S(2)}, u32[]{:S(2)}) collective-permute-start(bf16[3,24,1792]{2,1,0:T(8,128)(2,1)S(1)} %constant_dynamic-slice_fusion.3), channel_id=1, source_target_pairs={{0,16},{4,20},{8,24},{12,28},{16,0},{20,4},{24,8},{28,12},{1,17},{... | collective-permute-start | bytes 774152 | tf_op jit(solution)/shard_map/ppermute | solution.py:37
  47.2 0.1 add_convert_fusion.2
  47.4 1.5 %collective-permute-start.14 = (bf16[3,24,1792]{2,1,0:T(8,128)(2,1)S(1)}, bf16[3,24,1792]{2,1,0:T(8,128)(2,1)S(1)}, u32[]{:S(2)}, u32[]{:S(2)}) collective-permute-start(bf16[3,24,1792]{2,1,0:T(8,128)(2,1)S(1)} %constant_dynamic-slice_fusion), channel_id=1, source_target_pairs={{0,8},{4,12},{8,0},{12,4},{16,24},{20,28},{24,16},{28,20},{1,9},{5... | collective-permute-start | bytes 774152 | tf_op jit(solution)/shard_map/ppermute | solution.py:37
  48.9 4.2 %collective-permute-done.8 = bf16[3,24,1792]{2,1,0:T(8,128)(2,1)S(1)} collective-permute-done((bf16[3,24,1792]{2,1,0:T(8,128)(2,1)S(1)}, bf16[3,24,1792]{2,1,0:T(8,128)(2,1)S(1)}, u32[]{:S(2)}, u32[]{:S(2)}) %collective-permute-start.8) | collective-permute-done | bytes 258080 | tf_op jit(solution)/shard_map/ppermute | solution.py:37
  53.1 0.1 convert_add_fusion.1
  53.2 0.1 multiply_convert_fusion.5
  53.4 1.5 %collective-permute-start.9 = (bf16[3,24,1792]{2,1,0:T(8,128)(2,1)S(1)}, bf16[3,24,1792]{2,1,0:T(8,128)(2,1)S(1)}, u32[]{:S(2)}, u32[]{:S(2)}) collective-permute-start(bf16[3,24,1792]{2,1,0:T(8,128)(2,1)S(1)} %pad_maximum_fusion.2), channel_id=1, source_target_pairs={{0,16},{4,20},{8,24},{12,28},{16,0},{20,4},{24,8},{28,12},{1,17},{... | collective-permute-start | bytes 774152 | tf_op jit(solution)/shard_map/ppermute | solution.py:49
  54.9 0.1 convert_add_fusion
  55.0 0.1 multiply_convert_fusion.2
  55.1 1.5 %collective-permute-start.15 = (bf16[3,24,1792]{2,1,0:T(8,128)(2,1)S(1)}, bf16[3,24,1792]{2,1,0:T(8,128)(2,1)S(1)}, u32[]{:S(2)}, u32[]{:S(2)}) collective-permute-start(bf16[3,24,1792]{2,1,0:T(8,128)(2,1)S(1)} %pad_maximum_fusion.3), channel_id=1, source_target_pairs={{0,8},{4,12},{8,0},{12,4},{16,24},{20,28},{24,16},{28,20},{1,9},{5... | collective-permute-start | bytes 774152 | tf_op jit(solution)/shard_map/ppermute | solution.py:49
  56.7 3.3 %collective-permute-done.9 = bf16[3,24,1792]{2,1,0:T(8,128)(2,1)S(1)} collective-permute-done((bf16[3,24,1792]{2,1,0:T(8,128)(2,1)S(1)}, bf16[3,24,1792]{2,1,0:T(8,128)(2,1)S(1)}, u32[]{:S(2)}, u32[]{:S(2)}) %collective-permute-start.9) | collective-permute-done | bytes 258080 | tf_op jit(solution)/shard_map/ppermute | solution.py:49
  60.0 0.1 maximum_select_fusion.4
  60.1 1.5 %collective-permute-start.10 = (bf16[3,48,1792]{2,1,0:T(8,128)(2,1)S(1)}, bf16[3,48,1792]{2,1,0:T(8,128)(2,1)S(1)}, u32[]{:S(2)}, u32[]{:S(2)}) collective-permute-start(bf16[3,48,1792]{2,1,0:T(8,128)(2,1)S(1)} %maximum_select_fusion.4), channel_id=1, source_target_pairs={{0,8},{4,12},{8,0},{12,4},{16,24},{20,28},{24,16},{28,20},{1,9},{5... | collective-permute-start | bytes 1548296 | tf_op jit(solution)/shard_map/ppermute | solution.py:49
  61.6 1.1 %collective-permute-done.15 = bf16[3,24,1792]{2,1,0:T(8,128)(2,1)S(1)} collective-permute-done((bf16[3,24,1792]{2,1,0:T(8,128)(2,1)S(1)}, bf16[3,24,1792]{2,1,0:T(8,128)(2,1)S(1)}, u32[]{:S(2)}, u32[]{:S(2)}) %collective-permute-start.15) | collective-permute-done | bytes 258080 | tf_op jit(solution)/shard_map/ppermute | solution.py:49
  62.7 0.1 maximum_select_fusion.5
  62.8 0.6 collective-permute-start.16
  63.4 9.1 %collective-permute-done.10 = bf16[3,48,1792]{2,1,0:T(8,128)(2,1)S(1)} collective-permute-done((bf16[3,48,1792]{2,1,0:T(8,128)(2,1)S(1)}, bf16[3,48,1792]{2,1,0:T(8,128)(2,1)S(1)}, u32[]{:S(2)}, u32[]{:S(2)}) %collective-permute-start.10) | collective-permute-done | bytes 516128 | tf_op jit(solution)/shard_map/ppermute | solution.py:49
  72.6 0.3 maximum_select_fusion.2
  72.8 0.1 collective-permute-start.11
  72.9 0.3 maximum_select_fusion.3
  73.2 0.6 collective-permute-start.17
  73.7 1.8 %collective-permute-done.11 = bf16[3,96,1792]{2,1,0:T(8,128)(2,1)S(1)} collective-permute-done((bf16[3,96,1792]{2,1,0:T(8,128)(2,1)S(1)}, bf16[3,96,1792]{2,1,0:T(8,128)(2,1)S(1)}, u32[]{:S(2)}, u32[]{:S(2)}) %collective-permute-start.11) | collective-permute-done | bytes 1032224 | tf_op jit(solution)/shard_map/ppermute | solution.py:49
  75.5 0.8 maximum_select_fusion
  76.3 0.8 collective-permute-done.17
  77.1 2.0 %maximum_select_fusion.1 = bf16[3,192,1792]{2,1,0:T(8,128)(2,1)S(1)} fusion(bf16[3,96,1792]{2,1,0:T(8,128)(2,1)S(1)} %maximum_select_fusion.3, bf16[3,96,1792]{2,1,0:T(8,128)(2,1)} %collective-permute-done.17, pred[]{:T(512)S(6)} %eq.25), kind=kLoop, calls=%fused_computation.15 | loop fusion | flops 9289728 | bytes 4128769 | tf_op jit(solution)/shard_map/jit(_where)/select_n | solution.py:50
  79.2 0.0 slice-start.3
  79.2 0.0 slice-start.4
  79.2 0.4 fusion.7
  79.6 1.5 %slice-done.3 = s8[3145728]{0:T(1024)(128)(4,1)S(1)} async-done(((s8[7340032]{0:T(1024)(128)(4,1)}), s8[3145728]{0:T(1024)(128)(4,1)S(1)}, s32[]{:S(2)}) %slice-start.3) | async-done | bytes 3145752
  81.1 2.5 %fusion.11 = f32[192,1024]{1,0:T(8,128)S(1)} fusion(bf16[192,3584]{1,0:T(8,128)(2,1)S(1)} %get-tuple-element.18, bf16[1024,3584]{1,0:T(8,128)(2,1)S(1)} %bitcast.31), kind=kOutput, calls=%fused_computation.61 | convolution fusion | flops 1409286144 | bytes 9502720 | tf_op jit(solution)/shard_map/dot_general | solution.py:14
  83.6 2.5 %fusion.8 = bf16[192,1024]{1,0:T(8,128)(2,1)S(1)} fusion(f32[192,1024]{1,0:T(8,128)S(1)} %fusion.11, bf16[192,3584]{1,0:T(8,128)(2,1)S(1)} %get-tuple-element.13, bf16[1024,3584]{1,0:T(8,128)(2,1)S(1)} %bitcast.33), kind=kOutput, calls=%fused_computation.25 | convolution fusion | flops 1409679360 | bytes 9895936 | tf_op jit(solution)/shard_map/dot_general | solution.py:14
  86.1 5.2 %convolution_convert_fusion.2 = bf16[1024,3584]{1,0:T(8,128)(2,1)} fusion(bf16[192,1024]{1,0:T(8,128)(2,1)S(1)} %constant_dynamic-update-slice_fusion, bf16[192,3584]{1,0:T(8,128)(2,1)S(1)} %get-tuple-element.13), kind=kOutput, calls=%fused_computation.2 | convolution fusion | flops 1412956160 | bytes 9109504 | tf_op jit(solution)/shard_map/dot_general | solution.py:112
  91.4 8.0 %collective-permute-start.18 = (bf16[48,1024]{1,0:T(8,128)(2,1)S(1)}, bf16[48,1024]{1,0:T(8,128)(2,1)S(1)}, u32[]{:S(2)}, u32[]{:S(2)}) collective-permute-start(bf16[48,1024]{1,0:T(8,128)(2,1)S(1)} %get-tuple-element.31), channel_id=1, source_target_pairs={{0,3},{1,0},{2,1},{3,2},{4,7},{5,4},{6,5},{7,6},{8,11},{9,8},{10,9... | collective-permute-start | bytes 294920 | tf_op jit(solution)/shard_map/ppermute | solution.py:88
  99.4 0.8 collective-permute-start.19
  100.2 5.2 %convolution_convert_fusion.1 = bf16[1024,3584]{1,0:T(8,128)(2,1)} fusion(bf16[192,1024]{1,0:T(8,128)(2,1)S(1)} %constant_dynamic-update-slice_fusion, bf16[192,3584]{1,0:T(8,128)(2,1)S(1)} %get-tuple-element.18), kind=kOutput, calls=%fused_computation.1 | convolution fusion | flops 1412956160 | bytes 9109504 | tf_op jit(solution)/shard_map/dot_general | solution.py:115
  105.4 5.2 %convolution_convert_fusion = bf16[3584,1024]{1,0:T(8,128)(2,1)} fusion(bf16[192,3584]{1,0:T(8,128)(2,1)S(1)} %get-tuple-element.19, bf16[192,1024]{1,0:T(8,128)(2,1)S(1)} %copy-done.2), kind=kOutput, calls=%fused_computation | convolution fusion | flops 1412956160 | bytes 9109504 | tf_op jit(solution)/shard_map/dot_general | solution.py:8
  110.6 0.7 add_convert_fusion.4
  (44 shorter events, 0.3 us)
Async XLA Ops:
  0.6 13.7 %collective-permute-start.1 = (bf16[48,1024]{1,0:T(8,128)(2,1)}, bf16[48,1024]{1,0:T(8,128)(2,1)S(1)}, u32[]{:S(2)}, u32[]{:S(2)}) collective-permute-start(bf16[48,1024]{1,0:T(8,128)(2,1)} %param.5), channel_id=1, source_target_pairs={{0,2},{1,3},{2,0},{3,1},{4,6},{5,7},{6,4},{7,5},{8,10},{9,11},{10,... | collective-permute-start | bytes 294920 | tf_op jit(solution)/shard_map/ppermute | solution.py:80
  4.8 7.7 %collective-permute-start = (bf16[48,1024]{1,0:T(8,128)(2,1)}, bf16[48,1024]{1,0:T(8,128)(2,1)S(1)}, u32[]{:S(2)}, u32[]{:S(2)}) collective-permute-start(bf16[48,1024]{1,0:T(8,128)(2,1)} %param.5), channel_id=1, source_target_pairs={{0,1},{1,2},{2,3},{3,0},{4,5},{5,6},{6,7},{7,4},{8,9},{9,10},{10,1... | collective-permute-start | bytes 294920 | tf_op jit(solution)/shard_map/ppermute | solution.py:80
  6.3 8.0 %collective-permute-start.2 = (bf16[48,1024]{1,0:T(8,128)(2,1)}, bf16[48,1024]{1,0:T(8,128)(2,1)S(1)}, u32[]{:S(2)}, u32[]{:S(2)}) collective-permute-start(bf16[48,1024]{1,0:T(8,128)(2,1)} %param.5), channel_id=1, source_target_pairs={{0,3},{1,0},{2,1},{3,2},{4,7},{5,4},{6,5},{7,6},{8,11},{9,8},{10,9... | collective-permute-start | bytes 294920 | tf_op jit(solution)/shard_map/ppermute | solution.py:80
  8.6 12.6 %collective-permute-start.4 = (bf16[48,1024]{1,0:T(8,128)(2,1)}, bf16[48,1024]{1,0:T(8,128)(2,1)S(1)}, u32[]{:S(2)}, u32[]{:S(2)}) collective-permute-start(bf16[48,1024]{1,0:T(8,128)(2,1)} %param.6), channel_id=1, source_target_pairs={{0,2},{1,3},{2,0},{3,1},{4,6},{5,7},{6,4},{7,5},{8,10},{9,11},{10,... | collective-permute-start | bytes 294920 | tf_op jit(solution)/shard_map/ppermute | solution.py:80
  8.6 12.6 %collective-permute-start.3 = (bf16[48,1024]{1,0:T(8,128)(2,1)}, bf16[48,1024]{1,0:T(8,128)(2,1)S(1)}, u32[]{:S(2)}, u32[]{:S(2)}) collective-permute-start(bf16[48,1024]{1,0:T(8,128)(2,1)} %param.6), channel_id=1, source_target_pairs={{0,1},{1,2},{2,3},{3,0},{4,5},{5,6},{6,7},{7,4},{8,9},{9,10},{10,1... | collective-permute-start | bytes 294920 | tf_op jit(solution)/shard_map/ppermute | solution.py:80
  12.4 9.7 %collective-permute-start.5 = (bf16[48,1024]{1,0:T(8,128)(2,1)}, bf16[48,1024]{1,0:T(8,128)(2,1)S(1)}, u32[]{:S(2)}, u32[]{:S(2)}) collective-permute-start(bf16[48,1024]{1,0:T(8,128)(2,1)} %param.6), channel_id=1, source_target_pairs={{0,3},{1,0},{2,1},{3,2},{4,7},{5,4},{6,5},{7,6},{8,11},{9,8},{10,9... | collective-permute-start | bytes 294920 | tf_op jit(solution)/shard_map/ppermute | solution.py:80
  14.3 5.2 %copy-start.3 = (bf16[1024,3584]{1,0:T(8,128)(2,1)S(1)}, bf16[1024,3584]{1,0:T(8,128)(2,1)}, u32[]{:S(2)}) copy-start(bf16[1024,3584]{1,0:T(8,128)(2,1)} %param.7) | copy-start | bytes 22020100
  14.3 7.8 %slice-start = ((s8[7340032]{0:T(1024)(128)(4,1)}), s8[4194304]{0:T(1024)(128)(4,1)S(1)}, s32[]{:S(2)}) async-start(s8[7340032]{0:T(1024)(128)(4,1)} %bitcast.28), calls=%async_computation | async-start | bytes 8388608
  19.5 2.6 %slice-start.1 = ((s8[7340032]{0:T(1024)(128)(4,1)}), s8[3145728]{0:T(1024)(128)(4,1)S(1)}, s32[]{:S(2)}) async-start(s8[7340032]{0:T(1024)(128)(4,1)} %bitcast.28), calls=%async_computation.1 | async-start | bytes 6291456
  22.2 2.6 %copy-start.1 = (bf16[192,1024]{1,0:T(8,128)(2,1)}, bf16[192,1024]{1,0:T(8,128)(2,1)S(1)}, u32[]{:S(2)}) copy-start(bf16[192,1024]{1,0:T(8,128)(2,1)S(1)} %constant_dynamic-update-slice_fusion.4) | copy-start | bytes 1179652
  25.7 2.2 %copy-start = (bf16[3,192,1792]{2,1,0:T(8,128)(2,1)}, bf16[3,192,1792]{2,1,0:T(8,128)(2,1)S(1)}, u32[]{:S(2)}) copy-start(bf16[3,192,1792]{2,1,0:T(8,128)(2,1)S(1)} %get-tuple-element.24) | copy-start | bytes 6193156
  26.8 3.0 %collective-permute-start.6 = (bf16[3,96,1792]{2,1,0:T(8,128)(2,1)}, bf16[3,96,1792]{2,1,0:T(8,128)(2,1)}, u32[]{:S(2)}, u32[]{:S(2)}) collective-permute-start(bf16[3,96,1792]{2,1,0:T(8,128)(2,1)} %constant_dynamic-slice_fusion.5), channel_id=1, source_target_pairs={{0,4},{4,0},{8,12},{12,8},{16,20},{20,16},{24,28},{28,24},{1,5},{5... | collective-permute-start | bytes 3096584 | tf_op jit(solution)/shard_map/ppermute | solution.py:37
  27.9 5.3 %collective-permute-start.12 = (bf16[3,96,1792]{2,1,0:T(8,128)(2,1)}, bf16[3,96,1792]{2,1,0:T(8,128)(2,1)S(1)}, u32[]{:S(2)}, u32[]{:S(2)}) collective-permute-start(bf16[3,96,1792]{2,1,0:T(8,128)(2,1)} %constant_dynamic-slice_fusion.2), channel_id=1, source_target_pairs={{0,4},{4,0},{8,12},{12,8},{16,20},{20,16},{24,28},{28,24},{1,5},{5... | collective-permute-start | bytes 3096584 | tf_op jit(solution)/shard_map/ppermute | solution.py:37
  31.6 13.9 %collective-permute-start.7 = (bf16[3,48,1792]{2,1,0:T(8,128)(2,1)S(1)}, bf16[3,48,1792]{2,1,0:T(8,128)(2,1)S(1)}, u32[]{:S(2)}, u32[]{:S(2)}) collective-permute-start(bf16[3,48,1792]{2,1,0:T(8,128)(2,1)S(1)} %constant_dynamic-slice_fusion.4), channel_id=1, source_target_pairs={{0,8},{4,12},{8,0},{12,4},{16,24},{20,28},{24,16},{28,20},{1,9},{5... | collective-permute-start | bytes 1548296 | tf_op jit(solution)/shard_map/ppermute | solution.py:37
  33.5 13.7 %collective-permute-start.13 = (bf16[3,48,1792]{2,1,0:T(8,128)(2,1)S(1)}, bf16[3,48,1792]{2,1,0:T(8,128)(2,1)S(1)}, u32[]{:S(2)}, u32[]{:S(2)}) collective-permute-start(bf16[3,48,1792]{2,1,0:T(8,128)(2,1)S(1)} %constant_dynamic-slice_fusion.1), channel_id=1, source_target_pairs={{0,16},{4,20},{8,24},{12,28},{16,0},{20,4},{24,8},{28,12},{1,17},{... | collective-permute-start | bytes 1548296 | tf_op jit(solution)/shard_map/ppermute | solution.py:37
  45.7 7.5 %collective-permute-start.8 = (bf16[3,24,1792]{2,1,0:T(8,128)(2,1)S(1)}, bf16[3,24,1792]{2,1,0:T(8,128)(2,1)S(1)}, u32[]{:S(2)}, u32[]{:S(2)}) collective-permute-start(bf16[3,24,1792]{2,1,0:T(8,128)(2,1)S(1)} %constant_dynamic-slice_fusion.3), channel_id=1, source_target_pairs={{0,16},{4,20},{8,24},{12,28},{16,0},{20,4},{24,8},{28,12},{1,17},{... | collective-permute-start | bytes 774152 | tf_op jit(solution)/shard_map/ppermute | solution.py:37
  47.4 7.5 %collective-permute-start.14 = (bf16[3,24,1792]{2,1,0:T(8,128)(2,1)S(1)}, bf16[3,24,1792]{2,1,0:T(8,128)(2,1)S(1)}, u32[]{:S(2)}, u32[]{:S(2)}) collective-permute-start(bf16[3,24,1792]{2,1,0:T(8,128)(2,1)S(1)} %constant_dynamic-slice_fusion), channel_id=1, source_target_pairs={{0,8},{4,12},{8,0},{12,4},{16,24},{20,28},{24,16},{28,20},{1,9},{5... | collective-permute-start | bytes 774152 | tf_op jit(solution)/shard_map/ppermute | solution.py:37
  53.4 6.6 %collective-permute-start.9 = (bf16[3,24,1792]{2,1,0:T(8,128)(2,1)S(1)}, bf16[3,24,1792]{2,1,0:T(8,128)(2,1)S(1)}, u32[]{:S(2)}, u32[]{:S(2)}) collective-permute-start(bf16[3,24,1792]{2,1,0:T(8,128)(2,1)S(1)} %pad_maximum_fusion.2), channel_id=1, source_target_pairs={{0,16},{4,20},{8,24},{12,28},{16,0},{20,4},{24,8},{28,12},{1,17},{... | collective-permute-start | bytes 774152 | tf_op jit(solution)/shard_map/ppermute | solution.py:49
  55.1 7.6 %collective-permute-start.15 = (bf16[3,24,1792]{2,1,0:T(8,128)(2,1)S(1)}, bf16[3,24,1792]{2,1,0:T(8,128)(2,1)S(1)}, u32[]{:S(2)}, u32[]{:S(2)}) collective-permute-start(bf16[3,24,1792]{2,1,0:T(8,128)(2,1)S(1)} %pad_maximum_fusion.3), channel_id=1, source_target_pairs={{0,8},{4,12},{8,0},{12,4},{16,24},{20,28},{24,16},{28,20},{1,9},{5... | collective-permute-start | bytes 774152 | tf_op jit(solution)/shard_map/ppermute | solution.py:49
  60.1 12.5 %collective-permute-start.10 = (bf16[3,48,1792]{2,1,0:T(8,128)(2,1)S(1)}, bf16[3,48,1792]{2,1,0:T(8,128)(2,1)S(1)}, u32[]{:S(2)}, u32[]{:S(2)}) collective-permute-start(bf16[3,48,1792]{2,1,0:T(8,128)(2,1)S(1)} %maximum_select_fusion.4), channel_id=1, source_target_pairs={{0,8},{4,12},{8,0},{12,4},{16,24},{20,28},{24,16},{28,20},{1,9},{5... | collective-permute-start | bytes 1548296 | tf_op jit(solution)/shard_map/ppermute | solution.py:49
  62.8 10.1 %collective-permute-start.16 = (bf16[3,48,1792]{2,1,0:T(8,128)(2,1)S(1)}, bf16[3,48,1792]{2,1,0:T(8,128)(2,1)S(1)}, u32[]{:S(2)}, u32[]{:S(2)}) collective-permute-start(bf16[3,48,1792]{2,1,0:T(8,128)(2,1)S(1)} %maximum_select_fusion.5), channel_id=1, source_target_pairs={{0,16},{4,20},{8,24},{12,28},{16,0},{20,4},{24,8},{28,12},{1,17},{... | collective-permute-start | bytes 1548296 | tf_op jit(solution)/shard_map/ppermute | solution.py:49
  72.8 2.7 %collective-permute-start.11 = (bf16[3,96,1792]{2,1,0:T(8,128)(2,1)S(1)}, bf16[3,96,1792]{2,1,0:T(8,128)(2,1)S(1)}, u32[]{:S(2)}, u32[]{:S(2)}) collective-permute-start(bf16[3,96,1792]{2,1,0:T(8,128)(2,1)S(1)} %maximum_select_fusion.2), channel_id=1, source_target_pairs={{0,4},{4,0},{8,12},{12,8},{16,20},{20,16},{24,28},{28,24},{1,5},{5... | collective-permute-start | bytes 3096584 | tf_op jit(solution)/shard_map/ppermute | solution.py:49
  73.2 4.0 %collective-permute-start.17 = (bf16[3,96,1792]{2,1,0:T(8,128)(2,1)S(1)}, bf16[3,96,1792]{2,1,0:T(8,128)(2,1)}, u32[]{:S(2)}, u32[]{:S(2)}) collective-permute-start(bf16[3,96,1792]{2,1,0:T(8,128)(2,1)S(1)} %maximum_select_fusion.3), channel_id=1, source_target_pairs={{0,4},{4,0},{8,12},{12,8},{16,20},{20,16},{24,28},{28,24},{1,5},{5... | collective-permute-start | bytes 3096584 | tf_op jit(solution)/shard_map/ppermute | solution.py:49
  75.5 4.1 %slice-start.2 = ((s8[7340032]{0:T(1024)(128)(4,1)}), s8[4194304]{0:T(1024)(128)(4,1)S(1)}, s32[]{:S(2)}) async-start(s8[7340032]{0:T(1024)(128)(4,1)} %bitcast.30), calls=%async_computation.2 | async-start | bytes 8388608
  79.2 1.9 %slice-start.3 = ((s8[7340032]{0:T(1024)(128)(4,1)}), s8[3145728]{0:T(1024)(128)(4,1)S(1)}, s32[]{:S(2)}) async-start(s8[7340032]{0:T(1024)(128)(4,1)} %bitcast.30), calls=%async_computation.3 | async-start | bytes 6291456
  79.2 4.4 %slice-start.4 = ((s8[7340032]{0:T(1024)(128)(4,1)}), s8[4194304]{0:T(1024)(128)(4,1)S(1)}, s32[]{:S(2)}) async-start(s8[7340032]{0:T(1024)(128)(4,1)} %bitcast.32), calls=%async_computation.4 | async-start | bytes 8388608
  81.1 2.5 %slice-start.5 = ((s8[7340032]{0:T(1024)(128)(4,1)}), s8[3145728]{0:T(1024)(128)(4,1)S(1)}, s32[]{:S(2)}) async-start(s8[7340032]{0:T(1024)(128)(4,1)} %bitcast.32), calls=%async_computation.5 | async-start | bytes 6291456
  91.4 19.2 %collective-permute-start.18 = (bf16[48,1024]{1,0:T(8,128)(2,1)S(1)}, bf16[48,1024]{1,0:T(8,128)(2,1)S(1)}, u32[]{:S(2)}, u32[]{:S(2)}) collective-permute-start(bf16[48,1024]{1,0:T(8,128)(2,1)S(1)} %get-tuple-element.31), channel_id=1, source_target_pairs={{0,3},{1,0},{2,1},{3,2},{4,7},{5,4},{6,5},{7,6},{8,11},{9,8},{10,9... | collective-permute-start | bytes 294920 | tf_op jit(solution)/shard_map/ppermute | solution.py:88
  99.4 11.2 %collective-permute-start.20 = (bf16[48,1024]{1,0:T(8,128)(2,1)S(1)}, bf16[48,1024]{1,0:T(8,128)(2,1)S(1)}, u32[]{:S(2)}, u32[]{:S(2)}) collective-permute-start(bf16[48,1024]{1,0:T(8,128)(2,1)S(1)} %get-tuple-element.32), channel_id=1, source_target_pairs={{0,1},{1,2},{2,3},{3,0},{4,5},{5,6},{6,7},{7,4},{8,9},{9,10},{10,1... | collective-permute-start | bytes 294920 | tf_op jit(solution)/shard_map/ppermute | solution.py:88
  99.4 6.0 %copy-start.2 = (bf16[192,1024]{1,0:T(8,128)(2,1)S(1)}, bf16[192,1024]{1,0:T(8,128)(2,1)}, u32[]{:S(2)}) copy-start(bf16[192,1024]{1,0:T(8,128)(2,1)} %copy-done.1) | copy-start | bytes 1179652
  99.4 11.2 %collective-permute-start.19 = (bf16[48,1024]{1,0:T(8,128)(2,1)S(1)}, bf16[48,1024]{1,0:T(8,128)(2,1)S(1)}, u32[]{:S(2)}, u32[]{:S(2)}) collective-permute-start(bf16[48,1024]{1,0:T(8,128)(2,1)S(1)} %get-tuple-element.33), channel_id=1, source_target_pairs={{0,2},{1,3},{2,0},{3,1},{4,6},{5,7},{6,4},{7,5},{8,10},{9,11},{10,... | collective-permute-start | bytes 294920 | tf_op jit(solution)/shard_map/ppermute | solution.py:88

commit v7 on v6

--- a/solution.py
+++ b/solution.py
@@ -93,8 +93,10 @@
 def body(tokens, grad_out, gate_weight, up_weight, down_weight):
     n_row = lax.psum(1, "row")
     n_col = lax.psum(1, "col")
-    tok_all = col_gather(tokens, n_col)
-    grad_all = col_gather(grad_out, n_col)
+    feat = tokens.shape[1]
+    both_all = col_gather(jnp.concatenate([tokens, grad_out], axis=1), n_col)
+    tok_all = both_all[:, :feat]
+    grad_all = both_all[:, feat:]
     tok_t = tok_all.T
     stacked = jnp.stack(
         [

time: 112 us -> 120 us (1.071)
  waiting for transfers between devices: 34.7 us -> 51.3 us
  starting transfers between devices: 31.7 us -> 19.6 us
  other arithmetic: 7.94 us -> 10.6 us
    ppermute x6 -> x3, waiting for transfers between devices: 2.39 us -> 15.7 us  [col_gather(): lax.ppermute(x, 'col', [(j, (j + s) % n_col) for j in range(n_col)])]
    ppermute x6 -> x3, starting transfers between devices: 10.4 us -> 6.09 us  [col_gather(): lax.ppermute(x, 'col', [(j, (j + s) % n_col) for j in range(n_col)])]
    ppermute x3, starting transfers between devices: 8.85 us -> 4.89 us  [col_reduce_scatter(): lax.ppermute(x[s * span:(s + 1) * span], 'col', [(j, (j - s) % n_col) for...]
    ppermute x6, starting transfers between devices: 5.81 us -> 3.35 us  [doubling_gather(): got = lax.ppermute(cur, 'row', [(j, j ^ bit) for j in range(n_dev)])]
    ppermute x6, waiting for transfers between devices: 16.2 us -> 18.7 us  [doubling_gather(): got = lax.ppermute(cur, 'row', [(j, j ^ bit) for j in range(n_dev)])]
    select_n x6, other arithmetic: 3.52 us -> 4.94 us  [doubling_gather(): jnp.where(hi == 1, jnp.concatenate([got, cur], axis=1), jnp.concatenate([...]
    ppermute x6, starting transfers between devices: 6.67 us -> 5.3 us  [halving_reduce(): got = lax.ppermute(send, 'row', [(j, j ^ bit) for j in range(n_dev)])]
    convert_element_type x4, other arithmetic: 2.28 us -> 3.49 us  [halving_reduce(): cur = cur.astype(jnp.bfloat16)]
  transfers between devices with their start and end apart: 21 -> 18, of which waited for: 10 -> 11; matrix products, arithmetic and copies ran while one was open for 22% -> 15% of each run, Pallas kernels for 0% -> 0%
where the time goes in v7:
time: 120 us
  waiting for transfers between devices  51.3 us (43%)
  matrix products  29.6 us (25%)
  starting transfers between devices  19.6 us (16%)
  other arithmetic  10.6 us (9%)
  local copies, waits for them, and re-layouts  7.46 us (6%)
    ppermute x6, waiting for transfers between devices, doubling_gather(): got = lax.ppermute(cur, 'row', [(j, j ^ bit) for j in range(n_dev)])  18.7 us
    ppermute x6, waiting for transfers between devices, halving_reduce(): got = lax.ppermute(send, 'row', [(j, j ^ bit) for j in range(n_dev)])  17 us
    ppermute x3, waiting for transfers between devices, col_gather(): lax.ppermute(x, 'col', [(j, (j + s) % n_col) for j in range(n_col)])  15.7 us
    dot_general x3, matrix products, contract_last(): lax.dot_general(left, right, (((1,), (1,)), ((), ())), preferred_element_...  7.58 us
    ppermute x3, starting transfers between devices, col_gather(): lax.ppermute(x, 'col', [(j, (j + s) % n_col) for j in range(n_col)])  6.09 us
    ppermute x6, starting transfers between devices, halving_reduce(): got = lax.ppermute(send, 'row', [(j, j ^ bit) for j in range(n_dev)])  5.3 us
    dot_general x1, matrix products, contract_first(): lax.dot_general(left, right, (((0,), (0,)), ((), ())), preferred_element_...  5.19 us
    dot_general x1, matrix products, body(): jnp.dot(tok_t, grad_gate, preferred_element_type=jnp.float32)  5.18 us
  transfers between devices with their start and end apart: 18, of which 11 were waited for; matrix products, arithmetic and copies ran while one was open for 15% of the time, Pallas kernels for 0%

profile of v7, /device:TPU:0, one launch (start us, length us, event | category | flops | bytes accessed | tf_op | source)
XLA Modules:
  0.0 119.5 jit_solution(1687606505423169856)
XLA Ops:
  0.6 0.9 constant_dynamic-update-slice_fusion.1
  1.5 0.9 constant_dynamic-update-slice_fusion
  2.4 5.1 %collective-permute-start.2 = (bf16[48,2048]{1,0:T(8,128)(2,1)S(1)}, bf16[48,2048]{1,0:T(8,128)(2,1)S(1)}, u32[]{:S(2)}, u32[]{:S(2)}) collective-permute-start(bf16[48,2048]{1,0:T(8,128)(2,1)S(1)} %constant_dynamic-update-slice_fusion), channel_id=1, source_target_pairs={{0,3},{1,0},{2,1},{3,2},{4,7},{5,4},{6,5},{7,6},{8,11},{9,8},{10,9... | collective-permute-start | bytes 589832 | tf_op jit(solution)/shard_map/ppermute | solution.py:80
  7.5 1.0 collective-permute-start
  8.5 4.3 %collective-permute-done.2 = bf16[48,2048]{1,0:T(8,128)(2,1)S(1)} collective-permute-done((bf16[48,2048]{1,0:T(8,128)(2,1)S(1)}, bf16[48,2048]{1,0:T(8,128)(2,1)S(1)}, u32[]{:S(2)}, u32[]{:S(2)}) %collective-permute-start.2) | collective-permute-done | bytes 196640 | tf_op jit(solution)/shard_map/ppermute | solution.py:80
  12.8 11.4 %collective-permute-done.1 = bf16[48,2048]{1,0:T(8,128)(2,1)S(1)} collective-permute-done((bf16[48,2048]{1,0:T(8,128)(2,1)S(1)}, bf16[48,2048]{1,0:T(8,128)(2,1)S(1)}, u32[]{:S(2)}, u32[]{:S(2)}) %collective-permute-start.1) | collective-permute-done | bytes 196640 | tf_op jit(solution)/shard_map/ppermute | solution.py:80
  24.2 0.1 pad_maximum_fusion.2
  24.3 0.0 slice-start.1
  24.3 0.0 slice-start.5
  24.3 4.8 %fusion.1 = bf16[1,192,3584]{2,1,0:T(8,128)(2,1)S(1)} fusion(bf16[1024,3584]{1,0:T(8,128)(2,1)} %param.8, bf16[192,2048]{1,0:T(8,128)(2,1)S(1)} %pad_maximum_fusion.2), kind=kOutput, calls=%fused_computation.7 | convolution fusion | flops 1409974272 | bytes 9109504 | tf_op jit(solution)/shard_map/dot_general | solution.py:104
  29.1 1.5 %slice-done.1 = s8[3145728]{0:T(1024)(128)(4,1)S(1)} async-done(((s8[7340032]{0:T(1024)(128)(4,1)}), s8[3145728]{0:T(1024)(128)(4,1)S(1)}, s32[]{:S(2)}) %slice-start.1) | async-done | bytes 3145752
  30.7 2.6 %fusion.2 = bf16[1,192,3584]{2,1,0:T(8,128)(2,1)S(1)} fusion(bf16[3584,1024]{1,0:T(8,128)(2,1)S(1)} %bitcast.23, bf16[192,2048]{1,0:T(8,128)(2,1)S(1)} %pad_maximum_fusion.2), kind=kOutput, calls=%fused_computation.8 | convolution fusion | flops 1409974272 | bytes 9109504 | tf_op jit(solution)/shard_map/dot_general | solution.py:14
  33.3 1.6 %fusion = bf16[1,192,3584]{2,1,0:T(8,128)(2,1)S(1)} fusion(bf16[1024,3584]{1,0:T(8,128)(2,1)S(1)} %bitcast.27, bf16[192,2048]{1,0:T(8,128)(2,1)S(1)} %pad_maximum_fusion.2), kind=kOutput, calls=%fused_computation.6 | convolution fusion | flops 1409974272 | bytes 9109504 | tf_op jit(solution)/shard_map/dot_general | solution.py:103
  34.9 0.7 pad_maximum_fusion
  35.6 0.3 fusion.15
  35.9 1.1 constant_dynamic-slice_fusion.5
  37.0 1.0 constant_dynamic-slice_fusion.2
  38.0 0.5 collective-permute-start.9
  38.5 1.4 %collective-permute-done.3 = bf16[3,96,1792]{2,1,0:T(8,128)(2,1)} collective-permute-done((bf16[3,96,1792]{2,1,0:T(8,128)(2,1)}, bf16[3,96,1792]{2,1,0:T(8,128)(2,1)}, u32[]{:S(2)}, u32[]{:S(2)}) %collective-permute-start.3) | collective-permute-done | bytes 1032224 | tf_op jit(solution)/shard_map/ppermute | solution.py:37
  40.0 1.8 %add_convert_fusion.1 = bf16[3,96,1792]{2,1,0:T(8,128)(2,1)S(1)} fusion(bf16[3,96,1792]{2,1,0:T(8,128)(2,1)} %collective-permute-done.3, bf16[3,192,1792]{2,1,0:T(8,128)(2,1)} %copy-done, s32[]{:T(128)S(6)} %select_n.130), kind=kLoop, calls=%fused_computation.17 | loop fusion | flops 2064384 | bytes 3096580 | tf_op jit(solution)/shard_map/convert_element_type | solution.py:40
  41.8 1.6 %collective-permute-start.4 = (bf16[3,48,1792]{2,1,0:T(8,128)(2,1)S(1)}, bf16[3,48,1792]{2,1,0:T(8,128)(2,1)S(1)}, u32[]{:S(2)}, u32[]{:S(2)}) collective-permute-start(bf16[3,48,1792]{2,1,0:T(8,128)(2,1)S(1)} %constant_dynamic-slice_fusion.4), channel_id=1, source_target_pairs={{0,8},{4,12},{8,0},{12,4},{16,24},{20,28},{24,16},{28,20},{1,9},{5... | collective-permute-start | bytes 1548296 | tf_op jit(solution)/shard_map/ppermute | solution.py:37
  43.4 1.5 %add_convert_fusion = bf16[3,96,1792]{2,1,0:T(8,128)(2,1)S(1)} fusion(bf16[3,96,1792]{2,1,0:T(8,128)(2,1)} %collective-permute-done.9, bf16[3,192,1792]{2,1,0:T(8,128)(2,1)S(1)} %get-tuple-element.23, s32[]{:T(128)S(6)} %select_n.130), kind=kLoop, calls=%fused_computation.16 | loop fusion | flops 2064384 | bytes 3096580 | tf_op jit(solution)/shard_map/convert_element_type | solution.py:40
  44.9 1.6 %collective-permute-start.10 = (bf16[3,48,1792]{2,1,0:T(8,128)(2,1)S(1)}, bf16[3,48,1792]{2,1,0:T(8,128)(2,1)S(1)}, u32[]{:S(2)}, u32[]{:S(2)}) collective-permute-start(bf16[3,48,1792]{2,1,0:T(8,128)(2,1)S(1)} %constant_dynamic-slice_fusion.1), channel_id=1, source_target_pairs={{0,16},{4,20},{8,24},{12,28},{16,0},{20,4},{24,8},{28,12},{1,17},{... | collective-permute-start | bytes 1548296 | tf_op jit(solution)/shard_map/ppermute | solution.py:37
  46.5 9.2 %collective-permute-done.4 = bf16[3,48,1792]{2,1,0:T(8,128)(2,1)S(1)} collective-permute-done((bf16[3,48,1792]{2,1,0:T(8,128)(2,1)S(1)}, bf16[3,48,1792]{2,1,0:T(8,128)(2,1)S(1)}, u32[]{:S(2)}, u32[]{:S(2)}) %collective-permute-start.4) | collective-permute-done | bytes 516128 | tf_op jit(solution)/shard_map/ppermute | solution.py:37
  55.6 0.1 add_convert_fusion.3
  55.8 1.6 %collective-permute-start.5 = (bf16[3,24,1792]{2,1,0:T(8,128)(2,1)S(1)}, bf16[3,24,1792]{2,1,0:T(8,128)(2,1)S(1)}, u32[]{:S(2)}, u32[]{:S(2)}) collective-permute-start(bf16[3,24,1792]{2,1,0:T(8,128)(2,1)S(1)} %constant_dynamic-slice_fusion.3), channel_id=1, source_target_pairs={{0,16},{4,20},{8,24},{12,28},{16,0},{20,4},{24,8},{28,12},{1,17},{... | collective-permute-start | bytes 774152 | tf_op jit(solution)/shard_map/ppermute | solution.py:37
  57.4 1.7 %collective-permute-done.10 = bf16[3,48,1792]{2,1,0:T(8,128)(2,1)S(1)} collective-permute-done((bf16[3,48,1792]{2,1,0:T(8,128)(2,1)S(1)}, bf16[3,48,1792]{2,1,0:T(8,128)(2,1)S(1)}, u32[]{:S(2)}, u32[]{:S(2)}) %collective-permute-start.10) | collective-permute-done | bytes 516128 | tf_op jit(solution)/shard_map/ppermute | solution.py:37
  59.1 0.1 add_convert_fusion.2
  59.3 0.1 collective-permute-start.11
  59.4 4.6 %collective-permute-done.5 = bf16[3,24,1792]{2,1,0:T(8,128)(2,1)S(1)} collective-permute-done((bf16[3,24,1792]{2,1,0:T(8,128)(2,1)S(1)}, bf16[3,24,1792]{2,1,0:T(8,128)(2,1)S(1)}, u32[]{:S(2)}, u32[]{:S(2)}) %collective-permute-start.5) | collective-permute-done | bytes 258080 | tf_op jit(solution)/shard_map/ppermute | solution.py:37
  64.0 0.1 convert_add_fusion.1
  64.0 0.1 multiply_convert_fusion.5
  64.2 1.6 %collective-permute-start.6 = (bf16[3,24,1792]{2,1,0:T(8,128)(2,1)S(1)}, bf16[3,24,1792]{2,1,0:T(8,128)(2,1)S(1)}, u32[]{:S(2)}, u32[]{:S(2)}) collective-permute-start(bf16[3,24,1792]{2,1,0:T(8,128)(2,1)S(1)} %pad_maximum_fusion.3), channel_id=1, source_target_pairs={{0,16},{4,20},{8,24},{12,28},{16,0},{20,4},{24,8},{28,12},{1,17},{... | collective-permute-start | bytes 774152 | tf_op jit(solution)/shard_map/ppermute | solution.py:49
  65.8 0.0 collective-permute-done.11
  65.8 0.1 convert_add_fusion
  65.9 0.1 multiply_convert_fusion.2
  66.0 0.8 collective-permute-start.12
  66.8 4.6 %collective-permute-done.6 = bf16[3,24,1792]{2,1,0:T(8,128)(2,1)S(1)} collective-permute-done((bf16[3,24,1792]{2,1,0:T(8,128)(2,1)S(1)}, bf16[3,24,1792]{2,1,0:T(8,128)(2,1)S(1)}, u32[]{:S(2)}, u32[]{:S(2)}) %collective-permute-start.6) | collective-permute-done | bytes 258080 | tf_op jit(solution)/shard_map/ppermute | solution.py:49
  71.5 0.1 maximum_select_fusion.4
  71.6 0.2 collective-permute-start.7
  71.8 1.7 %collective-permute-done.12 = bf16[3,24,1792]{2,1,0:T(8,128)(2,1)S(1)} collective-permute-done((bf16[3,24,1792]{2,1,0:T(8,128)(2,1)S(1)}, bf16[3,24,1792]{2,1,0:T(8,128)(2,1)S(1)}, u32[]{:S(2)}, u32[]{:S(2)}) %collective-permute-start.12) | collective-permute-done | bytes 258080 | tf_op jit(solution)/shard_map/ppermute | solution.py:49
  73.5 0.1 maximum_select_fusion.5
  73.6 0.5 collective-permute-start.13
  74.1 10.0 %collective-permute-done.7 = bf16[3,48,1792]{2,1,0:T(8,128)(2,1)S(1)} collective-permute-done((bf16[3,48,1792]{2,1,0:T(8,128)(2,1)S(1)}, bf16[3,48,1792]{2,1,0:T(8,128)(2,1)S(1)}, u32[]{:S(2)}, u32[]{:S(2)}) %collective-permute-start.7) | collective-permute-done | bytes 516128 | tf_op jit(solution)/shard_map/ppermute | solution.py:49
  84.1 0.3 maximum_select_fusion.2
  84.3 0.1 collective-permute-start.8
  84.4 0.4 collective-permute-done.13
  84.8 0.3 maximum_select_fusion.3
  85.0 0.2 collective-permute-start.14
  85.2 1.9 %collective-permute-done.8 = bf16[3,96,1792]{2,1,0:T(8,128)(2,1)} collective-permute-done((bf16[3,96,1792]{2,1,0:T(8,128)(2,1)S(1)}, bf16[3,96,1792]{2,1,0:T(8,128)(2,1)}, u32[]{:S(2)}, u32[]{:S(2)}) %collective-permute-start.8) | collective-permute-done | bytes 1032224 | tf_op jit(solution)/shard_map/ppermute | solution.py:49
  87.2 2.2 %maximum_select_fusion = bf16[3,192,1792]{2,1,0:T(8,128)(2,1)S(1)} fusion(bf16[3,96,1792]{2,1,0:T(8,128)(2,1)S(1)} %maximum_select_fusion.2, bf16[3,96,1792]{2,1,0:T(8,128)(2,1)} %collective-permute-done.8, pred[]{:T(512)S(6)} %eq.25), kind=kLoop, calls=%fused_computation.14 | loop fusion | flops 9289728 | bytes 4128769 | tf_op jit(solution)/shard_map/jit(_where)/select_n | solution.py:50
  89.3 2.1 %maximum_select_fusion.1 = bf16[3,192,1792]{2,1,0:T(8,128)(2,1)S(1)} fusion(bf16[3,96,1792]{2,1,0:T(8,128)(2,1)S(1)} %maximum_select_fusion.3, bf16[3,96,1792]{2,1,0:T(8,128)(2,1)} %collective-permute-done.14, pred[]{:T(512)S(6)} %eq.25), kind=kLoop, calls=%fused_computation.15 | loop fusion | flops 9289728 | bytes 4128769 | tf_op jit(solution)/shard_map/jit(_where)/select_n | solution.py:50
  91.4 0.0 slice-start.3
  91.4 0.4 fusion.7
  91.8 1.5 %slice-done.3 = s8[3145728]{0:T(1024)(128)(4,1)S(1)} async-done(((s8[7340032]{0:T(1024)(128)(4,1)}), s8[3145728]{0:T(1024)(128)(4,1)S(1)}, s32[]{:S(2)}) %slice-start.3) | async-done | bytes 3145752
  93.3 2.5 %fusion.17 = f32[192,1024]{1,0:T(8,128)S(1)} fusion(bf16[192,3584]{1,0:T(8,128)(2,1)S(1)} %get-tuple-element.18, bf16[1024,3584]{1,0:T(8,128)(2,1)S(1)} %bitcast.25), kind=kOutput, calls=%fused_computation.62 | convolution fusion | flops 1409286144 | bytes 9502720 | tf_op jit(solution)/shard_map/dot_general | solution.py:14
  95.8 2.5 %fusion.8 = bf16[192,1024]{1,0:T(8,128)(2,1)S(1)} fusion(f32[192,1024]{1,0:T(8,128)S(1)} %fusion.17, bf16[192,3584]{1,0:T(8,128)(2,1)S(1)} %get-tuple-element.13, bf16[1024,3584]{1,0:T(8,128)(2,1)S(1)} %bitcast.29), kind=kOutput, calls=%fused_computation.25 | convolution fusion | flops 1409679360 | bytes 9895936 | tf_op jit(solution)/shard_map/dot_general | solution.py:14
  98.4 5.2 %convolution_convert_fusion.2 = bf16[1024,3584]{1,0:T(8,128)(2,1)} fusion(bf16[192,3584]{1,0:T(8,128)(2,1)S(1)} %get-tuple-element.13, bf16[192,2048]{1,0:T(8,128)(2,1)S(1)} %pad_maximum_fusion.2), kind=kOutput, calls=%fused_computation.2 | convolution fusion | flops 1412956160 | bytes 9109504 | tf_op jit(solution)/shard_map/dot_general | solution.py:114
  103.6 0.4 collective-permute-start.15
  103.9 1.7 %collective-permute-start.17 = (bf16[48,1024]{1,0:T(8,128)(2,1)S(1)}, bf16[48,1024]{1,0:T(8,128)(2,1)S(1)}, u32[]{:S(2)}, u32[]{:S(2)}) collective-permute-start(bf16[48,1024]{1,0:T(8,128)(2,1)S(1)} %get-tuple-element.32), channel_id=1, source_target_pairs={{0,1},{1,2},{2,3},{3,0},{4,5},{5,6},{6,7},{7,4},{8,9},{9,10},{10,1... | collective-permute-start | bytes 294920 | tf_op jit(solution)/shard_map/ppermute | solution.py:88
  105.7 2.8 %collective-permute-start.16 = (bf16[48,1024]{1,0:T(8,128)(2,1)S(1)}, bf16[48,1024]{1,0:T(8,128)(2,1)S(1)}, u32[]{:S(2)}, u32[]{:S(2)}) collective-permute-start(bf16[48,1024]{1,0:T(8,128)(2,1)S(1)} %get-tuple-element.33), channel_id=1, source_target_pairs={{0,2},{1,3},{2,0},{3,1},{4,6},{5,7},{6,4},{7,5},{8,10},{9,11},{10,... | collective-permute-start | bytes 294920 | tf_op jit(solution)/shard_map/ppermute | solution.py:88
  108.5 5.2 %convolution_convert_fusion.1 = bf16[1024,3584]{1,0:T(8,128)(2,1)} fusion(bf16[192,3584]{1,0:T(8,128)(2,1)S(1)} %get-tuple-element.18, bf16[192,2048]{1,0:T(8,128)(2,1)S(1)} %pad_maximum_fusion.2), kind=kOutput, calls=%fused_computation.1 | convolution fusion | flops 1412956160 | bytes 9109504 | tf_op jit(solution)/shard_map/dot_general | solution.py:117
  113.6 5.2 %convolution_convert_fusion = bf16[3584,1024]{1,0:T(8,128)(2,1)} fusion(bf16[192,3584]{1,0:T(8,128)(2,1)S(1)} %get-tuple-element.19, bf16[192,2048]{1,0:T(8,128)(2,1)S(1)} %pad_maximum_fusion.2), kind=kOutput, calls=%fused_computation | convolution fusion | flops 1412956160 | bytes 9109504 | tf_op jit(solution)/shard_map/dot_general | solution.py:8
  118.8 0.7 add_convert_fusion.4
  (32 shorter events, 0.3 us)
Async XLA Ops:
  2.4 10.4 %collective-permute-start.2 = (bf16[48,2048]{1,0:T(8,128)(2,1)S(1)}, bf16[48,2048]{1,0:T(8,128)(2,1)S(1)}, u32[]{:S(2)}, u32[]{:S(2)}) collective-permute-start(bf16[48,2048]{1,0:T(8,128)(2,1)S(1)} %constant_dynamic-update-slice_fusion), channel_id=1, source_target_pairs={{0,3},{1,0},{2,1},{3,2},{4,7},{5,4},{6,5},{7,6},{8,11},{9,8},{10,9... | collective-permute-start | bytes 589832 | tf_op jit(solution)/shard_map/ppermute | solution.py:80
  7.5 16.7 %collective-permute-start.1 = (bf16[48,2048]{1,0:T(8,128)(2,1)S(1)}, bf16[48,2048]{1,0:T(8,128)(2,1)S(1)}, u32[]{:S(2)}, u32[]{:S(2)}) collective-permute-start(bf16[48,2048]{1,0:T(8,128)(2,1)S(1)} %constant_dynamic-update-slice_fusion), channel_id=1, source_target_pairs={{0,2},{1,3},{2,0},{3,1},{4,6},{5,7},{6,4},{7,5},{8,10},{9,11},{10,... | collective-permute-start | bytes 589832 | tf_op jit(solution)/shard_map/ppermute | solution.py:80
  7.5 16.7 %collective-permute-start = (bf16[48,2048]{1,0:T(8,128)(2,1)S(1)}, bf16[48,2048]{1,0:T(8,128)(2,1)S(1)}, u32[]{:S(2)}, u32[]{:S(2)}) collective-permute-start(bf16[48,2048]{1,0:T(8,128)(2,1)S(1)} %constant_dynamic-update-slice_fusion), channel_id=1, source_target_pairs={{0,1},{1,2},{2,3},{3,0},{4,5},{5,6},{6,7},{7,4},{8,9},{9,10},{10,1... | collective-permute-start | bytes 589832 | tf_op jit(solution)/shard_map/ppermute | solution.py:80
  24.2 4.9 %slice-start = ((s8[7340032]{0:T(1024)(128)(4,1)}), s8[4194304]{0:T(1024)(128)(4,1)S(1)}, s32[]{:S(2)}) async-start(s8[7340032]{0:T(1024)(128)(4,1)} %bitcast.22), calls=%async_computation | async-start | bytes 8388608
  24.2 9.0 %slice-start.4 = ((s8[7340032]{0:T(1024)(128)(4,1)}), s8[4194304]{0:T(1024)(128)(4,1)S(1)}, s32[]{:S(2)}) async-start(s8[7340032]{0:T(1024)(128)(4,1)} %bitcast.26), calls=%async_computation.4 | async-start | bytes 8388608
  24.3 6.4 %slice-start.1 = ((s8[7340032]{0:T(1024)(128)(4,1)}), s8[3145728]{0:T(1024)(128)(4,1)S(1)}, s32[]{:S(2)}) async-start(s8[7340032]{0:T(1024)(128)(4,1)} %bitcast.22), calls=%async_computation.1 | async-start | bytes 6291456
  24.3 9.0 %slice-start.5 = ((s8[7340032]{0:T(1024)(128)(4,1)}), s8[3145728]{0:T(1024)(128)(4,1)S(1)}, s32[]{:S(2)}) async-start(s8[7340032]{0:T(1024)(128)(4,1)} %bitcast.26), calls=%async_computation.5 | async-start | bytes 6291456
  35.8 2.2 %copy-start = (bf16[3,192,1792]{2,1,0:T(8,128)(2,1)}, bf16[3,192,1792]{2,1,0:T(8,128)(2,1)S(1)}, u32[]{:S(2)}) copy-start(bf16[3,192,1792]{2,1,0:T(8,128)(2,1)S(1)} %get-tuple-element.24) | copy-start | bytes 6193156
  37.0 3.0 %collective-permute-start.3 = (bf16[3,96,1792]{2,1,0:T(8,128)(2,1)}, bf16[3,96,1792]{2,1,0:T(8,128)(2,1)}, u32[]{:S(2)}, u32[]{:S(2)}) collective-permute-start(bf16[3,96,1792]{2,1,0:T(8,128)(2,1)} %constant_dynamic-slice_fusion.5), channel_id=1, source_target_pairs={{0,4},{4,0},{8,12},{12,8},{16,20},{20,16},{24,28},{28,24},{1,5},{5... | collective-permute-start | bytes 3096584 | tf_op jit(solution)/shard_map/ppermute | solution.py:37
  38.0 5.3 %collective-permute-start.9 = (bf16[3,96,1792]{2,1,0:T(8,128)(2,1)}, bf16[3,96,1792]{2,1,0:T(8,128)(2,1)}, u32[]{:S(2)}, u32[]{:S(2)}) collective-permute-start(bf16[3,96,1792]{2,1,0:T(8,128)(2,1)} %constant_dynamic-slice_fusion.2), channel_id=1, source_target_pairs={{0,4},{4,0},{8,12},{12,8},{16,20},{20,16},{24,28},{28,24},{1,5},{5... | collective-permute-start | bytes 3096584 | tf_op jit(solution)/shard_map/ppermute | solution.py:37
  41.8 13.9 %collective-permute-start.4 = (bf16[3,48,1792]{2,1,0:T(8,128)(2,1)S(1)}, bf16[3,48,1792]{2,1,0:T(8,128)(2,1)S(1)}, u32[]{:S(2)}, u32[]{:S(2)}) collective-permute-start(bf16[3,48,1792]{2,1,0:T(8,128)(2,1)S(1)} %constant_dynamic-slice_fusion.4), channel_id=1, source_target_pairs={{0,8},{4,12},{8,0},{12,4},{16,24},{20,28},{24,16},{28,20},{1,9},{5... | collective-permute-start | bytes 1548296 | tf_op jit(solution)/shard_map/ppermute | solution.py:37
  44.9 14.3 %collective-permute-start.10 = (bf16[3,48,1792]{2,1,0:T(8,128)(2,1)S(1)}, bf16[3,48,1792]{2,1,0:T(8,128)(2,1)S(1)}, u32[]{:S(2)}, u32[]{:S(2)}) collective-permute-start(bf16[3,48,1792]{2,1,0:T(8,128)(2,1)S(1)} %constant_dynamic-slice_fusion.1), channel_id=1, source_target_pairs={{0,16},{4,20},{8,24},{12,28},{16,0},{20,4},{24,8},{28,12},{1,17},{... | collective-permute-start | bytes 1548296 | tf_op jit(solution)/shard_map/ppermute | solution.py:37
  55.8 8.2 %collective-permute-start.5 = (bf16[3,24,1792]{2,1,0:T(8,128)(2,1)S(1)}, bf16[3,24,1792]{2,1,0:T(8,128)(2,1)S(1)}, u32[]{:S(2)}, u32[]{:S(2)}) collective-permute-start(bf16[3,24,1792]{2,1,0:T(8,128)(2,1)S(1)} %constant_dynamic-slice_fusion.3), channel_id=1, source_target_pairs={{0,16},{4,20},{8,24},{12,28},{16,0},{20,4},{24,8},{28,12},{1,17},{... | collective-permute-start | bytes 774152 | tf_op jit(solution)/shard_map/ppermute | solution.py:37
  59.3 6.5 %collective-permute-start.11 = (bf16[3,24,1792]{2,1,0:T(8,128)(2,1)S(1)}, bf16[3,24,1792]{2,1,0:T(8,128)(2,1)S(1)}, u32[]{:S(2)}, u32[]{:S(2)}) collective-permute-start(bf16[3,24,1792]{2,1,0:T(8,128)(2,1)S(1)} %constant_dynamic-slice_fusion), channel_id=1, source_target_pairs={{0,8},{4,12},{8,0},{12,4},{16,24},{20,28},{24,16},{28,20},{1,9},{5... | collective-permute-start | bytes 774152 | tf_op jit(solution)/shard_map/ppermute | solution.py:37
  64.2 7.3 %collective-permute-start.6 = (bf16[3,24,1792]{2,1,0:T(8,128)(2,1)S(1)}, bf16[3,24,1792]{2,1,0:T(8,128)(2,1)S(1)}, u32[]{:S(2)}, u32[]{:S(2)}) collective-permute-start(bf16[3,24,1792]{2,1,0:T(8,128)(2,1)S(1)} %pad_maximum_fusion.3), channel_id=1, source_target_pairs={{0,16},{4,20},{8,24},{12,28},{16,0},{20,4},{24,8},{28,12},{1,17},{... | collective-permute-start | bytes 774152 | tf_op jit(solution)/shard_map/ppermute | solution.py:49
  66.0 7.5 %collective-permute-start.12 = (bf16[3,24,1792]{2,1,0:T(8,128)(2,1)S(1)}, bf16[3,24,1792]{2,1,0:T(8,128)(2,1)S(1)}, u32[]{:S(2)}, u32[]{:S(2)}) collective-permute-start(bf16[3,24,1792]{2,1,0:T(8,128)(2,1)S(1)} %pad_maximum_fusion.4), channel_id=1, source_target_pairs={{0,8},{4,12},{8,0},{12,4},{16,24},{20,28},{24,16},{28,20},{1,9},{5... | collective-permute-start | bytes 774152 | tf_op jit(solution)/shard_map/ppermute | solution.py:49
  71.6 12.5 %collective-permute-start.7 = (bf16[3,48,1792]{2,1,0:T(8,128)(2,1)S(1)}, bf16[3,48,1792]{2,1,0:T(8,128)(2,1)S(1)}, u32[]{:S(2)}, u32[]{:S(2)}) collective-permute-start(bf16[3,48,1792]{2,1,0:T(8,128)(2,1)S(1)} %maximum_select_fusion.4), channel_id=1, source_target_pairs={{0,8},{4,12},{8,0},{12,4},{16,24},{20,28},{24,16},{28,20},{1,9},{5... | collective-permute-start | bytes 1548296 | tf_op jit(solution)/shard_map/ppermute | solution.py:49
  73.6 11.2 %collective-permute-start.13 = (bf16[3,48,1792]{2,1,0:T(8,128)(2,1)S(1)}, bf16[3,48,1792]{2,1,0:T(8,128)(2,1)S(1)}, u32[]{:S(2)}, u32[]{:S(2)}) collective-permute-start(bf16[3,48,1792]{2,1,0:T(8,128)(2,1)S(1)} %maximum_select_fusion.5), channel_id=1, source_target_pairs={{0,16},{4,20},{8,24},{12,28},{16,0},{20,4},{24,8},{28,12},{1,17},{... | collective-permute-start | bytes 1548296 | tf_op jit(solution)/shard_map/ppermute | solution.py:49
  84.3 2.8 %collective-permute-start.8 = (bf16[3,96,1792]{2,1,0:T(8,128)(2,1)S(1)}, bf16[3,96,1792]{2,1,0:T(8,128)(2,1)}, u32[]{:S(2)}, u32[]{:S(2)}) collective-permute-start(bf16[3,96,1792]{2,1,0:T(8,128)(2,1)S(1)} %maximum_select_fusion.2), channel_id=1, source_target_pairs={{0,4},{4,0},{8,12},{12,8},{16,20},{20,16},{24,28},{28,24},{1,5},{5... | collective-permute-start | bytes 3096584 | tf_op jit(solution)/shard_map/ppermute | solution.py:49
  85.0 4.3 %collective-permute-start.14 = (bf16[3,96,1792]{2,1,0:T(8,128)(2,1)S(1)}, bf16[3,96,1792]{2,1,0:T(8,128)(2,1)}, u32[]{:S(2)}, u32[]{:S(2)}) collective-permute-start(bf16[3,96,1792]{2,1,0:T(8,128)(2,1)S(1)} %maximum_select_fusion.3), channel_id=1, source_target_pairs={{0,4},{4,0},{8,12},{12,8},{16,20},{20,16},{24,28},{28,24},{1,5},{5... | collective-permute-start | bytes 3096584 | tf_op jit(solution)/shard_map/ppermute | solution.py:49
  87.2 4.7 %slice-start.2 = ((s8[7340032]{0:T(1024)(128)(4,1)}), s8[4194304]{0:T(1024)(128)(4,1)S(1)}, s32[]{:S(2)}) async-start(s8[7340032]{0:T(1024)(128)(4,1)} %bitcast.24), calls=%async_computation.2 | async-start | bytes 8388608
  91.4 1.9 %slice-start.3 = ((s8[7340032]{0:T(1024)(128)(4,1)}), s8[3145728]{0:T(1024)(128)(4,1)S(1)}, s32[]{:S(2)}) async-start(s8[7340032]{0:T(1024)(128)(4,1)} %bitcast.24), calls=%async_computation.3 | async-start | bytes 6291456
  91.4 4.4 %slice-start.6 = ((s8[7340032]{0:T(1024)(128)(4,1)}), s8[4194304]{0:T(1024)(128)(4,1)S(1)}, s32[]{:S(2)}) async-start(s8[7340032]{0:T(1024)(128)(4,1)} %bitcast.28), calls=%async_computation.6 | async-start | bytes 8388608
  93.3 2.5 %slice-start.7 = ((s8[7340032]{0:T(1024)(128)(4,1)}), s8[3145728]{0:T(1024)(128)(4,1)S(1)}, s32[]{:S(2)}) async-start(s8[7340032]{0:T(1024)(128)(4,1)} %bitcast.28), calls=%async_computation.7 | async-start | bytes 6291456
  103.6 15.3 %collective-permute-start.15 = (bf16[48,1024]{1,0:T(8,128)(2,1)S(1)}, bf16[48,1024]{1,0:T(8,128)(2,1)S(1)}, u32[]{:S(2)}, u32[]{:S(2)}) collective-permute-start(bf16[48,1024]{1,0:T(8,128)(2,1)S(1)} %get-tuple-element.31), channel_id=1, source_target_pairs={{0,3},{1,0},{2,1},{3,2},{4,7},{5,4},{6,5},{7,6},{8,11},{9,8},{10,9... | collective-permute-start | bytes 294920 | tf_op jit(solution)/shard_map/ppermute | solution.py:88
  103.9 14.9 %collective-permute-start.17 = (bf16[48,1024]{1,0:T(8,128)(2,1)S(1)}, bf16[48,1024]{1,0:T(8,128)(2,1)S(1)}, u32[]{:S(2)}, u32[]{:S(2)}) collective-permute-start(bf16[48,1024]{1,0:T(8,128)(2,1)S(1)} %get-tuple-element.32), channel_id=1, source_target_pairs={{0,1},{1,2},{2,3},{3,0},{4,5},{5,6},{6,7},{7,4},{8,9},{9,10},{10,1... | collective-permute-start | bytes 294920 | tf_op jit(solution)/shard_map/ppermute | solution.py:88
  105.7 13.2 %collective-permute-start.16 = (bf16[48,1024]{1,0:T(8,128)(2,1)S(1)}, bf16[48,1024]{1,0:T(8,128)(2,1)S(1)}, u32[]{:S(2)}, u32[]{:S(2)}) collective-permute-start(bf16[48,1024]{1,0:T(8,128)(2,1)S(1)} %get-tuple-element.33), channel_id=1, source_target_pairs={{0,2},{1,3},{2,0},{3,1},{4,6},{5,7},{6,4},{7,5},{8,10},{9,11},{10,... | collective-permute-start | bytes 294920 | tf_op jit(solution)/shard_map/ppermute | solution.py:88

commit v8 on v7

--- a/solution.py
+++ b/solution.py
@@ -61,15 +61,22 @@
     return bits
 
 
-def row_gated(stacked, n_dev):
+def row_reduce(stacked, n_dev):
     _, tokens, units = stacked.shape
     bits = row_bits(n_dev, tokens, units)
     if bits is None:
-        sums = lax.psum(stacked, "row").astype(jnp.float32)
-        return jnp.stack(gated_grads(sums[0], sums[1], sums[2]))
+        return (lax.psum(stacked, "row").astype(jnp.float32),)
     orders = (bits, bits[:1] + bits[:0:-1])
     half = units // 2
-    reduced = [halving_reduce(stacked[:, :, h * half:(h + 1) * half], o, n_dev) for h, o in enumerate(orders)]
+    return tuple(halving_reduce(stacked[:, :, h * half:(h + 1) * half], o, n_dev) for h, o in enumerate(orders))
+
+
+def row_gather_gated(reduced, n_dev):
+    if len(reduced) == 1:
+        sums = reduced[0]
+        return jnp.stack(gated_grads(sums[0], sums[1], sums[2]))
+    bits = row_bits(n_dev, n_dev, 2)
+    orders = (bits, bits[:1] + bits[:0:-1])
     outs = [doubling_gather(jnp.stack(gated_grads(red[0], red[1], red[2])), o, n_dev) for red, o in zip(reduced, orders)]
     return jnp.concatenate(outs, axis=2)
 
@@ -90,22 +97,50 @@
     return total.astype(jnp.bfloat16)
 
 
+def col_gather_remote(x, n_col):
+    return [lax.ppermute(x, "col", [(j, (j + s) % n_col) for j in range(n_col)]) for s in range(1, n_col)]
+
+
 def body(tokens, grad_out, gate_weight, up_weight, down_weight):
     n_row = lax.psum(1, "row")
     n_col = lax.psum(1, "col")
     feat = tokens.shape[1]
-    both_all = col_gather(jnp.concatenate([tokens, grad_out], axis=1), n_col)
+    n_own = tokens.shape[0]
+    units = gate_weight.shape[1]
+    both = jnp.concatenate([tokens, grad_out], axis=1)
+    staged = (
+        n_col > 1
+        and row_bits(n_row, n_own, units) is not None
+        and (n_own * (n_col - 1)) % n_row == 0
+    )
+    if staged:
+        stages = [both, col_gather_remote(both, n_col)]
+    else:
+        stages = [col_gather(both, n_col)]
+    gated_parts = []
+    reduced = None
+    for i, st in enumerate(stages):
+        if i > 0:
+            st, reduced = lax.optimization_barrier((st, reduced))
+            st = jnp.concatenate(st, axis=0)
+            stages[i] = st
+            gated_parts.append(row_gather_gated(reduced, n_row))
+        tok_s = st[:, :feat]
+        grad_s = st[:, feat:]
+        stacked = jnp.stack(
+            [
+                jnp.dot(tok_s, gate_weight, preferred_element_type=jnp.float32).astype(jnp.bfloat16),
+                jnp.dot(tok_s, up_weight, preferred_element_type=jnp.float32).astype(jnp.bfloat16),
+                contract_last(grad_s, down_weight).astype(jnp.bfloat16),
+            ]
+        )
+        reduced = row_reduce(stacked, n_row)
+    gated_parts.append(row_gather_gated(reduced, n_row))
+    gated = jnp.concatenate(gated_parts, axis=1) if len(gated_parts) > 1 else gated_parts[0]
+    both_all = jnp.concatenate(stages, axis=0) if len(stages) > 1 else stages[0]
     tok_all = both_all[:, :feat]
     grad_all = both_all[:, feat:]
     tok_t = tok_all.T
-    stacked = jnp.stack(
-        [
-            jnp.dot(tok_all, gate_weight, preferred_element_type=jnp.float32).astype(jnp.bfloat16),
-            jnp.dot(tok_all, up_weight, preferred_element_type=jnp.float32).astype(jnp.bfloat16),
-            contract_last(grad_all, down_weight).astype(jnp.bfloat16),
-        ]
-    )
-    gated = row_gated(stacked, n_row)
     hidden, grad_gate, grad_up = gated[0], gated[1], gated[2]
     partial_grad = contract_last(grad_gate, gate_weight) + contract_last(grad_up, up_weight)
     partial_grad, grad_gate, grad_up, hidden = lax.optimization_barrier(

time: 120 us -> 130 us (1.083)
  waiting for transfers between devices: 51.3 us -> 39.4 us
  starting transfers between devices: 19.6 us -> 30.8 us
  matrix products: 29.6 us -> 37.2 us
  local copies, waits for them, and re-layouts: 7.46 us -> 9.48 us
  other arithmetic: 10.6 us -> 11.9 us
    ppermute x3, waiting for transfers between devices: 15.7 us -> 0.01 us  [col_gather_remote(): lax.ppermute(x, 'col', [(j, (j + s) % n_col) for j in range(n_col)])]
    ppermute x6 -> x12, starting transfers between devices: 3.35 us -> 9.41 us  [doubling_gather(): got = lax.ppermute(cur, 'row', [(j, j ^ bit) for j in range(n_dev)])]
    ppermute x6 -> x12, starting transfers between devices: 5.3 us -> 11.2 us  [halving_reduce(): got = lax.ppermute(send, 'row', [(j, j ^ bit) for j in range(n_dev)])]
    dot_general x2 -> x4, matrix products: 6.44 us -> 11.7 us  [the longest x2 9.13 us: body(): jnp.dot(tok_s, up_weight, preferred_element_type=jnp.float32)]
    ppermute x6 -> x12, waiting for transfers between devices: 17 us -> 22.1 us  [halving_reduce(): got = lax.ppermute(send, 'row', [(j, j ^ bit) for j in range(n_dev)])]
    concatenate x1 -> x2, other arithmetic: 0.05 us -> 4.23 us  [the longest x1 3.15 us: body(): jnp.concatenate(gated_parts, axis=1)]
    dot_general x3 -> x4, matrix products: 7.58 us -> 9.92 us  [contract_last(): lax.dot_general(left, right, (((1,), (1,)), ((), ())), preferred_element_...]
    select_n x6 -> x12, other arithmetic: 4.94 us -> 2.68 us  [doubling_gather(): jnp.where(hi == 1, jnp.concatenate([got, cur], axis=1), jnp.concatenate([...]
  transfers between devices with their start and end apart: 18 -> 30, of which waited for: 11 -> 15; matrix products, arithmetic and copies ran while one was open for 15% -> 17% of each run, Pallas kernels for 0% -> 0%
where the time goes in v8:
time: 130 us
  waiting for transfers between devices  39.4 us (30%)
  matrix products  37.2 us (29%)
  starting transfers between devices  30.8 us (24%)
  other arithmetic  11.9 us (9%)
  local copies, waits for them, and re-layouts  9.48 us (7%)
    ppermute x12, waiting for transfers between devices, halving_reduce(): got = lax.ppermute(send, 'row', [(j, j ^ bit) for j in range(n_dev)])  22.1 us
    ppermute x12, waiting for transfers between devices, doubling_gather(): got = lax.ppermute(cur, 'row', [(j, j ^ bit) for j in range(n_dev)])  17.3 us
    ppermute x12, starting transfers between devices, halving_reduce(): got = lax.ppermute(send, 'row', [(j, j ^ bit) for j in range(n_dev)])  11.2 us
    dot_general x4, matrix products, contract_last(): lax.dot_general(left, right, (((1,), (1,)), ((), ())), preferred_element_...  9.92 us
    ppermute x12, starting transfers between devices, doubling_gather(): got = lax.ppermute(cur, 'row', [(j, j ^ bit) for j in range(n_dev)])  9.41 us
    dot_general x2, matrix products, body(): jnp.dot(tok_s, up_weight, preferred_element_type=jnp.float32)  9.13 us
    ppermute x3, starting transfers between devices, col_gather_remote(): lax.ppermute(x, 'col', [(j, (j + s) % n_col) for j in range(n_col)])  5.6 us
    dot_general x1, matrix products, contract_first(): lax.dot_general(left, right, (((0,), (0,)), ((), ())), preferred_element_...  5.18 us
  transfers between devices with their start and end apart: 30, of which 15 were waited for; matrix products, arithmetic and copies ran while one was open for 17% of the time, Pallas kernels for 0%

profile of v8, /device:TPU:0, one launch (start us, length us, event | category | flops | bytes accessed | tf_op | source)
XLA Modules:
  0.0 129.9 jit_solution(4843223184563545070)
XLA Ops:
  0.7 4.6 %fusion.4 = bf16[1,48,3584]{2,1,0:T(8,128)(2,1)S(1)} fusion(bf16[48,1024]{1,0:T(8,128)(2,1)} %param.5, bf16[1024,3584]{1,0:T(8,128)(2,1)} %param.8), kind=kOutput, calls=%fused_computation.13 | convolution fusion | flops 352493568 | bytes 7782400 | tf_op jit(solution)/shard_map/dot_general | solution.py:133
  5.3 0.5 copy-done
  5.9 1.3 %fusion.3 = bf16[1,48,3584]{2,1,0:T(8,128)(2,1)S(1)} fusion(bf16[48,1024]{1,0:T(8,128)(2,1)S(1)} %copy-done.2, bf16[1024,3584]{1,0:T(8,128)(2,1)S(1)} %copy-done), kind=kOutput, calls=%fused_computation.12 | convolution fusion | flops 352493568 | bytes 7782400 | tf_op jit(solution)/shard_map/dot_general | solution.py:132
  7.2 1.0 slice-done.5
  8.2 2.3 %fusion.5 = bf16[1,48,3584]{2,1,0:T(8,128)(2,1)S(1)} fusion(bf16[48,1024]{1,0:T(8,128)(2,1)S(1)} %copy-done.3, bf16[3584,1024]{1,0:T(8,128)(2,1)S(1)} %bitcast.39), kind=kOutput, calls=%fused_computation.14 | convolution fusion | flops 352493568 | bytes 7782400 | tf_op jit(solution)/shard_map/dot_general | solution.py:14
  10.7 0.9 fusion.15
  11.5 0.8 constant_dynamic-slice_fusion.11
  12.3 0.5 collective-permute-start.3
  12.8 0.7 constant_dynamic-update-slice_fusion.1
  13.5 0.7 constant_dynamic-update-slice_fusion
  14.1 4.6 %collective-permute-start.2 = (bf16[48,2048]{1,0:T(8,128)(2,1)}, bf16[48,2048]{1,0:T(8,128)(2,1)S(1)}, u32[]{:S(2)}, u32[]{:S(2)}) collective-permute-start(bf16[48,2048]{1,0:T(8,128)(2,1)} %constant_dynamic-update-slice_fusion), channel_id=1, source_target_pairs={{0,3},{1,0},{2,1},{3,2},{4,7},{5,4},{6,5},{7,6},{8,11},{9,8},{10,9... | collective-permute-start | bytes 589832 | tf_op jit(solution)/shard_map/ppermute | solution.py:101
  18.7 1.0 collective-permute-start
  19.7 1.8 %constant_dynamic-slice_fusion.8 = bf16[3,24,1792]{2,1,0:T(8,128)(2,1)} fusion(bf16[3,48,1792]{2,1,0:T(8,128)(2,1)} %get-tuple-element.35, s32[]{:T(128)S(6)} %select_n.239), kind=kLoop, calls=%fused_computation.88 | loop fusion | bytes 516100 | tf_op jit(solution)/shard_map/dynamic_slice | solution.py:36
  21.6 1.1 add_convert_fusion.5
  22.8 1.6 %collective-permute-start.4 = (bf16[3,12,1792]{2,1,0:T(8,128)(2,1)S(1)}, bf16[3,12,1792]{2,1,0:T(8,128)(2,1)S(1)}, u32[]{:S(2)}, u32[]{:S(2)}) collective-permute-start(bf16[3,12,1792]{2,1,0:T(8,128)(2,1)S(1)} %constant_dynamic-slice_fusion.10), channel_id=1, source_target_pairs={{0,8},{4,12},{8,0},{12,4},{16,24},{20,28},{24,16},{28,20},{1,9},{5... | collective-permute-start | bytes 387080 | tf_op jit(solution)/shard_map/ppermute | solution.py:37
  24.3 1.1 add_convert_fusion.4
  25.5 1.6 %collective-permute-start.7 = (bf16[3,12,1792]{2,1,0:T(8,128)(2,1)S(1)}, bf16[3,12,1792]{2,1,0:T(8,128)(2,1)S(1)}, u32[]{:S(2)}, u32[]{:S(2)}) collective-permute-start(bf16[3,12,1792]{2,1,0:T(8,128)(2,1)S(1)} %constant_dynamic-slice_fusion.7), channel_id=1, source_target_pairs={{0,16},{4,20},{8,24},{12,28},{16,0},{20,4},{24,8},{28,12},{1,17},{... | collective-permute-start | bytes 387080 | tf_op jit(solution)/shard_map/ppermute | solution.py:37
  27.1 2.5 %collective-permute-done.4 = bf16[3,12,1792]{2,1,0:T(8,128)(2,1)S(1)} collective-permute-done((bf16[3,12,1792]{2,1,0:T(8,128)(2,1)S(1)}, bf16[3,12,1792]{2,1,0:T(8,128)(2,1)S(1)}, u32[]{:S(2)}, u32[]{:S(2)}) %collective-permute-start.4) | collective-permute-done | bytes 129056 | tf_op jit(solution)/shard_map/ppermute | solution.py:37
  29.7 1.6 %collective-permute-start.5 = (bf16[3,6,1792]{2,1,0:T(8,128)(2,1)S(1)}, bf16[3,6,1792]{2,1,0:T(8,128)(2,1)S(1)}, u32[]{:S(2)}, u32[]{:S(2)}) collective-permute-start(bf16[3,6,1792]{2,1,0:T(8,128)(2,1)S(1)} %constant_dynamic-slice_fusion.9), channel_id=1, source_target_pairs={{0,16},{4,20},{8,24},{12,28},{16,0},{20,4},{24,8},{28,12},{1,17},{... | collective-permute-start | bytes 193544 | tf_op jit(solution)/shard_map/ppermute | solution.py:37
  31.3 0.8 collective-permute-done.7
  32.3 0.7 collective-permute-start.8
  33.0 1.3 collective-permute-done.5
  34.3 2.5 %collective-permute-done.8 = bf16[3,6,1792]{2,1,0:T(8,128)(2,1)S(1)} collective-permute-done((bf16[3,6,1792]{2,1,0:T(8,128)(2,1)S(1)}, bf16[3,6,1792]{2,1,0:T(8,128)(2,1)S(1)}, u32[]{:S(2)}, u32[]{:S(2)}) %collective-permute-start.8) | collective-permute-done | bytes 64544 | tf_op jit(solution)/shard_map/ppermute | solution.py:37
  36.9 0.9 constant_dynamic-update-slice_fusion.4
  37.9 4.5 %fusion.1 = bf16[1,144,3584]{2,1,0:T(8,128)(2,1)S(1)} fusion(bf16[1024,3584]{1,0:T(8,128)(2,1)} %param.8, bf16[144,2048]{1,0:T(8,128)(2,1)S(1)} %constant_dynamic-update-slice_fusion.2), kind=kOutput, calls=%fused_computation.7 | convolution fusion | flops 1057480704 | bytes 8667136 | tf_op jit(solution)/shard_map/dot_general | solution.py:133
  42.4 1.0 slice-done.7
  43.4 2.6 %fusion.2 = bf16[1,144,3584]{2,1,0:T(8,128)(2,1)S(1)} fusion(bf16[3584,1024]{1,0:T(8,128)(2,1)S(1)} %bitcast.41, bf16[144,2048]{1,0:T(8,128)(2,1)S(1)} %constant_dynamic-update-slice_fusion.2), kind=kOutput, calls=%fused_computation.8 | convolution fusion | flops 1057480704 | bytes 8667136 | tf_op jit(solution)/shard_map/dot_general | solution.py:14
  46.0 1.3 fusion
  47.4 1.6 %collective-permute-start.9 = (bf16[3,6,1792]{2,1,0:T(8,128)(2,1)S(1)}, bf16[3,6,1792]{2,1,0:T(8,128)(2,1)S(1)}, u32[]{:S(2)}, u32[]{:S(2)}) collective-permute-start(bf16[3,6,1792]{2,1,0:T(8,128)(2,1)S(1)} %pad_maximum_fusion.5), channel_id=1, source_target_pairs={{0,16},{4,20},{8,24},{12,28},{16,0},{20,4},{24,8},{28,12},{1,17},{... | collective-permute-start | bytes 193544 | tf_op jit(solution)/shard_map/ppermute | solution.py:49
  49.0 1.0 collective-permute-start.12
  50.0 0.3 pad_maximum_fusion
  50.7 0.5 collective-permute-start.15
  51.3 0.7 collective-permute-done.9
  52.1 1.0 collective-permute-start.10
  53.0 0.5 collective-permute-done.12
  53.7 1.0 collective-permute-start.13
  54.7 3.0 %collective-permute-done.10 = bf16[3,12,1792]{2,1,0:T(8,128)(2,1)S(1)} collective-permute-done((bf16[3,12,1792]{2,1,0:T(8,128)(2,1)S(1)}, bf16[3,12,1792]{2,1,0:T(8,128)(2,1)S(1)}, u32[]{:S(2)}, u32[]{:S(2)}) %collective-permute-start.10) | collective-permute-done | bytes 129056 | tf_op jit(solution)/shard_map/ppermute | solution.py:49
  58.3 1.4 %collective-permute-start.22 = (bf16[3,36,1792]{2,1,0:T(8,128)(2,1)S(1)}, bf16[3,36,1792]{2,1,0:T(8,128)(2,1)S(1)}, u32[]{:S(2)}, u32[]{:S(2)}) collective-permute-start(bf16[3,36,1792]{2,1,0:T(8,128)(2,1)S(1)} %constant_dynamic-slice_fusion.1), channel_id=1, source_target_pairs={{0,16},{4,20},{8,24},{12,28},{16,0},{20,4},{24,8},{28,12},{1,17},{... | collective-permute-start | bytes 1161224 | tf_op jit(solution)/shard_map/ppermute | solution.py:37
  60.0 1.0 collective-permute-start.16
  61.0 9.7 %collective-permute-done.22 = bf16[3,36,1792]{2,1,0:T(8,128)(2,1)S(1)} collective-permute-done((bf16[3,36,1792]{2,1,0:T(8,128)(2,1)S(1)}, bf16[3,36,1792]{2,1,0:T(8,128)(2,1)S(1)}, u32[]{:S(2)}, u32[]{:S(2)}) %collective-permute-start.22) | collective-permute-done | bytes 387104 | tf_op jit(solution)/shard_map/ppermute | solution.py:37
  70.9 1.2 collective-permute-start.23
  72.4 1.1 collective-permute-start.17
  73.5 5.2 %collective-permute-done.23 = bf16[3,18,1792]{2,1,0:T(8,128)(2,1)S(1)} collective-permute-done((bf16[3,18,1792]{2,1,0:T(8,128)(2,1)S(1)}, bf16[3,18,1792]{2,1,0:T(8,128)(2,1)S(1)}, u32[]{:S(2)}, u32[]{:S(2)}) %collective-permute-start.23) | collective-permute-done | bytes 193568 | tf_op jit(solution)/shard_map/ppermute | solution.py:37
  79.0 1.2 collective-permute-start.24
  80.5 1.1 collective-permute-start.18
  81.6 4.4 %collective-permute-done.24 = bf16[3,18,1792]{2,1,0:T(8,128)(2,1)S(1)} collective-permute-done((bf16[3,18,1792]{2,1,0:T(8,128)(2,1)S(1)}, bf16[3,18,1792]{2,1,0:T(8,128)(2,1)S(1)}, u32[]{:S(2)}, u32[]{:S(2)}) %collective-permute-start.24) | collective-permute-done | bytes 193568 | tf_op jit(solution)/shard_map/ppermute | solution.py:49
  86.2 1.4 %collective-permute-start.25 = (bf16[3,36,1792]{2,1,0:T(8,128)(2,1)S(1)}, bf16[3,36,1792]{2,1,0:T(8,128)(2,1)S(1)}, u32[]{:S(2)}, u32[]{:S(2)}) collective-permute-start(bf16[3,36,1792]{2,1,0:T(8,128)(2,1)S(1)} %maximum_select_fusion.7), channel_id=1, source_target_pairs={{0,16},{4,20},{8,24},{12,28},{16,0},{20,4},{24,8},{28,12},{1,17},{... | collective-permute-start | bytes 1161224 | tf_op jit(solution)/shard_map/ppermute | solution.py:49
  87.8 0.9 collective-permute-start.19
  88.9 7.5 %collective-permute-done.25 = bf16[3,36,1792]{2,1,0:T(8,128)(2,1)S(1)} collective-permute-done((bf16[3,36,1792]{2,1,0:T(8,128)(2,1)S(1)}, bf16[3,36,1792]{2,1,0:T(8,128)(2,1)S(1)}, u32[]{:S(2)}, u32[]{:S(2)}) %collective-permute-start.25) | collective-permute-done | bytes 387104 | tf_op jit(solution)/shard_map/ppermute | solution.py:49
  96.4 0.3 maximum_select_fusion.3
  96.7 0.5 collective-permute-done.19
  97.6 1.1 pad_maximum_fusion.2
  99.0 0.5 maximum_select_fusion.1
  99.5 0.6 collective-permute-done.20
  100.1 0.5 maximum_select_fusion
  100.7 3.2 %maximum_maximum_fusion = bf16[3,192,3584]{2,1,0:T(8,128)(2,1)S(1)} fusion(bf16[3,144,1792]{2,1,0:T(8,128)(2,1)S(1)} %maximum_select_fusion.1, bf16[3,144,1792]{2,1,0:T(8,128)(2,1)S(1)} %maximum_select_fusion, bf16[3,48,1792]{2,1,0:T(8,128)(2,1)S(1)} %maximum_select_fusion.5, bf16[3,48,1792]{2,1,0:T(8,128)(2,1)S(1)} %maximum_select_fusion.4), kind=kLoop, calls=%fused_computation.15 | loop fusion | flops 16515072 | bytes 8257536 | tf_op jit(solution)/shard_map/concatenate | solution.py:139
  103.8 2.5 %fusion.13 = f32[192,1024]{1,0:T(8,128)S(1)} fusion(bf16[1024,3584]{1,0:T(8,128)(2,1)S(1)} %bitcast.35, bf16[3,192,3584]{2,1,0:T(8,128)(2,1)S(1)} %maximum_maximum_fusion), kind=kOutput, calls=%fused_computation.92 | convolution fusion | flops 1409286144 | bytes 9502720 | tf_op jit(solution)/shard_map/dot_general | solution.py:14
  106.6 2.5 %fusion.6 = bf16[192,1024]{1,0:T(8,128)(2,1)S(1)} fusion(f32[192,1024]{1,0:T(8,128)S(1)} %fusion.13, bf16[1024,3584]{1,0:T(8,128)(2,1)S(1)} %bitcast.37, bf16[3,192,3584]{2,1,0:T(8,128)(2,1)S(1)} %maximum_maximum_fusion), kind=kOutput, calls=%fused_computation.25 | convolution fusion | flops 1409679360 | bytes 9895936 | tf_op jit(solution)/shard_map/dot_general | solution.py:14
  109.2 5.2 %convolution_convert_fusion.2 = bf16[1024,3584]{1,0:T(8,128)(2,1)} fusion(bf16[192,3584]{1,0:T(8,128)(2,1)S(1)} %get-tuple-element.23, bf16[192,2048]{1,0:T(8,128)(2,1)S(1)} %pad_maximum_fusion.2), kind=kOutput, calls=%fused_computation.2 | convolution fusion | flops 1412956160 | bytes 9109504 | tf_op jit(solution)/shard_map/dot_general | solution.py:149
  114.3 2.8 %collective-permute-start.27 = (bf16[48,1024]{1,0:T(8,128)(2,1)S(1)}, bf16[48,1024]{1,0:T(8,128)(2,1)S(1)}, u32[]{:S(2)}, u32[]{:S(2)}) collective-permute-start(bf16[48,1024]{1,0:T(8,128)(2,1)S(1)} %get-tuple-element.43), channel_id=1, source_target_pairs={{0,3},{1,0},{2,1},{3,2},{4,7},{5,4},{6,5},{7,6},{8,11},{9,8},{10,9... | collective-permute-start | bytes 294920 | tf_op jit(solution)/shard_map/ppermute | solution.py:95
  117.2 1.7 %collective-permute-start.28 = (bf16[48,1024]{1,0:T(8,128)(2,1)S(1)}, bf16[48,1024]{1,0:T(8,128)(2,1)S(1)}, u32[]{:S(2)}, u32[]{:S(2)}) collective-permute-start(bf16[48,1024]{1,0:T(8,128)(2,1)S(1)} %get-tuple-element.45), channel_id=1, source_target_pairs={{0,2},{1,3},{2,0},{3,1},{4,6},{5,7},{6,4},{7,5},{8,10},{9,11},{10,... | collective-permute-start | bytes 294920 | tf_op jit(solution)/shard_map/ppermute | solution.py:95
  118.9 5.2 %convolution_convert_fusion.1 = bf16[1024,3584]{1,0:T(8,128)(2,1)} fusion(bf16[192,3584]{1,0:T(8,128)(2,1)S(1)} %get-tuple-element.28, bf16[192,2048]{1,0:T(8,128)(2,1)S(1)} %pad_maximum_fusion.2), kind=kOutput, calls=%fused_computation.1 | convolution fusion | flops 1412956160 | bytes 9109504 | tf_op jit(solution)/shard_map/dot_general | solution.py:152
  124.1 5.2 %convolution_convert_fusion = bf16[3584,1024]{1,0:T(8,128)(2,1)} fusion(bf16[192,3584]{1,0:T(8,128)(2,1)S(1)} %get-tuple-element.29, bf16[192,2048]{1,0:T(8,128)(2,1)S(1)} %pad_maximum_fusion.2), kind=kOutput, calls=%fused_computation | convolution fusion | flops 1412956160 | bytes 9109504 | tf_op jit(solution)/shard_map/dot_general | solution.py:8
  129.2 0.7 add_convert_fusion.8
  (92 shorter events, 4.9 us)
Async XLA Ops:
  0.6 5.2 %copy-start = (bf16[1024,3584]{1,0:T(8,128)(2,1)S(1)}, bf16[1024,3584]{1,0:T(8,128)(2,1)}, u32[]{:S(2)}) copy-start(bf16[1024,3584]{1,0:T(8,128)(2,1)} %param.7) | copy-start | bytes 22020100
  0.7 5.2 %copy-start.2 = (bf16[48,1024]{1,0:T(8,128)(2,1)S(1)}, bf16[48,1024]{1,0:T(8,128)(2,1)}, u32[]{:S(2)}) copy-start(bf16[48,1024]{1,0:T(8,128)(2,1)} %param.5) | copy-start | bytes 294916
  0.7 6.6 %slice-start.4 = ((s8[7340032]{0:T(1024)(128)(4,1)}), s8[4194304]{0:T(1024)(128)(4,1)S(1)}, s32[]{:S(2)}) async-start(s8[7340032]{0:T(1024)(128)(4,1)} %bitcast.38), calls=%async_computation.4 | async-start | bytes 8388608
  5.9 2.4 %slice-start.5 = ((s8[7340032]{0:T(1024)(128)(4,1)}), s8[3145728]{0:T(1024)(128)(4,1)S(1)}, s32[]{:S(2)}) async-start(s8[7340032]{0:T(1024)(128)(4,1)} %bitcast.38), calls=%async_computation.5 | async-start | bytes 6291456
  5.9 2.4 %copy-start.3 = (bf16[48,1024]{1,0:T(8,128)(2,1)S(1)}, bf16[48,1024]{1,0:T(8,128)(2,1)}, u32[]{:S(2)}) copy-start(bf16[48,1024]{1,0:T(8,128)(2,1)} %param.6) | copy-start | bytes 294916
  11.5 8.2 %copy-start.1 = (bf16[3,48,1792]{2,1,0:T(8,128)(2,1)}, bf16[3,48,1792]{2,1,0:T(8,128)(2,1)S(1)}, u32[]{:S(2)}) copy-start(bf16[3,48,1792]{2,1,0:T(8,128)(2,1)S(1)} %get-tuple-element.36) | copy-start | bytes 1548292
  12.3 9.3 %collective-permute-start.3 = (bf16[3,24,1792]{2,1,0:T(8,128)(2,1)}, bf16[3,24,1792]{2,1,0:T(8,128)(2,1)}, u32[]{:S(2)}, u32[]{:S(2)}) collective-permute-start(bf16[3,24,1792]{2,1,0:T(8,128)(2,1)} %constant_dynamic-slice_fusion.11), channel_id=1, source_target_pairs={{0,4},{4,0},{8,12},{12,8},{16,20},{20,16},{24,28},{28,24},{1,5},{5... | collective-permute-start | bytes 774152 | tf_op jit(solution)/shard_map/ppermute | solution.py:37
  14.1 22.7 %collective-permute-start.2 = (bf16[48,2048]{1,0:T(8,128)(2,1)}, bf16[48,2048]{1,0:T(8,128)(2,1)S(1)}, u32[]{:S(2)}, u32[]{:S(2)}) collective-permute-start(bf16[48,2048]{1,0:T(8,128)(2,1)} %constant_dynamic-update-slice_fusion), channel_id=1, source_target_pairs={{0,3},{1,0},{2,1},{3,2},{4,7},{5,4},{6,5},{7,6},{8,11},{9,8},{10,9... | collective-permute-start | bytes 589832 | tf_op jit(solution)/shard_map/ppermute | solution.py:101
  18.7 18.2 %collective-permute-start.1 = (bf16[48,2048]{1,0:T(8,128)(2,1)}, bf16[48,2048]{1,0:T(8,128)(2,1)S(1)}, u32[]{:S(2)}, u32[]{:S(2)}) collective-permute-start(bf16[48,2048]{1,0:T(8,128)(2,1)} %constant_dynamic-update-slice_fusion), channel_id=1, source_target_pairs={{0,2},{1,3},{2,0},{3,1},{4,6},{5,7},{6,4},{7,5},{8,10},{9,11},{10,... | collective-permute-start | bytes 589832 | tf_op jit(solution)/shard_map/ppermute | solution.py:101
  18.7 18.2 %collective-permute-start = (bf16[48,2048]{1,0:T(8,128)(2,1)}, bf16[48,2048]{1,0:T(8,128)(2,1)}, u32[]{:S(2)}, u32[]{:S(2)}) collective-permute-start(bf16[48,2048]{1,0:T(8,128)(2,1)} %constant_dynamic-update-slice_fusion), channel_id=1, source_target_pairs={{0,1},{1,2},{2,3},{3,0},{4,5},{5,6},{6,7},{7,4},{8,9},{9,10},{10,1... | collective-permute-start | bytes 589832 | tf_op jit(solution)/shard_map/ppermute | solution.py:101
  19.7 22.7 %slice-start.6 = ((s8[7340032]{0:T(1024)(128)(4,1)}), s8[3145728]{0:T(1024)(128)(4,1)S(1)}, s32[]{:S(2)}) async-start(s8[7340032]{0:T(1024)(128)(4,1)} %bitcast.40), calls=%async_computation.6 | async-start | bytes 6291456
  21.6 2.8 %collective-permute-start.6 = (bf16[3,24,1792]{2,1,0:T(8,128)(2,1)}, bf16[3,24,1792]{2,1,0:T(8,128)(2,1)}, u32[]{:S(2)}, u32[]{:S(2)}) collective-permute-start(bf16[3,24,1792]{2,1,0:T(8,128)(2,1)} %constant_dynamic-slice_fusion.8), channel_id=1, source_target_pairs={{0,4},{4,0},{8,12},{12,8},{16,20},{20,16},{24,28},{28,24},{1,5},{5... | collective-permute-start | bytes 774152 | tf_op jit(solution)/shard_map/ppermute | solution.py:37
  22.8 6.9 %collective-permute-start.4 = (bf16[3,12,1792]{2,1,0:T(8,128)(2,1)S(1)}, bf16[3,12,1792]{2,1,0:T(8,128)(2,1)S(1)}, u32[]{:S(2)}, u32[]{:S(2)}) collective-permute-start(bf16[3,12,1792]{2,1,0:T(8,128)(2,1)S(1)} %constant_dynamic-slice_fusion.10), channel_id=1, source_target_pairs={{0,8},{4,12},{8,0},{12,4},{16,24},{20,28},{24,16},{28,20},{1,9},{5... | collective-permute-start | bytes 387080 | tf_op jit(solution)/shard_map/ppermute | solution.py:37
  25.5 6.6 %collective-permute-start.7 = (bf16[3,12,1792]{2,1,0:T(8,128)(2,1)S(1)}, bf16[3,12,1792]{2,1,0:T(8,128)(2,1)S(1)}, u32[]{:S(2)}, u32[]{:S(2)}) collective-permute-start(bf16[3,12,1792]{2,1,0:T(8,128)(2,1)S(1)} %constant_dynamic-slice_fusion.7), channel_id=1, source_target_pairs={{0,16},{4,20},{8,24},{12,28},{16,0},{20,4},{24,8},{28,12},{1,17},{... | collective-permute-start | bytes 387080 | tf_op jit(solution)/shard_map/ppermute | solution.py:37
  29.7 4.6 %collective-permute-start.5 = (bf16[3,6,1792]{2,1,0:T(8,128)(2,1)S(1)}, bf16[3,6,1792]{2,1,0:T(8,128)(2,1)S(1)}, u32[]{:S(2)}, u32[]{:S(2)}) collective-permute-start(bf16[3,6,1792]{2,1,0:T(8,128)(2,1)S(1)} %constant_dynamic-slice_fusion.9), channel_id=1, source_target_pairs={{0,16},{4,20},{8,24},{12,28},{16,0},{20,4},{24,8},{28,12},{1,17},{... | collective-permute-start | bytes 193544 | tf_op jit(solution)/shard_map/ppermute | solution.py:37
  32.3 4.6 %collective-permute-start.8 = (bf16[3,6,1792]{2,1,0:T(8,128)(2,1)S(1)}, bf16[3,6,1792]{2,1,0:T(8,128)(2,1)S(1)}, u32[]{:S(2)}, u32[]{:S(2)}) collective-permute-start(bf16[3,6,1792]{2,1,0:T(8,128)(2,1)S(1)} %constant_dynamic-slice_fusion.6), channel_id=1, source_target_pairs={{0,8},{4,12},{8,0},{12,4},{16,24},{20,28},{24,16},{28,20},{1,9},{5... | collective-permute-start | bytes 193544 | tf_op jit(solution)/shard_map/ppermute | solution.py:37
  37.8 8.1 %slice-start.2 = ((s8[7340032]{0:T(1024)(128)(4,1)}), s8[4194304]{0:T(1024)(128)(4,1)S(1)}, s32[]{:S(2)}) async-start(s8[7340032]{0:T(1024)(128)(4,1)} %bitcast.36), calls=%async_computation.2 | async-start | bytes 8388608
  37.9 5.5 %slice-start.7 = ((s8[7340032]{0:T(1024)(128)(4,1)}), s8[4194304]{0:T(1024)(128)(4,1)S(1)}, s32[]{:S(2)}) async-start(s8[7340032]{0:T(1024)(128)(4,1)} %bitcast.40), calls=%async_computation.7 | async-start | bytes 8388608
  37.9 8.1 %slice-start.3 = ((s8[7340032]{0:T(1024)(128)(4,1)}), s8[3145728]{0:T(1024)(128)(4,1)S(1)}, s32[]{:S(2)}) async-start(s8[7340032]{0:T(1024)(128)(4,1)} %bitcast.36), calls=%async_computation.3 | async-start | bytes 6291456
  47.4 4.6 %collective-permute-start.9 = (bf16[3,6,1792]{2,1,0:T(8,128)(2,1)S(1)}, bf16[3,6,1792]{2,1,0:T(8,128)(2,1)S(1)}, u32[]{:S(2)}, u32[]{:S(2)}) collective-permute-start(bf16[3,6,1792]{2,1,0:T(8,128)(2,1)S(1)} %pad_maximum_fusion.5), channel_id=1, source_target_pairs={{0,16},{4,20},{8,24},{12,28},{16,0},{20,4},{24,8},{28,12},{1,17},{... | collective-permute-start | bytes 193544 | tf_op jit(solution)/shard_map/ppermute | solution.py:49
  49.0 4.6 %collective-permute-start.12 = (bf16[3,6,1792]{2,1,0:T(8,128)(2,1)S(1)}, bf16[3,6,1792]{2,1,0:T(8,128)(2,1)S(1)}, u32[]{:S(2)}, u32[]{:S(2)}) collective-permute-start(bf16[3,6,1792]{2,1,0:T(8,128)(2,1)S(1)} %pad_maximum_fusion.6), channel_id=1, source_target_pairs={{0,8},{4,12},{8,0},{12,4},{16,24},{20,28},{24,16},{28,20},{1,9},{5... | collective-permute-start | bytes 193544 | tf_op jit(solution)/shard_map/ppermute | solution.py:49
  50.6 7.4 %collective-permute-start.21 = (bf16[3,72,1792]{2,1,0:T(8,128)(2,1)S(1)}, bf16[3,72,1792]{2,1,0:T(8,128)(2,1)S(1)}, u32[]{:S(2)}, u32[]{:S(2)}) collective-permute-start(bf16[3,72,1792]{2,1,0:T(8,128)(2,1)S(1)} %constant_dynamic-slice_fusion.2), channel_id=1, source_target_pairs={{0,4},{4,0},{8,12},{12,8},{16,20},{20,16},{24,28},{28,24},{1,5},{5... | collective-permute-start | bytes 2322440 | tf_op jit(solution)/shard_map/ppermute | solution.py:37
  50.7 9.0 %collective-permute-start.15 = (bf16[3,72,1792]{2,1,0:T(8,128)(2,1)S(1)}, bf16[3,72,1792]{2,1,0:T(8,128)(2,1)S(1)}, u32[]{:S(2)}, u32[]{:S(2)}) collective-permute-start(bf16[3,72,1792]{2,1,0:T(8,128)(2,1)S(1)} %constant_dynamic-slice_fusion.5), channel_id=1, source_target_pairs={{0,4},{4,0},{8,12},{12,8},{16,20},{20,16},{24,28},{28,24},{1,5},{5... | collective-permute-start | bytes 2322440 | tf_op jit(solution)/shard_map/ppermute | solution.py:37
  52.1 5.7 %collective-permute-start.10 = (bf16[3,12,1792]{2,1,0:T(8,128)(2,1)S(1)}, bf16[3,12,1792]{2,1,0:T(8,128)(2,1)S(1)}, u32[]{:S(2)}, u32[]{:S(2)}) collective-permute-start(bf16[3,12,1792]{2,1,0:T(8,128)(2,1)S(1)} %maximum_select_fusion.10), channel_id=1, source_target_pairs={{0,8},{4,12},{8,0},{12,4},{16,24},{20,28},{24,16},{28,20},{1,9},{5... | collective-permute-start | bytes 387080 | tf_op jit(solution)/shard_map/ppermute | solution.py:49
  53.7 35.0 %collective-permute-start.13 = (bf16[3,12,1792]{2,1,0:T(8,128)(2,1)S(1)}, bf16[3,12,1792]{2,1,0:T(8,128)(2,1)S(1)}, u32[]{:S(2)}, u32[]{:S(2)}) collective-permute-start(bf16[3,12,1792]{2,1,0:T(8,128)(2,1)S(1)} %maximum_select_fusion.11), channel_id=1, source_target_pairs={{0,16},{4,20},{8,24},{12,28},{16,0},{20,4},{24,8},{28,12},{1,17},{... | collective-permute-start | bytes 387080 | tf_op jit(solution)/shard_map/ppermute | solution.py:49
  57.9 40.8 %collective-permute-start.11 = (bf16[3,24,1792]{2,1,0:T(8,128)(2,1)S(1)}, bf16[3,24,1792]{2,1,0:T(8,128)(2,1)S(1)}, u32[]{:S(2)}, u32[]{:S(2)}) collective-permute-start(bf16[3,24,1792]{2,1,0:T(8,128)(2,1)S(1)} %maximum_select_fusion.8), channel_id=1, source_target_pairs={{0,4},{4,0},{8,12},{12,8},{16,20},{20,16},{24,28},{28,24},{1,5},{5... | collective-permute-start | bytes 774152 | tf_op jit(solution)/shard_map/ppermute | solution.py:49
  58.3 12.4 %collective-permute-start.22 = (bf16[3,36,1792]{2,1,0:T(8,128)(2,1)S(1)}, bf16[3,36,1792]{2,1,0:T(8,128)(2,1)S(1)}, u32[]{:S(2)}, u32[]{:S(2)}) collective-permute-start(bf16[3,36,1792]{2,1,0:T(8,128)(2,1)S(1)} %constant_dynamic-slice_fusion.1), channel_id=1, source_target_pairs={{0,16},{4,20},{8,24},{12,28},{16,0},{20,4},{24,8},{28,12},{1,17},{... | collective-permute-start | bytes 1161224 | tf_op jit(solution)/shard_map/ppermute | solution.py:37
  60.0 12.1 %collective-permute-start.16 = (bf16[3,36,1792]{2,1,0:T(8,128)(2,1)S(1)}, bf16[3,36,1792]{2,1,0:T(8,128)(2,1)S(1)}, u32[]{:S(2)}, u32[]{:S(2)}) collective-permute-start(bf16[3,36,1792]{2,1,0:T(8,128)(2,1)S(1)} %constant_dynamic-slice_fusion.4), channel_id=1, source_target_pairs={{0,8},{4,12},{8,0},{12,4},{16,24},{20,28},{24,16},{28,20},{1,9},{5... | collective-permute-start | bytes 1161224 | tf_op jit(solution)/shard_map/ppermute | solution.py:37
  70.9 7.8 %collective-permute-start.23 = (bf16[3,18,1792]{2,1,0:T(8,128)(2,1)S(1)}, bf16[3,18,1792]{2,1,0:T(8,128)(2,1)S(1)}, u32[]{:S(2)}, u32[]{:S(2)}) collective-permute-start(bf16[3,18,1792]{2,1,0:T(8,128)(2,1)S(1)} %constant_dynamic-slice_fusion), channel_id=1, source_target_pairs={{0,8},{4,12},{8,0},{12,4},{16,24},{20,28},{24,16},{28,20},{1,9},{5... | collective-permute-start | bytes 580616 | tf_op jit(solution)/shard_map/ppermute | solution.py:37
  72.4 7.8 %collective-permute-start.17 = (bf16[3,18,1792]{2,1,0:T(8,128)(2,1)S(1)}, bf16[3,18,1792]{2,1,0:T(8,128)(2,1)S(1)}, u32[]{:S(2)}, u32[]{:S(2)}) collective-permute-start(bf16[3,18,1792]{2,1,0:T(8,128)(2,1)S(1)} %constant_dynamic-slice_fusion.3), channel_id=1, source_target_pairs={{0,16},{4,20},{8,24},{12,28},{16,0},{20,4},{24,8},{28,12},{1,17},{... | collective-permute-start | bytes 580616 | tf_op jit(solution)/shard_map/ppermute | solution.py:37
  79.0 7.0 %collective-permute-start.24 = (bf16[3,18,1792]{2,1,0:T(8,128)(2,1)S(1)}, bf16[3,18,1792]{2,1,0:T(8,128)(2,1)S(1)}, u32[]{:S(2)}, u32[]{:S(2)}) collective-permute-start(bf16[3,18,1792]{2,1,0:T(8,128)(2,1)S(1)} %pad_maximum_fusion.4), channel_id=1, source_target_pairs={{0,8},{4,12},{8,0},{12,4},{16,24},{20,28},{24,16},{28,20},{1,9},{5... | collective-permute-start | bytes 580616 | tf_op jit(solution)/shard_map/ppermute | solution.py:49
  80.5 7.1 %collective-permute-start.18 = (bf16[3,18,1792]{2,1,0:T(8,128)(2,1)S(1)}, bf16[3,18,1792]{2,1,0:T(8,128)(2,1)S(1)}, u32[]{:S(2)}, u32[]{:S(2)}) collective-permute-start(bf16[3,18,1792]{2,1,0:T(8,128)(2,1)S(1)} %pad_maximum_fusion.3), channel_id=1, source_target_pairs={{0,16},{4,20},{8,24},{12,28},{16,0},{20,4},{24,8},{28,12},{1,17},{... | collective-permute-start | bytes 580616 | tf_op jit(solution)/shard_map/ppermute | solution.py:49
  86.2 10.2 %collective-permute-start.25 = (bf16[3,36,1792]{2,1,0:T(8,128)(2,1)S(1)}, bf16[3,36,1792]{2,1,0:T(8,128)(2,1)S(1)}, u32[]{:S(2)}, u32[]{:S(2)}) collective-permute-start(bf16[3,36,1792]{2,1,0:T(8,128)(2,1)S(1)} %maximum_select_fusion.7), channel_id=1, source_target_pairs={{0,16},{4,20},{8,24},{12,28},{16,0},{20,4},{24,8},{28,12},{1,17},{... | collective-permute-start | bytes 1161224 | tf_op jit(solution)/shard_map/ppermute | solution.py:49
  87.8 9.4 %collective-permute-start.19 = (bf16[3,36,1792]{2,1,0:T(8,128)(2,1)S(1)}, bf16[3,36,1792]{2,1,0:T(8,128)(2,1)S(1)}, u32[]{:S(2)}, u32[]{:S(2)}) collective-permute-start(bf16[3,36,1792]{2,1,0:T(8,128)(2,1)S(1)} %maximum_select_fusion.6), channel_id=1, source_target_pairs={{0,8},{4,12},{8,0},{12,4},{16,24},{20,28},{24,16},{28,20},{1,9},{5... | collective-permute-start | bytes 1161224 | tf_op jit(solution)/shard_map/ppermute | solution.py:49
  88.8 10.0 %collective-permute-start.14 = (bf16[3,24,1792]{2,1,0:T(8,128)(2,1)S(1)}, bf16[3,24,1792]{2,1,0:T(8,128)(2,1)S(1)}, u32[]{:S(2)}, u32[]{:S(2)}) collective-permute-start(bf16[3,24,1792]{2,1,0:T(8,128)(2,1)S(1)} %maximum_select_fusion.9), channel_id=1, source_target_pairs={{0,4},{4,0},{8,12},{12,8},{16,20},{20,16},{24,28},{28,24},{1,5},{5... | collective-permute-start | bytes 774152 | tf_op jit(solution)/shard_map/ppermute | solution.py:49
  96.7 2.3 %collective-permute-start.26 = (bf16[3,72,1792]{2,1,0:T(8,128)(2,1)S(1)}, bf16[3,72,1792]{2,1,0:T(8,128)(2,1)S(1)}, u32[]{:S(2)}, u32[]{:S(2)}) collective-permute-start(bf16[3,72,1792]{2,1,0:T(8,128)(2,1)S(1)} %maximum_select_fusion.3), channel_id=1, source_target_pairs={{0,4},{4,0},{8,12},{12,8},{16,20},{20,16},{24,28},{28,24},{1,5},{5... | collective-permute-start | bytes 2322440 | tf_op jit(solution)/shard_map/ppermute | solution.py:49
  97.5 2.6 %collective-permute-start.20 = (bf16[3,72,1792]{2,1,0:T(8,128)(2,1)S(1)}, bf16[3,72,1792]{2,1,0:T(8,128)(2,1)S(1)}, u32[]{:S(2)}, u32[]{:S(2)}) collective-permute-start(bf16[3,72,1792]{2,1,0:T(8,128)(2,1)S(1)} %maximum_select_fusion.2), channel_id=1, source_target_pairs={{0,4},{4,0},{8,12},{12,8},{16,20},{20,16},{24,28},{28,24},{1,5},{5... | collective-permute-start | bytes 2322440 | tf_op jit(solution)/shard_map/ppermute | solution.py:49
  99.0 4.8 %slice-start = ((s8[7340032]{0:T(1024)(128)(4,1)}), s8[4194304]{0:T(1024)(128)(4,1)S(1)}, s32[]{:S(2)}) async-start(s8[7340032]{0:T(1024)(128)(4,1)} %bitcast.34), calls=%async_computation | async-start | bytes 8388608
  100.6 3.2 %slice-start.1 = ((s8[7340032]{0:T(1024)(128)(4,1)}), s8[3145728]{0:T(1024)(128)(4,1)S(1)}, s32[]{:S(2)}) async-start(s8[7340032]{0:T(1024)(128)(4,1)} %bitcast.34), calls=%async_computation.1 | async-start | bytes 6291456
  114.3 14.9 %collective-permute-start.27 = (bf16[48,1024]{1,0:T(8,128)(2,1)S(1)}, bf16[48,1024]{1,0:T(8,128)(2,1)S(1)}, u32[]{:S(2)}, u32[]{:S(2)}) collective-permute-start(bf16[48,1024]{1,0:T(8,128)(2,1)S(1)} %get-tuple-element.43), channel_id=1, source_target_pairs={{0,3},{1,0},{2,1},{3,2},{4,7},{5,4},{6,5},{7,6},{8,11},{9,8},{10,9... | collective-permute-start | bytes 294920 | tf_op jit(solution)/shard_map/ppermute | solution.py:95
  117.2 12.1 %collective-permute-start.29 = (bf16[48,1024]{1,0:T(8,128)(2,1)S(1)}, bf16[48,1024]{1,0:T(8,128)(2,1)S(1)}, u32[]{:S(2)}, u32[]{:S(2)}) collective-permute-start(bf16[48,1024]{1,0:T(8,128)(2,1)S(1)} %get-tuple-element.44), channel_id=1, source_target_pairs={{0,1},{1,2},{2,3},{3,0},{4,5},{5,6},{6,7},{7,4},{8,9},{9,10},{10,1... | collective-permute-start | bytes 294920 | tf_op jit(solution)/shard_map/ppermute | solution.py:95
  117.2 12.1 %collective-permute-start.28 = (bf16[48,1024]{1,0:T(8,128)(2,1)S(1)}, bf16[48,1024]{1,0:T(8,128)(2,1)S(1)}, u32[]{:S(2)}, u32[]{:S(2)}) collective-permute-start(bf16[48,1024]{1,0:T(8,128)(2,1)S(1)} %get-tuple-element.45), channel_id=1, source_target_pairs={{0,2},{1,3},{2,0},{3,1},{4,6},{5,7},{6,4},{7,5},{8,10},{9,11},{10,... | collective-permute-start | bytes 294920 | tf_op jit(solution)/shard_map/ppermute | solution.py:95

commit v9 on v8

--- a/solution.py
+++ b/solution.py
@@ -117,14 +117,10 @@
         stages = [both, col_gather_remote(both, n_col)]
     else:
         stages = [col_gather(both, n_col)]
+    if staged:
+        stages[1] = jnp.concatenate(stages[1], axis=0)
     gated_parts = []
-    reduced = None
-    for i, st in enumerate(stages):
-        if i > 0:
-            st, reduced = lax.optimization_barrier((st, reduced))
-            st = jnp.concatenate(st, axis=0)
-            stages[i] = st
-            gated_parts.append(row_gather_gated(reduced, n_row))
+    for st in stages:
         tok_s = st[:, :feat]
         grad_s = st[:, feat:]
         stacked = jnp.stack(
@@ -134,8 +130,7 @@
                 contract_last(grad_s, down_weight).astype(jnp.bfloat16),
             ]
         )
-        reduced = row_reduce(stacked, n_row)
-    gated_parts.append(row_gather_gated(reduced, n_row))
+        gated_parts.append(row_gather_gated(row_reduce(stacked, n_row), n_row))
     gated = jnp.concatenate(gated_parts, axis=1) if len(gated_parts) > 1 else gated_parts[0]
     both_all = jnp.concatenate(stages, axis=0) if len(stages) > 1 else stages[0]
     tok_all = both_all[:, :feat]

time: 130 us -> 133 us (1.023)
  waiting for transfers between devices: 39.4 us -> 34.7 us
  starting transfers between devices: 30.8 us -> 34.1 us
  matrix products: 37.2 us -> 40.4 us
  local copies, waits for them, and re-layouts: 9.48 us -> 11.1 us
    dot_general x2, matrix products: 9.13 us -> 5.83 us  [body(): jnp.dot(tok_s, up_weight, preferred_element_type=jnp.float32)]
    dot_general x4, matrix products: 9.92 us -> 13.2 us  [contract_last(): lax.dot_general(left, right, (((1,), (1,)), ((), ())), preferred_element_...]
    dot_general x2, matrix products: 2.6 us -> 5.84 us  [body(): jnp.dot(tok_s, gate_weight, preferred_element_type=jnp.float32)]
    ppermute x12, waiting for transfers between devices: 22.1 us -> 19.1 us  [halving_reduce(): got = lax.ppermute(send, 'row', [(j, j ^ bit) for j in range(n_dev)])]
    ppermute x12, starting transfers between devices: 9.41 us -> 11.5 us  [doubling_gather(): got = lax.ppermute(cur, 'row', [(j, j ^ bit) for j in range(n_dev)])]
    ppermute x12, waiting for transfers between devices: 17.3 us -> 15.6 us  [doubling_gather(): got = lax.ppermute(cur, 'row', [(j, j ^ bit) for j in range(n_dev)])]
    unnamed x27 -> x25, local copies, waits for them, and re-layouts: 4.17 us -> 3.8 us
  transfers between devices with their start and end apart: 30 -> 30, of which waited for: 15 -> 15; matrix products, arithmetic and copies ran while one was open for 17% -> 33% of each run, Pallas kernels for 0% -> 0%
where the time goes in v9:
time: 133 us
  matrix products  40.4 us (30%)
  waiting for transfers between devices  34.7 us (26%)
  starting transfers between devices  34.1 us (26%)
  other arithmetic  11.5 us (9%)
  local copies, waits for them, and re-layouts  11.1 us (8%)
    ppermute x12, waiting for transfers between devices, halving_reduce(): got = lax.ppermute(send, 'row', [(j, j ^ bit) for j in range(n_dev)])  19.1 us
    ppermute x12, waiting for transfers between devices, doubling_gather(): got = lax.ppermute(cur, 'row', [(j, j ^ bit) for j in range(n_dev)])  15.6 us
    dot_general x4, matrix products, contract_last(): lax.dot_general(left, right, (((1,), (1,)), ((), ())), preferred_element_...  13.2 us
    ppermute x12, starting transfers between devices, halving_reduce(): got = lax.ppermute(send, 'row', [(j, j ^ bit) for j in range(n_dev)])  12.5 us
    ppermute x12, starting transfers between devices, doubling_gather(): got = lax.ppermute(cur, 'row', [(j, j ^ bit) for j in range(n_dev)])  11.5 us
    ppermute x3, starting transfers between devices, col_gather_remote(): lax.ppermute(x, 'col', [(j, (j + s) % n_col) for j in range(n_col)])  6.09 us
    dot_general x2, matrix products, body(): jnp.dot(tok_s, gate_weight, preferred_element_type=jnp.float32)  5.84 us
    dot_general x2, matrix products, body(): jnp.dot(tok_s, up_weight, preferred_element_type=jnp.float32)  5.83 us
  transfers between devices with their start and end apart: 30, of which 15 were waited for; matrix products, arithmetic and copies ran while one was open for 33% of the time, Pallas kernels for 0%

profile of v9, /device:TPU:0, one launch (start us, length us, event | category | flops | bytes accessed | tf_op | source)
XLA Modules:
  0.0 132.9 jit_solution(7578199356321330853)
XLA Ops:
  0.6 1.6 %constant_dynamic-update-slice_fusion.1 = bf16[48,2048]{1,0:T(8,128)(2,1)} fusion(bf16[48,1024]{1,0:T(8,128)(2,1)} %param.5), kind=kLoop, calls=%fused_computation.76 | loop fusion | bytes 196608
  2.2 1.6 %constant_dynamic-update-slice_fusion = bf16[48,2048]{1,0:T(8,128)(2,1)} fusion(bf16[48,2048]{1,0:T(8,128)(2,1)} %constant_dynamic-update-slice_fusion.1, bf16[48,1024]{1,0:T(8,128)(2,1)} %param.6), kind=kLoop, calls=%fused_computation.75 | loop fusion | bytes 196608 | tf_op jit(solution)/shard_map/concatenate | solution.py:110
  3.8 5.1 %collective-permute-start.14 = (bf16[48,2048]{1,0:T(8,128)(2,1)}, bf16[48,2048]{1,0:T(8,128)(2,1)S(1)}, u32[]{:S(2)}, u32[]{:S(2)}) collective-permute-start(bf16[48,2048]{1,0:T(8,128)(2,1)} %constant_dynamic-update-slice_fusion), channel_id=1, source_target_pairs={{0,3},{1,0},{2,1},{3,2},{4,7},{5,4},{6,5},{7,6},{8,11},{9,8},{10,9... | collective-permute-start | bytes 589832 | tf_op jit(solution)/shard_map/ppermute | solution.py:101
  8.8 1.0 collective-permute-start.12
  9.8 5.6 %fusion.5 = bf16[1,48,3584]{2,1,0:T(8,128)(2,1)S(1)} fusion(bf16[48,1024]{1,0:T(8,128)(2,1)} %param.6, bf16[3584,1024]{1,0:T(8,128)(2,1)} %param.9), kind=kOutput, calls=%fused_computation.14 | convolution fusion | flops 352493568 | bytes 7782400 | tf_op jit(solution)/shard_map/dot_general | solution.py:14
  15.5 4.6 %fusion.3 = bf16[1,48,3584]{2,1,0:T(8,128)(2,1)S(1)} fusion(bf16[48,1024]{1,0:T(8,128)(2,1)S(1)} %copy-done.2, bf16[1024,3584]{1,0:T(8,128)(2,1)} %param.7), kind=kOutput, calls=%fused_computation.12 | convolution fusion | flops 352493568 | bytes 7782400 | tf_op jit(solution)/shard_map/dot_general | solution.py:128
  20.1 1.4 %fusion.4 = bf16[1,48,3584]{2,1,0:T(8,128)(2,1)S(1)} fusion(bf16[48,1024]{1,0:T(8,128)(2,1)S(1)} %copy-done.2, bf16[1024,3584]{1,0:T(8,128)(2,1)S(1)} %bitcast.35), kind=kOutput, calls=%fused_computation.13 | convolution fusion | flops 352493568 | bytes 7782400 | tf_op jit(solution)/shard_map/dot_general | solution.py:129
  21.6 1.0 fusion.15
  22.6 1.8 %constant_dynamic-slice_fusion.8 = bf16[3,24,1792]{2,1,0:T(8,128)(2,1)} fusion(bf16[3,48,1792]{2,1,0:T(8,128)(2,1)} %get-tuple-element.26, s32[]{:T(128)S(6)} %select_n.239), kind=kLoop, calls=%fused_computation.88 | loop fusion | bytes 516100 | tf_op jit(solution)/shard_map/dynamic_slice | solution.py:36
  24.5 1.7 %constant_dynamic-slice_fusion.11 = bf16[3,24,1792]{2,1,0:T(8,128)(2,1)} fusion(bf16[3,48,1792]{2,1,0:T(8,128)(2,1)} %get-tuple-element.25, s32[]{:T(128)S(6)} %select_n.239), kind=kLoop, calls=%fused_computation.91 | loop fusion | bytes 516100 | tf_op jit(solution)/shard_map/dynamic_slice | solution.py:36
  26.1 0.5 collective-permute-start
  26.6 0.9 constant_dynamic-update-slice_fusion.4
  27.7 4.5 %fusion.1 = bf16[1,144,3584]{2,1,0:T(8,128)(2,1)S(1)} fusion(bf16[1024,3584]{1,0:T(8,128)(2,1)} %param.8, bf16[144,2048]{1,0:T(8,128)(2,1)S(1)} %constant_dynamic-update-slice_fusion.2), kind=kOutput, calls=%fused_computation.7 | convolution fusion | flops 1057480704 | bytes 8667136 | tf_op jit(solution)/shard_map/dot_general | solution.py:129
  32.2 1.0 slice-done.7
  33.2 2.6 %fusion.2 = bf16[1,144,3584]{2,1,0:T(8,128)(2,1)S(1)} fusion(bf16[3584,1024]{1,0:T(8,128)(2,1)S(1)} %bitcast.41, bf16[144,2048]{1,0:T(8,128)(2,1)S(1)} %constant_dynamic-update-slice_fusion.2), kind=kOutput, calls=%fused_computation.8 | convolution fusion | flops 1057480704 | bytes 8667136 | tf_op jit(solution)/shard_map/dot_general | solution.py:14
  35.8 1.3 fusion
  37.0 0.3 pad_maximum_fusion
  37.8 0.5 collective-permute-start.15
  38.6 1.0 add_convert_fusion.4
  39.7 1.6 %collective-permute-start.7 = (bf16[3,12,1792]{2,1,0:T(8,128)(2,1)S(1)}, bf16[3,12,1792]{2,1,0:T(8,128)(2,1)S(1)}, u32[]{:S(2)}, u32[]{:S(2)}) collective-permute-start(bf16[3,12,1792]{2,1,0:T(8,128)(2,1)S(1)} %constant_dynamic-slice_fusion.7), channel_id=1, source_target_pairs={{0,16},{4,20},{8,24},{12,28},{16,0},{20,4},{24,8},{28,12},{1,17},{... | collective-permute-start | bytes 387080 | tf_op jit(solution)/shard_map/ppermute | solution.py:37
  41.3 1.0 add_convert_fusion.5
  42.4 1.6 %collective-permute-start.1 = (bf16[3,12,1792]{2,1,0:T(8,128)(2,1)S(1)}, bf16[3,12,1792]{2,1,0:T(8,128)(2,1)S(1)}, u32[]{:S(2)}, u32[]{:S(2)}) collective-permute-start(bf16[3,12,1792]{2,1,0:T(8,128)(2,1)S(1)} %constant_dynamic-slice_fusion.10), channel_id=1, source_target_pairs={{0,8},{4,12},{8,0},{12,4},{16,24},{20,28},{24,16},{28,20},{1,9},{5... | collective-permute-start | bytes 387080 | tf_op jit(solution)/shard_map/ppermute | solution.py:37
  44.0 2.1 %collective-permute-done.7 = bf16[3,12,1792]{2,1,0:T(8,128)(2,1)S(1)} collective-permute-done((bf16[3,12,1792]{2,1,0:T(8,128)(2,1)S(1)}, bf16[3,12,1792]{2,1,0:T(8,128)(2,1)S(1)}, u32[]{:S(2)}, u32[]{:S(2)}) %collective-permute-start.7) | collective-permute-done | bytes 129056 | tf_op jit(solution)/shard_map/ppermute | solution.py:37
  46.2 1.6 %collective-permute-start.8 = (bf16[3,6,1792]{2,1,0:T(8,128)(2,1)S(1)}, bf16[3,6,1792]{2,1,0:T(8,128)(2,1)S(1)}, u32[]{:S(2)}, u32[]{:S(2)}) collective-permute-start(bf16[3,6,1792]{2,1,0:T(8,128)(2,1)S(1)} %constant_dynamic-slice_fusion.6), channel_id=1, source_target_pairs={{0,8},{4,12},{8,0},{12,4},{16,24},{20,28},{24,16},{28,20},{1,9},{5... | collective-permute-start | bytes 193544 | tf_op jit(solution)/shard_map/ppermute | solution.py:37
  47.7 1.2 collective-permute-done.1
  49.1 0.4 collective-permute-start.2
  49.5 1.3 collective-permute-done.8
  50.9 1.6 %collective-permute-start.9 = (bf16[3,6,1792]{2,1,0:T(8,128)(2,1)S(1)}, bf16[3,6,1792]{2,1,0:T(8,128)(2,1)S(1)}, u32[]{:S(2)}, u32[]{:S(2)}) collective-permute-start(bf16[3,6,1792]{2,1,0:T(8,128)(2,1)S(1)} %pad_maximum_fusion.6), channel_id=1, source_target_pairs={{0,8},{4,12},{8,0},{12,4},{16,24},{20,28},{24,16},{28,20},{1,9},{5... | collective-permute-start | bytes 193544 | tf_op jit(solution)/shard_map/ppermute | solution.py:49
  52.4 1.2 collective-permute-done.2
  53.7 0.4 collective-permute-start.3
  54.1 1.3 collective-permute-done.9
  55.5 1.6 %collective-permute-start.10 = (bf16[3,12,1792]{2,1,0:T(8,128)(2,1)S(1)}, bf16[3,12,1792]{2,1,0:T(8,128)(2,1)S(1)}, u32[]{:S(2)}, u32[]{:S(2)}) collective-permute-start(bf16[3,12,1792]{2,1,0:T(8,128)(2,1)S(1)} %maximum_select_fusion.11), channel_id=1, source_target_pairs={{0,16},{4,20},{8,24},{12,28},{16,0},{20,4},{24,8},{28,12},{1,17},{... | collective-permute-start | bytes 387080 | tf_op jit(solution)/shard_map/ppermute | solution.py:49
  57.1 1.4 %collective-permute-done.3 = bf16[3,6,1792]{2,1,0:T(8,128)(2,1)S(1)} collective-permute-done((bf16[3,6,1792]{2,1,0:T(8,128)(2,1)S(1)}, bf16[3,6,1792]{2,1,0:T(8,128)(2,1)S(1)}, u32[]{:S(2)}, u32[]{:S(2)}) %collective-permute-start.3) | collective-permute-done | bytes 64544 | tf_op jit(solution)/shard_map/ppermute | solution.py:49
  58.7 1.6 %collective-permute-start.4 = (bf16[3,12,1792]{2,1,0:T(8,128)(2,1)S(1)}, bf16[3,12,1792]{2,1,0:T(8,128)(2,1)S(1)}, u32[]{:S(2)}, u32[]{:S(2)}) collective-permute-start(bf16[3,12,1792]{2,1,0:T(8,128)(2,1)S(1)} %maximum_select_fusion.10), channel_id=1, source_target_pairs={{0,8},{4,12},{8,0},{12,4},{16,24},{20,28},{24,16},{28,20},{1,9},{5... | collective-permute-start | bytes 387080 | tf_op jit(solution)/shard_map/ppermute | solution.py:49
  60.2 0.8 collective-permute-done.10
  61.6 1.6 %collective-permute-start.22 = (bf16[3,36,1792]{2,1,0:T(8,128)(2,1)S(1)}, bf16[3,36,1792]{2,1,0:T(8,128)(2,1)S(1)}, u32[]{:S(2)}, u32[]{:S(2)}) collective-permute-start(bf16[3,36,1792]{2,1,0:T(8,128)(2,1)S(1)} %constant_dynamic-slice_fusion.1), channel_id=1, source_target_pairs={{0,16},{4,20},{8,24},{12,28},{16,0},{20,4},{24,8},{28,12},{1,17},{... | collective-permute-start | bytes 1161224 | tf_op jit(solution)/shard_map/ppermute | solution.py:37
  63.5 1.6 %collective-permute-start.16 = (bf16[3,36,1792]{2,1,0:T(8,128)(2,1)S(1)}, bf16[3,36,1792]{2,1,0:T(8,128)(2,1)S(1)}, u32[]{:S(2)}, u32[]{:S(2)}) collective-permute-start(bf16[3,36,1792]{2,1,0:T(8,128)(2,1)S(1)} %constant_dynamic-slice_fusion.4), channel_id=1, source_target_pairs={{0,8},{4,12},{8,0},{12,4},{16,24},{20,28},{24,16},{28,20},{1,9},{5... | collective-permute-start | bytes 1161224 | tf_op jit(solution)/shard_map/ppermute | solution.py:37
  65.0 8.9 %collective-permute-done.22 = bf16[3,36,1792]{2,1,0:T(8,128)(2,1)S(1)} collective-permute-done((bf16[3,36,1792]{2,1,0:T(8,128)(2,1)S(1)}, bf16[3,36,1792]{2,1,0:T(8,128)(2,1)S(1)}, u32[]{:S(2)}, u32[]{:S(2)}) %collective-permute-start.22) | collective-permute-done | bytes 387104 | tf_op jit(solution)/shard_map/ppermute | solution.py:37
  74.2 1.6 %collective-permute-start.23 = (bf16[3,18,1792]{2,1,0:T(8,128)(2,1)S(1)}, bf16[3,18,1792]{2,1,0:T(8,128)(2,1)S(1)}, u32[]{:S(2)}, u32[]{:S(2)}) collective-permute-start(bf16[3,18,1792]{2,1,0:T(8,128)(2,1)S(1)} %constant_dynamic-slice_fusion), channel_id=1, source_target_pairs={{0,8},{4,12},{8,0},{12,4},{16,24},{20,28},{24,16},{28,20},{1,9},{5... | collective-permute-start | bytes 580616 | tf_op jit(solution)/shard_map/ppermute | solution.py:37
  76.0 1.6 %collective-permute-start.17 = (bf16[3,18,1792]{2,1,0:T(8,128)(2,1)S(1)}, bf16[3,18,1792]{2,1,0:T(8,128)(2,1)S(1)}, u32[]{:S(2)}, u32[]{:S(2)}) collective-permute-start(bf16[3,18,1792]{2,1,0:T(8,128)(2,1)S(1)} %constant_dynamic-slice_fusion.3), channel_id=1, source_target_pairs={{0,16},{4,20},{8,24},{12,28},{16,0},{20,4},{24,8},{28,12},{1,17},{... | collective-permute-start | bytes 580616 | tf_op jit(solution)/shard_map/ppermute | solution.py:37
  77.6 4.4 %collective-permute-done.23 = bf16[3,18,1792]{2,1,0:T(8,128)(2,1)S(1)} collective-permute-done((bf16[3,18,1792]{2,1,0:T(8,128)(2,1)S(1)}, bf16[3,18,1792]{2,1,0:T(8,128)(2,1)S(1)}, u32[]{:S(2)}, u32[]{:S(2)}) %collective-permute-start.23) | collective-permute-done | bytes 193568 | tf_op jit(solution)/shard_map/ppermute | solution.py:37
  82.3 1.7 %collective-permute-start.24 = (bf16[3,18,1792]{2,1,0:T(8,128)(2,1)S(1)}, bf16[3,18,1792]{2,1,0:T(8,128)(2,1)S(1)}, u32[]{:S(2)}, u32[]{:S(2)}) collective-permute-start(bf16[3,18,1792]{2,1,0:T(8,128)(2,1)S(1)} %pad_maximum_fusion.4), channel_id=1, source_target_pairs={{0,8},{4,12},{8,0},{12,4},{16,24},{20,28},{24,16},{28,20},{1,9},{5... | collective-permute-start | bytes 580616 | tf_op jit(solution)/shard_map/ppermute | solution.py:49
  84.2 1.6 %collective-permute-start.18 = (bf16[3,18,1792]{2,1,0:T(8,128)(2,1)S(1)}, bf16[3,18,1792]{2,1,0:T(8,128)(2,1)S(1)}, u32[]{:S(2)}, u32[]{:S(2)}) collective-permute-start(bf16[3,18,1792]{2,1,0:T(8,128)(2,1)S(1)} %pad_maximum_fusion.3), channel_id=1, source_target_pairs={{0,16},{4,20},{8,24},{12,28},{16,0},{20,4},{24,8},{28,12},{1,17},{... | collective-permute-start | bytes 580616 | tf_op jit(solution)/shard_map/ppermute | solution.py:49
  85.8 3.6 %collective-permute-done.24 = bf16[3,18,1792]{2,1,0:T(8,128)(2,1)S(1)} collective-permute-done((bf16[3,18,1792]{2,1,0:T(8,128)(2,1)S(1)}, bf16[3,18,1792]{2,1,0:T(8,128)(2,1)S(1)}, u32[]{:S(2)}, u32[]{:S(2)}) %collective-permute-start.24) | collective-permute-done | bytes 193568 | tf_op jit(solution)/shard_map/ppermute | solution.py:49
  89.6 1.6 %collective-permute-start.25 = (bf16[3,36,1792]{2,1,0:T(8,128)(2,1)S(1)}, bf16[3,36,1792]{2,1,0:T(8,128)(2,1)S(1)}, u32[]{:S(2)}, u32[]{:S(2)}) collective-permute-start(bf16[3,36,1792]{2,1,0:T(8,128)(2,1)S(1)} %maximum_select_fusion.7), channel_id=1, source_target_pairs={{0,16},{4,20},{8,24},{12,28},{16,0},{20,4},{24,8},{28,12},{1,17},{... | collective-permute-start | bytes 1161224 | tf_op jit(solution)/shard_map/ppermute | solution.py:49
  91.2 0.5 collective-permute-done.18
  91.9 1.0 collective-permute-start.19
  93.1 7.0 %collective-permute-done.25 = bf16[3,36,1792]{2,1,0:T(8,128)(2,1)S(1)} collective-permute-done((bf16[3,36,1792]{2,1,0:T(8,128)(2,1)S(1)}, bf16[3,36,1792]{2,1,0:T(8,128)(2,1)S(1)}, u32[]{:S(2)}, u32[]{:S(2)}) %collective-permute-start.25) | collective-permute-done | bytes 387104 | tf_op jit(solution)/shard_map/ppermute | solution.py:49
  100.1 0.3 maximum_select_fusion.3
  100.5 0.3 collective-permute-done.19
  100.9 0.3 maximum_select_fusion.2
  101.4 1.1 pad_maximum_fusion.2
  102.8 0.5 maximum_select_fusion.1
  103.3 0.6 collective-permute-done.20
  103.9 0.5 maximum_select_fusion
  104.4 2.9 %maximum_maximum_fusion = bf16[3,192,3584]{2,1,0:T(8,128)(2,1)S(1)} fusion(bf16[3,144,1792]{2,1,0:T(8,128)(2,1)S(1)} %maximum_select_fusion.1, bf16[3,144,1792]{2,1,0:T(8,128)(2,1)S(1)} %maximum_select_fusion, bf16[3,48,1792]{2,1,0:T(8,128)(2,1)S(1)} %maximum_select_fusion.5, bf16[3,48,1792]{2,1,0:T(8,128)(2,1)S(1)} %maximum_select_fusion.4), kind=kLoop, calls=%fused_computation.15 | loop fusion | flops 16515072 | bytes 8257536 | tf_op jit(solution)/shard_map/concatenate | solution.py:134
  107.4 2.5 %fusion.13 = f32[192,1024]{1,0:T(8,128)S(1)} fusion(bf16[1024,3584]{1,0:T(8,128)(2,1)S(1)} %bitcast.37, bf16[3,192,3584]{2,1,0:T(8,128)(2,1)S(1)} %maximum_maximum_fusion), kind=kOutput, calls=%fused_computation.92 | convolution fusion | flops 1409286144 | bytes 9502720 | tf_op jit(solution)/shard_map/dot_general | solution.py:14
  110.2 2.5 %fusion.6 = bf16[192,1024]{1,0:T(8,128)(2,1)S(1)} fusion(f32[192,1024]{1,0:T(8,128)S(1)} %fusion.13, bf16[1024,3584]{1,0:T(8,128)(2,1)S(1)} %bitcast.39, bf16[3,192,3584]{2,1,0:T(8,128)(2,1)S(1)} %maximum_maximum_fusion), kind=kOutput, calls=%fused_computation.25 | convolution fusion | flops 1409679360 | bytes 9895936 | tf_op jit(solution)/shard_map/dot_general | solution.py:14
  112.7 5.2 %convolution_convert_fusion.2 = bf16[1024,3584]{1,0:T(8,128)(2,1)} fusion(bf16[192,3584]{1,0:T(8,128)(2,1)S(1)} %get-tuple-element.13, bf16[192,2048]{1,0:T(8,128)(2,1)S(1)} %pad_maximum_fusion.2), kind=kOutput, calls=%fused_computation.2 | convolution fusion | flops 1412956160 | bytes 9109504 | tf_op jit(solution)/shard_map/dot_general | solution.py:144
  117.9 2.9 %collective-permute-start.27 = (bf16[48,1024]{1,0:T(8,128)(2,1)S(1)}, bf16[48,1024]{1,0:T(8,128)(2,1)S(1)}, u32[]{:S(2)}, u32[]{:S(2)}) collective-permute-start(bf16[48,1024]{1,0:T(8,128)(2,1)S(1)} %get-tuple-element.33), channel_id=1, source_target_pairs={{0,3},{1,0},{2,1},{3,2},{4,7},{5,4},{6,5},{7,6},{8,11},{9,8},{10,9... | collective-permute-start | bytes 294920 | tf_op jit(solution)/shard_map/ppermute | solution.py:95
  120.8 1.1 collective-permute-start.28
  121.9 5.2 %convolution_convert_fusion.1 = bf16[1024,3584]{1,0:T(8,128)(2,1)} fusion(bf16[192,3584]{1,0:T(8,128)(2,1)S(1)} %get-tuple-element.18, bf16[192,2048]{1,0:T(8,128)(2,1)S(1)} %pad_maximum_fusion.2), kind=kOutput, calls=%fused_computation.1 | convolution fusion | flops 1412956160 | bytes 9109504 | tf_op jit(solution)/shard_map/dot_general | solution.py:147
  127.1 5.2 %convolution_convert_fusion = bf16[3584,1024]{1,0:T(8,128)(2,1)} fusion(bf16[192,3584]{1,0:T(8,128)(2,1)S(1)} %get-tuple-element.19, bf16[192,2048]{1,0:T(8,128)(2,1)S(1)} %pad_maximum_fusion.2), kind=kOutput, calls=%fused_computation | convolution fusion | flops 1412956160 | bytes 9109504 | tf_op jit(solution)/shard_map/dot_general | solution.py:8
  132.2 0.7 add_convert_fusion.8
  (91 shorter events, 4.9 us)
Async XLA Ops:
  3.8 23.9 %collective-permute-start.14 = (bf16[48,2048]{1,0:T(8,128)(2,1)}, bf16[48,2048]{1,0:T(8,128)(2,1)S(1)}, u32[]{:S(2)}, u32[]{:S(2)}) collective-permute-start(bf16[48,2048]{1,0:T(8,128)(2,1)} %constant_dynamic-update-slice_fusion), channel_id=1, source_target_pairs={{0,3},{1,0},{2,1},{3,2},{4,7},{5,4},{6,5},{7,6},{8,11},{9,8},{10,9... | collective-permute-start | bytes 589832 | tf_op jit(solution)/shard_map/ppermute | solution.py:101
  8.8 18.8 %collective-permute-start.13 = (bf16[48,2048]{1,0:T(8,128)(2,1)}, bf16[48,2048]{1,0:T(8,128)(2,1)S(1)}, u32[]{:S(2)}, u32[]{:S(2)}) collective-permute-start(bf16[48,2048]{1,0:T(8,128)(2,1)} %constant_dynamic-update-slice_fusion), channel_id=1, source_target_pairs={{0,2},{1,3},{2,0},{3,1},{4,6},{5,7},{6,4},{7,5},{8,10},{9,11},{10,... | collective-permute-start | bytes 589832 | tf_op jit(solution)/shard_map/ppermute | solution.py:101
  8.8 17.8 %collective-permute-start.12 = (bf16[48,2048]{1,0:T(8,128)(2,1)}, bf16[48,2048]{1,0:T(8,128)(2,1)}, u32[]{:S(2)}, u32[]{:S(2)}) collective-permute-start(bf16[48,2048]{1,0:T(8,128)(2,1)} %constant_dynamic-update-slice_fusion), channel_id=1, source_target_pairs={{0,1},{1,2},{2,3},{3,0},{4,5},{5,6},{6,7},{7,4},{8,9},{9,10},{10,1... | collective-permute-start | bytes 589832 | tf_op jit(solution)/shard_map/ppermute | solution.py:101
  9.8 5.6 %copy-start.2 = (bf16[48,1024]{1,0:T(8,128)(2,1)S(1)}, bf16[48,1024]{1,0:T(8,128)(2,1)}, u32[]{:S(2)}) copy-start(bf16[48,1024]{1,0:T(8,128)(2,1)} %param.5) | copy-start | bytes 294916
  9.8 10.2 %slice-start = ((s8[7340032]{0:T(1024)(128)(4,1)}), s8[3145728]{0:T(1024)(128)(4,1)S(1)}, s32[]{:S(2)}) async-start(s8[7340032]{0:T(1024)(128)(4,1)} %bitcast.34), calls=%async_computation | async-start | bytes 6291456
  15.5 4.6 %slice-start.1 = ((s8[7340032]{0:T(1024)(128)(4,1)}), s8[4194304]{0:T(1024)(128)(4,1)S(1)}, s32[]{:S(2)}) async-start(s8[7340032]{0:T(1024)(128)(4,1)} %bitcast.34), calls=%async_computation.1 | async-start | bytes 8388608
  21.5 10.7 %slice-start.6 = ((s8[7340032]{0:T(1024)(128)(4,1)}), s8[3145728]{0:T(1024)(128)(4,1)S(1)}, s32[]{:S(2)}) async-start(s8[7340032]{0:T(1024)(128)(4,1)} %bitcast.40), calls=%async_computation.6 | async-start | bytes 6291456
  24.5 13.9 %collective-permute-start.6 = (bf16[3,24,1792]{2,1,0:T(8,128)(2,1)}, bf16[3,24,1792]{2,1,0:T(8,128)(2,1)}, u32[]{:S(2)}, u32[]{:S(2)}) collective-permute-start(bf16[3,24,1792]{2,1,0:T(8,128)(2,1)} %constant_dynamic-slice_fusion.8), channel_id=1, source_target_pairs={{0,4},{4,0},{8,12},{12,8},{16,20},{20,16},{24,28},{28,24},{1,5},{5... | collective-permute-start | bytes 774152 | tf_op jit(solution)/shard_map/ppermute | solution.py:37
  26.1 15.2 %collective-permute-start = (bf16[3,24,1792]{2,1,0:T(8,128)(2,1)}, bf16[3,24,1792]{2,1,0:T(8,128)(2,1)}, u32[]{:S(2)}, u32[]{:S(2)}) collective-permute-start(bf16[3,24,1792]{2,1,0:T(8,128)(2,1)} %constant_dynamic-slice_fusion.11), channel_id=1, source_target_pairs={{0,4},{4,0},{8,12},{12,8},{16,20},{20,16},{24,28},{28,24},{1,5},{5... | collective-permute-start | bytes 774152 | tf_op jit(solution)/shard_map/ppermute | solution.py:37
  27.6 8.2 %slice-start.4 = ((s8[7340032]{0:T(1024)(128)(4,1)}), s8[4194304]{0:T(1024)(128)(4,1)S(1)}, s32[]{:S(2)}) async-start(s8[7340032]{0:T(1024)(128)(4,1)} %bitcast.38), calls=%async_computation.4 | async-start | bytes 8388608
  27.7 5.5 %slice-start.7 = ((s8[7340032]{0:T(1024)(128)(4,1)}), s8[4194304]{0:T(1024)(128)(4,1)S(1)}, s32[]{:S(2)}) async-start(s8[7340032]{0:T(1024)(128)(4,1)} %bitcast.40), calls=%async_computation.7 | async-start | bytes 8388608
  27.7 8.1 %slice-start.5 = ((s8[7340032]{0:T(1024)(128)(4,1)}), s8[3145728]{0:T(1024)(128)(4,1)S(1)}, s32[]{:S(2)}) async-start(s8[7340032]{0:T(1024)(128)(4,1)} %bitcast.38), calls=%async_computation.5 | async-start | bytes 6291456
  37.6 1.0 copy-start.1
  37.6 3.7 %copy-start = (bf16[3,48,1792]{2,1,0:T(8,128)(2,1)S(1)}, bf16[3,48,1792]{2,1,0:T(8,128)(2,1)}, u32[]{:S(2)}) copy-start(bf16[3,48,1792]{2,1,0:T(8,128)(2,1)} %get-tuple-element.25) | copy-start | bytes 1548292
  37.7 23.5 %collective-permute-start.21 = (bf16[3,72,1792]{2,1,0:T(8,128)(2,1)S(1)}, bf16[3,72,1792]{2,1,0:T(8,128)(2,1)S(1)}, u32[]{:S(2)}, u32[]{:S(2)}) collective-permute-start(bf16[3,72,1792]{2,1,0:T(8,128)(2,1)S(1)} %constant_dynamic-slice_fusion.2), channel_id=1, source_target_pairs={{0,4},{4,0},{8,12},{12,8},{16,20},{20,16},{24,28},{28,24},{1,5},{5... | collective-permute-start | bytes 2322440 | tf_op jit(solution)/shard_map/ppermute | solution.py:37
  37.8 25.3 %collective-permute-start.15 = (bf16[3,72,1792]{2,1,0:T(8,128)(2,1)S(1)}, bf16[3,72,1792]{2,1,0:T(8,128)(2,1)S(1)}, u32[]{:S(2)}, u32[]{:S(2)}) collective-permute-start(bf16[3,72,1792]{2,1,0:T(8,128)(2,1)S(1)} %constant_dynamic-slice_fusion.5), channel_id=1, source_target_pairs={{0,4},{4,0},{8,12},{12,8},{16,20},{20,16},{24,28},{28,24},{1,5},{5... | collective-permute-start | bytes 2322440 | tf_op jit(solution)/shard_map/ppermute | solution.py:37
  39.7 6.3 %collective-permute-start.7 = (bf16[3,12,1792]{2,1,0:T(8,128)(2,1)S(1)}, bf16[3,12,1792]{2,1,0:T(8,128)(2,1)S(1)}, u32[]{:S(2)}, u32[]{:S(2)}) collective-permute-start(bf16[3,12,1792]{2,1,0:T(8,128)(2,1)S(1)} %constant_dynamic-slice_fusion.7), channel_id=1, source_target_pairs={{0,16},{4,20},{8,24},{12,28},{16,0},{20,4},{24,8},{28,12},{1,17},{... | collective-permute-start | bytes 387080 | tf_op jit(solution)/shard_map/ppermute | solution.py:37
  42.4 6.5 %collective-permute-start.1 = (bf16[3,12,1792]{2,1,0:T(8,128)(2,1)S(1)}, bf16[3,12,1792]{2,1,0:T(8,128)(2,1)S(1)}, u32[]{:S(2)}, u32[]{:S(2)}) collective-permute-start(bf16[3,12,1792]{2,1,0:T(8,128)(2,1)S(1)} %constant_dynamic-slice_fusion.10), channel_id=1, source_target_pairs={{0,8},{4,12},{8,0},{12,4},{16,24},{20,28},{24,16},{28,20},{1,9},{5... | collective-permute-start | bytes 387080 | tf_op jit(solution)/shard_map/ppermute | solution.py:37
  46.2 4.6 %collective-permute-start.8 = (bf16[3,6,1792]{2,1,0:T(8,128)(2,1)S(1)}, bf16[3,6,1792]{2,1,0:T(8,128)(2,1)S(1)}, u32[]{:S(2)}, u32[]{:S(2)}) collective-permute-start(bf16[3,6,1792]{2,1,0:T(8,128)(2,1)S(1)} %constant_dynamic-slice_fusion.6), channel_id=1, source_target_pairs={{0,8},{4,12},{8,0},{12,4},{16,24},{20,28},{24,16},{28,20},{1,9},{5... | collective-permute-start | bytes 193544 | tf_op jit(solution)/shard_map/ppermute | solution.py:37
  49.1 4.6 %collective-permute-start.2 = (bf16[3,6,1792]{2,1,0:T(8,128)(2,1)S(1)}, bf16[3,6,1792]{2,1,0:T(8,128)(2,1)S(1)}, u32[]{:S(2)}, u32[]{:S(2)}) collective-permute-start(bf16[3,6,1792]{2,1,0:T(8,128)(2,1)S(1)} %constant_dynamic-slice_fusion.9), channel_id=1, source_target_pairs={{0,16},{4,20},{8,24},{12,28},{16,0},{20,4},{24,8},{28,12},{1,17},{... | collective-permute-start | bytes 193544 | tf_op jit(solution)/shard_map/ppermute | solution.py:37
  50.9 4.6 %collective-permute-start.9 = (bf16[3,6,1792]{2,1,0:T(8,128)(2,1)S(1)}, bf16[3,6,1792]{2,1,0:T(8,128)(2,1)S(1)}, u32[]{:S(2)}, u32[]{:S(2)}) collective-permute-start(bf16[3,6,1792]{2,1,0:T(8,128)(2,1)S(1)} %pad_maximum_fusion.6), channel_id=1, source_target_pairs={{0,8},{4,12},{8,0},{12,4},{16,24},{20,28},{24,16},{28,20},{1,9},{5... | collective-permute-start | bytes 193544 | tf_op jit(solution)/shard_map/ppermute | solution.py:49
  53.7 4.8 %collective-permute-start.3 = (bf16[3,6,1792]{2,1,0:T(8,128)(2,1)S(1)}, bf16[3,6,1792]{2,1,0:T(8,128)(2,1)S(1)}, u32[]{:S(2)}, u32[]{:S(2)}) collective-permute-start(bf16[3,6,1792]{2,1,0:T(8,128)(2,1)S(1)} %pad_maximum_fusion.5), channel_id=1, source_target_pairs={{0,16},{4,20},{8,24},{12,28},{16,0},{20,4},{24,8},{28,12},{1,17},{... | collective-permute-start | bytes 193544 | tf_op jit(solution)/shard_map/ppermute | solution.py:49
  55.5 5.5 %collective-permute-start.10 = (bf16[3,12,1792]{2,1,0:T(8,128)(2,1)S(1)}, bf16[3,12,1792]{2,1,0:T(8,128)(2,1)S(1)}, u32[]{:S(2)}, u32[]{:S(2)}) collective-permute-start(bf16[3,12,1792]{2,1,0:T(8,128)(2,1)S(1)} %maximum_select_fusion.11), channel_id=1, source_target_pairs={{0,16},{4,20},{8,24},{12,28},{16,0},{20,4},{24,8},{28,12},{1,17},{... | collective-permute-start | bytes 387080 | tf_op jit(solution)/shard_map/ppermute | solution.py:49
  58.7 34.2 %collective-permute-start.4 = (bf16[3,12,1792]{2,1,0:T(8,128)(2,1)S(1)}, bf16[3,12,1792]{2,1,0:T(8,128)(2,1)S(1)}, u32[]{:S(2)}, u32[]{:S(2)}) collective-permute-start(bf16[3,12,1792]{2,1,0:T(8,128)(2,1)S(1)} %maximum_select_fusion.10), channel_id=1, source_target_pairs={{0,8},{4,12},{8,0},{12,4},{16,24},{20,28},{24,16},{28,20},{1,9},{5... | collective-permute-start | bytes 387080 | tf_op jit(solution)/shard_map/ppermute | solution.py:49
  61.1 41.3 %collective-permute-start.11 = (bf16[3,24,1792]{2,1,0:T(8,128)(2,1)S(1)}, bf16[3,24,1792]{2,1,0:T(8,128)(2,1)S(1)}, u32[]{:S(2)}, u32[]{:S(2)}) collective-permute-start(bf16[3,24,1792]{2,1,0:T(8,128)(2,1)S(1)} %maximum_select_fusion.9), channel_id=1, source_target_pairs={{0,4},{4,0},{8,12},{12,8},{16,20},{20,16},{24,28},{28,24},{1,5},{5... | collective-permute-start | bytes 774152 | tf_op jit(solution)/shard_map/ppermute | solution.py:49
  61.6 12.4 %collective-permute-start.22 = (bf16[3,36,1792]{2,1,0:T(8,128)(2,1)S(1)}, bf16[3,36,1792]{2,1,0:T(8,128)(2,1)S(1)}, u32[]{:S(2)}, u32[]{:S(2)}) collective-permute-start(bf16[3,36,1792]{2,1,0:T(8,128)(2,1)S(1)} %constant_dynamic-slice_fusion.1), channel_id=1, source_target_pairs={{0,16},{4,20},{8,24},{12,28},{16,0},{20,4},{24,8},{28,12},{1,17},{... | collective-permute-start | bytes 1161224 | tf_op jit(solution)/shard_map/ppermute | solution.py:37
  63.5 12.3 %collective-permute-start.16 = (bf16[3,36,1792]{2,1,0:T(8,128)(2,1)S(1)}, bf16[3,36,1792]{2,1,0:T(8,128)(2,1)S(1)}, u32[]{:S(2)}, u32[]{:S(2)}) collective-permute-start(bf16[3,36,1792]{2,1,0:T(8,128)(2,1)S(1)} %constant_dynamic-slice_fusion.4), channel_id=1, source_target_pairs={{0,8},{4,12},{8,0},{12,4},{16,24},{20,28},{24,16},{28,20},{1,9},{5... | collective-permute-start | bytes 1161224 | tf_op jit(solution)/shard_map/ppermute | solution.py:37
  74.2 7.8 %collective-permute-start.23 = (bf16[3,18,1792]{2,1,0:T(8,128)(2,1)S(1)}, bf16[3,18,1792]{2,1,0:T(8,128)(2,1)S(1)}, u32[]{:S(2)}, u32[]{:S(2)}) collective-permute-start(bf16[3,18,1792]{2,1,0:T(8,128)(2,1)S(1)} %constant_dynamic-slice_fusion), channel_id=1, source_target_pairs={{0,8},{4,12},{8,0},{12,4},{16,24},{20,28},{24,16},{28,20},{1,9},{5... | collective-permute-start | bytes 580616 | tf_op jit(solution)/shard_map/ppermute | solution.py:37
  76.0 8.0 %collective-permute-start.17 = (bf16[3,18,1792]{2,1,0:T(8,128)(2,1)S(1)}, bf16[3,18,1792]{2,1,0:T(8,128)(2,1)S(1)}, u32[]{:S(2)}, u32[]{:S(2)}) collective-permute-start(bf16[3,18,1792]{2,1,0:T(8,128)(2,1)S(1)} %constant_dynamic-slice_fusion.3), channel_id=1, source_target_pairs={{0,16},{4,20},{8,24},{12,28},{16,0},{20,4},{24,8},{28,12},{1,17},{... | collective-permute-start | bytes 580616 | tf_op jit(solution)/shard_map/ppermute | solution.py:37
  82.3 7.1 %collective-permute-start.24 = (bf16[3,18,1792]{2,1,0:T(8,128)(2,1)S(1)}, bf16[3,18,1792]{2,1,0:T(8,128)(2,1)S(1)}, u32[]{:S(2)}, u32[]{:S(2)}) collective-permute-start(bf16[3,18,1792]{2,1,0:T(8,128)(2,1)S(1)} %pad_maximum_fusion.4), channel_id=1, source_target_pairs={{0,8},{4,12},{8,0},{12,4},{16,24},{20,28},{24,16},{28,20},{1,9},{5... | collective-permute-start | bytes 580616 | tf_op jit(solution)/shard_map/ppermute | solution.py:49
  84.2 7.4 %collective-permute-start.18 = (bf16[3,18,1792]{2,1,0:T(8,128)(2,1)S(1)}, bf16[3,18,1792]{2,1,0:T(8,128)(2,1)S(1)}, u32[]{:S(2)}, u32[]{:S(2)}) collective-permute-start(bf16[3,18,1792]{2,1,0:T(8,128)(2,1)S(1)} %pad_maximum_fusion.3), channel_id=1, source_target_pairs={{0,16},{4,20},{8,24},{12,28},{16,0},{20,4},{24,8},{28,12},{1,17},{... | collective-permute-start | bytes 580616 | tf_op jit(solution)/shard_map/ppermute | solution.py:49
  89.6 10.6 %collective-permute-start.25 = (bf16[3,36,1792]{2,1,0:T(8,128)(2,1)S(1)}, bf16[3,36,1792]{2,1,0:T(8,128)(2,1)S(1)}, u32[]{:S(2)}, u32[]{:S(2)}) collective-permute-start(bf16[3,36,1792]{2,1,0:T(8,128)(2,1)S(1)} %maximum_select_fusion.7), channel_id=1, source_target_pairs={{0,16},{4,20},{8,24},{12,28},{16,0},{20,4},{24,8},{28,12},{1,17},{... | collective-permute-start | bytes 1161224 | tf_op jit(solution)/shard_map/ppermute | solution.py:49
  91.9 9.0 %collective-permute-start.19 = (bf16[3,36,1792]{2,1,0:T(8,128)(2,1)S(1)}, bf16[3,36,1792]{2,1,0:T(8,128)(2,1)S(1)}, u32[]{:S(2)}, u32[]{:S(2)}) collective-permute-start(bf16[3,36,1792]{2,1,0:T(8,128)(2,1)S(1)} %maximum_select_fusion.6), channel_id=1, source_target_pairs={{0,8},{4,12},{8,0},{12,4},{16,24},{20,28},{24,16},{28,20},{1,9},{5... | collective-permute-start | bytes 1161224 | tf_op jit(solution)/shard_map/ppermute | solution.py:49
  93.0 9.5 %collective-permute-start.5 = (bf16[3,24,1792]{2,1,0:T(8,128)(2,1)S(1)}, bf16[3,24,1792]{2,1,0:T(8,128)(2,1)S(1)}, u32[]{:S(2)}, u32[]{:S(2)}) collective-permute-start(bf16[3,24,1792]{2,1,0:T(8,128)(2,1)S(1)} %maximum_select_fusion.8), channel_id=1, source_target_pairs={{0,4},{4,0},{8,12},{12,8},{16,20},{20,16},{24,28},{28,24},{1,5},{5... | collective-permute-start | bytes 774152 | tf_op jit(solution)/shard_map/ppermute | solution.py:49
  100.4 2.3 %collective-permute-start.26 = (bf16[3,72,1792]{2,1,0:T(8,128)(2,1)S(1)}, bf16[3,72,1792]{2,1,0:T(8,128)(2,1)S(1)}, u32[]{:S(2)}, u32[]{:S(2)}) collective-permute-start(bf16[3,72,1792]{2,1,0:T(8,128)(2,1)S(1)} %maximum_select_fusion.3), channel_id=1, source_target_pairs={{0,4},{4,0},{8,12},{12,8},{16,20},{20,16},{24,28},{28,24},{1,5},{5... | collective-permute-start | bytes 2322440 | tf_op jit(solution)/shard_map/ppermute | solution.py:49
  101.1 2.7 %collective-permute-start.20 = (bf16[3,72,1792]{2,1,0:T(8,128)(2,1)S(1)}, bf16[3,72,1792]{2,1,0:T(8,128)(2,1)S(1)}, u32[]{:S(2)}, u32[]{:S(2)}) collective-permute-start(bf16[3,72,1792]{2,1,0:T(8,128)(2,1)S(1)} %maximum_select_fusion.2), channel_id=1, source_target_pairs={{0,4},{4,0},{8,12},{12,8},{16,20},{20,16},{24,28},{28,24},{1,5},{5... | collective-permute-start | bytes 2322440 | tf_op jit(solution)/shard_map/ppermute | solution.py:49
  102.8 4.6 %slice-start.2 = ((s8[7340032]{0:T(1024)(128)(4,1)}), s8[4194304]{0:T(1024)(128)(4,1)S(1)}, s32[]{:S(2)}) async-start(s8[7340032]{0:T(1024)(128)(4,1)} %bitcast.36), calls=%async_computation.2 | async-start | bytes 8388608
  104.4 3.0 %slice-start.3 = ((s8[7340032]{0:T(1024)(128)(4,1)}), s8[3145728]{0:T(1024)(128)(4,1)S(1)}, s32[]{:S(2)}) async-start(s8[7340032]{0:T(1024)(128)(4,1)} %bitcast.36), calls=%async_computation.3 | async-start | bytes 6291456
  117.9 14.3 %collective-permute-start.27 = (bf16[48,1024]{1,0:T(8,128)(2,1)S(1)}, bf16[48,1024]{1,0:T(8,128)(2,1)S(1)}, u32[]{:S(2)}, u32[]{:S(2)}) collective-permute-start(bf16[48,1024]{1,0:T(8,128)(2,1)S(1)} %get-tuple-element.33), channel_id=1, source_target_pairs={{0,3},{1,0},{2,1},{3,2},{4,7},{5,4},{6,5},{7,6},{8,11},{9,8},{10,9... | collective-permute-start | bytes 294920 | tf_op jit(solution)/shard_map/ppermute | solution.py:95
  120.8 11.5 %collective-permute-start.29 = (bf16[48,1024]{1,0:T(8,128)(2,1)S(1)}, bf16[48,1024]{1,0:T(8,128)(2,1)S(1)}, u32[]{:S(2)}, u32[]{:S(2)}) collective-permute-start(bf16[48,1024]{1,0:T(8,128)(2,1)S(1)} %get-tuple-element.34), channel_id=1, source_target_pairs={{0,1},{1,2},{2,3},{3,0},{4,5},{5,6},{6,7},{7,4},{8,9},{9,10},{10,1... | collective-permute-start | bytes 294920 | tf_op jit(solution)/shard_map/ppermute | solution.py:95
  120.8 11.5 %collective-permute-start.28 = (bf16[48,1024]{1,0:T(8,128)(2,1)S(1)}, bf16[48,1024]{1,0:T(8,128)(2,1)S(1)}, u32[]{:S(2)}, u32[]{:S(2)}) collective-permute-start(bf16[48,1024]{1,0:T(8,128)(2,1)S(1)} %get-tuple-element.35), channel_id=1, source_target_pairs={{0,2},{1,3},{2,0},{3,1},{4,6},{5,7},{6,4},{7,5},{8,10},{9,11},{10,... | collective-permute-start | bytes 294920 | tf_op jit(solution)/shard_map/ppermute | solution.py:95

commit v10 on v6

--- a/solution.py
+++ b/solution.py
@@ -52,7 +52,7 @@
 
 
 def row_bits(n_dev, tokens, units):
-    if n_dev < 2 or n_dev & (n_dev - 1) or tokens % n_dev or units % 2:
+    if n_dev < 2 or n_dev & (n_dev - 1) or tokens % n_dev or units % N_PARTS:
         return None
     bits, b = [], 1
     while b < n_dev:
@@ -67,11 +67,14 @@
     if bits is None:
         sums = lax.psum(stacked, "row").astype(jnp.float32)
         return jnp.stack(gated_grads(sums[0], sums[1], sums[2]))
-    orders = (bits, bits[:1] + bits[:0:-1])
-    half = units // 2
-    reduced = [halving_reduce(stacked[:, :, h * half:(h + 1) * half], o, n_dev) for h, o in enumerate(orders)]
+    orders = (bits, bits[:1] + bits[:0:-1]) * (N_PARTS // 2)
+    span = units // len(orders)
+    reduced = [halving_reduce(stacked[:, :, h * span:(h + 1) * span], o, n_dev) for h, o in enumerate(orders)]
     outs = [doubling_gather(jnp.stack(gated_grads(red[0], red[1], red[2])), o, n_dev) for red, o in zip(reduced, orders)]
     return jnp.concatenate(outs, axis=2)
+
+
+N_PARTS = 4
 
 
 def col_gather(x, n_col):

time: 112 us -> 113 us (level)
  waiting for transfers between devices: 34.7 us -> 25.9 us
  starting transfers between devices: 31.7 us -> 39.3 us
  other arithmetic: 7.94 us -> 9.71 us
    ppermute x6 -> x12, waiting for transfers between devices: 16.1 us -> 9.09 us  [halving_reduce(): got = lax.ppermute(send, 'row', [(j, j ^ bit) for j in range(n_dev)])]
    ppermute x6 -> x12, starting transfers between devices: 6.67 us -> 11.5 us  [halving_reduce(): got = lax.ppermute(send, 'row', [(j, j ^ bit) for j in range(n_dev)])]
    ppermute x6 -> x12, starting transfers between devices: 5.81 us -> 8.67 us  [doubling_gather(): got = lax.ppermute(cur, 'row', [(j, j ^ bit) for j in range(n_dev)])]
    select_n x6 -> x12, other arithmetic: 3.52 us -> 5.64 us  [doubling_gather(): jnp.where(hi == 1, jnp.concatenate([got, cur], axis=1), jnp.concatenate([...]
    ppermute x6 -> x12, waiting for transfers between devices: 16.2 us -> 14.4 us  [doubling_gather(): got = lax.ppermute(cur, 'row', [(j, j ^ bit) for j in range(n_dev)])]
    dynamic_slice x6 -> x12, local copies, waits for them, and re-layouts: 2.31 us -> 1.16 us  [halving_reduce(): send = lax.dynamic_slice_in_dim(cur, (1 - hi) * n, n, 1)]
    unnamed x26 -> x28, local copies, waits for them, and re-layouts: 3.68 us -> 4.61 us
    convert_element_type x4 -> x8, other arithmetic: 2.28 us -> 1.87 us  [halving_reduce(): cur = cur.astype(jnp.bfloat16)]
  transfers between devices with their start and end apart: 21 -> 33, of which waited for: 10 -> 14; matrix products, arithmetic and copies ran while one was open for 22% -> 23% of each run, Pallas kernels for 0% -> 0%
where the time goes in v10:
time: 113 us; the launch traced here: 112 us
  starting transfers between devices  39.3 us (35%)
  matrix products  29.6 us (26%)
  waiting for transfers between devices  25.9 us (23%)
  other arithmetic  9.71 us (9%)
  local copies, waits for them, and re-layouts  6.67 us (6%)
  between operations  1.21 us (1%)
    ppermute x12, waiting for transfers between devices, doubling_gather(): got = lax.ppermute(cur, 'row', [(j, j ^ bit) for j in range(n_dev)])  14.4 us
    ppermute x12, starting transfers between devices, halving_reduce(): got = lax.ppermute(send, 'row', [(j, j ^ bit) for j in range(n_dev)])  11.5 us
    ppermute x6, starting transfers between devices, col_gather(): lax.ppermute(x, 'col', [(j, (j + s) % n_col) for j in range(n_col)])  10.4 us
    ppermute x12, waiting for transfers between devices, halving_reduce(): got = lax.ppermute(send, 'row', [(j, j ^ bit) for j in range(n_dev)])  9.09 us
    ppermute x3, starting transfers between devices, col_reduce_scatter(): lax.ppermute(x[s * span:(s + 1) * span], 'col', [(j, (j - s) % n_col) for...  8.85 us
    ppermute x12, starting transfers between devices, doubling_gather(): got = lax.ppermute(cur, 'row', [(j, j ^ bit) for j in range(n_dev)])  8.67 us
    dot_general x3, matrix products, contract_last(): lax.dot_general(left, right, (((1,), (1,)), ((), ())), preferred_element_...  7.58 us
    select_n x12, other arithmetic, doubling_gather(): jnp.where(hi == 1, jnp.concatenate([got, cur], axis=1), jnp.concatenate([...  5.64 us
  transfers between devices with their start and end apart: 33, of which 14 were waited for; matrix products, arithmetic and copies ran while one was open for 23% of the time, Pallas kernels for 0%

profile of v10, /device:TPU:0, one launch (start us, length us, event | category | flops | bytes accessed | tf_op | source)
XLA Modules:
  0.0 112.5 jit_solution(17191687807213889674)
XLA Ops:
  0.6 4.1 %collective-permute-start.1 = (bf16[48,1024]{1,0:T(8,128)(2,1)}, bf16[48,1024]{1,0:T(8,128)(2,1)S(1)}, u32[]{:S(2)}, u32[]{:S(2)}) collective-permute-start(bf16[48,1024]{1,0:T(8,128)(2,1)} %param.5), channel_id=1, source_target_pairs={{0,2},{1,3},{2,0},{3,1},{4,6},{5,7},{6,4},{7,5},{8,10},{9,11},{10,... | collective-permute-start | bytes 294920 | tf_op jit(solution)/shard_map/ppermute | solution.py:83
  4.8 1.6 %collective-permute-start = (bf16[48,1024]{1,0:T(8,128)(2,1)}, bf16[48,1024]{1,0:T(8,128)(2,1)S(1)}, u32[]{:S(2)}, u32[]{:S(2)}) collective-permute-start(bf16[48,1024]{1,0:T(8,128)(2,1)} %param.5), channel_id=1, source_target_pairs={{0,1},{1,2},{2,3},{3,0},{4,5},{5,6},{6,7},{7,4},{8,9},{9,10},{10,1... | collective-permute-start | bytes 294920 | tf_op jit(solution)/shard_map/ppermute | solution.py:83
  6.3 2.2 %collective-permute-start.2 = (bf16[48,1024]{1,0:T(8,128)(2,1)}, bf16[48,1024]{1,0:T(8,128)(2,1)S(1)}, u32[]{:S(2)}, u32[]{:S(2)}) collective-permute-start(bf16[48,1024]{1,0:T(8,128)(2,1)} %param.5), channel_id=1, source_target_pairs={{0,3},{1,0},{2,1},{3,2},{4,7},{5,4},{6,5},{7,6},{8,11},{9,8},{10,9... | collective-permute-start | bytes 294920 | tf_op jit(solution)/shard_map/ppermute | solution.py:83
  8.6 0.6 collective-permute-start.3
  9.2 0.9 constant_dynamic-update-slice_fusion.3
  10.1 0.9 constant_dynamic-update-slice_fusion.7
  11.0 1.5 %collective-permute-done = bf16[48,1024]{1,0:T(8,128)(2,1)S(1)} collective-permute-done((bf16[48,1024]{1,0:T(8,128)(2,1)}, bf16[48,1024]{1,0:T(8,128)(2,1)S(1)}, u32[]{:S(2)}, u32[]{:S(2)}) %collective-permute-start) | collective-permute-done | bytes 98336 | tf_op jit(solution)/shard_map/ppermute | solution.py:83
  12.4 1.8 %collective-permute-start.5 = (bf16[48,1024]{1,0:T(8,128)(2,1)}, bf16[48,1024]{1,0:T(8,128)(2,1)S(1)}, u32[]{:S(2)}, u32[]{:S(2)}) collective-permute-start(bf16[48,1024]{1,0:T(8,128)(2,1)} %param.6), channel_id=1, source_target_pairs={{0,3},{1,0},{2,1},{3,2},{4,7},{5,4},{6,5},{7,6},{8,11},{9,8},{10,9... | collective-permute-start | bytes 294920 | tf_op jit(solution)/shard_map/ppermute | solution.py:83
  14.4 4.8 %fusion.1 = bf16[1,192,3584]{2,1,0:T(8,128)(2,1)S(1)} fusion(bf16[192,1024]{1,0:T(8,128)(2,1)S(1)} %constant_dynamic-update-slice_fusion, bf16[1024,3584]{1,0:T(8,128)(2,1)} %param.8), kind=kOutput, calls=%fused_computation.7 | convolution fusion | flops 1409974272 | bytes 9109504 | tf_op jit(solution)/shard_map/dot_general | solution.py:105
  19.2 0.3 copy-done.4
  19.5 1.7 %fusion = bf16[1,192,3584]{2,1,0:T(8,128)(2,1)S(1)} fusion(bf16[192,1024]{1,0:T(8,128)(2,1)S(1)} %constant_dynamic-update-slice_fusion, bf16[1024,3584]{1,0:T(8,128)(2,1)S(1)} %copy-done.4), kind=kOutput, calls=%fused_computation.6 | convolution fusion | flops 1409974272 | bytes 9109504 | tf_op jit(solution)/shard_map/dot_general | solution.py:104
  21.2 0.9 collective-permute-done.5
  22.2 2.6 %fusion.2 = bf16[1,192,3584]{2,1,0:T(8,128)(2,1)S(1)} fusion(bf16[192,1024]{1,0:T(8,128)(2,1)S(1)} %constant_dynamic-update-slice_fusion.4, bf16[3584,1024]{1,0:T(8,128)(2,1)S(1)} %bitcast.29), kind=kOutput, calls=%fused_computation.8 | convolution fusion | flops 1409974272 | bytes 9109504 | tf_op jit(solution)/shard_map/dot_general | solution.py:14
  24.7 0.7 pad_maximum_fusion
  25.4 0.6 fusion.5
  26.0 1.0 copy-done
  27.0 0.8 constant_dynamic-slice_fusion.8
  27.9 0.6 collective-permute-start.18
  28.6 0.5 collective-permute-start.6
  29.2 0.9 collective-permute-done.12
  30.1 1.2 %add_convert_fusion.2 = bf16[3,96,896]{2,1,0:T(8,128)(2,1)S(1)} fusion(bf16[3,96,896]{2,1,0:T(8,128)(2,1)} %collective-permute-done.12, bf16[3,192,896]{2,1,0:T(8,128)(2,1)S(1)} %copy-done.1, s32[]{:T(128)S(6)} %select_n.202), kind=kLoop, calls=%fused_computation.22 | loop fusion | flops 1032192 | bytes 1548292 | tf_op jit(solution)/shard_map/convert_element_type | solution.py:40
  31.3 1.5 %collective-permute-start.13 = (bf16[3,48,896]{2,1,0:T(8,128)(2,1)S(1)}, bf16[3,48,896]{2,1,0:T(8,128)(2,1)S(1)}, u32[]{:S(2)}, u32[]{:S(2)}) collective-permute-start(bf16[3,48,896]{2,1,0:T(8,128)(2,1)S(1)} %constant_dynamic-slice_fusion.7), channel_id=1, source_target_pairs={{0,16},{4,20},{8,24},{12,28},{16,0},{20,4},{24,8},{28,12},{1,17},{... | collective-permute-start | bytes 774152 | tf_op jit(solution)/shard_map/ppermute | solution.py:37
  32.8 0.1 add_convert_fusion.1
  33.0 1.6 %collective-permute-start.19 = (bf16[3,48,896]{2,1,0:T(8,128)(2,1)S(1)}, bf16[3,48,896]{2,1,0:T(8,128)(2,1)S(1)}, u32[]{:S(2)}, u32[]{:S(2)}) collective-permute-start(bf16[3,48,896]{2,1,0:T(8,128)(2,1)S(1)} %constant_dynamic-slice_fusion.4), channel_id=1, source_target_pairs={{0,8},{4,12},{8,0},{12,4},{16,24},{20,28},{24,16},{28,20},{1,9},{5... | collective-permute-start | bytes 774152 | tf_op jit(solution)/shard_map/ppermute | solution.py:37
  34.6 0.1 add_convert_fusion
  34.7 0.6 collective-permute-start.25
  35.3 0.1 add_convert_fusion.3
  35.5 0.7 collective-permute-start.7
  36.2 4.3 %collective-permute-done.13 = bf16[3,48,896]{2,1,0:T(8,128)(2,1)S(1)} collective-permute-done((bf16[3,48,896]{2,1,0:T(8,128)(2,1)S(1)}, bf16[3,48,896]{2,1,0:T(8,128)(2,1)S(1)}, u32[]{:S(2)}, u32[]{:S(2)}) %collective-permute-start.13) | collective-permute-done | bytes 258080 | tf_op jit(solution)/shard_map/ppermute | solution.py:37
  40.5 1.5 %collective-permute-start.14 = (bf16[3,24,896]{2,1,0:T(8,128)(2,1)S(1)}, bf16[3,24,896]{2,1,0:T(8,128)(2,1)S(1)}, u32[]{:S(2)}, u32[]{:S(2)}) collective-permute-start(bf16[3,24,896]{2,1,0:T(8,128)(2,1)S(1)} %constant_dynamic-slice_fusion.6), channel_id=1, source_target_pairs={{0,8},{4,12},{8,0},{12,4},{16,24},{20,28},{24,16},{28,20},{1,9},{5... | collective-permute-start | bytes 387080 | tf_op jit(solution)/shard_map/ppermute | solution.py:37
  42.3 1.5 %collective-permute-start.20 = (bf16[3,24,896]{2,1,0:T(8,128)(2,1)S(1)}, bf16[3,24,896]{2,1,0:T(8,128)(2,1)S(1)}, u32[]{:S(2)}, u32[]{:S(2)}) collective-permute-start(bf16[3,24,896]{2,1,0:T(8,128)(2,1)S(1)} %constant_dynamic-slice_fusion.3), channel_id=1, source_target_pairs={{0,16},{4,20},{8,24},{12,28},{16,0},{20,4},{24,8},{28,12},{1,17},{... | collective-permute-start | bytes 387080 | tf_op jit(solution)/shard_map/ppermute | solution.py:37
  43.7 2.2 %collective-permute-done.25 = bf16[3,48,896]{2,1,0:T(8,128)(2,1)S(1)} collective-permute-done((bf16[3,48,896]{2,1,0:T(8,128)(2,1)S(1)}, bf16[3,48,896]{2,1,0:T(8,128)(2,1)S(1)}, u32[]{:S(2)}, u32[]{:S(2)}) %collective-permute-start.25) | collective-permute-done | bytes 258080 | tf_op jit(solution)/shard_map/ppermute | solution.py:37
  46.1 1.5 %collective-permute-start.26 = (bf16[3,24,896]{2,1,0:T(8,128)(2,1)S(1)}, bf16[3,24,896]{2,1,0:T(8,128)(2,1)S(1)}, u32[]{:S(2)}, u32[]{:S(2)}) collective-permute-start(bf16[3,24,896]{2,1,0:T(8,128)(2,1)S(1)} %constant_dynamic-slice_fusion), channel_id=1, source_target_pairs={{0,8},{4,12},{8,0},{12,4},{16,24},{20,28},{24,16},{28,20},{1,9},{5... | collective-permute-start | bytes 387080 | tf_op jit(solution)/shard_map/ppermute | solution.py:37
  47.8 1.5 %collective-permute-start.8 = (bf16[3,24,896]{2,1,0:T(8,128)(2,1)S(1)}, bf16[3,24,896]{2,1,0:T(8,128)(2,1)S(1)}, u32[]{:S(2)}, u32[]{:S(2)}) collective-permute-start(bf16[3,24,896]{2,1,0:T(8,128)(2,1)S(1)} %constant_dynamic-slice_fusion.9), channel_id=1, source_target_pairs={{0,16},{4,20},{8,24},{12,28},{16,0},{20,4},{24,8},{28,12},{1,17},{... | collective-permute-start | bytes 387080 | tf_op jit(solution)/shard_map/ppermute | solution.py:37
  49.3 1.2 %collective-permute-done.14 = bf16[3,24,896]{2,1,0:T(8,128)(2,1)S(1)} collective-permute-done((bf16[3,24,896]{2,1,0:T(8,128)(2,1)S(1)}, bf16[3,24,896]{2,1,0:T(8,128)(2,1)S(1)}, u32[]{:S(2)}, u32[]{:S(2)}) %collective-permute-start.14) | collective-permute-done | bytes 129056 | tf_op jit(solution)/shard_map/ppermute | solution.py:37
  50.6 1.6 %collective-permute-start.15 = (bf16[3,24,896]{2,1,0:T(8,128)(2,1)S(1)}, bf16[3,24,896]{2,1,0:T(8,128)(2,1)S(1)}, u32[]{:S(2)}, u32[]{:S(2)}) collective-permute-start(bf16[3,24,896]{2,1,0:T(8,128)(2,1)S(1)} %pad_maximum_fusion.3), channel_id=1, source_target_pairs={{0,8},{4,12},{8,0},{12,4},{16,24},{20,28},{24,16},{28,20},{1,9},{5... | collective-permute-start | bytes 387080 | tf_op jit(solution)/shard_map/ppermute | solution.py:49
  52.3 0.6 collective-permute-start.21
  52.8 0.3 collective-permute-done.26
  53.2 1.6 %collective-permute-start.27 = (bf16[3,24,896]{2,1,0:T(8,128)(2,1)S(1)}, bf16[3,24,896]{2,1,0:T(8,128)(2,1)S(1)}, u32[]{:S(2)}, u32[]{:S(2)}) collective-permute-start(bf16[3,24,896]{2,1,0:T(8,128)(2,1)S(1)} %pad_maximum_fusion.5), channel_id=1, source_target_pairs={{0,8},{4,12},{8,0},{12,4},{16,24},{20,28},{24,16},{28,20},{1,9},{5... | collective-permute-start | bytes 387080 | tf_op jit(solution)/shard_map/ppermute | solution.py:49
  54.9 1.8 %collective-permute-done.15 = bf16[3,24,896]{2,1,0:T(8,128)(2,1)S(1)} collective-permute-done((bf16[3,24,896]{2,1,0:T(8,128)(2,1)S(1)}, bf16[3,24,896]{2,1,0:T(8,128)(2,1)S(1)}, u32[]{:S(2)}, u32[]{:S(2)}) %collective-permute-start.15) | collective-permute-done | bytes 129056 | tf_op jit(solution)/shard_map/ppermute | solution.py:49
  56.7 0.6 collective-permute-start.16
  57.4 1.5 %collective-permute-start.9 = (bf16[3,24,896]{2,1,0:T(8,128)(2,1)S(1)}, bf16[3,24,896]{2,1,0:T(8,128)(2,1)S(1)}, u32[]{:S(2)}, u32[]{:S(2)}) collective-permute-start(bf16[3,24,896]{2,1,0:T(8,128)(2,1)S(1)} %pad_maximum_fusion.2), channel_id=1, source_target_pairs={{0,16},{4,20},{8,24},{12,28},{16,0},{20,4},{24,8},{28,12},{1,17},{... | collective-permute-start | bytes 387080 | tf_op jit(solution)/shard_map/ppermute | solution.py:49
  59.0 1.6 %collective-permute-start.22 = (bf16[3,48,896]{2,1,0:T(8,128)(2,1)S(1)}, bf16[3,48,896]{2,1,0:T(8,128)(2,1)S(1)}, u32[]{:S(2)}, u32[]{:S(2)}) collective-permute-start(bf16[3,48,896]{2,1,0:T(8,128)(2,1)S(1)} %maximum_select_fusion.10), channel_id=1, source_target_pairs={{0,8},{4,12},{8,0},{12,4},{16,24},{20,28},{24,16},{28,20},{1,9},{5... | collective-permute-start | bytes 774152 | tf_op jit(solution)/shard_map/ppermute | solution.py:49
  60.6 0.4 collective-permute-start.28
  61.0 4.9 %collective-permute-done.16 = bf16[3,48,896]{2,1,0:T(8,128)(2,1)S(1)} collective-permute-done((bf16[3,48,896]{2,1,0:T(8,128)(2,1)S(1)}, bf16[3,48,896]{2,1,0:T(8,128)(2,1)S(1)}, u32[]{:S(2)}, u32[]{:S(2)}) %collective-permute-start.16) | collective-permute-done | bytes 258080 | tf_op jit(solution)/shard_map/ppermute | solution.py:49
  66.1 2.2 %collective-permute-done.9 = bf16[3,24,896]{2,1,0:T(8,128)(2,1)S(1)} collective-permute-done((bf16[3,24,896]{2,1,0:T(8,128)(2,1)S(1)}, bf16[3,24,896]{2,1,0:T(8,128)(2,1)S(1)}, u32[]{:S(2)}, u32[]{:S(2)}) %collective-permute-start.9) | collective-permute-done | bytes 129056 | tf_op jit(solution)/shard_map/ppermute | solution.py:49
  68.4 0.6 collective-permute-start.10
  69.2 1.9 %collective-permute-done.28 = bf16[3,48,896]{2,1,0:T(8,128)(2,1)S(1)} collective-permute-done((bf16[3,48,896]{2,1,0:T(8,128)(2,1)S(1)}, bf16[3,48,896]{2,1,0:T(8,128)(2,1)S(1)}, u32[]{:S(2)}, u32[]{:S(2)}) %collective-permute-start.28) | collective-permute-done | bytes 258080 | tf_op jit(solution)/shard_map/ppermute | solution.py:49
  71.3 3.5 %collective-permute-done.10 = bf16[3,48,896]{2,1,0:T(8,128)(2,1)S(1)} collective-permute-done((bf16[3,48,896]{2,1,0:T(8,128)(2,1)S(1)}, bf16[3,48,896]{2,1,0:T(8,128)(2,1)S(1)}, u32[]{:S(2)}, u32[]{:S(2)}) %collective-permute-start.10) | collective-permute-done | bytes 258080 | tf_op jit(solution)/shard_map/ppermute | solution.py:49
  75.1 0.4 maximum_select_fusion.1
  75.5 1.6 %maximum_select_fusion.2 = bf16[3,192,896]{2,1,0:T(8,128)(2,1)S(1)} fusion(bf16[3,96,896]{2,1,0:T(8,128)(2,1)S(1)} %maximum_select_fusion.6, bf16[3,96,896]{2,1,0:T(8,128)(2,1)} %collective-permute-done.23, pred[]{:T(512)S(6)} %eq.43), kind=kLoop, calls=%fused_computation.18 | loop fusion | flops 4644864 | bytes 2064385 | tf_op jit(solution)/shard_map/jit(_where)/select_n | solution.py:50
  77.1 1.5 %maximum_select_fusion.3 = bf16[3,192,896]{2,1,0:T(8,128)(2,1)S(1)} fusion(bf16[3,96,896]{2,1,0:T(8,128)(2,1)S(1)} %maximum_select_fusion.7, bf16[3,96,896]{2,1,0:T(8,128)(2,1)} %collective-permute-done.29, pred[]{:T(512)S(6)} %eq.43), kind=kLoop, calls=%fused_computation.19 | loop fusion | flops 4644864 | bytes 2064385 | tf_op jit(solution)/shard_map/jit(_where)/select_n | solution.py:50
  78.6 1.5 %maximum_select_fusion = bf16[3,192,896]{2,1,0:T(8,128)(2,1)S(1)} fusion(bf16[3,96,896]{2,1,0:T(8,128)(2,1)S(1)} %maximum_select_fusion.4, bf16[3,96,896]{2,1,0:T(8,128)(2,1)} %collective-permute-done.11, pred[]{:T(512)S(6)} %eq.43), kind=kLoop, calls=%fused_computation.16 | loop fusion | flops 4644864 | bytes 2064385 | tf_op jit(solution)/shard_map/jit(_where)/select_n | solution.py:50
  80.1 0.4 pad_maximum_fusion.1
  80.5 1.5 %slice-done.3 = s8[3145728]{0:T(1024)(128)(4,1)S(1)} async-done(((s8[7340032]{0:T(1024)(128)(4,1)}), s8[3145728]{0:T(1024)(128)(4,1)S(1)}, s32[]{:S(2)}) %slice-start.3) | async-done | bytes 3145752
  82.0 2.5 %fusion.4 = f32[192,1024]{1,0:T(8,128)S(1)} fusion(bf16[1024,3584]{1,0:T(8,128)(2,1)S(1)} %bitcast.31, bf16[3,192,3584]{2,1,0:T(8,128)(2,1)S(1)} %pad_maximum_fusion.1), kind=kOutput, calls=%fused_computation.81 | convolution fusion | flops 1409286144 | bytes 9502720 | tf_op jit(solution)/shard_map/dot_general | solution.py:14
  84.5 0.3 slice_bitcast_fusion
  84.8 2.5 %fusion.3 = bf16[192,1024]{1,0:T(8,128)(2,1)S(1)} fusion(f32[192,1024]{1,0:T(8,128)S(1)} %fusion.4, bf16[1024,3584]{1,0:T(8,128)(2,1)S(1)} %bitcast.33, bf16[3,192,3584]{2,1,0:T(8,128)(2,1)S(1)} %pad_maximum_fusion.1), kind=kOutput, calls=%fused_computation.15 | convolution fusion | flops 1409679360 | bytes 9895936 | tf_op jit(solution)/shard_map/dot_general | solution.py:14
  87.3 5.2 %convolution_convert_fusion.2 = bf16[1024,3584]{1,0:T(8,128)(2,1)} fusion(bf16[192,1024]{1,0:T(8,128)(2,1)S(1)} %constant_dynamic-update-slice_fusion, bf16[192,3584]{1,0:T(8,128)(2,1)S(1)} %get-tuple-element.13), kind=kOutput, calls=%fused_computation.2 | convolution fusion | flops 1412956160 | bytes 9109504 | tf_op jit(solution)/shard_map/dot_general | solution.py:115
  92.5 8.0 %collective-permute-start.30 = (bf16[48,1024]{1,0:T(8,128)(2,1)S(1)}, bf16[48,1024]{1,0:T(8,128)(2,1)S(1)}, u32[]{:S(2)}, u32[]{:S(2)}) collective-permute-start(bf16[48,1024]{1,0:T(8,128)(2,1)S(1)} %get-tuple-element.27), channel_id=1, source_target_pairs={{0,3},{1,0},{2,1},{3,2},{4,7},{5,4},{6,5},{7,6},{8,11},{9,8},{10,9... | collective-permute-start | bytes 294920 | tf_op jit(solution)/shard_map/ppermute | solution.py:91
  100.5 0.8 collective-permute-start.31
  101.4 5.2 %convolution_convert_fusion.1 = bf16[1024,3584]{1,0:T(8,128)(2,1)} fusion(bf16[192,1024]{1,0:T(8,128)(2,1)S(1)} %constant_dynamic-update-slice_fusion, bf16[192,3584]{1,0:T(8,128)(2,1)S(1)} %get-tuple-element.18), kind=kOutput, calls=%fused_computation.1 | convolution fusion | flops 1412956160 | bytes 9109504 | tf_op jit(solution)/shard_map/dot_general | solution.py:118
  106.6 5.2 %convolution_convert_fusion = bf16[3584,1024]{1,0:T(8,128)(2,1)} fusion(bf16[192,3584]{1,0:T(8,128)(2,1)S(1)} %get-tuple-element.19, bf16[192,1024]{1,0:T(8,128)(2,1)S(1)} %copy-done.3), kind=kOutput, calls=%fused_computation | convolution fusion | flops 1412956160 | bytes 9109504 | tf_op jit(solution)/shard_map/dot_general | solution.py:8
  111.8 0.7 add_convert_fusion.8
  (93 shorter events, 2.5 us)
Async XLA Ops:
  0.6 13.7 %collective-permute-start.1 = (bf16[48,1024]{1,0:T(8,128)(2,1)}, bf16[48,1024]{1,0:T(8,128)(2,1)S(1)}, u32[]{:S(2)}, u32[]{:S(2)}) collective-permute-start(bf16[48,1024]{1,0:T(8,128)(2,1)} %param.5), channel_id=1, source_target_pairs={{0,2},{1,3},{2,0},{3,1},{4,6},{5,7},{6,4},{7,5},{8,10},{9,11},{10,... | collective-permute-start | bytes 294920 | tf_op jit(solution)/shard_map/ppermute | solution.py:83
  4.8 7.7 %collective-permute-start = (bf16[48,1024]{1,0:T(8,128)(2,1)}, bf16[48,1024]{1,0:T(8,128)(2,1)S(1)}, u32[]{:S(2)}, u32[]{:S(2)}) collective-permute-start(bf16[48,1024]{1,0:T(8,128)(2,1)} %param.5), channel_id=1, source_target_pairs={{0,1},{1,2},{2,3},{3,0},{4,5},{5,6},{6,7},{7,4},{8,9},{9,10},{10,1... | collective-permute-start | bytes 294920 | tf_op jit(solution)/shard_map/ppermute | solution.py:83
  6.3 8.0 %collective-permute-start.2 = (bf16[48,1024]{1,0:T(8,128)(2,1)}, bf16[48,1024]{1,0:T(8,128)(2,1)S(1)}, u32[]{:S(2)}, u32[]{:S(2)}) collective-permute-start(bf16[48,1024]{1,0:T(8,128)(2,1)} %param.5), channel_id=1, source_target_pairs={{0,3},{1,0},{2,1},{3,2},{4,7},{5,4},{6,5},{7,6},{8,11},{9,8},{10,9... | collective-permute-start | bytes 294920 | tf_op jit(solution)/shard_map/ppermute | solution.py:83
  8.6 12.6 %collective-permute-start.4 = (bf16[48,1024]{1,0:T(8,128)(2,1)}, bf16[48,1024]{1,0:T(8,128)(2,1)S(1)}, u32[]{:S(2)}, u32[]{:S(2)}) collective-permute-start(bf16[48,1024]{1,0:T(8,128)(2,1)} %param.6), channel_id=1, source_target_pairs={{0,2},{1,3},{2,0},{3,1},{4,6},{5,7},{6,4},{7,5},{8,10},{9,11},{10,... | collective-permute-start | bytes 294920 | tf_op jit(solution)/shard_map/ppermute | solution.py:83
  8.6 12.6 %collective-permute-start.3 = (bf16[48,1024]{1,0:T(8,128)(2,1)}, bf16[48,1024]{1,0:T(8,128)(2,1)S(1)}, u32[]{:S(2)}, u32[]{:S(2)}) collective-permute-start(bf16[48,1024]{1,0:T(8,128)(2,1)} %param.6), channel_id=1, source_target_pairs={{0,1},{1,2},{2,3},{3,0},{4,5},{5,6},{6,7},{7,4},{8,9},{9,10},{10,1... | collective-permute-start | bytes 294920 | tf_op jit(solution)/shard_map/ppermute | solution.py:83
  12.4 9.7 %collective-permute-start.5 = (bf16[48,1024]{1,0:T(8,128)(2,1)}, bf16[48,1024]{1,0:T(8,128)(2,1)S(1)}, u32[]{:S(2)}, u32[]{:S(2)}) collective-permute-start(bf16[48,1024]{1,0:T(8,128)(2,1)} %param.6), channel_id=1, source_target_pairs={{0,3},{1,0},{2,1},{3,2},{4,7},{5,4},{6,5},{7,6},{8,11},{9,8},{10,9... | collective-permute-start | bytes 294920 | tf_op jit(solution)/shard_map/ppermute | solution.py:83
  14.3 5.2 %copy-start.4 = (bf16[1024,3584]{1,0:T(8,128)(2,1)S(1)}, bf16[1024,3584]{1,0:T(8,128)(2,1)}, u32[]{:S(2)}) copy-start(bf16[1024,3584]{1,0:T(8,128)(2,1)} %param.7) | copy-start | bytes 22020100
  14.3 7.8 %slice-start = ((s8[7340032]{0:T(1024)(128)(4,1)}), s8[4194304]{0:T(1024)(128)(4,1)S(1)}, s32[]{:S(2)}) async-start(s8[7340032]{0:T(1024)(128)(4,1)} %bitcast.28), calls=%async_computation | async-start | bytes 8388608
  19.5 2.6 %slice-start.1 = ((s8[7340032]{0:T(1024)(128)(4,1)}), s8[3145728]{0:T(1024)(128)(4,1)S(1)}, s32[]{:S(2)}) async-start(s8[7340032]{0:T(1024)(128)(4,1)} %bitcast.28), calls=%async_computation.1 | async-start | bytes 6291456
  22.2 2.6 %copy-start.2 = (bf16[192,1024]{1,0:T(8,128)(2,1)}, bf16[192,1024]{1,0:T(8,128)(2,1)S(1)}, u32[]{:S(2)}) copy-start(bf16[192,1024]{1,0:T(8,128)(2,1)S(1)} %constant_dynamic-update-slice_fusion.4) | copy-start | bytes 1179652
  26.0 1.0 copy-start
  27.8 2.2 %collective-permute-start.12 = (bf16[3,96,896]{2,1,0:T(8,128)(2,1)}, bf16[3,96,896]{2,1,0:T(8,128)(2,1)}, u32[]{:S(2)}, u32[]{:S(2)}) collective-permute-start(bf16[3,96,896]{2,1,0:T(8,128)(2,1)} %constant_dynamic-slice_fusion.8), channel_id=1, source_target_pairs={{0,4},{4,0},{8,12},{12,8},{16,20},{20,16},{24,28},{28,24},{1,5},{5... | collective-permute-start | bytes 1548296 | tf_op jit(solution)/shard_map/ppermute | solution.py:37
  27.8 2.2 %copy-start.1 = (bf16[3,192,896]{2,1,0:T(8,128)(2,1)S(1)}, bf16[3,192,896]{2,1,0:T(8,128)(2,1)}, u32[]{:S(2)}) copy-start(bf16[3,192,896]{2,1,0:T(8,128)(2,1)} %copy-done) | copy-start | bytes 3096580
  27.9 4.9 %collective-permute-start.18 = (bf16[3,96,896]{2,1,0:T(8,128)(2,1)S(1)}, bf16[3,96,896]{2,1,0:T(8,128)(2,1)S(1)}, u32[]{:S(2)}, u32[]{:S(2)}) collective-permute-start(bf16[3,96,896]{2,1,0:T(8,128)(2,1)S(1)} %constant_dynamic-slice_fusion.5), channel_id=1, source_target_pairs={{0,4},{4,0},{8,12},{12,8},{16,20},{20,16},{24,28},{28,24},{1,5},{5... | collective-permute-start | bytes 1548296 | tf_op jit(solution)/shard_map/ppermute | solution.py:37
  28.5 6.1 %collective-permute-start.24 = (bf16[3,96,896]{2,1,0:T(8,128)(2,1)S(1)}, bf16[3,96,896]{2,1,0:T(8,128)(2,1)S(1)}, u32[]{:S(2)}, u32[]{:S(2)}) collective-permute-start(bf16[3,96,896]{2,1,0:T(8,128)(2,1)S(1)} %constant_dynamic-slice_fusion.2), channel_id=1, source_target_pairs={{0,4},{4,0},{8,12},{12,8},{16,20},{20,16},{24,28},{28,24},{1,5},{5... | collective-permute-start | bytes 1548296 | tf_op jit(solution)/shard_map/ppermute | solution.py:37
  28.6 6.7 %collective-permute-start.6 = (bf16[3,96,896]{2,1,0:T(8,128)(2,1)S(1)}, bf16[3,96,896]{2,1,0:T(8,128)(2,1)S(1)}, u32[]{:S(2)}, u32[]{:S(2)}) collective-permute-start(bf16[3,96,896]{2,1,0:T(8,128)(2,1)S(1)} %constant_dynamic-slice_fusion.11), channel_id=1, source_target_pairs={{0,4},{4,0},{8,12},{12,8},{16,20},{20,16},{24,28},{28,24},{1,5},{5... | collective-permute-start | bytes 1548296 | tf_op jit(solution)/shard_map/ppermute | solution.py:37
  31.3 9.2 %collective-permute-start.13 = (bf16[3,48,896]{2,1,0:T(8,128)(2,1)S(1)}, bf16[3,48,896]{2,1,0:T(8,128)(2,1)S(1)}, u32[]{:S(2)}, u32[]{:S(2)}) collective-permute-start(bf16[3,48,896]{2,1,0:T(8,128)(2,1)S(1)} %constant_dynamic-slice_fusion.7), channel_id=1, source_target_pairs={{0,16},{4,20},{8,24},{12,28},{16,0},{20,4},{24,8},{28,12},{1,17},{... | collective-permute-start | bytes 774152 | tf_op jit(solution)/shard_map/ppermute | solution.py:37
  33.0 9.2 %collective-permute-start.19 = (bf16[3,48,896]{2,1,0:T(8,128)(2,1)S(1)}, bf16[3,48,896]{2,1,0:T(8,128)(2,1)S(1)}, u32[]{:S(2)}, u32[]{:S(2)}) collective-permute-start(bf16[3,48,896]{2,1,0:T(8,128)(2,1)S(1)} %constant_dynamic-slice_fusion.4), channel_id=1, source_target_pairs={{0,8},{4,12},{8,0},{12,4},{16,24},{20,28},{24,16},{28,20},{1,9},{5... | collective-permute-start | bytes 774152 | tf_op jit(solution)/shard_map/ppermute | solution.py:37
  34.7 11.2 %collective-permute-start.25 = (bf16[3,48,896]{2,1,0:T(8,128)(2,1)S(1)}, bf16[3,48,896]{2,1,0:T(8,128)(2,1)S(1)}, u32[]{:S(2)}, u32[]{:S(2)}) collective-permute-start(bf16[3,48,896]{2,1,0:T(8,128)(2,1)S(1)} %constant_dynamic-slice_fusion.1), channel_id=1, source_target_pairs={{0,16},{4,20},{8,24},{12,28},{16,0},{20,4},{24,8},{28,12},{1,17},{... | collective-permute-start | bytes 774152 | tf_op jit(solution)/shard_map/ppermute | solution.py:37
  35.5 12.2 %collective-permute-start.7 = (bf16[3,48,896]{2,1,0:T(8,128)(2,1)S(1)}, bf16[3,48,896]{2,1,0:T(8,128)(2,1)S(1)}, u32[]{:S(2)}, u32[]{:S(2)}) collective-permute-start(bf16[3,48,896]{2,1,0:T(8,128)(2,1)S(1)} %constant_dynamic-slice_fusion.10), channel_id=1, source_target_pairs={{0,8},{4,12},{8,0},{12,4},{16,24},{20,28},{24,16},{28,20},{1,9},{5... | collective-permute-start | bytes 774152 | tf_op jit(solution)/shard_map/ppermute | solution.py:37
  40.5 9.9 %collective-permute-start.14 = (bf16[3,24,896]{2,1,0:T(8,128)(2,1)S(1)}, bf16[3,24,896]{2,1,0:T(8,128)(2,1)S(1)}, u32[]{:S(2)}, u32[]{:S(2)}) collective-permute-start(bf16[3,24,896]{2,1,0:T(8,128)(2,1)S(1)} %constant_dynamic-slice_fusion.6), channel_id=1, source_target_pairs={{0,8},{4,12},{8,0},{12,4},{16,24},{20,28},{24,16},{28,20},{1,9},{5... | collective-permute-start | bytes 387080 | tf_op jit(solution)/shard_map/ppermute | solution.py:37
  42.3 9.9 %collective-permute-start.20 = (bf16[3,24,896]{2,1,0:T(8,128)(2,1)S(1)}, bf16[3,24,896]{2,1,0:T(8,128)(2,1)S(1)}, u32[]{:S(2)}, u32[]{:S(2)}) collective-permute-start(bf16[3,24,896]{2,1,0:T(8,128)(2,1)S(1)} %constant_dynamic-slice_fusion.3), channel_id=1, source_target_pairs={{0,16},{4,20},{8,24},{12,28},{16,0},{20,4},{24,8},{28,12},{1,17},{... | collective-permute-start | bytes 387080 | tf_op jit(solution)/shard_map/ppermute | solution.py:37
  46.1 7.0 %collective-permute-start.26 = (bf16[3,24,896]{2,1,0:T(8,128)(2,1)S(1)}, bf16[3,24,896]{2,1,0:T(8,128)(2,1)S(1)}, u32[]{:S(2)}, u32[]{:S(2)}) collective-permute-start(bf16[3,24,896]{2,1,0:T(8,128)(2,1)S(1)} %constant_dynamic-slice_fusion), channel_id=1, source_target_pairs={{0,8},{4,12},{8,0},{12,4},{16,24},{20,28},{24,16},{28,20},{1,9},{5... | collective-permute-start | bytes 387080 | tf_op jit(solution)/shard_map/ppermute | solution.py:37
  47.8 7.0 %collective-permute-start.8 = (bf16[3,24,896]{2,1,0:T(8,128)(2,1)S(1)}, bf16[3,24,896]{2,1,0:T(8,128)(2,1)S(1)}, u32[]{:S(2)}, u32[]{:S(2)}) collective-permute-start(bf16[3,24,896]{2,1,0:T(8,128)(2,1)S(1)} %constant_dynamic-slice_fusion.9), channel_id=1, source_target_pairs={{0,16},{4,20},{8,24},{12,28},{16,0},{20,4},{24,8},{28,12},{1,17},{... | collective-permute-start | bytes 387080 | tf_op jit(solution)/shard_map/ppermute | solution.py:37
  50.6 6.1 %collective-permute-start.15 = (bf16[3,24,896]{2,1,0:T(8,128)(2,1)S(1)}, bf16[3,24,896]{2,1,0:T(8,128)(2,1)S(1)}, u32[]{:S(2)}, u32[]{:S(2)}) collective-permute-start(bf16[3,24,896]{2,1,0:T(8,128)(2,1)S(1)} %pad_maximum_fusion.3), channel_id=1, source_target_pairs={{0,8},{4,12},{8,0},{12,4},{16,24},{20,28},{24,16},{28,20},{1,9},{5... | collective-permute-start | bytes 387080 | tf_op jit(solution)/shard_map/ppermute | solution.py:49
  52.3 6.7 %collective-permute-start.21 = (bf16[3,24,896]{2,1,0:T(8,128)(2,1)S(1)}, bf16[3,24,896]{2,1,0:T(8,128)(2,1)S(1)}, u32[]{:S(2)}, u32[]{:S(2)}) collective-permute-start(bf16[3,24,896]{2,1,0:T(8,128)(2,1)S(1)} %pad_maximum_fusion.4), channel_id=1, source_target_pairs={{0,16},{4,20},{8,24},{12,28},{16,0},{20,4},{24,8},{28,12},{1,17},{... | collective-permute-start | bytes 387080 | tf_op jit(solution)/shard_map/ppermute | solution.py:49
  53.2 7.3 %collective-permute-start.27 = (bf16[3,24,896]{2,1,0:T(8,128)(2,1)S(1)}, bf16[3,24,896]{2,1,0:T(8,128)(2,1)S(1)}, u32[]{:S(2)}, u32[]{:S(2)}) collective-permute-start(bf16[3,24,896]{2,1,0:T(8,128)(2,1)S(1)} %pad_maximum_fusion.5), channel_id=1, source_target_pairs={{0,8},{4,12},{8,0},{12,4},{16,24},{20,28},{24,16},{28,20},{1,9},{5... | collective-permute-start | bytes 387080 | tf_op jit(solution)/shard_map/ppermute | solution.py:49
  56.7 9.2 %collective-permute-start.16 = (bf16[3,48,896]{2,1,0:T(8,128)(2,1)S(1)}, bf16[3,48,896]{2,1,0:T(8,128)(2,1)S(1)}, u32[]{:S(2)}, u32[]{:S(2)}) collective-permute-start(bf16[3,48,896]{2,1,0:T(8,128)(2,1)S(1)} %maximum_select_fusion.9), channel_id=1, source_target_pairs={{0,16},{4,20},{8,24},{12,28},{16,0},{20,4},{24,8},{28,12},{1,17},{... | collective-permute-start | bytes 774152 | tf_op jit(solution)/shard_map/ppermute | solution.py:49
  57.4 10.9 %collective-permute-start.9 = (bf16[3,24,896]{2,1,0:T(8,128)(2,1)S(1)}, bf16[3,24,896]{2,1,0:T(8,128)(2,1)S(1)}, u32[]{:S(2)}, u32[]{:S(2)}) collective-permute-start(bf16[3,24,896]{2,1,0:T(8,128)(2,1)S(1)} %pad_maximum_fusion.2), channel_id=1, source_target_pairs={{0,16},{4,20},{8,24},{12,28},{16,0},{20,4},{24,8},{28,12},{1,17},{... | collective-permute-start | bytes 387080 | tf_op jit(solution)/shard_map/ppermute | solution.py:49
  59.0 10.0 %collective-permute-start.22 = (bf16[3,48,896]{2,1,0:T(8,128)(2,1)S(1)}, bf16[3,48,896]{2,1,0:T(8,128)(2,1)S(1)}, u32[]{:S(2)}, u32[]{:S(2)}) collective-permute-start(bf16[3,48,896]{2,1,0:T(8,128)(2,1)S(1)} %maximum_select_fusion.10), channel_id=1, source_target_pairs={{0,8},{4,12},{8,0},{12,4},{16,24},{20,28},{24,16},{28,20},{1,9},{5... | collective-permute-start | bytes 774152 | tf_op jit(solution)/shard_map/ppermute | solution.py:49
  60.6 10.5 %collective-permute-start.28 = (bf16[3,48,896]{2,1,0:T(8,128)(2,1)S(1)}, bf16[3,48,896]{2,1,0:T(8,128)(2,1)S(1)}, u32[]{:S(2)}, u32[]{:S(2)}) collective-permute-start(bf16[3,48,896]{2,1,0:T(8,128)(2,1)S(1)} %maximum_select_fusion.11), channel_id=1, source_target_pairs={{0,16},{4,20},{8,24},{12,28},{16,0},{20,4},{24,8},{28,12},{1,17},{... | collective-permute-start | bytes 774152 | tf_op jit(solution)/shard_map/ppermute | solution.py:49
  66.0 9.0 %collective-permute-start.17 = (bf16[3,96,896]{2,1,0:T(8,128)(2,1)S(1)}, bf16[3,96,896]{2,1,0:T(8,128)(2,1)S(1)}, u32[]{:S(2)}, u32[]{:S(2)}) collective-permute-start(bf16[3,96,896]{2,1,0:T(8,128)(2,1)S(1)} %maximum_select_fusion.5), channel_id=1, source_target_pairs={{0,4},{4,0},{8,12},{12,8},{16,20},{20,16},{24,28},{28,24},{1,5},{5... | collective-permute-start | bytes 1548296 | tf_op jit(solution)/shard_map/ppermute | solution.py:49
  68.4 6.5 %collective-permute-start.10 = (bf16[3,48,896]{2,1,0:T(8,128)(2,1)S(1)}, bf16[3,48,896]{2,1,0:T(8,128)(2,1)S(1)}, u32[]{:S(2)}, u32[]{:S(2)}) collective-permute-start(bf16[3,48,896]{2,1,0:T(8,128)(2,1)S(1)} %maximum_select_fusion.8), channel_id=1, source_target_pairs={{0,8},{4,12},{8,0},{12,4},{16,24},{20,28},{24,16},{28,20},{1,9},{5... | collective-permute-start | bytes 774152 | tf_op jit(solution)/shard_map/ppermute | solution.py:49
  69.1 6.3 %collective-permute-start.23 = (bf16[3,96,896]{2,1,0:T(8,128)(2,1)S(1)}, bf16[3,96,896]{2,1,0:T(8,128)(2,1)}, u32[]{:S(2)}, u32[]{:S(2)}) collective-permute-start(bf16[3,96,896]{2,1,0:T(8,128)(2,1)S(1)} %maximum_select_fusion.6), channel_id=1, source_target_pairs={{0,4},{4,0},{8,12},{12,8},{16,20},{20,16},{24,28},{28,24},{1,5},{5... | collective-permute-start | bytes 1548296 | tf_op jit(solution)/shard_map/ppermute | solution.py:49
  71.2 5.9 %collective-permute-start.29 = (bf16[3,96,896]{2,1,0:T(8,128)(2,1)S(1)}, bf16[3,96,896]{2,1,0:T(8,128)(2,1)}, u32[]{:S(2)}, u32[]{:S(2)}) collective-permute-start(bf16[3,96,896]{2,1,0:T(8,128)(2,1)S(1)} %maximum_select_fusion.7), channel_id=1, source_target_pairs={{0,4},{4,0},{8,12},{12,8},{16,20},{20,16},{24,28},{28,24},{1,5},{5... | collective-permute-start | bytes 1548296 | tf_op jit(solution)/shard_map/ppermute | solution.py:49
  75.0 3.6 %collective-permute-start.11 = (bf16[3,96,896]{2,1,0:T(8,128)(2,1)S(1)}, bf16[3,96,896]{2,1,0:T(8,128)(2,1)}, u32[]{:S(2)}, u32[]{:S(2)}) collective-permute-start(bf16[3,96,896]{2,1,0:T(8,128)(2,1)S(1)} %maximum_select_fusion.4), channel_id=1, source_target_pairs={{0,4},{4,0},{8,12},{12,8},{16,20},{20,16},{24,28},{28,24},{1,5},{5... | collective-permute-start | bytes 1548296 | tf_op jit(solution)/shard_map/ppermute | solution.py:49
  75.5 5.0 %slice-start.2 = ((s8[7340032]{0:T(1024)(128)(4,1)}), s8[4194304]{0:T(1024)(128)(4,1)S(1)}, s32[]{:S(2)}) async-start(s8[7340032]{0:T(1024)(128)(4,1)} %bitcast.30), calls=%async_computation.2 | async-start | bytes 8388608
  80.1 1.9 %slice-start.3 = ((s8[7340032]{0:T(1024)(128)(4,1)}), s8[3145728]{0:T(1024)(128)(4,1)S(1)}, s32[]{:S(2)}) async-start(s8[7340032]{0:T(1024)(128)(4,1)} %bitcast.30), calls=%async_computation.3 | async-start | bytes 6291456
  80.1 4.7 %slice-start.4 = ((s8[7340032]{0:T(1024)(128)(4,1)}), s8[4194304]{0:T(1024)(128)(4,1)S(1)}, s32[]{:S(2)}) async-start(s8[7340032]{0:T(1024)(128)(4,1)} %bitcast.32), calls=%async_computation.4 | async-start | bytes 8388608
  82.0 2.8 %slice-start.5 = ((s8[7340032]{0:T(1024)(128)(4,1)}), s8[3145728]{0:T(1024)(128)(4,1)S(1)}, s32[]{:S(2)}) async-start(s8[7340032]{0:T(1024)(128)(4,1)} %bitcast.32), calls=%async_computation.5 | async-start | bytes 6291456
  92.5 19.2 %collective-permute-start.30 = (bf16[48,1024]{1,0:T(8,128)(2,1)S(1)}, bf16[48,1024]{1,0:T(8,128)(2,1)S(1)}, u32[]{:S(2)}, u32[]{:S(2)}) collective-permute-start(bf16[48,1024]{1,0:T(8,128)(2,1)S(1)} %get-tuple-element.27), channel_id=1, source_target_pairs={{0,3},{1,0},{2,1},{3,2},{4,7},{5,4},{6,5},{7,6},{8,11},{9,8},{10,9... | collective-permute-start | bytes 294920 | tf_op jit(solution)/shard_map/ppermute | solution.py:91
  100.5 11.2 %collective-permute-start.32 = (bf16[48,1024]{1,0:T(8,128)(2,1)S(1)}, bf16[48,1024]{1,0:T(8,128)(2,1)S(1)}, u32[]{:S(2)}, u32[]{:S(2)}) collective-permute-start(bf16[48,1024]{1,0:T(8,128)(2,1)S(1)} %get-tuple-element.28), channel_id=1, source_target_pairs={{0,1},{1,2},{2,3},{3,0},{4,5},{5,6},{6,7},{7,4},{8,9},{9,10},{10,1... | collective-permute-start | bytes 294920 | tf_op jit(solution)/shard_map/ppermute | solution.py:91
  100.5 6.0 %copy-start.3 = (bf16[192,1024]{1,0:T(8,128)(2,1)S(1)}, bf16[192,1024]{1,0:T(8,128)(2,1)}, u32[]{:S(2)}) copy-start(bf16[192,1024]{1,0:T(8,128)(2,1)} %copy-done.2) | copy-start | bytes 1179652
  100.5 11.2 %collective-permute-start.31 = (bf16[48,1024]{1,0:T(8,128)(2,1)S(1)}, bf16[48,1024]{1,0:T(8,128)(2,1)S(1)}, u32[]{:S(2)}, u32[]{:S(2)}) collective-permute-start(bf16[48,1024]{1,0:T(8,128)(2,1)S(1)} %get-tuple-element.29), channel_id=1, source_target_pairs={{0,2},{1,3},{2,0},{3,1},{4,6},{5,7},{6,4},{7,5},{8,10},{9,11},{10,... | collective-permute-start | bytes 294920 | tf_op jit(solution)/shard_map/ppermute | solution.py:91

commit v11 on v6

--- a/solution.py
+++ b/solution.py
@@ -109,16 +109,34 @@
     partial_grad, grad_gate, grad_up, hidden = lax.optimization_barrier(
         (partial_grad.astype(jnp.bfloat16), grad_gate, grad_up, hidden)
     )
-    acc_gate = jnp.dot(tok_t, grad_gate, preferred_element_type=jnp.float32).astype(jnp.bfloat16)
-    partial_grad, acc_gate, grad_up, hidden = lax.optimization_barrier((partial_grad, acc_gate, grad_up, hidden))
-    grad_tokens = col_reduce_scatter(partial_grad, n_col)
-    acc_up = jnp.dot(tok_t, grad_up, preferred_element_type=jnp.float32)
-    acc_down = contract_first(hidden, grad_all)
+    span = partial_grad.shape[0] // n_col
+    shifts = list(range(1, n_col))
+    groups = [shifts[i::3] for i in range(3)]
+    total = partial_grad[:span].astype(jnp.float32)
+    received = []
+    weights = []
+    for i, (lhs, rhs, first) in enumerate(((tok_t, grad_gate, False), (tok_t, grad_up, False), (hidden, grad_all, True))):
+        for s in groups[i]:
+            received.append(
+                lax.ppermute(partial_grad[s * span:(s + 1) * span], "col", [(j, (j - s) % n_col) for j in range(n_col)])
+            )
+        if first:
+            acc = contract_first(lhs, rhs)
+        else:
+            acc = jnp.dot(lhs, rhs, preferred_element_type=jnp.float32)
+        acc = acc.astype(jnp.bfloat16)
+        if i < 2:
+            acc, partial_grad = lax.optimization_barrier((acc, partial_grad))
+        weights.append(acc)
+    for got in received:
+        total = total + got.astype(jnp.float32)
+    grad_tokens = total.astype(jnp.bfloat16)
+    acc_gate, acc_up, acc_down = weights
     return (
         grad_tokens,
         acc_gate,
-        acc_up.astype(jnp.bfloat16),
-        acc_down.astype(jnp.bfloat16),
+        acc_up,
+        acc_down,
     )
 
 

time: 112 us -> 112 us (level)
  transfers between devices with their start and end apart: 21 -> 21, of which waited for: 10 -> 11; matrix products, arithmetic and copies ran while one was open for 22% -> 26% of each run, Pallas kernels for 0% -> 0%
where the time goes in v11:
time: 112 us
  waiting for transfers between devices  35.4 us (32%)
  starting transfers between devices  31.7 us (28%)
  matrix products  29.6 us (26%)
  other arithmetic  7.76 us (7%)
  local copies, waits for them, and re-layouts  6.29 us (6%)
    ppermute x6, waiting for transfers between devices, doubling_gather(): got = lax.ppermute(cur, 'row', [(j, j ^ bit) for j in range(n_dev)])  16.2 us
    ppermute x6, waiting for transfers between devices, halving_reduce(): got = lax.ppermute(send, 'row', [(j, j ^ bit) for j in range(n_dev)])  16.1 us
    dot_general x2, matrix products, body(): acc = jnp.dot(lhs, rhs, preferred_element_type=jnp.float32)  10.4 us
    ppermute x6, starting transfers between devices, col_gather(): lax.ppermute(x, 'col', [(j, (j + s) % n_col) for j in range(n_col)])  10.4 us
    ppermute x3, starting transfers between devices, body(): lax.ppermute(partial_grad[s * span:(s + 1) * span], 'col', [(j, (j - s) %...  8.88 us
    dot_general x3, matrix products, contract_last(): lax.dot_general(left, right, (((1,), (1,)), ((), ())), preferred_element_...  7.59 us
    ppermute x6, starting transfers between devices, halving_reduce(): got = lax.ppermute(send, 'row', [(j, j ^ bit) for j in range(n_dev)])  6.67 us
    ppermute x6, starting transfers between devices, doubling_gather(): got = lax.ppermute(cur, 'row', [(j, j ^ bit) for j in range(n_dev)])  5.81 us
  transfers between devices with their start and end apart: 21, of which 11 were waited for; matrix products, arithmetic and copies ran while one was open for 26% of the time, Pallas kernels for 0%

profile of v11, /device:TPU:0, one launch (start us, length us, event | category | flops | bytes accessed | tf_op | source)
XLA Modules:
  0.0 111.8 jit_solution(3257684561488479280)
XLA Ops:
  0.6 4.1 %collective-permute-start.1 = (bf16[48,1024]{1,0:T(8,128)(2,1)}, bf16[48,1024]{1,0:T(8,128)(2,1)S(1)}, u32[]{:S(2)}, u32[]{:S(2)}) collective-permute-start(bf16[48,1024]{1,0:T(8,128)(2,1)} %param.5), channel_id=1, source_target_pairs={{0,2},{1,3},{2,0},{3,1},{4,6},{5,7},{6,4},{7,5},{8,10},{9,11},{10,... | collective-permute-start | bytes 294920 | tf_op jit(solution)/shard_map/ppermute | solution.py:80
  4.8 1.6 %collective-permute-start = (bf16[48,1024]{1,0:T(8,128)(2,1)}, bf16[48,1024]{1,0:T(8,128)(2,1)S(1)}, u32[]{:S(2)}, u32[]{:S(2)}) collective-permute-start(bf16[48,1024]{1,0:T(8,128)(2,1)} %param.5), channel_id=1, source_target_pairs={{0,1},{1,2},{2,3},{3,0},{4,5},{5,6},{6,7},{7,4},{8,9},{9,10},{10,1... | collective-permute-start | bytes 294920 | tf_op jit(solution)/shard_map/ppermute | solution.py:80
  6.3 2.2 %collective-permute-start.2 = (bf16[48,1024]{1,0:T(8,128)(2,1)}, bf16[48,1024]{1,0:T(8,128)(2,1)S(1)}, u32[]{:S(2)}, u32[]{:S(2)}) collective-permute-start(bf16[48,1024]{1,0:T(8,128)(2,1)} %param.5), channel_id=1, source_target_pairs={{0,3},{1,0},{2,1},{3,2},{4,7},{5,4},{6,5},{7,6},{8,11},{9,8},{10,9... | collective-permute-start | bytes 294920 | tf_op jit(solution)/shard_map/ppermute | solution.py:80
  8.6 0.6 collective-permute-start.3
  9.2 0.9 constant_dynamic-update-slice_fusion.3
  10.1 0.9 constant_dynamic-update-slice_fusion.7
  11.0 1.5 %collective-permute-done = bf16[48,1024]{1,0:T(8,128)(2,1)S(1)} collective-permute-done((bf16[48,1024]{1,0:T(8,128)(2,1)}, bf16[48,1024]{1,0:T(8,128)(2,1)S(1)}, u32[]{:S(2)}, u32[]{:S(2)}) %collective-permute-start) | collective-permute-done | bytes 98336 | tf_op jit(solution)/shard_map/ppermute | solution.py:80
  12.4 1.8 %collective-permute-start.5 = (bf16[48,1024]{1,0:T(8,128)(2,1)}, bf16[48,1024]{1,0:T(8,128)(2,1)S(1)}, u32[]{:S(2)}, u32[]{:S(2)}) collective-permute-start(bf16[48,1024]{1,0:T(8,128)(2,1)} %param.6), channel_id=1, source_target_pairs={{0,3},{1,0},{2,1},{3,2},{4,7},{5,4},{6,5},{7,6},{8,11},{9,8},{10,9... | collective-permute-start | bytes 294920 | tf_op jit(solution)/shard_map/ppermute | solution.py:80
  14.3 0.0 slice-start
  14.4 4.8 %fusion.1 = bf16[1,192,3584]{2,1,0:T(8,128)(2,1)S(1)} fusion(bf16[192,1024]{1,0:T(8,128)(2,1)S(1)} %constant_dynamic-update-slice_fusion, bf16[1024,3584]{1,0:T(8,128)(2,1)} %param.8), kind=kOutput, calls=%fused_computation.7 | convolution fusion | flops 1409974272 | bytes 9109504 | tf_op jit(solution)/shard_map/dot_general | solution.py:102
  19.2 0.3 copy-done.3
  19.5 1.7 %fusion = bf16[1,192,3584]{2,1,0:T(8,128)(2,1)S(1)} fusion(bf16[192,1024]{1,0:T(8,128)(2,1)S(1)} %constant_dynamic-update-slice_fusion, bf16[1024,3584]{1,0:T(8,128)(2,1)S(1)} %copy-done.3), kind=kOutput, calls=%fused_computation.6 | convolution fusion | flops 1409974272 | bytes 9109504 | tf_op jit(solution)/shard_map/dot_general | solution.py:101
  21.2 0.9 collective-permute-done.5
  22.2 2.6 %fusion.2 = bf16[1,192,3584]{2,1,0:T(8,128)(2,1)S(1)} fusion(bf16[192,1024]{1,0:T(8,128)(2,1)S(1)} %constant_dynamic-update-slice_fusion.4, bf16[3584,1024]{1,0:T(8,128)(2,1)S(1)} %bitcast.29), kind=kOutput, calls=%fused_computation.8 | convolution fusion | flops 1409974272 | bytes 9109504 | tf_op jit(solution)/shard_map/dot_general | solution.py:14
  24.7 0.5 pad_maximum_fusion
  25.2 0.3 fusion.9
  25.5 1.1 %constant_dynamic-slice_fusion.5 = bf16[3,96,1792]{2,1,0:T(8,128)(2,1)} fusion(bf16[3,192,1792]{2,1,0:T(8,128)(2,1)S(1)} %get-tuple-element.24, s32[]{:T(128)S(6)} %select_n.131), kind=kLoop, calls=%fused_computation.58 | loop fusion | bytes 2064388 | tf_op jit(solution)/shard_map/dynamic_slice | solution.py:36
  26.7 1.0 constant_dynamic-slice_fusion.2
  27.7 0.5 collective-permute-start.12
  28.2 1.4 %collective-permute-done.6 = bf16[3,96,1792]{2,1,0:T(8,128)(2,1)} collective-permute-done((bf16[3,96,1792]{2,1,0:T(8,128)(2,1)}, bf16[3,96,1792]{2,1,0:T(8,128)(2,1)}, u32[]{:S(2)}, u32[]{:S(2)}) %collective-permute-start.6) | collective-permute-done | bytes 1032224 | tf_op jit(solution)/shard_map/ppermute | solution.py:37
  29.6 1.8 %add_convert_fusion.1 = bf16[3,96,1792]{2,1,0:T(8,128)(2,1)S(1)} fusion(bf16[3,96,1792]{2,1,0:T(8,128)(2,1)} %collective-permute-done.6, bf16[3,192,1792]{2,1,0:T(8,128)(2,1)} %copy-done, s32[]{:T(128)S(6)} %select_n.130), kind=kLoop, calls=%fused_computation.17 | loop fusion | flops 2064384 | bytes 3096580 | tf_op jit(solution)/shard_map/convert_element_type | solution.py:40
  31.5 1.5 %collective-permute-start.7 = (bf16[3,48,1792]{2,1,0:T(8,128)(2,1)S(1)}, bf16[3,48,1792]{2,1,0:T(8,128)(2,1)S(1)}, u32[]{:S(2)}, u32[]{:S(2)}) collective-permute-start(bf16[3,48,1792]{2,1,0:T(8,128)(2,1)S(1)} %constant_dynamic-slice_fusion.4), channel_id=1, source_target_pairs={{0,8},{4,12},{8,0},{12,4},{16,24},{20,28},{24,16},{28,20},{1,9},{5... | collective-permute-start | bytes 1548296 | tf_op jit(solution)/shard_map/ppermute | solution.py:37
  33.0 0.3 add_convert_fusion
  33.3 1.6 %collective-permute-start.13 = (bf16[3,48,1792]{2,1,0:T(8,128)(2,1)S(1)}, bf16[3,48,1792]{2,1,0:T(8,128)(2,1)S(1)}, u32[]{:S(2)}, u32[]{:S(2)}) collective-permute-start(bf16[3,48,1792]{2,1,0:T(8,128)(2,1)S(1)} %constant_dynamic-slice_fusion.1), channel_id=1, source_target_pairs={{0,16},{4,20},{8,24},{12,28},{16,0},{20,4},{24,8},{28,12},{1,17},{... | collective-permute-start | bytes 1548296 | tf_op jit(solution)/shard_map/ppermute | solution.py:37
  34.9 10.5 %collective-permute-done.7 = bf16[3,48,1792]{2,1,0:T(8,128)(2,1)S(1)} collective-permute-done((bf16[3,48,1792]{2,1,0:T(8,128)(2,1)S(1)}, bf16[3,48,1792]{2,1,0:T(8,128)(2,1)S(1)}, u32[]{:S(2)}, u32[]{:S(2)}) %collective-permute-start.7) | collective-permute-done | bytes 516128 | tf_op jit(solution)/shard_map/ppermute | solution.py:37
  45.3 0.1 add_convert_fusion.3
  45.5 1.5 %collective-permute-start.8 = (bf16[3,24,1792]{2,1,0:T(8,128)(2,1)S(1)}, bf16[3,24,1792]{2,1,0:T(8,128)(2,1)S(1)}, u32[]{:S(2)}, u32[]{:S(2)}) collective-permute-start(bf16[3,24,1792]{2,1,0:T(8,128)(2,1)S(1)} %constant_dynamic-slice_fusion.3), channel_id=1, source_target_pairs={{0,16},{4,20},{8,24},{12,28},{16,0},{20,4},{24,8},{28,12},{1,17},{... | collective-permute-start | bytes 774152 | tf_op jit(solution)/shard_map/ppermute | solution.py:37
  47.0 0.1 add_convert_fusion.2
  47.2 1.5 %collective-permute-start.14 = (bf16[3,24,1792]{2,1,0:T(8,128)(2,1)S(1)}, bf16[3,24,1792]{2,1,0:T(8,128)(2,1)S(1)}, u32[]{:S(2)}, u32[]{:S(2)}) collective-permute-start(bf16[3,24,1792]{2,1,0:T(8,128)(2,1)S(1)} %constant_dynamic-slice_fusion), channel_id=1, source_target_pairs={{0,8},{4,12},{8,0},{12,4},{16,24},{20,28},{24,16},{28,20},{1,9},{5... | collective-permute-start | bytes 774152 | tf_op jit(solution)/shard_map/ppermute | solution.py:37
  48.7 4.2 %collective-permute-done.8 = bf16[3,24,1792]{2,1,0:T(8,128)(2,1)S(1)} collective-permute-done((bf16[3,24,1792]{2,1,0:T(8,128)(2,1)S(1)}, bf16[3,24,1792]{2,1,0:T(8,128)(2,1)S(1)}, u32[]{:S(2)}, u32[]{:S(2)}) %collective-permute-start.8) | collective-permute-done | bytes 258080 | tf_op jit(solution)/shard_map/ppermute | solution.py:37
  53.0 0.1 convert_add_fusion.1
  53.0 0.1 multiply_convert_fusion.5
  53.2 1.5 %collective-permute-start.9 = (bf16[3,24,1792]{2,1,0:T(8,128)(2,1)S(1)}, bf16[3,24,1792]{2,1,0:T(8,128)(2,1)S(1)}, u32[]{:S(2)}, u32[]{:S(2)}) collective-permute-start(bf16[3,24,1792]{2,1,0:T(8,128)(2,1)S(1)} %pad_maximum_fusion.2), channel_id=1, source_target_pairs={{0,16},{4,20},{8,24},{12,28},{16,0},{20,4},{24,8},{28,12},{1,17},{... | collective-permute-start | bytes 774152 | tf_op jit(solution)/shard_map/ppermute | solution.py:49
  54.7 0.1 convert_add_fusion
  54.8 0.1 multiply_convert_fusion.2
  54.9 1.5 %collective-permute-start.15 = (bf16[3,24,1792]{2,1,0:T(8,128)(2,1)S(1)}, bf16[3,24,1792]{2,1,0:T(8,128)(2,1)S(1)}, u32[]{:S(2)}, u32[]{:S(2)}) collective-permute-start(bf16[3,24,1792]{2,1,0:T(8,128)(2,1)S(1)} %pad_maximum_fusion.3), channel_id=1, source_target_pairs={{0,8},{4,12},{8,0},{12,4},{16,24},{20,28},{24,16},{28,20},{1,9},{5... | collective-permute-start | bytes 774152 | tf_op jit(solution)/shard_map/ppermute | solution.py:49
  56.5 3.3 %collective-permute-done.9 = bf16[3,24,1792]{2,1,0:T(8,128)(2,1)S(1)} collective-permute-done((bf16[3,24,1792]{2,1,0:T(8,128)(2,1)S(1)}, bf16[3,24,1792]{2,1,0:T(8,128)(2,1)S(1)}, u32[]{:S(2)}, u32[]{:S(2)}) %collective-permute-start.9) | collective-permute-done | bytes 258080 | tf_op jit(solution)/shard_map/ppermute | solution.py:49
  59.8 0.1 maximum_select_fusion.4
  59.9 1.5 %collective-permute-start.10 = (bf16[3,48,1792]{2,1,0:T(8,128)(2,1)S(1)}, bf16[3,48,1792]{2,1,0:T(8,128)(2,1)S(1)}, u32[]{:S(2)}, u32[]{:S(2)}) collective-permute-start(bf16[3,48,1792]{2,1,0:T(8,128)(2,1)S(1)} %maximum_select_fusion.4), channel_id=1, source_target_pairs={{0,8},{4,12},{8,0},{12,4},{16,24},{20,28},{24,16},{28,20},{1,9},{5... | collective-permute-start | bytes 1548296 | tf_op jit(solution)/shard_map/ppermute | solution.py:49
  61.4 1.1 %collective-permute-done.15 = bf16[3,24,1792]{2,1,0:T(8,128)(2,1)S(1)} collective-permute-done((bf16[3,24,1792]{2,1,0:T(8,128)(2,1)S(1)}, bf16[3,24,1792]{2,1,0:T(8,128)(2,1)S(1)}, u32[]{:S(2)}, u32[]{:S(2)}) %collective-permute-start.15) | collective-permute-done | bytes 258080 | tf_op jit(solution)/shard_map/ppermute | solution.py:49
  62.5 0.1 maximum_select_fusion.5
  62.6 0.6 collective-permute-start.16
  63.2 9.1 %collective-permute-done.10 = bf16[3,48,1792]{2,1,0:T(8,128)(2,1)S(1)} collective-permute-done((bf16[3,48,1792]{2,1,0:T(8,128)(2,1)S(1)}, bf16[3,48,1792]{2,1,0:T(8,128)(2,1)S(1)}, u32[]{:S(2)}, u32[]{:S(2)}) %collective-permute-start.10) | collective-permute-done | bytes 516128 | tf_op jit(solution)/shard_map/ppermute | solution.py:49
  72.4 0.3 maximum_select_fusion.2
  72.6 0.1 collective-permute-start.11
  72.7 0.3 maximum_select_fusion.3
  73.0 0.6 collective-permute-start.17
  73.5 1.8 %collective-permute-done.11 = bf16[3,96,1792]{2,1,0:T(8,128)(2,1)S(1)} collective-permute-done((bf16[3,96,1792]{2,1,0:T(8,128)(2,1)S(1)}, bf16[3,96,1792]{2,1,0:T(8,128)(2,1)S(1)}, u32[]{:S(2)}, u32[]{:S(2)}) %collective-permute-start.11) | collective-permute-done | bytes 1032224 | tf_op jit(solution)/shard_map/ppermute | solution.py:49
  75.3 0.8 maximum_select_fusion
  76.1 0.8 collective-permute-done.17
  77.0 2.1 %maximum_select_fusion.1 = bf16[3,192,1792]{2,1,0:T(8,128)(2,1)S(1)} fusion(bf16[3,96,1792]{2,1,0:T(8,128)(2,1)S(1)} %maximum_select_fusion.3, bf16[3,96,1792]{2,1,0:T(8,128)(2,1)} %collective-permute-done.17, pred[]{:T(512)S(6)} %eq.25), kind=kLoop, calls=%fused_computation.15 | loop fusion | flops 9289728 | bytes 4128769 | tf_op jit(solution)/shard_map/jit(_where)/select_n | solution.py:50
  79.0 0.0 slice-start.3
  79.0 0.4 fusion.7
  79.4 1.5 %slice-done.3 = s8[3145728]{0:T(1024)(128)(4,1)S(1)} async-done(((s8[7340032]{0:T(1024)(128)(4,1)}), s8[3145728]{0:T(1024)(128)(4,1)S(1)}, s32[]{:S(2)}) %slice-start.3) | async-done | bytes 3145752
  80.9 2.5 %fusion.10 = f32[192,1024]{1,0:T(8,128)S(1)} fusion(bf16[192,3584]{1,0:T(8,128)(2,1)S(1)} %get-tuple-element.15, bf16[1024,3584]{1,0:T(8,128)(2,1)S(1)} %bitcast.31), kind=kOutput, calls=%fused_computation.60 | convolution fusion | flops 1409286144 | bytes 9502720 | tf_op jit(solution)/shard_map/dot_general | solution.py:14
  83.5 2.5 %fusion.8 = bf16[192,1024]{1,0:T(8,128)(2,1)S(1)} fusion(f32[192,1024]{1,0:T(8,128)S(1)} %fusion.10, bf16[192,3584]{1,0:T(8,128)(2,1)S(1)} %get-tuple-element.13, bf16[1024,3584]{1,0:T(8,128)(2,1)S(1)} %bitcast.33), kind=kOutput, calls=%fused_computation.25 | convolution fusion | flops 1409679360 | bytes 9895936 | tf_op jit(solution)/shard_map/dot_general | solution.py:14
  86.0 8.2 %collective-permute-start.18 = (bf16[48,1024]{1,0:T(8,128)(2,1)S(1)}, bf16[48,1024]{1,0:T(8,128)(2,1)S(1)}, u32[]{:S(2)}, u32[]{:S(2)}) collective-permute-start(bf16[48,1024]{1,0:T(8,128)(2,1)S(1)} %slice.57), channel_id=1, source_target_pairs={{0,3},{1,0},{2,1},{3,2},{4,7},{5,4},{6,5},{7,6},{8,11},{9,8},{10,9... | collective-permute-start | bytes 294920 | tf_op jit(solution)/shard_map/ppermute | solution.py:121
  94.2 5.2 %convolution_convert_fusion.2 = bf16[1024,3584]{1,0:T(8,128)(2,1)} fusion(bf16[192,1024]{1,0:T(8,128)(2,1)S(1)} %constant_dynamic-update-slice_fusion, bf16[192,3584]{1,0:T(8,128)(2,1)S(1)} %get-tuple-element.13), kind=kOutput, calls=%fused_computation.2 | convolution fusion | flops 1412956160 | bytes 9109504 | tf_op jit(solution)/shard_map/dot_general | solution.py:126
  99.4 0.1 collective-permute-start.19
  99.4 5.2 %convolution_convert_fusion.1 = bf16[1024,3584]{1,0:T(8,128)(2,1)} fusion(bf16[192,1024]{1,0:T(8,128)(2,1)S(1)} %constant_dynamic-update-slice_fusion, bf16[192,3584]{1,0:T(8,128)(2,1)S(1)} %get-tuple-element.15), kind=kOutput, calls=%fused_computation.1 | convolution fusion | flops 1412956160 | bytes 9109504 | tf_op jit(solution)/shard_map/dot_general | solution.py:126
  104.6 0.6 collective-permute-start.20
  105.3 5.2 %convolution_convert_fusion = bf16[3584,1024]{1,0:T(8,128)(2,1)} fusion(bf16[192,3584]{1,0:T(8,128)(2,1)S(1)} %get-tuple-element.19, bf16[192,1024]{1,0:T(8,128)(2,1)S(1)} %copy-done.2), kind=kOutput, calls=%fused_computation | convolution fusion | flops 1412956160 | bytes 9109504 | tf_op jit(solution)/shard_map/dot_general | solution.py:8
  110.5 0.6 collective-permute-done.20
  111.1 0.7 add_convert_fusion.4
  (46 shorter events, 0.4 us)
Async XLA Ops:
  0.6 13.7 %collective-permute-start.1 = (bf16[48,1024]{1,0:T(8,128)(2,1)}, bf16[48,1024]{1,0:T(8,128)(2,1)S(1)}, u32[]{:S(2)}, u32[]{:S(2)}) collective-permute-start(bf16[48,1024]{1,0:T(8,128)(2,1)} %param.5), channel_id=1, source_target_pairs={{0,2},{1,3},{2,0},{3,1},{4,6},{5,7},{6,4},{7,5},{8,10},{9,11},{10,... | collective-permute-start | bytes 294920 | tf_op jit(solution)/shard_map/ppermute | solution.py:80
  4.8 7.7 %collective-permute-start = (bf16[48,1024]{1,0:T(8,128)(2,1)}, bf16[48,1024]{1,0:T(8,128)(2,1)S(1)}, u32[]{:S(2)}, u32[]{:S(2)}) collective-permute-start(bf16[48,1024]{1,0:T(8,128)(2,1)} %param.5), channel_id=1, source_target_pairs={{0,1},{1,2},{2,3},{3,0},{4,5},{5,6},{6,7},{7,4},{8,9},{9,10},{10,1... | collective-permute-start | bytes 294920 | tf_op jit(solution)/shard_map/ppermute | solution.py:80
  6.3 8.0 %collective-permute-start.2 = (bf16[48,1024]{1,0:T(8,128)(2,1)}, bf16[48,1024]{1,0:T(8,128)(2,1)S(1)}, u32[]{:S(2)}, u32[]{:S(2)}) collective-permute-start(bf16[48,1024]{1,0:T(8,128)(2,1)} %param.5), channel_id=1, source_target_pairs={{0,3},{1,0},{2,1},{3,2},{4,7},{5,4},{6,5},{7,6},{8,11},{9,8},{10,9... | collective-permute-start | bytes 294920 | tf_op jit(solution)/shard_map/ppermute | solution.py:80
  8.6 12.6 %collective-permute-start.4 = (bf16[48,1024]{1,0:T(8,128)(2,1)}, bf16[48,1024]{1,0:T(8,128)(2,1)S(1)}, u32[]{:S(2)}, u32[]{:S(2)}) collective-permute-start(bf16[48,1024]{1,0:T(8,128)(2,1)} %param.6), channel_id=1, source_target_pairs={{0,2},{1,3},{2,0},{3,1},{4,6},{5,7},{6,4},{7,5},{8,10},{9,11},{10,... | collective-permute-start | bytes 294920 | tf_op jit(solution)/shard_map/ppermute | solution.py:80
  8.6 12.6 %collective-permute-start.3 = (bf16[48,1024]{1,0:T(8,128)(2,1)}, bf16[48,1024]{1,0:T(8,128)(2,1)S(1)}, u32[]{:S(2)}, u32[]{:S(2)}) collective-permute-start(bf16[48,1024]{1,0:T(8,128)(2,1)} %param.6), channel_id=1, source_target_pairs={{0,1},{1,2},{2,3},{3,0},{4,5},{5,6},{6,7},{7,4},{8,9},{9,10},{10,1... | collective-permute-start | bytes 294920 | tf_op jit(solution)/shard_map/ppermute | solution.py:80
  12.4 9.7 %collective-permute-start.5 = (bf16[48,1024]{1,0:T(8,128)(2,1)}, bf16[48,1024]{1,0:T(8,128)(2,1)S(1)}, u32[]{:S(2)}, u32[]{:S(2)}) collective-permute-start(bf16[48,1024]{1,0:T(8,128)(2,1)} %param.6), channel_id=1, source_target_pairs={{0,3},{1,0},{2,1},{3,2},{4,7},{5,4},{6,5},{7,6},{8,11},{9,8},{10,9... | collective-permute-start | bytes 294920 | tf_op jit(solution)/shard_map/ppermute | solution.py:80
  14.3 5.2 %copy-start.3 = (bf16[1024,3584]{1,0:T(8,128)(2,1)S(1)}, bf16[1024,3584]{1,0:T(8,128)(2,1)}, u32[]{:S(2)}) copy-start(bf16[1024,3584]{1,0:T(8,128)(2,1)} %param.7) | copy-start | bytes 22020100
  14.3 7.8 %slice-start = ((s8[7340032]{0:T(1024)(128)(4,1)}), s8[4194304]{0:T(1024)(128)(4,1)S(1)}, s32[]{:S(2)}) async-start(s8[7340032]{0:T(1024)(128)(4,1)} %bitcast.28), calls=%async_computation | async-start | bytes 8388608
  19.5 2.6 %slice-start.1 = ((s8[7340032]{0:T(1024)(128)(4,1)}), s8[3145728]{0:T(1024)(128)(4,1)S(1)}, s32[]{:S(2)}) async-start(s8[7340032]{0:T(1024)(128)(4,1)} %bitcast.28), calls=%async_computation.1 | async-start | bytes 6291456
  22.2 2.6 %copy-start.1 = (bf16[192,1024]{1,0:T(8,128)(2,1)}, bf16[192,1024]{1,0:T(8,128)(2,1)S(1)}, u32[]{:S(2)}) copy-start(bf16[192,1024]{1,0:T(8,128)(2,1)S(1)} %constant_dynamic-update-slice_fusion.4) | copy-start | bytes 1179652
  25.5 2.2 %copy-start = (bf16[3,192,1792]{2,1,0:T(8,128)(2,1)}, bf16[3,192,1792]{2,1,0:T(8,128)(2,1)S(1)}, u32[]{:S(2)}) copy-start(bf16[3,192,1792]{2,1,0:T(8,128)(2,1)S(1)} %get-tuple-element.24) | copy-start | bytes 6193156
  26.7 3.0 %collective-permute-start.6 = (bf16[3,96,1792]{2,1,0:T(8,128)(2,1)}, bf16[3,96,1792]{2,1,0:T(8,128)(2,1)}, u32[]{:S(2)}, u32[]{:S(2)}) collective-permute-start(bf16[3,96,1792]{2,1,0:T(8,128)(2,1)} %constant_dynamic-slice_fusion.5), channel_id=1, source_target_pairs={{0,4},{4,0},{8,12},{12,8},{16,20},{20,16},{24,28},{28,24},{1,5},{5... | collective-permute-start | bytes 3096584 | tf_op jit(solution)/shard_map/ppermute | solution.py:37
  27.7 5.3 %collective-permute-start.12 = (bf16[3,96,1792]{2,1,0:T(8,128)(2,1)}, bf16[3,96,1792]{2,1,0:T(8,128)(2,1)S(1)}, u32[]{:S(2)}, u32[]{:S(2)}) collective-permute-start(bf16[3,96,1792]{2,1,0:T(8,128)(2,1)} %constant_dynamic-slice_fusion.2), channel_id=1, source_target_pairs={{0,4},{4,0},{8,12},{12,8},{16,20},{20,16},{24,28},{28,24},{1,5},{5... | collective-permute-start | bytes 3096584 | tf_op jit(solution)/shard_map/ppermute | solution.py:37
  31.5 13.9 %collective-permute-start.7 = (bf16[3,48,1792]{2,1,0:T(8,128)(2,1)S(1)}, bf16[3,48,1792]{2,1,0:T(8,128)(2,1)S(1)}, u32[]{:S(2)}, u32[]{:S(2)}) collective-permute-start(bf16[3,48,1792]{2,1,0:T(8,128)(2,1)S(1)} %constant_dynamic-slice_fusion.4), channel_id=1, source_target_pairs={{0,8},{4,12},{8,0},{12,4},{16,24},{20,28},{24,16},{28,20},{1,9},{5... | collective-permute-start | bytes 1548296 | tf_op jit(solution)/shard_map/ppermute | solution.py:37
  33.3 13.7 %collective-permute-start.13 = (bf16[3,48,1792]{2,1,0:T(8,128)(2,1)S(1)}, bf16[3,48,1792]{2,1,0:T(8,128)(2,1)S(1)}, u32[]{:S(2)}, u32[]{:S(2)}) collective-permute-start(bf16[3,48,1792]{2,1,0:T(8,128)(2,1)S(1)} %constant_dynamic-slice_fusion.1), channel_id=1, source_target_pairs={{0,16},{4,20},{8,24},{12,28},{16,0},{20,4},{24,8},{28,12},{1,17},{... | collective-permute-start | bytes 1548296 | tf_op jit(solution)/shard_map/ppermute | solution.py:37
  45.5 7.5 %collective-permute-start.8 = (bf16[3,24,1792]{2,1,0:T(8,128)(2,1)S(1)}, bf16[3,24,1792]{2,1,0:T(8,128)(2,1)S(1)}, u32[]{:S(2)}, u32[]{:S(2)}) collective-permute-start(bf16[3,24,1792]{2,1,0:T(8,128)(2,1)S(1)} %constant_dynamic-slice_fusion.3), channel_id=1, source_target_pairs={{0,16},{4,20},{8,24},{12,28},{16,0},{20,4},{24,8},{28,12},{1,17},{... | collective-permute-start | bytes 774152 | tf_op jit(solution)/shard_map/ppermute | solution.py:37
  47.2 7.5 %collective-permute-start.14 = (bf16[3,24,1792]{2,1,0:T(8,128)(2,1)S(1)}, bf16[3,24,1792]{2,1,0:T(8,128)(2,1)S(1)}, u32[]{:S(2)}, u32[]{:S(2)}) collective-permute-start(bf16[3,24,1792]{2,1,0:T(8,128)(2,1)S(1)} %constant_dynamic-slice_fusion), channel_id=1, source_target_pairs={{0,8},{4,12},{8,0},{12,4},{16,24},{20,28},{24,16},{28,20},{1,9},{5... | collective-permute-start | bytes 774152 | tf_op jit(solution)/shard_map/ppermute | solution.py:37
  53.2 6.6 %collective-permute-start.9 = (bf16[3,24,1792]{2,1,0:T(8,128)(2,1)S(1)}, bf16[3,24,1792]{2,1,0:T(8,128)(2,1)S(1)}, u32[]{:S(2)}, u32[]{:S(2)}) collective-permute-start(bf16[3,24,1792]{2,1,0:T(8,128)(2,1)S(1)} %pad_maximum_fusion.2), channel_id=1, source_target_pairs={{0,16},{4,20},{8,24},{12,28},{16,0},{20,4},{24,8},{28,12},{1,17},{... | collective-permute-start | bytes 774152 | tf_op jit(solution)/shard_map/ppermute | solution.py:49
  54.9 7.6 %collective-permute-start.15 = (bf16[3,24,1792]{2,1,0:T(8,128)(2,1)S(1)}, bf16[3,24,1792]{2,1,0:T(8,128)(2,1)S(1)}, u32[]{:S(2)}, u32[]{:S(2)}) collective-permute-start(bf16[3,24,1792]{2,1,0:T(8,128)(2,1)S(1)} %pad_maximum_fusion.3), channel_id=1, source_target_pairs={{0,8},{4,12},{8,0},{12,4},{16,24},{20,28},{24,16},{28,20},{1,9},{5... | collective-permute-start | bytes 774152 | tf_op jit(solution)/shard_map/ppermute | solution.py:49
  59.9 12.5 %collective-permute-start.10 = (bf16[3,48,1792]{2,1,0:T(8,128)(2,1)S(1)}, bf16[3,48,1792]{2,1,0:T(8,128)(2,1)S(1)}, u32[]{:S(2)}, u32[]{:S(2)}) collective-permute-start(bf16[3,48,1792]{2,1,0:T(8,128)(2,1)S(1)} %maximum_select_fusion.4), channel_id=1, source_target_pairs={{0,8},{4,12},{8,0},{12,4},{16,24},{20,28},{24,16},{28,20},{1,9},{5... | collective-permute-start | bytes 1548296 | tf_op jit(solution)/shard_map/ppermute | solution.py:49
  62.6 10.1 %collective-permute-start.16 = (bf16[3,48,1792]{2,1,0:T(8,128)(2,1)S(1)}, bf16[3,48,1792]{2,1,0:T(8,128)(2,1)S(1)}, u32[]{:S(2)}, u32[]{:S(2)}) collective-permute-start(bf16[3,48,1792]{2,1,0:T(8,128)(2,1)S(1)} %maximum_select_fusion.5), channel_id=1, source_target_pairs={{0,16},{4,20},{8,24},{12,28},{16,0},{20,4},{24,8},{28,12},{1,17},{... | collective-permute-start | bytes 1548296 | tf_op jit(solution)/shard_map/ppermute | solution.py:49
  72.6 2.7 %collective-permute-start.11 = (bf16[3,96,1792]{2,1,0:T(8,128)(2,1)S(1)}, bf16[3,96,1792]{2,1,0:T(8,128)(2,1)S(1)}, u32[]{:S(2)}, u32[]{:S(2)}) collective-permute-start(bf16[3,96,1792]{2,1,0:T(8,128)(2,1)S(1)} %maximum_select_fusion.2), channel_id=1, source_target_pairs={{0,4},{4,0},{8,12},{12,8},{16,20},{20,16},{24,28},{28,24},{1,5},{5... | collective-permute-start | bytes 3096584 | tf_op jit(solution)/shard_map/ppermute | solution.py:49
  73.0 4.0 %collective-permute-start.17 = (bf16[3,96,1792]{2,1,0:T(8,128)(2,1)S(1)}, bf16[3,96,1792]{2,1,0:T(8,128)(2,1)}, u32[]{:S(2)}, u32[]{:S(2)}) collective-permute-start(bf16[3,96,1792]{2,1,0:T(8,128)(2,1)S(1)} %maximum_select_fusion.3), channel_id=1, source_target_pairs={{0,4},{4,0},{8,12},{12,8},{16,20},{20,16},{24,28},{28,24},{1,5},{5... | collective-permute-start | bytes 3096584 | tf_op jit(solution)/shard_map/ppermute | solution.py:49
  75.3 4.1 %slice-start.2 = ((s8[7340032]{0:T(1024)(128)(4,1)}), s8[4194304]{0:T(1024)(128)(4,1)S(1)}, s32[]{:S(2)}) async-start(s8[7340032]{0:T(1024)(128)(4,1)} %bitcast.30), calls=%async_computation.2 | async-start | bytes 8388608
  79.0 1.9 %slice-start.3 = ((s8[7340032]{0:T(1024)(128)(4,1)}), s8[3145728]{0:T(1024)(128)(4,1)S(1)}, s32[]{:S(2)}) async-start(s8[7340032]{0:T(1024)(128)(4,1)} %bitcast.30), calls=%async_computation.3 | async-start | bytes 6291456
  79.0 4.4 %slice-start.4 = ((s8[7340032]{0:T(1024)(128)(4,1)}), s8[4194304]{0:T(1024)(128)(4,1)S(1)}, s32[]{:S(2)}) async-start(s8[7340032]{0:T(1024)(128)(4,1)} %bitcast.32), calls=%async_computation.4 | async-start | bytes 8388608
  80.9 2.5 %slice-start.5 = ((s8[7340032]{0:T(1024)(128)(4,1)}), s8[3145728]{0:T(1024)(128)(4,1)S(1)}, s32[]{:S(2)}) async-start(s8[7340032]{0:T(1024)(128)(4,1)} %bitcast.32), calls=%async_computation.5 | async-start | bytes 6291456
  86.0 24.5 %collective-permute-start.18 = (bf16[48,1024]{1,0:T(8,128)(2,1)S(1)}, bf16[48,1024]{1,0:T(8,128)(2,1)S(1)}, u32[]{:S(2)}, u32[]{:S(2)}) collective-permute-start(bf16[48,1024]{1,0:T(8,128)(2,1)S(1)} %slice.57), channel_id=1, source_target_pairs={{0,3},{1,0},{2,1},{3,2},{4,7},{5,4},{6,5},{7,6},{8,11},{9,8},{10,9... | collective-permute-start | bytes 294920 | tf_op jit(solution)/shard_map/ppermute | solution.py:121
  99.4 5.9 %copy-start.2 = (bf16[192,1024]{1,0:T(8,128)(2,1)S(1)}, bf16[192,1024]{1,0:T(8,128)(2,1)}, u32[]{:S(2)}) copy-start(bf16[192,1024]{1,0:T(8,128)(2,1)} %copy-done.1) | copy-start | bytes 1179652
  99.4 11.1 %collective-permute-start.19 = (bf16[48,1024]{1,0:T(8,128)(2,1)S(1)}, bf16[48,1024]{1,0:T(8,128)(2,1)S(1)}, u32[]{:S(2)}, u32[]{:S(2)}) collective-permute-start(bf16[48,1024]{1,0:T(8,128)(2,1)S(1)} %slice.58), channel_id=1, source_target_pairs={{0,2},{1,3},{2,0},{3,1},{4,6},{5,7},{6,4},{7,5},{8,10},{9,11},{10,... | collective-permute-start | bytes 294920 | tf_op jit(solution)/shard_map/ppermute | solution.py:121
  104.6 6.5 %collective-permute-start.20 = (bf16[48,1024]{1,0:T(8,128)(2,1)S(1)}, bf16[48,1024]{1,0:T(8,128)(2,1)S(1)}, u32[]{:S(2)}, u32[]{:S(2)}) collective-permute-start(bf16[48,1024]{1,0:T(8,128)(2,1)S(1)} %slice.59), channel_id=1, source_target_pairs={{0,1},{1,2},{2,3},{3,0},{4,5},{5,6},{6,7},{7,4},{8,9},{9,10},{10,1... | collective-permute-start | bytes 294920 | tf_op jit(solution)/shard_map/ppermute | solution.py:121

commit v12 on v6

--- a/solution.py
+++ b/solution.py
@@ -94,6 +94,7 @@
     n_row = lax.psum(1, "row")
     n_col = lax.psum(1, "col")
     tok_all = col_gather(tokens, n_col)
+    grad_out, tok_all = lax.optimization_barrier((grad_out, tok_all))
     grad_all = col_gather(grad_out, n_col)
     tok_t = tok_all.T
     stacked = jnp.stack(

time: 112 us -> 111 us (level)
  waiting for transfers between devices: 34.7 us -> 38.2 us
  starting transfers between devices: 31.7 us -> 29.4 us
  local copies, waits for them, and re-layouts: 6.29 us -> 4.17 us
    ppermute x3, starting transfers between devices: 8.85 us -> 3.53 us  [col_reduce_scatter(): lax.ppermute(x[s * span:(s + 1) * span], 'col', [(j, (j - s) % n_col) for...]
    ppermute x6, waiting for transfers between devices: 2.39 us -> 5.91 us  [col_gather(): lax.ppermute(x, 'col', [(j, (j + s) % n_col) for j in range(n_col)])]
    ppermute x6, starting transfers between devices: 10.4 us -> 13.2 us  [col_gather(): lax.ppermute(x, 'col', [(j, (j + s) % n_col) for j in range(n_col)])]
    unnamed x26 -> x27, local copies, waits for them, and re-layouts: 3.68 us -> 1.57 us
  transfers between devices with their start and end apart: 21 -> 21, of which waited for: 10 -> 12; matrix products, arithmetic and copies ran while one was open for 22% -> 20% of each run, Pallas kernels for 0% -> 0%
where the time goes in v12:
time: 111 us
  waiting for transfers between devices  38.2 us (34%)
  matrix products  29.6 us (27%)
  starting transfers between devices  29.4 us (26%)
  other arithmetic  9.01 us (8%)
  local copies, waits for them, and re-layouts  4.17 us (4%)
    ppermute x6, waiting for transfers between devices, doubling_gather(): got = lax.ppermute(cur, 'row', [(j, j ^ bit) for j in range(n_dev)])  16.2 us
    ppermute x6, waiting for transfers between devices, halving_reduce(): got = lax.ppermute(send, 'row', [(j, j ^ bit) for j in range(n_dev)])  16 us
    ppermute x6, starting transfers between devices, col_gather(): lax.ppermute(x, 'col', [(j, (j + s) % n_col) for j in range(n_col)])  13.2 us
    dot_general x3, matrix products, contract_last(): lax.dot_general(left, right, (((1,), (1,)), ((), ())), preferred_element_...  7.58 us
    ppermute x6, starting transfers between devices, halving_reduce(): got = lax.ppermute(send, 'row', [(j, j ^ bit) for j in range(n_dev)])  6.78 us
    ppermute x6, waiting for transfers between devices, col_gather(): lax.ppermute(x, 'col', [(j, (j + s) % n_col) for j in range(n_col)])  5.91 us
    ppermute x6, starting transfers between devices, doubling_gather(): got = lax.ppermute(cur, 'row', [(j, j ^ bit) for j in range(n_dev)])  5.86 us
    dot_general x1, matrix products, contract_first(): lax.dot_general(left, right, (((0,), (0,)), ((), ())), preferred_element_...  5.19 us
  transfers between devices with their start and end apart: 21, of which 12 were waited for; matrix products, arithmetic and copies ran while one was open for 20% of the time, Pallas kernels for 0%

profile of v12, /device:TPU:0, one launch (start us, length us, event | category | flops | bytes accessed | tf_op | source)
XLA Modules:
  0.0 111.3 jit_solution(14734984638489077977)
XLA Ops:
  0.6 4.1 %collective-permute-start.1 = (bf16[48,1024]{1,0:T(8,128)(2,1)}, bf16[48,1024]{1,0:T(8,128)(2,1)S(1)}, u32[]{:S(2)}, u32[]{:S(2)}) collective-permute-start(bf16[48,1024]{1,0:T(8,128)(2,1)} %param.5), channel_id=1, source_target_pairs={{0,2},{1,3},{2,0},{3,1},{4,6},{5,7},{6,4},{7,5},{8,10},{9,11},{10,... | collective-permute-start | bytes 294920 | tf_op jit(solution)/shard_map/ppermute | solution.py:80
  4.8 1.6 %collective-permute-start = (bf16[48,1024]{1,0:T(8,128)(2,1)}, bf16[48,1024]{1,0:T(8,128)(2,1)S(1)}, u32[]{:S(2)}, u32[]{:S(2)}) collective-permute-start(bf16[48,1024]{1,0:T(8,128)(2,1)} %param.5), channel_id=1, source_target_pairs={{0,1},{1,2},{2,3},{3,0},{4,5},{5,6},{6,7},{7,4},{8,9},{9,10},{10,1... | collective-permute-start | bytes 294920 | tf_op jit(solution)/shard_map/ppermute | solution.py:80
  6.3 2.2 %collective-permute-start.2 = (bf16[48,1024]{1,0:T(8,128)(2,1)}, bf16[48,1024]{1,0:T(8,128)(2,1)S(1)}, u32[]{:S(2)}, u32[]{:S(2)}) collective-permute-start(bf16[48,1024]{1,0:T(8,128)(2,1)} %param.5), channel_id=1, source_target_pairs={{0,3},{1,0},{2,1},{3,2},{4,7},{5,4},{6,5},{7,6},{8,11},{9,8},{10,9... | collective-permute-start | bytes 294920 | tf_op jit(solution)/shard_map/ppermute | solution.py:80
  8.6 4.3 %collective-permute-done.1 = bf16[48,1024]{1,0:T(8,128)(2,1)S(1)} collective-permute-done((bf16[48,1024]{1,0:T(8,128)(2,1)}, bf16[48,1024]{1,0:T(8,128)(2,1)S(1)}, u32[]{:S(2)}, u32[]{:S(2)}) %collective-permute-start.1) | collective-permute-done | bytes 98336 | tf_op jit(solution)/shard_map/ppermute | solution.py:80
  12.9 0.7 collective-permute-done.2
  13.6 1.1 pad_maximum_fusion.2
  14.6 0.0 slice-start.5
  14.7 2.1 %collective-permute-start.5 = (bf16[48,1024]{1,0:T(8,128)(2,1)}, bf16[48,1024]{1,0:T(8,128)(2,1)S(1)}, u32[]{:S(2)}, u32[]{:S(2)}) collective-permute-start(bf16[48,1024]{1,0:T(8,128)(2,1)} %param.6), channel_id=1, source_target_pairs={{0,3},{1,0},{2,1},{3,2},{4,7},{5,4},{6,5},{7,6},{8,11},{9,8},{10,9... | collective-permute-start | bytes 294920 | tf_op jit(solution)/shard_map/ppermute | solution.py:80
  16.8 1.2 %collective-permute-start.4 = (bf16[48,1024]{1,0:T(8,128)(2,1)}, bf16[48,1024]{1,0:T(8,128)(2,1)S(1)}, u32[]{:S(2)}, u32[]{:S(2)}) collective-permute-start(bf16[48,1024]{1,0:T(8,128)(2,1)} %param.6), channel_id=1, source_target_pairs={{0,2},{1,3},{2,0},{3,1},{4,6},{5,7},{6,4},{7,5},{8,10},{9,11},{10,... | collective-permute-start | bytes 294920 | tf_op jit(solution)/shard_map/ppermute | solution.py:80
  17.9 1.9 %collective-permute-start.3 = (bf16[48,1024]{1,0:T(8,128)(2,1)}, bf16[48,1024]{1,0:T(8,128)(2,1)S(1)}, u32[]{:S(2)}, u32[]{:S(2)}) collective-permute-start(bf16[48,1024]{1,0:T(8,128)(2,1)} %param.6), channel_id=1, source_target_pairs={{0,1},{1,2},{2,3},{3,0},{4,5},{5,6},{6,7},{7,4},{8,9},{9,10},{10,1... | collective-permute-start | bytes 294920 | tf_op jit(solution)/shard_map/ppermute | solution.py:80
  19.9 4.8 %fusion.1 = bf16[1,192,3584]{2,1,0:T(8,128)(2,1)S(1)} fusion(bf16[192,1024]{1,0:T(8,128)(2,1)S(1)} %pad_maximum_fusion.2, bf16[1024,3584]{1,0:T(8,128)(2,1)} %param.8), kind=kOutput, calls=%fused_computation.7 | convolution fusion | flops 1409974272 | bytes 9109504 | tf_op jit(solution)/shard_map/dot_general | solution.py:103
  24.8 0.0 slice-start.1
  24.8 1.6 %fusion = bf16[1,192,3584]{2,1,0:T(8,128)(2,1)S(1)} fusion(bf16[192,1024]{1,0:T(8,128)(2,1)S(1)} %pad_maximum_fusion.2, bf16[1024,3584]{1,0:T(8,128)(2,1)S(1)} %bitcast.33), kind=kOutput, calls=%fused_computation.6 | convolution fusion | flops 1409974272 | bytes 9109504 | tf_op jit(solution)/shard_map/dot_general | solution.py:102
  26.4 0.1 collective-permute-done.3
  26.6 0.8 collective-permute-done.4
  27.5 2.6 %fusion.2 = bf16[1,192,3584]{2,1,0:T(8,128)(2,1)S(1)} fusion(bf16[192,1024]{1,0:T(8,128)(2,1)S(1)} %constant_dynamic-update-slice_fusion, bf16[3584,1024]{1,0:T(8,128)(2,1)S(1)} %bitcast.29), kind=kOutput, calls=%fused_computation.8 | convolution fusion | flops 1409974272 | bytes 9109504 | tf_op jit(solution)/shard_map/dot_general | solution.py:14
  30.0 0.7 pad_maximum_fusion
  30.7 0.3 fusion.9
  31.0 1.1 %constant_dynamic-slice_fusion.5 = bf16[3,96,1792]{2,1,0:T(8,128)(2,1)} fusion(bf16[3,192,1792]{2,1,0:T(8,128)(2,1)S(1)} %get-tuple-element.28, s32[]{:T(128)S(6)} %select_n.131), kind=kLoop, calls=%fused_computation.55 | loop fusion | bytes 2064388 | tf_op jit(solution)/shard_map/dynamic_slice | solution.py:36
  32.1 1.0 constant_dynamic-slice_fusion.2
  33.2 0.5 collective-permute-start.12
  33.7 1.4 %collective-permute-done.6 = bf16[3,96,1792]{2,1,0:T(8,128)(2,1)} collective-permute-done((bf16[3,96,1792]{2,1,0:T(8,128)(2,1)}, bf16[3,96,1792]{2,1,0:T(8,128)(2,1)}, u32[]{:S(2)}, u32[]{:S(2)}) %collective-permute-start.6) | collective-permute-done | bytes 1032224 | tf_op jit(solution)/shard_map/ppermute | solution.py:37
  35.1 1.8 %add_convert_fusion.1 = bf16[3,96,1792]{2,1,0:T(8,128)(2,1)S(1)} fusion(bf16[3,96,1792]{2,1,0:T(8,128)(2,1)} %collective-permute-done.6, bf16[3,192,1792]{2,1,0:T(8,128)(2,1)} %copy-done, s32[]{:T(128)S(6)} %select_n.130), kind=kLoop, calls=%fused_computation.17 | loop fusion | flops 2064384 | bytes 3096580 | tf_op jit(solution)/shard_map/convert_element_type | solution.py:40
  36.9 1.6 %collective-permute-start.7 = (bf16[3,48,1792]{2,1,0:T(8,128)(2,1)S(1)}, bf16[3,48,1792]{2,1,0:T(8,128)(2,1)S(1)}, u32[]{:S(2)}, u32[]{:S(2)}) collective-permute-start(bf16[3,48,1792]{2,1,0:T(8,128)(2,1)S(1)} %constant_dynamic-slice_fusion.4), channel_id=1, source_target_pairs={{0,8},{4,12},{8,0},{12,4},{16,24},{20,28},{24,16},{28,20},{1,9},{5... | collective-permute-start | bytes 1548296 | tf_op jit(solution)/shard_map/ppermute | solution.py:37
  38.5 0.3 add_convert_fusion
  38.8 1.6 %collective-permute-start.13 = (bf16[3,48,1792]{2,1,0:T(8,128)(2,1)S(1)}, bf16[3,48,1792]{2,1,0:T(8,128)(2,1)S(1)}, u32[]{:S(2)}, u32[]{:S(2)}) collective-permute-start(bf16[3,48,1792]{2,1,0:T(8,128)(2,1)S(1)} %constant_dynamic-slice_fusion.1), channel_id=1, source_target_pairs={{0,16},{4,20},{8,24},{12,28},{16,0},{20,4},{24,8},{28,12},{1,17},{... | collective-permute-start | bytes 1548296 | tf_op jit(solution)/shard_map/ppermute | solution.py:37
  40.4 10.4 %collective-permute-done.7 = bf16[3,48,1792]{2,1,0:T(8,128)(2,1)S(1)} collective-permute-done((bf16[3,48,1792]{2,1,0:T(8,128)(2,1)S(1)}, bf16[3,48,1792]{2,1,0:T(8,128)(2,1)S(1)}, u32[]{:S(2)}, u32[]{:S(2)}) %collective-permute-start.7) | collective-permute-done | bytes 516128 | tf_op jit(solution)/shard_map/ppermute | solution.py:37
  50.8 0.1 add_convert_fusion.3
  51.0 1.6 %collective-permute-start.8 = (bf16[3,24,1792]{2,1,0:T(8,128)(2,1)S(1)}, bf16[3,24,1792]{2,1,0:T(8,128)(2,1)S(1)}, u32[]{:S(2)}, u32[]{:S(2)}) collective-permute-start(bf16[3,24,1792]{2,1,0:T(8,128)(2,1)S(1)} %constant_dynamic-slice_fusion.3), channel_id=1, source_target_pairs={{0,16},{4,20},{8,24},{12,28},{16,0},{20,4},{24,8},{28,12},{1,17},{... | collective-permute-start | bytes 774152 | tf_op jit(solution)/shard_map/ppermute | solution.py:37
  52.6 0.1 add_convert_fusion.2
  52.7 1.5 %collective-permute-start.14 = (bf16[3,24,1792]{2,1,0:T(8,128)(2,1)S(1)}, bf16[3,24,1792]{2,1,0:T(8,128)(2,1)S(1)}, u32[]{:S(2)}, u32[]{:S(2)}) collective-permute-start(bf16[3,24,1792]{2,1,0:T(8,128)(2,1)S(1)} %constant_dynamic-slice_fusion), channel_id=1, source_target_pairs={{0,8},{4,12},{8,0},{12,4},{16,24},{20,28},{24,16},{28,20},{1,9},{5... | collective-permute-start | bytes 774152 | tf_op jit(solution)/shard_map/ppermute | solution.py:37
  54.3 4.2 %collective-permute-done.8 = bf16[3,24,1792]{2,1,0:T(8,128)(2,1)S(1)} collective-permute-done((bf16[3,24,1792]{2,1,0:T(8,128)(2,1)S(1)}, bf16[3,24,1792]{2,1,0:T(8,128)(2,1)S(1)}, u32[]{:S(2)}, u32[]{:S(2)}) %collective-permute-start.8) | collective-permute-done | bytes 258080 | tf_op jit(solution)/shard_map/ppermute | solution.py:37
  58.4 0.1 convert_add_fusion.1
  58.5 0.1 multiply_convert_fusion.5
  58.6 1.6 %collective-permute-start.9 = (bf16[3,24,1792]{2,1,0:T(8,128)(2,1)S(1)}, bf16[3,24,1792]{2,1,0:T(8,128)(2,1)S(1)}, u32[]{:S(2)}, u32[]{:S(2)}) collective-permute-start(bf16[3,24,1792]{2,1,0:T(8,128)(2,1)S(1)} %pad_maximum_fusion.3), channel_id=1, source_target_pairs={{0,16},{4,20},{8,24},{12,28},{16,0},{20,4},{24,8},{28,12},{1,17},{... | collective-permute-start | bytes 774152 | tf_op jit(solution)/shard_map/ppermute | solution.py:49
  60.2 0.1 convert_add_fusion
  60.3 0.1 multiply_convert_fusion.2
  60.4 1.5 %collective-permute-start.15 = (bf16[3,24,1792]{2,1,0:T(8,128)(2,1)S(1)}, bf16[3,24,1792]{2,1,0:T(8,128)(2,1)S(1)}, u32[]{:S(2)}, u32[]{:S(2)}) collective-permute-start(bf16[3,24,1792]{2,1,0:T(8,128)(2,1)S(1)} %pad_maximum_fusion.4), channel_id=1, source_target_pairs={{0,8},{4,12},{8,0},{12,4},{16,24},{20,28},{24,16},{28,20},{1,9},{5... | collective-permute-start | bytes 774152 | tf_op jit(solution)/shard_map/ppermute | solution.py:49
  62.0 3.3 %collective-permute-done.9 = bf16[3,24,1792]{2,1,0:T(8,128)(2,1)S(1)} collective-permute-done((bf16[3,24,1792]{2,1,0:T(8,128)(2,1)S(1)}, bf16[3,24,1792]{2,1,0:T(8,128)(2,1)S(1)}, u32[]{:S(2)}, u32[]{:S(2)}) %collective-permute-start.9) | collective-permute-done | bytes 258080 | tf_op jit(solution)/shard_map/ppermute | solution.py:49
  65.3 0.1 maximum_select_fusion.4
  65.4 1.5 %collective-permute-start.10 = (bf16[3,48,1792]{2,1,0:T(8,128)(2,1)S(1)}, bf16[3,48,1792]{2,1,0:T(8,128)(2,1)S(1)}, u32[]{:S(2)}, u32[]{:S(2)}) collective-permute-start(bf16[3,48,1792]{2,1,0:T(8,128)(2,1)S(1)} %maximum_select_fusion.4), channel_id=1, source_target_pairs={{0,8},{4,12},{8,0},{12,4},{16,24},{20,28},{24,16},{28,20},{1,9},{5... | collective-permute-start | bytes 1548296 | tf_op jit(solution)/shard_map/ppermute | solution.py:49
  66.9 1.2 %collective-permute-done.15 = bf16[3,24,1792]{2,1,0:T(8,128)(2,1)S(1)} collective-permute-done((bf16[3,24,1792]{2,1,0:T(8,128)(2,1)S(1)}, bf16[3,24,1792]{2,1,0:T(8,128)(2,1)S(1)}, u32[]{:S(2)}, u32[]{:S(2)}) %collective-permute-start.15) | collective-permute-done | bytes 258080 | tf_op jit(solution)/shard_map/ppermute | solution.py:49
  68.1 0.1 maximum_select_fusion.5
  68.2 0.6 collective-permute-start.16
  68.8 9.1 %collective-permute-done.10 = bf16[3,48,1792]{2,1,0:T(8,128)(2,1)S(1)} collective-permute-done((bf16[3,48,1792]{2,1,0:T(8,128)(2,1)S(1)}, bf16[3,48,1792]{2,1,0:T(8,128)(2,1)S(1)}, u32[]{:S(2)}, u32[]{:S(2)}) %collective-permute-start.10) | collective-permute-done | bytes 516128 | tf_op jit(solution)/shard_map/ppermute | solution.py:49
  77.9 0.3 maximum_select_fusion.2
  78.2 0.1 collective-permute-start.11
  78.2 0.3 maximum_select_fusion.3
  78.5 0.6 collective-permute-start.17
  79.1 1.8 %collective-permute-done.11 = bf16[3,96,1792]{2,1,0:T(8,128)(2,1)S(1)} collective-permute-done((bf16[3,96,1792]{2,1,0:T(8,128)(2,1)S(1)}, bf16[3,96,1792]{2,1,0:T(8,128)(2,1)S(1)}, u32[]{:S(2)}, u32[]{:S(2)}) %collective-permute-start.11) | collective-permute-done | bytes 1032224 | tf_op jit(solution)/shard_map/ppermute | solution.py:49
  80.9 0.8 maximum_select_fusion
  81.6 0.8 collective-permute-done.17
  82.5 2.0 %maximum_select_fusion.1 = bf16[3,192,1792]{2,1,0:T(8,128)(2,1)S(1)} fusion(bf16[3,96,1792]{2,1,0:T(8,128)(2,1)S(1)} %maximum_select_fusion.3, bf16[3,96,1792]{2,1,0:T(8,128)(2,1)} %collective-permute-done.17, pred[]{:T(512)S(6)} %eq.25), kind=kLoop, calls=%fused_computation.15 | loop fusion | flops 9289728 | bytes 4128769 | tf_op jit(solution)/shard_map/jit(_where)/select_n | solution.py:50
  84.5 0.4 fusion.7
  84.9 1.5 %slice-done.3 = s8[3145728]{0:T(1024)(128)(4,1)S(1)} async-done(((s8[7340032]{0:T(1024)(128)(4,1)}), s8[3145728]{0:T(1024)(128)(4,1)S(1)}, s32[]{:S(2)}) %slice-start.3) | async-done | bytes 3145752
  86.4 2.5 %fusion.11 = f32[192,1024]{1,0:T(8,128)S(1)} fusion(bf16[192,3584]{1,0:T(8,128)(2,1)S(1)} %get-tuple-element.22, bf16[1024,3584]{1,0:T(8,128)(2,1)S(1)} %bitcast.31), kind=kOutput, calls=%fused_computation.58 | convolution fusion | flops 1409286144 | bytes 9502720 | tf_op jit(solution)/shard_map/dot_general | solution.py:14
  89.0 2.5 %fusion.8 = bf16[192,1024]{1,0:T(8,128)(2,1)S(1)} fusion(f32[192,1024]{1,0:T(8,128)S(1)} %fusion.11, bf16[192,3584]{1,0:T(8,128)(2,1)S(1)} %get-tuple-element.17, bf16[1024,3584]{1,0:T(8,128)(2,1)S(1)} %bitcast.35), kind=kOutput, calls=%fused_computation.25 | convolution fusion | flops 1409679360 | bytes 9895936 | tf_op jit(solution)/shard_map/dot_general | solution.py:14
  91.5 5.2 %convolution_convert_fusion.2 = bf16[1024,3584]{1,0:T(8,128)(2,1)} fusion(bf16[192,1024]{1,0:T(8,128)(2,1)S(1)} %pad_maximum_fusion.2, bf16[192,3584]{1,0:T(8,128)(2,1)S(1)} %get-tuple-element.17), kind=kOutput, calls=%fused_computation.2 | convolution fusion | flops 1412956160 | bytes 9109504 | tf_op jit(solution)/shard_map/dot_general | solution.py:113
  96.7 1.2 %collective-permute-start.18 = (bf16[48,1024]{1,0:T(8,128)(2,1)S(1)}, bf16[48,1024]{1,0:T(8,128)(2,1)S(1)}, u32[]{:S(2)}, u32[]{:S(2)}) collective-permute-start(bf16[48,1024]{1,0:T(8,128)(2,1)S(1)} %get-tuple-element.35), channel_id=1, source_target_pairs={{0,3},{1,0},{2,1},{3,2},{4,7},{5,4},{6,5},{7,6},{8,11},{9,8},{10,9... | collective-permute-start | bytes 294920 | tf_op jit(solution)/shard_map/ppermute | solution.py:88
  97.9 0.9 collective-permute-start.20
  98.8 1.5 %collective-permute-start.19 = (bf16[48,1024]{1,0:T(8,128)(2,1)S(1)}, bf16[48,1024]{1,0:T(8,128)(2,1)S(1)}, u32[]{:S(2)}, u32[]{:S(2)}) collective-permute-start(bf16[48,1024]{1,0:T(8,128)(2,1)S(1)} %get-tuple-element.37), channel_id=1, source_target_pairs={{0,2},{1,3},{2,0},{3,1},{4,6},{5,7},{6,4},{7,5},{8,10},{9,11},{10,... | collective-permute-start | bytes 294920 | tf_op jit(solution)/shard_map/ppermute | solution.py:88
  100.2 5.2 %convolution_convert_fusion.1 = bf16[1024,3584]{1,0:T(8,128)(2,1)} fusion(bf16[192,1024]{1,0:T(8,128)(2,1)S(1)} %pad_maximum_fusion.2, bf16[192,3584]{1,0:T(8,128)(2,1)S(1)} %get-tuple-element.22), kind=kOutput, calls=%fused_computation.1 | convolution fusion | flops 1412956160 | bytes 9109504 | tf_op jit(solution)/shard_map/dot_general | solution.py:116
  105.4 5.2 %convolution_convert_fusion = bf16[3584,1024]{1,0:T(8,128)(2,1)} fusion(bf16[192,3584]{1,0:T(8,128)(2,1)S(1)} %get-tuple-element.23, bf16[192,1024]{1,0:T(8,128)(2,1)S(1)} %copy-done.2), kind=kOutput, calls=%fused_computation | convolution fusion | flops 1412956160 | bytes 9109504 | tf_op jit(solution)/shard_map/dot_general | solution.py:8
  110.6 0.7 add_convert_fusion.4
  (46 shorter events, 0.3 us)
Async XLA Ops:
  0.6 12.2 %collective-permute-start.1 = (bf16[48,1024]{1,0:T(8,128)(2,1)}, bf16[48,1024]{1,0:T(8,128)(2,1)S(1)}, u32[]{:S(2)}, u32[]{:S(2)}) collective-permute-start(bf16[48,1024]{1,0:T(8,128)(2,1)} %param.5), channel_id=1, source_target_pairs={{0,2},{1,3},{2,0},{3,1},{4,6},{5,7},{6,4},{7,5},{8,10},{9,11},{10,... | collective-permute-start | bytes 294920 | tf_op jit(solution)/shard_map/ppermute | solution.py:80
  4.8 8.1 %collective-permute-start = (bf16[48,1024]{1,0:T(8,128)(2,1)}, bf16[48,1024]{1,0:T(8,128)(2,1)S(1)}, u32[]{:S(2)}, u32[]{:S(2)}) collective-permute-start(bf16[48,1024]{1,0:T(8,128)(2,1)} %param.5), channel_id=1, source_target_pairs={{0,1},{1,2},{2,3},{3,0},{4,5},{5,6},{6,7},{7,4},{8,9},{9,10},{10,1... | collective-permute-start | bytes 294920 | tf_op jit(solution)/shard_map/ppermute | solution.py:80
  6.3 7.2 %collective-permute-start.2 = (bf16[48,1024]{1,0:T(8,128)(2,1)}, bf16[48,1024]{1,0:T(8,128)(2,1)S(1)}, u32[]{:S(2)}, u32[]{:S(2)}) collective-permute-start(bf16[48,1024]{1,0:T(8,128)(2,1)} %param.5), channel_id=1, source_target_pairs={{0,3},{1,0},{2,1},{3,2},{4,7},{5,4},{6,5},{7,6},{8,11},{9,8},{10,9... | collective-permute-start | bytes 294920 | tf_op jit(solution)/shard_map/ppermute | solution.py:80
  13.6 11.2 %slice-start.4 = ((s8[7340032]{0:T(1024)(128)(4,1)}), s8[4194304]{0:T(1024)(128)(4,1)S(1)}, s32[]{:S(2)}) async-start(s8[7340032]{0:T(1024)(128)(4,1)} %bitcast.32), calls=%async_computation.4 | async-start | bytes 8388608
  14.6 10.1 %slice-start.5 = ((s8[7340032]{0:T(1024)(128)(4,1)}), s8[3145728]{0:T(1024)(128)(4,1)S(1)}, s32[]{:S(2)}) async-start(s8[7340032]{0:T(1024)(128)(4,1)} %bitcast.32), calls=%async_computation.5 | async-start | bytes 6291456
  14.7 12.7 %collective-permute-start.5 = (bf16[48,1024]{1,0:T(8,128)(2,1)}, bf16[48,1024]{1,0:T(8,128)(2,1)S(1)}, u32[]{:S(2)}, u32[]{:S(2)}) collective-permute-start(bf16[48,1024]{1,0:T(8,128)(2,1)} %param.6), channel_id=1, source_target_pairs={{0,3},{1,0},{2,1},{3,2},{4,7},{5,4},{6,5},{7,6},{8,11},{9,8},{10,9... | collective-permute-start | bytes 294920 | tf_op jit(solution)/shard_map/ppermute | solution.py:80
  16.8 10.6 %collective-permute-start.4 = (bf16[48,1024]{1,0:T(8,128)(2,1)}, bf16[48,1024]{1,0:T(8,128)(2,1)S(1)}, u32[]{:S(2)}, u32[]{:S(2)}) collective-permute-start(bf16[48,1024]{1,0:T(8,128)(2,1)} %param.6), channel_id=1, source_target_pairs={{0,2},{1,3},{2,0},{3,1},{4,6},{5,7},{6,4},{7,5},{8,10},{9,11},{10,... | collective-permute-start | bytes 294920 | tf_op jit(solution)/shard_map/ppermute | solution.py:80
  17.9 8.6 %collective-permute-start.3 = (bf16[48,1024]{1,0:T(8,128)(2,1)}, bf16[48,1024]{1,0:T(8,128)(2,1)S(1)}, u32[]{:S(2)}, u32[]{:S(2)}) collective-permute-start(bf16[48,1024]{1,0:T(8,128)(2,1)} %param.6), channel_id=1, source_target_pairs={{0,1},{1,2},{2,3},{3,0},{4,5},{5,6},{6,7},{7,4},{8,9},{9,10},{10,1... | collective-permute-start | bytes 294920 | tf_op jit(solution)/shard_map/ppermute | solution.py:80
  19.9 7.5 %slice-start = ((s8[7340032]{0:T(1024)(128)(4,1)}), s8[4194304]{0:T(1024)(128)(4,1)S(1)}, s32[]{:S(2)}) async-start(s8[7340032]{0:T(1024)(128)(4,1)} %bitcast.28), calls=%async_computation | async-start | bytes 8388608
  24.8 1.7 %copy-start.3 = (bf16[48,1024]{1,0:T(8,128)(2,1)S(1)}, bf16[48,1024]{1,0:T(8,128)(2,1)}, u32[]{:S(2)}) copy-start(bf16[48,1024]{1,0:T(8,128)(2,1)} %param.6) | copy-start | bytes 294916
  24.8 2.7 %slice-start.1 = ((s8[7340032]{0:T(1024)(128)(4,1)}), s8[3145728]{0:T(1024)(128)(4,1)S(1)}, s32[]{:S(2)}) async-start(s8[7340032]{0:T(1024)(128)(4,1)} %bitcast.28), calls=%async_computation.1 | async-start | bytes 6291456
  27.4 2.6 %copy-start.1 = (bf16[192,1024]{1,0:T(8,128)(2,1)}, bf16[192,1024]{1,0:T(8,128)(2,1)S(1)}, u32[]{:S(2)}) copy-start(bf16[192,1024]{1,0:T(8,128)(2,1)S(1)} %constant_dynamic-update-slice_fusion) | copy-start | bytes 1179652
  31.0 2.2 %copy-start = (bf16[3,192,1792]{2,1,0:T(8,128)(2,1)}, bf16[3,192,1792]{2,1,0:T(8,128)(2,1)S(1)}, u32[]{:S(2)}) copy-start(bf16[3,192,1792]{2,1,0:T(8,128)(2,1)S(1)} %get-tuple-element.28) | copy-start | bytes 6193156
  32.1 3.0 %collective-permute-start.6 = (bf16[3,96,1792]{2,1,0:T(8,128)(2,1)}, bf16[3,96,1792]{2,1,0:T(8,128)(2,1)}, u32[]{:S(2)}, u32[]{:S(2)}) collective-permute-start(bf16[3,96,1792]{2,1,0:T(8,128)(2,1)} %constant_dynamic-slice_fusion.5), channel_id=1, source_target_pairs={{0,4},{4,0},{8,12},{12,8},{16,20},{20,16},{24,28},{28,24},{1,5},{5... | collective-permute-start | bytes 3096584 | tf_op jit(solution)/shard_map/ppermute | solution.py:37
  33.2 5.3 %collective-permute-start.12 = (bf16[3,96,1792]{2,1,0:T(8,128)(2,1)}, bf16[3,96,1792]{2,1,0:T(8,128)(2,1)S(1)}, u32[]{:S(2)}, u32[]{:S(2)}) collective-permute-start(bf16[3,96,1792]{2,1,0:T(8,128)(2,1)} %constant_dynamic-slice_fusion.2), channel_id=1, source_target_pairs={{0,4},{4,0},{8,12},{12,8},{16,20},{20,16},{24,28},{28,24},{1,5},{5... | collective-permute-start | bytes 3096584 | tf_op jit(solution)/shard_map/ppermute | solution.py:37
  36.9 13.9 %collective-permute-start.7 = (bf16[3,48,1792]{2,1,0:T(8,128)(2,1)S(1)}, bf16[3,48,1792]{2,1,0:T(8,128)(2,1)S(1)}, u32[]{:S(2)}, u32[]{:S(2)}) collective-permute-start(bf16[3,48,1792]{2,1,0:T(8,128)(2,1)S(1)} %constant_dynamic-slice_fusion.4), channel_id=1, source_target_pairs={{0,8},{4,12},{8,0},{12,4},{16,24},{20,28},{24,16},{28,20},{1,9},{5... | collective-permute-start | bytes 1548296 | tf_op jit(solution)/shard_map/ppermute | solution.py:37
  38.8 13.7 %collective-permute-start.13 = (bf16[3,48,1792]{2,1,0:T(8,128)(2,1)S(1)}, bf16[3,48,1792]{2,1,0:T(8,128)(2,1)S(1)}, u32[]{:S(2)}, u32[]{:S(2)}) collective-permute-start(bf16[3,48,1792]{2,1,0:T(8,128)(2,1)S(1)} %constant_dynamic-slice_fusion.1), channel_id=1, source_target_pairs={{0,16},{4,20},{8,24},{12,28},{16,0},{20,4},{24,8},{28,12},{1,17},{... | collective-permute-start | bytes 1548296 | tf_op jit(solution)/shard_map/ppermute | solution.py:37
  51.0 7.5 %collective-permute-start.8 = (bf16[3,24,1792]{2,1,0:T(8,128)(2,1)S(1)}, bf16[3,24,1792]{2,1,0:T(8,128)(2,1)S(1)}, u32[]{:S(2)}, u32[]{:S(2)}) collective-permute-start(bf16[3,24,1792]{2,1,0:T(8,128)(2,1)S(1)} %constant_dynamic-slice_fusion.3), channel_id=1, source_target_pairs={{0,16},{4,20},{8,24},{12,28},{16,0},{20,4},{24,8},{28,12},{1,17},{... | collective-permute-start | bytes 774152 | tf_op jit(solution)/shard_map/ppermute | solution.py:37
  52.7 7.5 %collective-permute-start.14 = (bf16[3,24,1792]{2,1,0:T(8,128)(2,1)S(1)}, bf16[3,24,1792]{2,1,0:T(8,128)(2,1)S(1)}, u32[]{:S(2)}, u32[]{:S(2)}) collective-permute-start(bf16[3,24,1792]{2,1,0:T(8,128)(2,1)S(1)} %constant_dynamic-slice_fusion), channel_id=1, source_target_pairs={{0,8},{4,12},{8,0},{12,4},{16,24},{20,28},{24,16},{28,20},{1,9},{5... | collective-permute-start | bytes 774152 | tf_op jit(solution)/shard_map/ppermute | solution.py:37
  58.6 6.6 %collective-permute-start.9 = (bf16[3,24,1792]{2,1,0:T(8,128)(2,1)S(1)}, bf16[3,24,1792]{2,1,0:T(8,128)(2,1)S(1)}, u32[]{:S(2)}, u32[]{:S(2)}) collective-permute-start(bf16[3,24,1792]{2,1,0:T(8,128)(2,1)S(1)} %pad_maximum_fusion.3), channel_id=1, source_target_pairs={{0,16},{4,20},{8,24},{12,28},{16,0},{20,4},{24,8},{28,12},{1,17},{... | collective-permute-start | bytes 774152 | tf_op jit(solution)/shard_map/ppermute | solution.py:49
  60.4 7.6 %collective-permute-start.15 = (bf16[3,24,1792]{2,1,0:T(8,128)(2,1)S(1)}, bf16[3,24,1792]{2,1,0:T(8,128)(2,1)S(1)}, u32[]{:S(2)}, u32[]{:S(2)}) collective-permute-start(bf16[3,24,1792]{2,1,0:T(8,128)(2,1)S(1)} %pad_maximum_fusion.4), channel_id=1, source_target_pairs={{0,8},{4,12},{8,0},{12,4},{16,24},{20,28},{24,16},{28,20},{1,9},{5... | collective-permute-start | bytes 774152 | tf_op jit(solution)/shard_map/ppermute | solution.py:49
  65.4 12.5 %collective-permute-start.10 = (bf16[3,48,1792]{2,1,0:T(8,128)(2,1)S(1)}, bf16[3,48,1792]{2,1,0:T(8,128)(2,1)S(1)}, u32[]{:S(2)}, u32[]{:S(2)}) collective-permute-start(bf16[3,48,1792]{2,1,0:T(8,128)(2,1)S(1)} %maximum_select_fusion.4), channel_id=1, source_target_pairs={{0,8},{4,12},{8,0},{12,4},{16,24},{20,28},{24,16},{28,20},{1,9},{5... | collective-permute-start | bytes 1548296 | tf_op jit(solution)/shard_map/ppermute | solution.py:49
  68.2 10.1 %collective-permute-start.16 = (bf16[3,48,1792]{2,1,0:T(8,128)(2,1)S(1)}, bf16[3,48,1792]{2,1,0:T(8,128)(2,1)S(1)}, u32[]{:S(2)}, u32[]{:S(2)}) collective-permute-start(bf16[3,48,1792]{2,1,0:T(8,128)(2,1)S(1)} %maximum_select_fusion.5), channel_id=1, source_target_pairs={{0,16},{4,20},{8,24},{12,28},{16,0},{20,4},{24,8},{28,12},{1,17},{... | collective-permute-start | bytes 1548296 | tf_op jit(solution)/shard_map/ppermute | solution.py:49
  78.2 2.7 %collective-permute-start.11 = (bf16[3,96,1792]{2,1,0:T(8,128)(2,1)S(1)}, bf16[3,96,1792]{2,1,0:T(8,128)(2,1)S(1)}, u32[]{:S(2)}, u32[]{:S(2)}) collective-permute-start(bf16[3,96,1792]{2,1,0:T(8,128)(2,1)S(1)} %maximum_select_fusion.2), channel_id=1, source_target_pairs={{0,4},{4,0},{8,12},{12,8},{16,20},{20,16},{24,28},{28,24},{1,5},{5... | collective-permute-start | bytes 3096584 | tf_op jit(solution)/shard_map/ppermute | solution.py:49
  78.5 4.0 %collective-permute-start.17 = (bf16[3,96,1792]{2,1,0:T(8,128)(2,1)S(1)}, bf16[3,96,1792]{2,1,0:T(8,128)(2,1)}, u32[]{:S(2)}, u32[]{:S(2)}) collective-permute-start(bf16[3,96,1792]{2,1,0:T(8,128)(2,1)S(1)} %maximum_select_fusion.3), channel_id=1, source_target_pairs={{0,4},{4,0},{8,12},{12,8},{16,20},{20,16},{24,28},{28,24},{1,5},{5... | collective-permute-start | bytes 3096584 | tf_op jit(solution)/shard_map/ppermute | solution.py:49
  80.9 4.1 %slice-start.2 = ((s8[7340032]{0:T(1024)(128)(4,1)}), s8[4194304]{0:T(1024)(128)(4,1)S(1)}, s32[]{:S(2)}) async-start(s8[7340032]{0:T(1024)(128)(4,1)} %bitcast.30), calls=%async_computation.2 | async-start | bytes 8388608
  84.5 1.9 %slice-start.3 = ((s8[7340032]{0:T(1024)(128)(4,1)}), s8[3145728]{0:T(1024)(128)(4,1)S(1)}, s32[]{:S(2)}) async-start(s8[7340032]{0:T(1024)(128)(4,1)} %bitcast.30), calls=%async_computation.3 | async-start | bytes 6291456
  84.5 4.4 %slice-start.6 = ((s8[7340032]{0:T(1024)(128)(4,1)}), s8[4194304]{0:T(1024)(128)(4,1)S(1)}, s32[]{:S(2)}) async-start(s8[7340032]{0:T(1024)(128)(4,1)} %bitcast.34), calls=%async_computation.6 | async-start | bytes 8388608
  86.4 2.5 %slice-start.7 = ((s8[7340032]{0:T(1024)(128)(4,1)}), s8[3145728]{0:T(1024)(128)(4,1)S(1)}, s32[]{:S(2)}) async-start(s8[7340032]{0:T(1024)(128)(4,1)} %bitcast.34), calls=%async_computation.7 | async-start | bytes 6291456
  96.7 13.9 %collective-permute-start.18 = (bf16[48,1024]{1,0:T(8,128)(2,1)S(1)}, bf16[48,1024]{1,0:T(8,128)(2,1)S(1)}, u32[]{:S(2)}, u32[]{:S(2)}) collective-permute-start(bf16[48,1024]{1,0:T(8,128)(2,1)S(1)} %get-tuple-element.35), channel_id=1, source_target_pairs={{0,3},{1,0},{2,1},{3,2},{4,7},{5,4},{6,5},{7,6},{8,11},{9,8},{10,9... | collective-permute-start | bytes 294920 | tf_op jit(solution)/shard_map/ppermute | solution.py:88
  97.9 12.7 %collective-permute-start.20 = (bf16[48,1024]{1,0:T(8,128)(2,1)S(1)}, bf16[48,1024]{1,0:T(8,128)(2,1)S(1)}, u32[]{:S(2)}, u32[]{:S(2)}) collective-permute-start(bf16[48,1024]{1,0:T(8,128)(2,1)S(1)} %get-tuple-element.36), channel_id=1, source_target_pairs={{0,1},{1,2},{2,3},{3,0},{4,5},{5,6},{6,7},{7,4},{8,9},{9,10},{10,1... | collective-permute-start | bytes 294920 | tf_op jit(solution)/shard_map/ppermute | solution.py:88
  98.8 6.6 %copy-start.2 = (bf16[192,1024]{1,0:T(8,128)(2,1)S(1)}, bf16[192,1024]{1,0:T(8,128)(2,1)}, u32[]{:S(2)}) copy-start(bf16[192,1024]{1,0:T(8,128)(2,1)} %copy-done.1) | copy-start | bytes 1179652
  98.8 11.8 %collective-permute-start.19 = (bf16[48,1024]{1,0:T(8,128)(2,1)S(1)}, bf16[48,1024]{1,0:T(8,128)(2,1)S(1)}, u32[]{:S(2)}, u32[]{:S(2)}) collective-permute-start(bf16[48,1024]{1,0:T(8,128)(2,1)S(1)} %get-tuple-element.37), channel_id=1, source_target_pairs={{0,2},{1,3},{2,0},{3,1},{4,6},{5,7},{6,4},{7,5},{8,10},{9,11},{10,... | collective-permute-start | bytes 294920 | tf_op jit(solution)/shard_map/ppermute | solution.py:88

commit v13 on v12

--- a/solution.py
+++ b/solution.py
@@ -26,18 +26,27 @@
     return (hidden, grad_gate, grad_up)
 
 
-def halving_reduce(x, order, n_dev):
+def halving_reduce(parts, order, n_dev):
     r = lax.axis_index("row")
-    cur = x
+    cur = parts
     for step, bit in enumerate(order):
-        n = cur.shape[1] // 2
+        axis = 0 if step == 0 else 1
+        size = cur[0].shape[0] if step == 0 else cur.shape[1]
+        n = size // 2
         hi = (r // bit) % 2
-        keep = lax.dynamic_slice_in_dim(cur, hi * n, n, 1)
-        send = lax.dynamic_slice_in_dim(cur, (1 - hi) * n, n, 1)
-        got = lax.ppermute(send, "row", [(j, j ^ bit) for j in range(n_dev)])
-        cur = keep.astype(jnp.float32) + got.astype(jnp.float32)
+        perm = [(j, j ^ bit) for j in range(n_dev)]
+        if step == 0:
+            got = [lax.ppermute(lax.dynamic_slice_in_dim(c, (1 - hi) * n, n, 0), "row", perm) for c in cur]
+            keep = [lax.dynamic_slice_in_dim(c, hi * n, n, 0) for c in cur]
+            summed = jnp.stack([k.astype(jnp.float32) + g.astype(jnp.float32) for k, g in zip(keep, got)])
+        else:
+            keep = lax.dynamic_slice_in_dim(cur, hi * n, n, axis)
+            send = lax.dynamic_slice_in_dim(cur, (1 - hi) * n, n, axis)
+            got = lax.ppermute(send, "row", perm)
+            summed = keep.astype(jnp.float32) + got.astype(jnp.float32)
         if step + 1 < len(order):
-            cur = cur.astype(jnp.bfloat16)
+            summed = summed.astype(jnp.bfloat16)
+        cur = summed
     return cur
 
 
@@ -62,14 +71,14 @@
 
 
 def row_gated(stacked, n_dev):
-    _, tokens, units = stacked.shape
+    tokens, units = stacked[0].shape
     bits = row_bits(n_dev, tokens, units)
     if bits is None:
-        sums = lax.psum(stacked, "row").astype(jnp.float32)
+        sums = lax.psum(jnp.stack(stacked), "row").astype(jnp.float32)
         return jnp.stack(gated_grads(sums[0], sums[1], sums[2]))
     orders = (bits, bits[:1] + bits[:0:-1])
     half = units // 2
-    reduced = [halving_reduce(stacked[:, :, h * half:(h + 1) * half], o, n_dev) for h, o in enumerate(orders)]
+    reduced = [halving_reduce([a[:, h * half:(h + 1) * half] for a in stacked], o, n_dev) for h, o in enumerate(orders)]
     outs = [doubling_gather(jnp.stack(gated_grads(red[0], red[1], red[2])), o, n_dev) for red, o in zip(reduced, orders)]
     return jnp.concatenate(outs, axis=2)
 
@@ -97,13 +106,11 @@
     grad_out, tok_all = lax.optimization_barrier((grad_out, tok_all))
     grad_all = col_gather(grad_out, n_col)
     tok_t = tok_all.T
-    stacked = jnp.stack(
-        [
-            jnp.dot(tok_all, gate_weight, preferred_element_type=jnp.float32).astype(jnp.bfloat16),
-            jnp.dot(tok_all, up_weight, preferred_element_type=jnp.float32).astype(jnp.bfloat16),
-            contract_last(grad_all, down_weight).astype(jnp.bfloat16),
-        ]
-    )
+    stacked = [
+        jnp.dot(tok_all, gate_weight, preferred_element_type=jnp.float32).astype(jnp.bfloat16),
+        jnp.dot(tok_all, up_weight, preferred_element_type=jnp.float32).astype(jnp.bfloat16),
+        contract_last(grad_all, down_weight).astype(jnp.bfloat16),
+    ]
     gated = row_gated(stacked, n_row)
     hidden, grad_gate, grad_up = gated[0], gated[1], gated[2]
     partial_grad = contract_last(grad_gate, gate_weight) + contract_last(grad_up, up_weight)

time: 111 us -> 108 us (0.973)
  other arithmetic: 9.01 us -> 7.21 us
  local copies, waits for them, and re-layouts: 4.17 us -> 2.72 us
  waiting for transfers between devices: 38.2 us -> 36.8 us
    convert_element_type x4 -> x2, other arithmetic: 2.28 us -> 0.26 us  [halving_reduce(): summed = summed.astype(jnp.bfloat16)]
    dynamic_slice x6 -> x10, local copies, waits for them, and re-layouts: 2.31 us -> 0.33 us  [the longest x6 0.19 us: halving_reduce(): lax.dynamic_slice_in_dim(c, (1 - hi) * n, n, 0)]
    ppermute x6 -> x10, starting transfers between devices: 6.78 us -> 8.13 us  [the longest x4 6.28 us: halving_reduce(): got = lax.ppermute(send, 'row', perm)]
    ppermute x6 -> x10, waiting for transfers between devices: 16 us -> 15.8 us  [the longest x4 14.6 us: halving_reduce(): got = lax.ppermute(send, 'row', perm)]
  transfers between devices with their start and end apart: 21 -> 25, of which waited for: 12 -> 10; matrix products, arithmetic and copies ran while one was open for 20% -> 21% of each run, Pallas kernels for 0% -> 0%
where the time goes in v13:
time: 108 us
  waiting for transfers between devices  36.8 us (34%)
  starting transfers between devices  30.2 us (28%)
  matrix products  29.4 us (27%)
  other arithmetic  7.21 us (7%)
  local copies, waits for them, and re-layouts  2.72 us (3%)
  between operations  1.12 us (1%)
    ppermute x6, waiting for transfers between devices, doubling_gather(): got = lax.ppermute(cur, 'row', [(j, j ^ bit) for j in range(n_dev)])  16.1 us
    ppermute x4, waiting for transfers between devices, halving_reduce(): got = lax.ppermute(send, 'row', perm)  14.6 us
    ppermute x6, starting transfers between devices, col_gather(): lax.ppermute(x, 'col', [(j, (j + s) % n_col) for j in range(n_col)])  13.2 us
    dot_general x3, matrix products, contract_last(): lax.dot_general(left, right, (((1,), (1,)), ((), ())), preferred_element_...  7.58 us
    ppermute x4, starting transfers between devices, halving_reduce(): got = lax.ppermute(send, 'row', perm)  6.28 us
    ppermute x6, starting transfers between devices, doubling_gather(): got = lax.ppermute(cur, 'row', [(j, j ^ bit) for j in range(n_dev)])  5.98 us
    dot_general x1, matrix products, contract_first(): lax.dot_general(left, right, (((0,), (0,)), ((), ())), preferred_element_...  5.19 us
    dot_general x1, matrix products, body(): jnp.dot(tok_t, grad_gate, preferred_element_type=jnp.float32)  5.18 us
  transfers between devices with their start and end apart: 25, of which 10 were waited for; matrix products, arithmetic and copies ran while one was open for 21% of the time, Pallas kernels for 0%

profile of v13, /device:TPU:0, one launch (start us, length us, event | category | flops | bytes accessed | tf_op | source)
XLA Modules:
  0.0 107.5 jit_solution(17190972869271842246)
XLA Ops:
  0.6 4.1 %collective-permute-start.1 = (bf16[48,1024]{1,0:T(8,128)(2,1)}, bf16[48,1024]{1,0:T(8,128)(2,1)S(1)}, u32[]{:S(2)}, u32[]{:S(2)}) collective-permute-start(bf16[48,1024]{1,0:T(8,128)(2,1)} %param.5), channel_id=1, source_target_pairs={{0,2},{1,3},{2,0},{3,1},{4,6},{5,7},{6,4},{7,5},{8,10},{9,11},{10,... | collective-permute-start | bytes 294920 | tf_op jit(solution)/shard_map/ppermute | solution.py:89
  4.8 1.6 %collective-permute-start = (bf16[48,1024]{1,0:T(8,128)(2,1)}, bf16[48,1024]{1,0:T(8,128)(2,1)S(1)}, u32[]{:S(2)}, u32[]{:S(2)}) collective-permute-start(bf16[48,1024]{1,0:T(8,128)(2,1)} %param.5), channel_id=1, source_target_pairs={{0,1},{1,2},{2,3},{3,0},{4,5},{5,6},{6,7},{7,4},{8,9},{9,10},{10,1... | collective-permute-start | bytes 294920 | tf_op jit(solution)/shard_map/ppermute | solution.py:89
  6.3 2.2 %collective-permute-start.2 = (bf16[48,1024]{1,0:T(8,128)(2,1)}, bf16[48,1024]{1,0:T(8,128)(2,1)S(1)}, u32[]{:S(2)}, u32[]{:S(2)}) collective-permute-start(bf16[48,1024]{1,0:T(8,128)(2,1)} %param.5), channel_id=1, source_target_pairs={{0,3},{1,0},{2,1},{3,2},{4,7},{5,4},{6,5},{7,6},{8,11},{9,8},{10,9... | collective-permute-start | bytes 294920 | tf_op jit(solution)/shard_map/ppermute | solution.py:89
  8.6 4.3 %collective-permute-done.1 = bf16[48,1024]{1,0:T(8,128)(2,1)S(1)} collective-permute-done((bf16[48,1024]{1,0:T(8,128)(2,1)}, bf16[48,1024]{1,0:T(8,128)(2,1)S(1)}, u32[]{:S(2)}, u32[]{:S(2)}) %collective-permute-start.1) | collective-permute-done | bytes 98336 | tf_op jit(solution)/shard_map/ppermute | solution.py:89
  12.9 0.7 collective-permute-done.2
  13.6 1.1 pad_maximum_fusion.3
  14.7 2.1 %collective-permute-start.7 = (bf16[48,1024]{1,0:T(8,128)(2,1)}, bf16[48,1024]{1,0:T(8,128)(2,1)S(1)}, u32[]{:S(2)}, u32[]{:S(2)}) collective-permute-start(bf16[48,1024]{1,0:T(8,128)(2,1)} %param.6), channel_id=1, source_target_pairs={{0,3},{1,0},{2,1},{3,2},{4,7},{5,4},{6,5},{7,6},{8,11},{9,8},{10,9... | collective-permute-start | bytes 294920 | tf_op jit(solution)/shard_map/ppermute | solution.py:89
  16.8 1.2 %collective-permute-start.6 = (bf16[48,1024]{1,0:T(8,128)(2,1)}, bf16[48,1024]{1,0:T(8,128)(2,1)S(1)}, u32[]{:S(2)}, u32[]{:S(2)}) collective-permute-start(bf16[48,1024]{1,0:T(8,128)(2,1)} %param.6), channel_id=1, source_target_pairs={{0,2},{1,3},{2,0},{3,1},{4,6},{5,7},{6,4},{7,5},{8,10},{9,11},{10,... | collective-permute-start | bytes 294920 | tf_op jit(solution)/shard_map/ppermute | solution.py:89
  17.9 1.9 %collective-permute-start.5 = (bf16[48,1024]{1,0:T(8,128)(2,1)}, bf16[48,1024]{1,0:T(8,128)(2,1)S(1)}, u32[]{:S(2)}, u32[]{:S(2)}) collective-permute-start(bf16[48,1024]{1,0:T(8,128)(2,1)} %param.6), channel_id=1, source_target_pairs={{0,1},{1,2},{2,3},{3,0},{4,5},{5,6},{6,7},{7,4},{8,9},{9,10},{10,1... | collective-permute-start | bytes 294920 | tf_op jit(solution)/shard_map/ppermute | solution.py:89
  19.9 4.7 %convolution_convert_fusion.4 = bf16[192,3584]{1,0:T(8,128)(2,1)S(1)} fusion(bf16[192,1024]{1,0:T(8,128)(2,1)S(1)} %pad_maximum_fusion.3, bf16[1024,3584]{1,0:T(8,128)(2,1)} %param.8), kind=kOutput, calls=%fused_computation.4 | convolution fusion | flops 1409974272 | bytes 9109504 | tf_op jit(solution)/shard_map/dot_general | solution.py:111
  24.6 0.1 fusion.13
  24.9 0.5 collective-permute-start.15
  25.4 1.6 %convolution_convert_fusion.5 = bf16[192,3584]{1,0:T(8,128)(2,1)S(1)} fusion(bf16[192,1024]{1,0:T(8,128)(2,1)S(1)} %pad_maximum_fusion.3, bf16[1024,3584]{1,0:T(8,128)(2,1)S(1)} %bitcast.39), kind=kOutput, calls=%fused_computation.5 | convolution fusion | flops 1409974272 | bytes 9109504 | tf_op jit(solution)/shard_map/dot_general | solution.py:110
  27.0 0.1 fusion.12
  27.2 0.7 copy-done.2
  27.9 0.1 collective-permute-start.3
  28.1 0.5 collective-permute-start.14
  28.6 2.6 %convolution_convert_fusion.3 = bf16[192,3584]{1,0:T(8,128)(2,1)S(1)} fusion(bf16[192,1024]{1,0:T(8,128)(2,1)S(1)} %constant_dynamic-update-slice_fusion, bf16[3584,1024]{1,0:T(8,128)(2,1)S(1)} %bitcast.35), kind=kOutput, calls=%fused_computation.3 | convolution fusion | flops 1409974272 | bytes 9109504 | tf_op jit(solution)/shard_map/dot_general | solution.py:14
  31.2 0.1 fusion.14
  31.4 0.1 collective-permute-start.8
  31.5 0.5 collective-permute-start.16
  32.1 0.1 fusion.10
  32.2 0.1 fusion.6
  32.3 0.1 fusion.9
  32.4 1.1 %collective-permute-done.16 = bf16[96,1792]{1,0:T(8,128)(2,1)S(1)} collective-permute-done((bf16[96,1792]{1,0:T(8,128)(2,1)S(1)}, bf16[96,1792]{1,0:T(8,128)(2,1)S(1)}, u32[]{:S(2)}, u32[]{:S(2)}) %collective-permute-start.16) | collective-permute-done | bytes 344096 | tf_op jit(solution)/shard_map/ppermute | solution.py:39
  33.7 0.1 pad_maximum_fusion.2
  33.8 1.6 %collective-permute-start.17 = (bf16[3,48,1792]{2,1,0:T(8,128)(2,1)S(1)}, bf16[3,48,1792]{2,1,0:T(8,128)(2,1)S(1)}, u32[]{:S(2)}, u32[]{:S(2)}) collective-permute-start(bf16[3,48,1792]{2,1,0:T(8,128)(2,1)S(1)} %constant_dynamic-slice_fusion.1), channel_id=1, source_target_pairs={{0,16},{4,20},{8,24},{12,28},{16,0},{20,4},{24,8},{28,12},{1,17},{... | collective-permute-start | bytes 1548296 | tf_op jit(solution)/shard_map/ppermute | solution.py:45
  35.5 0.1 pad_maximum_fusion.1
  35.7 1.6 %collective-permute-start.9 = (bf16[3,48,1792]{2,1,0:T(8,128)(2,1)S(1)}, bf16[3,48,1792]{2,1,0:T(8,128)(2,1)S(1)}, u32[]{:S(2)}, u32[]{:S(2)}) collective-permute-start(bf16[3,48,1792]{2,1,0:T(8,128)(2,1)S(1)} %constant_dynamic-slice_fusion.6), channel_id=1, source_target_pairs={{0,8},{4,12},{8,0},{12,4},{16,24},{20,28},{24,16},{28,20},{1,9},{5... | collective-permute-start | bytes 1548296 | tf_op jit(solution)/shard_map/ppermute | solution.py:45
  37.2 10.4 %collective-permute-done.17 = bf16[3,48,1792]{2,1,0:T(8,128)(2,1)S(1)} collective-permute-done((bf16[3,48,1792]{2,1,0:T(8,128)(2,1)S(1)}, bf16[3,48,1792]{2,1,0:T(8,128)(2,1)S(1)}, u32[]{:S(2)}, u32[]{:S(2)}) %collective-permute-start.17) | collective-permute-done | bytes 516128 | tf_op jit(solution)/shard_map/ppermute | solution.py:45
  47.7 0.1 add_convert_fusion
  47.9 1.5 %collective-permute-start.18 = (bf16[3,24,1792]{2,1,0:T(8,128)(2,1)S(1)}, bf16[3,24,1792]{2,1,0:T(8,128)(2,1)S(1)}, u32[]{:S(2)}, u32[]{:S(2)}) collective-permute-start(bf16[3,24,1792]{2,1,0:T(8,128)(2,1)S(1)} %constant_dynamic-slice_fusion), channel_id=1, source_target_pairs={{0,8},{4,12},{8,0},{12,4},{16,24},{20,28},{24,16},{28,20},{1,9},{5... | collective-permute-start | bytes 774152 | tf_op jit(solution)/shard_map/ppermute | solution.py:45
  49.4 0.1 add_convert_fusion.1
  49.6 1.6 %collective-permute-start.10 = (bf16[3,24,1792]{2,1,0:T(8,128)(2,1)S(1)}, bf16[3,24,1792]{2,1,0:T(8,128)(2,1)S(1)}, u32[]{:S(2)}, u32[]{:S(2)}) collective-permute-start(bf16[3,24,1792]{2,1,0:T(8,128)(2,1)S(1)} %constant_dynamic-slice_fusion.5), channel_id=1, source_target_pairs={{0,16},{4,20},{8,24},{12,28},{16,0},{20,4},{24,8},{28,12},{1,17},{... | collective-permute-start | bytes 774152 | tf_op jit(solution)/shard_map/ppermute | solution.py:45
  51.2 4.2 %collective-permute-done.18 = bf16[3,24,1792]{2,1,0:T(8,128)(2,1)S(1)} collective-permute-done((bf16[3,24,1792]{2,1,0:T(8,128)(2,1)S(1)}, bf16[3,24,1792]{2,1,0:T(8,128)(2,1)S(1)}, u32[]{:S(2)}, u32[]{:S(2)}) %collective-permute-start.18) | collective-permute-done | bytes 258080 | tf_op jit(solution)/shard_map/ppermute | solution.py:45
  55.4 0.1 multiply_convert_fusion.2
  55.5 1.5 %collective-permute-start.19 = (bf16[3,24,1792]{2,1,0:T(8,128)(2,1)S(1)}, bf16[3,24,1792]{2,1,0:T(8,128)(2,1)S(1)}, u32[]{:S(2)}, u32[]{:S(2)}) collective-permute-start(bf16[3,24,1792]{2,1,0:T(8,128)(2,1)S(1)} %pad_maximum_fusion.5), channel_id=1, source_target_pairs={{0,8},{4,12},{8,0},{12,4},{16,24},{20,28},{24,16},{28,20},{1,9},{5... | collective-permute-start | bytes 774152 | tf_op jit(solution)/shard_map/ppermute | solution.py:58
  57.1 0.1 multiply_convert_fusion.5
  57.3 1.6 %collective-permute-start.11 = (bf16[3,24,1792]{2,1,0:T(8,128)(2,1)S(1)}, bf16[3,24,1792]{2,1,0:T(8,128)(2,1)S(1)}, u32[]{:S(2)}, u32[]{:S(2)}) collective-permute-start(bf16[3,24,1792]{2,1,0:T(8,128)(2,1)S(1)} %pad_maximum_fusion.4), channel_id=1, source_target_pairs={{0,16},{4,20},{8,24},{12,28},{16,0},{20,4},{24,8},{28,12},{1,17},{... | collective-permute-start | bytes 774152 | tf_op jit(solution)/shard_map/ppermute | solution.py:58
  58.9 3.3 %collective-permute-done.19 = bf16[3,24,1792]{2,1,0:T(8,128)(2,1)S(1)} collective-permute-done((bf16[3,24,1792]{2,1,0:T(8,128)(2,1)S(1)}, bf16[3,24,1792]{2,1,0:T(8,128)(2,1)S(1)}, u32[]{:S(2)}, u32[]{:S(2)}) %collective-permute-start.19) | collective-permute-done | bytes 258080 | tf_op jit(solution)/shard_map/ppermute | solution.py:58
  62.2 0.1 maximum_select_fusion.5
  62.3 1.5 %collective-permute-start.20 = (bf16[3,48,1792]{2,1,0:T(8,128)(2,1)S(1)}, bf16[3,48,1792]{2,1,0:T(8,128)(2,1)S(1)}, u32[]{:S(2)}, u32[]{:S(2)}) collective-permute-start(bf16[3,48,1792]{2,1,0:T(8,128)(2,1)S(1)} %maximum_select_fusion.5), channel_id=1, source_target_pairs={{0,16},{4,20},{8,24},{12,28},{16,0},{20,4},{24,8},{28,12},{1,17},{... | collective-permute-start | bytes 1548296 | tf_op jit(solution)/shard_map/ppermute | solution.py:58
  63.8 1.1 collective-permute-done.11
  64.9 0.1 maximum_select_fusion.4
  65.0 0.7 collective-permute-start.12
  65.6 9.1 %collective-permute-done.20 = bf16[3,48,1792]{2,1,0:T(8,128)(2,1)S(1)} collective-permute-done((bf16[3,48,1792]{2,1,0:T(8,128)(2,1)S(1)}, bf16[3,48,1792]{2,1,0:T(8,128)(2,1)S(1)}, u32[]{:S(2)}, u32[]{:S(2)}) %collective-permute-start.20) | collective-permute-done | bytes 516128 | tf_op jit(solution)/shard_map/ppermute | solution.py:58
  74.7 0.3 maximum_select_fusion.3
  75.1 0.3 maximum_select_fusion.2
  75.3 0.6 collective-permute-start.13
  75.9 1.8 %collective-permute-done.21 = bf16[3,96,1792]{2,1,0:T(8,128)(2,1)S(1)} collective-permute-done((bf16[3,96,1792]{2,1,0:T(8,128)(2,1)S(1)}, bf16[3,96,1792]{2,1,0:T(8,128)(2,1)S(1)}, u32[]{:S(2)}, u32[]{:S(2)}) %collective-permute-start.21) | collective-permute-done | bytes 1032224 | tf_op jit(solution)/shard_map/ppermute | solution.py:58
  77.7 0.8 maximum_select_fusion.1
  78.5 0.8 collective-permute-done.13
  79.3 2.0 %maximum_select_fusion = bf16[3,192,1792]{2,1,0:T(8,128)(2,1)S(1)} fusion(bf16[3,96,1792]{2,1,0:T(8,128)(2,1)S(1)} %maximum_select_fusion.2, bf16[3,96,1792]{2,1,0:T(8,128)(2,1)} %collective-permute-done.13, pred[]{:T(512)S(6)} %eq.25), kind=kLoop, calls=%fused_computation.10 | loop fusion | flops 9289728 | bytes 4128769 | tf_op jit(solution)/shard_map/jit(_where)/select_n | solution.py:59
  81.4 0.5 fusion.4
  81.9 1.3 %slice-done.3 = s8[3145728]{0:T(1024)(128)(4,1)S(1)} async-done(((s8[7340032]{0:T(1024)(128)(4,1)}), s8[3145728]{0:T(1024)(128)(4,1)S(1)}, s32[]{:S(2)}) %slice-start.3) | async-done | bytes 3145752
  83.2 2.5 %fusion.16 = f32[192,1024]{1,0:T(8,128)S(1)} fusion(bf16[192,3584]{1,0:T(8,128)(2,1)S(1)} %get-tuple-element.22, bf16[1024,3584]{1,0:T(8,128)(2,1)S(1)} %bitcast.37), kind=kOutput, calls=%fused_computation.72 | convolution fusion | flops 1409286144 | bytes 9502720 | tf_op jit(solution)/shard_map/dot_general | solution.py:14
  85.8 2.5 %fusion.5 = bf16[192,1024]{1,0:T(8,128)(2,1)S(1)} fusion(f32[192,1024]{1,0:T(8,128)S(1)} %fusion.16, bf16[192,3584]{1,0:T(8,128)(2,1)S(1)} %get-tuple-element.17, bf16[1024,3584]{1,0:T(8,128)(2,1)S(1)} %bitcast.41), kind=kOutput, calls=%fused_computation.19 | convolution fusion | flops 1409679360 | bytes 9895936 | tf_op jit(solution)/shard_map/dot_general | solution.py:14
  88.3 5.2 %convolution_convert_fusion.2 = bf16[1024,3584]{1,0:T(8,128)(2,1)} fusion(bf16[192,1024]{1,0:T(8,128)(2,1)S(1)} %pad_maximum_fusion.3, bf16[192,3584]{1,0:T(8,128)(2,1)S(1)} %get-tuple-element.17), kind=kOutput, calls=%fused_computation.2 | convolution fusion | flops 1412956160 | bytes 9109504 | tf_op jit(solution)/shard_map/dot_general | solution.py:120
  93.5 1.9 %collective-permute-start.22 = (bf16[48,1024]{1,0:T(8,128)(2,1)S(1)}, bf16[48,1024]{1,0:T(8,128)(2,1)S(1)}, u32[]{:S(2)}, u32[]{:S(2)}) collective-permute-start(bf16[48,1024]{1,0:T(8,128)(2,1)S(1)} %get-tuple-element.39), channel_id=1, source_target_pairs={{0,3},{1,0},{2,1},{3,2},{4,7},{5,4},{6,5},{7,6},{8,11},{9,8},{10,9... | collective-permute-start | bytes 294920 | tf_op jit(solution)/shard_map/ppermute | solution.py:97
  95.4 0.1 collective-permute-start.24
  95.6 0.8 collective-permute-start.23
  96.4 5.2 %convolution_convert_fusion.1 = bf16[1024,3584]{1,0:T(8,128)(2,1)} fusion(bf16[192,1024]{1,0:T(8,128)(2,1)S(1)} %pad_maximum_fusion.3, bf16[192,3584]{1,0:T(8,128)(2,1)S(1)} %get-tuple-element.22), kind=kOutput, calls=%fused_computation.1 | convolution fusion | flops 1412956160 | bytes 9109504 | tf_op jit(solution)/shard_map/dot_general | solution.py:123
  101.6 5.2 %convolution_convert_fusion = bf16[3584,1024]{1,0:T(8,128)(2,1)} fusion(bf16[192,3584]{1,0:T(8,128)(2,1)S(1)} %get-tuple-element.23, bf16[192,1024]{1,0:T(8,128)(2,1)S(1)} %copy-done.1), kind=kOutput, calls=%fused_computation | convolution fusion | flops 1412956160 | bytes 9109504 | tf_op jit(solution)/shard_map/dot_general | solution.py:8
  106.8 0.7 add_convert_fusion.8
  (63 shorter events, 1.1 us)
Async XLA Ops:
  0.6 12.2 %collective-permute-start.1 = (bf16[48,1024]{1,0:T(8,128)(2,1)}, bf16[48,1024]{1,0:T(8,128)(2,1)S(1)}, u32[]{:S(2)}, u32[]{:S(2)}) collective-permute-start(bf16[48,1024]{1,0:T(8,128)(2,1)} %param.5), channel_id=1, source_target_pairs={{0,2},{1,3},{2,0},{3,1},{4,6},{5,7},{6,4},{7,5},{8,10},{9,11},{10,... | collective-permute-start | bytes 294920 | tf_op jit(solution)/shard_map/ppermute | solution.py:89
  4.8 8.1 %collective-permute-start = (bf16[48,1024]{1,0:T(8,128)(2,1)}, bf16[48,1024]{1,0:T(8,128)(2,1)S(1)}, u32[]{:S(2)}, u32[]{:S(2)}) collective-permute-start(bf16[48,1024]{1,0:T(8,128)(2,1)} %param.5), channel_id=1, source_target_pairs={{0,1},{1,2},{2,3},{3,0},{4,5},{5,6},{6,7},{7,4},{8,9},{9,10},{10,1... | collective-permute-start | bytes 294920 | tf_op jit(solution)/shard_map/ppermute | solution.py:89
  6.3 7.2 %collective-permute-start.2 = (bf16[48,1024]{1,0:T(8,128)(2,1)}, bf16[48,1024]{1,0:T(8,128)(2,1)S(1)}, u32[]{:S(2)}, u32[]{:S(2)}) collective-permute-start(bf16[48,1024]{1,0:T(8,128)(2,1)} %param.5), channel_id=1, source_target_pairs={{0,3},{1,0},{2,1},{3,2},{4,7},{5,4},{6,5},{7,6},{8,11},{9,8},{10,9... | collective-permute-start | bytes 294920 | tf_op jit(solution)/shard_map/ppermute | solution.py:89
  13.6 11.8 %slice-start.4 = ((s8[7340032]{0:T(1024)(128)(4,1)}), s8[4194304]{0:T(1024)(128)(4,1)S(1)}, s32[]{:S(2)}) async-start(s8[7340032]{0:T(1024)(128)(4,1)} %bitcast.38), calls=%async_computation.4 | async-start | bytes 8388608
  14.6 10.7 %slice-start.5 = ((s8[7340032]{0:T(1024)(128)(4,1)}), s8[3145728]{0:T(1024)(128)(4,1)S(1)}, s32[]{:S(2)}) async-start(s8[7340032]{0:T(1024)(128)(4,1)} %bitcast.38), calls=%async_computation.5 | async-start | bytes 6291456
  14.7 13.9 %collective-permute-start.7 = (bf16[48,1024]{1,0:T(8,128)(2,1)}, bf16[48,1024]{1,0:T(8,128)(2,1)S(1)}, u32[]{:S(2)}, u32[]{:S(2)}) collective-permute-start(bf16[48,1024]{1,0:T(8,128)(2,1)} %param.6), channel_id=1, source_target_pairs={{0,3},{1,0},{2,1},{3,2},{4,7},{5,4},{6,5},{7,6},{8,11},{9,8},{10,9... | collective-permute-start | bytes 294920 | tf_op jit(solution)/shard_map/ppermute | solution.py:89
  16.8 11.3 %collective-permute-start.6 = (bf16[48,1024]{1,0:T(8,128)(2,1)}, bf16[48,1024]{1,0:T(8,128)(2,1)S(1)}, u32[]{:S(2)}, u32[]{:S(2)}) collective-permute-start(bf16[48,1024]{1,0:T(8,128)(2,1)} %param.6), channel_id=1, source_target_pairs={{0,2},{1,3},{2,0},{3,1},{4,6},{5,7},{6,4},{7,5},{8,10},{9,11},{10,... | collective-permute-start | bytes 294920 | tf_op jit(solution)/shard_map/ppermute | solution.py:89
  17.9 10.0 %collective-permute-start.5 = (bf16[48,1024]{1,0:T(8,128)(2,1)}, bf16[48,1024]{1,0:T(8,128)(2,1)S(1)}, u32[]{:S(2)}, u32[]{:S(2)}) collective-permute-start(bf16[48,1024]{1,0:T(8,128)(2,1)} %param.6), channel_id=1, source_target_pairs={{0,1},{1,2},{2,3},{3,0},{4,5},{5,6},{6,7},{7,4},{8,9},{9,10},{10,1... | collective-permute-start | bytes 294920 | tf_op jit(solution)/shard_map/ppermute | solution.py:89
  24.7 3.9 %slice-start = ((s8[7340032]{0:T(1024)(128)(4,1)}), s8[4194304]{0:T(1024)(128)(4,1)S(1)}, s32[]{:S(2)}) async-start(s8[7340032]{0:T(1024)(128)(4,1)} %bitcast.34), calls=%async_computation | async-start | bytes 8388608
  24.8 3.9 %slice-start.1 = ((s8[7340032]{0:T(1024)(128)(4,1)}), s8[3145728]{0:T(1024)(128)(4,1)S(1)}, s32[]{:S(2)}) async-start(s8[7340032]{0:T(1024)(128)(4,1)} %bitcast.34), calls=%async_computation.1 | async-start | bytes 6291456
  24.8 6.7 %collective-permute-start.4 = (bf16[96,1792]{1,0:T(8,128)(2,1)S(1)}, bf16[96,1792]{1,0:T(8,128)(2,1)S(1)}, u32[]{:S(2)}, u32[]{:S(2)}) collective-permute-start(bf16[96,1792]{1,0:T(8,128)(2,1)S(1)} %constant_dynamic-slice_fusion.8), channel_id=1, source_target_pairs={{0,4},{4,0},{8,12},{12,8},{16,20},{20,16},{24,28},{28,24},{1,5},{5... | collective-permute-start | bytes 1032200 | tf_op jit(solution)/shard_map/ppermute | solution.py:39
  24.9 7.3 %collective-permute-start.15 = (bf16[96,1792]{1,0:T(8,128)(2,1)S(1)}, bf16[96,1792]{1,0:T(8,128)(2,1)S(1)}, u32[]{:S(2)}, u32[]{:S(2)}) collective-permute-start(bf16[96,1792]{1,0:T(8,128)(2,1)S(1)} %constant_dynamic-slice_fusion.3), channel_id=1, source_target_pairs={{0,4},{4,0},{8,12},{12,8},{16,20},{20,16},{24,28},{28,24},{1,5},{5... | collective-permute-start | bytes 1032200 | tf_op jit(solution)/shard_map/ppermute | solution.py:39
  27.0 0.9 copy-start.2
  27.9 4.3 %collective-permute-start.3 = (bf16[96,1792]{1,0:T(8,128)(2,1)S(1)}, bf16[96,1792]{1,0:T(8,128)(2,1)S(1)}, u32[]{:S(2)}, u32[]{:S(2)}) collective-permute-start(bf16[96,1792]{1,0:T(8,128)(2,1)S(1)} %constant_dynamic-slice_fusion.9), channel_id=1, source_target_pairs={{0,4},{4,0},{8,12},{12,8},{16,20},{20,16},{24,28},{28,24},{1,5},{5... | collective-permute-start | bytes 1032200 | tf_op jit(solution)/shard_map/ppermute | solution.py:39
  28.1 4.3 %collective-permute-start.14 = (bf16[96,1792]{1,0:T(8,128)(2,1)S(1)}, bf16[96,1792]{1,0:T(8,128)(2,1)S(1)}, u32[]{:S(2)}, u32[]{:S(2)}) collective-permute-start(bf16[96,1792]{1,0:T(8,128)(2,1)S(1)} %constant_dynamic-slice_fusion.4), channel_id=1, source_target_pairs={{0,4},{4,0},{8,12},{12,8},{16,20},{20,16},{24,28},{28,24},{1,5},{5... | collective-permute-start | bytes 1032200 | tf_op jit(solution)/shard_map/ppermute | solution.py:39
  28.6 2.6 %copy-start = (bf16[192,1024]{1,0:T(8,128)(2,1)}, bf16[192,1024]{1,0:T(8,128)(2,1)S(1)}, u32[]{:S(2)}) copy-start(bf16[192,1024]{1,0:T(8,128)(2,1)S(1)} %constant_dynamic-update-slice_fusion) | copy-start | bytes 1179652
  31.4 4.0 %collective-permute-start.8 = (bf16[96,1792]{1,0:T(8,128)(2,1)S(1)}, bf16[96,1792]{1,0:T(8,128)(2,1)S(1)}, u32[]{:S(2)}, u32[]{:S(2)}) collective-permute-start(bf16[96,1792]{1,0:T(8,128)(2,1)S(1)} %constant_dynamic-slice_fusion.7), channel_id=1, source_target_pairs={{0,4},{4,0},{8,12},{12,8},{16,20},{20,16},{24,28},{28,24},{1,5},{5... | collective-permute-start | bytes 1032200 | tf_op jit(solution)/shard_map/ppermute | solution.py:39
  31.5 2.0 %collective-permute-start.16 = (bf16[96,1792]{1,0:T(8,128)(2,1)S(1)}, bf16[96,1792]{1,0:T(8,128)(2,1)S(1)}, u32[]{:S(2)}, u32[]{:S(2)}) collective-permute-start(bf16[96,1792]{1,0:T(8,128)(2,1)S(1)} %constant_dynamic-slice_fusion.2), channel_id=1, source_target_pairs={{0,4},{4,0},{8,12},{12,8},{16,20},{20,16},{24,28},{28,24},{1,5},{5... | collective-permute-start | bytes 1032200 | tf_op jit(solution)/shard_map/ppermute | solution.py:39
  33.8 13.9 %collective-permute-start.17 = (bf16[3,48,1792]{2,1,0:T(8,128)(2,1)S(1)}, bf16[3,48,1792]{2,1,0:T(8,128)(2,1)S(1)}, u32[]{:S(2)}, u32[]{:S(2)}) collective-permute-start(bf16[3,48,1792]{2,1,0:T(8,128)(2,1)S(1)} %constant_dynamic-slice_fusion.1), channel_id=1, source_target_pairs={{0,16},{4,20},{8,24},{12,28},{16,0},{20,4},{24,8},{28,12},{1,17},{... | collective-permute-start | bytes 1548296 | tf_op jit(solution)/shard_map/ppermute | solution.py:45
  35.7 13.7 %collective-permute-start.9 = (bf16[3,48,1792]{2,1,0:T(8,128)(2,1)S(1)}, bf16[3,48,1792]{2,1,0:T(8,128)(2,1)S(1)}, u32[]{:S(2)}, u32[]{:S(2)}) collective-permute-start(bf16[3,48,1792]{2,1,0:T(8,128)(2,1)S(1)} %constant_dynamic-slice_fusion.6), channel_id=1, source_target_pairs={{0,8},{4,12},{8,0},{12,4},{16,24},{20,28},{24,16},{28,20},{1,9},{5... | collective-permute-start | bytes 1548296 | tf_op jit(solution)/shard_map/ppermute | solution.py:45
  47.9 7.5 %collective-permute-start.18 = (bf16[3,24,1792]{2,1,0:T(8,128)(2,1)S(1)}, bf16[3,24,1792]{2,1,0:T(8,128)(2,1)S(1)}, u32[]{:S(2)}, u32[]{:S(2)}) collective-permute-start(bf16[3,24,1792]{2,1,0:T(8,128)(2,1)S(1)} %constant_dynamic-slice_fusion), channel_id=1, source_target_pairs={{0,8},{4,12},{8,0},{12,4},{16,24},{20,28},{24,16},{28,20},{1,9},{5... | collective-permute-start | bytes 774152 | tf_op jit(solution)/shard_map/ppermute | solution.py:45
  49.6 7.5 %collective-permute-start.10 = (bf16[3,24,1792]{2,1,0:T(8,128)(2,1)S(1)}, bf16[3,24,1792]{2,1,0:T(8,128)(2,1)S(1)}, u32[]{:S(2)}, u32[]{:S(2)}) collective-permute-start(bf16[3,24,1792]{2,1,0:T(8,128)(2,1)S(1)} %constant_dynamic-slice_fusion.5), channel_id=1, source_target_pairs={{0,16},{4,20},{8,24},{12,28},{16,0},{20,4},{24,8},{28,12},{1,17},{... | collective-permute-start | bytes 774152 | tf_op jit(solution)/shard_map/ppermute | solution.py:45
  55.5 6.6 %collective-permute-start.19 = (bf16[3,24,1792]{2,1,0:T(8,128)(2,1)S(1)}, bf16[3,24,1792]{2,1,0:T(8,128)(2,1)S(1)}, u32[]{:S(2)}, u32[]{:S(2)}) collective-permute-start(bf16[3,24,1792]{2,1,0:T(8,128)(2,1)S(1)} %pad_maximum_fusion.5), channel_id=1, source_target_pairs={{0,8},{4,12},{8,0},{12,4},{16,24},{20,28},{24,16},{28,20},{1,9},{5... | collective-permute-start | bytes 774152 | tf_op jit(solution)/shard_map/ppermute | solution.py:58
  57.3 7.6 %collective-permute-start.11 = (bf16[3,24,1792]{2,1,0:T(8,128)(2,1)S(1)}, bf16[3,24,1792]{2,1,0:T(8,128)(2,1)S(1)}, u32[]{:S(2)}, u32[]{:S(2)}) collective-permute-start(bf16[3,24,1792]{2,1,0:T(8,128)(2,1)S(1)} %pad_maximum_fusion.4), channel_id=1, source_target_pairs={{0,16},{4,20},{8,24},{12,28},{16,0},{20,4},{24,8},{28,12},{1,17},{... | collective-permute-start | bytes 774152 | tf_op jit(solution)/shard_map/ppermute | solution.py:58
  62.3 12.5 %collective-permute-start.20 = (bf16[3,48,1792]{2,1,0:T(8,128)(2,1)S(1)}, bf16[3,48,1792]{2,1,0:T(8,128)(2,1)S(1)}, u32[]{:S(2)}, u32[]{:S(2)}) collective-permute-start(bf16[3,48,1792]{2,1,0:T(8,128)(2,1)S(1)} %maximum_select_fusion.5), channel_id=1, source_target_pairs={{0,16},{4,20},{8,24},{12,28},{16,0},{20,4},{24,8},{28,12},{1,17},{... | collective-permute-start | bytes 1548296 | tf_op jit(solution)/shard_map/ppermute | solution.py:58
  65.0 10.1 %collective-permute-start.12 = (bf16[3,48,1792]{2,1,0:T(8,128)(2,1)S(1)}, bf16[3,48,1792]{2,1,0:T(8,128)(2,1)S(1)}, u32[]{:S(2)}, u32[]{:S(2)}) collective-permute-start(bf16[3,48,1792]{2,1,0:T(8,128)(2,1)S(1)} %maximum_select_fusion.4), channel_id=1, source_target_pairs={{0,8},{4,12},{8,0},{12,4},{16,24},{20,28},{24,16},{28,20},{1,9},{5... | collective-permute-start | bytes 1548296 | tf_op jit(solution)/shard_map/ppermute | solution.py:58
  75.0 2.7 %collective-permute-start.21 = (bf16[3,96,1792]{2,1,0:T(8,128)(2,1)S(1)}, bf16[3,96,1792]{2,1,0:T(8,128)(2,1)S(1)}, u32[]{:S(2)}, u32[]{:S(2)}) collective-permute-start(bf16[3,96,1792]{2,1,0:T(8,128)(2,1)S(1)} %maximum_select_fusion.3), channel_id=1, source_target_pairs={{0,4},{4,0},{8,12},{12,8},{16,20},{20,16},{24,28},{28,24},{1,5},{5... | collective-permute-start | bytes 3096584 | tf_op jit(solution)/shard_map/ppermute | solution.py:58
  75.3 4.0 %collective-permute-start.13 = (bf16[3,96,1792]{2,1,0:T(8,128)(2,1)S(1)}, bf16[3,96,1792]{2,1,0:T(8,128)(2,1)}, u32[]{:S(2)}, u32[]{:S(2)}) collective-permute-start(bf16[3,96,1792]{2,1,0:T(8,128)(2,1)S(1)} %maximum_select_fusion.2), channel_id=1, source_target_pairs={{0,4},{4,0},{8,12},{12,8},{16,20},{20,16},{24,28},{28,24},{1,5},{5... | collective-permute-start | bytes 3096584 | tf_op jit(solution)/shard_map/ppermute | solution.py:58
  77.7 4.2 %slice-start.2 = ((s8[7340032]{0:T(1024)(128)(4,1)}), s8[4194304]{0:T(1024)(128)(4,1)S(1)}, s32[]{:S(2)}) async-start(s8[7340032]{0:T(1024)(128)(4,1)} %bitcast.36), calls=%async_computation.2 | async-start | bytes 8388608
  81.3 1.9 %slice-start.3 = ((s8[7340032]{0:T(1024)(128)(4,1)}), s8[3145728]{0:T(1024)(128)(4,1)S(1)}, s32[]{:S(2)}) async-start(s8[7340032]{0:T(1024)(128)(4,1)} %bitcast.36), calls=%async_computation.3 | async-start | bytes 6291456
  81.4 4.4 %slice-start.6 = ((s8[7340032]{0:T(1024)(128)(4,1)}), s8[4194304]{0:T(1024)(128)(4,1)S(1)}, s32[]{:S(2)}) async-start(s8[7340032]{0:T(1024)(128)(4,1)} %bitcast.40), calls=%async_computation.6 | async-start | bytes 8388608
  83.2 2.5 %slice-start.7 = ((s8[7340032]{0:T(1024)(128)(4,1)}), s8[3145728]{0:T(1024)(128)(4,1)S(1)}, s32[]{:S(2)}) async-start(s8[7340032]{0:T(1024)(128)(4,1)} %bitcast.40), calls=%async_computation.7 | async-start | bytes 6291456
  93.5 13.3 %collective-permute-start.22 = (bf16[48,1024]{1,0:T(8,128)(2,1)S(1)}, bf16[48,1024]{1,0:T(8,128)(2,1)S(1)}, u32[]{:S(2)}, u32[]{:S(2)}) collective-permute-start(bf16[48,1024]{1,0:T(8,128)(2,1)S(1)} %get-tuple-element.39), channel_id=1, source_target_pairs={{0,3},{1,0},{2,1},{3,2},{4,7},{5,4},{6,5},{7,6},{8,11},{9,8},{10,9... | collective-permute-start | bytes 294920 | tf_op jit(solution)/shard_map/ppermute | solution.py:97
  95.4 11.4 %collective-permute-start.24 = (bf16[48,1024]{1,0:T(8,128)(2,1)S(1)}, bf16[48,1024]{1,0:T(8,128)(2,1)S(1)}, u32[]{:S(2)}, u32[]{:S(2)}) collective-permute-start(bf16[48,1024]{1,0:T(8,128)(2,1)S(1)} %get-tuple-element.40), channel_id=1, source_target_pairs={{0,1},{1,2},{2,3},{3,0},{4,5},{5,6},{6,7},{7,4},{8,9},{9,10},{10,1... | collective-permute-start | bytes 294920 | tf_op jit(solution)/shard_map/ppermute | solution.py:97
  95.6 6.0 %copy-start.1 = (bf16[192,1024]{1,0:T(8,128)(2,1)S(1)}, bf16[192,1024]{1,0:T(8,128)(2,1)}, u32[]{:S(2)}) copy-start(bf16[192,1024]{1,0:T(8,128)(2,1)} %copy-done) | copy-start | bytes 1179652
  95.6 11.2 %collective-permute-start.23 = (bf16[48,1024]{1,0:T(8,128)(2,1)S(1)}, bf16[48,1024]{1,0:T(8,128)(2,1)S(1)}, u32[]{:S(2)}, u32[]{:S(2)}) collective-permute-start(bf16[48,1024]{1,0:T(8,128)(2,1)S(1)} %get-tuple-element.41), channel_id=1, source_target_pairs={{0,2},{1,3},{2,0},{3,1},{4,6},{5,7},{6,4},{7,5},{8,10},{9,11},{10,... | collective-permute-start | bytes 294920 | tf_op jit(solution)/shard_map/ppermute | solution.py:97

commit v14 on v13

--- a/solution.py
+++ b/solution.py
@@ -53,10 +53,18 @@
 def doubling_gather(x, order, n_dev):
     r = lax.axis_index("row")
     cur = x
-    for bit in reversed(order):
+    for step, bit in enumerate(reversed(order)):
         hi = (r // bit) % 2
-        got = lax.ppermute(cur, "row", [(j, j ^ bit) for j in range(n_dev)])
-        cur = jnp.where(hi == 1, jnp.concatenate([got, cur], axis=1), jnp.concatenate([cur, got], axis=1))
+        perm = [(j, j ^ bit) for j in range(n_dev)]
+        if step + 1 < len(order):
+            got = lax.ppermute(cur, "row", perm)
+            cur = jnp.where(hi == 1, jnp.concatenate([got, cur], axis=1), jnp.concatenate([cur, got], axis=1))
+        else:
+            out = []
+            for i in (1, 2, 0):
+                got = lax.ppermute(cur[i], "row", perm)
+                out.append((i, jnp.where(hi == 1, jnp.concatenate([got, cur[i]], axis=0), jnp.concatenate([cur[i], got], axis=0))))
+            cur = tuple(a for _, a in sorted(out))
     return cur
 
 
@@ -75,12 +83,12 @@
     bits = row_bits(n_dev, tokens, units)
     if bits is None:
         sums = lax.psum(jnp.stack(stacked), "row").astype(jnp.float32)
-        return jnp.stack(gated_grads(sums[0], sums[1], sums[2]))
+        return gated_grads(sums[0], sums[1], sums[2])
     orders = (bits, bits[:1] + bits[:0:-1])
     half = units // 2
     reduced = [halving_reduce([a[:, h * half:(h + 1) * half] for a in stacked], o, n_dev) for h, o in enumerate(orders)]
     outs = [doubling_gather(jnp.stack(gated_grads(red[0], red[1], red[2])), o, n_dev) for red, o in zip(reduced, orders)]
-    return jnp.concatenate(outs, axis=2)
+    return tuple(jnp.concatenate([outs[0][i], outs[1][i]], axis=1) for i in range(3))
 
 
 def col_gather(x, n_col):

time: 108 us -> 120 us (1.11)
  waiting for transfers between devices: 36.8 us -> 48.7 us
  matrix products: 29.4 us -> 32.6 us
  other arithmetic: 7.21 us -> 5.01 us
    ppermute x6 -> x10, waiting for transfers between devices: 16.1 us -> 28.5 us  [the longest x4 28 us: doubling_gather(): got = lax.ppermute(cur, 'row', perm)]
    dot_general x3, matrix products: 7.58 us -> 10.8 us  [contract_last(): lax.dot_general(left, right, (((1,), (1,)), ((), ())), preferred_element_...]
    select_n x6 -> x4, other arithmetic: 3.5 us -> 0.7 us  [doubling_gather(): jnp.where(hi == 1, jnp.concatenate([got, cur], axis=1), jnp.concatenate([...]
    unnamed x25 -> x17, local copies, waits for them, and re-layouts: 2.09 us -> 0.87 us
    ppermute x6 -> x10, starting transfers between devices: 5.98 us -> 6.45 us  [the longest x4 5.22 us: doubling_gather(): got = lax.ppermute(cur, 'row', perm)]
  transfers between devices with their start and end apart: 25 -> 29, of which waited for: 10 -> 9; matrix products, arithmetic and copies ran while one was open for 21% -> 26% of each run, Pallas kernels for 0% -> 0%
where the time goes in v14:
time: 120 us
  waiting for transfers between devices  48.7 us (41%)
  matrix products  32.6 us (27%)
  starting transfers between devices  30.6 us (26%)
  other arithmetic  5.01 us (4%)
  local copies, waits for them, and re-layouts  1.64 us (1%)
    ppermute x4, waiting for transfers between devices, doubling_gather(): got = lax.ppermute(cur, 'row', perm)  28 us
    ppermute x4, waiting for transfers between devices, halving_reduce(): got = lax.ppermute(send, 'row', perm)  14.6 us
    ppermute x6, starting transfers between devices, col_gather(): lax.ppermute(x, 'col', [(j, (j + s) % n_col) for j in range(n_col)])  13.2 us
    dot_general x3, matrix products, contract_last(): lax.dot_general(left, right, (((1,), (1,)), ((), ())), preferred_element_...  10.8 us
    ppermute x4, starting transfers between devices, halving_reduce(): got = lax.ppermute(send, 'row', perm)  6.28 us
    ppermute x4, starting transfers between devices, doubling_gather(): got = lax.ppermute(cur, 'row', perm)  5.22 us
    dot_general x1, matrix products, body(): jnp.dot(tok_t, grad_gate, preferred_element_type=jnp.float32)  5.18 us
    dot_general x1, matrix products, contract_first(): lax.dot_general(left, right, (((0,), (0,)), ((), ())), preferred_element_...  5.18 us
  transfers between devices with their start and end apart: 29, of which 9 were waited for; matrix products, arithmetic and copies ran while one was open for 26% of the time, Pallas kernels for 0%

profile of v14, /device:TPU:0, one launch (start us, length us, event | category | flops | bytes accessed | tf_op | source)
XLA Modules:
  0.0 119.7 jit_solution(11909418629468727519)
XLA Ops:
  0.6 4.1 %collective-permute-start.1 = (bf16[48,1024]{1,0:T(8,128)(2,1)}, bf16[48,1024]{1,0:T(8,128)(2,1)S(1)}, u32[]{:S(2)}, u32[]{:S(2)}) collective-permute-start(bf16[48,1024]{1,0:T(8,128)(2,1)} %param.5), channel_id=1, source_target_pairs={{0,2},{1,3},{2,0},{3,1},{4,6},{5,7},{6,4},{7,5},{8,10},{9,11},{10,... | collective-permute-start | bytes 294920 | tf_op jit(solution)/shard_map/ppermute | solution.py:97
  4.8 1.6 %collective-permute-start = (bf16[48,1024]{1,0:T(8,128)(2,1)}, bf16[48,1024]{1,0:T(8,128)(2,1)S(1)}, u32[]{:S(2)}, u32[]{:S(2)}) collective-permute-start(bf16[48,1024]{1,0:T(8,128)(2,1)} %param.5), channel_id=1, source_target_pairs={{0,1},{1,2},{2,3},{3,0},{4,5},{5,6},{6,7},{7,4},{8,9},{9,10},{10,1... | collective-permute-start | bytes 294920 | tf_op jit(solution)/shard_map/ppermute | solution.py:97
  6.3 2.2 %collective-permute-start.2 = (bf16[48,1024]{1,0:T(8,128)(2,1)}, bf16[48,1024]{1,0:T(8,128)(2,1)S(1)}, u32[]{:S(2)}, u32[]{:S(2)}) collective-permute-start(bf16[48,1024]{1,0:T(8,128)(2,1)} %param.5), channel_id=1, source_target_pairs={{0,3},{1,0},{2,1},{3,2},{4,7},{5,4},{6,5},{7,6},{8,11},{9,8},{10,9... | collective-permute-start | bytes 294920 | tf_op jit(solution)/shard_map/ppermute | solution.py:97
  8.6 4.3 %collective-permute-done.1 = bf16[48,1024]{1,0:T(8,128)(2,1)S(1)} collective-permute-done((bf16[48,1024]{1,0:T(8,128)(2,1)}, bf16[48,1024]{1,0:T(8,128)(2,1)S(1)}, u32[]{:S(2)}, u32[]{:S(2)}) %collective-permute-start.1) | collective-permute-done | bytes 98336 | tf_op jit(solution)/shard_map/ppermute | solution.py:97
  12.9 0.7 collective-permute-done.2
  13.6 1.1 pad_maximum_fusion.5
  14.7 2.1 %collective-permute-start.7 = (bf16[48,1024]{1,0:T(8,128)(2,1)}, bf16[48,1024]{1,0:T(8,128)(2,1)S(1)}, u32[]{:S(2)}, u32[]{:S(2)}) collective-permute-start(bf16[48,1024]{1,0:T(8,128)(2,1)} %param.6), channel_id=1, source_target_pairs={{0,3},{1,0},{2,1},{3,2},{4,7},{5,4},{6,5},{7,6},{8,11},{9,8},{10,9... | collective-permute-start | bytes 294920 | tf_op jit(solution)/shard_map/ppermute | solution.py:97
  16.8 1.2 collective-permute-start.6
  17.9 1.9 %collective-permute-start.5 = (bf16[48,1024]{1,0:T(8,128)(2,1)}, bf16[48,1024]{1,0:T(8,128)(2,1)S(1)}, u32[]{:S(2)}, u32[]{:S(2)}) collective-permute-start(bf16[48,1024]{1,0:T(8,128)(2,1)} %param.6), channel_id=1, source_target_pairs={{0,1},{1,2},{2,3},{3,0},{4,5},{5,6},{6,7},{7,4},{8,9},{9,10},{10,1... | collective-permute-start | bytes 294920 | tf_op jit(solution)/shard_map/ppermute | solution.py:97
  19.9 4.7 %convolution_convert_fusion.4 = bf16[192,3584]{1,0:T(8,128)(2,1)S(1)} fusion(bf16[192,1024]{1,0:T(8,128)(2,1)S(1)} %pad_maximum_fusion.5, bf16[1024,3584]{1,0:T(8,128)(2,1)} %param.8), kind=kOutput, calls=%fused_computation.4 | convolution fusion | flops 1409974272 | bytes 9109504 | tf_op jit(solution)/shard_map/dot_general | solution.py:119
  24.6 0.1 fusion.9
  24.9 0.5 collective-permute-start.4
  25.4 1.6 %convolution_convert_fusion.5 = bf16[192,3584]{1,0:T(8,128)(2,1)S(1)} fusion(bf16[192,1024]{1,0:T(8,128)(2,1)S(1)} %pad_maximum_fusion.5, bf16[1024,3584]{1,0:T(8,128)(2,1)S(1)} %bitcast.41), kind=kOutput, calls=%fused_computation.5 | convolution fusion | flops 1409974272 | bytes 9109504 | tf_op jit(solution)/shard_map/dot_general | solution.py:118
  27.0 0.1 fusion.8
  27.2 0.8 copy-done
  28.0 0.1 collective-permute-start.14
  28.2 0.5 collective-permute-start.3
  28.7 2.6 %convolution_convert_fusion.3 = bf16[192,3584]{1,0:T(8,128)(2,1)S(1)} fusion(bf16[192,1024]{1,0:T(8,128)(2,1)S(1)} %constant_dynamic-update-slice_fusion, bf16[3584,1024]{1,0:T(8,128)(2,1)S(1)} %bitcast.39), kind=kOutput, calls=%fused_computation.3 | convolution fusion | flops 1409974272 | bytes 9109504 | tf_op jit(solution)/shard_map/dot_general | solution.py:14
  31.4 0.1 collective-permute-start.16
  31.6 0.5 collective-permute-start.8
  32.5 0.6 collective-permute-done.16
  33.2 0.1 pad_maximum_fusion.4
  33.4 1.6 %collective-permute-start.17 = (bf16[3,48,1792]{2,1,0:T(8,128)(2,1)S(1)}, bf16[3,48,1792]{2,1,0:T(8,128)(2,1)S(1)}, u32[]{:S(2)}, u32[]{:S(2)}) collective-permute-start(bf16[3,48,1792]{2,1,0:T(8,128)(2,1)S(1)} %constant_dynamic-slice_fusion.1), channel_id=1, source_target_pairs={{0,16},{4,20},{8,24},{12,28},{16,0},{20,4},{24,8},{28,12},{1,17},{... | collective-permute-start | bytes 1548296 | tf_op jit(solution)/shard_map/ppermute | solution.py:45
  35.1 0.1 pad_maximum_fusion.3
  35.2 1.6 %collective-permute-start.9 = (bf16[3,48,1792]{2,1,0:T(8,128)(2,1)S(1)}, bf16[3,48,1792]{2,1,0:T(8,128)(2,1)S(1)}, u32[]{:S(2)}, u32[]{:S(2)}) collective-permute-start(bf16[3,48,1792]{2,1,0:T(8,128)(2,1)S(1)} %constant_dynamic-slice_fusion.6), channel_id=1, source_target_pairs={{0,8},{4,12},{8,0},{12,4},{16,24},{20,28},{24,16},{28,20},{1,9},{5... | collective-permute-start | bytes 1548296 | tf_op jit(solution)/shard_map/ppermute | solution.py:45
  36.8 10.4 %collective-permute-done.17 = bf16[3,48,1792]{2,1,0:T(8,128)(2,1)S(1)} collective-permute-done((bf16[3,48,1792]{2,1,0:T(8,128)(2,1)S(1)}, bf16[3,48,1792]{2,1,0:T(8,128)(2,1)S(1)}, u32[]{:S(2)}, u32[]{:S(2)}) %collective-permute-start.17) | collective-permute-done | bytes 516128 | tf_op jit(solution)/shard_map/ppermute | solution.py:45
  47.3 0.1 add_convert_fusion
  47.4 1.5 %collective-permute-start.18 = (bf16[3,24,1792]{2,1,0:T(8,128)(2,1)S(1)}, bf16[3,24,1792]{2,1,0:T(8,128)(2,1)S(1)}, u32[]{:S(2)}, u32[]{:S(2)}) collective-permute-start(bf16[3,24,1792]{2,1,0:T(8,128)(2,1)S(1)} %constant_dynamic-slice_fusion), channel_id=1, source_target_pairs={{0,8},{4,12},{8,0},{12,4},{16,24},{20,28},{24,16},{28,20},{1,9},{5... | collective-permute-start | bytes 774152 | tf_op jit(solution)/shard_map/ppermute | solution.py:45
  49.0 0.1 add_convert_fusion.1
  49.1 1.6 %collective-permute-start.10 = (bf16[3,24,1792]{2,1,0:T(8,128)(2,1)S(1)}, bf16[3,24,1792]{2,1,0:T(8,128)(2,1)S(1)}, u32[]{:S(2)}, u32[]{:S(2)}) collective-permute-start(bf16[3,24,1792]{2,1,0:T(8,128)(2,1)S(1)} %constant_dynamic-slice_fusion.5), channel_id=1, source_target_pairs={{0,16},{4,20},{8,24},{12,28},{16,0},{20,4},{24,8},{28,12},{1,17},{... | collective-permute-start | bytes 774152 | tf_op jit(solution)/shard_map/ppermute | solution.py:45
  50.7 4.2 %collective-permute-done.18 = bf16[3,24,1792]{2,1,0:T(8,128)(2,1)S(1)} collective-permute-done((bf16[3,24,1792]{2,1,0:T(8,128)(2,1)S(1)}, bf16[3,24,1792]{2,1,0:T(8,128)(2,1)S(1)}, u32[]{:S(2)}, u32[]{:S(2)}) %collective-permute-start.18) | collective-permute-done | bytes 258080 | tf_op jit(solution)/shard_map/ppermute | solution.py:45
  55.0 0.1 multiply_convert_fusion.2
  55.1 1.5 %collective-permute-start.19 = (bf16[3,24,1792]{2,1,0:T(8,128)(2,1)S(1)}, bf16[3,24,1792]{2,1,0:T(8,128)(2,1)S(1)}, u32[]{:S(2)}, u32[]{:S(2)}) collective-permute-start(bf16[3,24,1792]{2,1,0:T(8,128)(2,1)S(1)} %pad_maximum_fusion.7), channel_id=1, source_target_pairs={{0,8},{4,12},{8,0},{12,4},{16,24},{20,28},{24,16},{28,20},{1,9},{5... | collective-permute-start | bytes 774152 | tf_op jit(solution)/shard_map/ppermute | solution.py:60
  56.7 0.1 multiply_convert_fusion.5
  56.8 4.9 %collective-permute-done.19 = bf16[3,24,1792]{2,1,0:T(8,128)(2,1)S(1)} collective-permute-done((bf16[3,24,1792]{2,1,0:T(8,128)(2,1)S(1)}, bf16[3,24,1792]{2,1,0:T(8,128)(2,1)S(1)}, u32[]{:S(2)}, u32[]{:S(2)}) %collective-permute-start.19) | collective-permute-done | bytes 258080 | tf_op jit(solution)/shard_map/ppermute | solution.py:60
  61.7 0.1 maximum_select_fusion.9
  61.8 1.5 %collective-permute-start.20 = (bf16[3,48,1792]{2,1,0:T(8,128)(2,1)S(1)}, bf16[3,48,1792]{2,1,0:T(8,128)(2,1)S(1)}, u32[]{:S(2)}, u32[]{:S(2)}) collective-permute-start(bf16[3,48,1792]{2,1,0:T(8,128)(2,1)S(1)} %maximum_select_fusion.9), channel_id=1, source_target_pairs={{0,16},{4,20},{8,24},{12,28},{16,0},{20,4},{24,8},{28,12},{1,17},{... | collective-permute-start | bytes 1548296 | tf_op jit(solution)/shard_map/ppermute | solution.py:60
  63.4 0.6 collective-permute-start.11
  64.0 14.6 %collective-permute-done.11 = bf16[3,24,1792]{2,1,0:T(8,128)(2,1)S(1)} collective-permute-done((bf16[3,24,1792]{2,1,0:T(8,128)(2,1)S(1)}, bf16[3,24,1792]{2,1,0:T(8,128)(2,1)S(1)}, u32[]{:S(2)}, u32[]{:S(2)}) %collective-permute-start.11) | collective-permute-done | bytes 258080 | tf_op jit(solution)/shard_map/ppermute | solution.py:60
  78.6 0.1 maximum_select_fusion.8
  78.7 1.5 %collective-permute-start.12 = (bf16[3,48,1792]{2,1,0:T(8,128)(2,1)S(1)}, bf16[3,48,1792]{2,1,0:T(8,128)(2,1)S(1)}, u32[]{:S(2)}, u32[]{:S(2)}) collective-permute-start(bf16[3,48,1792]{2,1,0:T(8,128)(2,1)S(1)} %maximum_select_fusion.8), channel_id=1, source_target_pairs={{0,8},{4,12},{8,0},{12,4},{16,24},{20,28},{24,16},{28,20},{1,9},{5... | collective-permute-start | bytes 1548296 | tf_op jit(solution)/shard_map/ppermute | solution.py:60
  80.3 0.3 maximum_select_fusion.1
  80.7 8.5 %collective-permute-done.12 = bf16[3,48,1792]{2,1,0:T(8,128)(2,1)S(1)} collective-permute-done((bf16[3,48,1792]{2,1,0:T(8,128)(2,1)S(1)}, bf16[3,48,1792]{2,1,0:T(8,128)(2,1)S(1)}, u32[]{:S(2)}, u32[]{:S(2)}) %collective-permute-start.12) | collective-permute-done | bytes 516128 | tf_op jit(solution)/shard_map/ppermute | solution.py:60
  89.2 0.3 maximum_select_fusion
  89.6 0.5 collective-permute-start.25
  90.2 0.4 collective-permute-start.24
  90.7 0.1 maximum_select_fusion.5
  90.8 0.4 collective-permute-done.22
  91.2 0.1 maximum_select_fusion.4
  91.4 5.7 %fusion.7 = f32[192,1024]{1,0:T(8,128)S(1)} fusion(bf16[1024,3584]{1,0:T(8,128)(2,1)} %param.8, bf16[192,1792]{1,0:T(8,128)(2,1)S(1)} %maximum_select_fusion.5, bf16[192,1792]{1,0:T(8,128)(2,1)S(1)} %maximum_select_fusion.4), kind=kOutput, calls=%fused_computation.71 | convolution fusion | flops 1412038656 | bytes 9502720 | tf_op jit(solution)/shard_map/dot_general | solution.py:14
  97.1 0.1 maximum_select_fusion.3
  97.3 0.1 maximum_select_fusion.2
  97.4 0.1 pad_maximum_fusion
  97.5 2.5 %fusion = bf16[192,1024]{1,0:T(8,128)(2,1)S(1)} fusion(f32[192,1024]{1,0:T(8,128)S(1)} %fusion.7, bf16[1024,3584]{1,0:T(8,128)(2,1)S(1)} %bitcast.43, bf16[192,1792]{1,0:T(8,128)(2,1)S(1)} %maximum_select_fusion.3, bf16[192,1792]{1,0:T(8,128)(2,1)S(1)} %maximum_select_fusion.2), kind=kOutput, calls=%fused_computation.10 | convolution fusion | flops 1412431872 | bytes 9895936 | tf_op jit(solution)/shard_map/dot_general | solution.py:14
  100.2 0.1 maximum_select_fusion.7
  100.3 0.3 maximum_select_fusion.6
  100.6 0.1 pad_maximum_fusion.2
  100.7 5.2 %convolution_convert_fusion.2 = bf16[1024,3584]{1,0:T(8,128)(2,1)} fusion(bf16[192,1024]{1,0:T(8,128)(2,1)S(1)} %pad_maximum_fusion.5, bf16[192,3584]{1,0:T(8,128)(2,1)S(1)} %pad_maximum_fusion), kind=kOutput, calls=%fused_computation.2 | convolution fusion | flops 1412956160 | bytes 9109504 | tf_op jit(solution)/shard_map/dot_general | solution.py:128
  105.9 1.9 %collective-permute-start.26 = (bf16[48,1024]{1,0:T(8,128)(2,1)S(1)}, bf16[48,1024]{1,0:T(8,128)(2,1)S(1)}, u32[]{:S(2)}, u32[]{:S(2)}) collective-permute-start(bf16[48,1024]{1,0:T(8,128)(2,1)S(1)} %get-tuple-element.42), channel_id=1, source_target_pairs={{0,3},{1,0},{2,1},{3,2},{4,7},{5,4},{6,5},{7,6},{8,11},{9,8},{10,9... | collective-permute-start | bytes 294920 | tf_op jit(solution)/shard_map/ppermute | solution.py:105
  107.8 0.1 collective-permute-start.28
  108.0 0.7 collective-permute-start.27
  108.7 5.2 %convolution_convert_fusion.1 = bf16[1024,3584]{1,0:T(8,128)(2,1)} fusion(bf16[192,1024]{1,0:T(8,128)(2,1)S(1)} %pad_maximum_fusion.5, bf16[192,3584]{1,0:T(8,128)(2,1)S(1)} %pad_maximum_fusion.1), kind=kOutput, calls=%fused_computation.1 | convolution fusion | flops 1412956160 | bytes 9109504 | tf_op jit(solution)/shard_map/dot_general | solution.py:131
  113.9 5.2 %convolution_convert_fusion = bf16[3584,1024]{1,0:T(8,128)(2,1)} fusion(bf16[192,3584]{1,0:T(8,128)(2,1)S(1)} %pad_maximum_fusion.2, bf16[192,1024]{1,0:T(8,128)(2,1)S(1)} %constant_dynamic-update-slice_fusion), kind=kOutput, calls=%fused_computation | convolution fusion | flops 1412956160 | bytes 9109504 | tf_op jit(solution)/shard_map/dot_general | solution.py:8
  119.0 0.7 add_convert_fusion.8
  (70 shorter events, 1.9 us)
Async XLA Ops:
  0.6 12.2 %collective-permute-start.1 = (bf16[48,1024]{1,0:T(8,128)(2,1)}, bf16[48,1024]{1,0:T(8,128)(2,1)S(1)}, u32[]{:S(2)}, u32[]{:S(2)}) collective-permute-start(bf16[48,1024]{1,0:T(8,128)(2,1)} %param.5), channel_id=1, source_target_pairs={{0,2},{1,3},{2,0},{3,1},{4,6},{5,7},{6,4},{7,5},{8,10},{9,11},{10,... | collective-permute-start | bytes 294920 | tf_op jit(solution)/shard_map/ppermute | solution.py:97
  4.8 8.1 %collective-permute-start = (bf16[48,1024]{1,0:T(8,128)(2,1)}, bf16[48,1024]{1,0:T(8,128)(2,1)S(1)}, u32[]{:S(2)}, u32[]{:S(2)}) collective-permute-start(bf16[48,1024]{1,0:T(8,128)(2,1)} %param.5), channel_id=1, source_target_pairs={{0,1},{1,2},{2,3},{3,0},{4,5},{5,6},{6,7},{7,4},{8,9},{9,10},{10,1... | collective-permute-start | bytes 294920 | tf_op jit(solution)/shard_map/ppermute | solution.py:97
  6.3 7.2 %collective-permute-start.2 = (bf16[48,1024]{1,0:T(8,128)(2,1)}, bf16[48,1024]{1,0:T(8,128)(2,1)S(1)}, u32[]{:S(2)}, u32[]{:S(2)}) collective-permute-start(bf16[48,1024]{1,0:T(8,128)(2,1)} %param.5), channel_id=1, source_target_pairs={{0,3},{1,0},{2,1},{3,2},{4,7},{5,4},{6,5},{7,6},{8,11},{9,8},{10,9... | collective-permute-start | bytes 294920 | tf_op jit(solution)/shard_map/ppermute | solution.py:97
  13.6 11.8 %slice-start.2 = ((s8[7340032]{0:T(1024)(128)(4,1)}), s8[4194304]{0:T(1024)(128)(4,1)S(1)}, s32[]{:S(2)}) async-start(s8[7340032]{0:T(1024)(128)(4,1)} %bitcast.40), calls=%async_computation.2 | async-start | bytes 8388608
  14.6 10.7 %slice-start.3 = ((s8[7340032]{0:T(1024)(128)(4,1)}), s8[3145728]{0:T(1024)(128)(4,1)S(1)}, s32[]{:S(2)}) async-start(s8[7340032]{0:T(1024)(128)(4,1)} %bitcast.40), calls=%async_computation.3 | async-start | bytes 6291456
  14.7 14.0 %collective-permute-start.7 = (bf16[48,1024]{1,0:T(8,128)(2,1)}, bf16[48,1024]{1,0:T(8,128)(2,1)S(1)}, u32[]{:S(2)}, u32[]{:S(2)}) collective-permute-start(bf16[48,1024]{1,0:T(8,128)(2,1)} %param.6), channel_id=1, source_target_pairs={{0,3},{1,0},{2,1},{3,2},{4,7},{5,4},{6,5},{7,6},{8,11},{9,8},{10,9... | collective-permute-start | bytes 294920 | tf_op jit(solution)/shard_map/ppermute | solution.py:97
  16.8 11.4 %collective-permute-start.6 = (bf16[48,1024]{1,0:T(8,128)(2,1)}, bf16[48,1024]{1,0:T(8,128)(2,1)S(1)}, u32[]{:S(2)}, u32[]{:S(2)}) collective-permute-start(bf16[48,1024]{1,0:T(8,128)(2,1)} %param.6), channel_id=1, source_target_pairs={{0,2},{1,3},{2,0},{3,1},{4,6},{5,7},{6,4},{7,5},{8,10},{9,11},{10,... | collective-permute-start | bytes 294920 | tf_op jit(solution)/shard_map/ppermute | solution.py:97
  17.9 10.1 %collective-permute-start.5 = (bf16[48,1024]{1,0:T(8,128)(2,1)}, bf16[48,1024]{1,0:T(8,128)(2,1)S(1)}, u32[]{:S(2)}, u32[]{:S(2)}) collective-permute-start(bf16[48,1024]{1,0:T(8,128)(2,1)} %param.6), channel_id=1, source_target_pairs={{0,1},{1,2},{2,3},{3,0},{4,5},{5,6},{6,7},{7,4},{8,9},{9,10},{10,1... | collective-permute-start | bytes 294920 | tf_op jit(solution)/shard_map/ppermute | solution.py:97
  24.7 4.0 %slice-start = ((s8[7340032]{0:T(1024)(128)(4,1)}), s8[4194304]{0:T(1024)(128)(4,1)S(1)}, s32[]{:S(2)}) async-start(s8[7340032]{0:T(1024)(128)(4,1)} %bitcast.38), calls=%async_computation | async-start | bytes 8388608
  24.8 4.0 %slice-start.1 = ((s8[7340032]{0:T(1024)(128)(4,1)}), s8[3145728]{0:T(1024)(128)(4,1)S(1)}, s32[]{:S(2)}) async-start(s8[7340032]{0:T(1024)(128)(4,1)} %bitcast.38), calls=%async_computation.1 | async-start | bytes 6291456
  24.8 6.8 %collective-permute-start.15 = (bf16[96,1792]{1,0:T(8,128)(2,1)S(1)}, bf16[96,1792]{1,0:T(8,128)(2,1)S(1)}, u32[]{:S(2)}, u32[]{:S(2)}) collective-permute-start(bf16[96,1792]{1,0:T(8,128)(2,1)S(1)} %constant_dynamic-slice_fusion.3), channel_id=1, source_target_pairs={{0,4},{4,0},{8,12},{12,8},{16,20},{20,16},{24,28},{28,24},{1,5},{5... | collective-permute-start | bytes 1032200 | tf_op jit(solution)/shard_map/ppermute | solution.py:39
  24.9 7.3 %collective-permute-start.4 = (bf16[96,1792]{1,0:T(8,128)(2,1)S(1)}, bf16[96,1792]{1,0:T(8,128)(2,1)S(1)}, u32[]{:S(2)}, u32[]{:S(2)}) collective-permute-start(bf16[96,1792]{1,0:T(8,128)(2,1)S(1)} %constant_dynamic-slice_fusion.8), channel_id=1, source_target_pairs={{0,4},{4,0},{8,12},{12,8},{16,20},{20,16},{24,28},{28,24},{1,5},{5... | collective-permute-start | bytes 1032200 | tf_op jit(solution)/shard_map/ppermute | solution.py:39
  27.1 0.9 copy-start
  28.0 4.3 %collective-permute-start.14 = (bf16[96,1792]{1,0:T(8,128)(2,1)S(1)}, bf16[96,1792]{1,0:T(8,128)(2,1)S(1)}, u32[]{:S(2)}, u32[]{:S(2)}) collective-permute-start(bf16[96,1792]{1,0:T(8,128)(2,1)S(1)} %constant_dynamic-slice_fusion.4), channel_id=1, source_target_pairs={{0,4},{4,0},{8,12},{12,8},{16,20},{20,16},{24,28},{28,24},{1,5},{5... | collective-permute-start | bytes 1032200 | tf_op jit(solution)/shard_map/ppermute | solution.py:39
  28.2 4.2 %collective-permute-start.3 = (bf16[96,1792]{1,0:T(8,128)(2,1)S(1)}, bf16[96,1792]{1,0:T(8,128)(2,1)S(1)}, u32[]{:S(2)}, u32[]{:S(2)}) collective-permute-start(bf16[96,1792]{1,0:T(8,128)(2,1)S(1)} %constant_dynamic-slice_fusion.9), channel_id=1, source_target_pairs={{0,4},{4,0},{8,12},{12,8},{16,20},{20,16},{24,28},{28,24},{1,5},{5... | collective-permute-start | bytes 1032200 | tf_op jit(solution)/shard_map/ppermute | solution.py:39
  31.4 1.7 %collective-permute-start.16 = (bf16[96,1792]{1,0:T(8,128)(2,1)S(1)}, bf16[96,1792]{1,0:T(8,128)(2,1)S(1)}, u32[]{:S(2)}, u32[]{:S(2)}) collective-permute-start(bf16[96,1792]{1,0:T(8,128)(2,1)S(1)} %constant_dynamic-slice_fusion.2), channel_id=1, source_target_pairs={{0,4},{4,0},{8,12},{12,8},{16,20},{20,16},{24,28},{28,24},{1,5},{5... | collective-permute-start | bytes 1032200 | tf_op jit(solution)/shard_map/ppermute | solution.py:39
  31.6 3.4 %collective-permute-start.8 = (bf16[96,1792]{1,0:T(8,128)(2,1)S(1)}, bf16[96,1792]{1,0:T(8,128)(2,1)S(1)}, u32[]{:S(2)}, u32[]{:S(2)}) collective-permute-start(bf16[96,1792]{1,0:T(8,128)(2,1)S(1)} %constant_dynamic-slice_fusion.7), channel_id=1, source_target_pairs={{0,4},{4,0},{8,12},{12,8},{16,20},{20,16},{24,28},{28,24},{1,5},{5... | collective-permute-start | bytes 1032200 | tf_op jit(solution)/shard_map/ppermute | solution.py:39
  33.4 13.9 %collective-permute-start.17 = (bf16[3,48,1792]{2,1,0:T(8,128)(2,1)S(1)}, bf16[3,48,1792]{2,1,0:T(8,128)(2,1)S(1)}, u32[]{:S(2)}, u32[]{:S(2)}) collective-permute-start(bf16[3,48,1792]{2,1,0:T(8,128)(2,1)S(1)} %constant_dynamic-slice_fusion.1), channel_id=1, source_target_pairs={{0,16},{4,20},{8,24},{12,28},{16,0},{20,4},{24,8},{28,12},{1,17},{... | collective-permute-start | bytes 1548296 | tf_op jit(solution)/shard_map/ppermute | solution.py:45
  35.2 13.7 %collective-permute-start.9 = (bf16[3,48,1792]{2,1,0:T(8,128)(2,1)S(1)}, bf16[3,48,1792]{2,1,0:T(8,128)(2,1)S(1)}, u32[]{:S(2)}, u32[]{:S(2)}) collective-permute-start(bf16[3,48,1792]{2,1,0:T(8,128)(2,1)S(1)} %constant_dynamic-slice_fusion.6), channel_id=1, source_target_pairs={{0,8},{4,12},{8,0},{12,4},{16,24},{20,28},{24,16},{28,20},{1,9},{5... | collective-permute-start | bytes 1548296 | tf_op jit(solution)/shard_map/ppermute | solution.py:45
  47.4 7.5 %collective-permute-start.18 = (bf16[3,24,1792]{2,1,0:T(8,128)(2,1)S(1)}, bf16[3,24,1792]{2,1,0:T(8,128)(2,1)S(1)}, u32[]{:S(2)}, u32[]{:S(2)}) collective-permute-start(bf16[3,24,1792]{2,1,0:T(8,128)(2,1)S(1)} %constant_dynamic-slice_fusion), channel_id=1, source_target_pairs={{0,8},{4,12},{8,0},{12,4},{16,24},{20,28},{24,16},{28,20},{1,9},{5... | collective-permute-start | bytes 774152 | tf_op jit(solution)/shard_map/ppermute | solution.py:45
  49.1 7.5 %collective-permute-start.10 = (bf16[3,24,1792]{2,1,0:T(8,128)(2,1)S(1)}, bf16[3,24,1792]{2,1,0:T(8,128)(2,1)S(1)}, u32[]{:S(2)}, u32[]{:S(2)}) collective-permute-start(bf16[3,24,1792]{2,1,0:T(8,128)(2,1)S(1)} %constant_dynamic-slice_fusion.5), channel_id=1, source_target_pairs={{0,16},{4,20},{8,24},{12,28},{16,0},{20,4},{24,8},{28,12},{1,17},{... | collective-permute-start | bytes 774152 | tf_op jit(solution)/shard_map/ppermute | solution.py:45
  55.1 6.6 %collective-permute-start.19 = (bf16[3,24,1792]{2,1,0:T(8,128)(2,1)S(1)}, bf16[3,24,1792]{2,1,0:T(8,128)(2,1)S(1)}, u32[]{:S(2)}, u32[]{:S(2)}) collective-permute-start(bf16[3,24,1792]{2,1,0:T(8,128)(2,1)S(1)} %pad_maximum_fusion.7), channel_id=1, source_target_pairs={{0,8},{4,12},{8,0},{12,4},{16,24},{20,28},{24,16},{28,20},{1,9},{5... | collective-permute-start | bytes 774152 | tf_op jit(solution)/shard_map/ppermute | solution.py:60
  61.8 18.5 %collective-permute-start.20 = (bf16[3,48,1792]{2,1,0:T(8,128)(2,1)S(1)}, bf16[3,48,1792]{2,1,0:T(8,128)(2,1)S(1)}, u32[]{:S(2)}, u32[]{:S(2)}) collective-permute-start(bf16[3,48,1792]{2,1,0:T(8,128)(2,1)S(1)} %maximum_select_fusion.9), channel_id=1, source_target_pairs={{0,16},{4,20},{8,24},{12,28},{16,0},{20,4},{24,8},{28,12},{1,17},{... | collective-permute-start | bytes 1548296 | tf_op jit(solution)/shard_map/ppermute | solution.py:60
  63.4 15.2 %collective-permute-start.11 = (bf16[3,24,1792]{2,1,0:T(8,128)(2,1)S(1)}, bf16[3,24,1792]{2,1,0:T(8,128)(2,1)S(1)}, u32[]{:S(2)}, u32[]{:S(2)}) collective-permute-start(bf16[3,24,1792]{2,1,0:T(8,128)(2,1)S(1)} %pad_maximum_fusion.6), channel_id=1, source_target_pairs={{0,16},{4,20},{8,24},{12,28},{16,0},{20,4},{24,8},{28,12},{1,17},{... | collective-permute-start | bytes 774152 | tf_op jit(solution)/shard_map/ppermute | solution.py:60
  78.7 10.4 %collective-permute-start.12 = (bf16[3,48,1792]{2,1,0:T(8,128)(2,1)S(1)}, bf16[3,48,1792]{2,1,0:T(8,128)(2,1)S(1)}, u32[]{:S(2)}, u32[]{:S(2)}) collective-permute-start(bf16[3,48,1792]{2,1,0:T(8,128)(2,1)S(1)} %maximum_select_fusion.8), channel_id=1, source_target_pairs={{0,8},{4,12},{8,0},{12,4},{16,24},{20,28},{24,16},{28,20},{1,9},{5... | collective-permute-start | bytes 1548296 | tf_op jit(solution)/shard_map/ppermute | solution.py:60
  80.6 10.0 %collective-permute-start.23 = (bf16[96,1792]{1,0:T(8,128)(2,1)S(1)}, bf16[96,1792]{1,0:T(8,128)(2,1)S(1)}, u32[]{:S(2)}, u32[]{:S(2)}) collective-permute-start(bf16[96,1792]{1,0:T(8,128)(2,1)S(1)} %get-tuple-element.34), channel_id=1, source_target_pairs={{0,4},{4,0},{8,12},{12,8},{16,20},{20,16},{24,28},{28,24},{1,5},{5... | collective-permute-start | bytes 1032200 | tf_op jit(solution)/shard_map/ppermute | solution.py:65
  89.5 1.7 %collective-permute-start.22 = (bf16[96,1792]{1,0:T(8,128)(2,1)S(1)}, bf16[96,1792]{1,0:T(8,128)(2,1)S(1)}, u32[]{:S(2)}, u32[]{:S(2)}) collective-permute-start(bf16[96,1792]{1,0:T(8,128)(2,1)S(1)} %get-tuple-element.31), channel_id=1, source_target_pairs={{0,4},{4,0},{8,12},{12,8},{16,20},{20,16},{24,28},{28,24},{1,5},{5... | collective-permute-start | bytes 1032200 | tf_op jit(solution)/shard_map/ppermute | solution.py:65
  89.6 10.5 %collective-permute-start.25 = (bf16[96,1792]{1,0:T(8,128)(2,1)S(1)}, bf16[96,1792]{1,0:T(8,128)(2,1)S(1)}, u32[]{:S(2)}, u32[]{:S(2)}) collective-permute-start(bf16[96,1792]{1,0:T(8,128)(2,1)S(1)} %get-tuple-element.33), channel_id=1, source_target_pairs={{0,4},{4,0},{8,12},{12,8},{16,20},{20,16},{24,28},{28,24},{1,5},{5... | collective-permute-start | bytes 1032200 | tf_op jit(solution)/shard_map/ppermute | solution.py:65
  90.1 7.0 %collective-permute-start.21 = (bf16[96,1792]{1,0:T(8,128)(2,1)S(1)}, bf16[96,1792]{1,0:T(8,128)(2,1)S(1)}, u32[]{:S(2)}, u32[]{:S(2)}) collective-permute-start(bf16[96,1792]{1,0:T(8,128)(2,1)S(1)} %get-tuple-element.35), channel_id=1, source_target_pairs={{0,4},{4,0},{8,12},{12,8},{16,20},{20,16},{24,28},{28,24},{1,5},{5... | collective-permute-start | bytes 1032200 | tf_op jit(solution)/shard_map/ppermute | solution.py:65
  90.2 10.1 %collective-permute-start.24 = (bf16[96,1792]{1,0:T(8,128)(2,1)S(1)}, bf16[96,1792]{1,0:T(8,128)(2,1)S(1)}, u32[]{:S(2)}, u32[]{:S(2)}) collective-permute-start(bf16[96,1792]{1,0:T(8,128)(2,1)S(1)} %get-tuple-element.30), channel_id=1, source_target_pairs={{0,4},{4,0},{8,12},{12,8},{16,20},{20,16},{24,28},{28,24},{1,5},{5... | collective-permute-start | bytes 1032200 | tf_op jit(solution)/shard_map/ppermute | solution.py:65
  90.6 6.7 %collective-permute-start.13 = (bf16[96,1792]{1,0:T(8,128)(2,1)S(1)}, bf16[96,1792]{1,0:T(8,128)(2,1)S(1)}, u32[]{:S(2)}, u32[]{:S(2)}) collective-permute-start(bf16[96,1792]{1,0:T(8,128)(2,1)S(1)} %get-tuple-element.32), channel_id=1, source_target_pairs={{0,4},{4,0},{8,12},{12,8},{16,20},{20,16},{24,28},{28,24},{1,5},{5... | collective-permute-start | bytes 1032200 | tf_op jit(solution)/shard_map/ppermute | solution.py:65
  91.2 6.3 %slice-start.4 = ((s8[7340032]{0:T(1024)(128)(4,1)}), s8[4194304]{0:T(1024)(128)(4,1)S(1)}, s32[]{:S(2)}) async-start(s8[7340032]{0:T(1024)(128)(4,1)} %bitcast.42), calls=%async_computation.4 | async-start | bytes 8388608
  91.4 6.1 %slice-start.5 = ((s8[7340032]{0:T(1024)(128)(4,1)}), s8[3145728]{0:T(1024)(128)(4,1)S(1)}, s32[]{:S(2)}) async-start(s8[7340032]{0:T(1024)(128)(4,1)} %bitcast.42), calls=%async_computation.5 | async-start | bytes 6291456
  105.9 13.1 %collective-permute-start.26 = (bf16[48,1024]{1,0:T(8,128)(2,1)S(1)}, bf16[48,1024]{1,0:T(8,128)(2,1)S(1)}, u32[]{:S(2)}, u32[]{:S(2)}) collective-permute-start(bf16[48,1024]{1,0:T(8,128)(2,1)S(1)} %get-tuple-element.42), channel_id=1, source_target_pairs={{0,3},{1,0},{2,1},{3,2},{4,7},{5,4},{6,5},{7,6},{8,11},{9,8},{10,9... | collective-permute-start | bytes 294920 | tf_op jit(solution)/shard_map/ppermute | solution.py:105
  107.8 11.2 %collective-permute-start.28 = (bf16[48,1024]{1,0:T(8,128)(2,1)S(1)}, bf16[48,1024]{1,0:T(8,128)(2,1)S(1)}, u32[]{:S(2)}, u32[]{:S(2)}) collective-permute-start(bf16[48,1024]{1,0:T(8,128)(2,1)S(1)} %get-tuple-element.43), channel_id=1, source_target_pairs={{0,1},{1,2},{2,3},{3,0},{4,5},{5,6},{6,7},{7,4},{8,9},{9,10},{10,1... | collective-permute-start | bytes 294920 | tf_op jit(solution)/shard_map/ppermute | solution.py:105
  108.0 11.1 %collective-permute-start.27 = (bf16[48,1024]{1,0:T(8,128)(2,1)S(1)}, bf16[48,1024]{1,0:T(8,128)(2,1)S(1)}, u32[]{:S(2)}, u32[]{:S(2)}) collective-permute-start(bf16[48,1024]{1,0:T(8,128)(2,1)S(1)} %get-tuple-element.44), channel_id=1, source_target_pairs={{0,2},{1,3},{2,0},{3,1},{4,6},{5,7},{6,4},{7,5},{8,10},{9,11},{10,... | collective-permute-start | bytes 294920 | tf_op jit(solution)/shard_map/ppermute | solution.py:105

commit v15 on v13

--- a/solution.py
+++ b/solution.py
@@ -30,15 +30,21 @@
     r = lax.axis_index("row")
     cur = parts
     for step, bit in enumerate(order):
-        axis = 0 if step == 0 else 1
-        size = cur[0].shape[0] if step == 0 else cur.shape[1]
+        axis = 0 if step < PER_ARRAY_STEPS else 1
+        size = cur[0].shape[0] if step < PER_ARRAY_STEPS else cur.shape[1]
         n = size // 2
         hi = (r // bit) % 2
         perm = [(j, j ^ bit) for j in range(n_dev)]
-        if step == 0:
+        if step < PER_ARRAY_STEPS:
             got = [lax.ppermute(lax.dynamic_slice_in_dim(c, (1 - hi) * n, n, 0), "row", perm) for c in cur]
             keep = [lax.dynamic_slice_in_dim(c, hi * n, n, 0) for c in cur]
-            summed = jnp.stack([k.astype(jnp.float32) + g.astype(jnp.float32) for k, g in zip(keep, got)])
+            summed = [k.astype(jnp.float32) + g.astype(jnp.float32) for k, g in zip(keep, got)]
+            if step + 1 == PER_ARRAY_STEPS or step + 1 == len(order):
+                summed = jnp.stack(summed)
+            elif step + 1 < len(order):
+                summed = [a.astype(jnp.bfloat16) for a in summed]
+                cur = summed
+                continue
         else:
             keep = lax.dynamic_slice_in_dim(cur, hi * n, n, axis)
             send = lax.dynamic_slice_in_dim(cur, (1 - hi) * n, n, axis)
@@ -48,6 +54,9 @@
             summed = summed.astype(jnp.bfloat16)
         cur = summed
     return cur
+
+
+PER_ARRAY_STEPS = 2
 
 
 def doubling_gather(x, order, n_dev):

time: 108 us -> 106 us (0.981)
  waiting for transfers between devices: 36.8 us -> 31.5 us
  starting transfers between devices: 30.2 us -> 33.7 us
    ppermute x4 -> x2, waiting for transfers between devices: 14.6 us -> 4.15 us  [halving_reduce(): got = lax.ppermute(send, 'row', perm)]
    ppermute x6 -> x12, starting transfers between devices: 1.85 us -> 9.24 us  [halving_reduce(): lax.ppermute(lax.dynamic_slice_in_dim(c, (1 - hi) * n, n, 0), 'row', perm)]
    ppermute x6 -> x12, waiting for transfers between devices: 1.14 us -> 5.57 us  [halving_reduce(): lax.ppermute(lax.dynamic_slice_in_dim(c, (1 - hi) * n, n, 0), 'row', perm)]
    ppermute x4 -> x2, starting transfers between devices: 6.28 us -> 3.15 us  [halving_reduce(): got = lax.ppermute(send, 'row', perm)]
  transfers between devices with their start and end apart: 25 -> 29, of which waited for: 10 -> 12; matrix products, arithmetic and copies ran while one was open for 21% -> 21% of each run, Pallas kernels for 0% -> 0%
where the time goes in v15:
time: 106 us
  starting transfers between devices  33.7 us (32%)
  waiting for transfers between devices  31.5 us (30%)
  matrix products  29.4 us (28%)
  other arithmetic  7.1 us (7%)
  local copies, waits for them, and re-layouts  2.76 us (3%)
  between operations  1.18 us (1%)
    ppermute x6, waiting for transfers between devices, doubling_gather(): got = lax.ppermute(cur, 'row', [(j, j ^ bit) for j in range(n_dev)])  16.7 us
    ppermute x6, starting transfers between devices, col_gather(): lax.ppermute(x, 'col', [(j, (j + s) % n_col) for j in range(n_col)])  13.2 us
    ppermute x12, starting transfers between devices, halving_reduce(): lax.ppermute(lax.dynamic_slice_in_dim(c, (1 - hi) * n, n, 0), 'row', perm)  9.24 us
    dot_general x3, matrix products, contract_last(): lax.dot_general(left, right, (((1,), (1,)), ((), ())), preferred_element_...  7.58 us
    ppermute x12, waiting for transfers between devices, halving_reduce(): lax.ppermute(lax.dynamic_slice_in_dim(c, (1 - hi) * n, n, 0), 'row', perm)  5.57 us
    ppermute x6, starting transfers between devices, doubling_gather(): got = lax.ppermute(cur, 'row', [(j, j ^ bit) for j in range(n_dev)])  5.4 us
    dot_general x1, matrix products, contract_first(): lax.dot_general(left, right, (((0,), (0,)), ((), ())), preferred_element_...  5.19 us
    dot_general x1, matrix products, body(): jnp.dot(tok_t, grad_gate, preferred_element_type=jnp.float32)  5.18 us
  transfers between devices with their start and end apart: 29, of which 12 were waited for; matrix products, arithmetic and copies ran while one was open for 21% of the time, Pallas kernels for 0%

profile of v15, /device:TPU:0, one launch (start us, length us, event | category | flops | bytes accessed | tf_op | source)
XLA Modules:
  0.0 105.7 jit_solution(10191800489385596484)
XLA Ops:
  0.6 4.1 %collective-permute-start.1 = (bf16[48,1024]{1,0:T(8,128)(2,1)}, bf16[48,1024]{1,0:T(8,128)(2,1)S(1)}, u32[]{:S(2)}, u32[]{:S(2)}) collective-permute-start(bf16[48,1024]{1,0:T(8,128)(2,1)} %param.5), channel_id=1, source_target_pairs={{0,2},{1,3},{2,0},{3,1},{4,6},{5,7},{6,4},{7,5},{8,10},{9,11},{10,... | collective-permute-start | bytes 294920 | tf_op jit(solution)/shard_map/ppermute | solution.py:98
  4.8 1.6 %collective-permute-start = (bf16[48,1024]{1,0:T(8,128)(2,1)}, bf16[48,1024]{1,0:T(8,128)(2,1)S(1)}, u32[]{:S(2)}, u32[]{:S(2)}) collective-permute-start(bf16[48,1024]{1,0:T(8,128)(2,1)} %param.5), channel_id=1, source_target_pairs={{0,1},{1,2},{2,3},{3,0},{4,5},{5,6},{6,7},{7,4},{8,9},{9,10},{10,1... | collective-permute-start | bytes 294920 | tf_op jit(solution)/shard_map/ppermute | solution.py:98
  6.3 2.2 %collective-permute-start.2 = (bf16[48,1024]{1,0:T(8,128)(2,1)}, bf16[48,1024]{1,0:T(8,128)(2,1)S(1)}, u32[]{:S(2)}, u32[]{:S(2)}) collective-permute-start(bf16[48,1024]{1,0:T(8,128)(2,1)} %param.5), channel_id=1, source_target_pairs={{0,3},{1,0},{2,1},{3,2},{4,7},{5,4},{6,5},{7,6},{8,11},{9,8},{10,9... | collective-permute-start | bytes 294920 | tf_op jit(solution)/shard_map/ppermute | solution.py:98
  8.6 4.3 %collective-permute-done.1 = bf16[48,1024]{1,0:T(8,128)(2,1)S(1)} collective-permute-done((bf16[48,1024]{1,0:T(8,128)(2,1)}, bf16[48,1024]{1,0:T(8,128)(2,1)S(1)}, u32[]{:S(2)}, u32[]{:S(2)}) %collective-permute-start.1) | collective-permute-done | bytes 98336 | tf_op jit(solution)/shard_map/ppermute | solution.py:98
  12.9 0.7 collective-permute-done.2
  13.6 1.1 %pad_maximum_fusion.3 = bf16[192,1024]{1,0:T(8,128)(2,1)S(1)} fusion(bf16[48,1024]{1,0:T(8,128)(2,1)S(1)} %collective-permute-done.2, bf16[48,1024]{1,0:T(8,128)(2,1)S(1)} %collective-permute-done.1, bf16[48,1024]{1,0:T(8,128)(2,1)S(1)} %collective-permute-done, bf16[48,1024]{1,0:T(8,128)(2,1)} %param.5), kind=kLoop, calls=%fused_computation.34 | loop fusion | flops 1572864 | bytes 786432 | tf_op jit(solution)/shard_map/concatenate | solution.py:99
  14.7 2.1 %collective-permute-start.9 = (bf16[48,1024]{1,0:T(8,128)(2,1)}, bf16[48,1024]{1,0:T(8,128)(2,1)S(1)}, u32[]{:S(2)}, u32[]{:S(2)}) collective-permute-start(bf16[48,1024]{1,0:T(8,128)(2,1)} %param.6), channel_id=1, source_target_pairs={{0,3},{1,0},{2,1},{3,2},{4,7},{5,4},{6,5},{7,6},{8,11},{9,8},{10,9... | collective-permute-start | bytes 294920 | tf_op jit(solution)/shard_map/ppermute | solution.py:98
  16.8 1.2 %collective-permute-start.8 = (bf16[48,1024]{1,0:T(8,128)(2,1)}, bf16[48,1024]{1,0:T(8,128)(2,1)S(1)}, u32[]{:S(2)}, u32[]{:S(2)}) collective-permute-start(bf16[48,1024]{1,0:T(8,128)(2,1)} %param.6), channel_id=1, source_target_pairs={{0,2},{1,3},{2,0},{3,1},{4,6},{5,7},{6,4},{7,5},{8,10},{9,11},{10,... | collective-permute-start | bytes 294920 | tf_op jit(solution)/shard_map/ppermute | solution.py:98
  17.9 1.9 %collective-permute-start.7 = (bf16[48,1024]{1,0:T(8,128)(2,1)}, bf16[48,1024]{1,0:T(8,128)(2,1)S(1)}, u32[]{:S(2)}, u32[]{:S(2)}) collective-permute-start(bf16[48,1024]{1,0:T(8,128)(2,1)} %param.6), channel_id=1, source_target_pairs={{0,1},{1,2},{2,3},{3,0},{4,5},{5,6},{6,7},{7,4},{8,9},{9,10},{10,1... | collective-permute-start | bytes 294920 | tf_op jit(solution)/shard_map/ppermute | solution.py:98
  19.9 4.7 %convolution_convert_fusion.4 = bf16[192,3584]{1,0:T(8,128)(2,1)S(1)} fusion(bf16[192,1024]{1,0:T(8,128)(2,1)S(1)} %pad_maximum_fusion.3, bf16[1024,3584]{1,0:T(8,128)(2,1)} %param.8), kind=kOutput, calls=%fused_computation.4 | convolution fusion | flops 1409974272 | bytes 9109504 | tf_op jit(solution)/shard_map/dot_general | solution.py:120
  24.6 0.1 fusion.13
  24.9 0.5 collective-permute-start.18
  25.4 1.6 %convolution_convert_fusion.5 = bf16[192,3584]{1,0:T(8,128)(2,1)S(1)} fusion(bf16[192,1024]{1,0:T(8,128)(2,1)S(1)} %pad_maximum_fusion.3, bf16[1024,3584]{1,0:T(8,128)(2,1)S(1)} %bitcast.39), kind=kOutput, calls=%fused_computation.5 | convolution fusion | flops 1409974272 | bytes 9109504 | tf_op jit(solution)/shard_map/dot_general | solution.py:119
  27.0 0.1 fusion.12
  27.2 0.7 copy-done.2
  27.9 0.1 collective-permute-start.3
  28.1 0.5 collective-permute-start.16
  28.6 2.6 %convolution_convert_fusion.3 = bf16[192,3584]{1,0:T(8,128)(2,1)S(1)} fusion(bf16[192,1024]{1,0:T(8,128)(2,1)S(1)} %constant_dynamic-update-slice_fusion, bf16[3584,1024]{1,0:T(8,128)(2,1)S(1)} %bitcast.35), kind=kOutput, calls=%fused_computation.3 | convolution fusion | flops 1409974272 | bytes 9109504 | tf_op jit(solution)/shard_map/dot_general | solution.py:14
  31.2 0.1 fusion.14
  31.4 0.1 collective-permute-start.10
  31.5 0.5 collective-permute-start.20
  32.2 1.5 %collective-permute-start.6 = (bf16[48,1792]{1,0:T(8,128)(2,1)S(1)}, bf16[48,1792]{1,0:T(8,128)(2,1)S(1)}, u32[]{:S(2)}, u32[]{:S(2)}) collective-permute-start(bf16[48,1792]{1,0:T(8,128)(2,1)S(1)} %constant_dynamic-slice_fusion.10), channel_id=1, source_target_pairs={{0,8},{4,12},{8,0},{12,4},{16,24},{20,28},{24,16},{28,20},{1,9},{5... | collective-permute-start | bytes 516104 | tf_op jit(solution)/shard_map/ppermute | solution.py:39
  33.8 1.6 %collective-permute-start.19 = (bf16[48,1792]{1,0:T(8,128)(2,1)S(1)}, bf16[48,1792]{1,0:T(8,128)(2,1)S(1)}, u32[]{:S(2)}, u32[]{:S(2)}) collective-permute-start(bf16[48,1792]{1,0:T(8,128)(2,1)S(1)} %constant_dynamic-slice_fusion.3), channel_id=1, source_target_pairs={{0,16},{4,20},{8,24},{12,28},{16,0},{20,4},{24,8},{28,12},{1,17},{... | collective-permute-start | bytes 516104 | tf_op jit(solution)/shard_map/ppermute | solution.py:39
  35.6 0.6 collective-permute-start.4
  36.3 0.6 collective-permute-start.17
  36.9 0.1 add_convert_fusion.3
  37.0 1.5 %collective-permute-start.11 = (bf16[48,1792]{1,0:T(8,128)(2,1)S(1)}, bf16[48,1792]{1,0:T(8,128)(2,1)S(1)}, u32[]{:S(2)}, u32[]{:S(2)}) collective-permute-start(bf16[48,1792]{1,0:T(8,128)(2,1)S(1)} %constant_dynamic-slice_fusion.8), channel_id=1, source_target_pairs={{0,8},{4,12},{8,0},{12,4},{16,24},{20,28},{24,16},{28,20},{1,9},{5... | collective-permute-start | bytes 516104 | tf_op jit(solution)/shard_map/ppermute | solution.py:39
  38.6 0.8 collective-permute-done.6
  39.4 1.6 %collective-permute-start.21 = (bf16[48,1792]{1,0:T(8,128)(2,1)S(1)}, bf16[48,1792]{1,0:T(8,128)(2,1)S(1)}, u32[]{:S(2)}, u32[]{:S(2)}) collective-permute-start(bf16[48,1792]{1,0:T(8,128)(2,1)S(1)} %constant_dynamic-slice_fusion.1), channel_id=1, source_target_pairs={{0,16},{4,20},{8,24},{12,28},{16,0},{20,4},{24,8},{28,12},{1,17},{... | collective-permute-start | bytes 516104 | tf_op jit(solution)/shard_map/ppermute | solution.py:39
  41.0 2.1 %collective-permute-done.4 = bf16[48,1792]{1,0:T(8,128)(2,1)S(1)} collective-permute-done((bf16[48,1792]{1,0:T(8,128)(2,1)S(1)}, bf16[48,1792]{1,0:T(8,128)(2,1)S(1)}, u32[]{:S(2)}, u32[]{:S(2)}) %collective-permute-start.4) | collective-permute-done | bytes 172064 | tf_op jit(solution)/shard_map/ppermute | solution.py:39
  43.2 1.6 %collective-permute-done.17 = bf16[48,1792]{1,0:T(8,128)(2,1)S(1)} collective-permute-done((bf16[48,1792]{1,0:T(8,128)(2,1)S(1)}, bf16[48,1792]{1,0:T(8,128)(2,1)S(1)}, u32[]{:S(2)}, u32[]{:S(2)}) %collective-permute-start.17) | collective-permute-done | bytes 172064 | tf_op jit(solution)/shard_map/ppermute | solution.py:39
  44.9 1.1 %collective-permute-done.11 = bf16[48,1792]{1,0:T(8,128)(2,1)S(1)} collective-permute-done((bf16[48,1792]{1,0:T(8,128)(2,1)S(1)}, bf16[48,1792]{1,0:T(8,128)(2,1)S(1)}, u32[]{:S(2)}, u32[]{:S(2)}) %collective-permute-start.11) | collective-permute-done | bytes 172064 | tf_op jit(solution)/shard_map/ppermute | solution.py:39
  46.1 1.6 %collective-permute-start.12 = (bf16[3,24,1792]{2,1,0:T(8,128)(2,1)S(1)}, bf16[3,24,1792]{2,1,0:T(8,128)(2,1)S(1)}, u32[]{:S(2)}, u32[]{:S(2)}) collective-permute-start(bf16[3,24,1792]{2,1,0:T(8,128)(2,1)S(1)} %constant_dynamic-slice_fusion.7), channel_id=1, source_target_pairs={{0,16},{4,20},{8,24},{12,28},{16,0},{20,4},{24,8},{28,12},{1,17},{... | collective-permute-start | bytes 774152 | tf_op jit(solution)/shard_map/ppermute | solution.py:51
  47.9 1.5 %collective-permute-start.22 = (bf16[3,24,1792]{2,1,0:T(8,128)(2,1)S(1)}, bf16[3,24,1792]{2,1,0:T(8,128)(2,1)S(1)}, u32[]{:S(2)}, u32[]{:S(2)}) collective-permute-start(bf16[3,24,1792]{2,1,0:T(8,128)(2,1)S(1)} %constant_dynamic-slice_fusion), channel_id=1, source_target_pairs={{0,8},{4,12},{8,0},{12,4},{16,24},{20,28},{24,16},{28,20},{1,9},{5... | collective-permute-start | bytes 774152 | tf_op jit(solution)/shard_map/ppermute | solution.py:51
  49.4 4.2 %collective-permute-done.12 = bf16[3,24,1792]{2,1,0:T(8,128)(2,1)S(1)} collective-permute-done((bf16[3,24,1792]{2,1,0:T(8,128)(2,1)S(1)}, bf16[3,24,1792]{2,1,0:T(8,128)(2,1)S(1)}, u32[]{:S(2)}, u32[]{:S(2)}) %collective-permute-start.12) | collective-permute-done | bytes 258080 | tf_op jit(solution)/shard_map/ppermute | solution.py:51
  53.6 0.1 multiply_convert_fusion.5
  53.8 1.6 %collective-permute-start.13 = (bf16[3,24,1792]{2,1,0:T(8,128)(2,1)S(1)}, bf16[3,24,1792]{2,1,0:T(8,128)(2,1)S(1)}, u32[]{:S(2)}, u32[]{:S(2)}) collective-permute-start(bf16[3,24,1792]{2,1,0:T(8,128)(2,1)S(1)} %pad_maximum_fusion.4), channel_id=1, source_target_pairs={{0,16},{4,20},{8,24},{12,28},{16,0},{20,4},{24,8},{28,12},{1,17},{... | collective-permute-start | bytes 774152 | tf_op jit(solution)/shard_map/ppermute | solution.py:67
  55.4 0.1 multiply_convert_fusion.2
  55.6 1.5 %collective-permute-start.23 = (bf16[3,24,1792]{2,1,0:T(8,128)(2,1)S(1)}, bf16[3,24,1792]{2,1,0:T(8,128)(2,1)S(1)}, u32[]{:S(2)}, u32[]{:S(2)}) collective-permute-start(bf16[3,24,1792]{2,1,0:T(8,128)(2,1)S(1)} %pad_maximum_fusion.5), channel_id=1, source_target_pairs={{0,8},{4,12},{8,0},{12,4},{16,24},{20,28},{24,16},{28,20},{1,9},{5... | collective-permute-start | bytes 774152 | tf_op jit(solution)/shard_map/ppermute | solution.py:67
  57.1 3.3 %collective-permute-done.13 = bf16[3,24,1792]{2,1,0:T(8,128)(2,1)S(1)} collective-permute-done((bf16[3,24,1792]{2,1,0:T(8,128)(2,1)S(1)}, bf16[3,24,1792]{2,1,0:T(8,128)(2,1)S(1)}, u32[]{:S(2)}, u32[]{:S(2)}) %collective-permute-start.13) | collective-permute-done | bytes 258080 | tf_op jit(solution)/shard_map/ppermute | solution.py:67
  60.4 0.1 maximum_select_fusion.4
  60.5 1.5 %collective-permute-start.14 = (bf16[3,48,1792]{2,1,0:T(8,128)(2,1)S(1)}, bf16[3,48,1792]{2,1,0:T(8,128)(2,1)S(1)}, u32[]{:S(2)}, u32[]{:S(2)}) collective-permute-start(bf16[3,48,1792]{2,1,0:T(8,128)(2,1)S(1)} %maximum_select_fusion.4), channel_id=1, source_target_pairs={{0,8},{4,12},{8,0},{12,4},{16,24},{20,28},{24,16},{28,20},{1,9},{5... | collective-permute-start | bytes 1548296 | tf_op jit(solution)/shard_map/ppermute | solution.py:67
  62.0 1.3 %collective-permute-done.23 = bf16[3,24,1792]{2,1,0:T(8,128)(2,1)S(1)} collective-permute-done((bf16[3,24,1792]{2,1,0:T(8,128)(2,1)S(1)}, bf16[3,24,1792]{2,1,0:T(8,128)(2,1)S(1)}, u32[]{:S(2)}, u32[]{:S(2)}) %collective-permute-start.23) | collective-permute-done | bytes 258080 | tf_op jit(solution)/shard_map/ppermute | solution.py:67
  63.3 0.1 maximum_select_fusion.5
  63.4 0.2 collective-permute-start.24
  63.6 9.5 %collective-permute-done.14 = bf16[3,48,1792]{2,1,0:T(8,128)(2,1)S(1)} collective-permute-done((bf16[3,48,1792]{2,1,0:T(8,128)(2,1)S(1)}, bf16[3,48,1792]{2,1,0:T(8,128)(2,1)S(1)}, u32[]{:S(2)}, u32[]{:S(2)}) %collective-permute-start.14) | collective-permute-done | bytes 516128 | tf_op jit(solution)/shard_map/ppermute | solution.py:67
  73.0 0.3 maximum_select_fusion.2
  73.4 0.3 maximum_select_fusion.3
  73.7 0.6 collective-permute-start.25
  74.2 1.8 %collective-permute-done.15 = bf16[3,96,1792]{2,1,0:T(8,128)(2,1)S(1)} collective-permute-done((bf16[3,96,1792]{2,1,0:T(8,128)(2,1)S(1)}, bf16[3,96,1792]{2,1,0:T(8,128)(2,1)S(1)}, u32[]{:S(2)}, u32[]{:S(2)}) %collective-permute-start.15) | collective-permute-done | bytes 1032224 | tf_op jit(solution)/shard_map/ppermute | solution.py:67
  76.0 0.8 maximum_select_fusion
  76.8 0.8 collective-permute-done.25
  77.6 2.0 %maximum_select_fusion.1 = bf16[3,192,1792]{2,1,0:T(8,128)(2,1)S(1)} fusion(bf16[3,96,1792]{2,1,0:T(8,128)(2,1)S(1)} %maximum_select_fusion.3, bf16[3,96,1792]{2,1,0:T(8,128)(2,1)} %collective-permute-done.25, pred[]{:T(512)S(6)} %eq.25), kind=kLoop, calls=%fused_computation.11 | loop fusion | flops 9289728 | bytes 4128769 | tf_op jit(solution)/shard_map/jit(_where)/select_n | solution.py:68
  79.7 0.5 fusion.4
  80.2 1.3 %slice-done.3 = s8[3145728]{0:T(1024)(128)(4,1)S(1)} async-done(((s8[7340032]{0:T(1024)(128)(4,1)}), s8[3145728]{0:T(1024)(128)(4,1)S(1)}, s32[]{:S(2)}) %slice-start.3) | async-done | bytes 3145752
  81.5 2.5 %fusion.16 = f32[192,1024]{1,0:T(8,128)S(1)} fusion(bf16[192,3584]{1,0:T(8,128)(2,1)S(1)} %get-tuple-element.22, bf16[1024,3584]{1,0:T(8,128)(2,1)S(1)} %bitcast.37), kind=kOutput, calls=%fused_computation.80 | convolution fusion | flops 1409286144 | bytes 9502720 | tf_op jit(solution)/shard_map/dot_general | solution.py:14
  84.1 2.5 %fusion.5 = bf16[192,1024]{1,0:T(8,128)(2,1)S(1)} fusion(f32[192,1024]{1,0:T(8,128)S(1)} %fusion.16, bf16[192,3584]{1,0:T(8,128)(2,1)S(1)} %get-tuple-element.17, bf16[1024,3584]{1,0:T(8,128)(2,1)S(1)} %bitcast.41), kind=kOutput, calls=%fused_computation.19 | convolution fusion | flops 1409679360 | bytes 9895936 | tf_op jit(solution)/shard_map/dot_general | solution.py:14
  86.6 5.2 %convolution_convert_fusion.2 = bf16[1024,3584]{1,0:T(8,128)(2,1)} fusion(bf16[192,1024]{1,0:T(8,128)(2,1)S(1)} %pad_maximum_fusion.3, bf16[192,3584]{1,0:T(8,128)(2,1)S(1)} %get-tuple-element.17), kind=kOutput, calls=%fused_computation.2 | convolution fusion | flops 1412956160 | bytes 9109504 | tf_op jit(solution)/shard_map/dot_general | solution.py:129
  91.8 1.9 %collective-permute-start.26 = (bf16[48,1024]{1,0:T(8,128)(2,1)S(1)}, bf16[48,1024]{1,0:T(8,128)(2,1)S(1)}, u32[]{:S(2)}, u32[]{:S(2)}) collective-permute-start(bf16[48,1024]{1,0:T(8,128)(2,1)S(1)} %get-tuple-element.39), channel_id=1, source_target_pairs={{0,3},{1,0},{2,1},{3,2},{4,7},{5,4},{6,5},{7,6},{8,11},{9,8},{10,9... | collective-permute-start | bytes 294920 | tf_op jit(solution)/shard_map/ppermute | solution.py:106
  93.8 0.1 collective-permute-start.28
  93.9 0.7 collective-permute-start.27
  94.6 5.2 %convolution_convert_fusion.1 = bf16[1024,3584]{1,0:T(8,128)(2,1)} fusion(bf16[192,1024]{1,0:T(8,128)(2,1)S(1)} %pad_maximum_fusion.3, bf16[192,3584]{1,0:T(8,128)(2,1)S(1)} %get-tuple-element.22), kind=kOutput, calls=%fused_computation.1 | convolution fusion | flops 1412956160 | bytes 9109504 | tf_op jit(solution)/shard_map/dot_general | solution.py:132
  99.8 5.2 %convolution_convert_fusion = bf16[3584,1024]{1,0:T(8,128)(2,1)} fusion(bf16[192,3584]{1,0:T(8,128)(2,1)S(1)} %get-tuple-element.23, bf16[192,1024]{1,0:T(8,128)(2,1)S(1)} %copy-done.1), kind=kOutput, calls=%fused_computation | convolution fusion | flops 1412956160 | bytes 9109504 | tf_op jit(solution)/shard_map/dot_general | solution.py:8
  105.0 0.7 add_convert_fusion.12
  (79 shorter events, 1.7 us)
Async XLA Ops:
  0.6 12.2 %collective-permute-start.1 = (bf16[48,1024]{1,0:T(8,128)(2,1)}, bf16[48,1024]{1,0:T(8,128)(2,1)S(1)}, u32[]{:S(2)}, u32[]{:S(2)}) collective-permute-start(bf16[48,1024]{1,0:T(8,128)(2,1)} %param.5), channel_id=1, source_target_pairs={{0,2},{1,3},{2,0},{3,1},{4,6},{5,7},{6,4},{7,5},{8,10},{9,11},{10,... | collective-permute-start | bytes 294920 | tf_op jit(solution)/shard_map/ppermute | solution.py:98
  4.8 8.1 %collective-permute-start = (bf16[48,1024]{1,0:T(8,128)(2,1)}, bf16[48,1024]{1,0:T(8,128)(2,1)S(1)}, u32[]{:S(2)}, u32[]{:S(2)}) collective-permute-start(bf16[48,1024]{1,0:T(8,128)(2,1)} %param.5), channel_id=1, source_target_pairs={{0,1},{1,2},{2,3},{3,0},{4,5},{5,6},{6,7},{7,4},{8,9},{9,10},{10,1... | collective-permute-start | bytes 294920 | tf_op jit(solution)/shard_map/ppermute | solution.py:98
  6.3 7.2 %collective-permute-start.2 = (bf16[48,1024]{1,0:T(8,128)(2,1)}, bf16[48,1024]{1,0:T(8,128)(2,1)S(1)}, u32[]{:S(2)}, u32[]{:S(2)}) collective-permute-start(bf16[48,1024]{1,0:T(8,128)(2,1)} %param.5), channel_id=1, source_target_pairs={{0,3},{1,0},{2,1},{3,2},{4,7},{5,4},{6,5},{7,6},{8,11},{9,8},{10,9... | collective-permute-start | bytes 294920 | tf_op jit(solution)/shard_map/ppermute | solution.py:98
  13.6 11.8 %slice-start.4 = ((s8[7340032]{0:T(1024)(128)(4,1)}), s8[4194304]{0:T(1024)(128)(4,1)S(1)}, s32[]{:S(2)}) async-start(s8[7340032]{0:T(1024)(128)(4,1)} %bitcast.38), calls=%async_computation.4 | async-start | bytes 8388608
  14.6 10.7 %slice-start.5 = ((s8[7340032]{0:T(1024)(128)(4,1)}), s8[3145728]{0:T(1024)(128)(4,1)S(1)}, s32[]{:S(2)}) async-start(s8[7340032]{0:T(1024)(128)(4,1)} %bitcast.38), calls=%async_computation.5 | async-start | bytes 6291456
  14.7 13.9 %collective-permute-start.9 = (bf16[48,1024]{1,0:T(8,128)(2,1)}, bf16[48,1024]{1,0:T(8,128)(2,1)S(1)}, u32[]{:S(2)}, u32[]{:S(2)}) collective-permute-start(bf16[48,1024]{1,0:T(8,128)(2,1)} %param.6), channel_id=1, source_target_pairs={{0,3},{1,0},{2,1},{3,2},{4,7},{5,4},{6,5},{7,6},{8,11},{9,8},{10,9... | collective-permute-start | bytes 294920 | tf_op jit(solution)/shard_map/ppermute | solution.py:98
  16.8 11.3 %collective-permute-start.8 = (bf16[48,1024]{1,0:T(8,128)(2,1)}, bf16[48,1024]{1,0:T(8,128)(2,1)S(1)}, u32[]{:S(2)}, u32[]{:S(2)}) collective-permute-start(bf16[48,1024]{1,0:T(8,128)(2,1)} %param.6), channel_id=1, source_target_pairs={{0,2},{1,3},{2,0},{3,1},{4,6},{5,7},{6,4},{7,5},{8,10},{9,11},{10,... | collective-permute-start | bytes 294920 | tf_op jit(solution)/shard_map/ppermute | solution.py:98
  17.9 10.0 %collective-permute-start.7 = (bf16[48,1024]{1,0:T(8,128)(2,1)}, bf16[48,1024]{1,0:T(8,128)(2,1)S(1)}, u32[]{:S(2)}, u32[]{:S(2)}) collective-permute-start(bf16[48,1024]{1,0:T(8,128)(2,1)} %param.6), channel_id=1, source_target_pairs={{0,1},{1,2},{2,3},{3,0},{4,5},{5,6},{6,7},{7,4},{8,9},{9,10},{10,1... | collective-permute-start | bytes 294920 | tf_op jit(solution)/shard_map/ppermute | solution.py:98
  24.7 3.9 %slice-start = ((s8[7340032]{0:T(1024)(128)(4,1)}), s8[4194304]{0:T(1024)(128)(4,1)S(1)}, s32[]{:S(2)}) async-start(s8[7340032]{0:T(1024)(128)(4,1)} %bitcast.34), calls=%async_computation | async-start | bytes 8388608
  24.8 3.9 %slice-start.1 = ((s8[7340032]{0:T(1024)(128)(4,1)}), s8[3145728]{0:T(1024)(128)(4,1)S(1)}, s32[]{:S(2)}) async-start(s8[7340032]{0:T(1024)(128)(4,1)} %bitcast.34), calls=%async_computation.1 | async-start | bytes 6291456
  24.8 6.7 %collective-permute-start.5 = (bf16[96,1792]{1,0:T(8,128)(2,1)S(1)}, bf16[96,1792]{1,0:T(8,128)(2,1)S(1)}, u32[]{:S(2)}, u32[]{:S(2)}) collective-permute-start(bf16[96,1792]{1,0:T(8,128)(2,1)S(1)} %constant_dynamic-slice_fusion.11), channel_id=1, source_target_pairs={{0,4},{4,0},{8,12},{12,8},{16,20},{20,16},{24,28},{28,24},{1,5},{5... | collective-permute-start | bytes 1032200 | tf_op jit(solution)/shard_map/ppermute | solution.py:39
  24.9 7.3 %collective-permute-start.18 = (bf16[96,1792]{1,0:T(8,128)(2,1)S(1)}, bf16[96,1792]{1,0:T(8,128)(2,1)S(1)}, u32[]{:S(2)}, u32[]{:S(2)}) collective-permute-start(bf16[96,1792]{1,0:T(8,128)(2,1)S(1)} %constant_dynamic-slice_fusion.4), channel_id=1, source_target_pairs={{0,4},{4,0},{8,12},{12,8},{16,20},{20,16},{24,28},{28,24},{1,5},{5... | collective-permute-start | bytes 1032200 | tf_op jit(solution)/shard_map/ppermute | solution.py:39
  27.0 0.9 copy-start.2
  27.9 5.9 %collective-permute-start.3 = (bf16[96,1792]{1,0:T(8,128)(2,1)S(1)}, bf16[96,1792]{1,0:T(8,128)(2,1)S(1)}, u32[]{:S(2)}, u32[]{:S(2)}) collective-permute-start(bf16[96,1792]{1,0:T(8,128)(2,1)S(1)} %constant_dynamic-slice_fusion.13), channel_id=1, source_target_pairs={{0,4},{4,0},{8,12},{12,8},{16,20},{20,16},{24,28},{28,24},{1,5},{5... | collective-permute-start | bytes 1032200 | tf_op jit(solution)/shard_map/ppermute | solution.py:39
  28.1 7.5 %collective-permute-start.16 = (bf16[96,1792]{1,0:T(8,128)(2,1)S(1)}, bf16[96,1792]{1,0:T(8,128)(2,1)S(1)}, u32[]{:S(2)}, u32[]{:S(2)}) collective-permute-start(bf16[96,1792]{1,0:T(8,128)(2,1)S(1)} %constant_dynamic-slice_fusion.6), channel_id=1, source_target_pairs={{0,4},{4,0},{8,12},{12,8},{16,20},{20,16},{24,28},{28,24},{1,5},{5... | collective-permute-start | bytes 1032200 | tf_op jit(solution)/shard_map/ppermute | solution.py:39
  28.6 2.6 %copy-start = (bf16[192,1024]{1,0:T(8,128)(2,1)}, bf16[192,1024]{1,0:T(8,128)(2,1)S(1)}, u32[]{:S(2)}) copy-start(bf16[192,1024]{1,0:T(8,128)(2,1)S(1)} %constant_dynamic-update-slice_fusion) | copy-start | bytes 1179652
  31.4 4.9 %collective-permute-start.10 = (bf16[96,1792]{1,0:T(8,128)(2,1)S(1)}, bf16[96,1792]{1,0:T(8,128)(2,1)S(1)}, u32[]{:S(2)}, u32[]{:S(2)}) collective-permute-start(bf16[96,1792]{1,0:T(8,128)(2,1)S(1)} %constant_dynamic-slice_fusion.9), channel_id=1, source_target_pairs={{0,4},{4,0},{8,12},{12,8},{16,20},{20,16},{24,28},{28,24},{1,5},{5... | collective-permute-start | bytes 1032200 | tf_op jit(solution)/shard_map/ppermute | solution.py:39
  31.5 5.5 %collective-permute-start.20 = (bf16[96,1792]{1,0:T(8,128)(2,1)S(1)}, bf16[96,1792]{1,0:T(8,128)(2,1)S(1)}, u32[]{:S(2)}, u32[]{:S(2)}) collective-permute-start(bf16[96,1792]{1,0:T(8,128)(2,1)S(1)} %constant_dynamic-slice_fusion.2), channel_id=1, source_target_pairs={{0,4},{4,0},{8,12},{12,8},{16,20},{20,16},{24,28},{28,24},{1,5},{5... | collective-permute-start | bytes 1032200 | tf_op jit(solution)/shard_map/ppermute | solution.py:39
  32.2 7.3 %collective-permute-start.6 = (bf16[48,1792]{1,0:T(8,128)(2,1)S(1)}, bf16[48,1792]{1,0:T(8,128)(2,1)S(1)}, u32[]{:S(2)}, u32[]{:S(2)}) collective-permute-start(bf16[48,1792]{1,0:T(8,128)(2,1)S(1)} %constant_dynamic-slice_fusion.10), channel_id=1, source_target_pairs={{0,8},{4,12},{8,0},{12,4},{16,24},{20,28},{24,16},{28,20},{1,9},{5... | collective-permute-start | bytes 516104 | tf_op jit(solution)/shard_map/ppermute | solution.py:39
  33.8 9.3 %collective-permute-start.19 = (bf16[48,1792]{1,0:T(8,128)(2,1)S(1)}, bf16[48,1792]{1,0:T(8,128)(2,1)S(1)}, u32[]{:S(2)}, u32[]{:S(2)}) collective-permute-start(bf16[48,1792]{1,0:T(8,128)(2,1)S(1)} %constant_dynamic-slice_fusion.3), channel_id=1, source_target_pairs={{0,16},{4,20},{8,24},{12,28},{16,0},{20,4},{24,8},{28,12},{1,17},{... | collective-permute-start | bytes 516104 | tf_op jit(solution)/shard_map/ppermute | solution.py:39
  35.6 7.5 %collective-permute-start.4 = (bf16[48,1792]{1,0:T(8,128)(2,1)S(1)}, bf16[48,1792]{1,0:T(8,128)(2,1)S(1)}, u32[]{:S(2)}, u32[]{:S(2)}) collective-permute-start(bf16[48,1792]{1,0:T(8,128)(2,1)S(1)} %constant_dynamic-slice_fusion.12), channel_id=1, source_target_pairs={{0,8},{4,12},{8,0},{12,4},{16,24},{20,28},{24,16},{28,20},{1,9},{5... | collective-permute-start | bytes 516104 | tf_op jit(solution)/shard_map/ppermute | solution.py:39
  36.3 8.6 %collective-permute-start.17 = (bf16[48,1792]{1,0:T(8,128)(2,1)S(1)}, bf16[48,1792]{1,0:T(8,128)(2,1)S(1)}, u32[]{:S(2)}, u32[]{:S(2)}) collective-permute-start(bf16[48,1792]{1,0:T(8,128)(2,1)S(1)} %constant_dynamic-slice_fusion.5), channel_id=1, source_target_pairs={{0,16},{4,20},{8,24},{12,28},{16,0},{20,4},{24,8},{28,12},{1,17},{... | collective-permute-start | bytes 516104 | tf_op jit(solution)/shard_map/ppermute | solution.py:39
  37.0 9.0 %collective-permute-start.11 = (bf16[48,1792]{1,0:T(8,128)(2,1)S(1)}, bf16[48,1792]{1,0:T(8,128)(2,1)S(1)}, u32[]{:S(2)}, u32[]{:S(2)}) collective-permute-start(bf16[48,1792]{1,0:T(8,128)(2,1)S(1)} %constant_dynamic-slice_fusion.8), channel_id=1, source_target_pairs={{0,8},{4,12},{8,0},{12,4},{16,24},{20,28},{24,16},{28,20},{1,9},{5... | collective-permute-start | bytes 516104 | tf_op jit(solution)/shard_map/ppermute | solution.py:39
  39.4 8.3 %collective-permute-start.21 = (bf16[48,1792]{1,0:T(8,128)(2,1)S(1)}, bf16[48,1792]{1,0:T(8,128)(2,1)S(1)}, u32[]{:S(2)}, u32[]{:S(2)}) collective-permute-start(bf16[48,1792]{1,0:T(8,128)(2,1)S(1)} %constant_dynamic-slice_fusion.1), channel_id=1, source_target_pairs={{0,16},{4,20},{8,24},{12,28},{16,0},{20,4},{24,8},{28,12},{1,17},{... | collective-permute-start | bytes 516104 | tf_op jit(solution)/shard_map/ppermute | solution.py:39
  46.1 7.5 %collective-permute-start.12 = (bf16[3,24,1792]{2,1,0:T(8,128)(2,1)S(1)}, bf16[3,24,1792]{2,1,0:T(8,128)(2,1)S(1)}, u32[]{:S(2)}, u32[]{:S(2)}) collective-permute-start(bf16[3,24,1792]{2,1,0:T(8,128)(2,1)S(1)} %constant_dynamic-slice_fusion.7), channel_id=1, source_target_pairs={{0,16},{4,20},{8,24},{12,28},{16,0},{20,4},{24,8},{28,12},{1,17},{... | collective-permute-start | bytes 774152 | tf_op jit(solution)/shard_map/ppermute | solution.py:51
  47.9 7.5 %collective-permute-start.22 = (bf16[3,24,1792]{2,1,0:T(8,128)(2,1)S(1)}, bf16[3,24,1792]{2,1,0:T(8,128)(2,1)S(1)}, u32[]{:S(2)}, u32[]{:S(2)}) collective-permute-start(bf16[3,24,1792]{2,1,0:T(8,128)(2,1)S(1)} %constant_dynamic-slice_fusion), channel_id=1, source_target_pairs={{0,8},{4,12},{8,0},{12,4},{16,24},{20,28},{24,16},{28,20},{1,9},{5... | collective-permute-start | bytes 774152 | tf_op jit(solution)/shard_map/ppermute | solution.py:51
  53.8 6.6 %collective-permute-start.13 = (bf16[3,24,1792]{2,1,0:T(8,128)(2,1)S(1)}, bf16[3,24,1792]{2,1,0:T(8,128)(2,1)S(1)}, u32[]{:S(2)}, u32[]{:S(2)}) collective-permute-start(bf16[3,24,1792]{2,1,0:T(8,128)(2,1)S(1)} %pad_maximum_fusion.4), channel_id=1, source_target_pairs={{0,16},{4,20},{8,24},{12,28},{16,0},{20,4},{24,8},{28,12},{1,17},{... | collective-permute-start | bytes 774152 | tf_op jit(solution)/shard_map/ppermute | solution.py:67
  55.6 7.7 %collective-permute-start.23 = (bf16[3,24,1792]{2,1,0:T(8,128)(2,1)S(1)}, bf16[3,24,1792]{2,1,0:T(8,128)(2,1)S(1)}, u32[]{:S(2)}, u32[]{:S(2)}) collective-permute-start(bf16[3,24,1792]{2,1,0:T(8,128)(2,1)S(1)} %pad_maximum_fusion.5), channel_id=1, source_target_pairs={{0,8},{4,12},{8,0},{12,4},{16,24},{20,28},{24,16},{28,20},{1,9},{5... | collective-permute-start | bytes 774152 | tf_op jit(solution)/shard_map/ppermute | solution.py:67
  60.5 12.6 %collective-permute-start.14 = (bf16[3,48,1792]{2,1,0:T(8,128)(2,1)S(1)}, bf16[3,48,1792]{2,1,0:T(8,128)(2,1)S(1)}, u32[]{:S(2)}, u32[]{:S(2)}) collective-permute-start(bf16[3,48,1792]{2,1,0:T(8,128)(2,1)S(1)} %maximum_select_fusion.4), channel_id=1, source_target_pairs={{0,8},{4,12},{8,0},{12,4},{16,24},{20,28},{24,16},{28,20},{1,9},{5... | collective-permute-start | bytes 1548296 | tf_op jit(solution)/shard_map/ppermute | solution.py:67
  63.4 10.0 %collective-permute-start.24 = (bf16[3,48,1792]{2,1,0:T(8,128)(2,1)S(1)}, bf16[3,48,1792]{2,1,0:T(8,128)(2,1)S(1)}, u32[]{:S(2)}, u32[]{:S(2)}) collective-permute-start(bf16[3,48,1792]{2,1,0:T(8,128)(2,1)S(1)} %maximum_select_fusion.5), channel_id=1, source_target_pairs={{0,16},{4,20},{8,24},{12,28},{16,0},{20,4},{24,8},{28,12},{1,17},{... | collective-permute-start | bytes 1548296 | tf_op jit(solution)/shard_map/ppermute | solution.py:67
  73.3 2.7 %collective-permute-start.15 = (bf16[3,96,1792]{2,1,0:T(8,128)(2,1)S(1)}, bf16[3,96,1792]{2,1,0:T(8,128)(2,1)S(1)}, u32[]{:S(2)}, u32[]{:S(2)}) collective-permute-start(bf16[3,96,1792]{2,1,0:T(8,128)(2,1)S(1)} %maximum_select_fusion.2), channel_id=1, source_target_pairs={{0,4},{4,0},{8,12},{12,8},{16,20},{20,16},{24,28},{28,24},{1,5},{5... | collective-permute-start | bytes 3096584 | tf_op jit(solution)/shard_map/ppermute | solution.py:67
  73.7 4.0 %collective-permute-start.25 = (bf16[3,96,1792]{2,1,0:T(8,128)(2,1)S(1)}, bf16[3,96,1792]{2,1,0:T(8,128)(2,1)}, u32[]{:S(2)}, u32[]{:S(2)}) collective-permute-start(bf16[3,96,1792]{2,1,0:T(8,128)(2,1)S(1)} %maximum_select_fusion.3), channel_id=1, source_target_pairs={{0,4},{4,0},{8,12},{12,8},{16,20},{20,16},{24,28},{28,24},{1,5},{5... | collective-permute-start | bytes 3096584 | tf_op jit(solution)/shard_map/ppermute | solution.py:67
  76.0 4.2 %slice-start.2 = ((s8[7340032]{0:T(1024)(128)(4,1)}), s8[4194304]{0:T(1024)(128)(4,1)S(1)}, s32[]{:S(2)}) async-start(s8[7340032]{0:T(1024)(128)(4,1)} %bitcast.36), calls=%async_computation.2 | async-start | bytes 8388608
  79.7 1.9 %slice-start.3 = ((s8[7340032]{0:T(1024)(128)(4,1)}), s8[3145728]{0:T(1024)(128)(4,1)S(1)}, s32[]{:S(2)}) async-start(s8[7340032]{0:T(1024)(128)(4,1)} %bitcast.36), calls=%async_computation.3 | async-start | bytes 6291456
  79.7 4.4 %slice-start.6 = ((s8[7340032]{0:T(1024)(128)(4,1)}), s8[4194304]{0:T(1024)(128)(4,1)S(1)}, s32[]{:S(2)}) async-start(s8[7340032]{0:T(1024)(128)(4,1)} %bitcast.40), calls=%async_computation.6 | async-start | bytes 8388608
  81.5 2.5 %slice-start.7 = ((s8[7340032]{0:T(1024)(128)(4,1)}), s8[3145728]{0:T(1024)(128)(4,1)S(1)}, s32[]{:S(2)}) async-start(s8[7340032]{0:T(1024)(128)(4,1)} %bitcast.40), calls=%async_computation.7 | async-start | bytes 6291456
  91.8 13.1 %collective-permute-start.26 = (bf16[48,1024]{1,0:T(8,128)(2,1)S(1)}, bf16[48,1024]{1,0:T(8,128)(2,1)S(1)}, u32[]{:S(2)}, u32[]{:S(2)}) collective-permute-start(bf16[48,1024]{1,0:T(8,128)(2,1)S(1)} %get-tuple-element.39), channel_id=1, source_target_pairs={{0,3},{1,0},{2,1},{3,2},{4,7},{5,4},{6,5},{7,6},{8,11},{9,8},{10,9... | collective-permute-start | bytes 294920 | tf_op jit(solution)/shard_map/ppermute | solution.py:106
  93.8 11.2 %collective-permute-start.28 = (bf16[48,1024]{1,0:T(8,128)(2,1)S(1)}, bf16[48,1024]{1,0:T(8,128)(2,1)S(1)}, u32[]{:S(2)}, u32[]{:S(2)}) collective-permute-start(bf16[48,1024]{1,0:T(8,128)(2,1)S(1)} %get-tuple-element.40), channel_id=1, source_target_pairs={{0,1},{1,2},{2,3},{3,0},{4,5},{5,6},{6,7},{7,4},{8,9},{9,10},{10,1... | collective-permute-start | bytes 294920 | tf_op jit(solution)/shard_map/ppermute | solution.py:106
  93.9 5.8 %copy-start.1 = (bf16[192,1024]{1,0:T(8,128)(2,1)S(1)}, bf16[192,1024]{1,0:T(8,128)(2,1)}, u32[]{:S(2)}) copy-start(bf16[192,1024]{1,0:T(8,128)(2,1)} %copy-done) | copy-start | bytes 1179652
  93.9 11.0 %collective-permute-start.27 = (bf16[48,1024]{1,0:T(8,128)(2,1)S(1)}, bf16[48,1024]{1,0:T(8,128)(2,1)S(1)}, u32[]{:S(2)}, u32[]{:S(2)}) collective-permute-start(bf16[48,1024]{1,0:T(8,128)(2,1)S(1)} %get-tuple-element.41), channel_id=1, source_target_pairs={{0,2},{1,3},{2,0},{3,1},{4,6},{5,7},{6,4},{7,5},{8,10},{9,11},{10,... | collective-permute-start | bytes 294920 | tf_op jit(solution)/shard_map/ppermute | solution.py:106

commit v16 on v15

--- a/solution.py
+++ b/solution.py
@@ -56,7 +56,7 @@
     return cur
 
 
-PER_ARRAY_STEPS = 2
+PER_ARRAY_STEPS = 3
 
 
 def doubling_gather(x, order, n_dev):

time: 106 us -> 106 us (level)
  waiting for transfers between devices: 31.5 us -> 27 us
  starting transfers between devices: 33.7 us -> 38.1 us
    ppermute x12 -> x18, starting transfers between devices: 9.24 us -> 17.3 us  [halving_reduce(): lax.ppermute(lax.dynamic_slice_in_dim(c, (1 - hi) * n, n, 0), 'row', perm)]
    ppermute x2 -> x0, waiting for transfers between devices: 4.15 us -> none  [halving_reduce(): got = lax.ppermute(send, 'row', perm)]
    ppermute x2 -> x0, starting transfers between devices: 3.15 us -> none  [halving_reduce(): got = lax.ppermute(send, 'row', perm)]
    ppermute x12 -> x18, waiting for transfers between devices: 5.57 us -> 4.35 us  [halving_reduce(): lax.ppermute(lax.dynamic_slice_in_dim(c, (1 - hi) * n, n, 0), 'row', perm)]
  transfers between devices with their start and end apart: 29 -> 33, of which waited for: 12 -> 17; matrix products, arithmetic and copies ran while one was open for 21% -> 21% of each run, Pallas kernels for 0% -> 0%
where the time goes in v16:
time: 106 us; the launch traced here: 105 us
  starting transfers between devices  38.1 us (36%)
  matrix products  29.4 us (28%)
  waiting for transfers between devices  27 us (25%)
  other arithmetic  6.98 us (7%)
  local copies, waits for them, and re-layouts  2.8 us (3%)
  between operations  1.16 us (1%)
    ppermute x6, waiting for transfers between devices, doubling_gather(): got = lax.ppermute(cur, 'row', [(j, j ^ bit) for j in range(n_dev)])  17.7 us
    ppermute x18, starting transfers between devices, halving_reduce(): lax.ppermute(lax.dynamic_slice_in_dim(c, (1 - hi) * n, n, 0), 'row', perm)  17.3 us
    ppermute x6, starting transfers between devices, col_gather(): lax.ppermute(x, 'col', [(j, (j + s) % n_col) for j in range(n_col)])  13.2 us
    dot_general x3, matrix products, contract_last(): lax.dot_general(left, right, (((1,), (1,)), ((), ())), preferred_element_...  7.59 us
    dot_general x1, matrix products, contract_first(): lax.dot_general(left, right, (((0,), (0,)), ((), ())), preferred_element_...  5.19 us
    dot_general x1, matrix products, body(): jnp.dot(tok_t, grad_gate, preferred_element_type=jnp.float32)  5.18 us
    dot_general x1, matrix products, body(): acc_up = jnp.dot(tok_t, grad_up, preferred_element_type=jnp.float32)  5.18 us
    ppermute x6, waiting for transfers between devices, col_gather(): lax.ppermute(x, 'col', [(j, (j + s) % n_col) for j in range(n_col)])  4.99 us
  transfers between devices with their start and end apart: 33, of which 17 were waited for; matrix products, arithmetic and copies ran while one was open for 21% of the time, Pallas kernels for 0%

profile of v16, /device:TPU:0, one launch (start us, length us, event | category | flops | bytes accessed | tf_op | source)
XLA Modules:
  0.0 105.5 jit_solution(302827348279743957)
XLA Ops:
  0.6 4.1 %collective-permute-start.1 = (bf16[48,1024]{1,0:T(8,128)(2,1)}, bf16[48,1024]{1,0:T(8,128)(2,1)S(1)}, u32[]{:S(2)}, u32[]{:S(2)}) collective-permute-start(bf16[48,1024]{1,0:T(8,128)(2,1)} %param.5), channel_id=1, source_target_pairs={{0,2},{1,3},{2,0},{3,1},{4,6},{5,7},{6,4},{7,5},{8,10},{9,11},{10,... | collective-permute-start | bytes 294920 | tf_op jit(solution)/shard_map/ppermute | solution.py:98
  4.8 1.6 %collective-permute-start = (bf16[48,1024]{1,0:T(8,128)(2,1)}, bf16[48,1024]{1,0:T(8,128)(2,1)S(1)}, u32[]{:S(2)}, u32[]{:S(2)}) collective-permute-start(bf16[48,1024]{1,0:T(8,128)(2,1)} %param.5), channel_id=1, source_target_pairs={{0,1},{1,2},{2,3},{3,0},{4,5},{5,6},{6,7},{7,4},{8,9},{9,10},{10,1... | collective-permute-start | bytes 294920 | tf_op jit(solution)/shard_map/ppermute | solution.py:98
  6.3 2.2 %collective-permute-start.2 = (bf16[48,1024]{1,0:T(8,128)(2,1)}, bf16[48,1024]{1,0:T(8,128)(2,1)S(1)}, u32[]{:S(2)}, u32[]{:S(2)}) collective-permute-start(bf16[48,1024]{1,0:T(8,128)(2,1)} %param.5), channel_id=1, source_target_pairs={{0,3},{1,0},{2,1},{3,2},{4,7},{5,4},{6,5},{7,6},{8,11},{9,8},{10,9... | collective-permute-start | bytes 294920 | tf_op jit(solution)/shard_map/ppermute | solution.py:98
  8.6 4.3 %collective-permute-done.1 = bf16[48,1024]{1,0:T(8,128)(2,1)S(1)} collective-permute-done((bf16[48,1024]{1,0:T(8,128)(2,1)}, bf16[48,1024]{1,0:T(8,128)(2,1)S(1)}, u32[]{:S(2)}, u32[]{:S(2)}) %collective-permute-start.1) | collective-permute-done | bytes 98336 | tf_op jit(solution)/shard_map/ppermute | solution.py:98
  12.9 0.7 collective-permute-done.2
  13.6 1.1 %pad_maximum_fusion.1 = bf16[192,1024]{1,0:T(8,128)(2,1)S(1)} fusion(bf16[48,1024]{1,0:T(8,128)(2,1)S(1)} %collective-permute-done.2, bf16[48,1024]{1,0:T(8,128)(2,1)S(1)} %collective-permute-done.1, bf16[48,1024]{1,0:T(8,128)(2,1)S(1)} %collective-permute-done, bf16[48,1024]{1,0:T(8,128)(2,1)} %param.5), kind=kLoop, calls=%fused_computation.30 | loop fusion | flops 1572864 | bytes 786432 | tf_op jit(solution)/shard_map/concatenate | solution.py:99
  14.7 2.1 %collective-permute-start.11 = (bf16[48,1024]{1,0:T(8,128)(2,1)}, bf16[48,1024]{1,0:T(8,128)(2,1)S(1)}, u32[]{:S(2)}, u32[]{:S(2)}) collective-permute-start(bf16[48,1024]{1,0:T(8,128)(2,1)} %param.6), channel_id=1, source_target_pairs={{0,3},{1,0},{2,1},{3,2},{4,7},{5,4},{6,5},{7,6},{8,11},{9,8},{10,9... | collective-permute-start | bytes 294920 | tf_op jit(solution)/shard_map/ppermute | solution.py:98
  16.8 1.2 %collective-permute-start.10 = (bf16[48,1024]{1,0:T(8,128)(2,1)}, bf16[48,1024]{1,0:T(8,128)(2,1)S(1)}, u32[]{:S(2)}, u32[]{:S(2)}) collective-permute-start(bf16[48,1024]{1,0:T(8,128)(2,1)} %param.6), channel_id=1, source_target_pairs={{0,2},{1,3},{2,0},{3,1},{4,6},{5,7},{6,4},{7,5},{8,10},{9,11},{10,... | collective-permute-start | bytes 294920 | tf_op jit(solution)/shard_map/ppermute | solution.py:98
  17.9 1.9 %collective-permute-start.9 = (bf16[48,1024]{1,0:T(8,128)(2,1)}, bf16[48,1024]{1,0:T(8,128)(2,1)S(1)}, u32[]{:S(2)}, u32[]{:S(2)}) collective-permute-start(bf16[48,1024]{1,0:T(8,128)(2,1)} %param.6), channel_id=1, source_target_pairs={{0,1},{1,2},{2,3},{3,0},{4,5},{5,6},{6,7},{7,4},{8,9},{9,10},{10,1... | collective-permute-start | bytes 294920 | tf_op jit(solution)/shard_map/ppermute | solution.py:98
  19.9 4.7 %convolution_convert_fusion.4 = bf16[192,3584]{1,0:T(8,128)(2,1)S(1)} fusion(bf16[192,1024]{1,0:T(8,128)(2,1)S(1)} %pad_maximum_fusion.1, bf16[1024,3584]{1,0:T(8,128)(2,1)} %param.8), kind=kOutput, calls=%fused_computation.4 | convolution fusion | flops 1409974272 | bytes 9109504 | tf_op jit(solution)/shard_map/dot_general | solution.py:120
  24.9 0.5 collective-permute-start.21
  25.4 1.6 %convolution_convert_fusion.5 = bf16[192,3584]{1,0:T(8,128)(2,1)S(1)} fusion(bf16[192,1024]{1,0:T(8,128)(2,1)S(1)} %pad_maximum_fusion.1, bf16[1024,3584]{1,0:T(8,128)(2,1)S(1)} %bitcast.39), kind=kOutput, calls=%fused_computation.5 | convolution fusion | flops 1409974272 | bytes 9109504 | tf_op jit(solution)/shard_map/dot_general | solution.py:119
  27.2 0.7 copy-done.2
  27.9 0.1 collective-permute-start.3
  28.1 0.5 collective-permute-start.18
  28.6 2.6 %convolution_convert_fusion.3 = bf16[192,3584]{1,0:T(8,128)(2,1)S(1)} fusion(bf16[192,1024]{1,0:T(8,128)(2,1)S(1)} %constant_dynamic-update-slice_fusion, bf16[3584,1024]{1,0:T(8,128)(2,1)S(1)} %bitcast.35), kind=kOutput, calls=%fused_computation.3 | convolution fusion | flops 1409974272 | bytes 9109504 | tf_op jit(solution)/shard_map/dot_general | solution.py:14
  31.4 0.1 collective-permute-start.12
  31.5 0.5 collective-permute-start.24
  32.2 1.5 %collective-permute-start.7 = (bf16[48,1792]{1,0:T(8,128)(2,1)S(1)}, bf16[48,1792]{1,0:T(8,128)(2,1)S(1)}, u32[]{:S(2)}, u32[]{:S(2)}) collective-permute-start(bf16[48,1792]{1,0:T(8,128)(2,1)S(1)} %constant_dynamic-slice_fusion.13), channel_id=1, source_target_pairs={{0,8},{4,12},{8,0},{12,4},{16,24},{20,28},{24,16},{28,20},{1,9},{5... | collective-permute-start | bytes 516104 | tf_op jit(solution)/shard_map/ppermute | solution.py:39
  33.8 1.6 %collective-permute-start.22 = (bf16[48,1792]{1,0:T(8,128)(2,1)S(1)}, bf16[48,1792]{1,0:T(8,128)(2,1)S(1)}, u32[]{:S(2)}, u32[]{:S(2)}) collective-permute-start(bf16[48,1792]{1,0:T(8,128)(2,1)S(1)} %constant_dynamic-slice_fusion.4), channel_id=1, source_target_pairs={{0,16},{4,20},{8,24},{12,28},{16,0},{20,4},{24,8},{28,12},{1,17},{... | collective-permute-start | bytes 516104 | tf_op jit(solution)/shard_map/ppermute | solution.py:39
  35.6 0.6 collective-permute-start.4
  36.3 0.6 collective-permute-start.19
  37.0 1.5 %collective-permute-start.13 = (bf16[48,1792]{1,0:T(8,128)(2,1)S(1)}, bf16[48,1792]{1,0:T(8,128)(2,1)S(1)}, u32[]{:S(2)}, u32[]{:S(2)}) collective-permute-start(bf16[48,1792]{1,0:T(8,128)(2,1)S(1)} %constant_dynamic-slice_fusion.10), channel_id=1, source_target_pairs={{0,8},{4,12},{8,0},{12,4},{16,24},{20,28},{24,16},{28,20},{1,9},{5... | collective-permute-start | bytes 516104 | tf_op jit(solution)/shard_map/ppermute | solution.py:39
  38.6 0.8 collective-permute-done.7
  39.4 1.6 %collective-permute-start.25 = (bf16[48,1792]{1,0:T(8,128)(2,1)S(1)}, bf16[48,1792]{1,0:T(8,128)(2,1)S(1)}, u32[]{:S(2)}, u32[]{:S(2)}) collective-permute-start(bf16[48,1792]{1,0:T(8,128)(2,1)S(1)} %constant_dynamic-slice_fusion.1), channel_id=1, source_target_pairs={{0,16},{4,20},{8,24},{12,28},{16,0},{20,4},{24,8},{28,12},{1,17},{... | collective-permute-start | bytes 516104 | tf_op jit(solution)/shard_map/ppermute | solution.py:39
  41.1 1.6 %collective-permute-start.8 = (bf16[24,1792]{1,0:T(8,128)(2,1)S(1)}, bf16[24,1792]{1,0:T(8,128)(2,1)S(1)}, u32[]{:S(2)}, u32[]{:S(2)}) collective-permute-start(bf16[24,1792]{1,0:T(8,128)(2,1)S(1)} %constant_dynamic-slice_fusion.12), channel_id=1, source_target_pairs={{0,16},{4,20},{8,24},{12,28},{16,0},{20,4},{24,8},{28,12},{1,17},{... | collective-permute-start | bytes 258056 | tf_op jit(solution)/shard_map/ppermute | solution.py:39
  42.8 0.3 collective-permute-done.4
  43.1 1.5 %collective-permute-start.23 = (bf16[24,1792]{1,0:T(8,128)(2,1)S(1)}, bf16[24,1792]{1,0:T(8,128)(2,1)S(1)}, u32[]{:S(2)}, u32[]{:S(2)}) collective-permute-start(bf16[24,1792]{1,0:T(8,128)(2,1)S(1)} %constant_dynamic-slice_fusion.3), channel_id=1, source_target_pairs={{0,8},{4,12},{8,0},{12,4},{16,24},{20,28},{24,16},{28,20},{1,9},{5... | collective-permute-start | bytes 258056 | tf_op jit(solution)/shard_map/ppermute | solution.py:39
  44.7 0.1 collective-permute-done.19
  44.8 1.6 %collective-permute-start.5 = (bf16[24,1792]{1,0:T(8,128)(2,1)S(1)}, bf16[24,1792]{1,0:T(8,128)(2,1)S(1)}, u32[]{:S(2)}, u32[]{:S(2)}) collective-permute-start(bf16[24,1792]{1,0:T(8,128)(2,1)S(1)} %constant_dynamic-slice_fusion.15), channel_id=1, source_target_pairs={{0,16},{4,20},{8,24},{12,28},{16,0},{20,4},{24,8},{28,12},{1,17},{... | collective-permute-start | bytes 258056 | tf_op jit(solution)/shard_map/ppermute | solution.py:39
  46.4 0.3 collective-permute-done.13
  46.8 1.5 %collective-permute-start.20 = (bf16[24,1792]{1,0:T(8,128)(2,1)S(1)}, bf16[24,1792]{1,0:T(8,128)(2,1)S(1)}, u32[]{:S(2)}, u32[]{:S(2)}) collective-permute-start(bf16[24,1792]{1,0:T(8,128)(2,1)S(1)} %constant_dynamic-slice_fusion.6), channel_id=1, source_target_pairs={{0,8},{4,12},{8,0},{12,4},{16,24},{20,28},{24,16},{28,20},{1,9},{5... | collective-permute-start | bytes 258056 | tf_op jit(solution)/shard_map/ppermute | solution.py:39
  48.5 1.6 %collective-permute-start.14 = (bf16[24,1792]{1,0:T(8,128)(2,1)S(1)}, bf16[24,1792]{1,0:T(8,128)(2,1)S(1)}, u32[]{:S(2)}, u32[]{:S(2)}) collective-permute-start(bf16[24,1792]{1,0:T(8,128)(2,1)S(1)} %constant_dynamic-slice_fusion.9), channel_id=1, source_target_pairs={{0,16},{4,20},{8,24},{12,28},{16,0},{20,4},{24,8},{28,12},{1,17},{... | collective-permute-start | bytes 258056 | tf_op jit(solution)/shard_map/ppermute | solution.py:39
  50.1 0.2 collective-permute-done.8
  50.3 0.4 collective-permute-start.26
  50.7 1.3 %collective-permute-done.5 = bf16[24,1792]{1,0:T(8,128)(2,1)S(1)} collective-permute-done((bf16[24,1792]{1,0:T(8,128)(2,1)S(1)}, bf16[24,1792]{1,0:T(8,128)(2,1)S(1)}, u32[]{:S(2)}, u32[]{:S(2)}) %collective-permute-start.5) | collective-permute-done | bytes 86048 | tf_op jit(solution)/shard_map/ppermute | solution.py:39
  52.0 1.0 collective-permute-done.14
  53.0 0.2 fusion.6
  53.2 1.6 %collective-permute-start.15 = (bf16[3,24,1792]{2,1,0:T(8,128)(2,1)S(1)}, bf16[3,24,1792]{2,1,0:T(8,128)(2,1)S(1)}, u32[]{:S(2)}, u32[]{:S(2)}) collective-permute-start(bf16[3,24,1792]{2,1,0:T(8,128)(2,1)S(1)} %pad_maximum_fusion.2), channel_id=1, source_target_pairs={{0,16},{4,20},{8,24},{12,28},{16,0},{20,4},{24,8},{28,12},{1,17},{... | collective-permute-start | bytes 774152 | tf_op jit(solution)/shard_map/ppermute | solution.py:67
  54.8 0.2 fusion.8
  55.0 0.6 collective-permute-start.27
  55.6 4.6 %collective-permute-done.15 = bf16[3,24,1792]{2,1,0:T(8,128)(2,1)S(1)} collective-permute-done((bf16[3,24,1792]{2,1,0:T(8,128)(2,1)S(1)}, bf16[3,24,1792]{2,1,0:T(8,128)(2,1)S(1)}, u32[]{:S(2)}, u32[]{:S(2)}) %collective-permute-start.15) | collective-permute-done | bytes 258080 | tf_op jit(solution)/shard_map/ppermute | solution.py:67
  60.3 0.8 collective-permute-start.16
  61.2 1.3 %collective-permute-done.27 = bf16[3,24,1792]{2,1,0:T(8,128)(2,1)S(1)} collective-permute-done((bf16[3,24,1792]{2,1,0:T(8,128)(2,1)S(1)}, bf16[3,24,1792]{2,1,0:T(8,128)(2,1)S(1)}, u32[]{:S(2)}, u32[]{:S(2)}) %collective-permute-start.27) | collective-permute-done | bytes 258080 | tf_op jit(solution)/shard_map/ppermute | solution.py:67
  62.5 1.2 %collective-permute-start.28 = (bf16[3,48,1792]{2,1,0:T(8,128)(2,1)S(1)}, bf16[3,48,1792]{2,1,0:T(8,128)(2,1)S(1)}, u32[]{:S(2)}, u32[]{:S(2)}) collective-permute-start(bf16[3,48,1792]{2,1,0:T(8,128)(2,1)S(1)} %maximum_select_fusion.5), channel_id=1, source_target_pairs={{0,16},{4,20},{8,24},{12,28},{16,0},{20,4},{24,8},{28,12},{1,17},{... | collective-permute-start | bytes 1548296 | tf_op jit(solution)/shard_map/ppermute | solution.py:67
  63.7 9.1 %collective-permute-done.16 = bf16[3,48,1792]{2,1,0:T(8,128)(2,1)S(1)} collective-permute-done((bf16[3,48,1792]{2,1,0:T(8,128)(2,1)S(1)}, bf16[3,48,1792]{2,1,0:T(8,128)(2,1)S(1)}, u32[]{:S(2)}, u32[]{:S(2)}) %collective-permute-start.16) | collective-permute-done | bytes 516128 | tf_op jit(solution)/shard_map/ppermute | solution.py:67
  72.8 0.3 maximum_select_fusion.2
  73.2 0.3 maximum_select_fusion.3
  73.4 0.5 collective-permute-start.29
  73.9 1.8 %collective-permute-done.17 = bf16[3,96,1792]{2,1,0:T(8,128)(2,1)S(1)} collective-permute-done((bf16[3,96,1792]{2,1,0:T(8,128)(2,1)S(1)}, bf16[3,96,1792]{2,1,0:T(8,128)(2,1)S(1)}, u32[]{:S(2)}, u32[]{:S(2)}) %collective-permute-start.17) | collective-permute-done | bytes 1032224 | tf_op jit(solution)/shard_map/ppermute | solution.py:67
  75.7 0.8 maximum_select_fusion
  76.5 0.8 collective-permute-done.29
  77.3 2.1 %maximum_select_fusion.1 = bf16[3,192,1792]{2,1,0:T(8,128)(2,1)S(1)} fusion(bf16[3,96,1792]{2,1,0:T(8,128)(2,1)S(1)} %maximum_select_fusion.3, bf16[3,96,1792]{2,1,0:T(8,128)(2,1)} %collective-permute-done.29, pred[]{:T(512)S(6)} %eq.25), kind=kLoop, calls=%fused_computation.11 | loop fusion | flops 9289728 | bytes 4128769 | tf_op jit(solution)/shard_map/jit(_where)/select_n | solution.py:68
  79.4 0.5 fusion.4
  80.0 1.3 %slice-done.3 = s8[3145728]{0:T(1024)(128)(4,1)S(1)} async-done(((s8[7340032]{0:T(1024)(128)(4,1)}), s8[3145728]{0:T(1024)(128)(4,1)S(1)}, s32[]{:S(2)}) %slice-start.3) | async-done | bytes 3145752
  81.3 2.5 %fusion.16 = f32[192,1024]{1,0:T(8,128)S(1)} fusion(bf16[192,3584]{1,0:T(8,128)(2,1)S(1)} %get-tuple-element.22, bf16[1024,3584]{1,0:T(8,128)(2,1)S(1)} %bitcast.37), kind=kOutput, calls=%fused_computation.86 | convolution fusion | flops 1409286144 | bytes 9502720 | tf_op jit(solution)/shard_map/dot_general | solution.py:14
  83.8 2.5 %fusion.5 = bf16[192,1024]{1,0:T(8,128)(2,1)S(1)} fusion(f32[192,1024]{1,0:T(8,128)S(1)} %fusion.16, bf16[192,3584]{1,0:T(8,128)(2,1)S(1)} %get-tuple-element.17, bf16[1024,3584]{1,0:T(8,128)(2,1)S(1)} %bitcast.41), kind=kOutput, calls=%fused_computation.19 | convolution fusion | flops 1409679360 | bytes 9895936 | tf_op jit(solution)/shard_map/dot_general | solution.py:14
  86.4 5.2 %convolution_convert_fusion.2 = bf16[1024,3584]{1,0:T(8,128)(2,1)} fusion(bf16[192,1024]{1,0:T(8,128)(2,1)S(1)} %pad_maximum_fusion.1, bf16[192,3584]{1,0:T(8,128)(2,1)S(1)} %get-tuple-element.17), kind=kOutput, calls=%fused_computation.2 | convolution fusion | flops 1412956160 | bytes 9109504 | tf_op jit(solution)/shard_map/dot_general | solution.py:129
  91.6 1.9 %collective-permute-start.30 = (bf16[48,1024]{1,0:T(8,128)(2,1)S(1)}, bf16[48,1024]{1,0:T(8,128)(2,1)S(1)}, u32[]{:S(2)}, u32[]{:S(2)}) collective-permute-start(bf16[48,1024]{1,0:T(8,128)(2,1)S(1)} %get-tuple-element.39), channel_id=1, source_target_pairs={{0,3},{1,0},{2,1},{3,2},{4,7},{5,4},{6,5},{7,6},{8,11},{9,8},{10,9... | collective-permute-start | bytes 294920 | tf_op jit(solution)/shard_map/ppermute | solution.py:106
  93.5 0.1 collective-permute-start.32
  93.7 0.7 collective-permute-start.31
  94.4 5.2 %convolution_convert_fusion.1 = bf16[1024,3584]{1,0:T(8,128)(2,1)} fusion(bf16[192,1024]{1,0:T(8,128)(2,1)S(1)} %pad_maximum_fusion.1, bf16[192,3584]{1,0:T(8,128)(2,1)S(1)} %get-tuple-element.22), kind=kOutput, calls=%fused_computation.1 | convolution fusion | flops 1412956160 | bytes 9109504 | tf_op jit(solution)/shard_map/dot_general | solution.py:132
  99.6 5.2 %convolution_convert_fusion = bf16[3584,1024]{1,0:T(8,128)(2,1)} fusion(bf16[192,3584]{1,0:T(8,128)(2,1)S(1)} %get-tuple-element.23, bf16[192,1024]{1,0:T(8,128)(2,1)S(1)} %copy-done.1), kind=kOutput, calls=%fused_computation | convolution fusion | flops 1412956160 | bytes 9109504 | tf_op jit(solution)/shard_map/dot_general | solution.py:8
  104.8 0.7 add_convert_fusion.12
  (87 shorter events, 2.3 us)
Async XLA Ops:
  0.6 12.2 %collective-permute-start.1 = (bf16[48,1024]{1,0:T(8,128)(2,1)}, bf16[48,1024]{1,0:T(8,128)(2,1)S(1)}, u32[]{:S(2)}, u32[]{:S(2)}) collective-permute-start(bf16[48,1024]{1,0:T(8,128)(2,1)} %param.5), channel_id=1, source_target_pairs={{0,2},{1,3},{2,0},{3,1},{4,6},{5,7},{6,4},{7,5},{8,10},{9,11},{10,... | collective-permute-start | bytes 294920 | tf_op jit(solution)/shard_map/ppermute | solution.py:98
  4.8 8.1 %collective-permute-start = (bf16[48,1024]{1,0:T(8,128)(2,1)}, bf16[48,1024]{1,0:T(8,128)(2,1)S(1)}, u32[]{:S(2)}, u32[]{:S(2)}) collective-permute-start(bf16[48,1024]{1,0:T(8,128)(2,1)} %param.5), channel_id=1, source_target_pairs={{0,1},{1,2},{2,3},{3,0},{4,5},{5,6},{6,7},{7,4},{8,9},{9,10},{10,1... | collective-permute-start | bytes 294920 | tf_op jit(solution)/shard_map/ppermute | solution.py:98
  6.3 7.2 %collective-permute-start.2 = (bf16[48,1024]{1,0:T(8,128)(2,1)}, bf16[48,1024]{1,0:T(8,128)(2,1)S(1)}, u32[]{:S(2)}, u32[]{:S(2)}) collective-permute-start(bf16[48,1024]{1,0:T(8,128)(2,1)} %param.5), channel_id=1, source_target_pairs={{0,3},{1,0},{2,1},{3,2},{4,7},{5,4},{6,5},{7,6},{8,11},{9,8},{10,9... | collective-permute-start | bytes 294920 | tf_op jit(solution)/shard_map/ppermute | solution.py:98
  13.6 11.8 %slice-start.4 = ((s8[7340032]{0:T(1024)(128)(4,1)}), s8[4194304]{0:T(1024)(128)(4,1)S(1)}, s32[]{:S(2)}) async-start(s8[7340032]{0:T(1024)(128)(4,1)} %bitcast.38), calls=%async_computation.4 | async-start | bytes 8388608
  14.6 10.7 %slice-start.5 = ((s8[7340032]{0:T(1024)(128)(4,1)}), s8[3145728]{0:T(1024)(128)(4,1)S(1)}, s32[]{:S(2)}) async-start(s8[7340032]{0:T(1024)(128)(4,1)} %bitcast.38), calls=%async_computation.5 | async-start | bytes 6291456
  14.7 13.9 %collective-permute-start.11 = (bf16[48,1024]{1,0:T(8,128)(2,1)}, bf16[48,1024]{1,0:T(8,128)(2,1)S(1)}, u32[]{:S(2)}, u32[]{:S(2)}) collective-permute-start(bf16[48,1024]{1,0:T(8,128)(2,1)} %param.6), channel_id=1, source_target_pairs={{0,3},{1,0},{2,1},{3,2},{4,7},{5,4},{6,5},{7,6},{8,11},{9,8},{10,9... | collective-permute-start | bytes 294920 | tf_op jit(solution)/shard_map/ppermute | solution.py:98
  16.8 11.3 %collective-permute-start.10 = (bf16[48,1024]{1,0:T(8,128)(2,1)}, bf16[48,1024]{1,0:T(8,128)(2,1)S(1)}, u32[]{:S(2)}, u32[]{:S(2)}) collective-permute-start(bf16[48,1024]{1,0:T(8,128)(2,1)} %param.6), channel_id=1, source_target_pairs={{0,2},{1,3},{2,0},{3,1},{4,6},{5,7},{6,4},{7,5},{8,10},{9,11},{10,... | collective-permute-start | bytes 294920 | tf_op jit(solution)/shard_map/ppermute | solution.py:98
  17.9 10.0 %collective-permute-start.9 = (bf16[48,1024]{1,0:T(8,128)(2,1)}, bf16[48,1024]{1,0:T(8,128)(2,1)S(1)}, u32[]{:S(2)}, u32[]{:S(2)}) collective-permute-start(bf16[48,1024]{1,0:T(8,128)(2,1)} %param.6), channel_id=1, source_target_pairs={{0,1},{1,2},{2,3},{3,0},{4,5},{5,6},{6,7},{7,4},{8,9},{9,10},{10,1... | collective-permute-start | bytes 294920 | tf_op jit(solution)/shard_map/ppermute | solution.py:98
  24.7 3.9 %slice-start = ((s8[7340032]{0:T(1024)(128)(4,1)}), s8[4194304]{0:T(1024)(128)(4,1)S(1)}, s32[]{:S(2)}) async-start(s8[7340032]{0:T(1024)(128)(4,1)} %bitcast.34), calls=%async_computation | async-start | bytes 8388608
  24.8 3.9 %slice-start.1 = ((s8[7340032]{0:T(1024)(128)(4,1)}), s8[3145728]{0:T(1024)(128)(4,1)S(1)}, s32[]{:S(2)}) async-start(s8[7340032]{0:T(1024)(128)(4,1)} %bitcast.34), calls=%async_computation.1 | async-start | bytes 6291456
  24.8 6.7 %collective-permute-start.6 = (bf16[96,1792]{1,0:T(8,128)(2,1)S(1)}, bf16[96,1792]{1,0:T(8,128)(2,1)S(1)}, u32[]{:S(2)}, u32[]{:S(2)}) collective-permute-start(bf16[96,1792]{1,0:T(8,128)(2,1)S(1)} %constant_dynamic-slice_fusion.14), channel_id=1, source_target_pairs={{0,4},{4,0},{8,12},{12,8},{16,20},{20,16},{24,28},{28,24},{1,5},{5... | collective-permute-start | bytes 1032200 | tf_op jit(solution)/shard_map/ppermute | solution.py:39
  24.9 7.3 %collective-permute-start.21 = (bf16[96,1792]{1,0:T(8,128)(2,1)S(1)}, bf16[96,1792]{1,0:T(8,128)(2,1)S(1)}, u32[]{:S(2)}, u32[]{:S(2)}) collective-permute-start(bf16[96,1792]{1,0:T(8,128)(2,1)S(1)} %constant_dynamic-slice_fusion.5), channel_id=1, source_target_pairs={{0,4},{4,0},{8,12},{12,8},{16,20},{20,16},{24,28},{28,24},{1,5},{5... | collective-permute-start | bytes 1032200 | tf_op jit(solution)/shard_map/ppermute | solution.py:39
  27.0 0.9 copy-start.2
  27.9 5.9 %collective-permute-start.3 = (bf16[96,1792]{1,0:T(8,128)(2,1)S(1)}, bf16[96,1792]{1,0:T(8,128)(2,1)S(1)}, u32[]{:S(2)}, u32[]{:S(2)}) collective-permute-start(bf16[96,1792]{1,0:T(8,128)(2,1)S(1)} %constant_dynamic-slice_fusion.17), channel_id=1, source_target_pairs={{0,4},{4,0},{8,12},{12,8},{16,20},{20,16},{24,28},{28,24},{1,5},{5... | collective-permute-start | bytes 1032200 | tf_op jit(solution)/shard_map/ppermute | solution.py:39
  28.1 7.5 %collective-permute-start.18 = (bf16[96,1792]{1,0:T(8,128)(2,1)S(1)}, bf16[96,1792]{1,0:T(8,128)(2,1)S(1)}, u32[]{:S(2)}, u32[]{:S(2)}) collective-permute-start(bf16[96,1792]{1,0:T(8,128)(2,1)S(1)} %constant_dynamic-slice_fusion.8), channel_id=1, source_target_pairs={{0,4},{4,0},{8,12},{12,8},{16,20},{20,16},{24,28},{28,24},{1,5},{5... | collective-permute-start | bytes 1032200 | tf_op jit(solution)/shard_map/ppermute | solution.py:39
  28.6 2.6 %copy-start = (bf16[192,1024]{1,0:T(8,128)(2,1)}, bf16[192,1024]{1,0:T(8,128)(2,1)S(1)}, u32[]{:S(2)}) copy-start(bf16[192,1024]{1,0:T(8,128)(2,1)S(1)} %constant_dynamic-update-slice_fusion) | copy-start | bytes 1179652
  31.4 4.9 %collective-permute-start.12 = (bf16[96,1792]{1,0:T(8,128)(2,1)S(1)}, bf16[96,1792]{1,0:T(8,128)(2,1)S(1)}, u32[]{:S(2)}, u32[]{:S(2)}) collective-permute-start(bf16[96,1792]{1,0:T(8,128)(2,1)S(1)} %constant_dynamic-slice_fusion.11), channel_id=1, source_target_pairs={{0,4},{4,0},{8,12},{12,8},{16,20},{20,16},{24,28},{28,24},{1,5},{5... | collective-permute-start | bytes 1032200 | tf_op jit(solution)/shard_map/ppermute | solution.py:39
  31.5 5.5 %collective-permute-start.24 = (bf16[96,1792]{1,0:T(8,128)(2,1)S(1)}, bf16[96,1792]{1,0:T(8,128)(2,1)S(1)}, u32[]{:S(2)}, u32[]{:S(2)}) collective-permute-start(bf16[96,1792]{1,0:T(8,128)(2,1)S(1)} %constant_dynamic-slice_fusion.2), channel_id=1, source_target_pairs={{0,4},{4,0},{8,12},{12,8},{16,20},{20,16},{24,28},{28,24},{1,5},{5... | collective-permute-start | bytes 1032200 | tf_op jit(solution)/shard_map/ppermute | solution.py:39
  32.2 7.3 %collective-permute-start.7 = (bf16[48,1792]{1,0:T(8,128)(2,1)S(1)}, bf16[48,1792]{1,0:T(8,128)(2,1)S(1)}, u32[]{:S(2)}, u32[]{:S(2)}) collective-permute-start(bf16[48,1792]{1,0:T(8,128)(2,1)S(1)} %constant_dynamic-slice_fusion.13), channel_id=1, source_target_pairs={{0,8},{4,12},{8,0},{12,4},{16,24},{20,28},{24,16},{28,20},{1,9},{5... | collective-permute-start | bytes 516104 | tf_op jit(solution)/shard_map/ppermute | solution.py:39
  33.8 7.3 %collective-permute-start.22 = (bf16[48,1792]{1,0:T(8,128)(2,1)S(1)}, bf16[48,1792]{1,0:T(8,128)(2,1)S(1)}, u32[]{:S(2)}, u32[]{:S(2)}) collective-permute-start(bf16[48,1792]{1,0:T(8,128)(2,1)S(1)} %constant_dynamic-slice_fusion.4), channel_id=1, source_target_pairs={{0,16},{4,20},{8,24},{12,28},{16,0},{20,4},{24,8},{28,12},{1,17},{... | collective-permute-start | bytes 516104 | tf_op jit(solution)/shard_map/ppermute | solution.py:39
  35.6 7.5 %collective-permute-start.4 = (bf16[48,1792]{1,0:T(8,128)(2,1)S(1)}, bf16[48,1792]{1,0:T(8,128)(2,1)S(1)}, u32[]{:S(2)}, u32[]{:S(2)}) collective-permute-start(bf16[48,1792]{1,0:T(8,128)(2,1)S(1)} %constant_dynamic-slice_fusion.16), channel_id=1, source_target_pairs={{0,8},{4,12},{8,0},{12,4},{16,24},{20,28},{24,16},{28,20},{1,9},{5... | collective-permute-start | bytes 516104 | tf_op jit(solution)/shard_map/ppermute | solution.py:39
  36.3 8.6 %collective-permute-start.19 = (bf16[48,1792]{1,0:T(8,128)(2,1)S(1)}, bf16[48,1792]{1,0:T(8,128)(2,1)S(1)}, u32[]{:S(2)}, u32[]{:S(2)}) collective-permute-start(bf16[48,1792]{1,0:T(8,128)(2,1)S(1)} %constant_dynamic-slice_fusion.7), channel_id=1, source_target_pairs={{0,16},{4,20},{8,24},{12,28},{16,0},{20,4},{24,8},{28,12},{1,17},{... | collective-permute-start | bytes 516104 | tf_op jit(solution)/shard_map/ppermute | solution.py:39
  37.0 9.8 %collective-permute-start.13 = (bf16[48,1792]{1,0:T(8,128)(2,1)S(1)}, bf16[48,1792]{1,0:T(8,128)(2,1)S(1)}, u32[]{:S(2)}, u32[]{:S(2)}) collective-permute-start(bf16[48,1792]{1,0:T(8,128)(2,1)S(1)} %constant_dynamic-slice_fusion.10), channel_id=1, source_target_pairs={{0,8},{4,12},{8,0},{12,4},{16,24},{20,28},{24,16},{28,20},{1,9},{5... | collective-permute-start | bytes 516104 | tf_op jit(solution)/shard_map/ppermute | solution.py:39
  39.4 9.1 %collective-permute-start.25 = (bf16[48,1792]{1,0:T(8,128)(2,1)S(1)}, bf16[48,1792]{1,0:T(8,128)(2,1)S(1)}, u32[]{:S(2)}, u32[]{:S(2)}) collective-permute-start(bf16[48,1792]{1,0:T(8,128)(2,1)S(1)} %constant_dynamic-slice_fusion.1), channel_id=1, source_target_pairs={{0,16},{4,20},{8,24},{12,28},{16,0},{20,4},{24,8},{28,12},{1,17},{... | collective-permute-start | bytes 516104 | tf_op jit(solution)/shard_map/ppermute | solution.py:39
  41.1 9.2 %collective-permute-start.8 = (bf16[24,1792]{1,0:T(8,128)(2,1)S(1)}, bf16[24,1792]{1,0:T(8,128)(2,1)S(1)}, u32[]{:S(2)}, u32[]{:S(2)}) collective-permute-start(bf16[24,1792]{1,0:T(8,128)(2,1)S(1)} %constant_dynamic-slice_fusion.12), channel_id=1, source_target_pairs={{0,16},{4,20},{8,24},{12,28},{16,0},{20,4},{24,8},{28,12},{1,17},{... | collective-permute-start | bytes 258056 | tf_op jit(solution)/shard_map/ppermute | solution.py:39
  43.1 11.7 %collective-permute-start.23 = (bf16[24,1792]{1,0:T(8,128)(2,1)S(1)}, bf16[24,1792]{1,0:T(8,128)(2,1)S(1)}, u32[]{:S(2)}, u32[]{:S(2)}) collective-permute-start(bf16[24,1792]{1,0:T(8,128)(2,1)S(1)} %constant_dynamic-slice_fusion.3), channel_id=1, source_target_pairs={{0,8},{4,12},{8,0},{12,4},{16,24},{20,28},{24,16},{28,20},{1,9},{5... | collective-permute-start | bytes 258056 | tf_op jit(solution)/shard_map/ppermute | solution.py:39
  44.8 7.1 %collective-permute-start.5 = (bf16[24,1792]{1,0:T(8,128)(2,1)S(1)}, bf16[24,1792]{1,0:T(8,128)(2,1)S(1)}, u32[]{:S(2)}, u32[]{:S(2)}) collective-permute-start(bf16[24,1792]{1,0:T(8,128)(2,1)S(1)} %constant_dynamic-slice_fusion.15), channel_id=1, source_target_pairs={{0,16},{4,20},{8,24},{12,28},{16,0},{20,4},{24,8},{28,12},{1,17},{... | collective-permute-start | bytes 258056 | tf_op jit(solution)/shard_map/ppermute | solution.py:39
  46.8 8.0 %collective-permute-start.20 = (bf16[24,1792]{1,0:T(8,128)(2,1)S(1)}, bf16[24,1792]{1,0:T(8,128)(2,1)S(1)}, u32[]{:S(2)}, u32[]{:S(2)}) collective-permute-start(bf16[24,1792]{1,0:T(8,128)(2,1)S(1)} %constant_dynamic-slice_fusion.6), channel_id=1, source_target_pairs={{0,8},{4,12},{8,0},{12,4},{16,24},{20,28},{24,16},{28,20},{1,9},{5... | collective-permute-start | bytes 258056 | tf_op jit(solution)/shard_map/ppermute | solution.py:39
  48.5 4.5 %collective-permute-start.14 = (bf16[24,1792]{1,0:T(8,128)(2,1)S(1)}, bf16[24,1792]{1,0:T(8,128)(2,1)S(1)}, u32[]{:S(2)}, u32[]{:S(2)}) collective-permute-start(bf16[24,1792]{1,0:T(8,128)(2,1)S(1)} %constant_dynamic-slice_fusion.9), channel_id=1, source_target_pairs={{0,16},{4,20},{8,24},{12,28},{16,0},{20,4},{24,8},{28,12},{1,17},{... | collective-permute-start | bytes 258056 | tf_op jit(solution)/shard_map/ppermute | solution.py:39
  50.3 4.5 %collective-permute-start.26 = (bf16[24,1792]{1,0:T(8,128)(2,1)S(1)}, bf16[24,1792]{1,0:T(8,128)(2,1)S(1)}, u32[]{:S(2)}, u32[]{:S(2)}) collective-permute-start(bf16[24,1792]{1,0:T(8,128)(2,1)S(1)} %constant_dynamic-slice_fusion), channel_id=1, source_target_pairs={{0,8},{4,12},{8,0},{12,4},{16,24},{20,28},{24,16},{28,20},{1,9},{5... | collective-permute-start | bytes 258056 | tf_op jit(solution)/shard_map/ppermute | solution.py:39
  53.2 7.0 %collective-permute-start.15 = (bf16[3,24,1792]{2,1,0:T(8,128)(2,1)S(1)}, bf16[3,24,1792]{2,1,0:T(8,128)(2,1)S(1)}, u32[]{:S(2)}, u32[]{:S(2)}) collective-permute-start(bf16[3,24,1792]{2,1,0:T(8,128)(2,1)S(1)} %pad_maximum_fusion.2), channel_id=1, source_target_pairs={{0,16},{4,20},{8,24},{12,28},{16,0},{20,4},{24,8},{28,12},{1,17},{... | collective-permute-start | bytes 774152 | tf_op jit(solution)/shard_map/ppermute | solution.py:67
  55.0 7.4 %collective-permute-start.27 = (bf16[3,24,1792]{2,1,0:T(8,128)(2,1)S(1)}, bf16[3,24,1792]{2,1,0:T(8,128)(2,1)S(1)}, u32[]{:S(2)}, u32[]{:S(2)}) collective-permute-start(bf16[3,24,1792]{2,1,0:T(8,128)(2,1)S(1)} %pad_maximum_fusion.3), channel_id=1, source_target_pairs={{0,8},{4,12},{8,0},{12,4},{16,24},{20,28},{24,16},{28,20},{1,9},{5... | collective-permute-start | bytes 774152 | tf_op jit(solution)/shard_map/ppermute | solution.py:67
  60.3 12.4 %collective-permute-start.16 = (bf16[3,48,1792]{2,1,0:T(8,128)(2,1)S(1)}, bf16[3,48,1792]{2,1,0:T(8,128)(2,1)S(1)}, u32[]{:S(2)}, u32[]{:S(2)}) collective-permute-start(bf16[3,48,1792]{2,1,0:T(8,128)(2,1)S(1)} %maximum_select_fusion.4), channel_id=1, source_target_pairs={{0,8},{4,12},{8,0},{12,4},{16,24},{20,28},{24,16},{28,20},{1,9},{5... | collective-permute-start | bytes 1548296 | tf_op jit(solution)/shard_map/ppermute | solution.py:67
  62.5 10.6 %collective-permute-start.28 = (bf16[3,48,1792]{2,1,0:T(8,128)(2,1)S(1)}, bf16[3,48,1792]{2,1,0:T(8,128)(2,1)S(1)}, u32[]{:S(2)}, u32[]{:S(2)}) collective-permute-start(bf16[3,48,1792]{2,1,0:T(8,128)(2,1)S(1)} %maximum_select_fusion.5), channel_id=1, source_target_pairs={{0,16},{4,20},{8,24},{12,28},{16,0},{20,4},{24,8},{28,12},{1,17},{... | collective-permute-start | bytes 1548296 | tf_op jit(solution)/shard_map/ppermute | solution.py:67
  73.0 2.7 %collective-permute-start.17 = (bf16[3,96,1792]{2,1,0:T(8,128)(2,1)S(1)}, bf16[3,96,1792]{2,1,0:T(8,128)(2,1)S(1)}, u32[]{:S(2)}, u32[]{:S(2)}) collective-permute-start(bf16[3,96,1792]{2,1,0:T(8,128)(2,1)S(1)} %maximum_select_fusion.2), channel_id=1, source_target_pairs={{0,4},{4,0},{8,12},{12,8},{16,20},{20,16},{24,28},{28,24},{1,5},{5... | collective-permute-start | bytes 3096584 | tf_op jit(solution)/shard_map/ppermute | solution.py:67
  73.4 3.9 %collective-permute-start.29 = (bf16[3,96,1792]{2,1,0:T(8,128)(2,1)S(1)}, bf16[3,96,1792]{2,1,0:T(8,128)(2,1)}, u32[]{:S(2)}, u32[]{:S(2)}) collective-permute-start(bf16[3,96,1792]{2,1,0:T(8,128)(2,1)S(1)} %maximum_select_fusion.3), channel_id=1, source_target_pairs={{0,4},{4,0},{8,12},{12,8},{16,20},{20,16},{24,28},{28,24},{1,5},{5... | collective-permute-start | bytes 3096584 | tf_op jit(solution)/shard_map/ppermute | solution.py:67
  75.7 4.3 %slice-start.2 = ((s8[7340032]{0:T(1024)(128)(4,1)}), s8[4194304]{0:T(1024)(128)(4,1)S(1)}, s32[]{:S(2)}) async-start(s8[7340032]{0:T(1024)(128)(4,1)} %bitcast.36), calls=%async_computation.2 | async-start | bytes 8388608
  79.4 1.9 %slice-start.3 = ((s8[7340032]{0:T(1024)(128)(4,1)}), s8[3145728]{0:T(1024)(128)(4,1)S(1)}, s32[]{:S(2)}) async-start(s8[7340032]{0:T(1024)(128)(4,1)} %bitcast.36), calls=%async_computation.3 | async-start | bytes 6291456
  79.4 4.4 %slice-start.6 = ((s8[7340032]{0:T(1024)(128)(4,1)}), s8[4194304]{0:T(1024)(128)(4,1)S(1)}, s32[]{:S(2)}) async-start(s8[7340032]{0:T(1024)(128)(4,1)} %bitcast.40), calls=%async_computation.6 | async-start | bytes 8388608
  81.3 2.5 %slice-start.7 = ((s8[7340032]{0:T(1024)(128)(4,1)}), s8[3145728]{0:T(1024)(128)(4,1)S(1)}, s32[]{:S(2)}) async-start(s8[7340032]{0:T(1024)(128)(4,1)} %bitcast.40), calls=%async_computation.7 | async-start | bytes 6291456
  91.6 13.2 %collective-permute-start.30 = (bf16[48,1024]{1,0:T(8,128)(2,1)S(1)}, bf16[48,1024]{1,0:T(8,128)(2,1)S(1)}, u32[]{:S(2)}, u32[]{:S(2)}) collective-permute-start(bf16[48,1024]{1,0:T(8,128)(2,1)S(1)} %get-tuple-element.39), channel_id=1, source_target_pairs={{0,3},{1,0},{2,1},{3,2},{4,7},{5,4},{6,5},{7,6},{8,11},{9,8},{10,9... | collective-permute-start | bytes 294920 | tf_op jit(solution)/shard_map/ppermute | solution.py:106
  93.5 11.3 %collective-permute-start.32 = (bf16[48,1024]{1,0:T(8,128)(2,1)S(1)}, bf16[48,1024]{1,0:T(8,128)(2,1)S(1)}, u32[]{:S(2)}, u32[]{:S(2)}) collective-permute-start(bf16[48,1024]{1,0:T(8,128)(2,1)S(1)} %get-tuple-element.40), channel_id=1, source_target_pairs={{0,1},{1,2},{2,3},{3,0},{4,5},{5,6},{6,7},{7,4},{8,9},{9,10},{10,1... | collective-permute-start | bytes 294920 | tf_op jit(solution)/shard_map/ppermute | solution.py:106
  93.7 5.9 %copy-start.1 = (bf16[192,1024]{1,0:T(8,128)(2,1)S(1)}, bf16[192,1024]{1,0:T(8,128)(2,1)}, u32[]{:S(2)}) copy-start(bf16[192,1024]{1,0:T(8,128)(2,1)} %copy-done) | copy-start | bytes 1179652
  93.7 11.1 %collective-permute-start.31 = (bf16[48,1024]{1,0:T(8,128)(2,1)S(1)}, bf16[48,1024]{1,0:T(8,128)(2,1)S(1)}, u32[]{:S(2)}, u32[]{:S(2)}) collective-permute-start(bf16[48,1024]{1,0:T(8,128)(2,1)S(1)} %get-tuple-element.41), channel_id=1, source_target_pairs={{0,2},{1,3},{2,0},{3,1},{4,6},{5,7},{6,4},{7,5},{8,10},{9,11},{10,... | collective-permute-start | bytes 294920 | tf_op jit(solution)/shard_map/ppermute | solution.py:106

commit v17 on v16

--- a/solution.py
+++ b/solution.py
@@ -103,8 +103,10 @@
     span = x.shape[0] // n_col
     total = x[:span].astype(jnp.float32)
     for s in range(1, n_col):
-        got = lax.ppermute(x[s * span:(s + 1) * span], "col", [(j, (j - s) % n_col) for j in range(n_col)])
-        total = total + got.astype(jnp.float32)
+        block = x[s * span:(s + 1) * span]
+        left = lax.ppermute(block, "col", [(j, j - s) for j in range(s, n_col)])
+        right = lax.ppermute(block, "col", [(j, j - s + n_col) for j in range(s)])
+        total = total + left.astype(jnp.float32) + right.astype(jnp.float32)
     return total.astype(jnp.bfloat16)
 
 

time: 106 us -> 120 us (1.13)
  the two profiles are of different devices: /device:TPU:0 before, /device:TPU:24 now
where the time goes in v17:
time: 120 us
  starting transfers between devices  50.4 us (42%)
  matrix products  29.4 us (24%)
  waiting for transfers between devices  29.1 us (24%)
  other arithmetic  7.03 us (6%)
  local copies, waits for them, and re-layouts  2.81 us (2%)
  between operations  1.24 us (1%)
    ppermute x6, waiting for transfers between devices, doubling_gather(): got = lax.ppermute(cur, 'row', [(j, j ^ bit) for j in range(n_dev)])  17.7 us
    ppermute x18, starting transfers between devices, halving_reduce(): lax.ppermute(lax.dynamic_slice_in_dim(c, (1 - hi) * n, n, 0), 'row', perm)  17.3 us
    ppermute x3, starting transfers between devices, col_reduce_scatter(): left = lax.ppermute(block, 'col', [(j, j - s) for j in range(s, n_col)])  16.3 us
    ppermute x6, starting transfers between devices, col_gather(): lax.ppermute(x, 'col', [(j, (j + s) % n_col) for j in range(n_col)])  7.94 us
    dot_general x3, matrix products, contract_last(): lax.dot_general(left, right, (((1,), (1,)), ((), ())), preferred_element_...  7.58 us
    ppermute x6, waiting for transfers between devices, col_gather(): lax.ppermute(x, 'col', [(j, (j + s) % n_col) for j in range(n_col)])  7.04 us
    dot_general x1, matrix products, body(): acc_up = jnp.dot(tok_t, grad_up, preferred_element_type=jnp.float32)  5.18 us
    dot_general x1, matrix products, body(): jnp.dot(tok_t, grad_gate, preferred_element_type=jnp.float32)  5.18 us
  transfers between devices with their start and end apart: 36, of which 16 were waited for; matrix products, arithmetic and copies ran while one was open for 19% of the time, Pallas kernels for 0%

profile of v17, /device:TPU:24, one launch (start us, length us, event | category | flops | bytes accessed | tf_op | source)
XLA Modules:
  0.0 119.9 jit_solution(9530568260954067331)
XLA Ops:
  0.6 0.4 collective-permute-start.1
  1.0 2.5 %collective-permute-start = (bf16[48,1024]{1,0:T(8,128)(2,1)}, bf16[48,1024]{1,0:T(8,128)(2,1)S(1)}, u32[]{:S(2)}, u32[]{:S(2)}) collective-permute-start(bf16[48,1024]{1,0:T(8,128)(2,1)} %param.5), channel_id=1, source_target_pairs={{0,1},{1,2},{2,3},{3,0},{4,5},{5,6},{6,7},{7,4},{8,9},{9,10},{10,1... | collective-permute-start | bytes 294920 | tf_op jit(solution)/shard_map/ppermute | solution.py:98
  3.5 7.0 %collective-permute-done.1 = bf16[48,1024]{1,0:T(8,128)(2,1)S(1)} collective-permute-done((bf16[48,1024]{1,0:T(8,128)(2,1)}, bf16[48,1024]{1,0:T(8,128)(2,1)S(1)}, u32[]{:S(2)}, u32[]{:S(2)}) %collective-permute-start.1) | collective-permute-done | bytes 98336 | tf_op jit(solution)/shard_map/ppermute | solution.py:98
  10.5 1.1 pad_maximum_fusion.1
  11.6 2.6 %collective-permute-start.11 = (bf16[48,1024]{1,0:T(8,128)(2,1)}, bf16[48,1024]{1,0:T(8,128)(2,1)S(1)}, u32[]{:S(2)}, u32[]{:S(2)}) collective-permute-start(bf16[48,1024]{1,0:T(8,128)(2,1)} %param.6), channel_id=1, source_target_pairs={{0,3},{1,0},{2,1},{3,2},{4,7},{5,4},{6,5},{7,6},{8,11},{9,8},{10,9... | collective-permute-start | bytes 294920 | tf_op jit(solution)/shard_map/ppermute | solution.py:98
  14.3 2.4 %collective-permute-start.9 = (bf16[48,1024]{1,0:T(8,128)(2,1)}, bf16[48,1024]{1,0:T(8,128)(2,1)S(1)}, u32[]{:S(2)}, u32[]{:S(2)}) collective-permute-start(bf16[48,1024]{1,0:T(8,128)(2,1)} %param.6), channel_id=1, source_target_pairs={{0,1},{1,2},{2,3},{3,0},{4,5},{5,6},{6,7},{7,4},{8,9},{9,10},{10,1... | collective-permute-start | bytes 294920 | tf_op jit(solution)/shard_map/ppermute | solution.py:98
  16.7 4.7 %convolution_convert_fusion.4 = bf16[192,3584]{1,0:T(8,128)(2,1)S(1)} fusion(bf16[192,1024]{1,0:T(8,128)(2,1)S(1)} %pad_maximum_fusion.1, bf16[1024,3584]{1,0:T(8,128)(2,1)} %param.8), kind=kOutput, calls=%fused_computation.4 | convolution fusion | flops 1409974272 | bytes 9109504 | tf_op jit(solution)/shard_map/dot_general | solution.py:122
  21.7 0.5 collective-permute-start.21
  22.2 1.6 %convolution_convert_fusion.5 = bf16[192,3584]{1,0:T(8,128)(2,1)S(1)} fusion(bf16[192,1024]{1,0:T(8,128)(2,1)S(1)} %pad_maximum_fusion.1, bf16[1024,3584]{1,0:T(8,128)(2,1)S(1)} %bitcast.39), kind=kOutput, calls=%fused_computation.5 | convolution fusion | flops 1409974272 | bytes 9109504 | tf_op jit(solution)/shard_map/dot_general | solution.py:121
  24.0 0.7 copy-done.2
  24.7 0.1 collective-permute-start.3
  24.9 0.5 collective-permute-start.18
  25.4 2.6 %convolution_convert_fusion.3 = bf16[192,3584]{1,0:T(8,128)(2,1)S(1)} fusion(bf16[192,1024]{1,0:T(8,128)(2,1)S(1)} %constant_dynamic-update-slice_fusion, bf16[3584,1024]{1,0:T(8,128)(2,1)S(1)} %bitcast.35), kind=kOutput, calls=%fused_computation.3 | convolution fusion | flops 1409974272 | bytes 9109504 | tf_op jit(solution)/shard_map/dot_general | solution.py:14
  28.2 0.1 collective-permute-start.12
  28.3 0.5 collective-permute-start.24
  29.0 1.5 %collective-permute-start.7 = (bf16[48,1792]{1,0:T(8,128)(2,1)S(1)}, bf16[48,1792]{1,0:T(8,128)(2,1)S(1)}, u32[]{:S(2)}, u32[]{:S(2)}) collective-permute-start(bf16[48,1792]{1,0:T(8,128)(2,1)S(1)} %constant_dynamic-slice_fusion.13), channel_id=1, source_target_pairs={{0,8},{4,12},{8,0},{12,4},{16,24},{20,28},{24,16},{28,20},{1,9},{5... | collective-permute-start | bytes 516104 | tf_op jit(solution)/shard_map/ppermute | solution.py:39
  30.6 1.6 %collective-permute-start.22 = (bf16[48,1792]{1,0:T(8,128)(2,1)S(1)}, bf16[48,1792]{1,0:T(8,128)(2,1)S(1)}, u32[]{:S(2)}, u32[]{:S(2)}) collective-permute-start(bf16[48,1792]{1,0:T(8,128)(2,1)S(1)} %constant_dynamic-slice_fusion.4), channel_id=1, source_target_pairs={{0,16},{4,20},{8,24},{12,28},{16,0},{20,4},{24,8},{28,12},{1,17},{... | collective-permute-start | bytes 516104 | tf_op jit(solution)/shard_map/ppermute | solution.py:39
  32.4 0.6 collective-permute-start.4
  33.1 0.6 collective-permute-start.19
  33.8 1.5 %collective-permute-start.13 = (bf16[48,1792]{1,0:T(8,128)(2,1)S(1)}, bf16[48,1792]{1,0:T(8,128)(2,1)S(1)}, u32[]{:S(2)}, u32[]{:S(2)}) collective-permute-start(bf16[48,1792]{1,0:T(8,128)(2,1)S(1)} %constant_dynamic-slice_fusion.10), channel_id=1, source_target_pairs={{0,8},{4,12},{8,0},{12,4},{16,24},{20,28},{24,16},{28,20},{1,9},{5... | collective-permute-start | bytes 516104 | tf_op jit(solution)/shard_map/ppermute | solution.py:39
  35.4 0.8 collective-permute-done.7
  36.2 1.6 %collective-permute-start.25 = (bf16[48,1792]{1,0:T(8,128)(2,1)S(1)}, bf16[48,1792]{1,0:T(8,128)(2,1)S(1)}, u32[]{:S(2)}, u32[]{:S(2)}) collective-permute-start(bf16[48,1792]{1,0:T(8,128)(2,1)S(1)} %constant_dynamic-slice_fusion.1), channel_id=1, source_target_pairs={{0,16},{4,20},{8,24},{12,28},{16,0},{20,4},{24,8},{28,12},{1,17},{... | collective-permute-start | bytes 516104 | tf_op jit(solution)/shard_map/ppermute | solution.py:39
  37.9 1.6 %collective-permute-start.8 = (bf16[24,1792]{1,0:T(8,128)(2,1)S(1)}, bf16[24,1792]{1,0:T(8,128)(2,1)S(1)}, u32[]{:S(2)}, u32[]{:S(2)}) collective-permute-start(bf16[24,1792]{1,0:T(8,128)(2,1)S(1)} %constant_dynamic-slice_fusion.12), channel_id=1, source_target_pairs={{0,16},{4,20},{8,24},{12,28},{16,0},{20,4},{24,8},{28,12},{1,17},{... | collective-permute-start | bytes 258056 | tf_op jit(solution)/shard_map/ppermute | solution.py:39
  39.6 0.3 collective-permute-done.4
  39.9 1.5 %collective-permute-start.23 = (bf16[24,1792]{1,0:T(8,128)(2,1)S(1)}, bf16[24,1792]{1,0:T(8,128)(2,1)S(1)}, u32[]{:S(2)}, u32[]{:S(2)}) collective-permute-start(bf16[24,1792]{1,0:T(8,128)(2,1)S(1)} %constant_dynamic-slice_fusion.3), channel_id=1, source_target_pairs={{0,8},{4,12},{8,0},{12,4},{16,24},{20,28},{24,16},{28,20},{1,9},{5... | collective-permute-start | bytes 258056 | tf_op jit(solution)/shard_map/ppermute | solution.py:39
  41.5 0.1 collective-permute-done.19
  41.6 1.6 %collective-permute-start.5 = (bf16[24,1792]{1,0:T(8,128)(2,1)S(1)}, bf16[24,1792]{1,0:T(8,128)(2,1)S(1)}, u32[]{:S(2)}, u32[]{:S(2)}) collective-permute-start(bf16[24,1792]{1,0:T(8,128)(2,1)S(1)} %constant_dynamic-slice_fusion.15), channel_id=1, source_target_pairs={{0,16},{4,20},{8,24},{12,28},{16,0},{20,4},{24,8},{28,12},{1,17},{... | collective-permute-start | bytes 258056 | tf_op jit(solution)/shard_map/ppermute | solution.py:39
  43.2 0.3 collective-permute-done.13
  43.6 1.5 %collective-permute-start.20 = (bf16[24,1792]{1,0:T(8,128)(2,1)S(1)}, bf16[24,1792]{1,0:T(8,128)(2,1)S(1)}, u32[]{:S(2)}, u32[]{:S(2)}) collective-permute-start(bf16[24,1792]{1,0:T(8,128)(2,1)S(1)} %constant_dynamic-slice_fusion.6), channel_id=1, source_target_pairs={{0,8},{4,12},{8,0},{12,4},{16,24},{20,28},{24,16},{28,20},{1,9},{5... | collective-permute-start | bytes 258056 | tf_op jit(solution)/shard_map/ppermute | solution.py:39
  45.3 1.6 %collective-permute-start.14 = (bf16[24,1792]{1,0:T(8,128)(2,1)S(1)}, bf16[24,1792]{1,0:T(8,128)(2,1)S(1)}, u32[]{:S(2)}, u32[]{:S(2)}) collective-permute-start(bf16[24,1792]{1,0:T(8,128)(2,1)S(1)} %constant_dynamic-slice_fusion.9), channel_id=1, source_target_pairs={{0,16},{4,20},{8,24},{12,28},{16,0},{20,4},{24,8},{28,12},{1,17},{... | collective-permute-start | bytes 258056 | tf_op jit(solution)/shard_map/ppermute | solution.py:39
  46.9 0.2 collective-permute-done.8
  47.2 0.4 collective-permute-start.26
  47.5 1.3 %collective-permute-done.5 = bf16[24,1792]{1,0:T(8,128)(2,1)S(1)} collective-permute-done((bf16[24,1792]{1,0:T(8,128)(2,1)S(1)}, bf16[24,1792]{1,0:T(8,128)(2,1)S(1)}, u32[]{:S(2)}, u32[]{:S(2)}) %collective-permute-start.5) | collective-permute-done | bytes 86048 | tf_op jit(solution)/shard_map/ppermute | solution.py:39
  48.8 1.0 collective-permute-done.14
  49.8 0.2 fusion.6
  50.0 1.6 %collective-permute-start.15 = (bf16[3,24,1792]{2,1,0:T(8,128)(2,1)S(1)}, bf16[3,24,1792]{2,1,0:T(8,128)(2,1)S(1)}, u32[]{:S(2)}, u32[]{:S(2)}) collective-permute-start(bf16[3,24,1792]{2,1,0:T(8,128)(2,1)S(1)} %pad_maximum_fusion.2), channel_id=1, source_target_pairs={{0,16},{4,20},{8,24},{12,28},{16,0},{20,4},{24,8},{28,12},{1,17},{... | collective-permute-start | bytes 774152 | tf_op jit(solution)/shard_map/ppermute | solution.py:67
  51.6 0.2 fusion.8
  51.8 0.6 collective-permute-start.27
  52.4 4.6 %collective-permute-done.15 = bf16[3,24,1792]{2,1,0:T(8,128)(2,1)S(1)} collective-permute-done((bf16[3,24,1792]{2,1,0:T(8,128)(2,1)S(1)}, bf16[3,24,1792]{2,1,0:T(8,128)(2,1)S(1)}, u32[]{:S(2)}, u32[]{:S(2)}) %collective-permute-start.15) | collective-permute-done | bytes 258080 | tf_op jit(solution)/shard_map/ppermute | solution.py:67
  57.1 0.8 collective-permute-start.16
  58.0 1.3 %collective-permute-done.27 = bf16[3,24,1792]{2,1,0:T(8,128)(2,1)S(1)} collective-permute-done((bf16[3,24,1792]{2,1,0:T(8,128)(2,1)S(1)}, bf16[3,24,1792]{2,1,0:T(8,128)(2,1)S(1)}, u32[]{:S(2)}, u32[]{:S(2)}) %collective-permute-start.27) | collective-permute-done | bytes 258080 | tf_op jit(solution)/shard_map/ppermute | solution.py:67
  59.3 1.2 collective-permute-start.28
  60.5 9.1 %collective-permute-done.16 = bf16[3,48,1792]{2,1,0:T(8,128)(2,1)S(1)} collective-permute-done((bf16[3,48,1792]{2,1,0:T(8,128)(2,1)S(1)}, bf16[3,48,1792]{2,1,0:T(8,128)(2,1)S(1)}, u32[]{:S(2)}, u32[]{:S(2)}) %collective-permute-start.16) | collective-permute-done | bytes 516128 | tf_op jit(solution)/shard_map/ppermute | solution.py:67
  69.6 0.3 maximum_select_fusion.2
  70.0 0.3 maximum_select_fusion.3
  70.2 0.5 collective-permute-start.29
  70.7 1.8 %collective-permute-done.17 = bf16[3,96,1792]{2,1,0:T(8,128)(2,1)S(1)} collective-permute-done((bf16[3,96,1792]{2,1,0:T(8,128)(2,1)S(1)}, bf16[3,96,1792]{2,1,0:T(8,128)(2,1)S(1)}, u32[]{:S(2)}, u32[]{:S(2)}) %collective-permute-start.17) | collective-permute-done | bytes 1032224 | tf_op jit(solution)/shard_map/ppermute | solution.py:67
  72.5 0.8 maximum_select_fusion
  73.3 0.8 collective-permute-done.29
  74.1 2.1 %maximum_select_fusion.1 = bf16[3,192,1792]{2,1,0:T(8,128)(2,1)S(1)} fusion(bf16[3,96,1792]{2,1,0:T(8,128)(2,1)S(1)} %maximum_select_fusion.3, bf16[3,96,1792]{2,1,0:T(8,128)(2,1)} %collective-permute-done.29, pred[]{:T(512)S(6)} %eq.25), kind=kLoop, calls=%fused_computation.11 | loop fusion | flops 9289728 | bytes 4128769 | tf_op jit(solution)/shard_map/jit(_where)/select_n | solution.py:68
  76.2 0.5 fusion.4
  76.8 1.3 %slice-done.3 = s8[3145728]{0:T(1024)(128)(4,1)S(1)} async-done(((s8[7340032]{0:T(1024)(128)(4,1)}), s8[3145728]{0:T(1024)(128)(4,1)S(1)}, s32[]{:S(2)}) %slice-start.3) | async-done | bytes 3145752
  78.1 2.5 %fusion.16 = f32[192,1024]{1,0:T(8,128)S(1)} fusion(bf16[192,3584]{1,0:T(8,128)(2,1)S(1)} %get-tuple-element.22, bf16[1024,3584]{1,0:T(8,128)(2,1)S(1)} %bitcast.37), kind=kOutput, calls=%fused_computation.86 | convolution fusion | flops 1409286144 | bytes 9502720 | tf_op jit(solution)/shard_map/dot_general | solution.py:14
  80.6 2.5 %fusion.5 = bf16[192,1024]{1,0:T(8,128)(2,1)S(1)} fusion(f32[192,1024]{1,0:T(8,128)S(1)} %fusion.16, bf16[192,3584]{1,0:T(8,128)(2,1)S(1)} %get-tuple-element.17, bf16[1024,3584]{1,0:T(8,128)(2,1)S(1)} %bitcast.41), kind=kOutput, calls=%fused_computation.19 | convolution fusion | flops 1409679360 | bytes 9895936 | tf_op jit(solution)/shard_map/dot_general | solution.py:14
  83.2 5.2 %convolution_convert_fusion.2 = bf16[1024,3584]{1,0:T(8,128)(2,1)} fusion(bf16[192,1024]{1,0:T(8,128)(2,1)S(1)} %pad_maximum_fusion.1, bf16[192,3584]{1,0:T(8,128)(2,1)S(1)} %get-tuple-element.17), kind=kOutput, calls=%fused_computation.2 | convolution fusion | flops 1412956160 | bytes 9109504 | tf_op jit(solution)/shard_map/dot_general | solution.py:131
  88.4 1.3 %collective-permute-start.31 = (bf16[48,1024]{1,0:T(8,128)(2,1)S(1)}, bf16[48,1024]{1,0:T(8,128)(2,1)S(1)}, u32[]{:S(2)}, u32[]{:S(2)}) collective-permute-start(bf16[48,1024]{1,0:T(8,128)(2,1)S(1)} %get-tuple-element.39), channel_id=1, source_target_pairs={{0,3},{4,7},{8,11},{12,15},{16,19},{20,23},{24,27},{28,31}} | collective-permute-start | bytes 294920 | tf_op jit(solution)/shard_map/ppermute | solution.py:108
  89.7 1.6 %collective-permute-start.30 = (bf16[48,1024]{1,0:T(8,128)(2,1)S(1)}, bf16[48,1024]{1,0:T(8,128)(2,1)S(1)}, u32[]{:S(2)}, u32[]{:S(2)}) collective-permute-start(bf16[48,1024]{1,0:T(8,128)(2,1)S(1)} %get-tuple-element.39), channel_id=1, source_target_pairs={{1,0},{2,1},{3,2},{5,4},{6,5},{7,6},{9,8},{10,9},{11,10},{13,12},{... | collective-permute-start | bytes 294920 | tf_op jit(solution)/shard_map/ppermute | solution.py:107
  91.3 1.3 %collective-permute-start.35 = (bf16[48,1024]{1,0:T(8,128)(2,1)S(1)}, bf16[48,1024]{1,0:T(8,128)(2,1)S(1)}, u32[]{:S(2)}, u32[]{:S(2)}) collective-permute-start(bf16[48,1024]{1,0:T(8,128)(2,1)S(1)} %get-tuple-element.40), channel_id=1, source_target_pairs={{0,1},{1,2},{2,3},{4,5},{5,6},{6,7},{8,9},{9,10},{10,11},{12,13},{... | collective-permute-start | bytes 294920 | tf_op jit(solution)/shard_map/ppermute | solution.py:108
  92.6 9.3 %collective-permute-start.34 = (bf16[48,1024]{1,0:T(8,128)(2,1)S(1)}, bf16[48,1024]{1,0:T(8,128)(2,1)S(1)}, u32[]{:S(2)}, u32[]{:S(2)}) collective-permute-start(bf16[48,1024]{1,0:T(8,128)(2,1)S(1)} %get-tuple-element.40), channel_id=1, source_target_pairs={{3,0},{7,4},{11,8},{15,12},{19,16},{23,20},{27,24},{31,28}} | collective-permute-start | bytes 294920 | tf_op jit(solution)/shard_map/ppermute | solution.py:107
  101.9 1.4 %collective-permute-start.33 = (bf16[48,1024]{1,0:T(8,128)(2,1)S(1)}, bf16[48,1024]{1,0:T(8,128)(2,1)S(1)}, u32[]{:S(2)}, u32[]{:S(2)}) collective-permute-start(bf16[48,1024]{1,0:T(8,128)(2,1)S(1)} %get-tuple-element.41), channel_id=1, source_target_pairs={{0,2},{1,3},{4,6},{5,7},{8,10},{9,11},{12,14},{13,15},{16,18},{17,... | collective-permute-start | bytes 294920 | tf_op jit(solution)/shard_map/ppermute | solution.py:108
  103.3 5.2 %convolution_convert_fusion.1 = bf16[1024,3584]{1,0:T(8,128)(2,1)} fusion(bf16[192,1024]{1,0:T(8,128)(2,1)S(1)} %pad_maximum_fusion.1, bf16[192,3584]{1,0:T(8,128)(2,1)S(1)} %get-tuple-element.22), kind=kOutput, calls=%fused_computation.1 | convolution fusion | flops 1412956160 | bytes 9109504 | tf_op jit(solution)/shard_map/dot_general | solution.py:134
  108.5 5.4 %collective-permute-start.32 = (bf16[48,1024]{1,0:T(8,128)(2,1)S(1)}, bf16[48,1024]{1,0:T(8,128)(2,1)S(1)}, u32[]{:S(2)}, u32[]{:S(2)}) collective-permute-start(bf16[48,1024]{1,0:T(8,128)(2,1)S(1)} %get-tuple-element.41), channel_id=1, source_target_pairs={{2,0},{3,1},{6,4},{7,5},{10,8},{11,9},{14,12},{15,13},{18,16},{19,... | collective-permute-start | bytes 294920 | tf_op jit(solution)/shard_map/ppermute | solution.py:107
  114.0 5.2 %convolution_convert_fusion = bf16[3584,1024]{1,0:T(8,128)(2,1)} fusion(bf16[192,3584]{1,0:T(8,128)(2,1)S(1)} %get-tuple-element.23, bf16[192,1024]{1,0:T(8,128)(2,1)S(1)} %copy-done.1), kind=kOutput, calls=%fused_computation | convolution fusion | flops 1412956160 | bytes 9109504 | tf_op jit(solution)/shard_map/dot_general | solution.py:8
  119.2 0.7 add_convert_fusion.12
  (93 shorter events, 2.3 us)
Async XLA Ops:
  0.6 9.9 %collective-permute-start.1 = (bf16[48,1024]{1,0:T(8,128)(2,1)}, bf16[48,1024]{1,0:T(8,128)(2,1)S(1)}, u32[]{:S(2)}, u32[]{:S(2)}) collective-permute-start(bf16[48,1024]{1,0:T(8,128)(2,1)} %param.5), channel_id=1, source_target_pairs={{0,2},{1,3},{2,0},{3,1},{4,6},{5,7},{6,4},{7,5},{8,10},{9,11},{10,... | collective-permute-start | bytes 294920 | tf_op jit(solution)/shard_map/ppermute | solution.py:98
  1.0 9.5 %collective-permute-start = (bf16[48,1024]{1,0:T(8,128)(2,1)}, bf16[48,1024]{1,0:T(8,128)(2,1)S(1)}, u32[]{:S(2)}, u32[]{:S(2)}) collective-permute-start(bf16[48,1024]{1,0:T(8,128)(2,1)} %param.5), channel_id=1, source_target_pairs={{0,1},{1,2},{2,3},{3,0},{4,5},{5,6},{6,7},{7,4},{8,9},{9,10},{10,1... | collective-permute-start | bytes 294920 | tf_op jit(solution)/shard_map/ppermute | solution.py:98
  3.5 7.0 %collective-permute-start.2 = (bf16[48,1024]{1,0:T(8,128)(2,1)}, bf16[48,1024]{1,0:T(8,128)(2,1)S(1)}, u32[]{:S(2)}, u32[]{:S(2)}) collective-permute-start(bf16[48,1024]{1,0:T(8,128)(2,1)} %param.5), channel_id=1, source_target_pairs={{0,3},{1,0},{2,1},{3,2},{4,7},{5,4},{6,5},{7,6},{8,11},{9,8},{10,9... | collective-permute-start | bytes 294920 | tf_op jit(solution)/shard_map/ppermute | solution.py:98
  10.5 11.6 %slice-start.4 = ((s8[7340032]{0:T(1024)(128)(4,1)}), s8[4194304]{0:T(1024)(128)(4,1)S(1)}, s32[]{:S(2)}) async-start(s8[7340032]{0:T(1024)(128)(4,1)} %bitcast.38), calls=%async_computation.4 | async-start | bytes 8388608
  11.6 10.5 %slice-start.5 = ((s8[7340032]{0:T(1024)(128)(4,1)}), s8[3145728]{0:T(1024)(128)(4,1)S(1)}, s32[]{:S(2)}) async-start(s8[7340032]{0:T(1024)(128)(4,1)} %bitcast.38), calls=%async_computation.5 | async-start | bytes 6291456
  11.6 13.8 %collective-permute-start.11 = (bf16[48,1024]{1,0:T(8,128)(2,1)}, bf16[48,1024]{1,0:T(8,128)(2,1)S(1)}, u32[]{:S(2)}, u32[]{:S(2)}) collective-permute-start(bf16[48,1024]{1,0:T(8,128)(2,1)} %param.6), channel_id=1, source_target_pairs={{0,3},{1,0},{2,1},{3,2},{4,7},{5,4},{6,5},{7,6},{8,11},{9,8},{10,9... | collective-permute-start | bytes 294920 | tf_op jit(solution)/shard_map/ppermute | solution.py:98
  14.3 10.6 %collective-permute-start.10 = (bf16[48,1024]{1,0:T(8,128)(2,1)}, bf16[48,1024]{1,0:T(8,128)(2,1)S(1)}, u32[]{:S(2)}, u32[]{:S(2)}) collective-permute-start(bf16[48,1024]{1,0:T(8,128)(2,1)} %param.6), channel_id=1, source_target_pairs={{0,2},{1,3},{2,0},{3,1},{4,6},{5,7},{6,4},{7,5},{8,10},{9,11},{10,... | collective-permute-start | bytes 294920 | tf_op jit(solution)/shard_map/ppermute | solution.py:98
  14.3 10.5 %collective-permute-start.9 = (bf16[48,1024]{1,0:T(8,128)(2,1)}, bf16[48,1024]{1,0:T(8,128)(2,1)S(1)}, u32[]{:S(2)}, u32[]{:S(2)}) collective-permute-start(bf16[48,1024]{1,0:T(8,128)(2,1)} %param.6), channel_id=1, source_target_pairs={{0,1},{1,2},{2,3},{3,0},{4,5},{5,6},{6,7},{7,4},{8,9},{9,10},{10,1... | collective-permute-start | bytes 294920 | tf_op jit(solution)/shard_map/ppermute | solution.py:98
  21.5 3.9 %slice-start = ((s8[7340032]{0:T(1024)(128)(4,1)}), s8[4194304]{0:T(1024)(128)(4,1)S(1)}, s32[]{:S(2)}) async-start(s8[7340032]{0:T(1024)(128)(4,1)} %bitcast.34), calls=%async_computation | async-start | bytes 8388608
  21.6 3.9 %slice-start.1 = ((s8[7340032]{0:T(1024)(128)(4,1)}), s8[3145728]{0:T(1024)(128)(4,1)S(1)}, s32[]{:S(2)}) async-start(s8[7340032]{0:T(1024)(128)(4,1)} %bitcast.34), calls=%async_computation.1 | async-start | bytes 6291456
  21.6 6.7 %collective-permute-start.6 = (bf16[96,1792]{1,0:T(8,128)(2,1)S(1)}, bf16[96,1792]{1,0:T(8,128)(2,1)S(1)}, u32[]{:S(2)}, u32[]{:S(2)}) collective-permute-start(bf16[96,1792]{1,0:T(8,128)(2,1)S(1)} %constant_dynamic-slice_fusion.14), channel_id=1, source_target_pairs={{0,4},{4,0},{8,12},{12,8},{16,20},{20,16},{24,28},{28,24},{1,5},{5... | collective-permute-start | bytes 1032200 | tf_op jit(solution)/shard_map/ppermute | solution.py:39
  21.7 7.3 %collective-permute-start.21 = (bf16[96,1792]{1,0:T(8,128)(2,1)S(1)}, bf16[96,1792]{1,0:T(8,128)(2,1)S(1)}, u32[]{:S(2)}, u32[]{:S(2)}) collective-permute-start(bf16[96,1792]{1,0:T(8,128)(2,1)S(1)} %constant_dynamic-slice_fusion.5), channel_id=1, source_target_pairs={{0,4},{4,0},{8,12},{12,8},{16,20},{20,16},{24,28},{28,24},{1,5},{5... | collective-permute-start | bytes 1032200 | tf_op jit(solution)/shard_map/ppermute | solution.py:39
  23.8 0.9 copy-start.2
  24.7 5.9 %collective-permute-start.3 = (bf16[96,1792]{1,0:T(8,128)(2,1)S(1)}, bf16[96,1792]{1,0:T(8,128)(2,1)S(1)}, u32[]{:S(2)}, u32[]{:S(2)}) collective-permute-start(bf16[96,1792]{1,0:T(8,128)(2,1)S(1)} %constant_dynamic-slice_fusion.17), channel_id=1, source_target_pairs={{0,4},{4,0},{8,12},{12,8},{16,20},{20,16},{24,28},{28,24},{1,5},{5... | collective-permute-start | bytes 1032200 | tf_op jit(solution)/shard_map/ppermute | solution.py:39
  24.9 7.5 %collective-permute-start.18 = (bf16[96,1792]{1,0:T(8,128)(2,1)S(1)}, bf16[96,1792]{1,0:T(8,128)(2,1)S(1)}, u32[]{:S(2)}, u32[]{:S(2)}) collective-permute-start(bf16[96,1792]{1,0:T(8,128)(2,1)S(1)} %constant_dynamic-slice_fusion.8), channel_id=1, source_target_pairs={{0,4},{4,0},{8,12},{12,8},{16,20},{20,16},{24,28},{28,24},{1,5},{5... | collective-permute-start | bytes 1032200 | tf_op jit(solution)/shard_map/ppermute | solution.py:39
  25.4 2.6 %copy-start = (bf16[192,1024]{1,0:T(8,128)(2,1)}, bf16[192,1024]{1,0:T(8,128)(2,1)S(1)}, u32[]{:S(2)}) copy-start(bf16[192,1024]{1,0:T(8,128)(2,1)S(1)} %constant_dynamic-update-slice_fusion) | copy-start | bytes 1179652
  28.2 4.9 %collective-permute-start.12 = (bf16[96,1792]{1,0:T(8,128)(2,1)S(1)}, bf16[96,1792]{1,0:T(8,128)(2,1)S(1)}, u32[]{:S(2)}, u32[]{:S(2)}) collective-permute-start(bf16[96,1792]{1,0:T(8,128)(2,1)S(1)} %constant_dynamic-slice_fusion.11), channel_id=1, source_target_pairs={{0,4},{4,0},{8,12},{12,8},{16,20},{20,16},{24,28},{28,24},{1,5},{5... | collective-permute-start | bytes 1032200 | tf_op jit(solution)/shard_map/ppermute | solution.py:39
  28.3 5.5 %collective-permute-start.24 = (bf16[96,1792]{1,0:T(8,128)(2,1)S(1)}, bf16[96,1792]{1,0:T(8,128)(2,1)S(1)}, u32[]{:S(2)}, u32[]{:S(2)}) collective-permute-start(bf16[96,1792]{1,0:T(8,128)(2,1)S(1)} %constant_dynamic-slice_fusion.2), channel_id=1, source_target_pairs={{0,4},{4,0},{8,12},{12,8},{16,20},{20,16},{24,28},{28,24},{1,5},{5... | collective-permute-start | bytes 1032200 | tf_op jit(solution)/shard_map/ppermute | solution.py:39
  29.0 7.3 %collective-permute-start.7 = (bf16[48,1792]{1,0:T(8,128)(2,1)S(1)}, bf16[48,1792]{1,0:T(8,128)(2,1)S(1)}, u32[]{:S(2)}, u32[]{:S(2)}) collective-permute-start(bf16[48,1792]{1,0:T(8,128)(2,1)S(1)} %constant_dynamic-slice_fusion.13), channel_id=1, source_target_pairs={{0,8},{4,12},{8,0},{12,4},{16,24},{20,28},{24,16},{28,20},{1,9},{5... | collective-permute-start | bytes 516104 | tf_op jit(solution)/shard_map/ppermute | solution.py:39
  30.6 7.3 %collective-permute-start.22 = (bf16[48,1792]{1,0:T(8,128)(2,1)S(1)}, bf16[48,1792]{1,0:T(8,128)(2,1)S(1)}, u32[]{:S(2)}, u32[]{:S(2)}) collective-permute-start(bf16[48,1792]{1,0:T(8,128)(2,1)S(1)} %constant_dynamic-slice_fusion.4), channel_id=1, source_target_pairs={{0,16},{4,20},{8,24},{12,28},{16,0},{20,4},{24,8},{28,12},{1,17},{... | collective-permute-start | bytes 516104 | tf_op jit(solution)/shard_map/ppermute | solution.py:39
  32.4 7.5 %collective-permute-start.4 = (bf16[48,1792]{1,0:T(8,128)(2,1)S(1)}, bf16[48,1792]{1,0:T(8,128)(2,1)S(1)}, u32[]{:S(2)}, u32[]{:S(2)}) collective-permute-start(bf16[48,1792]{1,0:T(8,128)(2,1)S(1)} %constant_dynamic-slice_fusion.16), channel_id=1, source_target_pairs={{0,8},{4,12},{8,0},{12,4},{16,24},{20,28},{24,16},{28,20},{1,9},{5... | collective-permute-start | bytes 516104 | tf_op jit(solution)/shard_map/ppermute | solution.py:39
  33.1 8.6 %collective-permute-start.19 = (bf16[48,1792]{1,0:T(8,128)(2,1)S(1)}, bf16[48,1792]{1,0:T(8,128)(2,1)S(1)}, u32[]{:S(2)}, u32[]{:S(2)}) collective-permute-start(bf16[48,1792]{1,0:T(8,128)(2,1)S(1)} %constant_dynamic-slice_fusion.7), channel_id=1, source_target_pairs={{0,16},{4,20},{8,24},{12,28},{16,0},{20,4},{24,8},{28,12},{1,17},{... | collective-permute-start | bytes 516104 | tf_op jit(solution)/shard_map/ppermute | solution.py:39
  33.8 9.8 %collective-permute-start.13 = (bf16[48,1792]{1,0:T(8,128)(2,1)S(1)}, bf16[48,1792]{1,0:T(8,128)(2,1)S(1)}, u32[]{:S(2)}, u32[]{:S(2)}) collective-permute-start(bf16[48,1792]{1,0:T(8,128)(2,1)S(1)} %constant_dynamic-slice_fusion.10), channel_id=1, source_target_pairs={{0,8},{4,12},{8,0},{12,4},{16,24},{20,28},{24,16},{28,20},{1,9},{5... | collective-permute-start | bytes 516104 | tf_op jit(solution)/shard_map/ppermute | solution.py:39
  36.2 9.1 %collective-permute-start.25 = (bf16[48,1792]{1,0:T(8,128)(2,1)S(1)}, bf16[48,1792]{1,0:T(8,128)(2,1)S(1)}, u32[]{:S(2)}, u32[]{:S(2)}) collective-permute-start(bf16[48,1792]{1,0:T(8,128)(2,1)S(1)} %constant_dynamic-slice_fusion.1), channel_id=1, source_target_pairs={{0,16},{4,20},{8,24},{12,28},{16,0},{20,4},{24,8},{28,12},{1,17},{... | collective-permute-start | bytes 516104 | tf_op jit(solution)/shard_map/ppermute | solution.py:39
  37.9 9.2 %collective-permute-start.8 = (bf16[24,1792]{1,0:T(8,128)(2,1)S(1)}, bf16[24,1792]{1,0:T(8,128)(2,1)S(1)}, u32[]{:S(2)}, u32[]{:S(2)}) collective-permute-start(bf16[24,1792]{1,0:T(8,128)(2,1)S(1)} %constant_dynamic-slice_fusion.12), channel_id=1, source_target_pairs={{0,16},{4,20},{8,24},{12,28},{16,0},{20,4},{24,8},{28,12},{1,17},{... | collective-permute-start | bytes 258056 | tf_op jit(solution)/shard_map/ppermute | solution.py:39
  39.9 11.7 %collective-permute-start.23 = (bf16[24,1792]{1,0:T(8,128)(2,1)S(1)}, bf16[24,1792]{1,0:T(8,128)(2,1)S(1)}, u32[]{:S(2)}, u32[]{:S(2)}) collective-permute-start(bf16[24,1792]{1,0:T(8,128)(2,1)S(1)} %constant_dynamic-slice_fusion.3), channel_id=1, source_target_pairs={{0,8},{4,12},{8,0},{12,4},{16,24},{20,28},{24,16},{28,20},{1,9},{5... | collective-permute-start | bytes 258056 | tf_op jit(solution)/shard_map/ppermute | solution.py:39
  41.6 7.1 %collective-permute-start.5 = (bf16[24,1792]{1,0:T(8,128)(2,1)S(1)}, bf16[24,1792]{1,0:T(8,128)(2,1)S(1)}, u32[]{:S(2)}, u32[]{:S(2)}) collective-permute-start(bf16[24,1792]{1,0:T(8,128)(2,1)S(1)} %constant_dynamic-slice_fusion.15), channel_id=1, source_target_pairs={{0,16},{4,20},{8,24},{12,28},{16,0},{20,4},{24,8},{28,12},{1,17},{... | collective-permute-start | bytes 258056 | tf_op jit(solution)/shard_map/ppermute | solution.py:39
  43.6 8.0 %collective-permute-start.20 = (bf16[24,1792]{1,0:T(8,128)(2,1)S(1)}, bf16[24,1792]{1,0:T(8,128)(2,1)S(1)}, u32[]{:S(2)}, u32[]{:S(2)}) collective-permute-start(bf16[24,1792]{1,0:T(8,128)(2,1)S(1)} %constant_dynamic-slice_fusion.6), channel_id=1, source_target_pairs={{0,8},{4,12},{8,0},{12,4},{16,24},{20,28},{24,16},{28,20},{1,9},{5... | collective-permute-start | bytes 258056 | tf_op jit(solution)/shard_map/ppermute | solution.py:39
  45.3 4.5 %collective-permute-start.14 = (bf16[24,1792]{1,0:T(8,128)(2,1)S(1)}, bf16[24,1792]{1,0:T(8,128)(2,1)S(1)}, u32[]{:S(2)}, u32[]{:S(2)}) collective-permute-start(bf16[24,1792]{1,0:T(8,128)(2,1)S(1)} %constant_dynamic-slice_fusion.9), channel_id=1, source_target_pairs={{0,16},{4,20},{8,24},{12,28},{16,0},{20,4},{24,8},{28,12},{1,17},{... | collective-permute-start | bytes 258056 | tf_op jit(solution)/shard_map/ppermute | solution.py:39
  47.2 4.5 %collective-permute-start.26 = (bf16[24,1792]{1,0:T(8,128)(2,1)S(1)}, bf16[24,1792]{1,0:T(8,128)(2,1)S(1)}, u32[]{:S(2)}, u32[]{:S(2)}) collective-permute-start(bf16[24,1792]{1,0:T(8,128)(2,1)S(1)} %constant_dynamic-slice_fusion), channel_id=1, source_target_pairs={{0,8},{4,12},{8,0},{12,4},{16,24},{20,28},{24,16},{28,20},{1,9},{5... | collective-permute-start | bytes 258056 | tf_op jit(solution)/shard_map/ppermute | solution.py:39
  50.0 7.0 %collective-permute-start.15 = (bf16[3,24,1792]{2,1,0:T(8,128)(2,1)S(1)}, bf16[3,24,1792]{2,1,0:T(8,128)(2,1)S(1)}, u32[]{:S(2)}, u32[]{:S(2)}) collective-permute-start(bf16[3,24,1792]{2,1,0:T(8,128)(2,1)S(1)} %pad_maximum_fusion.2), channel_id=1, source_target_pairs={{0,16},{4,20},{8,24},{12,28},{16,0},{20,4},{24,8},{28,12},{1,17},{... | collective-permute-start | bytes 774152 | tf_op jit(solution)/shard_map/ppermute | solution.py:67
  51.8 7.4 %collective-permute-start.27 = (bf16[3,24,1792]{2,1,0:T(8,128)(2,1)S(1)}, bf16[3,24,1792]{2,1,0:T(8,128)(2,1)S(1)}, u32[]{:S(2)}, u32[]{:S(2)}) collective-permute-start(bf16[3,24,1792]{2,1,0:T(8,128)(2,1)S(1)} %pad_maximum_fusion.3), channel_id=1, source_target_pairs={{0,8},{4,12},{8,0},{12,4},{16,24},{20,28},{24,16},{28,20},{1,9},{5... | collective-permute-start | bytes 774152 | tf_op jit(solution)/shard_map/ppermute | solution.py:67
  57.1 12.4 %collective-permute-start.16 = (bf16[3,48,1792]{2,1,0:T(8,128)(2,1)S(1)}, bf16[3,48,1792]{2,1,0:T(8,128)(2,1)S(1)}, u32[]{:S(2)}, u32[]{:S(2)}) collective-permute-start(bf16[3,48,1792]{2,1,0:T(8,128)(2,1)S(1)} %maximum_select_fusion.4), channel_id=1, source_target_pairs={{0,8},{4,12},{8,0},{12,4},{16,24},{20,28},{24,16},{28,20},{1,9},{5... | collective-permute-start | bytes 1548296 | tf_op jit(solution)/shard_map/ppermute | solution.py:67
  59.3 10.6 %collective-permute-start.28 = (bf16[3,48,1792]{2,1,0:T(8,128)(2,1)S(1)}, bf16[3,48,1792]{2,1,0:T(8,128)(2,1)S(1)}, u32[]{:S(2)}, u32[]{:S(2)}) collective-permute-start(bf16[3,48,1792]{2,1,0:T(8,128)(2,1)S(1)} %maximum_select_fusion.5), channel_id=1, source_target_pairs={{0,16},{4,20},{8,24},{12,28},{16,0},{20,4},{24,8},{28,12},{1,17},{... | collective-permute-start | bytes 1548296 | tf_op jit(solution)/shard_map/ppermute | solution.py:67
  69.8 2.7 %collective-permute-start.17 = (bf16[3,96,1792]{2,1,0:T(8,128)(2,1)S(1)}, bf16[3,96,1792]{2,1,0:T(8,128)(2,1)S(1)}, u32[]{:S(2)}, u32[]{:S(2)}) collective-permute-start(bf16[3,96,1792]{2,1,0:T(8,128)(2,1)S(1)} %maximum_select_fusion.2), channel_id=1, source_target_pairs={{0,4},{4,0},{8,12},{12,8},{16,20},{20,16},{24,28},{28,24},{1,5},{5... | collective-permute-start | bytes 3096584 | tf_op jit(solution)/shard_map/ppermute | solution.py:67
  70.2 3.9 %collective-permute-start.29 = (bf16[3,96,1792]{2,1,0:T(8,128)(2,1)S(1)}, bf16[3,96,1792]{2,1,0:T(8,128)(2,1)}, u32[]{:S(2)}, u32[]{:S(2)}) collective-permute-start(bf16[3,96,1792]{2,1,0:T(8,128)(2,1)S(1)} %maximum_select_fusion.3), channel_id=1, source_target_pairs={{0,4},{4,0},{8,12},{12,8},{16,20},{20,16},{24,28},{28,24},{1,5},{5... | collective-permute-start | bytes 3096584 | tf_op jit(solution)/shard_map/ppermute | solution.py:67
  72.5 4.3 %slice-start.2 = ((s8[7340032]{0:T(1024)(128)(4,1)}), s8[4194304]{0:T(1024)(128)(4,1)S(1)}, s32[]{:S(2)}) async-start(s8[7340032]{0:T(1024)(128)(4,1)} %bitcast.36), calls=%async_computation.2 | async-start | bytes 8388608
  76.2 1.9 %slice-start.3 = ((s8[7340032]{0:T(1024)(128)(4,1)}), s8[3145728]{0:T(1024)(128)(4,1)S(1)}, s32[]{:S(2)}) async-start(s8[7340032]{0:T(1024)(128)(4,1)} %bitcast.36), calls=%async_computation.3 | async-start | bytes 6291456
  76.2 4.4 %slice-start.6 = ((s8[7340032]{0:T(1024)(128)(4,1)}), s8[4194304]{0:T(1024)(128)(4,1)S(1)}, s32[]{:S(2)}) async-start(s8[7340032]{0:T(1024)(128)(4,1)} %bitcast.40), calls=%async_computation.6 | async-start | bytes 8388608
  78.1 2.5 %slice-start.7 = ((s8[7340032]{0:T(1024)(128)(4,1)}), s8[3145728]{0:T(1024)(128)(4,1)S(1)}, s32[]{:S(2)}) async-start(s8[7340032]{0:T(1024)(128)(4,1)} %bitcast.40), calls=%async_computation.7 | async-start | bytes 6291456
  88.4 20.1 %collective-permute-start.31 = (bf16[48,1024]{1,0:T(8,128)(2,1)S(1)}, bf16[48,1024]{1,0:T(8,128)(2,1)S(1)}, u32[]{:S(2)}, u32[]{:S(2)}) collective-permute-start(bf16[48,1024]{1,0:T(8,128)(2,1)S(1)} %get-tuple-element.39), channel_id=1, source_target_pairs={{0,3},{4,7},{8,11},{12,15},{16,19},{20,23},{24,27},{28,31}} | collective-permute-start | bytes 294920 | tf_op jit(solution)/shard_map/ppermute | solution.py:108
  89.7 29.5 %collective-permute-start.30 = (bf16[48,1024]{1,0:T(8,128)(2,1)S(1)}, bf16[48,1024]{1,0:T(8,128)(2,1)S(1)}, u32[]{:S(2)}, u32[]{:S(2)}) collective-permute-start(bf16[48,1024]{1,0:T(8,128)(2,1)S(1)} %get-tuple-element.39), channel_id=1, source_target_pairs={{1,0},{2,1},{3,2},{5,4},{6,5},{7,6},{9,8},{10,9},{11,10},{13,12},{... | collective-permute-start | bytes 294920 | tf_op jit(solution)/shard_map/ppermute | solution.py:107
  91.3 27.9 %collective-permute-start.35 = (bf16[48,1024]{1,0:T(8,128)(2,1)S(1)}, bf16[48,1024]{1,0:T(8,128)(2,1)S(1)}, u32[]{:S(2)}, u32[]{:S(2)}) collective-permute-start(bf16[48,1024]{1,0:T(8,128)(2,1)S(1)} %get-tuple-element.40), channel_id=1, source_target_pairs={{0,1},{1,2},{2,3},{4,5},{5,6},{6,7},{8,9},{9,10},{10,11},{12,13},{... | collective-permute-start | bytes 294920 | tf_op jit(solution)/shard_map/ppermute | solution.py:108
  92.6 26.6 %collective-permute-start.34 = (bf16[48,1024]{1,0:T(8,128)(2,1)S(1)}, bf16[48,1024]{1,0:T(8,128)(2,1)S(1)}, u32[]{:S(2)}, u32[]{:S(2)}) collective-permute-start(bf16[48,1024]{1,0:T(8,128)(2,1)S(1)} %get-tuple-element.40), channel_id=1, source_target_pairs={{3,0},{7,4},{11,8},{15,12},{19,16},{23,20},{27,24},{31,28}} | collective-permute-start | bytes 294920 | tf_op jit(solution)/shard_map/ppermute | solution.py:107
  101.9 12.1 %copy-start.1 = (bf16[192,1024]{1,0:T(8,128)(2,1)S(1)}, bf16[192,1024]{1,0:T(8,128)(2,1)}, u32[]{:S(2)}) copy-start(bf16[192,1024]{1,0:T(8,128)(2,1)} %copy-done) | copy-start | bytes 1179652
  101.9 17.3 %collective-permute-start.33 = (bf16[48,1024]{1,0:T(8,128)(2,1)S(1)}, bf16[48,1024]{1,0:T(8,128)(2,1)S(1)}, u32[]{:S(2)}, u32[]{:S(2)}) collective-permute-start(bf16[48,1024]{1,0:T(8,128)(2,1)S(1)} %get-tuple-element.41), channel_id=1, source_target_pairs={{0,2},{1,3},{4,6},{5,7},{8,10},{9,11},{12,14},{13,15},{16,18},{17,... | collective-permute-start | bytes 294920 | tf_op jit(solution)/shard_map/ppermute | solution.py:108
  108.5 10.7 %collective-permute-start.32 = (bf16[48,1024]{1,0:T(8,128)(2,1)S(1)}, bf16[48,1024]{1,0:T(8,128)(2,1)S(1)}, u32[]{:S(2)}, u32[]{:S(2)}) collective-permute-start(bf16[48,1024]{1,0:T(8,128)(2,1)S(1)} %get-tuple-element.41), channel_id=1, source_target_pairs={{2,0},{3,1},{6,4},{7,5},{10,8},{11,9},{14,12},{15,13},{18,16},{19,... | collective-permute-start | bytes 294920 | tf_op jit(solution)/shard_map/ppermute | solution.py:107

commit v18 on v16

--- a/solution.py
+++ b/solution.py
@@ -112,7 +112,6 @@
     n_row = lax.psum(1, "row")
     n_col = lax.psum(1, "col")
     tok_all = col_gather(tokens, n_col)
-    grad_out, tok_all = lax.optimization_barrier((grad_out, tok_all))
     grad_all = col_gather(grad_out, n_col)
     tok_t = tok_all.T
     stacked = [

time: 106 us -> 115 us (1.085)
  waiting for transfers between devices: 27 us -> 37.3 us
  local copies, waits for them, and re-layouts: 2.8 us -> 4.62 us
  starting transfers between devices: 38.1 us -> 36.4 us
    ppermute x6, waiting for transfers between devices: 4.99 us -> 15.3 us  [col_gather(): lax.ppermute(x, 'col', [(j, (j + s) % n_col) for j in range(n_col)])]
    ppermute x6, starting transfers between devices: 13.2 us -> 8.8 us  [col_gather(): lax.ppermute(x, 'col', [(j, (j + s) % n_col) for j in range(n_col)])]
    dot_general x3, matrix products: 7.59 us -> 10.9 us  [contract_last(): lax.dot_general(left, right, (((1,), (1,)), ((), ())), preferred_element_...]
    dot_general x1, matrix products: 4.67 us -> 1.61 us  [body(): jnp.dot(tok_all, up_weight, preferred_element_type=jnp.float32)]
    ppermute x3, starting transfers between devices: 2.83 us -> 5.63 us  [col_reduce_scatter(): lax.ppermute(x[s * span:(s + 1) * span], 'col', [(j, (j - s) % n_col) for...]
    unnamed x25 -> x26, local copies, waits for them, and re-layouts: 2.09 us -> 3.9 us
  transfers between devices with their start and end apart: 33 -> 33, of which waited for: 17 -> 18; matrix products, arithmetic and copies ran while one was open for 21% -> 21% of each run, Pallas kernels for 0% -> 0%
where the time goes in v18:
time: 115 us
  waiting for transfers between devices  37.3 us (32%)
  starting transfers between devices  36.4 us (32%)
  matrix products  29.6 us (26%)
  other arithmetic  5.92 us (5%)
  local copies, waits for them, and re-layouts  4.62 us (4%)
  between operations  1.17 us (1%)
    ppermute x6, waiting for transfers between devices, doubling_gather(): got = lax.ppermute(cur, 'row', [(j, j ^ bit) for j in range(n_dev)])  17.6 us
    ppermute x18, starting transfers between devices, halving_reduce(): lax.ppermute(lax.dynamic_slice_in_dim(c, (1 - hi) * n, n, 0), 'row', perm)  17.2 us
    ppermute x6, waiting for transfers between devices, col_gather(): lax.ppermute(x, 'col', [(j, (j + s) % n_col) for j in range(n_col)])  15.3 us
    dot_general x3, matrix products, contract_last(): lax.dot_general(left, right, (((1,), (1,)), ((), ())), preferred_element_...  10.9 us
    ppermute x6, starting transfers between devices, col_gather(): lax.ppermute(x, 'col', [(j, (j + s) % n_col) for j in range(n_col)])  8.8 us
    ppermute x3, starting transfers between devices, col_reduce_scatter(): lax.ppermute(x[s * span:(s + 1) * span], 'col', [(j, (j - s) % n_col) for...  5.63 us
    dot_general x1, matrix products, contract_first(): lax.dot_general(left, right, (((0,), (0,)), ((), ())), preferred_element_...  5.19 us
    dot_general x1, matrix products, body(): jnp.dot(tok_t, grad_gate, preferred_element_type=jnp.float32)  5.18 us
  transfers between devices with their start and end apart: 33, of which 18 were waited for; matrix products, arithmetic and copies ran while one was open for 21% of the time, Pallas kernels for 0%

profile of v18, /device:TPU:0, one launch (start us, length us, event | category | flops | bytes accessed | tf_op | source)
XLA Modules:
  0.0 115.1 jit_solution(16009540311874556757)
XLA Ops:
  0.6 4.1 %collective-permute-start.1 = (bf16[48,1024]{1,0:T(8,128)(2,1)}, bf16[48,1024]{1,0:T(8,128)(2,1)S(1)}, u32[]{:S(2)}, u32[]{:S(2)}) collective-permute-start(bf16[48,1024]{1,0:T(8,128)(2,1)} %param.5), channel_id=1, source_target_pairs={{0,2},{1,3},{2,0},{3,1},{4,6},{5,7},{6,4},{7,5},{8,10},{9,11},{10,... | collective-permute-start | bytes 294920 | tf_op jit(solution)/shard_map/ppermute | solution.py:98
  4.8 1.6 %collective-permute-start = (bf16[48,1024]{1,0:T(8,128)(2,1)}, bf16[48,1024]{1,0:T(8,128)(2,1)S(1)}, u32[]{:S(2)}, u32[]{:S(2)}) collective-permute-start(bf16[48,1024]{1,0:T(8,128)(2,1)} %param.5), channel_id=1, source_target_pairs={{0,1},{1,2},{2,3},{3,0},{4,5},{5,6},{6,7},{7,4},{8,9},{9,10},{10,1... | collective-permute-start | bytes 294920 | tf_op jit(solution)/shard_map/ppermute | solution.py:98
  6.3 2.2 %collective-permute-start.2 = (bf16[48,1024]{1,0:T(8,128)(2,1)}, bf16[48,1024]{1,0:T(8,128)(2,1)S(1)}, u32[]{:S(2)}, u32[]{:S(2)}) collective-permute-start(bf16[48,1024]{1,0:T(8,128)(2,1)} %param.5), channel_id=1, source_target_pairs={{0,3},{1,0},{2,1},{3,2},{4,7},{5,4},{6,5},{7,6},{8,11},{9,8},{10,9... | collective-permute-start | bytes 294920 | tf_op jit(solution)/shard_map/ppermute | solution.py:98
  8.6 0.6 collective-permute-start.9
  9.2 0.9 constant_dynamic-update-slice_fusion.3
  10.1 0.9 constant_dynamic-update-slice_fusion.7
  11.0 6.4 %collective-permute-done.9 = bf16[48,1024]{1,0:T(8,128)(2,1)S(1)} collective-permute-done((bf16[48,1024]{1,0:T(8,128)(2,1)}, bf16[48,1024]{1,0:T(8,128)(2,1)S(1)}, u32[]{:S(2)}, u32[]{:S(2)}) %collective-permute-start.9) | collective-permute-done | bytes 98336 | tf_op jit(solution)/shard_map/ppermute | solution.py:98
  17.3 0.3 collective-permute-start.11
  17.6 2.8 %collective-permute-done.10 = bf16[48,1024]{1,0:T(8,128)(2,1)S(1)} collective-permute-done((bf16[48,1024]{1,0:T(8,128)(2,1)}, bf16[48,1024]{1,0:T(8,128)(2,1)S(1)}, u32[]{:S(2)}, u32[]{:S(2)}) %collective-permute-start.10) | collective-permute-done | bytes 98336 | tf_op jit(solution)/shard_map/ppermute | solution.py:98
  20.5 6.1 %collective-permute-done.11 = bf16[48,1024]{1,0:T(8,128)(2,1)S(1)} collective-permute-done((bf16[48,1024]{1,0:T(8,128)(2,1)}, bf16[48,1024]{1,0:T(8,128)(2,1)S(1)}, u32[]{:S(2)}, u32[]{:S(2)}) %collective-permute-start.11) | collective-permute-done | bytes 98336 | tf_op jit(solution)/shard_map/ppermute | solution.py:98
  26.6 5.8 %convolution_convert_fusion.3 = bf16[192,3584]{1,0:T(8,128)(2,1)S(1)} fusion(bf16[192,1024]{1,0:T(8,128)(2,1)S(1)} %constant_dynamic-update-slice_fusion.4, bf16[3584,1024]{1,0:T(8,128)(2,1)} %param.9), kind=kOutput, calls=%fused_computation.3 | convolution fusion | flops 1409974272 | bytes 9109504 | tf_op jit(solution)/shard_map/dot_general | solution.py:14
  32.7 0.5 collective-permute-start.24
  33.3 1.6 %convolution_convert_fusion.4 = bf16[192,3584]{1,0:T(8,128)(2,1)S(1)} fusion(bf16[192,1024]{1,0:T(8,128)(2,1)S(1)} %constant_dynamic-update-slice_fusion, bf16[1024,3584]{1,0:T(8,128)(2,1)S(1)} %bitcast.35), kind=kOutput, calls=%fused_computation.4 | convolution fusion | flops 1409974272 | bytes 9109504 | tf_op jit(solution)/shard_map/dot_general | solution.py:119
  35.1 0.1 collective-permute-start.6
  35.2 0.4 collective-permute-start.21
  35.7 0.7 slice-done.5
  36.4 1.6 %convolution_convert_fusion.5 = bf16[192,3584]{1,0:T(8,128)(2,1)S(1)} fusion(bf16[192,1024]{1,0:T(8,128)(2,1)S(1)} %constant_dynamic-update-slice_fusion, bf16[1024,3584]{1,0:T(8,128)(2,1)S(1)} %bitcast.39), kind=kOutput, calls=%fused_computation.5 | convolution fusion | flops 1409974272 | bytes 9109504 | tf_op jit(solution)/shard_map/dot_general | solution.py:118
  38.2 0.1 collective-permute-start.3
  38.3 0.5 collective-permute-start.18
  39.0 1.6 %collective-permute-start.13 = (bf16[48,1792]{1,0:T(8,128)(2,1)S(1)}, bf16[48,1792]{1,0:T(8,128)(2,1)S(1)}, u32[]{:S(2)}, u32[]{:S(2)}) collective-permute-start(bf16[48,1792]{1,0:T(8,128)(2,1)S(1)} %constant_dynamic-slice_fusion.10), channel_id=1, source_target_pairs={{0,8},{4,12},{8,0},{12,4},{16,24},{20,28},{24,16},{28,20},{1,9},{5... | collective-permute-start | bytes 516104 | tf_op jit(solution)/shard_map/ppermute | solution.py:39
  40.7 1.6 %collective-permute-start.25 = (bf16[48,1792]{1,0:T(8,128)(2,1)S(1)}, bf16[48,1792]{1,0:T(8,128)(2,1)S(1)}, u32[]{:S(2)}, u32[]{:S(2)}) collective-permute-start(bf16[48,1792]{1,0:T(8,128)(2,1)S(1)} %constant_dynamic-slice_fusion.1), channel_id=1, source_target_pairs={{0,16},{4,20},{8,24},{12,28},{16,0},{20,4},{24,8},{28,12},{1,17},{... | collective-permute-start | bytes 516104 | tf_op jit(solution)/shard_map/ppermute | solution.py:39
  42.4 0.6 collective-permute-start.7
  43.1 0.6 collective-permute-start.22
  43.8 1.6 %collective-permute-start.4 = (bf16[48,1792]{1,0:T(8,128)(2,1)S(1)}, bf16[48,1792]{1,0:T(8,128)(2,1)S(1)}, u32[]{:S(2)}, u32[]{:S(2)}) collective-permute-start(bf16[48,1792]{1,0:T(8,128)(2,1)S(1)} %constant_dynamic-slice_fusion.16), channel_id=1, source_target_pairs={{0,8},{4,12},{8,0},{12,4},{16,24},{20,28},{24,16},{28,20},{1,9},{5... | collective-permute-start | bytes 516104 | tf_op jit(solution)/shard_map/ppermute | solution.py:39
  45.5 0.8 collective-permute-done.13
  46.2 1.6 %collective-permute-start.19 = (bf16[48,1792]{1,0:T(8,128)(2,1)S(1)}, bf16[48,1792]{1,0:T(8,128)(2,1)S(1)}, u32[]{:S(2)}, u32[]{:S(2)}) collective-permute-start(bf16[48,1792]{1,0:T(8,128)(2,1)S(1)} %constant_dynamic-slice_fusion.7), channel_id=1, source_target_pairs={{0,16},{4,20},{8,24},{12,28},{16,0},{20,4},{24,8},{28,12},{1,17},{... | collective-permute-start | bytes 516104 | tf_op jit(solution)/shard_map/ppermute | solution.py:39
  48.0 1.5 %collective-permute-start.14 = (bf16[24,1792]{1,0:T(8,128)(2,1)S(1)}, bf16[24,1792]{1,0:T(8,128)(2,1)S(1)}, u32[]{:S(2)}, u32[]{:S(2)}) collective-permute-start(bf16[24,1792]{1,0:T(8,128)(2,1)S(1)} %constant_dynamic-slice_fusion.9), channel_id=1, source_target_pairs={{0,16},{4,20},{8,24},{12,28},{16,0},{20,4},{24,8},{28,12},{1,17},{... | collective-permute-start | bytes 258056 | tf_op jit(solution)/shard_map/ppermute | solution.py:39
  49.6 0.4 collective-permute-done.7
  49.9 1.6 %collective-permute-start.26 = (bf16[24,1792]{1,0:T(8,128)(2,1)S(1)}, bf16[24,1792]{1,0:T(8,128)(2,1)S(1)}, u32[]{:S(2)}, u32[]{:S(2)}) collective-permute-start(bf16[24,1792]{1,0:T(8,128)(2,1)S(1)} %constant_dynamic-slice_fusion), channel_id=1, source_target_pairs={{0,8},{4,12},{8,0},{12,4},{16,24},{20,28},{24,16},{28,20},{1,9},{5... | collective-permute-start | bytes 258056 | tf_op jit(solution)/shard_map/ppermute | solution.py:39
  51.5 0.1 collective-permute-done.22
  51.7 1.5 %collective-permute-start.8 = (bf16[24,1792]{1,0:T(8,128)(2,1)S(1)}, bf16[24,1792]{1,0:T(8,128)(2,1)S(1)}, u32[]{:S(2)}, u32[]{:S(2)}) collective-permute-start(bf16[24,1792]{1,0:T(8,128)(2,1)S(1)} %constant_dynamic-slice_fusion.12), channel_id=1, source_target_pairs={{0,16},{4,20},{8,24},{12,28},{16,0},{20,4},{24,8},{28,12},{1,17},{... | collective-permute-start | bytes 258056 | tf_op jit(solution)/shard_map/ppermute | solution.py:39
  53.2 0.4 collective-permute-done.4
  53.6 1.5 %collective-permute-start.23 = (bf16[24,1792]{1,0:T(8,128)(2,1)S(1)}, bf16[24,1792]{1,0:T(8,128)(2,1)S(1)}, u32[]{:S(2)}, u32[]{:S(2)}) collective-permute-start(bf16[24,1792]{1,0:T(8,128)(2,1)S(1)} %constant_dynamic-slice_fusion.3), channel_id=1, source_target_pairs={{0,8},{4,12},{8,0},{12,4},{16,24},{20,28},{24,16},{28,20},{1,9},{5... | collective-permute-start | bytes 258056 | tf_op jit(solution)/shard_map/ppermute | solution.py:39
  55.3 1.5 %collective-permute-start.5 = (bf16[24,1792]{1,0:T(8,128)(2,1)S(1)}, bf16[24,1792]{1,0:T(8,128)(2,1)S(1)}, u32[]{:S(2)}, u32[]{:S(2)}) collective-permute-start(bf16[24,1792]{1,0:T(8,128)(2,1)S(1)} %constant_dynamic-slice_fusion.15), channel_id=1, source_target_pairs={{0,16},{4,20},{8,24},{12,28},{16,0},{20,4},{24,8},{28,12},{1,17},{... | collective-permute-start | bytes 258056 | tf_op jit(solution)/shard_map/ppermute | solution.py:39
  56.9 0.3 collective-permute-done.14
  57.2 0.4 collective-permute-start.20
  57.5 1.2 %collective-permute-done.8 = bf16[24,1792]{1,0:T(8,128)(2,1)S(1)} collective-permute-done((bf16[24,1792]{1,0:T(8,128)(2,1)S(1)}, bf16[24,1792]{1,0:T(8,128)(2,1)S(1)}, u32[]{:S(2)}, u32[]{:S(2)}) %collective-permute-start.8) | collective-permute-done | bytes 86048 | tf_op jit(solution)/shard_map/ppermute | solution.py:39
  58.8 1.1 collective-permute-done.5
  59.8 0.2 fusion.6
  60.0 1.6 %collective-permute-start.15 = (bf16[3,24,1792]{2,1,0:T(8,128)(2,1)S(1)}, bf16[3,24,1792]{2,1,0:T(8,128)(2,1)S(1)}, u32[]{:S(2)}, u32[]{:S(2)}) collective-permute-start(bf16[3,24,1792]{2,1,0:T(8,128)(2,1)S(1)} %pad_maximum_fusion.1), channel_id=1, source_target_pairs={{0,16},{4,20},{8,24},{12,28},{16,0},{20,4},{24,8},{28,12},{1,17},{... | collective-permute-start | bytes 774152 | tf_op jit(solution)/shard_map/ppermute | solution.py:67
  61.7 0.2 fusion.8
  61.9 0.6 collective-permute-start.27
  62.4 4.6 %collective-permute-done.15 = bf16[3,24,1792]{2,1,0:T(8,128)(2,1)S(1)} collective-permute-done((bf16[3,24,1792]{2,1,0:T(8,128)(2,1)S(1)}, bf16[3,24,1792]{2,1,0:T(8,128)(2,1)S(1)}, u32[]{:S(2)}, u32[]{:S(2)}) %collective-permute-start.15) | collective-permute-done | bytes 258080 | tf_op jit(solution)/shard_map/ppermute | solution.py:67
  67.1 0.9 collective-permute-start.16
  68.0 1.4 %collective-permute-done.27 = bf16[3,24,1792]{2,1,0:T(8,128)(2,1)S(1)} collective-permute-done((bf16[3,24,1792]{2,1,0:T(8,128)(2,1)S(1)}, bf16[3,24,1792]{2,1,0:T(8,128)(2,1)S(1)}, u32[]{:S(2)}, u32[]{:S(2)}) %collective-permute-start.27) | collective-permute-done | bytes 258080 | tf_op jit(solution)/shard_map/ppermute | solution.py:67
  69.4 1.1 collective-permute-start.28
  70.5 9.0 %collective-permute-done.16 = bf16[3,48,1792]{2,1,0:T(8,128)(2,1)S(1)} collective-permute-done((bf16[3,48,1792]{2,1,0:T(8,128)(2,1)S(1)}, bf16[3,48,1792]{2,1,0:T(8,128)(2,1)S(1)}, u32[]{:S(2)}, u32[]{:S(2)}) %collective-permute-start.16) | collective-permute-done | bytes 516128 | tf_op jit(solution)/shard_map/ppermute | solution.py:67
  79.6 0.3 maximum_select_fusion.2
  79.9 0.3 maximum_select_fusion.3
  80.2 0.6 collective-permute-start.29
  80.7 1.8 %collective-permute-done.17 = bf16[3,96,1792]{2,1,0:T(8,128)(2,1)S(1)} collective-permute-done((bf16[3,96,1792]{2,1,0:T(8,128)(2,1)S(1)}, bf16[3,96,1792]{2,1,0:T(8,128)(2,1)S(1)}, u32[]{:S(2)}, u32[]{:S(2)}) %collective-permute-start.17) | collective-permute-done | bytes 1032224 | tf_op jit(solution)/shard_map/ppermute | solution.py:67
  82.5 0.8 maximum_select_fusion
  83.3 0.8 collective-permute-done.29
  84.1 2.1 %maximum_select_fusion.1 = bf16[3,192,1792]{2,1,0:T(8,128)(2,1)S(1)} fusion(bf16[3,96,1792]{2,1,0:T(8,128)(2,1)S(1)} %maximum_select_fusion.3, bf16[3,96,1792]{2,1,0:T(8,128)(2,1)} %collective-permute-done.29, pred[]{:T(512)S(6)} %eq.25), kind=kLoop, calls=%fused_computation.11 | loop fusion | flops 9289728 | bytes 4128769 | tf_op jit(solution)/shard_map/jit(_where)/select_n | solution.py:68
  86.2 0.5 fusion.4
  86.8 1.3 %slice-done.3 = s8[3145728]{0:T(1024)(128)(4,1)S(1)} async-done(((s8[7340032]{0:T(1024)(128)(4,1)}), s8[3145728]{0:T(1024)(128)(4,1)S(1)}, s32[]{:S(2)}) %slice-start.3) | async-done | bytes 3145752
  88.1 2.5 %fusion.16 = f32[192,1024]{1,0:T(8,128)S(1)} fusion(bf16[192,3584]{1,0:T(8,128)(2,1)S(1)} %get-tuple-element.18, bf16[1024,3584]{1,0:T(8,128)(2,1)S(1)} %bitcast.37), kind=kOutput, calls=%fused_computation.89 | convolution fusion | flops 1409286144 | bytes 9502720 | tf_op jit(solution)/shard_map/dot_general | solution.py:14
  90.6 2.5 %fusion.5 = bf16[192,1024]{1,0:T(8,128)(2,1)S(1)} fusion(f32[192,1024]{1,0:T(8,128)S(1)} %fusion.16, bf16[192,3584]{1,0:T(8,128)(2,1)S(1)} %get-tuple-element.13, bf16[1024,3584]{1,0:T(8,128)(2,1)S(1)} %bitcast.41), kind=kOutput, calls=%fused_computation.19 | convolution fusion | flops 1409679360 | bytes 9895936 | tf_op jit(solution)/shard_map/dot_general | solution.py:14
  93.2 5.2 %convolution_convert_fusion.2 = bf16[1024,3584]{1,0:T(8,128)(2,1)} fusion(bf16[192,1024]{1,0:T(8,128)(2,1)S(1)} %constant_dynamic-update-slice_fusion, bf16[192,3584]{1,0:T(8,128)(2,1)S(1)} %get-tuple-element.13), kind=kOutput, calls=%fused_computation.2 | convolution fusion | flops 1412956160 | bytes 9109504 | tf_op jit(solution)/shard_map/dot_general | solution.py:128
  98.4 2.7 %collective-permute-start.30 = (bf16[48,1024]{1,0:T(8,128)(2,1)S(1)}, bf16[48,1024]{1,0:T(8,128)(2,1)S(1)}, u32[]{:S(2)}, u32[]{:S(2)}) collective-permute-start(bf16[48,1024]{1,0:T(8,128)(2,1)S(1)} %get-tuple-element.35), channel_id=1, source_target_pairs={{0,3},{1,0},{2,1},{3,2},{4,7},{5,4},{6,5},{7,6},{8,11},{9,8},{10,9... | collective-permute-start | bytes 294920 | tf_op jit(solution)/shard_map/ppermute | solution.py:106
  101.1 2.9 %collective-permute-start.31 = (bf16[48,1024]{1,0:T(8,128)(2,1)S(1)}, bf16[48,1024]{1,0:T(8,128)(2,1)S(1)}, u32[]{:S(2)}, u32[]{:S(2)}) collective-permute-start(bf16[48,1024]{1,0:T(8,128)(2,1)S(1)} %get-tuple-element.37), channel_id=1, source_target_pairs={{0,2},{1,3},{2,0},{3,1},{4,6},{5,7},{6,4},{7,5},{8,10},{9,11},{10,... | collective-permute-start | bytes 294920 | tf_op jit(solution)/shard_map/ppermute | solution.py:106
  104.0 5.2 %convolution_convert_fusion.1 = bf16[1024,3584]{1,0:T(8,128)(2,1)} fusion(bf16[192,1024]{1,0:T(8,128)(2,1)S(1)} %constant_dynamic-update-slice_fusion, bf16[192,3584]{1,0:T(8,128)(2,1)S(1)} %get-tuple-element.18), kind=kOutput, calls=%fused_computation.1 | convolution fusion | flops 1412956160 | bytes 9109504 | tf_op jit(solution)/shard_map/dot_general | solution.py:131
  109.2 5.2 %convolution_convert_fusion = bf16[3584,1024]{1,0:T(8,128)(2,1)} fusion(bf16[192,3584]{1,0:T(8,128)(2,1)S(1)} %get-tuple-element.19, bf16[192,1024]{1,0:T(8,128)(2,1)S(1)} %copy-done.1), kind=kOutput, calls=%fused_computation | convolution fusion | flops 1412956160 | bytes 9109504 | tf_op jit(solution)/shard_map/dot_general | solution.py:8
  114.4 0.7 add_convert_fusion.12
  (88 shorter events, 2.3 us)
Async XLA Ops:
  0.6 32.6 %collective-permute-start.1 = (bf16[48,1024]{1,0:T(8,128)(2,1)}, bf16[48,1024]{1,0:T(8,128)(2,1)S(1)}, u32[]{:S(2)}, u32[]{:S(2)}) collective-permute-start(bf16[48,1024]{1,0:T(8,128)(2,1)} %param.5), channel_id=1, source_target_pairs={{0,2},{1,3},{2,0},{3,1},{4,6},{5,7},{6,4},{7,5},{8,10},{9,11},{10,... | collective-permute-start | bytes 294920 | tf_op jit(solution)/shard_map/ppermute | solution.py:98
  4.8 28.4 %collective-permute-start = (bf16[48,1024]{1,0:T(8,128)(2,1)}, bf16[48,1024]{1,0:T(8,128)(2,1)S(1)}, u32[]{:S(2)}, u32[]{:S(2)}) collective-permute-start(bf16[48,1024]{1,0:T(8,128)(2,1)} %param.5), channel_id=1, source_target_pairs={{0,1},{1,2},{2,3},{3,0},{4,5},{5,6},{6,7},{7,4},{8,9},{9,10},{10,1... | collective-permute-start | bytes 294920 | tf_op jit(solution)/shard_map/ppermute | solution.py:98
  6.3 26.9 %collective-permute-start.2 = (bf16[48,1024]{1,0:T(8,128)(2,1)}, bf16[48,1024]{1,0:T(8,128)(2,1)S(1)}, u32[]{:S(2)}, u32[]{:S(2)}) collective-permute-start(bf16[48,1024]{1,0:T(8,128)(2,1)} %param.5), channel_id=1, source_target_pairs={{0,3},{1,0},{2,1},{3,2},{4,7},{5,4},{6,5},{7,6},{8,11},{9,8},{10,9... | collective-permute-start | bytes 294920 | tf_op jit(solution)/shard_map/ppermute | solution.py:98
  8.6 11.9 %collective-permute-start.10 = (bf16[48,1024]{1,0:T(8,128)(2,1)}, bf16[48,1024]{1,0:T(8,128)(2,1)S(1)}, u32[]{:S(2)}, u32[]{:S(2)}) collective-permute-start(bf16[48,1024]{1,0:T(8,128)(2,1)} %param.6), channel_id=1, source_target_pairs={{0,2},{1,3},{2,0},{3,1},{4,6},{5,7},{6,4},{7,5},{8,10},{9,11},{10,... | collective-permute-start | bytes 294920 | tf_op jit(solution)/shard_map/ppermute | solution.py:98
  8.6 8.8 %collective-permute-start.9 = (bf16[48,1024]{1,0:T(8,128)(2,1)}, bf16[48,1024]{1,0:T(8,128)(2,1)S(1)}, u32[]{:S(2)}, u32[]{:S(2)}) collective-permute-start(bf16[48,1024]{1,0:T(8,128)(2,1)} %param.6), channel_id=1, source_target_pairs={{0,1},{1,2},{2,3},{3,0},{4,5},{5,6},{6,7},{7,4},{8,9},{9,10},{10,1... | collective-permute-start | bytes 294920 | tf_op jit(solution)/shard_map/ppermute | solution.py:98
  17.3 9.2 %collective-permute-start.11 = (bf16[48,1024]{1,0:T(8,128)(2,1)}, bf16[48,1024]{1,0:T(8,128)(2,1)S(1)}, u32[]{:S(2)}, u32[]{:S(2)}) collective-permute-start(bf16[48,1024]{1,0:T(8,128)(2,1)} %param.6), channel_id=1, source_target_pairs={{0,3},{1,0},{2,1},{3,2},{4,7},{5,4},{6,5},{7,6},{8,11},{9,8},{10,9... | collective-permute-start | bytes 294920 | tf_op jit(solution)/shard_map/ppermute | solution.py:98
  26.5 6.7 %slice-start = ((s8[7340032]{0:T(1024)(128)(4,1)}), s8[4194304]{0:T(1024)(128)(4,1)S(1)}, s32[]{:S(2)}) async-start(s8[7340032]{0:T(1024)(128)(4,1)} %bitcast.34), calls=%async_computation | async-start | bytes 8388608
  26.5 5.9 %copy-start = (bf16[192,1024]{1,0:T(8,128)(2,1)}, bf16[192,1024]{1,0:T(8,128)(2,1)S(1)}, u32[]{:S(2)}) copy-start(bf16[192,1024]{1,0:T(8,128)(2,1)S(1)} %constant_dynamic-update-slice_fusion.4) | copy-start | bytes 1179652
  26.5 6.7 %slice-start.1 = ((s8[7340032]{0:T(1024)(128)(4,1)}), s8[3145728]{0:T(1024)(128)(4,1)S(1)}, s32[]{:S(2)}) async-start(s8[7340032]{0:T(1024)(128)(4,1)} %bitcast.34), calls=%async_computation.1 | async-start | bytes 6291456
  32.6 5.7 %collective-permute-start.12 = (bf16[96,1792]{1,0:T(8,128)(2,1)S(1)}, bf16[96,1792]{1,0:T(8,128)(2,1)S(1)}, u32[]{:S(2)}, u32[]{:S(2)}) collective-permute-start(bf16[96,1792]{1,0:T(8,128)(2,1)S(1)} %constant_dynamic-slice_fusion.11), channel_id=1, source_target_pairs={{0,4},{4,0},{8,12},{12,8},{16,20},{20,16},{24,28},{28,24},{1,5},{5... | collective-permute-start | bytes 1032200 | tf_op jit(solution)/shard_map/ppermute | solution.py:39
  32.7 6.3 %collective-permute-start.24 = (bf16[96,1792]{1,0:T(8,128)(2,1)S(1)}, bf16[96,1792]{1,0:T(8,128)(2,1)S(1)}, u32[]{:S(2)}, u32[]{:S(2)}) collective-permute-start(bf16[96,1792]{1,0:T(8,128)(2,1)S(1)} %constant_dynamic-slice_fusion.2), channel_id=1, source_target_pairs={{0,4},{4,0},{8,12},{12,8},{16,20},{20,16},{24,28},{28,24},{1,5},{5... | collective-permute-start | bytes 1032200 | tf_op jit(solution)/shard_map/ppermute | solution.py:39
  33.2 2.5 %slice-start.4 = ((s8[7340032]{0:T(1024)(128)(4,1)}), s8[4194304]{0:T(1024)(128)(4,1)S(1)}, s32[]{:S(2)}) async-start(s8[7340032]{0:T(1024)(128)(4,1)} %bitcast.38), calls=%async_computation.4 | async-start | bytes 8388608
  33.3 3.1 %slice-start.5 = ((s8[7340032]{0:T(1024)(128)(4,1)}), s8[3145728]{0:T(1024)(128)(4,1)S(1)}, s32[]{:S(2)}) async-start(s8[7340032]{0:T(1024)(128)(4,1)} %bitcast.38), calls=%async_computation.5 | async-start | bytes 6291456
  35.1 5.6 %collective-permute-start.6 = (bf16[96,1792]{1,0:T(8,128)(2,1)S(1)}, bf16[96,1792]{1,0:T(8,128)(2,1)S(1)}, u32[]{:S(2)}, u32[]{:S(2)}) collective-permute-start(bf16[96,1792]{1,0:T(8,128)(2,1)S(1)} %constant_dynamic-slice_fusion.14), channel_id=1, source_target_pairs={{0,4},{4,0},{8,12},{12,8},{16,20},{20,16},{24,28},{28,24},{1,5},{5... | collective-permute-start | bytes 1032200 | tf_op jit(solution)/shard_map/ppermute | solution.py:39
  35.2 7.1 %collective-permute-start.21 = (bf16[96,1792]{1,0:T(8,128)(2,1)S(1)}, bf16[96,1792]{1,0:T(8,128)(2,1)S(1)}, u32[]{:S(2)}, u32[]{:S(2)}) collective-permute-start(bf16[96,1792]{1,0:T(8,128)(2,1)S(1)} %constant_dynamic-slice_fusion.5), channel_id=1, source_target_pairs={{0,4},{4,0},{8,12},{12,8},{16,20},{20,16},{24,28},{28,24},{1,5},{5... | collective-permute-start | bytes 1032200 | tf_op jit(solution)/shard_map/ppermute | solution.py:39
  38.2 4.9 %collective-permute-start.3 = (bf16[96,1792]{1,0:T(8,128)(2,1)S(1)}, bf16[96,1792]{1,0:T(8,128)(2,1)S(1)}, u32[]{:S(2)}, u32[]{:S(2)}) collective-permute-start(bf16[96,1792]{1,0:T(8,128)(2,1)S(1)} %constant_dynamic-slice_fusion.17), channel_id=1, source_target_pairs={{0,4},{4,0},{8,12},{12,8},{16,20},{20,16},{24,28},{28,24},{1,5},{5... | collective-permute-start | bytes 1032200 | tf_op jit(solution)/shard_map/ppermute | solution.py:39
  38.3 5.5 %collective-permute-start.18 = (bf16[96,1792]{1,0:T(8,128)(2,1)S(1)}, bf16[96,1792]{1,0:T(8,128)(2,1)S(1)}, u32[]{:S(2)}, u32[]{:S(2)}) collective-permute-start(bf16[96,1792]{1,0:T(8,128)(2,1)S(1)} %constant_dynamic-slice_fusion.8), channel_id=1, source_target_pairs={{0,4},{4,0},{8,12},{12,8},{16,20},{20,16},{24,28},{28,24},{1,5},{5... | collective-permute-start | bytes 1032200 | tf_op jit(solution)/shard_map/ppermute | solution.py:39
  39.0 7.3 %collective-permute-start.13 = (bf16[48,1792]{1,0:T(8,128)(2,1)S(1)}, bf16[48,1792]{1,0:T(8,128)(2,1)S(1)}, u32[]{:S(2)}, u32[]{:S(2)}) collective-permute-start(bf16[48,1792]{1,0:T(8,128)(2,1)S(1)} %constant_dynamic-slice_fusion.10), channel_id=1, source_target_pairs={{0,8},{4,12},{8,0},{12,4},{16,24},{20,28},{24,16},{28,20},{1,9},{5... | collective-permute-start | bytes 516104 | tf_op jit(solution)/shard_map/ppermute | solution.py:39
  40.7 7.3 %collective-permute-start.25 = (bf16[48,1792]{1,0:T(8,128)(2,1)S(1)}, bf16[48,1792]{1,0:T(8,128)(2,1)S(1)}, u32[]{:S(2)}, u32[]{:S(2)}) collective-permute-start(bf16[48,1792]{1,0:T(8,128)(2,1)S(1)} %constant_dynamic-slice_fusion.1), channel_id=1, source_target_pairs={{0,16},{4,20},{8,24},{12,28},{16,0},{20,4},{24,8},{28,12},{1,17},{... | collective-permute-start | bytes 516104 | tf_op jit(solution)/shard_map/ppermute | solution.py:39
  42.4 7.5 %collective-permute-start.7 = (bf16[48,1792]{1,0:T(8,128)(2,1)S(1)}, bf16[48,1792]{1,0:T(8,128)(2,1)S(1)}, u32[]{:S(2)}, u32[]{:S(2)}) collective-permute-start(bf16[48,1792]{1,0:T(8,128)(2,1)S(1)} %constant_dynamic-slice_fusion.13), channel_id=1, source_target_pairs={{0,8},{4,12},{8,0},{12,4},{16,24},{20,28},{24,16},{28,20},{1,9},{5... | collective-permute-start | bytes 516104 | tf_op jit(solution)/shard_map/ppermute | solution.py:39
  43.1 8.6 %collective-permute-start.22 = (bf16[48,1792]{1,0:T(8,128)(2,1)S(1)}, bf16[48,1792]{1,0:T(8,128)(2,1)S(1)}, u32[]{:S(2)}, u32[]{:S(2)}) collective-permute-start(bf16[48,1792]{1,0:T(8,128)(2,1)S(1)} %constant_dynamic-slice_fusion.4), channel_id=1, source_target_pairs={{0,16},{4,20},{8,24},{12,28},{16,0},{20,4},{24,8},{28,12},{1,17},{... | collective-permute-start | bytes 516104 | tf_op jit(solution)/shard_map/ppermute | solution.py:39
  43.8 9.8 %collective-permute-start.4 = (bf16[48,1792]{1,0:T(8,128)(2,1)S(1)}, bf16[48,1792]{1,0:T(8,128)(2,1)S(1)}, u32[]{:S(2)}, u32[]{:S(2)}) collective-permute-start(bf16[48,1792]{1,0:T(8,128)(2,1)S(1)} %constant_dynamic-slice_fusion.16), channel_id=1, source_target_pairs={{0,8},{4,12},{8,0},{12,4},{16,24},{20,28},{24,16},{28,20},{1,9},{5... | collective-permute-start | bytes 516104 | tf_op jit(solution)/shard_map/ppermute | solution.py:39
  46.2 9.1 %collective-permute-start.19 = (bf16[48,1792]{1,0:T(8,128)(2,1)S(1)}, bf16[48,1792]{1,0:T(8,128)(2,1)S(1)}, u32[]{:S(2)}, u32[]{:S(2)}) collective-permute-start(bf16[48,1792]{1,0:T(8,128)(2,1)S(1)} %constant_dynamic-slice_fusion.7), channel_id=1, source_target_pairs={{0,16},{4,20},{8,24},{12,28},{16,0},{20,4},{24,8},{28,12},{1,17},{... | collective-permute-start | bytes 516104 | tf_op jit(solution)/shard_map/ppermute | solution.py:39
  48.0 9.2 %collective-permute-start.14 = (bf16[24,1792]{1,0:T(8,128)(2,1)S(1)}, bf16[24,1792]{1,0:T(8,128)(2,1)S(1)}, u32[]{:S(2)}, u32[]{:S(2)}) collective-permute-start(bf16[24,1792]{1,0:T(8,128)(2,1)S(1)} %constant_dynamic-slice_fusion.9), channel_id=1, source_target_pairs={{0,16},{4,20},{8,24},{12,28},{16,0},{20,4},{24,8},{28,12},{1,17},{... | collective-permute-start | bytes 258056 | tf_op jit(solution)/shard_map/ppermute | solution.py:39
  49.9 11.7 %collective-permute-start.26 = (bf16[24,1792]{1,0:T(8,128)(2,1)S(1)}, bf16[24,1792]{1,0:T(8,128)(2,1)S(1)}, u32[]{:S(2)}, u32[]{:S(2)}) collective-permute-start(bf16[24,1792]{1,0:T(8,128)(2,1)S(1)} %constant_dynamic-slice_fusion), channel_id=1, source_target_pairs={{0,8},{4,12},{8,0},{12,4},{16,24},{20,28},{24,16},{28,20},{1,9},{5... | collective-permute-start | bytes 258056 | tf_op jit(solution)/shard_map/ppermute | solution.py:39
  51.7 7.1 %collective-permute-start.8 = (bf16[24,1792]{1,0:T(8,128)(2,1)S(1)}, bf16[24,1792]{1,0:T(8,128)(2,1)S(1)}, u32[]{:S(2)}, u32[]{:S(2)}) collective-permute-start(bf16[24,1792]{1,0:T(8,128)(2,1)S(1)} %constant_dynamic-slice_fusion.12), channel_id=1, source_target_pairs={{0,16},{4,20},{8,24},{12,28},{16,0},{20,4},{24,8},{28,12},{1,17},{... | collective-permute-start | bytes 258056 | tf_op jit(solution)/shard_map/ppermute | solution.py:39
  53.6 8.0 %collective-permute-start.23 = (bf16[24,1792]{1,0:T(8,128)(2,1)S(1)}, bf16[24,1792]{1,0:T(8,128)(2,1)S(1)}, u32[]{:S(2)}, u32[]{:S(2)}) collective-permute-start(bf16[24,1792]{1,0:T(8,128)(2,1)S(1)} %constant_dynamic-slice_fusion.3), channel_id=1, source_target_pairs={{0,8},{4,12},{8,0},{12,4},{16,24},{20,28},{24,16},{28,20},{1,9},{5... | collective-permute-start | bytes 258056 | tf_op jit(solution)/shard_map/ppermute | solution.py:39
  55.3 4.5 %collective-permute-start.5 = (bf16[24,1792]{1,0:T(8,128)(2,1)S(1)}, bf16[24,1792]{1,0:T(8,128)(2,1)S(1)}, u32[]{:S(2)}, u32[]{:S(2)}) collective-permute-start(bf16[24,1792]{1,0:T(8,128)(2,1)S(1)} %constant_dynamic-slice_fusion.15), channel_id=1, source_target_pairs={{0,16},{4,20},{8,24},{12,28},{16,0},{20,4},{24,8},{28,12},{1,17},{... | collective-permute-start | bytes 258056 | tf_op jit(solution)/shard_map/ppermute | solution.py:39
  57.2 4.5 %collective-permute-start.20 = (bf16[24,1792]{1,0:T(8,128)(2,1)S(1)}, bf16[24,1792]{1,0:T(8,128)(2,1)S(1)}, u32[]{:S(2)}, u32[]{:S(2)}) collective-permute-start(bf16[24,1792]{1,0:T(8,128)(2,1)S(1)} %constant_dynamic-slice_fusion.6), channel_id=1, source_target_pairs={{0,8},{4,12},{8,0},{12,4},{16,24},{20,28},{24,16},{28,20},{1,9},{5... | collective-permute-start | bytes 258056 | tf_op jit(solution)/shard_map/ppermute | solution.py:39
  60.0 7.0 %collective-permute-start.15 = (bf16[3,24,1792]{2,1,0:T(8,128)(2,1)S(1)}, bf16[3,24,1792]{2,1,0:T(8,128)(2,1)S(1)}, u32[]{:S(2)}, u32[]{:S(2)}) collective-permute-start(bf16[3,24,1792]{2,1,0:T(8,128)(2,1)S(1)} %pad_maximum_fusion.1), channel_id=1, source_target_pairs={{0,16},{4,20},{8,24},{12,28},{16,0},{20,4},{24,8},{28,12},{1,17},{... | collective-permute-start | bytes 774152 | tf_op jit(solution)/shard_map/ppermute | solution.py:67
  61.9 7.5 %collective-permute-start.27 = (bf16[3,24,1792]{2,1,0:T(8,128)(2,1)S(1)}, bf16[3,24,1792]{2,1,0:T(8,128)(2,1)S(1)}, u32[]{:S(2)}, u32[]{:S(2)}) collective-permute-start(bf16[3,24,1792]{2,1,0:T(8,128)(2,1)S(1)} %pad_maximum_fusion.2), channel_id=1, source_target_pairs={{0,8},{4,12},{8,0},{12,4},{16,24},{20,28},{24,16},{28,20},{1,9},{5... | collective-permute-start | bytes 774152 | tf_op jit(solution)/shard_map/ppermute | solution.py:67
  67.1 12.5 %collective-permute-start.16 = (bf16[3,48,1792]{2,1,0:T(8,128)(2,1)S(1)}, bf16[3,48,1792]{2,1,0:T(8,128)(2,1)S(1)}, u32[]{:S(2)}, u32[]{:S(2)}) collective-permute-start(bf16[3,48,1792]{2,1,0:T(8,128)(2,1)S(1)} %maximum_select_fusion.4), channel_id=1, source_target_pairs={{0,8},{4,12},{8,0},{12,4},{16,24},{20,28},{24,16},{28,20},{1,9},{5... | collective-permute-start | bytes 1548296 | tf_op jit(solution)/shard_map/ppermute | solution.py:67
  69.4 10.5 %collective-permute-start.28 = (bf16[3,48,1792]{2,1,0:T(8,128)(2,1)S(1)}, bf16[3,48,1792]{2,1,0:T(8,128)(2,1)S(1)}, u32[]{:S(2)}, u32[]{:S(2)}) collective-permute-start(bf16[3,48,1792]{2,1,0:T(8,128)(2,1)S(1)} %maximum_select_fusion.5), channel_id=1, source_target_pairs={{0,16},{4,20},{8,24},{12,28},{16,0},{20,4},{24,8},{28,12},{1,17},{... | collective-permute-start | bytes 1548296 | tf_op jit(solution)/shard_map/ppermute | solution.py:67
  79.8 2.7 %collective-permute-start.17 = (bf16[3,96,1792]{2,1,0:T(8,128)(2,1)S(1)}, bf16[3,96,1792]{2,1,0:T(8,128)(2,1)S(1)}, u32[]{:S(2)}, u32[]{:S(2)}) collective-permute-start(bf16[3,96,1792]{2,1,0:T(8,128)(2,1)S(1)} %maximum_select_fusion.2), channel_id=1, source_target_pairs={{0,4},{4,0},{8,12},{12,8},{16,20},{20,16},{24,28},{28,24},{1,5},{5... | collective-permute-start | bytes 3096584 | tf_op jit(solution)/shard_map/ppermute | solution.py:67
  80.2 4.0 %collective-permute-start.29 = (bf16[3,96,1792]{2,1,0:T(8,128)(2,1)S(1)}, bf16[3,96,1792]{2,1,0:T(8,128)(2,1)}, u32[]{:S(2)}, u32[]{:S(2)}) collective-permute-start(bf16[3,96,1792]{2,1,0:T(8,128)(2,1)S(1)} %maximum_select_fusion.3), channel_id=1, source_target_pairs={{0,4},{4,0},{8,12},{12,8},{16,20},{20,16},{24,28},{28,24},{1,5},{5... | collective-permute-start | bytes 3096584 | tf_op jit(solution)/shard_map/ppermute | solution.py:67
  82.5 4.3 %slice-start.2 = ((s8[7340032]{0:T(1024)(128)(4,1)}), s8[4194304]{0:T(1024)(128)(4,1)S(1)}, s32[]{:S(2)}) async-start(s8[7340032]{0:T(1024)(128)(4,1)} %bitcast.36), calls=%async_computation.2 | async-start | bytes 8388608
  86.2 1.9 %slice-start.3 = ((s8[7340032]{0:T(1024)(128)(4,1)}), s8[3145728]{0:T(1024)(128)(4,1)S(1)}, s32[]{:S(2)}) async-start(s8[7340032]{0:T(1024)(128)(4,1)} %bitcast.36), calls=%async_computation.3 | async-start | bytes 6291456
  86.2 4.4 %slice-start.6 = ((s8[7340032]{0:T(1024)(128)(4,1)}), s8[4194304]{0:T(1024)(128)(4,1)S(1)}, s32[]{:S(2)}) async-start(s8[7340032]{0:T(1024)(128)(4,1)} %bitcast.40), calls=%async_computation.6 | async-start | bytes 8388608
  88.1 2.5 %slice-start.7 = ((s8[7340032]{0:T(1024)(128)(4,1)}), s8[3145728]{0:T(1024)(128)(4,1)S(1)}, s32[]{:S(2)}) async-start(s8[7340032]{0:T(1024)(128)(4,1)} %bitcast.40), calls=%async_computation.7 | async-start | bytes 6291456
  98.4 16.0 %collective-permute-start.30 = (bf16[48,1024]{1,0:T(8,128)(2,1)S(1)}, bf16[48,1024]{1,0:T(8,128)(2,1)S(1)}, u32[]{:S(2)}, u32[]{:S(2)}) collective-permute-start(bf16[48,1024]{1,0:T(8,128)(2,1)S(1)} %get-tuple-element.35), channel_id=1, source_target_pairs={{0,3},{1,0},{2,1},{3,2},{4,7},{5,4},{6,5},{7,6},{8,11},{9,8},{10,9... | collective-permute-start | bytes 294920 | tf_op jit(solution)/shard_map/ppermute | solution.py:106
  101.1 13.3 %collective-permute-start.32 = (bf16[48,1024]{1,0:T(8,128)(2,1)S(1)}, bf16[48,1024]{1,0:T(8,128)(2,1)S(1)}, u32[]{:S(2)}, u32[]{:S(2)}) collective-permute-start(bf16[48,1024]{1,0:T(8,128)(2,1)S(1)} %get-tuple-element.36), channel_id=1, source_target_pairs={{0,1},{1,2},{2,3},{3,0},{4,5},{5,6},{6,7},{7,4},{8,9},{9,10},{10,1... | collective-permute-start | bytes 294920 | tf_op jit(solution)/shard_map/ppermute | solution.py:106
  101.1 8.1 %copy-start.1 = (bf16[192,1024]{1,0:T(8,128)(2,1)S(1)}, bf16[192,1024]{1,0:T(8,128)(2,1)}, u32[]{:S(2)}) copy-start(bf16[192,1024]{1,0:T(8,128)(2,1)} %copy-done) | copy-start | bytes 1179652
  101.1 13.3 %collective-permute-start.31 = (bf16[48,1024]{1,0:T(8,128)(2,1)S(1)}, bf16[48,1024]{1,0:T(8,128)(2,1)S(1)}, u32[]{:S(2)}, u32[]{:S(2)}) collective-permute-start(bf16[48,1024]{1,0:T(8,128)(2,1)S(1)} %get-tuple-element.37), channel_id=1, source_target_pairs={{0,2},{1,3},{2,0},{3,1},{4,6},{5,7},{6,4},{7,5},{8,10},{9,11},{10,... | collective-permute-start | bytes 294920 | tf_op jit(solution)/shard_map/ppermute | solution.py:106

commit v19 on v16

--- a/solution.py
+++ b/solution.py
@@ -61,11 +61,17 @@
 
 def doubling_gather(x, order, n_dev):
     r = lax.axis_index("row")
-    cur = x
-    for bit in reversed(order):
+    cur = list(x)
+    for step, bit in enumerate(reversed(order)):
         hi = (r // bit) % 2
-        got = lax.ppermute(cur, "row", [(j, j ^ bit) for j in range(n_dev)])
-        cur = jnp.where(hi == 1, jnp.concatenate([got, cur], axis=1), jnp.concatenate([cur, got], axis=1))
+        perm = [(j, j ^ bit) for j in range(n_dev)]
+        if step + 1 == len(order):
+            cur = jnp.stack(cur)
+            got = lax.ppermute(cur, "row", perm)
+            cur = jnp.where(hi == 1, jnp.concatenate([got, cur], axis=1), jnp.concatenate([cur, got], axis=1))
+        else:
+            got = [lax.ppermute(c, "row", perm) for c in cur]
+            cur = [jnp.where(hi == 1, jnp.concatenate([g, c], axis=0), jnp.concatenate([c, g], axis=0)) for c, g in zip(cur, got)]
     return cur
 
 
@@ -88,7 +94,7 @@
     orders = (bits, bits[:1] + bits[:0:-1])
     half = units // 2
     reduced = [halving_reduce([a[:, h * half:(h + 1) * half] for a in stacked], o, n_dev) for h, o in enumerate(orders)]
-    outs = [doubling_gather(jnp.stack(gated_grads(red[0], red[1], red[2])), o, n_dev) for red, o in zip(reduced, orders)]
+    outs = [doubling_gather(gated_grads(red[0], red[1], red[2]), o, n_dev) for red, o in zip(reduced, orders)]
     return jnp.concatenate(outs, axis=2)
 
 

time: 106 us -> 110 us (1.038)
  starting transfers between devices: 38.1 us -> 45.7 us
  waiting for transfers between devices: 27 us -> 21.4 us
  other arithmetic: 6.98 us -> 8.32 us
    ppermute x6 -> x14, starting transfers between devices: 4.75 us -> 12.5 us  [the longest x12 12.4 us: doubling_gather(): got = [lax.ppermute(c, 'row', perm) for c in cur]]
    ppermute x6 -> x14, waiting for transfers between devices: 17.7 us -> 12.1 us  [the longest x12 9.67 us: doubling_gather(): got = [lax.ppermute(c, 'row', perm) for c in cur]]
    another operation x4 -> x2, other arithmetic: 0.37 us -> 2.15 us  [doubling_gather(): cur = jnp.stack(cur)]
    select_n x6 -> x2, other arithmetic: 3.52 us -> 2.4 us  [doubling_gather(): jnp.where(hi == 1, jnp.concatenate([got, cur], axis=1), jnp.concatenate([...]
  transfers between devices with their start and end apart: 33 -> 41, of which waited for: 17 -> 19; matrix products, arithmetic and copies ran while one was open for 21% -> 22% of each run, Pallas kernels for 0% -> 0%
where the time goes in v19:
time: 110 us; the launch traced here: 109 us
  starting transfers between devices  45.7 us (42%)
  matrix products  29.5 us (27%)
  waiting for transfers between devices  21.4 us (19%)
  other arithmetic  8.32 us (8%)
  local copies, waits for them, and re-layouts  2.98 us (3%)
  between operations  1.22 us (1%)
    ppermute x18, starting transfers between devices, halving_reduce(): lax.ppermute(lax.dynamic_slice_in_dim(c, (1 - hi) * n, n, 0), 'row', perm)  17.3 us
    ppermute x6, starting transfers between devices, col_gather(): lax.ppermute(x, 'col', [(j, (j + s) % n_col) for j in range(n_col)])  13.2 us
    ppermute x12, starting transfers between devices, doubling_gather(): got = [lax.ppermute(c, 'row', perm) for c in cur]  12.4 us
    ppermute x12, waiting for transfers between devices, doubling_gather(): got = [lax.ppermute(c, 'row', perm) for c in cur]  9.67 us
    dot_general x3, matrix products, contract_last(): lax.dot_general(left, right, (((1,), (1,)), ((), ())), preferred_element_...  7.58 us
    dot_general x1, matrix products, contract_first(): lax.dot_general(left, right, (((0,), (0,)), ((), ())), preferred_element_...  5.19 us
    dot_general x1, matrix products, body(): jnp.dot(tok_t, grad_gate, preferred_element_type=jnp.float32)  5.18 us
    dot_general x1, matrix products, body(): acc_up = jnp.dot(tok_t, grad_up, preferred_element_type=jnp.float32)  5.18 us
  transfers between devices with their start and end apart: 41, of which 19 were waited for; matrix products, arithmetic and copies ran while one was open for 22% of the time, Pallas kernels for 0%

profile of v19, /device:TPU:0, one launch (start us, length us, event | category | flops | bytes accessed | tf_op | source)
XLA Modules:
  0.0 109.1 jit_solution(16700246032224790829)
XLA Ops:
  0.6 4.1 %collective-permute-start.1 = (bf16[48,1024]{1,0:T(8,128)(2,1)}, bf16[48,1024]{1,0:T(8,128)(2,1)S(1)}, u32[]{:S(2)}, u32[]{:S(2)}) collective-permute-start(bf16[48,1024]{1,0:T(8,128)(2,1)} %param.5), channel_id=1, source_target_pairs={{0,2},{1,3},{2,0},{3,1},{4,6},{5,7},{6,4},{7,5},{8,10},{9,11},{10,... | collective-permute-start | bytes 294920 | tf_op jit(solution)/shard_map/ppermute | solution.py:104
  4.8 1.6 %collective-permute-start = (bf16[48,1024]{1,0:T(8,128)(2,1)}, bf16[48,1024]{1,0:T(8,128)(2,1)S(1)}, u32[]{:S(2)}, u32[]{:S(2)}) collective-permute-start(bf16[48,1024]{1,0:T(8,128)(2,1)} %param.5), channel_id=1, source_target_pairs={{0,1},{1,2},{2,3},{3,0},{4,5},{5,6},{6,7},{7,4},{8,9},{9,10},{10,1... | collective-permute-start | bytes 294920 | tf_op jit(solution)/shard_map/ppermute | solution.py:104
  6.3 2.2 %collective-permute-start.2 = (bf16[48,1024]{1,0:T(8,128)(2,1)}, bf16[48,1024]{1,0:T(8,128)(2,1)S(1)}, u32[]{:S(2)}, u32[]{:S(2)}) collective-permute-start(bf16[48,1024]{1,0:T(8,128)(2,1)} %param.5), channel_id=1, source_target_pairs={{0,3},{1,0},{2,1},{3,2},{4,7},{5,4},{6,5},{7,6},{8,11},{9,8},{10,9... | collective-permute-start | bytes 294920 | tf_op jit(solution)/shard_map/ppermute | solution.py:104
  8.6 4.3 %collective-permute-done.1 = bf16[48,1024]{1,0:T(8,128)(2,1)S(1)} collective-permute-done((bf16[48,1024]{1,0:T(8,128)(2,1)}, bf16[48,1024]{1,0:T(8,128)(2,1)S(1)}, u32[]{:S(2)}, u32[]{:S(2)}) %collective-permute-start.1) | collective-permute-done | bytes 98336 | tf_op jit(solution)/shard_map/ppermute | solution.py:104
  12.9 0.7 collective-permute-done.2
  13.6 1.1 pad_maximum_fusion.3
  14.7 2.1 %collective-permute-start.13 = (bf16[48,1024]{1,0:T(8,128)(2,1)}, bf16[48,1024]{1,0:T(8,128)(2,1)S(1)}, u32[]{:S(2)}, u32[]{:S(2)}) collective-permute-start(bf16[48,1024]{1,0:T(8,128)(2,1)} %param.6), channel_id=1, source_target_pairs={{0,3},{1,0},{2,1},{3,2},{4,7},{5,4},{6,5},{7,6},{8,11},{9,8},{10,9... | collective-permute-start | bytes 294920 | tf_op jit(solution)/shard_map/ppermute | solution.py:104
  16.8 1.2 %collective-permute-start.12 = (bf16[48,1024]{1,0:T(8,128)(2,1)}, bf16[48,1024]{1,0:T(8,128)(2,1)S(1)}, u32[]{:S(2)}, u32[]{:S(2)}) collective-permute-start(bf16[48,1024]{1,0:T(8,128)(2,1)} %param.6), channel_id=1, source_target_pairs={{0,2},{1,3},{2,0},{3,1},{4,6},{5,7},{6,4},{7,5},{8,10},{9,11},{10,... | collective-permute-start | bytes 294920 | tf_op jit(solution)/shard_map/ppermute | solution.py:104
  18.0 1.9 %collective-permute-start.11 = (bf16[48,1024]{1,0:T(8,128)(2,1)}, bf16[48,1024]{1,0:T(8,128)(2,1)S(1)}, u32[]{:S(2)}, u32[]{:S(2)}) collective-permute-start(bf16[48,1024]{1,0:T(8,128)(2,1)} %param.6), channel_id=1, source_target_pairs={{0,1},{1,2},{2,3},{3,0},{4,5},{5,6},{6,7},{7,4},{8,9},{9,10},{10,1... | collective-permute-start | bytes 294920 | tf_op jit(solution)/shard_map/ppermute | solution.py:104
  19.9 4.7 %convolution_convert_fusion.4 = bf16[192,3584]{1,0:T(8,128)(2,1)S(1)} fusion(bf16[192,1024]{1,0:T(8,128)(2,1)S(1)} %pad_maximum_fusion.3, bf16[1024,3584]{1,0:T(8,128)(2,1)} %param.8), kind=kOutput, calls=%fused_computation.4 | convolution fusion | flops 1409974272 | bytes 9109504 | tf_op jit(solution)/shard_map/dot_general | solution.py:126
  24.9 0.5 collective-permute-start.25
  25.4 1.6 %convolution_convert_fusion.5 = bf16[192,3584]{1,0:T(8,128)(2,1)S(1)} fusion(bf16[192,1024]{1,0:T(8,128)(2,1)S(1)} %pad_maximum_fusion.3, bf16[1024,3584]{1,0:T(8,128)(2,1)S(1)} %bitcast.51), kind=kOutput, calls=%fused_computation.5 | convolution fusion | flops 1409974272 | bytes 9109504 | tf_op jit(solution)/shard_map/dot_general | solution.py:125
  27.2 0.7 copy-done.2
  28.1 0.5 collective-permute-start.22
  28.7 2.6 %convolution_convert_fusion.3 = bf16[192,3584]{1,0:T(8,128)(2,1)S(1)} fusion(bf16[192,1024]{1,0:T(8,128)(2,1)S(1)} %constant_dynamic-update-slice_fusion, bf16[3584,1024]{1,0:T(8,128)(2,1)S(1)} %bitcast.47), kind=kOutput, calls=%fused_computation.3 | convolution fusion | flops 1409974272 | bytes 9109504 | tf_op jit(solution)/shard_map/dot_general | solution.py:14
  31.5 0.5 collective-permute-start.30
  32.2 1.5 %collective-permute-start.7 = (bf16[48,1792]{1,0:T(8,128)(2,1)S(1)}, bf16[48,1792]{1,0:T(8,128)(2,1)S(1)}, u32[]{:S(2)}, u32[]{:S(2)}) collective-permute-start(bf16[48,1792]{1,0:T(8,128)(2,1)S(1)} %constant_dynamic-slice_fusion.13), channel_id=1, source_target_pairs={{0,8},{4,12},{8,0},{12,4},{16,24},{20,28},{24,16},{28,20},{1,9},{5... | collective-permute-start | bytes 516104 | tf_op jit(solution)/shard_map/ppermute | solution.py:39
  33.8 1.6 %collective-permute-start.26 = (bf16[48,1792]{1,0:T(8,128)(2,1)S(1)}, bf16[48,1792]{1,0:T(8,128)(2,1)S(1)}, u32[]{:S(2)}, u32[]{:S(2)}) collective-permute-start(bf16[48,1792]{1,0:T(8,128)(2,1)S(1)} %constant_dynamic-slice_fusion.4), channel_id=1, source_target_pairs={{0,16},{4,20},{8,24},{12,28},{16,0},{20,4},{24,8},{28,12},{1,17},{... | collective-permute-start | bytes 516104 | tf_op jit(solution)/shard_map/ppermute | solution.py:39
  35.6 0.6 collective-permute-start.4
  36.3 0.6 collective-permute-start.23
  37.0 1.5 %collective-permute-start.15 = (bf16[48,1792]{1,0:T(8,128)(2,1)S(1)}, bf16[48,1792]{1,0:T(8,128)(2,1)S(1)}, u32[]{:S(2)}, u32[]{:S(2)}) collective-permute-start(bf16[48,1792]{1,0:T(8,128)(2,1)S(1)} %constant_dynamic-slice_fusion.10), channel_id=1, source_target_pairs={{0,8},{4,12},{8,0},{12,4},{16,24},{20,28},{24,16},{28,20},{1,9},{5... | collective-permute-start | bytes 516104 | tf_op jit(solution)/shard_map/ppermute | solution.py:39
  38.6 0.8 collective-permute-done.7
  39.4 1.5 %collective-permute-start.31 = (bf16[48,1792]{1,0:T(8,128)(2,1)S(1)}, bf16[48,1792]{1,0:T(8,128)(2,1)S(1)}, u32[]{:S(2)}, u32[]{:S(2)}) collective-permute-start(bf16[48,1792]{1,0:T(8,128)(2,1)S(1)} %constant_dynamic-slice_fusion.1), channel_id=1, source_target_pairs={{0,16},{4,20},{8,24},{12,28},{16,0},{20,4},{24,8},{28,12},{1,17},{... | collective-permute-start | bytes 516104 | tf_op jit(solution)/shard_map/ppermute | solution.py:39
  41.1 1.6 %collective-permute-start.8 = (bf16[24,1792]{1,0:T(8,128)(2,1)S(1)}, bf16[24,1792]{1,0:T(8,128)(2,1)S(1)}, u32[]{:S(2)}, u32[]{:S(2)}) collective-permute-start(bf16[24,1792]{1,0:T(8,128)(2,1)S(1)} %constant_dynamic-slice_fusion.12), channel_id=1, source_target_pairs={{0,16},{4,20},{8,24},{12,28},{16,0},{20,4},{24,8},{28,12},{1,17},{... | collective-permute-start | bytes 258056 | tf_op jit(solution)/shard_map/ppermute | solution.py:39
  43.1 1.5 %collective-permute-start.27 = (bf16[24,1792]{1,0:T(8,128)(2,1)S(1)}, bf16[24,1792]{1,0:T(8,128)(2,1)S(1)}, u32[]{:S(2)}, u32[]{:S(2)}) collective-permute-start(bf16[24,1792]{1,0:T(8,128)(2,1)S(1)} %constant_dynamic-slice_fusion.3), channel_id=1, source_target_pairs={{0,8},{4,12},{8,0},{12,4},{16,24},{20,28},{24,16},{28,20},{1,9},{5... | collective-permute-start | bytes 258056 | tf_op jit(solution)/shard_map/ppermute | solution.py:39
  44.8 1.6 %collective-permute-start.5 = (bf16[24,1792]{1,0:T(8,128)(2,1)S(1)}, bf16[24,1792]{1,0:T(8,128)(2,1)S(1)}, u32[]{:S(2)}, u32[]{:S(2)}) collective-permute-start(bf16[24,1792]{1,0:T(8,128)(2,1)S(1)} %constant_dynamic-slice_fusion.15), channel_id=1, source_target_pairs={{0,16},{4,20},{8,24},{12,28},{16,0},{20,4},{24,8},{28,12},{1,17},{... | collective-permute-start | bytes 258056 | tf_op jit(solution)/shard_map/ppermute | solution.py:39
  46.8 1.5 %collective-permute-start.24 = (bf16[24,1792]{1,0:T(8,128)(2,1)S(1)}, bf16[24,1792]{1,0:T(8,128)(2,1)S(1)}, u32[]{:S(2)}, u32[]{:S(2)}) collective-permute-start(bf16[24,1792]{1,0:T(8,128)(2,1)S(1)} %constant_dynamic-slice_fusion.6), channel_id=1, source_target_pairs={{0,8},{4,12},{8,0},{12,4},{16,24},{20,28},{24,16},{28,20},{1,9},{5... | collective-permute-start | bytes 258056 | tf_op jit(solution)/shard_map/ppermute | solution.py:39
  48.5 1.6 %collective-permute-start.16 = (bf16[24,1792]{1,0:T(8,128)(2,1)S(1)}, bf16[24,1792]{1,0:T(8,128)(2,1)S(1)}, u32[]{:S(2)}, u32[]{:S(2)}) collective-permute-start(bf16[24,1792]{1,0:T(8,128)(2,1)S(1)} %constant_dynamic-slice_fusion.9), channel_id=1, source_target_pairs={{0,16},{4,20},{8,24},{12,28},{16,0},{20,4},{24,8},{28,12},{1,17},{... | collective-permute-start | bytes 258056 | tf_op jit(solution)/shard_map/ppermute | solution.py:39
  50.7 1.2 %collective-permute-done.5 = bf16[24,1792]{1,0:T(8,128)(2,1)S(1)} collective-permute-done((bf16[24,1792]{1,0:T(8,128)(2,1)S(1)}, bf16[24,1792]{1,0:T(8,128)(2,1)S(1)}, u32[]{:S(2)}, u32[]{:S(2)}) %collective-permute-start.5) | collective-permute-done | bytes 86048 | tf_op jit(solution)/shard_map/ppermute | solution.py:39
  51.9 1.1 collective-permute-done.16
  53.1 1.6 %collective-permute-start.9 = (bf16[24,1792]{1,0:T(8,128)(2,1)S(1)}, bf16[24,1792]{1,0:T(8,128)(2,1)S(1)}, u32[]{:S(2)}, u32[]{:S(2)}) collective-permute-start(bf16[24,1792]{1,0:T(8,128)(2,1)S(1)} %get-tuple-element.36), channel_id=1, source_target_pairs={{0,16},{4,20},{8,24},{12,28},{16,0},{20,4},{24,8},{28,12},{1,17},{... | collective-permute-start | bytes 258056 | tf_op jit(solution)/shard_map/ppermute | solution.py:73
  54.8 0.5 collective-permute-start.17
  55.2 1.6 %collective-permute-start.19 = (bf16[24,1792]{1,0:T(8,128)(2,1)S(1)}, bf16[24,1792]{1,0:T(8,128)(2,1)S(1)}, u32[]{:S(2)}, u32[]{:S(2)}) collective-permute-start(bf16[24,1792]{1,0:T(8,128)(2,1)S(1)} %get-tuple-element.38), channel_id=1, source_target_pairs={{0,16},{4,20},{8,24},{12,28},{16,0},{20,4},{24,8},{28,12},{1,17},{... | collective-permute-start | bytes 258056 | tf_op jit(solution)/shard_map/ppermute | solution.py:73
  57.0 0.6 collective-permute-start.28
  57.5 1.5 %collective-permute-start.33 = (bf16[24,1792]{1,0:T(8,128)(2,1)S(1)}, bf16[24,1792]{1,0:T(8,128)(2,1)S(1)}, u32[]{:S(2)}, u32[]{:S(2)}) collective-permute-start(bf16[24,1792]{1,0:T(8,128)(2,1)S(1)} %get-tuple-element.34), channel_id=1, source_target_pairs={{0,8},{4,12},{8,0},{12,4},{16,24},{20,28},{24,16},{28,20},{1,9},{5... | collective-permute-start | bytes 258056 | tf_op jit(solution)/shard_map/ppermute | solution.py:73
  59.1 1.4 %collective-permute-done.19 = bf16[24,1792]{1,0:T(8,128)(2,1)S(1)} collective-permute-done((bf16[24,1792]{1,0:T(8,128)(2,1)S(1)}, bf16[24,1792]{1,0:T(8,128)(2,1)S(1)}, u32[]{:S(2)}, u32[]{:S(2)}) %collective-permute-start.19) | collective-permute-done | bytes 86048 | tf_op jit(solution)/shard_map/ppermute | solution.py:73
  60.5 0.6 collective-permute-start.35
  61.1 1.5 %collective-permute-start.20 = (bf16[48,1792]{1,0:T(8,128)(2,1)S(1)}, bf16[48,1792]{1,0:T(8,128)(2,1)S(1)}, u32[]{:S(2)}, u32[]{:S(2)}) collective-permute-start(bf16[48,1792]{1,0:T(8,128)(2,1)S(1)} %maximum_select_fusion.10), channel_id=1, source_target_pairs={{0,8},{4,12},{8,0},{12,4},{16,24},{20,28},{24,16},{28,20},{1,9},{5... | collective-permute-start | bytes 516104 | tf_op jit(solution)/shard_map/ppermute | solution.py:73
  62.7 0.7 collective-permute-start.18
  63.4 2.5 %collective-permute-done.35 = bf16[24,1792]{1,0:T(8,128)(2,1)S(1)} collective-permute-done((bf16[24,1792]{1,0:T(8,128)(2,1)S(1)}, bf16[24,1792]{1,0:T(8,128)(2,1)S(1)}, u32[]{:S(2)}, u32[]{:S(2)}) %collective-permute-start.35) | collective-permute-done | bytes 86048 | tf_op jit(solution)/shard_map/ppermute | solution.py:73
  65.9 0.6 collective-permute-start.10
  66.5 1.3 %collective-permute-start.36 = (bf16[48,1792]{1,0:T(8,128)(2,1)S(1)}, bf16[48,1792]{1,0:T(8,128)(2,1)S(1)}, u32[]{:S(2)}, u32[]{:S(2)}) collective-permute-start(bf16[48,1792]{1,0:T(8,128)(2,1)S(1)} %maximum_select_fusion.13), channel_id=1, source_target_pairs={{0,16},{4,20},{8,24},{12,28},{16,0},{20,4},{24,8},{28,12},{1,17},{... | collective-permute-start | bytes 516104 | tf_op jit(solution)/shard_map/ppermute | solution.py:73
  67.8 0.9 collective-permute-start.34
  68.8 0.8 collective-permute-done.20
  69.6 1.2 %collective-permute-start.29 = (bf16[48,1792]{1,0:T(8,128)(2,1)S(1)}, bf16[48,1792]{1,0:T(8,128)(2,1)S(1)}, u32[]{:S(2)}, u32[]{:S(2)}) collective-permute-start(bf16[48,1792]{1,0:T(8,128)(2,1)S(1)} %maximum_select_fusion.11), channel_id=1, source_target_pairs={{0,16},{4,20},{8,24},{12,28},{16,0},{20,4},{24,8},{28,12},{1,17},{... | collective-permute-start | bytes 516104 | tf_op jit(solution)/shard_map/ppermute | solution.py:73
  70.8 2.4 %collective-permute-done.18 = bf16[48,1792]{1,0:T(8,128)(2,1)S(1)} collective-permute-done((bf16[48,1792]{1,0:T(8,128)(2,1)S(1)}, bf16[48,1792]{1,0:T(8,128)(2,1)S(1)}, u32[]{:S(2)}, u32[]{:S(2)}) %collective-permute-start.18) | collective-permute-done | bytes 172064 | tf_op jit(solution)/shard_map/ppermute | solution.py:73
  73.3 2.0 %collective-permute-done.10 = bf16[48,1792]{1,0:T(8,128)(2,1)S(1)} collective-permute-done((bf16[48,1792]{1,0:T(8,128)(2,1)S(1)}, bf16[48,1792]{1,0:T(8,128)(2,1)S(1)}, u32[]{:S(2)}, u32[]{:S(2)}) %collective-permute-start.10) | collective-permute-done | bytes 172064 | tf_op jit(solution)/shard_map/ppermute | solution.py:73
  75.4 1.1 pad_maximum_fusion.1
  76.6 0.5 collective-permute-done.29
  77.1 1.1 pad_maximum_fusion.2
  78.3 1.0 collective-permute-done.21
  79.3 0.5 maximum_select_fusion
  79.8 1.4 %collective-permute-done.37 = bf16[3,96,1792]{2,1,0:T(8,128)(2,1)} collective-permute-done((bf16[3,96,1792]{2,1,0:T(8,128)(2,1)}, bf16[3,96,1792]{2,1,0:T(8,128)(2,1)}, u32[]{:S(2)}, u32[]{:S(2)}) %collective-permute-start.37) | collective-permute-done | bytes 1032224 | tf_op jit(solution)/shard_map/ppermute | solution.py:70
  81.2 1.9 %maximum_select_fusion.1 = bf16[3,192,1792]{2,1,0:T(8,128)(2,1)S(1)} fusion(bf16[1,96,1792]{2,1,0:T(8,128)(2,1)S(1)} %maximum_select_fusion.7, bf16[1,96,1792]{2,1,0:T(8,128)(2,1)S(1)} %maximum_select_fusion.6, bf16[1,96,1792]{2,1,0:T(8,128)(2,1)S(1)} %maximum_select_fusion.5, bf16[3,96,1792]{2,1,0:T(8,128)(2,1)} %collective-permute-done.37, pred[]{:T(512)S(6)} %eq.33), kind=kLoop, calls=%fused_computation.11 | loop fusion | flops 17547264 | bytes 4128769 | tf_op jit(solution)/shard_map/jit(_where)/select_n | solution.py:71
  83.1 0.4 fusion.4
  83.5 1.5 %slice-done.3 = s8[3145728]{0:T(1024)(128)(4,1)S(1)} async-done(((s8[7340032]{0:T(1024)(128)(4,1)}), s8[3145728]{0:T(1024)(128)(4,1)S(1)}, s32[]{:S(2)}) %slice-start.3) | async-done | bytes 3145752
  85.0 2.5 %fusion.10 = f32[192,1024]{1,0:T(8,128)S(1)} fusion(bf16[192,3584]{1,0:T(8,128)(2,1)S(1)} %get-tuple-element.22, bf16[1024,3584]{1,0:T(8,128)(2,1)S(1)} %bitcast.49), kind=kOutput, calls=%fused_computation.88 | convolution fusion | flops 1409286144 | bytes 9502720 | tf_op jit(solution)/shard_map/dot_general | solution.py:14
  87.5 2.5 %fusion.5 = bf16[192,1024]{1,0:T(8,128)(2,1)S(1)} fusion(f32[192,1024]{1,0:T(8,128)S(1)} %fusion.10, bf16[192,3584]{1,0:T(8,128)(2,1)S(1)} %get-tuple-element.17, bf16[1024,3584]{1,0:T(8,128)(2,1)S(1)} %bitcast.53), kind=kOutput, calls=%fused_computation.19 | convolution fusion | flops 1409679360 | bytes 9895936 | tf_op jit(solution)/shard_map/dot_general | solution.py:14
  90.1 5.2 %convolution_convert_fusion.2 = bf16[1024,3584]{1,0:T(8,128)(2,1)} fusion(bf16[192,1024]{1,0:T(8,128)(2,1)S(1)} %pad_maximum_fusion.3, bf16[192,3584]{1,0:T(8,128)(2,1)S(1)} %get-tuple-element.17), kind=kOutput, calls=%fused_computation.2 | convolution fusion | flops 1412956160 | bytes 9109504 | tf_op jit(solution)/shard_map/dot_general | solution.py:135
  95.3 1.9 %collective-permute-start.38 = (bf16[48,1024]{1,0:T(8,128)(2,1)S(1)}, bf16[48,1024]{1,0:T(8,128)(2,1)S(1)}, u32[]{:S(2)}, u32[]{:S(2)}) collective-permute-start(bf16[48,1024]{1,0:T(8,128)(2,1)S(1)} %get-tuple-element.39), channel_id=1, source_target_pairs={{0,3},{1,0},{2,1},{3,2},{4,7},{5,4},{6,5},{7,6},{8,11},{9,8},{10,9... | collective-permute-start | bytes 294920 | tf_op jit(solution)/shard_map/ppermute | solution.py:112
  97.4 0.6 collective-permute-start.39
  98.0 5.2 %convolution_convert_fusion.1 = bf16[1024,3584]{1,0:T(8,128)(2,1)} fusion(bf16[192,1024]{1,0:T(8,128)(2,1)S(1)} %pad_maximum_fusion.3, bf16[192,3584]{1,0:T(8,128)(2,1)S(1)} %get-tuple-element.22), kind=kOutput, calls=%fused_computation.1 | convolution fusion | flops 1412956160 | bytes 9109504 | tf_op jit(solution)/shard_map/dot_general | solution.py:138
  103.2 5.2 %convolution_convert_fusion = bf16[3584,1024]{1,0:T(8,128)(2,1)} fusion(bf16[192,3584]{1,0:T(8,128)(2,1)S(1)} %get-tuple-element.23, bf16[192,1024]{1,0:T(8,128)(2,1)S(1)} %copy-done.1), kind=kOutput, calls=%fused_computation | convolution fusion | flops 1412956160 | bytes 9109504 | tf_op jit(solution)/shard_map/dot_general | solution.py:8
  108.4 0.7 add_convert_fusion.12
  (111 shorter events, 4.6 us)
Async XLA Ops:
  0.6 12.2 %collective-permute-start.1 = (bf16[48,1024]{1,0:T(8,128)(2,1)}, bf16[48,1024]{1,0:T(8,128)(2,1)S(1)}, u32[]{:S(2)}, u32[]{:S(2)}) collective-permute-start(bf16[48,1024]{1,0:T(8,128)(2,1)} %param.5), channel_id=1, source_target_pairs={{0,2},{1,3},{2,0},{3,1},{4,6},{5,7},{6,4},{7,5},{8,10},{9,11},{10,... | collective-permute-start | bytes 294920 | tf_op jit(solution)/shard_map/ppermute | solution.py:104
  4.8 8.1 %collective-permute-start = (bf16[48,1024]{1,0:T(8,128)(2,1)}, bf16[48,1024]{1,0:T(8,128)(2,1)S(1)}, u32[]{:S(2)}, u32[]{:S(2)}) collective-permute-start(bf16[48,1024]{1,0:T(8,128)(2,1)} %param.5), channel_id=1, source_target_pairs={{0,1},{1,2},{2,3},{3,0},{4,5},{5,6},{6,7},{7,4},{8,9},{9,10},{10,1... | collective-permute-start | bytes 294920 | tf_op jit(solution)/shard_map/ppermute | solution.py:104
  6.3 7.2 %collective-permute-start.2 = (bf16[48,1024]{1,0:T(8,128)(2,1)}, bf16[48,1024]{1,0:T(8,128)(2,1)S(1)}, u32[]{:S(2)}, u32[]{:S(2)}) collective-permute-start(bf16[48,1024]{1,0:T(8,128)(2,1)} %param.5), channel_id=1, source_target_pairs={{0,3},{1,0},{2,1},{3,2},{4,7},{5,4},{6,5},{7,6},{8,11},{9,8},{10,9... | collective-permute-start | bytes 294920 | tf_op jit(solution)/shard_map/ppermute | solution.py:104
  13.6 11.8 %slice-start.4 = ((s8[7340032]{0:T(1024)(128)(4,1)}), s8[4194304]{0:T(1024)(128)(4,1)S(1)}, s32[]{:S(2)}) async-start(s8[7340032]{0:T(1024)(128)(4,1)} %bitcast.50), calls=%async_computation.4 | async-start | bytes 8388608
  14.6 10.7 %slice-start.5 = ((s8[7340032]{0:T(1024)(128)(4,1)}), s8[3145728]{0:T(1024)(128)(4,1)S(1)}, s32[]{:S(2)}) async-start(s8[7340032]{0:T(1024)(128)(4,1)} %bitcast.50), calls=%async_computation.5 | async-start | bytes 6291456
  14.7 13.9 %collective-permute-start.13 = (bf16[48,1024]{1,0:T(8,128)(2,1)}, bf16[48,1024]{1,0:T(8,128)(2,1)S(1)}, u32[]{:S(2)}, u32[]{:S(2)}) collective-permute-start(bf16[48,1024]{1,0:T(8,128)(2,1)} %param.6), channel_id=1, source_target_pairs={{0,3},{1,0},{2,1},{3,2},{4,7},{5,4},{6,5},{7,6},{8,11},{9,8},{10,9... | collective-permute-start | bytes 294920 | tf_op jit(solution)/shard_map/ppermute | solution.py:104
  16.8 11.3 %collective-permute-start.12 = (bf16[48,1024]{1,0:T(8,128)(2,1)}, bf16[48,1024]{1,0:T(8,128)(2,1)S(1)}, u32[]{:S(2)}, u32[]{:S(2)}) collective-permute-start(bf16[48,1024]{1,0:T(8,128)(2,1)} %param.6), channel_id=1, source_target_pairs={{0,2},{1,3},{2,0},{3,1},{4,6},{5,7},{6,4},{7,5},{8,10},{9,11},{10,... | collective-permute-start | bytes 294920 | tf_op jit(solution)/shard_map/ppermute | solution.py:104
  18.0 10.0 %collective-permute-start.11 = (bf16[48,1024]{1,0:T(8,128)(2,1)}, bf16[48,1024]{1,0:T(8,128)(2,1)S(1)}, u32[]{:S(2)}, u32[]{:S(2)}) collective-permute-start(bf16[48,1024]{1,0:T(8,128)(2,1)} %param.6), channel_id=1, source_target_pairs={{0,1},{1,2},{2,3},{3,0},{4,5},{5,6},{6,7},{7,4},{8,9},{9,10},{10,1... | collective-permute-start | bytes 294920 | tf_op jit(solution)/shard_map/ppermute | solution.py:104
  24.7 3.9 %slice-start = ((s8[7340032]{0:T(1024)(128)(4,1)}), s8[4194304]{0:T(1024)(128)(4,1)S(1)}, s32[]{:S(2)}) async-start(s8[7340032]{0:T(1024)(128)(4,1)} %bitcast.46), calls=%async_computation | async-start | bytes 8388608
  24.8 3.9 %slice-start.1 = ((s8[7340032]{0:T(1024)(128)(4,1)}), s8[3145728]{0:T(1024)(128)(4,1)S(1)}, s32[]{:S(2)}) async-start(s8[7340032]{0:T(1024)(128)(4,1)} %bitcast.46), calls=%async_computation.1 | async-start | bytes 6291456
  24.8 6.7 %collective-permute-start.6 = (bf16[96,1792]{1,0:T(8,128)(2,1)S(1)}, bf16[96,1792]{1,0:T(8,128)(2,1)S(1)}, u32[]{:S(2)}, u32[]{:S(2)}) collective-permute-start(bf16[96,1792]{1,0:T(8,128)(2,1)S(1)} %constant_dynamic-slice_fusion.14), channel_id=1, source_target_pairs={{0,4},{4,0},{8,12},{12,8},{16,20},{20,16},{24,28},{28,24},{1,5},{5... | collective-permute-start | bytes 1032200 | tf_op jit(solution)/shard_map/ppermute | solution.py:39
  24.9 7.3 %collective-permute-start.25 = (bf16[96,1792]{1,0:T(8,128)(2,1)S(1)}, bf16[96,1792]{1,0:T(8,128)(2,1)S(1)}, u32[]{:S(2)}, u32[]{:S(2)}) collective-permute-start(bf16[96,1792]{1,0:T(8,128)(2,1)S(1)} %constant_dynamic-slice_fusion.5), channel_id=1, source_target_pairs={{0,4},{4,0},{8,12},{12,8},{16,20},{20,16},{24,28},{28,24},{1,5},{5... | collective-permute-start | bytes 1032200 | tf_op jit(solution)/shard_map/ppermute | solution.py:39
  27.0 0.9 copy-start.2
  27.9 5.9 %collective-permute-start.3 = (bf16[96,1792]{1,0:T(8,128)(2,1)S(1)}, bf16[96,1792]{1,0:T(8,128)(2,1)S(1)}, u32[]{:S(2)}, u32[]{:S(2)}) collective-permute-start(bf16[96,1792]{1,0:T(8,128)(2,1)S(1)} %constant_dynamic-slice_fusion.17), channel_id=1, source_target_pairs={{0,4},{4,0},{8,12},{12,8},{16,20},{20,16},{24,28},{28,24},{1,5},{5... | collective-permute-start | bytes 1032200 | tf_op jit(solution)/shard_map/ppermute | solution.py:39
  28.1 7.5 %collective-permute-start.22 = (bf16[96,1792]{1,0:T(8,128)(2,1)S(1)}, bf16[96,1792]{1,0:T(8,128)(2,1)S(1)}, u32[]{:S(2)}, u32[]{:S(2)}) collective-permute-start(bf16[96,1792]{1,0:T(8,128)(2,1)S(1)} %constant_dynamic-slice_fusion.8), channel_id=1, source_target_pairs={{0,4},{4,0},{8,12},{12,8},{16,20},{20,16},{24,28},{28,24},{1,5},{5... | collective-permute-start | bytes 1032200 | tf_op jit(solution)/shard_map/ppermute | solution.py:39
  28.6 2.6 %copy-start = (bf16[192,1024]{1,0:T(8,128)(2,1)}, bf16[192,1024]{1,0:T(8,128)(2,1)S(1)}, u32[]{:S(2)}) copy-start(bf16[192,1024]{1,0:T(8,128)(2,1)S(1)} %constant_dynamic-update-slice_fusion) | copy-start | bytes 1179652
  31.4 4.9 %collective-permute-start.14 = (bf16[96,1792]{1,0:T(8,128)(2,1)S(1)}, bf16[96,1792]{1,0:T(8,128)(2,1)S(1)}, u32[]{:S(2)}, u32[]{:S(2)}) collective-permute-start(bf16[96,1792]{1,0:T(8,128)(2,1)S(1)} %constant_dynamic-slice_fusion.11), channel_id=1, source_target_pairs={{0,4},{4,0},{8,12},{12,8},{16,20},{20,16},{24,28},{28,24},{1,5},{5... | collective-permute-start | bytes 1032200 | tf_op jit(solution)/shard_map/ppermute | solution.py:39
  31.5 5.5 %collective-permute-start.30 = (bf16[96,1792]{1,0:T(8,128)(2,1)S(1)}, bf16[96,1792]{1,0:T(8,128)(2,1)S(1)}, u32[]{:S(2)}, u32[]{:S(2)}) collective-permute-start(bf16[96,1792]{1,0:T(8,128)(2,1)S(1)} %constant_dynamic-slice_fusion.2), channel_id=1, source_target_pairs={{0,4},{4,0},{8,12},{12,8},{16,20},{20,16},{24,28},{28,24},{1,5},{5... | collective-permute-start | bytes 1032200 | tf_op jit(solution)/shard_map/ppermute | solution.py:39
  32.2 7.3 %collective-permute-start.7 = (bf16[48,1792]{1,0:T(8,128)(2,1)S(1)}, bf16[48,1792]{1,0:T(8,128)(2,1)S(1)}, u32[]{:S(2)}, u32[]{:S(2)}) collective-permute-start(bf16[48,1792]{1,0:T(8,128)(2,1)S(1)} %constant_dynamic-slice_fusion.13), channel_id=1, source_target_pairs={{0,8},{4,12},{8,0},{12,4},{16,24},{20,28},{24,16},{28,20},{1,9},{5... | collective-permute-start | bytes 516104 | tf_op jit(solution)/shard_map/ppermute | solution.py:39
  33.8 7.3 %collective-permute-start.26 = (bf16[48,1792]{1,0:T(8,128)(2,1)S(1)}, bf16[48,1792]{1,0:T(8,128)(2,1)S(1)}, u32[]{:S(2)}, u32[]{:S(2)}) collective-permute-start(bf16[48,1792]{1,0:T(8,128)(2,1)S(1)} %constant_dynamic-slice_fusion.4), channel_id=1, source_target_pairs={{0,16},{4,20},{8,24},{12,28},{16,0},{20,4},{24,8},{28,12},{1,17},{... | collective-permute-start | bytes 516104 | tf_op jit(solution)/shard_map/ppermute | solution.py:39
  35.6 7.5 %collective-permute-start.4 = (bf16[48,1792]{1,0:T(8,128)(2,1)S(1)}, bf16[48,1792]{1,0:T(8,128)(2,1)S(1)}, u32[]{:S(2)}, u32[]{:S(2)}) collective-permute-start(bf16[48,1792]{1,0:T(8,128)(2,1)S(1)} %constant_dynamic-slice_fusion.16), channel_id=1, source_target_pairs={{0,8},{4,12},{8,0},{12,4},{16,24},{20,28},{24,16},{28,20},{1,9},{5... | collective-permute-start | bytes 516104 | tf_op jit(solution)/shard_map/ppermute | solution.py:39
  36.3 8.6 %collective-permute-start.23 = (bf16[48,1792]{1,0:T(8,128)(2,1)S(1)}, bf16[48,1792]{1,0:T(8,128)(2,1)S(1)}, u32[]{:S(2)}, u32[]{:S(2)}) collective-permute-start(bf16[48,1792]{1,0:T(8,128)(2,1)S(1)} %constant_dynamic-slice_fusion.7), channel_id=1, source_target_pairs={{0,16},{4,20},{8,24},{12,28},{16,0},{20,4},{24,8},{28,12},{1,17},{... | collective-permute-start | bytes 516104 | tf_op jit(solution)/shard_map/ppermute | solution.py:39
  37.0 9.8 %collective-permute-start.15 = (bf16[48,1792]{1,0:T(8,128)(2,1)S(1)}, bf16[48,1792]{1,0:T(8,128)(2,1)S(1)}, u32[]{:S(2)}, u32[]{:S(2)}) collective-permute-start(bf16[48,1792]{1,0:T(8,128)(2,1)S(1)} %constant_dynamic-slice_fusion.10), channel_id=1, source_target_pairs={{0,8},{4,12},{8,0},{12,4},{16,24},{20,28},{24,16},{28,20},{1,9},{5... | collective-permute-start | bytes 516104 | tf_op jit(solution)/shard_map/ppermute | solution.py:39
  39.4 9.1 %collective-permute-start.31 = (bf16[48,1792]{1,0:T(8,128)(2,1)S(1)}, bf16[48,1792]{1,0:T(8,128)(2,1)S(1)}, u32[]{:S(2)}, u32[]{:S(2)}) collective-permute-start(bf16[48,1792]{1,0:T(8,128)(2,1)S(1)} %constant_dynamic-slice_fusion.1), channel_id=1, source_target_pairs={{0,16},{4,20},{8,24},{12,28},{16,0},{20,4},{24,8},{28,12},{1,17},{... | collective-permute-start | bytes 516104 | tf_op jit(solution)/shard_map/ppermute | solution.py:39
  41.1 9.2 %collective-permute-start.8 = (bf16[24,1792]{1,0:T(8,128)(2,1)S(1)}, bf16[24,1792]{1,0:T(8,128)(2,1)S(1)}, u32[]{:S(2)}, u32[]{:S(2)}) collective-permute-start(bf16[24,1792]{1,0:T(8,128)(2,1)S(1)} %constant_dynamic-slice_fusion.12), channel_id=1, source_target_pairs={{0,16},{4,20},{8,24},{12,28},{16,0},{20,4},{24,8},{28,12},{1,17},{... | collective-permute-start | bytes 258056 | tf_op jit(solution)/shard_map/ppermute | solution.py:39
  43.1 12.1 %collective-permute-start.27 = (bf16[24,1792]{1,0:T(8,128)(2,1)S(1)}, bf16[24,1792]{1,0:T(8,128)(2,1)S(1)}, u32[]{:S(2)}, u32[]{:S(2)}) collective-permute-start(bf16[24,1792]{1,0:T(8,128)(2,1)S(1)} %constant_dynamic-slice_fusion.3), channel_id=1, source_target_pairs={{0,8},{4,12},{8,0},{12,4},{16,24},{20,28},{24,16},{28,20},{1,9},{5... | collective-permute-start | bytes 258056 | tf_op jit(solution)/shard_map/ppermute | solution.py:39
  44.8 7.1 %collective-permute-start.5 = (bf16[24,1792]{1,0:T(8,128)(2,1)S(1)}, bf16[24,1792]{1,0:T(8,128)(2,1)S(1)}, u32[]{:S(2)}, u32[]{:S(2)}) collective-permute-start(bf16[24,1792]{1,0:T(8,128)(2,1)S(1)} %constant_dynamic-slice_fusion.15), channel_id=1, source_target_pairs={{0,16},{4,20},{8,24},{12,28},{16,0},{20,4},{24,8},{28,12},{1,17},{... | collective-permute-start | bytes 258056 | tf_op jit(solution)/shard_map/ppermute | solution.py:39
  46.8 10.0 %collective-permute-start.24 = (bf16[24,1792]{1,0:T(8,128)(2,1)S(1)}, bf16[24,1792]{1,0:T(8,128)(2,1)S(1)}, u32[]{:S(2)}, u32[]{:S(2)}) collective-permute-start(bf16[24,1792]{1,0:T(8,128)(2,1)S(1)} %constant_dynamic-slice_fusion.6), channel_id=1, source_target_pairs={{0,8},{4,12},{8,0},{12,4},{16,24},{20,28},{24,16},{28,20},{1,9},{5... | collective-permute-start | bytes 258056 | tf_op jit(solution)/shard_map/ppermute | solution.py:39
  48.5 4.5 %collective-permute-start.16 = (bf16[24,1792]{1,0:T(8,128)(2,1)S(1)}, bf16[24,1792]{1,0:T(8,128)(2,1)S(1)}, u32[]{:S(2)}, u32[]{:S(2)}) collective-permute-start(bf16[24,1792]{1,0:T(8,128)(2,1)S(1)} %constant_dynamic-slice_fusion.9), channel_id=1, source_target_pairs={{0,16},{4,20},{8,24},{12,28},{16,0},{20,4},{24,8},{28,12},{1,17},{... | collective-permute-start | bytes 258056 | tf_op jit(solution)/shard_map/ppermute | solution.py:39
  50.3 6.5 %collective-permute-start.32 = (bf16[24,1792]{1,0:T(8,128)(2,1)S(1)}, bf16[24,1792]{1,0:T(8,128)(2,1)S(1)}, u32[]{:S(2)}, u32[]{:S(2)}) collective-permute-start(bf16[24,1792]{1,0:T(8,128)(2,1)S(1)} %constant_dynamic-slice_fusion), channel_id=1, source_target_pairs={{0,8},{4,12},{8,0},{12,4},{16,24},{20,28},{24,16},{28,20},{1,9},{5... | collective-permute-start | bytes 258056 | tf_op jit(solution)/shard_map/ppermute | solution.py:39
  53.1 9.5 %collective-permute-start.9 = (bf16[24,1792]{1,0:T(8,128)(2,1)S(1)}, bf16[24,1792]{1,0:T(8,128)(2,1)S(1)}, u32[]{:S(2)}, u32[]{:S(2)}) collective-permute-start(bf16[24,1792]{1,0:T(8,128)(2,1)S(1)} %get-tuple-element.36), channel_id=1, source_target_pairs={{0,16},{4,20},{8,24},{12,28},{16,0},{20,4},{24,8},{28,12},{1,17},{... | collective-permute-start | bytes 258056 | tf_op jit(solution)/shard_map/ppermute | solution.py:73
  54.8 6.3 %collective-permute-start.17 = (bf16[24,1792]{1,0:T(8,128)(2,1)S(1)}, bf16[24,1792]{1,0:T(8,128)(2,1)S(1)}, u32[]{:S(2)}, u32[]{:S(2)}) collective-permute-start(bf16[24,1792]{1,0:T(8,128)(2,1)S(1)} %get-tuple-element.37), channel_id=1, source_target_pairs={{0,16},{4,20},{8,24},{12,28},{16,0},{20,4},{24,8},{28,12},{1,17},{... | collective-permute-start | bytes 258056 | tf_op jit(solution)/shard_map/ppermute | solution.py:73
  55.2 5.2 %collective-permute-start.19 = (bf16[24,1792]{1,0:T(8,128)(2,1)S(1)}, bf16[24,1792]{1,0:T(8,128)(2,1)S(1)}, u32[]{:S(2)}, u32[]{:S(2)}) collective-permute-start(bf16[24,1792]{1,0:T(8,128)(2,1)S(1)} %get-tuple-element.38), channel_id=1, source_target_pairs={{0,16},{4,20},{8,24},{12,28},{16,0},{20,4},{24,8},{28,12},{1,17},{... | collective-permute-start | bytes 258056 | tf_op jit(solution)/shard_map/ppermute | solution.py:73
  57.0 10.9 %collective-permute-start.28 = (bf16[24,1792]{1,0:T(8,128)(2,1)S(1)}, bf16[24,1792]{1,0:T(8,128)(2,1)S(1)}, u32[]{:S(2)}, u32[]{:S(2)}) collective-permute-start(bf16[24,1792]{1,0:T(8,128)(2,1)S(1)} %get-tuple-element.33), channel_id=1, source_target_pairs={{0,8},{4,12},{8,0},{12,4},{16,24},{20,28},{24,16},{28,20},{1,9},{5... | collective-permute-start | bytes 258056 | tf_op jit(solution)/shard_map/ppermute | solution.py:73
  57.5 9.0 %collective-permute-start.33 = (bf16[24,1792]{1,0:T(8,128)(2,1)S(1)}, bf16[24,1792]{1,0:T(8,128)(2,1)S(1)}, u32[]{:S(2)}, u32[]{:S(2)}) collective-permute-start(bf16[24,1792]{1,0:T(8,128)(2,1)S(1)} %get-tuple-element.34), channel_id=1, source_target_pairs={{0,8},{4,12},{8,0},{12,4},{16,24},{20,28},{24,16},{28,20},{1,9},{5... | collective-permute-start | bytes 258056 | tf_op jit(solution)/shard_map/ppermute | solution.py:73
  60.5 5.4 %collective-permute-start.35 = (bf16[24,1792]{1,0:T(8,128)(2,1)S(1)}, bf16[24,1792]{1,0:T(8,128)(2,1)S(1)}, u32[]{:S(2)}, u32[]{:S(2)}) collective-permute-start(bf16[24,1792]{1,0:T(8,128)(2,1)S(1)} %get-tuple-element.35), channel_id=1, source_target_pairs={{0,8},{4,12},{8,0},{12,4},{16,24},{20,28},{24,16},{28,20},{1,9},{5... | collective-permute-start | bytes 258056 | tf_op jit(solution)/shard_map/ppermute | solution.py:73
  61.1 8.5 %collective-permute-start.20 = (bf16[48,1792]{1,0:T(8,128)(2,1)S(1)}, bf16[48,1792]{1,0:T(8,128)(2,1)S(1)}, u32[]{:S(2)}, u32[]{:S(2)}) collective-permute-start(bf16[48,1792]{1,0:T(8,128)(2,1)S(1)} %maximum_select_fusion.10), channel_id=1, source_target_pairs={{0,8},{4,12},{8,0},{12,4},{16,24},{20,28},{24,16},{28,20},{1,9},{5... | collective-permute-start | bytes 516104 | tf_op jit(solution)/shard_map/ppermute | solution.py:73
  62.7 10.6 %collective-permute-start.18 = (bf16[48,1792]{1,0:T(8,128)(2,1)S(1)}, bf16[48,1792]{1,0:T(8,128)(2,1)S(1)}, u32[]{:S(2)}, u32[]{:S(2)}) collective-permute-start(bf16[48,1792]{1,0:T(8,128)(2,1)S(1)} %maximum_select_fusion.9), channel_id=1, source_target_pairs={{0,8},{4,12},{8,0},{12,4},{16,24},{20,28},{24,16},{28,20},{1,9},{5... | collective-permute-start | bytes 516104 | tf_op jit(solution)/shard_map/ppermute | solution.py:73
  65.9 9.5 %collective-permute-start.10 = (bf16[48,1792]{1,0:T(8,128)(2,1)S(1)}, bf16[48,1792]{1,0:T(8,128)(2,1)S(1)}, u32[]{:S(2)}, u32[]{:S(2)}) collective-permute-start(bf16[48,1792]{1,0:T(8,128)(2,1)S(1)} %maximum_select_fusion.8), channel_id=1, source_target_pairs={{0,8},{4,12},{8,0},{12,4},{16,24},{20,28},{24,16},{28,20},{1,9},{5... | collective-permute-start | bytes 516104 | tf_op jit(solution)/shard_map/ppermute | solution.py:73
  66.5 10.0 %collective-permute-start.36 = (bf16[48,1792]{1,0:T(8,128)(2,1)S(1)}, bf16[48,1792]{1,0:T(8,128)(2,1)S(1)}, u32[]{:S(2)}, u32[]{:S(2)}) collective-permute-start(bf16[48,1792]{1,0:T(8,128)(2,1)S(1)} %maximum_select_fusion.13), channel_id=1, source_target_pairs={{0,16},{4,20},{8,24},{12,28},{16,0},{20,4},{24,8},{28,12},{1,17},{... | collective-permute-start | bytes 516104 | tf_op jit(solution)/shard_map/ppermute | solution.py:73
  67.8 8.7 %collective-permute-start.34 = (bf16[48,1792]{1,0:T(8,128)(2,1)S(1)}, bf16[48,1792]{1,0:T(8,128)(2,1)S(1)}, u32[]{:S(2)}, u32[]{:S(2)}) collective-permute-start(bf16[48,1792]{1,0:T(8,128)(2,1)S(1)} %maximum_select_fusion.12), channel_id=1, source_target_pairs={{0,16},{4,20},{8,24},{12,28},{16,0},{20,4},{24,8},{28,12},{1,17},{... | collective-permute-start | bytes 516104 | tf_op jit(solution)/shard_map/ppermute | solution.py:73
  69.6 7.5 %collective-permute-start.29 = (bf16[48,1792]{1,0:T(8,128)(2,1)S(1)}, bf16[48,1792]{1,0:T(8,128)(2,1)S(1)}, u32[]{:S(2)}, u32[]{:S(2)}) collective-permute-start(bf16[48,1792]{1,0:T(8,128)(2,1)S(1)} %maximum_select_fusion.11), channel_id=1, source_target_pairs={{0,16},{4,20},{8,24},{12,28},{16,0},{20,4},{24,8},{28,12},{1,17},{... | collective-permute-start | bytes 516104 | tf_op jit(solution)/shard_map/ppermute | solution.py:73
  76.5 2.8 %collective-permute-start.21 = (bf16[3,96,1792]{2,1,0:T(8,128)(2,1)}, bf16[3,96,1792]{2,1,0:T(8,128)(2,1)S(1)}, u32[]{:S(2)}, u32[]{:S(2)}) collective-permute-start(bf16[3,96,1792]{2,1,0:T(8,128)(2,1)} %pad_maximum_fusion.1), channel_id=1, source_target_pairs={{0,4},{4,0},{8,12},{12,8},{16,20},{20,16},{24,28},{28,24},{1,5},{5... | collective-permute-start | bytes 3096584 | tf_op jit(solution)/shard_map/ppermute | solution.py:70
  78.2 3.0 %collective-permute-start.37 = (bf16[3,96,1792]{2,1,0:T(8,128)(2,1)}, bf16[3,96,1792]{2,1,0:T(8,128)(2,1)}, u32[]{:S(2)}, u32[]{:S(2)}) collective-permute-start(bf16[3,96,1792]{2,1,0:T(8,128)(2,1)} %pad_maximum_fusion.2), channel_id=1, source_target_pairs={{0,4},{4,0},{8,12},{12,8},{16,20},{20,16},{24,28},{28,24},{1,5},{5... | collective-permute-start | bytes 3096584 | tf_op jit(solution)/shard_map/ppermute | solution.py:70
  79.3 4.2 %slice-start.2 = ((s8[7340032]{0:T(1024)(128)(4,1)}), s8[4194304]{0:T(1024)(128)(4,1)S(1)}, s32[]{:S(2)}) async-start(s8[7340032]{0:T(1024)(128)(4,1)} %bitcast.48), calls=%async_computation.2 | async-start | bytes 8388608
  83.1 1.9 %slice-start.3 = ((s8[7340032]{0:T(1024)(128)(4,1)}), s8[3145728]{0:T(1024)(128)(4,1)S(1)}, s32[]{:S(2)}) async-start(s8[7340032]{0:T(1024)(128)(4,1)} %bitcast.48), calls=%async_computation.3 | async-start | bytes 6291456
  83.1 4.4 %slice-start.6 = ((s8[7340032]{0:T(1024)(128)(4,1)}), s8[4194304]{0:T(1024)(128)(4,1)S(1)}, s32[]{:S(2)}) async-start(s8[7340032]{0:T(1024)(128)(4,1)} %bitcast.52), calls=%async_computation.6 | async-start | bytes 8388608
  85.0 2.5 %slice-start.7 = ((s8[7340032]{0:T(1024)(128)(4,1)}), s8[3145728]{0:T(1024)(128)(4,1)S(1)}, s32[]{:S(2)}) async-start(s8[7340032]{0:T(1024)(128)(4,1)} %bitcast.52), calls=%async_computation.7 | async-start | bytes 6291456
  95.3 13.1 %collective-permute-start.38 = (bf16[48,1024]{1,0:T(8,128)(2,1)S(1)}, bf16[48,1024]{1,0:T(8,128)(2,1)S(1)}, u32[]{:S(2)}, u32[]{:S(2)}) collective-permute-start(bf16[48,1024]{1,0:T(8,128)(2,1)S(1)} %get-tuple-element.39), channel_id=1, source_target_pairs={{0,3},{1,0},{2,1},{3,2},{4,7},{5,4},{6,5},{7,6},{8,11},{9,8},{10,9... | collective-permute-start | bytes 294920 | tf_op jit(solution)/shard_map/ppermute | solution.py:112
  97.2 11.2 %collective-permute-start.40 = (bf16[48,1024]{1,0:T(8,128)(2,1)S(1)}, bf16[48,1024]{1,0:T(8,128)(2,1)S(1)}, u32[]{:S(2)}, u32[]{:S(2)}) collective-permute-start(bf16[48,1024]{1,0:T(8,128)(2,1)S(1)} %get-tuple-element.40), channel_id=1, source_target_pairs={{0,1},{1,2},{2,3},{3,0},{4,5},{5,6},{6,7},{7,4},{8,9},{9,10},{10,1... | collective-permute-start | bytes 294920 | tf_op jit(solution)/shard_map/ppermute | solution.py:112
  97.4 5.8 %copy-start.1 = (bf16[192,1024]{1,0:T(8,128)(2,1)S(1)}, bf16[192,1024]{1,0:T(8,128)(2,1)}, u32[]{:S(2)}) copy-start(bf16[192,1024]{1,0:T(8,128)(2,1)} %copy-done) | copy-start | bytes 1179652
  97.4 11.0 %collective-permute-start.39 = (bf16[48,1024]{1,0:T(8,128)(2,1)S(1)}, bf16[48,1024]{1,0:T(8,128)(2,1)S(1)}, u32[]{:S(2)}, u32[]{:S(2)}) collective-permute-start(bf16[48,1024]{1,0:T(8,128)(2,1)S(1)} %get-tuple-element.41), channel_id=1, source_target_pairs={{0,2},{1,3},{2,0},{3,1},{4,6},{5,7},{6,4},{7,5},{8,10},{9,11},{10,... | collective-permute-start | bytes 294920 | tf_op jit(solution)/shard_map/ppermute | solution.py:112

commit v20 on v16

--- a/solution.py
+++ b/solution.py
@@ -126,9 +126,8 @@
     partial_grad, grad_gate, grad_up, hidden = lax.optimization_barrier(
         (partial_grad.astype(jnp.bfloat16), grad_gate, grad_up, hidden)
     )
+    grad_tokens = col_reduce_scatter(partial_grad, n_col)
     acc_gate = jnp.dot(tok_t, grad_gate, preferred_element_type=jnp.float32).astype(jnp.bfloat16)
-    partial_grad, acc_gate, grad_up, hidden = lax.optimization_barrier((partial_grad, acc_gate, grad_up, hidden))
-    grad_tokens = col_reduce_scatter(partial_grad, n_col)
     acc_up = jnp.dot(tok_t, grad_up, preferred_element_type=jnp.float32)
     acc_down = contract_first(hidden, grad_all)
     return (

time: 106 us -> 106 us (level)
  transfers between devices with their start and end apart: 33 -> 33, of which waited for: 17 -> 17; matrix products, arithmetic and copies ran while one was open for 21% -> 26% of each run, Pallas kernels for 0% -> 0%
where the time goes in v20:
time: 106 us; the launch traced here: 105 us
  starting transfers between devices  38.1 us (36%)
  matrix products  29.4 us (28%)
  waiting for transfers between devices  27 us (25%)
  other arithmetic  6.98 us (7%)
  local copies, waits for them, and re-layouts  2.8 us (3%)
  between operations  1.16 us (1%)
    ppermute x6, waiting for transfers between devices, doubling_gather(): got = lax.ppermute(cur, 'row', [(j, j ^ bit) for j in range(n_dev)])  17.7 us
    ppermute x18, starting transfers between devices, halving_reduce(): lax.ppermute(lax.dynamic_slice_in_dim(c, (1 - hi) * n, n, 0), 'row', perm)  17.3 us
    ppermute x6, starting transfers between devices, col_gather(): lax.ppermute(x, 'col', [(j, (j + s) % n_col) for j in range(n_col)])  13.2 us
    dot_general x3, matrix products, contract_last(): lax.dot_general(left, right, (((1,), (1,)), ((), ())), preferred_element_...  7.59 us
    dot_general x1, matrix products, contract_first(): lax.dot_general(left, right, (((0,), (0,)), ((), ())), preferred_element_...  5.19 us
    dot_general x1, matrix products, body(): jnp.dot(tok_t, grad_gate, preferred_element_type=jnp.float32)  5.18 us
    dot_general x1, matrix products, body(): acc_up = jnp.dot(tok_t, grad_up, preferred_element_type=jnp.float32)  5.18 us
    ppermute x6, waiting for transfers between devices, col_gather(): lax.ppermute(x, 'col', [(j, (j + s) % n_col) for j in range(n_col)])  4.99 us
  transfers between devices with their start and end apart: 33, of which 17 were waited for; matrix products, arithmetic and copies ran while one was open for 26% of the time, Pallas kernels for 0%

profile of v20, /device:TPU:0, one launch (start us, length us, event | category | flops | bytes accessed | tf_op | source)
XLA Modules:
  0.0 105.5 jit_solution(16155617456303341634)
XLA Ops:
  0.6 4.1 %collective-permute-start.1 = (bf16[48,1024]{1,0:T(8,128)(2,1)}, bf16[48,1024]{1,0:T(8,128)(2,1)S(1)}, u32[]{:S(2)}, u32[]{:S(2)}) collective-permute-start(bf16[48,1024]{1,0:T(8,128)(2,1)} %param.5), channel_id=1, source_target_pairs={{0,2},{1,3},{2,0},{3,1},{4,6},{5,7},{6,4},{7,5},{8,10},{9,11},{10,... | collective-permute-start | bytes 294920 | tf_op jit(solution)/shard_map/ppermute | solution.py:98
  4.8 1.6 %collective-permute-start = (bf16[48,1024]{1,0:T(8,128)(2,1)}, bf16[48,1024]{1,0:T(8,128)(2,1)S(1)}, u32[]{:S(2)}, u32[]{:S(2)}) collective-permute-start(bf16[48,1024]{1,0:T(8,128)(2,1)} %param.5), channel_id=1, source_target_pairs={{0,1},{1,2},{2,3},{3,0},{4,5},{5,6},{6,7},{7,4},{8,9},{9,10},{10,1... | collective-permute-start | bytes 294920 | tf_op jit(solution)/shard_map/ppermute | solution.py:98
  6.3 2.2 %collective-permute-start.2 = (bf16[48,1024]{1,0:T(8,128)(2,1)}, bf16[48,1024]{1,0:T(8,128)(2,1)S(1)}, u32[]{:S(2)}, u32[]{:S(2)}) collective-permute-start(bf16[48,1024]{1,0:T(8,128)(2,1)} %param.5), channel_id=1, source_target_pairs={{0,3},{1,0},{2,1},{3,2},{4,7},{5,4},{6,5},{7,6},{8,11},{9,8},{10,9... | collective-permute-start | bytes 294920 | tf_op jit(solution)/shard_map/ppermute | solution.py:98
  8.6 4.3 %collective-permute-done.1 = bf16[48,1024]{1,0:T(8,128)(2,1)S(1)} collective-permute-done((bf16[48,1024]{1,0:T(8,128)(2,1)}, bf16[48,1024]{1,0:T(8,128)(2,1)S(1)}, u32[]{:S(2)}, u32[]{:S(2)}) %collective-permute-start.1) | collective-permute-done | bytes 98336 | tf_op jit(solution)/shard_map/ppermute | solution.py:98
  12.9 0.7 collective-permute-done.2
  13.6 1.1 %pad_maximum_fusion.1 = bf16[192,1024]{1,0:T(8,128)(2,1)S(1)} fusion(bf16[48,1024]{1,0:T(8,128)(2,1)S(1)} %collective-permute-done.2, bf16[48,1024]{1,0:T(8,128)(2,1)S(1)} %collective-permute-done.1, bf16[48,1024]{1,0:T(8,128)(2,1)S(1)} %collective-permute-done, bf16[48,1024]{1,0:T(8,128)(2,1)} %param.5), kind=kLoop, calls=%fused_computation.30 | loop fusion | flops 1572864 | bytes 786432 | tf_op jit(solution)/shard_map/concatenate | solution.py:99
  14.7 2.1 %collective-permute-start.11 = (bf16[48,1024]{1,0:T(8,128)(2,1)}, bf16[48,1024]{1,0:T(8,128)(2,1)S(1)}, u32[]{:S(2)}, u32[]{:S(2)}) collective-permute-start(bf16[48,1024]{1,0:T(8,128)(2,1)} %param.6), channel_id=1, source_target_pairs={{0,3},{1,0},{2,1},{3,2},{4,7},{5,4},{6,5},{7,6},{8,11},{9,8},{10,9... | collective-permute-start | bytes 294920 | tf_op jit(solution)/shard_map/ppermute | solution.py:98
  16.8 1.2 %collective-permute-start.10 = (bf16[48,1024]{1,0:T(8,128)(2,1)}, bf16[48,1024]{1,0:T(8,128)(2,1)S(1)}, u32[]{:S(2)}, u32[]{:S(2)}) collective-permute-start(bf16[48,1024]{1,0:T(8,128)(2,1)} %param.6), channel_id=1, source_target_pairs={{0,2},{1,3},{2,0},{3,1},{4,6},{5,7},{6,4},{7,5},{8,10},{9,11},{10,... | collective-permute-start | bytes 294920 | tf_op jit(solution)/shard_map/ppermute | solution.py:98
  17.9 1.9 %collective-permute-start.9 = (bf16[48,1024]{1,0:T(8,128)(2,1)}, bf16[48,1024]{1,0:T(8,128)(2,1)S(1)}, u32[]{:S(2)}, u32[]{:S(2)}) collective-permute-start(bf16[48,1024]{1,0:T(8,128)(2,1)} %param.6), channel_id=1, source_target_pairs={{0,1},{1,2},{2,3},{3,0},{4,5},{5,6},{6,7},{7,4},{8,9},{9,10},{10,1... | collective-permute-start | bytes 294920 | tf_op jit(solution)/shard_map/ppermute | solution.py:98
  19.9 4.7 %convolution_convert_fusion.4 = bf16[192,3584]{1,0:T(8,128)(2,1)S(1)} fusion(bf16[192,1024]{1,0:T(8,128)(2,1)S(1)} %pad_maximum_fusion.1, bf16[1024,3584]{1,0:T(8,128)(2,1)} %param.8), kind=kOutput, calls=%fused_computation.4 | convolution fusion | flops 1409974272 | bytes 9109504 | tf_op jit(solution)/shard_map/dot_general | solution.py:120
  24.9 0.5 collective-permute-start.21
  25.4 1.6 %convolution_convert_fusion.5 = bf16[192,3584]{1,0:T(8,128)(2,1)S(1)} fusion(bf16[192,1024]{1,0:T(8,128)(2,1)S(1)} %pad_maximum_fusion.1, bf16[1024,3584]{1,0:T(8,128)(2,1)S(1)} %bitcast.39), kind=kOutput, calls=%fused_computation.5 | convolution fusion | flops 1409974272 | bytes 9109504 | tf_op jit(solution)/shard_map/dot_general | solution.py:119
  27.2 0.7 copy-done.2
  27.9 0.1 collective-permute-start.3
  28.1 0.5 collective-permute-start.18
  28.6 2.6 %convolution_convert_fusion.3 = bf16[192,3584]{1,0:T(8,128)(2,1)S(1)} fusion(bf16[192,1024]{1,0:T(8,128)(2,1)S(1)} %constant_dynamic-update-slice_fusion, bf16[3584,1024]{1,0:T(8,128)(2,1)S(1)} %bitcast.35), kind=kOutput, calls=%fused_computation.3 | convolution fusion | flops 1409974272 | bytes 9109504 | tf_op jit(solution)/shard_map/dot_general | solution.py:14
  31.4 0.1 collective-permute-start.12
  31.5 0.5 collective-permute-start.24
  32.2 1.5 %collective-permute-start.7 = (bf16[48,1792]{1,0:T(8,128)(2,1)S(1)}, bf16[48,1792]{1,0:T(8,128)(2,1)S(1)}, u32[]{:S(2)}, u32[]{:S(2)}) collective-permute-start(bf16[48,1792]{1,0:T(8,128)(2,1)S(1)} %constant_dynamic-slice_fusion.13), channel_id=1, source_target_pairs={{0,8},{4,12},{8,0},{12,4},{16,24},{20,28},{24,16},{28,20},{1,9},{5... | collective-permute-start | bytes 516104 | tf_op jit(solution)/shard_map/ppermute | solution.py:39
  33.8 1.6 %collective-permute-start.22 = (bf16[48,1792]{1,0:T(8,128)(2,1)S(1)}, bf16[48,1792]{1,0:T(8,128)(2,1)S(1)}, u32[]{:S(2)}, u32[]{:S(2)}) collective-permute-start(bf16[48,1792]{1,0:T(8,128)(2,1)S(1)} %constant_dynamic-slice_fusion.4), channel_id=1, source_target_pairs={{0,16},{4,20},{8,24},{12,28},{16,0},{20,4},{24,8},{28,12},{1,17},{... | collective-permute-start | bytes 516104 | tf_op jit(solution)/shard_map/ppermute | solution.py:39
  35.6 0.6 collective-permute-start.4
  36.3 0.6 collective-permute-start.19
  37.0 1.5 %collective-permute-start.13 = (bf16[48,1792]{1,0:T(8,128)(2,1)S(1)}, bf16[48,1792]{1,0:T(8,128)(2,1)S(1)}, u32[]{:S(2)}, u32[]{:S(2)}) collective-permute-start(bf16[48,1792]{1,0:T(8,128)(2,1)S(1)} %constant_dynamic-slice_fusion.10), channel_id=1, source_target_pairs={{0,8},{4,12},{8,0},{12,4},{16,24},{20,28},{24,16},{28,20},{1,9},{5... | collective-permute-start | bytes 516104 | tf_op jit(solution)/shard_map/ppermute | solution.py:39
  38.6 0.8 collective-permute-done.7
  39.4 1.6 %collective-permute-start.25 = (bf16[48,1792]{1,0:T(8,128)(2,1)S(1)}, bf16[48,1792]{1,0:T(8,128)(2,1)S(1)}, u32[]{:S(2)}, u32[]{:S(2)}) collective-permute-start(bf16[48,1792]{1,0:T(8,128)(2,1)S(1)} %constant_dynamic-slice_fusion.1), channel_id=1, source_target_pairs={{0,16},{4,20},{8,24},{12,28},{16,0},{20,4},{24,8},{28,12},{1,17},{... | collective-permute-start | bytes 516104 | tf_op jit(solution)/shard_map/ppermute | solution.py:39
  41.1 1.6 %collective-permute-start.8 = (bf16[24,1792]{1,0:T(8,128)(2,1)S(1)}, bf16[24,1792]{1,0:T(8,128)(2,1)S(1)}, u32[]{:S(2)}, u32[]{:S(2)}) collective-permute-start(bf16[24,1792]{1,0:T(8,128)(2,1)S(1)} %constant_dynamic-slice_fusion.12), channel_id=1, source_target_pairs={{0,16},{4,20},{8,24},{12,28},{16,0},{20,4},{24,8},{28,12},{1,17},{... | collective-permute-start | bytes 258056 | tf_op jit(solution)/shard_map/ppermute | solution.py:39
  42.8 0.3 collective-permute-done.4
  43.1 1.5 %collective-permute-start.23 = (bf16[24,1792]{1,0:T(8,128)(2,1)S(1)}, bf16[24,1792]{1,0:T(8,128)(2,1)S(1)}, u32[]{:S(2)}, u32[]{:S(2)}) collective-permute-start(bf16[24,1792]{1,0:T(8,128)(2,1)S(1)} %constant_dynamic-slice_fusion.3), channel_id=1, source_target_pairs={{0,8},{4,12},{8,0},{12,4},{16,24},{20,28},{24,16},{28,20},{1,9},{5... | collective-permute-start | bytes 258056 | tf_op jit(solution)/shard_map/ppermute | solution.py:39
  44.7 0.1 collective-permute-done.19
  44.8 1.6 %collective-permute-start.5 = (bf16[24,1792]{1,0:T(8,128)(2,1)S(1)}, bf16[24,1792]{1,0:T(8,128)(2,1)S(1)}, u32[]{:S(2)}, u32[]{:S(2)}) collective-permute-start(bf16[24,1792]{1,0:T(8,128)(2,1)S(1)} %constant_dynamic-slice_fusion.15), channel_id=1, source_target_pairs={{0,16},{4,20},{8,24},{12,28},{16,0},{20,4},{24,8},{28,12},{1,17},{... | collective-permute-start | bytes 258056 | tf_op jit(solution)/shard_map/ppermute | solution.py:39
  46.4 0.3 collective-permute-done.13
  46.8 1.5 %collective-permute-start.20 = (bf16[24,1792]{1,0:T(8,128)(2,1)S(1)}, bf16[24,1792]{1,0:T(8,128)(2,1)S(1)}, u32[]{:S(2)}, u32[]{:S(2)}) collective-permute-start(bf16[24,1792]{1,0:T(8,128)(2,1)S(1)} %constant_dynamic-slice_fusion.6), channel_id=1, source_target_pairs={{0,8},{4,12},{8,0},{12,4},{16,24},{20,28},{24,16},{28,20},{1,9},{5... | collective-permute-start | bytes 258056 | tf_op jit(solution)/shard_map/ppermute | solution.py:39
  48.5 1.6 %collective-permute-start.14 = (bf16[24,1792]{1,0:T(8,128)(2,1)S(1)}, bf16[24,1792]{1,0:T(8,128)(2,1)S(1)}, u32[]{:S(2)}, u32[]{:S(2)}) collective-permute-start(bf16[24,1792]{1,0:T(8,128)(2,1)S(1)} %constant_dynamic-slice_fusion.9), channel_id=1, source_target_pairs={{0,16},{4,20},{8,24},{12,28},{16,0},{20,4},{24,8},{28,12},{1,17},{... | collective-permute-start | bytes 258056 | tf_op jit(solution)/shard_map/ppermute | solution.py:39
  50.1 0.2 collective-permute-done.8
  50.3 0.4 collective-permute-start.26
  50.7 1.3 %collective-permute-done.5 = bf16[24,1792]{1,0:T(8,128)(2,1)S(1)} collective-permute-done((bf16[24,1792]{1,0:T(8,128)(2,1)S(1)}, bf16[24,1792]{1,0:T(8,128)(2,1)S(1)}, u32[]{:S(2)}, u32[]{:S(2)}) %collective-permute-start.5) | collective-permute-done | bytes 86048 | tf_op jit(solution)/shard_map/ppermute | solution.py:39
  52.0 1.0 collective-permute-done.14
  53.0 0.2 fusion.6
  53.2 1.6 %collective-permute-start.15 = (bf16[3,24,1792]{2,1,0:T(8,128)(2,1)S(1)}, bf16[3,24,1792]{2,1,0:T(8,128)(2,1)S(1)}, u32[]{:S(2)}, u32[]{:S(2)}) collective-permute-start(bf16[3,24,1792]{2,1,0:T(8,128)(2,1)S(1)} %pad_maximum_fusion.2), channel_id=1, source_target_pairs={{0,16},{4,20},{8,24},{12,28},{16,0},{20,4},{24,8},{28,12},{1,17},{... | collective-permute-start | bytes 774152 | tf_op jit(solution)/shard_map/ppermute | solution.py:67
  54.8 0.2 fusion.8
  55.0 0.6 collective-permute-start.27
  55.6 4.6 %collective-permute-done.15 = bf16[3,24,1792]{2,1,0:T(8,128)(2,1)S(1)} collective-permute-done((bf16[3,24,1792]{2,1,0:T(8,128)(2,1)S(1)}, bf16[3,24,1792]{2,1,0:T(8,128)(2,1)S(1)}, u32[]{:S(2)}, u32[]{:S(2)}) %collective-permute-start.15) | collective-permute-done | bytes 258080 | tf_op jit(solution)/shard_map/ppermute | solution.py:67
  60.3 0.8 collective-permute-start.16
  61.2 1.3 %collective-permute-done.27 = bf16[3,24,1792]{2,1,0:T(8,128)(2,1)S(1)} collective-permute-done((bf16[3,24,1792]{2,1,0:T(8,128)(2,1)S(1)}, bf16[3,24,1792]{2,1,0:T(8,128)(2,1)S(1)}, u32[]{:S(2)}, u32[]{:S(2)}) %collective-permute-start.27) | collective-permute-done | bytes 258080 | tf_op jit(solution)/shard_map/ppermute | solution.py:67
  62.5 1.2 %collective-permute-start.28 = (bf16[3,48,1792]{2,1,0:T(8,128)(2,1)S(1)}, bf16[3,48,1792]{2,1,0:T(8,128)(2,1)S(1)}, u32[]{:S(2)}, u32[]{:S(2)}) collective-permute-start(bf16[3,48,1792]{2,1,0:T(8,128)(2,1)S(1)} %maximum_select_fusion.5), channel_id=1, source_target_pairs={{0,16},{4,20},{8,24},{12,28},{16,0},{20,4},{24,8},{28,12},{1,17},{... | collective-permute-start | bytes 1548296 | tf_op jit(solution)/shard_map/ppermute | solution.py:67
  63.7 9.1 %collective-permute-done.16 = bf16[3,48,1792]{2,1,0:T(8,128)(2,1)S(1)} collective-permute-done((bf16[3,48,1792]{2,1,0:T(8,128)(2,1)S(1)}, bf16[3,48,1792]{2,1,0:T(8,128)(2,1)S(1)}, u32[]{:S(2)}, u32[]{:S(2)}) %collective-permute-start.16) | collective-permute-done | bytes 516128 | tf_op jit(solution)/shard_map/ppermute | solution.py:67
  72.8 0.3 maximum_select_fusion.2
  73.2 0.3 maximum_select_fusion.3
  73.4 0.5 collective-permute-start.29
  73.9 1.8 %collective-permute-done.17 = bf16[3,96,1792]{2,1,0:T(8,128)(2,1)S(1)} collective-permute-done((bf16[3,96,1792]{2,1,0:T(8,128)(2,1)S(1)}, bf16[3,96,1792]{2,1,0:T(8,128)(2,1)S(1)}, u32[]{:S(2)}, u32[]{:S(2)}) %collective-permute-start.17) | collective-permute-done | bytes 1032224 | tf_op jit(solution)/shard_map/ppermute | solution.py:67
  75.7 0.8 maximum_select_fusion
  76.5 0.8 collective-permute-done.29
  77.3 2.1 %maximum_select_fusion.1 = bf16[3,192,1792]{2,1,0:T(8,128)(2,1)S(1)} fusion(bf16[3,96,1792]{2,1,0:T(8,128)(2,1)S(1)} %maximum_select_fusion.3, bf16[3,96,1792]{2,1,0:T(8,128)(2,1)} %collective-permute-done.29, pred[]{:T(512)S(6)} %eq.25), kind=kLoop, calls=%fused_computation.11 | loop fusion | flops 9289728 | bytes 4128769 | tf_op jit(solution)/shard_map/jit(_where)/select_n | solution.py:68
  79.4 0.5 fusion.4
  80.0 1.3 %slice-done.3 = s8[3145728]{0:T(1024)(128)(4,1)S(1)} async-done(((s8[7340032]{0:T(1024)(128)(4,1)}), s8[3145728]{0:T(1024)(128)(4,1)S(1)}, s32[]{:S(2)}) %slice-start.3) | async-done | bytes 3145752
  81.3 2.5 %fusion.16 = f32[192,1024]{1,0:T(8,128)S(1)} fusion(bf16[192,3584]{1,0:T(8,128)(2,1)S(1)} %get-tuple-element.14, bf16[1024,3584]{1,0:T(8,128)(2,1)S(1)} %bitcast.37), kind=kOutput, calls=%fused_computation.86 | convolution fusion | flops 1409286144 | bytes 9502720 | tf_op jit(solution)/shard_map/dot_general | solution.py:14
  83.8 2.5 %fusion.5 = bf16[192,1024]{1,0:T(8,128)(2,1)S(1)} fusion(f32[192,1024]{1,0:T(8,128)S(1)} %fusion.16, bf16[192,3584]{1,0:T(8,128)(2,1)S(1)} %get-tuple-element.13, bf16[1024,3584]{1,0:T(8,128)(2,1)S(1)} %bitcast.41), kind=kOutput, calls=%fused_computation.19 | convolution fusion | flops 1409679360 | bytes 9895936 | tf_op jit(solution)/shard_map/dot_general | solution.py:14
  86.4 1.9 %collective-permute-start.30 = (bf16[48,1024]{1,0:T(8,128)(2,1)S(1)}, bf16[48,1024]{1,0:T(8,128)(2,1)S(1)}, u32[]{:S(2)}, u32[]{:S(2)}) collective-permute-start(bf16[48,1024]{1,0:T(8,128)(2,1)S(1)} %get-tuple-element.31), channel_id=1, source_target_pairs={{0,3},{1,0},{2,1},{3,2},{4,7},{5,4},{6,5},{7,6},{8,11},{9,8},{10,9... | collective-permute-start | bytes 294920 | tf_op jit(solution)/shard_map/ppermute | solution.py:106
  88.3 0.1 collective-permute-start.32
  88.5 0.7 collective-permute-start.31
  89.2 5.2 %convolution_convert_fusion.2 = bf16[1024,3584]{1,0:T(8,128)(2,1)} fusion(bf16[192,1024]{1,0:T(8,128)(2,1)S(1)} %pad_maximum_fusion.1, bf16[192,3584]{1,0:T(8,128)(2,1)S(1)} %get-tuple-element.13), kind=kOutput, calls=%fused_computation.2 | convolution fusion | flops 1412956160 | bytes 9109504 | tf_op jit(solution)/shard_map/dot_general | solution.py:130
  94.4 5.2 %convolution_convert_fusion.1 = bf16[1024,3584]{1,0:T(8,128)(2,1)} fusion(bf16[192,1024]{1,0:T(8,128)(2,1)S(1)} %pad_maximum_fusion.1, bf16[192,3584]{1,0:T(8,128)(2,1)S(1)} %get-tuple-element.14), kind=kOutput, calls=%fused_computation.1 | convolution fusion | flops 1412956160 | bytes 9109504 | tf_op jit(solution)/shard_map/dot_general | solution.py:131
  99.6 5.2 %convolution_convert_fusion = bf16[3584,1024]{1,0:T(8,128)(2,1)} fusion(bf16[192,3584]{1,0:T(8,128)(2,1)S(1)} %get-tuple-element.15, bf16[192,1024]{1,0:T(8,128)(2,1)S(1)} %copy-done.1), kind=kOutput, calls=%fused_computation | convolution fusion | flops 1412956160 | bytes 9109504 | tf_op jit(solution)/shard_map/dot_general | solution.py:8
  104.8 0.7 add_convert_fusion.12
  (87 shorter events, 2.3 us)
Async XLA Ops:
  0.6 12.2 %collective-permute-start.1 = (bf16[48,1024]{1,0:T(8,128)(2,1)}, bf16[48,1024]{1,0:T(8,128)(2,1)S(1)}, u32[]{:S(2)}, u32[]{:S(2)}) collective-permute-start(bf16[48,1024]{1,0:T(8,128)(2,1)} %param.5), channel_id=1, source_target_pairs={{0,2},{1,3},{2,0},{3,1},{4,6},{5,7},{6,4},{7,5},{8,10},{9,11},{10,... | collective-permute-start | bytes 294920 | tf_op jit(solution)/shard_map/ppermute | solution.py:98
  4.8 8.1 %collective-permute-start = (bf16[48,1024]{1,0:T(8,128)(2,1)}, bf16[48,1024]{1,0:T(8,128)(2,1)S(1)}, u32[]{:S(2)}, u32[]{:S(2)}) collective-permute-start(bf16[48,1024]{1,0:T(8,128)(2,1)} %param.5), channel_id=1, source_target_pairs={{0,1},{1,2},{2,3},{3,0},{4,5},{5,6},{6,7},{7,4},{8,9},{9,10},{10,1... | collective-permute-start | bytes 294920 | tf_op jit(solution)/shard_map/ppermute | solution.py:98
  6.3 7.2 %collective-permute-start.2 = (bf16[48,1024]{1,0:T(8,128)(2,1)}, bf16[48,1024]{1,0:T(8,128)(2,1)S(1)}, u32[]{:S(2)}, u32[]{:S(2)}) collective-permute-start(bf16[48,1024]{1,0:T(8,128)(2,1)} %param.5), channel_id=1, source_target_pairs={{0,3},{1,0},{2,1},{3,2},{4,7},{5,4},{6,5},{7,6},{8,11},{9,8},{10,9... | collective-permute-start | bytes 294920 | tf_op jit(solution)/shard_map/ppermute | solution.py:98
  13.6 11.8 %slice-start.4 = ((s8[7340032]{0:T(1024)(128)(4,1)}), s8[4194304]{0:T(1024)(128)(4,1)S(1)}, s32[]{:S(2)}) async-start(s8[7340032]{0:T(1024)(128)(4,1)} %bitcast.38), calls=%async_computation.4 | async-start | bytes 8388608
  14.6 10.7 %slice-start.5 = ((s8[7340032]{0:T(1024)(128)(4,1)}), s8[3145728]{0:T(1024)(128)(4,1)S(1)}, s32[]{:S(2)}) async-start(s8[7340032]{0:T(1024)(128)(4,1)} %bitcast.38), calls=%async_computation.5 | async-start | bytes 6291456
  14.7 13.9 %collective-permute-start.11 = (bf16[48,1024]{1,0:T(8,128)(2,1)}, bf16[48,1024]{1,0:T(8,128)(2,1)S(1)}, u32[]{:S(2)}, u32[]{:S(2)}) collective-permute-start(bf16[48,1024]{1,0:T(8,128)(2,1)} %param.6), channel_id=1, source_target_pairs={{0,3},{1,0},{2,1},{3,2},{4,7},{5,4},{6,5},{7,6},{8,11},{9,8},{10,9... | collective-permute-start | bytes 294920 | tf_op jit(solution)/shard_map/ppermute | solution.py:98
  16.8 11.3 %collective-permute-start.10 = (bf16[48,1024]{1,0:T(8,128)(2,1)}, bf16[48,1024]{1,0:T(8,128)(2,1)S(1)}, u32[]{:S(2)}, u32[]{:S(2)}) collective-permute-start(bf16[48,1024]{1,0:T(8,128)(2,1)} %param.6), channel_id=1, source_target_pairs={{0,2},{1,3},{2,0},{3,1},{4,6},{5,7},{6,4},{7,5},{8,10},{9,11},{10,... | collective-permute-start | bytes 294920 | tf_op jit(solution)/shard_map/ppermute | solution.py:98
  17.9 10.0 %collective-permute-start.9 = (bf16[48,1024]{1,0:T(8,128)(2,1)}, bf16[48,1024]{1,0:T(8,128)(2,1)S(1)}, u32[]{:S(2)}, u32[]{:S(2)}) collective-permute-start(bf16[48,1024]{1,0:T(8,128)(2,1)} %param.6), channel_id=1, source_target_pairs={{0,1},{1,2},{2,3},{3,0},{4,5},{5,6},{6,7},{7,4},{8,9},{9,10},{10,1... | collective-permute-start | bytes 294920 | tf_op jit(solution)/shard_map/ppermute | solution.py:98
  24.7 3.9 %slice-start = ((s8[7340032]{0:T(1024)(128)(4,1)}), s8[4194304]{0:T(1024)(128)(4,1)S(1)}, s32[]{:S(2)}) async-start(s8[7340032]{0:T(1024)(128)(4,1)} %bitcast.34), calls=%async_computation | async-start | bytes 8388608
  24.8 3.9 %slice-start.1 = ((s8[7340032]{0:T(1024)(128)(4,1)}), s8[3145728]{0:T(1024)(128)(4,1)S(1)}, s32[]{:S(2)}) async-start(s8[7340032]{0:T(1024)(128)(4,1)} %bitcast.34), calls=%async_computation.1 | async-start | bytes 6291456
  24.8 6.7 %collective-permute-start.6 = (bf16[96,1792]{1,0:T(8,128)(2,1)S(1)}, bf16[96,1792]{1,0:T(8,128)(2,1)S(1)}, u32[]{:S(2)}, u32[]{:S(2)}) collective-permute-start(bf16[96,1792]{1,0:T(8,128)(2,1)S(1)} %constant_dynamic-slice_fusion.14), channel_id=1, source_target_pairs={{0,4},{4,0},{8,12},{12,8},{16,20},{20,16},{24,28},{28,24},{1,5},{5... | collective-permute-start | bytes 1032200 | tf_op jit(solution)/shard_map/ppermute | solution.py:39
  24.9 7.3 %collective-permute-start.21 = (bf16[96,1792]{1,0:T(8,128)(2,1)S(1)}, bf16[96,1792]{1,0:T(8,128)(2,1)S(1)}, u32[]{:S(2)}, u32[]{:S(2)}) collective-permute-start(bf16[96,1792]{1,0:T(8,128)(2,1)S(1)} %constant_dynamic-slice_fusion.5), channel_id=1, source_target_pairs={{0,4},{4,0},{8,12},{12,8},{16,20},{20,16},{24,28},{28,24},{1,5},{5... | collective-permute-start | bytes 1032200 | tf_op jit(solution)/shard_map/ppermute | solution.py:39
  27.0 0.9 copy-start.2
  27.9 5.9 %collective-permute-start.3 = (bf16[96,1792]{1,0:T(8,128)(2,1)S(1)}, bf16[96,1792]{1,0:T(8,128)(2,1)S(1)}, u32[]{:S(2)}, u32[]{:S(2)}) collective-permute-start(bf16[96,1792]{1,0:T(8,128)(2,1)S(1)} %constant_dynamic-slice_fusion.17), channel_id=1, source_target_pairs={{0,4},{4,0},{8,12},{12,8},{16,20},{20,16},{24,28},{28,24},{1,5},{5... | collective-permute-start | bytes 1032200 | tf_op jit(solution)/shard_map/ppermute | solution.py:39
  28.1 7.5 %collective-permute-start.18 = (bf16[96,1792]{1,0:T(8,128)(2,1)S(1)}, bf16[96,1792]{1,0:T(8,128)(2,1)S(1)}, u32[]{:S(2)}, u32[]{:S(2)}) collective-permute-start(bf16[96,1792]{1,0:T(8,128)(2,1)S(1)} %constant_dynamic-slice_fusion.8), channel_id=1, source_target_pairs={{0,4},{4,0},{8,12},{12,8},{16,20},{20,16},{24,28},{28,24},{1,5},{5... | collective-permute-start | bytes 1032200 | tf_op jit(solution)/shard_map/ppermute | solution.py:39
  28.6 2.6 %copy-start = (bf16[192,1024]{1,0:T(8,128)(2,1)}, bf16[192,1024]{1,0:T(8,128)(2,1)S(1)}, u32[]{:S(2)}) copy-start(bf16[192,1024]{1,0:T(8,128)(2,1)S(1)} %constant_dynamic-update-slice_fusion) | copy-start | bytes 1179652
  31.4 4.9 %collective-permute-start.12 = (bf16[96,1792]{1,0:T(8,128)(2,1)S(1)}, bf16[96,1792]{1,0:T(8,128)(2,1)S(1)}, u32[]{:S(2)}, u32[]{:S(2)}) collective-permute-start(bf16[96,1792]{1,0:T(8,128)(2,1)S(1)} %constant_dynamic-slice_fusion.11), channel_id=1, source_target_pairs={{0,4},{4,0},{8,12},{12,8},{16,20},{20,16},{24,28},{28,24},{1,5},{5... | collective-permute-start | bytes 1032200 | tf_op jit(solution)/shard_map/ppermute | solution.py:39
  31.5 5.5 %collective-permute-start.24 = (bf16[96,1792]{1,0:T(8,128)(2,1)S(1)}, bf16[96,1792]{1,0:T(8,128)(2,1)S(1)}, u32[]{:S(2)}, u32[]{:S(2)}) collective-permute-start(bf16[96,1792]{1,0:T(8,128)(2,1)S(1)} %constant_dynamic-slice_fusion.2), channel_id=1, source_target_pairs={{0,4},{4,0},{8,12},{12,8},{16,20},{20,16},{24,28},{28,24},{1,5},{5... | collective-permute-start | bytes 1032200 | tf_op jit(solution)/shard_map/ppermute | solution.py:39
  32.2 7.3 %collective-permute-start.7 = (bf16[48,1792]{1,0:T(8,128)(2,1)S(1)}, bf16[48,1792]{1,0:T(8,128)(2,1)S(1)}, u32[]{:S(2)}, u32[]{:S(2)}) collective-permute-start(bf16[48,1792]{1,0:T(8,128)(2,1)S(1)} %constant_dynamic-slice_fusion.13), channel_id=1, source_target_pairs={{0,8},{4,12},{8,0},{12,4},{16,24},{20,28},{24,16},{28,20},{1,9},{5... | collective-permute-start | bytes 516104 | tf_op jit(solution)/shard_map/ppermute | solution.py:39
  33.8 7.3 %collective-permute-start.22 = (bf16[48,1792]{1,0:T(8,128)(2,1)S(1)}, bf16[48,1792]{1,0:T(8,128)(2,1)S(1)}, u32[]{:S(2)}, u32[]{:S(2)}) collective-permute-start(bf16[48,1792]{1,0:T(8,128)(2,1)S(1)} %constant_dynamic-slice_fusion.4), channel_id=1, source_target_pairs={{0,16},{4,20},{8,24},{12,28},{16,0},{20,4},{24,8},{28,12},{1,17},{... | collective-permute-start | bytes 516104 | tf_op jit(solution)/shard_map/ppermute | solution.py:39
  35.6 7.5 %collective-permute-start.4 = (bf16[48,1792]{1,0:T(8,128)(2,1)S(1)}, bf16[48,1792]{1,0:T(8,128)(2,1)S(1)}, u32[]{:S(2)}, u32[]{:S(2)}) collective-permute-start(bf16[48,1792]{1,0:T(8,128)(2,1)S(1)} %constant_dynamic-slice_fusion.16), channel_id=1, source_target_pairs={{0,8},{4,12},{8,0},{12,4},{16,24},{20,28},{24,16},{28,20},{1,9},{5... | collective-permute-start | bytes 516104 | tf_op jit(solution)/shard_map/ppermute | solution.py:39
  36.3 8.6 %collective-permute-start.19 = (bf16[48,1792]{1,0:T(8,128)(2,1)S(1)}, bf16[48,1792]{1,0:T(8,128)(2,1)S(1)}, u32[]{:S(2)}, u32[]{:S(2)}) collective-permute-start(bf16[48,1792]{1,0:T(8,128)(2,1)S(1)} %constant_dynamic-slice_fusion.7), channel_id=1, source_target_pairs={{0,16},{4,20},{8,24},{12,28},{16,0},{20,4},{24,8},{28,12},{1,17},{... | collective-permute-start | bytes 516104 | tf_op jit(solution)/shard_map/ppermute | solution.py:39
  37.0 9.8 %collective-permute-start.13 = (bf16[48,1792]{1,0:T(8,128)(2,1)S(1)}, bf16[48,1792]{1,0:T(8,128)(2,1)S(1)}, u32[]{:S(2)}, u32[]{:S(2)}) collective-permute-start(bf16[48,1792]{1,0:T(8,128)(2,1)S(1)} %constant_dynamic-slice_fusion.10), channel_id=1, source_target_pairs={{0,8},{4,12},{8,0},{12,4},{16,24},{20,28},{24,16},{28,20},{1,9},{5... | collective-permute-start | bytes 516104 | tf_op jit(solution)/shard_map/ppermute | solution.py:39
  39.4 9.1 %collective-permute-start.25 = (bf16[48,1792]{1,0:T(8,128)(2,1)S(1)}, bf16[48,1792]{1,0:T(8,128)(2,1)S(1)}, u32[]{:S(2)}, u32[]{:S(2)}) collective-permute-start(bf16[48,1792]{1,0:T(8,128)(2,1)S(1)} %constant_dynamic-slice_fusion.1), channel_id=1, source_target_pairs={{0,16},{4,20},{8,24},{12,28},{16,0},{20,4},{24,8},{28,12},{1,17},{... | collective-permute-start | bytes 516104 | tf_op jit(solution)/shard_map/ppermute | solution.py:39
  41.1 9.2 %collective-permute-start.8 = (bf16[24,1792]{1,0:T(8,128)(2,1)S(1)}, bf16[24,1792]{1,0:T(8,128)(2,1)S(1)}, u32[]{:S(2)}, u32[]{:S(2)}) collective-permute-start(bf16[24,1792]{1,0:T(8,128)(2,1)S(1)} %constant_dynamic-slice_fusion.12), channel_id=1, source_target_pairs={{0,16},{4,20},{8,24},{12,28},{16,0},{20,4},{24,8},{28,12},{1,17},{... | collective-permute-start | bytes 258056 | tf_op jit(solution)/shard_map/ppermute | solution.py:39
  43.1 11.7 %collective-permute-start.23 = (bf16[24,1792]{1,0:T(8,128)(2,1)S(1)}, bf16[24,1792]{1,0:T(8,128)(2,1)S(1)}, u32[]{:S(2)}, u32[]{:S(2)}) collective-permute-start(bf16[24,1792]{1,0:T(8,128)(2,1)S(1)} %constant_dynamic-slice_fusion.3), channel_id=1, source_target_pairs={{0,8},{4,12},{8,0},{12,4},{16,24},{20,28},{24,16},{28,20},{1,9},{5... | collective-permute-start | bytes 258056 | tf_op jit(solution)/shard_map/ppermute | solution.py:39
  44.8 7.1 %collective-permute-start.5 = (bf16[24,1792]{1,0:T(8,128)(2,1)S(1)}, bf16[24,1792]{1,0:T(8,128)(2,1)S(1)}, u32[]{:S(2)}, u32[]{:S(2)}) collective-permute-start(bf16[24,1792]{1,0:T(8,128)(2,1)S(1)} %constant_dynamic-slice_fusion.15), channel_id=1, source_target_pairs={{0,16},{4,20},{8,24},{12,28},{16,0},{20,4},{24,8},{28,12},{1,17},{... | collective-permute-start | bytes 258056 | tf_op jit(solution)/shard_map/ppermute | solution.py:39
  46.8 8.0 %collective-permute-start.20 = (bf16[24,1792]{1,0:T(8,128)(2,1)S(1)}, bf16[24,1792]{1,0:T(8,128)(2,1)S(1)}, u32[]{:S(2)}, u32[]{:S(2)}) collective-permute-start(bf16[24,1792]{1,0:T(8,128)(2,1)S(1)} %constant_dynamic-slice_fusion.6), channel_id=1, source_target_pairs={{0,8},{4,12},{8,0},{12,4},{16,24},{20,28},{24,16},{28,20},{1,9},{5... | collective-permute-start | bytes 258056 | tf_op jit(solution)/shard_map/ppermute | solution.py:39
  48.5 4.5 %collective-permute-start.14 = (bf16[24,1792]{1,0:T(8,128)(2,1)S(1)}, bf16[24,1792]{1,0:T(8,128)(2,1)S(1)}, u32[]{:S(2)}, u32[]{:S(2)}) collective-permute-start(bf16[24,1792]{1,0:T(8,128)(2,1)S(1)} %constant_dynamic-slice_fusion.9), channel_id=1, source_target_pairs={{0,16},{4,20},{8,24},{12,28},{16,0},{20,4},{24,8},{28,12},{1,17},{... | collective-permute-start | bytes 258056 | tf_op jit(solution)/shard_map/ppermute | solution.py:39
  50.3 4.5 %collective-permute-start.26 = (bf16[24,1792]{1,0:T(8,128)(2,1)S(1)}, bf16[24,1792]{1,0:T(8,128)(2,1)S(1)}, u32[]{:S(2)}, u32[]{:S(2)}) collective-permute-start(bf16[24,1792]{1,0:T(8,128)(2,1)S(1)} %constant_dynamic-slice_fusion), channel_id=1, source_target_pairs={{0,8},{4,12},{8,0},{12,4},{16,24},{20,28},{24,16},{28,20},{1,9},{5... | collective-permute-start | bytes 258056 | tf_op jit(solution)/shard_map/ppermute | solution.py:39
  53.2 7.0 %collective-permute-start.15 = (bf16[3,24,1792]{2,1,0:T(8,128)(2,1)S(1)}, bf16[3,24,1792]{2,1,0:T(8,128)(2,1)S(1)}, u32[]{:S(2)}, u32[]{:S(2)}) collective-permute-start(bf16[3,24,1792]{2,1,0:T(8,128)(2,1)S(1)} %pad_maximum_fusion.2), channel_id=1, source_target_pairs={{0,16},{4,20},{8,24},{12,28},{16,0},{20,4},{24,8},{28,12},{1,17},{... | collective-permute-start | bytes 774152 | tf_op jit(solution)/shard_map/ppermute | solution.py:67
  55.0 7.4 %collective-permute-start.27 = (bf16[3,24,1792]{2,1,0:T(8,128)(2,1)S(1)}, bf16[3,24,1792]{2,1,0:T(8,128)(2,1)S(1)}, u32[]{:S(2)}, u32[]{:S(2)}) collective-permute-start(bf16[3,24,1792]{2,1,0:T(8,128)(2,1)S(1)} %pad_maximum_fusion.3), channel_id=1, source_target_pairs={{0,8},{4,12},{8,0},{12,4},{16,24},{20,28},{24,16},{28,20},{1,9},{5... | collective-permute-start | bytes 774152 | tf_op jit(solution)/shard_map/ppermute | solution.py:67
  60.3 12.4 %collective-permute-start.16 = (bf16[3,48,1792]{2,1,0:T(8,128)(2,1)S(1)}, bf16[3,48,1792]{2,1,0:T(8,128)(2,1)S(1)}, u32[]{:S(2)}, u32[]{:S(2)}) collective-permute-start(bf16[3,48,1792]{2,1,0:T(8,128)(2,1)S(1)} %maximum_select_fusion.4), channel_id=1, source_target_pairs={{0,8},{4,12},{8,0},{12,4},{16,24},{20,28},{24,16},{28,20},{1,9},{5... | collective-permute-start | bytes 1548296 | tf_op jit(solution)/shard_map/ppermute | solution.py:67
  62.5 10.6 %collective-permute-start.28 = (bf16[3,48,1792]{2,1,0:T(8,128)(2,1)S(1)}, bf16[3,48,1792]{2,1,0:T(8,128)(2,1)S(1)}, u32[]{:S(2)}, u32[]{:S(2)}) collective-permute-start(bf16[3,48,1792]{2,1,0:T(8,128)(2,1)S(1)} %maximum_select_fusion.5), channel_id=1, source_target_pairs={{0,16},{4,20},{8,24},{12,28},{16,0},{20,4},{24,8},{28,12},{1,17},{... | collective-permute-start | bytes 1548296 | tf_op jit(solution)/shard_map/ppermute | solution.py:67
  73.0 2.7 %collective-permute-start.17 = (bf16[3,96,1792]{2,1,0:T(8,128)(2,1)S(1)}, bf16[3,96,1792]{2,1,0:T(8,128)(2,1)S(1)}, u32[]{:S(2)}, u32[]{:S(2)}) collective-permute-start(bf16[3,96,1792]{2,1,0:T(8,128)(2,1)S(1)} %maximum_select_fusion.2), channel_id=1, source_target_pairs={{0,4},{4,0},{8,12},{12,8},{16,20},{20,16},{24,28},{28,24},{1,5},{5... | collective-permute-start | bytes 3096584 | tf_op jit(solution)/shard_map/ppermute | solution.py:67
  73.4 3.9 %collective-permute-start.29 = (bf16[3,96,1792]{2,1,0:T(8,128)(2,1)S(1)}, bf16[3,96,1792]{2,1,0:T(8,128)(2,1)}, u32[]{:S(2)}, u32[]{:S(2)}) collective-permute-start(bf16[3,96,1792]{2,1,0:T(8,128)(2,1)S(1)} %maximum_select_fusion.3), channel_id=1, source_target_pairs={{0,4},{4,0},{8,12},{12,8},{16,20},{20,16},{24,28},{28,24},{1,5},{5... | collective-permute-start | bytes 3096584 | tf_op jit(solution)/shard_map/ppermute | solution.py:67
  75.7 4.3 %slice-start.2 = ((s8[7340032]{0:T(1024)(128)(4,1)}), s8[4194304]{0:T(1024)(128)(4,1)S(1)}, s32[]{:S(2)}) async-start(s8[7340032]{0:T(1024)(128)(4,1)} %bitcast.36), calls=%async_computation.2 | async-start | bytes 8388608
  79.4 1.9 %slice-start.3 = ((s8[7340032]{0:T(1024)(128)(4,1)}), s8[3145728]{0:T(1024)(128)(4,1)S(1)}, s32[]{:S(2)}) async-start(s8[7340032]{0:T(1024)(128)(4,1)} %bitcast.36), calls=%async_computation.3 | async-start | bytes 6291456
  79.4 4.4 %slice-start.6 = ((s8[7340032]{0:T(1024)(128)(4,1)}), s8[4194304]{0:T(1024)(128)(4,1)S(1)}, s32[]{:S(2)}) async-start(s8[7340032]{0:T(1024)(128)(4,1)} %bitcast.40), calls=%async_computation.6 | async-start | bytes 8388608
  81.3 2.5 %slice-start.7 = ((s8[7340032]{0:T(1024)(128)(4,1)}), s8[3145728]{0:T(1024)(128)(4,1)S(1)}, s32[]{:S(2)}) async-start(s8[7340032]{0:T(1024)(128)(4,1)} %bitcast.40), calls=%async_computation.7 | async-start | bytes 6291456
  86.4 18.4 %collective-permute-start.30 = (bf16[48,1024]{1,0:T(8,128)(2,1)S(1)}, bf16[48,1024]{1,0:T(8,128)(2,1)S(1)}, u32[]{:S(2)}, u32[]{:S(2)}) collective-permute-start(bf16[48,1024]{1,0:T(8,128)(2,1)S(1)} %get-tuple-element.31), channel_id=1, source_target_pairs={{0,3},{1,0},{2,1},{3,2},{4,7},{5,4},{6,5},{7,6},{8,11},{9,8},{10,9... | collective-permute-start | bytes 294920 | tf_op jit(solution)/shard_map/ppermute | solution.py:106
  88.3 16.5 %collective-permute-start.32 = (bf16[48,1024]{1,0:T(8,128)(2,1)S(1)}, bf16[48,1024]{1,0:T(8,128)(2,1)S(1)}, u32[]{:S(2)}, u32[]{:S(2)}) collective-permute-start(bf16[48,1024]{1,0:T(8,128)(2,1)S(1)} %get-tuple-element.32), channel_id=1, source_target_pairs={{0,1},{1,2},{2,3},{3,0},{4,5},{5,6},{6,7},{7,4},{8,9},{9,10},{10,1... | collective-permute-start | bytes 294920 | tf_op jit(solution)/shard_map/ppermute | solution.py:106
  88.5 16.3 %collective-permute-start.31 = (bf16[48,1024]{1,0:T(8,128)(2,1)S(1)}, bf16[48,1024]{1,0:T(8,128)(2,1)S(1)}, u32[]{:S(2)}, u32[]{:S(2)}) collective-permute-start(bf16[48,1024]{1,0:T(8,128)(2,1)S(1)} %get-tuple-element.33), channel_id=1, source_target_pairs={{0,2},{1,3},{2,0},{3,1},{4,6},{5,7},{6,4},{7,5},{8,10},{9,11},{10,... | collective-permute-start | bytes 294920 | tf_op jit(solution)/shard_map/ppermute | solution.py:106
  94.4 5.2 %copy-start.1 = (bf16[192,1024]{1,0:T(8,128)(2,1)S(1)}, bf16[192,1024]{1,0:T(8,128)(2,1)}, u32[]{:S(2)}) copy-start(bf16[192,1024]{1,0:T(8,128)(2,1)} %copy-done) | copy-start | bytes 1179652
